TPU v7x, 32 devices: a whole 2x2x4 slice. The times are simulated.
32 devices in a mesh: groups: 2 (over y), pool: 4 (over z), col: 2 (over x), side: 2 (over core).
Axes of the slice: x: 2, y: 2, z: 4, core: 2. Of those that a mesh axis runs over, the one named last changes fastest.
Arguments:
- tokens: bfloat16 [64, 8192], P(('groups', 'col', 'side'), 'pool'), parts along dimension 0, may hold values from -35 to 35
- attn_gain: float32 [8192], P('pool'), may hold values from 0.25 to 1.75
- w_qkv: bfloat16 [8192, 8, 1280], P('pool', ('col', 'side')), may hold values from -0.0625 to 0.0625
- w_out: bfloat16 [8192, 8192], P(('col', 'side'), 'pool'), may hold values from -0.25 to 0.25
- ffn_gain: float32 [8192], P('pool'), may hold values from 0.25 to 1.75
- w_gate: bfloat16 [8192, 14336], P('pool', ('col', 'side')), may hold values from -0.0625 to 0.0625
- w_up: bfloat16 [8192, 14336], P('pool', ('col', 'side')), may hold values from -0.0625 to 0.0625
- w_down: bfloat16 [14336, 8192], P(('col', 'side'), 'pool'), may hold values from -0.046875 to 0.046875
- kv_cache: bfloat16 [64, 256, 2, 8, 128], P(('groups', 'pool'), None, None, ('col', 'side')), parts along dimension 0, may hold values from -240 to 240
- lengths: int32 [64], P('groups'), parts along dimension 0, may hold values from 1 to 256, 4096 in all
- request_slot: int32 [64], P('groups'), parts along dimension 0, may hold values from 0 to 31, each once
- row_request: int32 [64], P('groups'), parts along dimension 0, may hold values from 0 to 31, each once
Outputs:
- layer_out: float32 [64, 8192], P(('groups', 'col', 'side'), 'pool'), parts along dimension 0
There are 2 independent parts, one for each index of `groups`. A program takes and returns all parts, laid end to end along the dimension named above; an argument that names none is the same for every part. Nothing has to cross between parts.
Inputs may be any that keep to these rules, and one draw needn't show every extreme that they name: `lengths`: tokens in the cache of each request; over one part they sum to 4096 and one request has exactly 256. A permutation: the cache of request r is kv_cache[request_slot[r]]. A permutation: row j of tokens is request row_request[j].
All inputs are finite; a program needn't handle non-finite values.
Results may differ from a plain program's by a relative error of at most 0.009.
The roundings to bfloat16 on the way count: a program that leaves them out, or rounds other values in their place, can miss the bound.
Values may be sent and summed in bfloat16 or wider, within the bound.
No kernel may reach another device: no remote copies, remote signals or barrier semaphores. Data moves between devices by JAX's collectives and lax.ppermute only.
A program may use at most 192 MiB of HBM per device.

v0:
```python
import math

import jax
import jax.numpy as jnp
from jax import lax
from jax.sharding import PartitionSpec as P

D = 8192
H = 64
KVH = 8
HD = 128


epsilon = 1e-05
rope_base = 500000.0


def rotate(heads_in, positions):
    half_width = heads_in.shape[-1] // 2
    frequency = 1.0 / rope_base ** (
        jnp.arange(half_width, dtype=jnp.float32) * 2.0 / heads_in.shape[-1]
    )
    angles = positions.astype(jnp.float32)[:, None] * frequency[None, :]
    cosine_part = jnp.cos(angles)[:, None, :]
    sine_part = jnp.sin(angles)[:, None, :]
    first_half = heads_in[..., :half_width]
    second_half = heads_in[..., half_width:]
    return jnp.concatenate(
        [
            first_half * cosine_part - second_half * sine_part,
            second_half * cosine_part + first_half * sine_part,
        ],
        axis=-1,
    )


def rope_rows(qkv_sum, positions, per_group, head_dim):
    row_count = qkv_sum.shape[0]
    shaped = qkv_sum.reshape(row_count, -1, per_group + 2, head_dim)
    group_count = shaped.shape[1]
    turned = rotate(
        shaped[:, :, : per_group + 1].reshape(row_count, group_count * (per_group + 1), head_dim),
        positions,
    )
    turned = turned.reshape(row_count, group_count, per_group + 1, head_dim)
    return (
        jnp.concatenate([turned, shaped[:, :, per_group + 1 :]], axis=2)
        .reshape(row_count, -1)
        .astype(jnp.bfloat16)
    )


def attend(qkv_rot, kv_block, seen_count, per_group, head_dim):
    slot_count = qkv_rot.shape[0]
    cache_keys = kv_block[:, :, 0]
    values_all = kv_block[:, :, 1]
    shaped = qkv_rot.reshape(slot_count, cache_keys.shape[2], per_group + 2, head_dim)
    queries = shaped[:, :, :per_group]
    own_key = shaped[:, :, per_group]
    own_value = shaped[:, :, per_group + 1]
    score_scale = 1.0 / math.sqrt(head_dim)
    scores = (
        jnp.einsum("sgqd,stgd->sgqt", queries, cache_keys, preferred_element_type=jnp.float32)
        * score_scale
    )
    own_score = (
        jnp.einsum("sgqd,sgd->sgq", queries, own_key, preferred_element_type=jnp.float32)
        * score_scale
    )
    live_mask = (jnp.arange(cache_keys.shape[1], dtype=jnp.int32)[None, :] < seen_count[:, None])[
        :, None, None, :
    ]
    peak_score = jnp.maximum(jnp.max(jnp.where(live_mask, scores, -jnp.inf), axis=-1), own_score)
    weights = jnp.where(live_mask, jnp.exp(scores - peak_score[..., None]), 0.0)
    own_weight = jnp.exp(own_score - peak_score)
    denominator = jnp.sum(weights, axis=-1) + own_weight
    prob_weights = (weights / denominator[..., None]).astype(jnp.bfloat16)
    own_prob = (own_weight / denominator).astype(jnp.bfloat16)
    mixture = jnp.einsum(
        "sgqt,stgd->sgqd", prob_weights, values_all, preferred_element_type=jnp.float32
    )
    mixture = (
        mixture
        + own_prob.astype(jnp.float32)[..., None] * own_value.astype(jnp.float32)[:, :, None, :]
    )
    return mixture.reshape(slot_count, -1).astype(jnp.bfloat16)


def local(
    tokens,
    attn_gain,
    w_qkv,
    w_out,
    ffn_gain,
    w_gate,
    w_up,
    w_down,
    kv_cache,
    lengths,
    request_slot,
    row_request,
):
    pool_index = lax.axis_index("pool")
    per_owner = kv_cache.shape[0]
    per_group = H // KVH
    my_start = pool_index * per_owner
    slot_of_row = jnp.take(request_slot, row_request)
    row_of_slot = jnp.argsort(slot_of_row)
    length_of_row = jnp.take(lengths, row_request)
    length_of_slot = jnp.take(length_of_row, row_of_slot)
    residual = tokens.astype(jnp.float32)
    squares = lax.psum(jnp.sum(residual * residual, axis=1), "pool")
    normed = (residual * lax.rsqrt(squares / D + epsilon)[:, None] * attn_gain[None, :]).astype(
        jnp.bfloat16
    )
    normed_all = lax.all_gather(normed, ("col", "side"), axis=0, tiled=True)
    local_qkv = w_qkv.reshape(w_qkv.shape[0], -1)
    positions = lax.dynamic_slice_in_dim(length_of_row, my_start, per_owner, 0)
    picked = normed_all
    summed = lax.psum_scatter(
        jnp.dot(picked, local_qkv, preferred_element_type=jnp.float32),
        "pool",
        scatter_dimension=0,
        tiled=True,
    )
    rotated = rope_rows(summed, positions, per_group, HD)
    all_rows = lax.all_gather(rotated, "pool", axis=0, tiled=True)
    own_rows = jnp.take(
        all_rows, lax.dynamic_slice_in_dim(row_of_slot, my_start, per_owner, 0), axis=0
    )
    seen_count = lax.dynamic_slice_in_dim(length_of_slot, my_start, per_owner, 0)
    attended = attend(own_rows, kv_cache, seen_count, per_group, HD)
    gathered = lax.all_gather(attended, "pool", axis=0, tiled=True)
    by_row = jnp.take(gathered, slot_of_row, axis=0)
    picked = by_row
    residual = residual + lax.psum_scatter(
        jnp.dot(picked, w_out, preferred_element_type=jnp.float32).astype(jnp.bfloat16),
        ("col", "side"),
        scatter_dimension=0,
        tiled=True,
    ).astype(jnp.float32)
    squares_mid = lax.psum(jnp.sum(residual * residual, axis=1), "pool")
    ffn_normed = (
        residual * lax.rsqrt(squares_mid / D + epsilon)[:, None] * ffn_gain[None, :]
    ).astype(jnp.bfloat16)
    ffn_all = lax.all_gather(ffn_normed, ("col", "side"), axis=0, tiled=True)
    gate_part = jnp.dot(ffn_all, w_gate, preferred_element_type=jnp.float32)
    up_part = jnp.dot(ffn_all, w_up, preferred_element_type=jnp.float32)
    gate_total, up_total = (
        lax.psum(gate_part.astype(jnp.bfloat16), "pool").astype(jnp.float32),
        lax.psum(up_part.astype(jnp.bfloat16), "pool").astype(jnp.float32),
    )
    hidden_all = (jax.nn.silu(gate_total) * up_total).astype(jnp.bfloat16)
    picked = hidden_all
    return residual + lax.psum_scatter(
        jnp.dot(picked, w_down, preferred_element_type=jnp.float32).astype(jnp.bfloat16),
        ("col", "side"),
        scatter_dimension=0,
        tiled=True,
    ).astype(jnp.float32)


def solution(mesh):
    return jax.shard_map(
        local,
        mesh=mesh,
        in_specs=(
            P(("groups", "col", "side"), "pool"),
            P("pool"),
            P("pool", ("col", "side"), None),
            P(("col", "side"), "pool"),
            P("pool"),
            P("pool", ("col", "side")),
            P("pool", ("col", "side")),
            P(("col", "side"), "pool"),
            P(("groups", "pool"), None, None, ("col", "side"), None),
            P("groups"),
            P("groups"),
            P("groups"),
        ),
        out_specs=P(("groups", "col", "side"), "pool"),
        check_vma=False,
    )
```

profile of v0, /device:TPU:0, one launch (start us, length us, event | category | flops | bytes accessed | tf_op | source)
XLA Modules:
  0.0 225.1 jit_solution(14973798794183425735)
XLA Ops:
  6.5 1.0 fusion.12
  7.5 10.2 %copy.23 = bf16[256,8,2,1280]{3,1,2,0:T(8,128)(2,1)} copy(bf16[256,8,2,1280]{3,2,1,0:T(2,128)(2,1)} %bitcast.37) | data formatting | bytes 20971520
  17.7 13.6 %psum.28 = f32[8]{0:T(128)S(1)} all-reduce(f32[8]{0:T(128)S(1)} %fusion.12), channel_id=1, replica_groups=mesh['groups'=2,'pool'=4,'col'=2,'side'=2] {'pool'}, use_global_device_ids=true, to_apply=%region_2.4 | all-reduce | flops 8 | bytes 64 | tf_op jit(solution)/shard_map/psum | solution.py:112
  31.4 5.4 %all_gather.12 = bf16[32,2048]{1,0:T(8,128)(2,1)S(1)} all-gather(bf16[8,2048]{1,0:T(8,128)(2,1)S(1)} %fusion.14), channel_id=1, replica_groups=mesh['groups'=2,'pool'=4,'col'=2,'side'=2] {'col','side'}, dimensions={0}, use_global_device_ids=true | all-gather | bytes 163840 | tf_op jit(solution)/shard_map/all_gather | solution.py:116
  36.8 6.6 %fusion.30 = f32[32,2560]{1,0:T(8,128)} fusion(bf16[32,2048]{1,0:T(8,128)(2,1)S(1)} %all_gather.12, bf16[2048,2560]{1,0:T(8,128)(2,1)} %bitcast.36), kind=kOutput, calls=%fused_computation.86 | convolution fusion | flops 335544320 | bytes 10944512 | tf_op jit(solution)/shard_map/dot_general | solution.py:121
  43.5 0.7 gather_fusion.3
  44.2 0.7 gather_fusion.2
  45.0 1.6 sort.17
  46.7 0.7 gather_fusion.4
  47.7 2.3 %fusion.29 = (bf16[8,256,1,2,128]{4,3,2,1,0:T(2,128)(2,1)S(1)}, bf16[8,256,1,2,128]{4,3,2,1,0:T(2,128)(2,1)}) fusion(bf16[8,256,2,2,128]{4,3,2,1,0:T(2,128)(2,1)S(1)} %copy-done.3), kind=kLoop, calls=%fused_computation.85 | loop fusion | bytes 4194304 | tf_op jit(solution)/shard_map/slice | solution.py:55
  50.0 11.8 %reduce-scatter.4.cloned.1.call-done = f32[8,2560]{1,0:T(8,128)} async-done(((f32[32,2560]{1,0:T(8,128)}), f32[8,2560]{1,0:T(8,128)}) %reduce-scatter.4.cloned.1.call-update) | async-done | bytes 81936 | tf_op jit(solution)/shard_map/reduce_scatter | solution.py:120
  61.8 0.9 slice.47
  62.7 0.7 slice.64
  63.6 13.5 %all_gather.13 = bf16[32,2560]{1,0:T(8,128)(2,1)S(1)} all-gather(bf16[8,2560]{1,0:T(8,128)(2,1)S(1)} %bitcast.39), channel_id=1, replica_groups=mesh['groups'=2,'pool'=4,'col'=2,'side'=2] {'pool'}, dimensions={0}, use_global_device_ids=true | all-gather | bytes 204800 | tf_op jit(solution)/shard_map/all_gather | solution.py:127
  77.1 0.6 gather_fusion
  77.9 0.5 select_reduce_fusion
  78.4 0.2 fusion.11
  78.6 1.5 fusion.1
  80.2 13.7 %all_gather.14 = bf16[32,2048]{1,0:T(8,128)(2,1)S(1)} all-gather(bf16[8,2048]{1,0:T(8,128)(2,1)S(1)} %bitcast.42), channel_id=1, replica_groups=mesh['groups'=2,'pool'=4,'col'=2,'side'=2] {'pool'}, dimensions={0}, use_global_device_ids=true | all-gather | bytes 163840 | tf_op jit(solution)/shard_map/all_gather | solution.py:133
  93.8 0.6 gather_fusion.1
  94.5 5.6 %convolution_convert_fusion.3 = bf16[32,2048]{1,0:T(8,128)(2,1)} fusion(bf16[2048,2048]{1,0:T(8,128)(2,1)} %param.17, bf16[32,2048]{1,0:T(8,128)(2,1)S(1)} %gather_fusion.1, pred[32]{0:T(512)(128)(4,1)S(1)} %get-tuple-element.10), kind=kOutput, calls=%fused_computation.8 | convolution fusion | flops 268566528 | bytes 8650784 | tf_op jit(solution)/shard_map/dot_general | solution.py:137
  100.2 17.8 %reduce-scatter.6.cloned.1.call-done = bf16[8,2048]{1,0:T(8,128)(2,1)} async-done(((bf16[32,2048]{1,0:T(8,128)(2,1)}), bf16[8,2048]{1,0:T(8,128)(2,1)}) %reduce-scatter.6.cloned.1.call-update) | async-done | bytes 32784 | tf_op jit(solution)/shard_map/reduce_scatter | solution.py:136
  117.9 0.9 multiply_reduce_fusion
  118.8 11.7 %psum.29 = f32[8]{0:T(128)S(1)} all-reduce(f32[8]{0:T(128)S(1)} %multiply_reduce_fusion), channel_id=1, replica_groups=mesh['groups'=2,'pool'=4,'col'=2,'side'=2] {'pool'}, use_global_device_ids=true, to_apply=%region_8.10 | all-reduce | flops 8 | bytes 64 | tf_op jit(solution)/shard_map/psum | solution.py:142
  130.5 0.8 multiply_convert_fusion
  131.4 5.4 %all_gather.15 = bf16[32,2048]{1,0:T(8,128)(2,1)S(1)} all-gather(bf16[8,2048]{1,0:T(8,128)(2,1)S(1)} %multiply_convert_fusion), channel_id=1, replica_groups=mesh['groups'=2,'pool'=4,'col'=2,'side'=2] {'col','side'}, dimensions={0}, use_global_device_ids=true | all-gather | bytes 163840 | tf_op jit(solution)/shard_map/all_gather | solution.py:146
  136.8 8.4 %convolution_convert_fusion = bf16[32,3584]{1,0:T(8,128)(2,1)} fusion(bf16[32,2048]{1,0:T(8,128)(2,1)S(1)} %all_gather.15, bf16[2048,3584]{1,0:T(8,128)(2,1)} %param.20), kind=kOutput, calls=%fused_computation.5 | convolution fusion | flops 469876736 | bytes 15040512 | tf_op jit(solution)/shard_map/dot_general | solution.py:148
  145.2 8.4 %convolution_convert_fusion.1 = bf16[32,3584]{1,0:T(8,128)(2,1)} fusion(bf16[32,2048]{1,0:T(8,128)(2,1)S(1)} %all_gather.15, bf16[2048,3584]{1,0:T(8,128)(2,1)} %param.19), kind=kOutput, calls=%fused_computation.6 | convolution fusion | flops 469876736 | bytes 15040512 | tf_op jit(solution)/shard_map/dot_general | solution.py:147
  153.7 35.3 %all-reduce.3.cloned.1.call-done = (bf16[32,3584]{1,0:T(8,128)(2,1)}, bf16[32,3584]{1,0:T(8,128)(2,1)}) async-done(((bf16[32,3584]{1,0:T(8,128)(2,1)}, bf16[32,3584]{1,0:T(8,128)(2,1)}), (bf16[32,3584]{1,0:T(8,128)(2,1)}, bf16[32,3584]{1,0:T(8,128)(2,1)})) %all-reduce.3.cloned.1.call-update) | async-done | bytes 458768 | tf_op jit(solution)/shard_map/psum | solution.py:151
  189.1 8.7 %convolution_convert_fusion.2 = bf16[32,2048]{1,0:T(8,128)(2,1)} fusion(bf16[3584,2048]{1,0:T(8,128)(2,1)} %param.21, bf16[32,3584]{1,0:T(8,128)(2,1)} %get-tuple-element.8, bf16[32,3584]{1,0:T(8,128)(2,1)} %get-tuple-element.9), kind=kOutput, calls=%fused_computation.7 | convolution fusion | flops 470745088 | bytes 15269888 | tf_op jit(solution)/shard_map/dot_general | solution.py:156
  197.8 19.3 %reduce-scatter.8.cloned.1.call-done = bf16[8,2048]{1,0:T(8,128)(2,1)} async-done(((bf16[32,2048]{1,0:T(8,128)(2,1)}), bf16[8,2048]{1,0:T(8,128)(2,1)}) %reduce-scatter.8.cloned.1.call-update) | async-done | bytes 32784 | tf_op jit(solution)/shard_map/reduce_scatter | solution.py:155
  217.1 1.4 convert_add_fusion.1
  (56 shorter events, 1.3 us)
Async XLA Ops:
  6.5 37.0 %copy-start = (s32[32]{0:T(128)S(1)}, s32[32]{0:T(128)}, u32[]{:S(2)}) copy-start(s32[32]{0:T(128)} %param.23) | copy-start | bytes 388
  6.5 24.8 %copy-start.4 = (bf16[8,2048]{1,0:T(8,128)(2,1)S(1)}, bf16[8,2048]{1,0:T(8,128)(2,1)}, u32[]{:S(2)}) copy-start(bf16[8,2048]{1,0:T(8,128)(2,1)} %param.14) | copy-start | bytes 98308
  6.5 24.8 %copy-start.6 = (f32[2048]{0:T(1024)S(1)}, f32[2048]{0:T(1024)}, u32[]{:S(2)}) copy-start(f32[2048]{0:T(1024)} %param.15) | copy-start | bytes 24580
  6.5 55.3 %reduce-scatter.4.cloned.1.call-start = ((), (), s32[]{:S(2)}) async-start(), calls=%async_computation.3 | async-start | bytes 409600 | tf_op jit(solution)/shard_map/reduce_scatter | solution.py:120
  7.5 36.0 %copy-start.8 = (s32[32]{0:T(128)S(1)}, s32[32]{0:T(128)}, u32[]{:S(2)}) copy-start(s32[32]{0:T(128)} %param.25) | copy-start | bytes 388
  7.5 36.7 %copy-start.2 = (s32[32]{0:T(128)S(1)}, s32[32]{0:T(128)}, u32[]{:S(2)}) copy-start(s32[32]{0:T(128)} %param.24) | copy-start | bytes 388
  17.7 30.0 %copy-start.3 = (bf16[8,256,2,2,128]{4,3,2,1,0:T(2,128)(2,1)S(1)}, bf16[8,256,2,2,128]{4,3,2,1,0:T(2,128)(2,1)}, u32[]{:S(2)}) copy-start(bf16[8,256,2,2,128]{4,3,2,1,0:T(2,128)(2,1)} %param.22) | copy-start | bytes 6291460
  43.4 87.1 %copy-start.7 = (f32[2048]{0:T(1024)S(1)}, f32[2048]{0:T(1024)}, u32[]{:S(2)}) copy-start(f32[2048]{0:T(1024)} %param.18) | copy-start | bytes 24580
  43.4 74.5 %reduce-scatter.6.cloned.1.call-start = ((), (), s32[]{:S(2)}) async-start(), calls=%async_computation.4 | async-start | bytes 163840 | tf_op jit(solution)/shard_map/reduce_scatter | solution.py:136
  100.1 89.0 %all-reduce.3.cloned.1.call-start = ((), (), s32[]{:S(2)}) async-start(), calls=%async_computation.6 | async-start | bytes 917504 | tf_op jit(solution)/shard_map/psum | solution.py:151
  145.2 73.3 %copy-start.1 = (s32[32]{0:T(128)S(1)}, s32[32]{0:T(128)}, u32[]{:S(2)}) copy-start(s32[32]{0:T(128)} %param.23) | copy-start | bytes 388
  153.7 63.5 %copy-start.5 = (bf16[8,2048]{1,0:T(8,128)(2,1)S(1)}, bf16[8,2048]{1,0:T(8,128)(2,1)}, u32[]{:S(2)}) copy-start(bf16[8,2048]{1,0:T(8,128)(2,1)} %reduce-scatter.6.cloned.1.call-done) | copy-start | bytes 98308
  153.7 63.4 %reduce-scatter.8.cloned.1.call-start = ((), (), s32[]{:S(2)}) async-start(), calls=%async_computation.5 | async-start | bytes 163840 | tf_op jit(solution)/shard_map/reduce_scatter | solution.py:155
Sparse Core Ops, SparseCore 0:
  43.5 18.2 reduce-scatter.3
  100.2 17.6 reduce-scatter.5
  153.8 35.2 all-reduce.2
  197.9 19.1 reduce-scatter.7
where the time goes:
time: 226 us; the launch traced here: 225 us
  waiting for transfers between devices  84.3 us (37%)
  blocking collectives  63.2 us (28%)
  matrix products  39.9 us (18%)
  local copies, waits for them, and re-layouts  17.6 us (8%)
  between operations  13.3 us (6%)
  other arithmetic  6.69 us (3%)
    psum x1, waiting for transfers between devices, local(): lax.psum(up_part.astype(jnp.bfloat16), 'pool').astype(jnp.float32)  35.3 us
    reduce_scatter x1, waiting for transfers between devices, local(): lax.psum_scatter(jnp.dot(picked, w_down, preferred_element_type=jnp.float...  19.3 us
    reduce_scatter x1, waiting for transfers between devices, local(): lax.psum_scatter(jnp.dot(picked, w_out, preferred_element_type=jnp.float3...  17.8 us
    all_gather x1, blocking collectives, local(): gathered = lax.all_gather(attended, 'pool', axis=0, tiled=True)  13.7 us
    psum x1, blocking collectives, local(): squares = lax.psum(jnp.sum(residual * residual, axis=1), 'pool')  13.6 us
    all_gather x1, blocking collectives, local(): all_rows = lax.all_gather(rotated, 'pool', axis=0, tiled=True)  13.5 us
    reduce_scatter x1, waiting for transfers between devices, local(): lax.psum_scatter(jnp.dot(picked, local_qkv, preferred_element_type=jnp.fl...  11.8 us
    psum x1, blocking collectives, local(): squares_mid = lax.psum(jnp.sum(residual * residual, axis=1), 'pool')  11.7 us
  transfers between devices with their start and end apart: 4, of which 4 were waited for; matrix products, arithmetic and copies ran while one was open for 3% of the time, Pallas kernels for 0%

commit v1 on v0

--- a/solution.py
+++ b/solution.py
@@ -13,6 +13,7 @@
 
 epsilon = 1e-05
 rope_base = 500000.0
+CS = ("col", "side")
 
 
 def rotate(heads_in, positions):
@@ -84,6 +85,33 @@
         + own_prob.astype(jnp.float32)[..., None] * own_value.astype(jnp.float32)[:, :, None, :]
     )
     return mixture.reshape(slot_count, -1).astype(jnp.bfloat16)
+
+
+def shift_pairs(n, k):
+    return [(i, (i + k) % n) for i in range(n)]
+
+
+def gather_blocks(x, axis, n):
+    idx = lax.axis_index(axis)
+    got = [x] + [lax.ppermute(x, axis, shift_pairs(n, k)) for k in range(1, n)]
+    stacked = jnp.stack(got)
+    return jnp.take(stacked, (idx - jnp.arange(n)) % n, axis=0)
+
+
+def scatter_sum(blocks, axis, n):
+    idx = lax.axis_index(axis)
+    total = jnp.take(blocks, idx, axis=0).astype(jnp.float32)
+    for k in range(1, n):
+        piece = jnp.take(blocks, (idx + k) % n, axis=0)
+        total = total + lax.ppermute(piece, axis, shift_pairs(n, k)).astype(jnp.float32)
+    return total
+
+
+def all_sum(x, axis, n):
+    total = x
+    for k in range(1, n):
+        total = total + lax.ppermute(x, axis, shift_pairs(n, k))
+    return total
 
 
 def local(
@@ -100,64 +128,56 @@
     request_slot,
     row_request,
 ):
+    n_pool = lax.axis_size("pool")
+    n_cs = lax.axis_size(CS)
     pool_index = lax.axis_index("pool")
     per_owner = kv_cache.shape[0]
     per_group = H // KVH
+    rows_here = tokens.shape[0]
+    rows_total = rows_here * n_cs
     my_start = pool_index * per_owner
     slot_of_row = jnp.take(request_slot, row_request)
-    row_of_slot = jnp.argsort(slot_of_row)
+    row_of_slot = jnp.zeros_like(slot_of_row).at[slot_of_row].set(
+        jnp.arange(rows_total, dtype=slot_of_row.dtype)
+    )
     length_of_row = jnp.take(lengths, row_request)
     length_of_slot = jnp.take(length_of_row, row_of_slot)
+
     residual = tokens.astype(jnp.float32)
-    squares = lax.psum(jnp.sum(residual * residual, axis=1), "pool")
+    squares = all_sum(jnp.sum(residual * residual, axis=1), "pool", n_pool)
     normed = (residual * lax.rsqrt(squares / D + epsilon)[:, None] * attn_gain[None, :]).astype(
         jnp.bfloat16
     )
-    normed_all = lax.all_gather(normed, ("col", "side"), axis=0, tiled=True)
-    local_qkv = w_qkv.reshape(w_qkv.shape[0], -1)
-    positions = lax.dynamic_slice_in_dim(length_of_row, my_start, per_owner, 0)
-    picked = normed_all
-    summed = lax.psum_scatter(
-        jnp.dot(picked, local_qkv, preferred_element_type=jnp.float32),
-        "pool",
-        scatter_dimension=0,
-        tiled=True,
-    )
+    normed_all = gather_blocks(normed, CS, n_cs).reshape(rows_total, -1)
+    by_slot = jnp.take(normed_all, row_of_slot, axis=0)
+    qkv_part = jnp.dot(by_slot, w_qkv.reshape(w_qkv.shape[0], -1), preferred_element_type=jnp.float32)
+    summed = scatter_sum(qkv_part.reshape(n_pool, per_owner, -1), "pool", n_pool)
+    positions = lax.dynamic_slice_in_dim(length_of_slot, my_start, per_owner, 0)
     rotated = rope_rows(summed, positions, per_group, HD)
-    all_rows = lax.all_gather(rotated, "pool", axis=0, tiled=True)
-    own_rows = jnp.take(
-        all_rows, lax.dynamic_slice_in_dim(row_of_slot, my_start, per_owner, 0), axis=0
-    )
-    seen_count = lax.dynamic_slice_in_dim(length_of_slot, my_start, per_owner, 0)
-    attended = attend(own_rows, kv_cache, seen_count, per_group, HD)
-    gathered = lax.all_gather(attended, "pool", axis=0, tiled=True)
+    attended = attend(rotated, kv_cache, positions, per_group, HD)
+    gathered = gather_blocks(attended, "pool", n_pool).reshape(rows_total, -1)
     by_row = jnp.take(gathered, slot_of_row, axis=0)
-    picked = by_row
-    residual = residual + lax.psum_scatter(
-        jnp.dot(picked, w_out, preferred_element_type=jnp.float32).astype(jnp.bfloat16),
-        ("col", "side"),
-        scatter_dimension=0,
-        tiled=True,
-    ).astype(jnp.float32)
-    squares_mid = lax.psum(jnp.sum(residual * residual, axis=1), "pool")
+    out_part = jnp.dot(by_row, w_out, preferred_element_type=jnp.float32)
+    residual = residual + scatter_sum(out_part.reshape(n_cs, rows_here, -1), CS, n_cs)
+
+    squares_mid = all_sum(jnp.sum(residual * residual, axis=1), "pool", n_pool)
     ffn_normed = (
         residual * lax.rsqrt(squares_mid / D + epsilon)[:, None] * ffn_gain[None, :]
     ).astype(jnp.bfloat16)
-    ffn_all = lax.all_gather(ffn_normed, ("col", "side"), axis=0, tiled=True)
-    gate_part = jnp.dot(ffn_all, w_gate, preferred_element_type=jnp.float32)
-    up_part = jnp.dot(ffn_all, w_up, preferred_element_type=jnp.float32)
-    gate_total, up_total = (
-        lax.psum(gate_part.astype(jnp.bfloat16), "pool").astype(jnp.float32),
-        lax.psum(up_part.astype(jnp.bfloat16), "pool").astype(jnp.float32),
-    )
-    hidden_all = (jax.nn.silu(gate_total) * up_total).astype(jnp.bfloat16)
-    picked = hidden_all
-    return residual + lax.psum_scatter(
-        jnp.dot(picked, w_down, preferred_element_type=jnp.float32).astype(jnp.bfloat16),
-        ("col", "side"),
-        scatter_dimension=0,
-        tiled=True,
-    ).astype(jnp.float32)
+    ffn_all = gather_blocks(ffn_normed, CS, n_cs).reshape(rows_total, -1)
+    gate_part = jnp.dot(ffn_all, w_gate, preferred_element_type=jnp.float32).astype(jnp.bfloat16)
+    up_part = jnp.dot(ffn_all, w_up, preferred_element_type=jnp.float32).astype(jnp.bfloat16)
+    hidden_cols = w_gate.shape[1]
+    chunk = hidden_cols // n_pool
+    gate_blocks = gate_part.reshape(rows_total, n_pool, chunk).transpose(1, 0, 2)
+    up_blocks = up_part.reshape(rows_total, n_pool, chunk).transpose(1, 0, 2)
+    both = scatter_sum(jnp.concatenate([gate_blocks, up_blocks], axis=2), "pool", n_pool)
+    gate_total = both[:, :chunk]
+    up_total = both[:, chunk:]
+    hidden = (jax.nn.silu(gate_total) * up_total).astype(jnp.bfloat16)
+    hidden_all = gather_blocks(hidden, "pool", n_pool).transpose(1, 0, 2).reshape(rows_total, -1)
+    down_part = jnp.dot(hidden_all, w_down, preferred_element_type=jnp.float32)
+    return residual + scatter_sum(down_part.reshape(n_cs, rows_here, -1), CS, n_cs)
 
 
 def solution(mesh):

time: 226 us -> 147 us (0.65)
  blocking collectives: 63.2 us -> 0 us
  waiting for transfers between devices: 84.3 us -> 30.6 us
  starting transfers between devices: 0.13 us -> 40.9 us
  local copies, waits for them, and re-layouts: 17.6 us -> 32.8 us
  between operations: 13.3 us -> 0.42 us
  matrix products: 39.9 us -> 35.2 us
    reduce_scatter x3 -> x0, waiting for transfers between devices: 48.8 us -> none  [the longest x1 19.3 us: local(): lax.psum_scatter(jnp.dot(picked, w_down, preferred_element_type=jnp.float...]
    ppermute x0 -> x30, starting transfers between devices: none -> 40.9 us  [the longest x12 15.5 us: gather_blocks(): got = [x] + [lax.ppermute(x, axis, shift_pairs(n, k)) for k in range(1, n)]]
    all_gather x4 -> x0, blocking collectives: 37.9 us -> none  [the longest x1 13.7 us: local(): gathered = lax.all_gather(attended, 'pool', axis=0, tiled=True)]
    psum x1 -> x0, waiting for transfers between devices: 35.3 us -> none  [local(): lax.psum(up_part.astype(jnp.bfloat16), 'pool').astype(jnp.float32)]
    ppermute x0 -> x30, waiting for transfers between devices: none -> 30.6 us  [the longest x12 18.8 us: scatter_sum(): lax.ppermute(piece, axis, shift_pairs(n, k)).astype(jnp.float32)]
    psum x2 -> x0, blocking collectives: 25.2 us -> none  [the longest x1 13.6 us: local(): squares = lax.psum(jnp.sum(residual * residual, axis=1), 'pool')]
    reshape x0 -> x3, local copies, waits for them, and re-layouts: none -> 23.3 us  [the longest x1 23.2 us: local(): w_qkv.reshape(w_qkv.shape[0], -1)]
    unnamed x20 -> x15, local copies, waits for them, and re-layouts: 10.3 us -> 0.05 us
  transfers between devices with their start and end apart: 4 -> 30, of which waited for: 4 -> 24; matrix products, arithmetic and copies ran while one was open for 3% -> 22% of each run, Pallas kernels for 0% -> 0%
where the time goes in v1:
time: 147 us; the launch traced here: 145 us
  starting transfers between devices  40.9 us (28%)
  matrix products  35.2 us (24%)
  local copies, waits for them, and re-layouts  32.8 us (22%)
  waiting for transfers between devices  30.6 us (21%)
  other arithmetic  5.6 us (4%)
    reshape x1, local copies, waits for them, and re-layouts, local(): w_qkv.reshape(w_qkv.shape[0], -1)  23.2 us
    ppermute x12, waiting for transfers between devices, scatter_sum(): lax.ppermute(piece, axis, shift_pairs(n, k)).astype(jnp.float32)  18.8 us
    ppermute x12, starting transfers between devices, gather_blocks(): got = [x] + [lax.ppermute(x, axis, shift_pairs(n, k)) for k in range(1, n)]  15.5 us
    ppermute x12, starting transfers between devices, scatter_sum(): lax.ppermute(piece, axis, shift_pairs(n, k)).astype(jnp.float32)  13.8 us
    ppermute x6, starting transfers between devices, all_sum(): total = total + lax.ppermute(x, axis, shift_pairs(n, k))  11.6 us
    ppermute x12, waiting for transfers between devices, gather_blocks(): got = [x] + [lax.ppermute(x, axis, shift_pairs(n, k)) for k in range(1, n)]  9.32 us
    dot_general x1, matrix products, local(): jnp.dot(ffn_all, w_gate, preferred_element_type=jnp.float32)  7.85 us
    dot_general x1, matrix products, local(): jnp.dot(ffn_all, w_up, preferred_element_type=jnp.float32)  7.85 us
  transfers between devices with their start and end apart: 30, of which 24 were waited for; matrix products, arithmetic and copies ran while one was open for 22% of the time, Pallas kernels for 0%

profile of v1, /device:TPU:0, one launch (start us, length us, event | category | flops | bytes accessed | tf_op | source)
XLA Modules:
  0.0 145.5 jit_solution(5454543770525688006)
XLA Ops:
  1.1 3.1 %collective-permute-start = (f32[8]{0:T(128)S(1)}, f32[8]{0:T(128)S(1)}, u32[]{:S(2)}, u32[]{:S(2)}) collective-permute-start(f32[8]{0:T(128)S(1)} %fusion.27), channel_id=1, source_target_pairs={{0,4},{4,8},{8,12},{12,0},{1,5},{5,9},{9,13},{13,1},{2,6},{6,10},{... | collective-permute-start | bytes 104 | tf_op jit(solution)/shard_map/ppermute | solution.py:113
  4.1 2.6 %collective-permute-start.1 = (f32[8]{0:T(128)S(1)}, f32[8]{0:T(128)S(1)}, u32[]{:S(2)}, u32[]{:S(2)}) collective-permute-start(f32[8]{0:T(128)S(1)} %fusion.27), channel_id=1, source_target_pairs={{0,8},{4,12},{8,0},{12,4},{1,9},{5,13},{9,1},{13,5},{2,10},{6,14},... | collective-permute-start | bytes 104 | tf_op jit(solution)/shard_map/ppermute | solution.py:113
  10.9 1.4 gather_fusion.1
  13.6 23.2 %reshape.596 = bf16[2048,2560,1]{1,0,2:T(8,128)(2,1)} reshape(bf16[2048,2,1280]{2,1,0:T(2,128)(2,1)} %param.26) | data formatting | bytes 20971520 | tf_op jit(solution)/shard_map/reshape | solution.py:153
  37.0 2.2 %fusion.61 = (bf16[8,256,1,2,128]{4,3,2,1,0:T(2,128)(2,1)S(1)}, bf16[8,256,1,2,128]{4,3,2,1,0:T(2,128)(2,1)}) fusion(bf16[8,256,2,2,128]{4,3,2,1,0:T(2,128)(2,1)S(1)} %copy-done.2), kind=kLoop, calls=%fused_computation.161 | loop fusion | bytes 4194304 | tf_op jit(solution)/shard_map/slice | solution.py:56
  39.5 1.6 %collective-permute-start.4 = (bf16[8,2048]{1,0:T(8,128)(2,1)S(1)}, bf16[8,2048]{1,0:T(8,128)(2,1)S(1)}, u32[]{:S(2)}, u32[]{:S(2)}) collective-permute-start(bf16[8,2048]{1,0:T(8,128)(2,1)S(1)} %fusion.29), channel_id=1, source_target_pairs={{0,2},{1,3},{2,0},{3,1},{4,6},{5,7},{6,4},{7,5},{8,10},{9,11},{10,... | collective-permute-start | bytes 98312 | tf_op jit(solution)/shard_map/ppermute | solution.py:96
  41.1 1.4 collective-permute-start.5
  45.4 5.9 %fusion.5 = f32[4,8,2560]{2,1,0:T(8,128)S(1)} fusion(bf16[2048,2560,1]{1,0,2:T(8,128)(2,1)} %reshape.596, bf16[32,2048]{1,0:T(8,128)(2,1)S(1)} %gather_fusion.5, pred[32]{0:T(512)(128)(4,1)S(1)} %get-tuple-element.51), kind=kOutput, calls=%fused_computation.38 | convolution fusion | flops 335609856 | bytes 10944544 | tf_op jit(solution)/shard_map/dot_general | solution.py:153
  52.4 2.8 %collective-permute-start.8 = (f32[8,2560]{1,0:T(8,128)S(1)}, f32[8,2560]{1,0:T(8,128)S(1)}, u32[]{:S(2)}, u32[]{:S(2)}) collective-permute-start(f32[8,2560]{1,0:T(8,128)S(1)} %get-tuple-element.58), channel_id=1, source_target_pairs={{0,12},{4,0},{8,4},{12,8},{1,13},{5,1},{9,5},{13,9},{2,14},{6,2},{... | collective-permute-start | bytes 245768 | tf_op jit(solution)/shard_map/ppermute | solution.py:106
  55.2 3.4 %collective-permute-done.6 = f32[8,2560]{1,0:T(8,128)S(1)} collective-permute-done((f32[8,2560]{1,0:T(8,128)S(1)}, f32[8,2560]{1,0:T(8,128)S(1)}, u32[]{:S(2)}, u32[]{:S(2)}) %collective-permute-start.6) | collective-permute-done | bytes 81952 | tf_op jit(solution)/shard_map/ppermute | solution.py:106
  58.6 3.1 %collective-permute-done.7 = f32[8,2560]{1,0:T(8,128)S(1)} collective-permute-done((f32[8,2560]{1,0:T(8,128)S(1)}, f32[8,2560]{1,0:T(8,128)S(1)}, u32[]{:S(2)}, u32[]{:S(2)}) %collective-permute-start.7) | collective-permute-done | bytes 81952 | tf_op jit(solution)/shard_map/ppermute | solution.py:106
  63.2 1.8 %collective-permute-start.9 = (bf16[8,2048]{1,0:T(8,128)(2,1)S(1)}, bf16[8,2048]{1,0:T(8,128)(2,1)S(1)}, u32[]{:S(2)}, u32[]{:S(2)}) collective-permute-start(bf16[8,2048]{1,0:T(8,128)(2,1)S(1)} %bitcast.154), channel_id=1, source_target_pairs={{0,4},{4,8},{8,12},{12,0},{1,5},{5,9},{9,13},{13,1},{2,6},{6,10},{... | collective-permute-start | bytes 98312 | tf_op jit(solution)/shard_map/ppermute | solution.py:96
  67.5 1.5 %collective-permute-done.9 = bf16[8,2048]{1,0:T(8,128)(2,1)S(1)} collective-permute-done((bf16[8,2048]{1,0:T(8,128)(2,1)S(1)}, bf16[8,2048]{1,0:T(8,128)(2,1)S(1)}, u32[]{:S(2)}, u32[]{:S(2)}) %collective-permute-start.9) | collective-permute-done | bytes 32800 | tf_op jit(solution)/shard_map/ppermute | solution.py:96
  71.6 5.0 %convolution_bitcast_fusion = f32[4,8,2048]{2,1,0:T(8,128)S(1)} fusion(bf16[2048,2048]{1,0:T(8,128)(2,1)} %param.27, bf16[32,2048]{1,0:T(8,128)(2,1)S(1)} %gather_fusion.7, pred[32]{0:T(512)(128)(4,1)S(1)} %get-tuple-element.46), kind=kOutput, calls=%fused_computation.14 | convolution fusion | flops 268500992 | bytes 8781856 | tf_op jit(solution)/shard_map/dot_general | solution.py:160
  76.7 1.5 %collective-permute-start.13 = (f32[8,2048]{1,0:T(8,128)S(1)}, f32[8,2048]{1,0:T(8,128)S(1)}, u32[]{:S(2)}, u32[]{:S(2)}) collective-permute-start(f32[8,2048]{1,0:T(8,128)S(1)} %get-tuple-element.65), channel_id=1, source_target_pairs={{0,2},{1,3},{2,0},{3,1},{4,6},{5,7},{6,4},{7,5},{8,10},{9,11},{10,... | collective-permute-start | bytes 196616 | tf_op jit(solution)/shard_map/ppermute | solution.py:106
  78.2 1.4 collective-permute-start.14
  81.6 1.5 %collective-permute-start.15 = (f32[8]{0:T(128)S(1)}, f32[8]{0:T(128)S(1)}, u32[]{:S(2)}, u32[]{:S(2)}) collective-permute-start(f32[8]{0:T(128)S(1)} %get-tuple-element.44), channel_id=1, source_target_pairs={{0,4},{4,8},{8,12},{12,0},{1,5},{5,9},{9,13},{13,1},{2,6},{6,10},{... | collective-permute-start | bytes 104 | tf_op jit(solution)/shard_map/ppermute | solution.py:113
  83.1 2.0 %collective-permute-start.16 = (f32[8]{0:T(128)S(1)}, f32[8]{0:T(128)S(1)}, u32[]{:S(2)}, u32[]{:S(2)}) collective-permute-start(f32[8]{0:T(128)S(1)} %get-tuple-element.44), channel_id=1, source_target_pairs={{0,8},{4,12},{8,0},{12,4},{1,9},{5,13},{9,1},{13,5},{2,10},{6,14},... | collective-permute-start | bytes 104 | tf_op jit(solution)/shard_map/ppermute | solution.py:113
  88.8 1.7 %collective-permute-start.19 = (bf16[8,2048]{1,0:T(8,128)(2,1)S(1)}, bf16[8,2048]{1,0:T(8,128)(2,1)S(1)}, u32[]{:S(2)}, u32[]{:S(2)}) collective-permute-start(bf16[8,2048]{1,0:T(8,128)(2,1)S(1)} %multiply_convert_fusion), channel_id=1, source_target_pairs={{0,2},{1,3},{2,0},{3,1},{4,6},{5,7},{6,4},{7,5},{8,10},{9,11},{10,... | collective-permute-start | bytes 98312 | tf_op jit(solution)/shard_map/ppermute | solution.py:96
  90.5 1.4 collective-permute-start.20
  94.1 7.9 %convolution_convert_fusion = bf16[32,3584]{1,0:T(8,128)(2,1)S(1)} fusion(bf16[2048,3584]{1,0:T(8,128)(2,1)} %param.30, bf16[4,8,2048]{2,1,0:T(8,128)(2,1)S(1)} %gather_fusion.8, pred[4]{0:T(512)(128)(4,1)S(1)} %get-tuple-element.77), kind=kOutput, calls=%fused_computation.12 | convolution fusion | flops 469942272 | bytes 15040516 | tf_op jit(solution)/shard_map/dot_general | solution.py:169
  102.0 7.9 %convolution_convert_fusion.1 = bf16[32,3584]{1,0:T(8,128)(2,1)S(1)} fusion(bf16[2048,3584]{1,0:T(8,128)(2,1)} %param.29, bf16[4,8,2048]{2,1,0:T(8,128)(2,1)S(1)} %gather_fusion.8, pred[4]{0:T(512)(128)(4,1)S(1)} %get-tuple-element.77), kind=kOutput, calls=%fused_computation.13 | convolution fusion | flops 469942272 | bytes 15040516 | tf_op jit(solution)/shard_map/dot_general | solution.py:168
  110.9 2.5 %collective-permute-start.22 = (bf16[32,1792]{1,0:T(8,128)(2,1)S(1)}, bf16[32,1792]{1,0:T(8,128)(2,1)S(1)}, u32[]{:S(2)}, u32[]{:S(2)}) collective-permute-start(bf16[32,1792]{1,0:T(8,128)(2,1)S(1)} %get-tuple-element.55), channel_id=1, source_target_pairs={{0,8},{4,12},{8,0},{12,4},{1,9},{5,13},{9,1},{13,5},{2,10},{6,14},... | collective-permute-start | bytes 344072 | tf_op jit(solution)/shard_map/ppermute | solution.py:106
  113.9 4.0 %collective-permute-done.21 = bf16[32,1792]{1,0:T(8,128)(2,1)S(1)} collective-permute-done((bf16[32,1792]{1,0:T(8,128)(2,1)S(1)}, bf16[32,1792]{1,0:T(8,128)(2,1)S(1)}, u32[]{:S(2)}, u32[]{:S(2)}) %collective-permute-start.21) | collective-permute-done | bytes 114720 | tf_op jit(solution)/shard_map/ppermute | solution.py:106
  117.9 4.5 %collective-permute-done.22 = bf16[32,1792]{1,0:T(8,128)(2,1)S(1)} collective-permute-done((bf16[32,1792]{1,0:T(8,128)(2,1)S(1)}, bf16[32,1792]{1,0:T(8,128)(2,1)S(1)}, u32[]{:S(2)}, u32[]{:S(2)}) %collective-permute-start.22) | collective-permute-done | bytes 114720 | tf_op jit(solution)/shard_map/ppermute | solution.py:106
  122.5 2.7 %collective-permute-start.24 = (bf16[32,896]{1,0:T(8,128)(2,1)S(1)}, bf16[32,896]{1,0:T(8,128)(2,1)S(1)}, u32[]{:S(2)}, u32[]{:S(2)}) collective-permute-start(bf16[32,896]{1,0:T(8,128)(2,1)S(1)} %fusion.23), channel_id=1, source_target_pairs={{0,4},{4,8},{8,12},{12,0},{1,5},{5,9},{9,13},{13,1},{2,6},{6,10},{... | collective-permute-start | bytes 172040 | tf_op jit(solution)/shard_map/ppermute | solution.py:96
  125.7 2.0 %collective-permute-start.26 = (bf16[32,896]{1,0:T(8,128)(2,1)S(1)}, bf16[32,896]{1,0:T(8,128)(2,1)S(1)}, u32[]{:S(2)}, u32[]{:S(2)}) collective-permute-start(bf16[32,896]{1,0:T(8,128)(2,1)S(1)} %fusion.23), channel_id=1, source_target_pairs={{0,12},{4,0},{8,4},{12,8},{1,13},{5,1},{9,5},{13,9},{2,14},{6,2},{... | collective-permute-start | bytes 172040 | tf_op jit(solution)/shard_map/ppermute | solution.py:96
  127.7 1.4 collective-permute-done.24
  129.1 2.1 %collective-permute-done.25 = bf16[32,896]{1,0:T(8,128)(2,1)S(1)} collective-permute-done((bf16[32,896]{1,0:T(8,128)(2,1)S(1)}, bf16[32,896]{1,0:T(8,128)(2,1)S(1)}, u32[]{:S(2)}, u32[]{:S(2)}) %collective-permute-start.25) | collective-permute-done | bytes 57376 | tf_op jit(solution)/shard_map/ppermute | solution.py:96
  132.1 7.7 %fusion = f32[4,8,2048]{2,1,0:T(8,128)S(1)} fusion(bf16[4,8,3584]{2,1,0:T(8,128)(2,1)S(1)} %dot_general.36, bf16[3584,2048]{1,0:T(8,128)(2,1)} %param.31), kind=kOutput, calls=%fused_computation.10 | convolution fusion | flops 469762048 | bytes 15171584 | tf_op jit(solution)/shard_map/dot_general | solution.py:179
  139.9 1.6 %collective-permute-start.28 = (f32[8,2048]{1,0:T(8,128)S(1)}, f32[8,2048]{1,0:T(8,128)S(1)}, u32[]{:S(2)}, u32[]{:S(2)}) collective-permute-start(f32[8,2048]{1,0:T(8,128)S(1)} %get-tuple-element.62), channel_id=1, source_target_pairs={{0,2},{1,3},{2,0},{3,1},{4,6},{5,7},{6,4},{7,5},{8,10},{9,11},{10,... | collective-permute-start | bytes 196616 | tf_op jit(solution)/shard_map/ppermute | solution.py:106
  141.5 1.4 collective-permute-start.29
  (121 shorter events, 31.1 us)
Async XLA Ops:
  0.0 39.4 %copy-start.5 = (f32[2048]{0:T(1024)S(1)}, f32[2048]{0:T(1024)}, u32[]{:S(2)}) copy-start(f32[2048]{0:T(1024)} %param.25) | copy-start | bytes 24580
  1.1 38.3 %collective-permute-start = (f32[8]{0:T(128)S(1)}, f32[8]{0:T(128)S(1)}, u32[]{:S(2)}, u32[]{:S(2)}) collective-permute-start(f32[8]{0:T(128)S(1)} %fusion.27), channel_id=1, source_target_pairs={{0,4},{4,8},{8,12},{12,0},{1,5},{5,9},{9,13},{13,1},{2,6},{6,10},{... | collective-permute-start | bytes 104 | tf_op jit(solution)/shard_map/ppermute | solution.py:113
  4.1 35.2 %collective-permute-start.1 = (f32[8]{0:T(128)S(1)}, f32[8]{0:T(128)S(1)}, u32[]{:S(2)}, u32[]{:S(2)}) collective-permute-start(f32[8]{0:T(128)S(1)} %fusion.27), channel_id=1, source_target_pairs={{0,8},{4,12},{8,0},{12,4},{1,9},{5,13},{9,1},{13,5},{2,10},{6,14},... | collective-permute-start | bytes 104 | tf_op jit(solution)/shard_map/ppermute | solution.py:113
  6.7 32.7 %collective-permute-start.2 = (f32[8]{0:T(128)S(1)}, f32[8]{0:T(128)S(1)}, u32[]{:S(2)}, u32[]{:S(2)}) collective-permute-start(f32[8]{0:T(128)S(1)} %fusion.27), channel_id=1, source_target_pairs={{0,12},{4,0},{8,4},{12,8},{1,13},{5,1},{9,5},{13,9},{2,14},{6,2},{... | collective-permute-start | bytes 104 | tf_op jit(solution)/shard_map/ppermute | solution.py:113
  39.5 3.4 %collective-permute-start.3 = (bf16[8,2048]{1,0:T(8,128)(2,1)S(1)}, bf16[8,2048]{1,0:T(8,128)(2,1)S(1)}, u32[]{:S(2)}, u32[]{:S(2)}) collective-permute-start(bf16[8,2048]{1,0:T(8,128)(2,1)S(1)} %fusion.29), channel_id=1, source_target_pairs={{0,1},{1,2},{2,3},{3,0},{4,5},{5,6},{6,7},{7,4},{8,9},{9,10},{10,1... | collective-permute-start | bytes 98312 | tf_op jit(solution)/shard_map/ppermute | solution.py:96
  39.5 4.0 %collective-permute-start.4 = (bf16[8,2048]{1,0:T(8,128)(2,1)S(1)}, bf16[8,2048]{1,0:T(8,128)(2,1)S(1)}, u32[]{:S(2)}, u32[]{:S(2)}) collective-permute-start(bf16[8,2048]{1,0:T(8,128)(2,1)S(1)} %fusion.29), channel_id=1, source_target_pairs={{0,2},{1,3},{2,0},{3,1},{4,6},{5,7},{6,4},{7,5},{8,10},{9,11},{10,... | collective-permute-start | bytes 98312 | tf_op jit(solution)/shard_map/ppermute | solution.py:96
  41.1 3.0 %collective-permute-start.5 = (bf16[8,2048]{1,0:T(8,128)(2,1)S(1)}, bf16[8,2048]{1,0:T(8,128)(2,1)S(1)}, u32[]{:S(2)}, u32[]{:S(2)}) collective-permute-start(bf16[8,2048]{1,0:T(8,128)(2,1)S(1)} %fusion.29), channel_id=1, source_target_pairs={{0,3},{1,0},{2,1},{3,2},{4,7},{5,4},{6,5},{7,6},{8,11},{9,8},{10,9... | collective-permute-start | bytes 98312 | tf_op jit(solution)/shard_map/ppermute | solution.py:96
  51.3 7.3 %collective-permute-start.6 = (f32[8,2560]{1,0:T(8,128)S(1)}, f32[8,2560]{1,0:T(8,128)S(1)}, u32[]{:S(2)}, u32[]{:S(2)}) collective-permute-start(f32[8,2560]{1,0:T(8,128)S(1)} %get-tuple-element.57), channel_id=1, source_target_pairs={{0,4},{4,8},{8,12},{12,0},{1,5},{5,9},{9,13},{13,1},{2,6},{6,10},{... | collective-permute-start | bytes 245768 | tf_op jit(solution)/shard_map/ppermute | solution.py:106
  52.1 9.7 %collective-permute-start.7 = (f32[8,2560]{1,0:T(8,128)S(1)}, f32[8,2560]{1,0:T(8,128)S(1)}, u32[]{:S(2)}, u32[]{:S(2)}) collective-permute-start(f32[8,2560]{1,0:T(8,128)S(1)} %get-tuple-element.59), channel_id=1, source_target_pairs={{0,8},{4,12},{8,0},{12,4},{1,9},{5,13},{9,1},{13,5},{2,10},{6,14},... | collective-permute-start | bytes 245768 | tf_op jit(solution)/shard_map/ppermute | solution.py:106
  52.4 9.3 %collective-permute-start.8 = (f32[8,2560]{1,0:T(8,128)S(1)}, f32[8,2560]{1,0:T(8,128)S(1)}, u32[]{:S(2)}, u32[]{:S(2)}) collective-permute-start(f32[8,2560]{1,0:T(8,128)S(1)} %get-tuple-element.58), channel_id=1, source_target_pairs={{0,12},{4,0},{8,4},{12,8},{1,13},{5,1},{9,5},{13,9},{2,14},{6,2},{... | collective-permute-start | bytes 245768 | tf_op jit(solution)/shard_map/ppermute | solution.py:106
  63.2 5.8 %collective-permute-start.9 = (bf16[8,2048]{1,0:T(8,128)(2,1)S(1)}, bf16[8,2048]{1,0:T(8,128)(2,1)S(1)}, u32[]{:S(2)}, u32[]{:S(2)}) collective-permute-start(bf16[8,2048]{1,0:T(8,128)(2,1)S(1)} %bitcast.154), channel_id=1, source_target_pairs={{0,4},{4,8},{8,12},{12,0},{1,5},{5,9},{9,13},{13,1},{2,6},{6,10},{... | collective-permute-start | bytes 98312 | tf_op jit(solution)/shard_map/ppermute | solution.py:96
  65.0 4.9 %collective-permute-start.10 = (bf16[8,2048]{1,0:T(8,128)(2,1)S(1)}, bf16[8,2048]{1,0:T(8,128)(2,1)S(1)}, u32[]{:S(2)}, u32[]{:S(2)}) collective-permute-start(bf16[8,2048]{1,0:T(8,128)(2,1)S(1)} %bitcast.155), channel_id=1, source_target_pairs={{0,8},{4,12},{8,0},{12,4},{1,9},{5,13},{9,1},{13,5},{2,10},{6,14},... | collective-permute-start | bytes 98312 | tf_op jit(solution)/shard_map/ppermute | solution.py:96
  66.1 4.1 %collective-permute-start.11 = (bf16[8,2048]{1,0:T(8,128)(2,1)S(1)}, bf16[8,2048]{1,0:T(8,128)(2,1)S(1)}, u32[]{:S(2)}, u32[]{:S(2)}) collective-permute-start(bf16[8,2048]{1,0:T(8,128)(2,1)S(1)} %bitcast.156), channel_id=1, source_target_pairs={{0,12},{4,0},{8,4},{12,8},{1,13},{5,1},{9,5},{13,9},{2,14},{6,2},{... | collective-permute-start | bytes 98312 | tf_op jit(solution)/shard_map/ppermute | solution.py:96
  76.6 3.8 %collective-permute-start.12 = (f32[8,2048]{1,0:T(8,128)S(1)}, f32[8,2048]{1,0:T(8,128)S(1)}, u32[]{:S(2)}, u32[]{:S(2)}) collective-permute-start(f32[8,2048]{1,0:T(8,128)S(1)} %get-tuple-element.63), channel_id=1, source_target_pairs={{0,1},{1,2},{2,3},{3,0},{4,5},{5,6},{6,7},{7,4},{8,9},{9,10},{10,1... | collective-permute-start | bytes 196616 | tf_op jit(solution)/shard_map/ppermute | solution.py:106
  76.7 4.7 %collective-permute-start.13 = (f32[8,2048]{1,0:T(8,128)S(1)}, f32[8,2048]{1,0:T(8,128)S(1)}, u32[]{:S(2)}, u32[]{:S(2)}) collective-permute-start(f32[8,2048]{1,0:T(8,128)S(1)} %get-tuple-element.65), channel_id=1, source_target_pairs={{0,2},{1,3},{2,0},{3,1},{4,6},{5,7},{6,4},{7,5},{8,10},{9,11},{10,... | collective-permute-start | bytes 196616 | tf_op jit(solution)/shard_map/ppermute | solution.py:106
  78.2 3.3 %collective-permute-start.14 = (f32[8,2048]{1,0:T(8,128)S(1)}, f32[8,2048]{1,0:T(8,128)S(1)}, u32[]{:S(2)}, u32[]{:S(2)}) collective-permute-start(f32[8,2048]{1,0:T(8,128)S(1)} %get-tuple-element.64), channel_id=1, source_target_pairs={{0,3},{1,0},{2,1},{3,2},{4,7},{5,4},{6,5},{7,6},{8,11},{9,8},{10,9... | collective-permute-start | bytes 196616 | tf_op jit(solution)/shard_map/ppermute | solution.py:106
  81.6 5.4 %collective-permute-start.15 = (f32[8]{0:T(128)S(1)}, f32[8]{0:T(128)S(1)}, u32[]{:S(2)}, u32[]{:S(2)}) collective-permute-start(f32[8]{0:T(128)S(1)} %get-tuple-element.44), channel_id=1, source_target_pairs={{0,4},{4,8},{8,12},{12,0},{1,5},{5,9},{9,13},{13,1},{2,6},{6,10},{... | collective-permute-start | bytes 104 | tf_op jit(solution)/shard_map/ppermute | solution.py:113
  83.1 4.4 %collective-permute-start.16 = (f32[8]{0:T(128)S(1)}, f32[8]{0:T(128)S(1)}, u32[]{:S(2)}, u32[]{:S(2)}) collective-permute-start(f32[8]{0:T(128)S(1)} %get-tuple-element.44), channel_id=1, source_target_pairs={{0,8},{4,12},{8,0},{12,4},{1,9},{5,13},{9,1},{13,5},{2,10},{6,14},... | collective-permute-start | bytes 104 | tf_op jit(solution)/shard_map/ppermute | solution.py:113
  85.2 3.5 %collective-permute-start.17 = (f32[8]{0:T(128)S(1)}, f32[8]{0:T(128)S(1)}, u32[]{:S(2)}, u32[]{:S(2)}) collective-permute-start(f32[8]{0:T(128)S(1)} %get-tuple-element.44), channel_id=1, source_target_pairs={{0,12},{4,0},{8,4},{12,8},{1,13},{5,1},{9,5},{13,9},{2,14},{6,2},{... | collective-permute-start | bytes 104 | tf_op jit(solution)/shard_map/ppermute | solution.py:113
  88.8 3.4 %collective-permute-start.18 = (bf16[8,2048]{1,0:T(8,128)(2,1)S(1)}, bf16[8,2048]{1,0:T(8,128)(2,1)S(1)}, u32[]{:S(2)}, u32[]{:S(2)}) collective-permute-start(bf16[8,2048]{1,0:T(8,128)(2,1)S(1)} %multiply_convert_fusion), channel_id=1, source_target_pairs={{0,1},{1,2},{2,3},{3,0},{4,5},{5,6},{6,7},{7,4},{8,9},{9,10},{10,1... | collective-permute-start | bytes 98312 | tf_op jit(solution)/shard_map/ppermute | solution.py:96
  88.8 4.0 %collective-permute-start.19 = (bf16[8,2048]{1,0:T(8,128)(2,1)S(1)}, bf16[8,2048]{1,0:T(8,128)(2,1)S(1)}, u32[]{:S(2)}, u32[]{:S(2)}) collective-permute-start(bf16[8,2048]{1,0:T(8,128)(2,1)S(1)} %multiply_convert_fusion), channel_id=1, source_target_pairs={{0,2},{1,3},{2,0},{3,1},{4,6},{5,7},{6,4},{7,5},{8,10},{9,11},{10,... | collective-permute-start | bytes 98312 | tf_op jit(solution)/shard_map/ppermute | solution.py:96
  90.5 3.0 %collective-permute-start.20 = (bf16[8,2048]{1,0:T(8,128)(2,1)S(1)}, bf16[8,2048]{1,0:T(8,128)(2,1)S(1)}, u32[]{:S(2)}, u32[]{:S(2)}) collective-permute-start(bf16[8,2048]{1,0:T(8,128)(2,1)S(1)} %multiply_convert_fusion), channel_id=1, source_target_pairs={{0,3},{1,0},{2,1},{3,2},{4,7},{5,4},{6,5},{7,6},{8,11},{9,8},{10,9... | collective-permute-start | bytes 98312 | tf_op jit(solution)/shard_map/ppermute | solution.py:96
  102.0 43.5 %copy-start.1 = (s32[32]{0:T(128)S(1)}, s32[32]{0:T(128)}, u32[]{:S(2)}) copy-start(s32[32]{0:T(128)} %param.34) | copy-start | bytes 388
  110.0 7.9 %collective-permute-start.21 = (bf16[32,1792]{1,0:T(8,128)(2,1)S(1)}, bf16[32,1792]{1,0:T(8,128)(2,1)S(1)}, u32[]{:S(2)}, u32[]{:S(2)}) collective-permute-start(bf16[32,1792]{1,0:T(8,128)(2,1)S(1)} %get-tuple-element.54), channel_id=1, source_target_pairs={{0,4},{4,8},{8,12},{12,0},{1,5},{5,9},{9,13},{13,1},{2,6},{6,10},{... | collective-permute-start | bytes 344072 | tf_op jit(solution)/shard_map/ppermute | solution.py:106
  110.9 11.4 %collective-permute-start.22 = (bf16[32,1792]{1,0:T(8,128)(2,1)S(1)}, bf16[32,1792]{1,0:T(8,128)(2,1)S(1)}, u32[]{:S(2)}, u32[]{:S(2)}) collective-permute-start(bf16[32,1792]{1,0:T(8,128)(2,1)S(1)} %get-tuple-element.55), channel_id=1, source_target_pairs={{0,8},{4,12},{8,0},{12,4},{1,9},{5,13},{9,1},{13,5},{2,10},{6,14},... | collective-permute-start | bytes 344072 | tf_op jit(solution)/shard_map/ppermute | solution.py:106
  113.4 8.9 %collective-permute-start.23 = (bf16[32,1792]{1,0:T(8,128)(2,1)S(1)}, bf16[32,1792]{1,0:T(8,128)(2,1)S(1)}, u32[]{:S(2)}, u32[]{:S(2)}) collective-permute-start(bf16[32,1792]{1,0:T(8,128)(2,1)S(1)} %get-tuple-element.56), channel_id=1, source_target_pairs={{0,12},{4,0},{8,4},{12,8},{1,13},{5,1},{9,5},{13,9},{2,14},{6,2},{... | collective-permute-start | bytes 344072 | tf_op jit(solution)/shard_map/ppermute | solution.py:106
  122.5 6.6 %collective-permute-start.24 = (bf16[32,896]{1,0:T(8,128)(2,1)S(1)}, bf16[32,896]{1,0:T(8,128)(2,1)S(1)}, u32[]{:S(2)}, u32[]{:S(2)}) collective-permute-start(bf16[32,896]{1,0:T(8,128)(2,1)S(1)} %fusion.23), channel_id=1, source_target_pairs={{0,4},{4,8},{8,12},{12,0},{1,5},{5,9},{9,13},{13,1},{2,6},{6,10},{... | collective-permute-start | bytes 172040 | tf_op jit(solution)/shard_map/ppermute | solution.py:96
  125.2 6.0 %collective-permute-start.25 = (bf16[32,896]{1,0:T(8,128)(2,1)S(1)}, bf16[32,896]{1,0:T(8,128)(2,1)S(1)}, u32[]{:S(2)}, u32[]{:S(2)}) collective-permute-start(bf16[32,896]{1,0:T(8,128)(2,1)S(1)} %fusion.23), channel_id=1, source_target_pairs={{0,8},{4,12},{8,0},{12,4},{1,9},{5,13},{9,1},{13,5},{2,10},{6,14},... | collective-permute-start | bytes 172040 | tf_op jit(solution)/shard_map/ppermute | solution.py:96
  125.7 5.5 %collective-permute-start.26 = (bf16[32,896]{1,0:T(8,128)(2,1)S(1)}, bf16[32,896]{1,0:T(8,128)(2,1)S(1)}, u32[]{:S(2)}, u32[]{:S(2)}) collective-permute-start(bf16[32,896]{1,0:T(8,128)(2,1)S(1)} %fusion.23), channel_id=1, source_target_pairs={{0,12},{4,0},{8,4},{12,8},{1,13},{5,1},{9,5},{13,9},{2,14},{6,2},{... | collective-permute-start | bytes 172040 | tf_op jit(solution)/shard_map/ppermute | solution.py:96
  139.9 3.8 %collective-permute-start.27 = (f32[8,2048]{1,0:T(8,128)S(1)}, f32[8,2048]{1,0:T(8,128)S(1)}, u32[]{:S(2)}, u32[]{:S(2)}) collective-permute-start(f32[8,2048]{1,0:T(8,128)S(1)} %get-tuple-element.60), channel_id=1, source_target_pairs={{0,1},{1,2},{2,3},{3,0},{4,5},{5,6},{6,7},{7,4},{8,9},{9,10},{10,1... | collective-permute-start | bytes 196616 | tf_op jit(solution)/shard_map/ppermute | solution.py:106
  139.9 4.6 %collective-permute-start.28 = (f32[8,2048]{1,0:T(8,128)S(1)}, f32[8,2048]{1,0:T(8,128)S(1)}, u32[]{:S(2)}, u32[]{:S(2)}) collective-permute-start(f32[8,2048]{1,0:T(8,128)S(1)} %get-tuple-element.62), channel_id=1, source_target_pairs={{0,2},{1,3},{2,0},{3,1},{4,6},{5,7},{6,4},{7,5},{8,10},{9,11},{10,... | collective-permute-start | bytes 196616 | tf_op jit(solution)/shard_map/ppermute | solution.py:106
  141.5 3.3 %collective-permute-start.29 = (f32[8,2048]{1,0:T(8,128)S(1)}, f32[8,2048]{1,0:T(8,128)S(1)}, u32[]{:S(2)}, u32[]{:S(2)}) collective-permute-start(f32[8,2048]{1,0:T(8,128)S(1)} %get-tuple-element.61), channel_id=1, source_target_pairs={{0,3},{1,0},{2,1},{3,2},{4,7},{5,4},{6,5},{7,6},{8,11},{9,8},{10,9... | collective-permute-start | bytes 196616 | tf_op jit(solution)/shard_map/ppermute | solution.py:106
  (5 other events, 146.3 us)

commit v2 on v1

--- a/solution.py
+++ b/solution.py
@@ -150,7 +150,9 @@
     )
     normed_all = gather_blocks(normed, CS, n_cs).reshape(rows_total, -1)
     by_slot = jnp.take(normed_all, row_of_slot, axis=0)
-    qkv_part = jnp.dot(by_slot, w_qkv.reshape(w_qkv.shape[0], -1), preferred_element_type=jnp.float32)
+    qkv_part = jnp.einsum(
+        "rf,fgc->rgc", by_slot, w_qkv, preferred_element_type=jnp.float32
+    ).reshape(rows_total, -1)
     summed = scatter_sum(qkv_part.reshape(n_pool, per_owner, -1), "pool", n_pool)
     positions = lax.dynamic_slice_in_dim(length_of_slot, my_start, per_owner, 0)
     rotated = rope_rows(summed, positions, per_group, HD)

time: 147 us -> 128 us (0.87)
  local copies, waits for them, and re-layouts: 32.8 us -> 10.5 us
  waiting for transfers between devices: 30.6 us -> 36.6 us
  starting transfers between devices: 40.9 us -> 37.8 us
    reshape x1 -> x0, local copies, waits for them, and re-layouts: 23.2 us -> none  [local(): w_qkv.reshape(w_qkv.shape[0], -1)]
    ppermute x12, waiting for transfers between devices: 18.8 us -> 22.7 us  [scatter_sum(): lax.ppermute(piece, axis, shift_pairs(n, k)).astype(jnp.float32)]
    ppermute x6, starting transfers between devices: 11.6 us -> 9.3 us  [all_sum(): total = total + lax.ppermute(x, axis, shift_pairs(n, k))]
  transfers between devices with their start and end apart: 30 -> 30, of which waited for: 24 -> 20; matrix products, arithmetic and copies ran while one was open for 22% -> 7% of each run, Pallas kernels for 0% -> 0%
where the time goes in v2:
time: 128 us
  starting transfers between devices  37.8 us (30%)
  waiting for transfers between devices  36.6 us (29%)
  matrix products  35.2 us (28%)
  local copies, waits for them, and re-layouts  10.5 us (8%)
  other arithmetic  6.99 us (5%)
    ppermute x12, waiting for transfers between devices, scatter_sum(): lax.ppermute(piece, axis, shift_pairs(n, k)).astype(jnp.float32)  22.7 us
    ppermute x12, starting transfers between devices, gather_blocks(): got = [x] + [lax.ppermute(x, axis, shift_pairs(n, k)) for k in range(1, n)]  14.4 us
    ppermute x12, starting transfers between devices, scatter_sum(): lax.ppermute(piece, axis, shift_pairs(n, k)).astype(jnp.float32)  14.1 us
    ppermute x12, waiting for transfers between devices, gather_blocks(): got = [x] + [lax.ppermute(x, axis, shift_pairs(n, k)) for k in range(1, n)]  10.5 us
    ppermute x6, starting transfers between devices, all_sum(): total = total + lax.ppermute(x, axis, shift_pairs(n, k))  9.3 us
    dot_general x1, matrix products, local(): jnp.dot(ffn_all, w_gate, preferred_element_type=jnp.float32)  7.85 us
    dot_general x1, matrix products, local(): jnp.dot(ffn_all, w_up, preferred_element_type=jnp.float32)  7.85 us
    dot_general x1, matrix products, local(): down_part = jnp.dot(hidden_all, w_down, preferred_element_type=jnp.float32)  7.7 us
  transfers between devices with their start and end apart: 30, of which 20 were waited for; matrix products, arithmetic and copies ran while one was open for 7% of the time, Pallas kernels for 0%

profile of v2, /device:TPU:0, one launch (start us, length us, event | category | flops | bytes accessed | tf_op | source)
XLA Modules:
  0.0 127.6 jit_solution(12470094980049427907)
XLA Ops:
  0.9 5.1 %collective-permute-start.2 = (f32[8]{0:T(128)S(1)}, f32[8]{0:T(128)S(1)}, u32[]{:S(2)}, u32[]{:S(2)}) collective-permute-start(f32[8]{0:T(128)S(1)} %fusion.28), channel_id=1, source_target_pairs={{0,12},{4,0},{8,4},{12,8},{1,13},{5,1},{9,5},{13,9},{2,14},{6,2},{... | collective-permute-start | bytes 104 | tf_op jit(solution)/shard_map/ppermute | solution.py:113
  12.7 2.7 %fusion.62 = (bf16[8,256,1,2,128]{4,3,2,1,0:T(2,128)(2,1)S(1)}, bf16[8,256,1,2,128]{4,3,2,1,0:T(2,128)(2,1)S(1)}) fusion(bf16[8,256,2,2,128]{4,3,2,1,0:T(2,128)(2,1)} %param.32), kind=kLoop, calls=%fused_computation.162 | loop fusion | bytes 4194304 | tf_op jit(solution)/shard_map/slice | solution.py:56
  16.4 1.6 %collective-permute-start.4 = (bf16[8,2048]{1,0:T(8,128)(2,1)S(1)}, bf16[8,2048]{1,0:T(8,128)(2,1)S(1)}, u32[]{:S(2)}, u32[]{:S(2)}) collective-permute-start(bf16[8,2048]{1,0:T(8,128)(2,1)S(1)} %fusion.30), channel_id=1, source_target_pairs={{0,2},{1,3},{2,0},{3,1},{4,6},{5,7},{6,4},{7,5},{8,10},{9,11},{10,... | collective-permute-start | bytes 98312 | tf_op jit(solution)/shard_map/ppermute | solution.py:96
  18.0 1.7 %collective-permute-start.5 = (bf16[8,2048]{1,0:T(8,128)(2,1)S(1)}, bf16[8,2048]{1,0:T(8,128)(2,1)S(1)}, u32[]{:S(2)}, u32[]{:S(2)}) collective-permute-start(bf16[8,2048]{1,0:T(8,128)(2,1)S(1)} %fusion.30), channel_id=1, source_target_pairs={{0,3},{1,0},{2,1},{3,2},{4,7},{5,4},{6,5},{7,6},{8,11},{9,8},{10,9... | collective-permute-start | bytes 98312 | tf_op jit(solution)/shard_map/ppermute | solution.py:96
  22.6 5.9 %fusion.2 = f32[32,2,1280]{2,0,1:T(8,128)S(1)} fusion(bf16[2048,2,1280]{2,1,0:T(2,128)(2,1)} %param.26, bf16[32,2048]{1,0:T(8,128)(2,1)S(1)} %gather_fusion.5, pred[32]{0:T(512)(128)(4,1)S(1)} %get-tuple-element.51), kind=kOutput, calls=%fused_computation.12 | convolution fusion | flops 335609856 | bytes 10944544 | tf_op jit(solution)/shard_map/rf,fgc->rgc/dot_general | solution.py:153
  29.2 2.5 %collective-permute-start.6 = (f32[8,2560]{1,0:T(8,128)S(1)}, f32[8,2560]{1,0:T(8,128)S(1)}, u32[]{:S(2)}, u32[]{:S(2)}) collective-permute-start(f32[8,2560]{1,0:T(8,128)S(1)} %get-tuple-element.57), channel_id=1, source_target_pairs={{0,4},{4,8},{8,12},{12,0},{1,5},{5,9},{9,13},{13,1},{2,6},{6,10},{... | collective-permute-start | bytes 245768 | tf_op jit(solution)/shard_map/ppermute | solution.py:106
  33.3 3.1 %collective-permute-done.6 = f32[8,2560]{1,0:T(8,128)S(1)} collective-permute-done((f32[8,2560]{1,0:T(8,128)S(1)}, f32[8,2560]{1,0:T(8,128)S(1)}, u32[]{:S(2)}, u32[]{:S(2)}) %collective-permute-start.6) | collective-permute-done | bytes 81952 | tf_op jit(solution)/shard_map/ppermute | solution.py:106
  36.3 1.4 %collective-permute-done.8 = f32[8,2560]{1,0:T(8,128)S(1)} collective-permute-done((f32[8,2560]{1,0:T(8,128)S(1)}, f32[8,2560]{1,0:T(8,128)S(1)}, u32[]{:S(2)}, u32[]{:S(2)}) %collective-permute-start.8) | collective-permute-done | bytes 81952 | tf_op jit(solution)/shard_map/ppermute | solution.py:106
  37.8 3.5 %collective-permute-done.7 = f32[8,2560]{1,0:T(8,128)S(1)} collective-permute-done((f32[8,2560]{1,0:T(8,128)S(1)}, f32[8,2560]{1,0:T(8,128)S(1)}, u32[]{:S(2)}, u32[]{:S(2)}) %collective-permute-start.7) | collective-permute-done | bytes 81952 | tf_op jit(solution)/shard_map/ppermute | solution.py:106
  42.7 1.7 %collective-permute-start.11 = (bf16[8,2048]{1,0:T(8,128)(2,1)S(1)}, bf16[8,2048]{1,0:T(8,128)(2,1)S(1)}, u32[]{:S(2)}, u32[]{:S(2)}) collective-permute-start(bf16[8,2048]{1,0:T(8,128)(2,1)S(1)} %bitcast.154), channel_id=1, source_target_pairs={{0,12},{4,0},{8,4},{12,8},{1,13},{5,1},{9,5},{13,9},{2,14},{6,2},{... | collective-permute-start | bytes 98312 | tf_op jit(solution)/shard_map/ppermute | solution.py:96
  45.1 1.6 %collective-permute-done.11 = bf16[8,2048]{1,0:T(8,128)(2,1)S(1)} collective-permute-done((bf16[8,2048]{1,0:T(8,128)(2,1)S(1)}, bf16[8,2048]{1,0:T(8,128)(2,1)S(1)}, u32[]{:S(2)}, u32[]{:S(2)}) %collective-permute-start.11) | collective-permute-done | bytes 32800 | tf_op jit(solution)/shard_map/ppermute | solution.py:96
  46.7 2.7 %collective-permute-done.10 = bf16[8,2048]{1,0:T(8,128)(2,1)S(1)} collective-permute-done((bf16[8,2048]{1,0:T(8,128)(2,1)S(1)}, bf16[8,2048]{1,0:T(8,128)(2,1)S(1)}, u32[]{:S(2)}, u32[]{:S(2)}) %collective-permute-start.10) | collective-permute-done | bytes 32800 | tf_op jit(solution)/shard_map/ppermute | solution.py:96
  51.5 5.0 %convolution_bitcast_fusion = f32[4,8,2048]{2,1,0:T(8,128)S(1)} fusion(bf16[2048,2048]{1,0:T(8,128)(2,1)} %param.27, bf16[32,2048]{1,0:T(8,128)(2,1)S(1)} %gather_fusion.7, pred[32]{0:T(512)(128)(4,1)S(1)} %get-tuple-element.46), kind=kOutput, calls=%fused_computation.16 | convolution fusion | flops 268500992 | bytes 8781856 | tf_op jit(solution)/shard_map/dot_general | solution.py:162
  56.5 1.7 %collective-permute-start.14 = (f32[8,2048]{1,0:T(8,128)S(1)}, f32[8,2048]{1,0:T(8,128)S(1)}, u32[]{:S(2)}, u32[]{:S(2)}) collective-permute-start(f32[8,2048]{1,0:T(8,128)S(1)} %get-tuple-element.64), channel_id=1, source_target_pairs={{0,3},{1,0},{2,1},{3,2},{4,7},{5,4},{6,5},{7,6},{8,11},{9,8},{10,9... | collective-permute-start | bytes 196616 | tf_op jit(solution)/shard_map/ppermute | solution.py:106
  58.3 1.5 %collective-permute-start.13 = (f32[8,2048]{1,0:T(8,128)S(1)}, f32[8,2048]{1,0:T(8,128)S(1)}, u32[]{:S(2)}, u32[]{:S(2)}) collective-permute-start(f32[8,2048]{1,0:T(8,128)S(1)} %get-tuple-element.65), channel_id=1, source_target_pairs={{0,2},{1,3},{2,0},{3,1},{4,6},{5,7},{6,4},{7,5},{8,10},{9,11},{10,... | collective-permute-start | bytes 196616 | tf_op jit(solution)/shard_map/ppermute | solution.py:106
  60.6 2.2 %collective-permute-done.13 = f32[8,2048]{1,0:T(8,128)S(1)} collective-permute-done((f32[8,2048]{1,0:T(8,128)S(1)}, f32[8,2048]{1,0:T(8,128)S(1)}, u32[]{:S(2)}, u32[]{:S(2)}) %collective-permute-start.13) | collective-permute-done | bytes 65568 | tf_op jit(solution)/shard_map/ppermute | solution.py:106
  64.3 1.9 %collective-permute-start.15 = (f32[8]{0:T(128)S(1)}, f32[8]{0:T(128)S(1)}, u32[]{:S(2)}, u32[]{:S(2)}) collective-permute-start(f32[8]{0:T(128)S(1)} %get-tuple-element.44), channel_id=1, source_target_pairs={{0,4},{4,8},{8,12},{12,0},{1,5},{5,9},{9,13},{13,1},{2,6},{6,10},{... | collective-permute-start | bytes 104 | tf_op jit(solution)/shard_map/ppermute | solution.py:113
  66.6 1.6 %collective-permute-done.16 = f32[8]{0:T(128)S(1)} collective-permute-done((f32[8]{0:T(128)S(1)}, f32[8]{0:T(128)S(1)}, u32[]{:S(2)}, u32[]{:S(2)}) %collective-permute-start.16) | collective-permute-done | bytes 64 | tf_op jit(solution)/shard_map/ppermute | solution.py:113
  70.9 1.7 %collective-permute-start.20 = (bf16[8,2048]{1,0:T(8,128)(2,1)S(1)}, bf16[8,2048]{1,0:T(8,128)(2,1)S(1)}, u32[]{:S(2)}, u32[]{:S(2)}) collective-permute-start(bf16[8,2048]{1,0:T(8,128)(2,1)S(1)} %multiply_convert_fusion), channel_id=1, source_target_pairs={{0,3},{1,0},{2,1},{3,2},{4,7},{5,4},{6,5},{7,6},{8,11},{9,8},{10,9... | collective-permute-start | bytes 98312 | tf_op jit(solution)/shard_map/ppermute | solution.py:96
  74.8 7.8 %convolution_convert_fusion = bf16[32,3584]{1,0:T(8,128)(2,1)S(1)} fusion(bf16[2048,3584]{1,0:T(8,128)(2,1)} %param.30, bf16[4,8,2048]{2,1,0:T(8,128)(2,1)S(1)} %gather_fusion.8, pred[4]{0:T(512)(128)(4,1)S(1)} %get-tuple-element.77), kind=kOutput, calls=%fused_computation.14 | convolution fusion | flops 469942272 | bytes 15040516 | tf_op jit(solution)/shard_map/dot_general | solution.py:171
  82.7 7.9 %convolution_convert_fusion.1 = bf16[32,3584]{1,0:T(8,128)(2,1)S(1)} fusion(bf16[2048,3584]{1,0:T(8,128)(2,1)} %param.29, bf16[4,8,2048]{2,1,0:T(8,128)(2,1)S(1)} %gather_fusion.8, pred[4]{0:T(512)(128)(4,1)S(1)} %get-tuple-element.77), kind=kOutput, calls=%fused_computation.15 | convolution fusion | flops 469942272 | bytes 15040516 | tf_op jit(solution)/shard_map/dot_general | solution.py:170
  91.1 1.8 %collective-permute-start.22 = (bf16[32,1792]{1,0:T(8,128)(2,1)S(1)}, bf16[32,1792]{1,0:T(8,128)(2,1)S(1)}, u32[]{:S(2)}, u32[]{:S(2)}) collective-permute-start(bf16[32,1792]{1,0:T(8,128)(2,1)S(1)} %get-tuple-element.55), channel_id=1, source_target_pairs={{0,8},{4,12},{8,0},{12,4},{1,9},{5,13},{9,1},{13,5},{2,10},{6,14},... | collective-permute-start | bytes 344072 | tf_op jit(solution)/shard_map/ppermute | solution.py:106
  92.9 1.9 %collective-permute-start.23 = (bf16[32,1792]{1,0:T(8,128)(2,1)S(1)}, bf16[32,1792]{1,0:T(8,128)(2,1)S(1)}, u32[]{:S(2)}, u32[]{:S(2)}) collective-permute-start(bf16[32,1792]{1,0:T(8,128)(2,1)S(1)} %get-tuple-element.56), channel_id=1, source_target_pairs={{0,12},{4,0},{8,4},{12,8},{1,13},{5,1},{9,5},{13,9},{2,14},{6,2},{... | collective-permute-start | bytes 344072 | tf_op jit(solution)/shard_map/ppermute | solution.py:106
  94.8 4.2 %collective-permute-done.21 = bf16[32,1792]{1,0:T(8,128)(2,1)S(1)} collective-permute-done((bf16[32,1792]{1,0:T(8,128)(2,1)S(1)}, bf16[32,1792]{1,0:T(8,128)(2,1)S(1)}, u32[]{:S(2)}, u32[]{:S(2)}) %collective-permute-start.21) | collective-permute-done | bytes 114720 | tf_op jit(solution)/shard_map/ppermute | solution.py:106
  98.9 4.0 %collective-permute-done.22 = bf16[32,1792]{1,0:T(8,128)(2,1)S(1)} collective-permute-done((bf16[32,1792]{1,0:T(8,128)(2,1)S(1)}, bf16[32,1792]{1,0:T(8,128)(2,1)S(1)}, u32[]{:S(2)}, u32[]{:S(2)}) %collective-permute-start.22) | collective-permute-done | bytes 114720 | tf_op jit(solution)/shard_map/ppermute | solution.py:106
  103.1 2.0 %collective-permute-start.25 = (bf16[32,896]{1,0:T(8,128)(2,1)S(1)}, bf16[32,896]{1,0:T(8,128)(2,1)S(1)}, u32[]{:S(2)}, u32[]{:S(2)}) collective-permute-start(bf16[32,896]{1,0:T(8,128)(2,1)S(1)} %fusion.24), channel_id=1, source_target_pairs={{0,8},{4,12},{8,0},{12,4},{1,9},{5,13},{9,1},{13,5},{2,10},{6,14},... | collective-permute-start | bytes 172040 | tf_op jit(solution)/shard_map/ppermute | solution.py:96
  105.1 1.9 %collective-permute-start.24 = (bf16[32,896]{1,0:T(8,128)(2,1)S(1)}, bf16[32,896]{1,0:T(8,128)(2,1)S(1)}, u32[]{:S(2)}, u32[]{:S(2)}) collective-permute-start(bf16[32,896]{1,0:T(8,128)(2,1)S(1)} %fusion.24), channel_id=1, source_target_pairs={{0,4},{4,8},{8,12},{12,0},{1,5},{5,9},{9,13},{13,1},{2,6},{6,10},{... | collective-permute-start | bytes 172040 | tf_op jit(solution)/shard_map/ppermute | solution.py:96
  107.0 1.9 %collective-permute-start.26 = (bf16[32,896]{1,0:T(8,128)(2,1)S(1)}, bf16[32,896]{1,0:T(8,128)(2,1)S(1)}, u32[]{:S(2)}, u32[]{:S(2)}) collective-permute-start(bf16[32,896]{1,0:T(8,128)(2,1)S(1)} %fusion.24), channel_id=1, source_target_pairs={{0,12},{4,0},{8,4},{12,8},{1,13},{5,1},{9,5},{13,9},{2,14},{6,2},{... | collective-permute-start | bytes 172040 | tf_op jit(solution)/shard_map/ppermute | solution.py:96
  109.0 3.2 %collective-permute-done.24 = bf16[32,896]{1,0:T(8,128)(2,1)S(1)} collective-permute-done((bf16[32,896]{1,0:T(8,128)(2,1)S(1)}, bf16[32,896]{1,0:T(8,128)(2,1)S(1)}, u32[]{:S(2)}, u32[]{:S(2)}) %collective-permute-start.24) | collective-permute-done | bytes 57376 | tf_op jit(solution)/shard_map/ppermute | solution.py:96
  113.1 7.7 %fusion = f32[4,8,2048]{2,1,0:T(8,128)S(1)} fusion(bf16[4,8,3584]{2,1,0:T(8,128)(2,1)S(1)} %dot_general.33, bf16[3584,2048]{1,0:T(8,128)(2,1)} %param.31), kind=kOutput, calls=%fused_computation.10 | convolution fusion | flops 469762048 | bytes 15171584 | tf_op jit(solution)/shard_map/dot_general | solution.py:181
  120.9 1.7 %collective-permute-start.29 = (f32[8,2048]{1,0:T(8,128)S(1)}, f32[8,2048]{1,0:T(8,128)S(1)}, u32[]{:S(2)}, u32[]{:S(2)}) collective-permute-start(f32[8,2048]{1,0:T(8,128)S(1)} %get-tuple-element.61), channel_id=1, source_target_pairs={{0,3},{1,0},{2,1},{3,2},{4,7},{5,4},{6,5},{7,6},{8,11},{9,8},{10,9... | collective-permute-start | bytes 196616 | tf_op jit(solution)/shard_map/ppermute | solution.py:106
  124.6 2.3 %collective-permute-done.28 = f32[8,2048]{1,0:T(8,128)S(1)} collective-permute-done((f32[8,2048]{1,0:T(8,128)S(1)}, f32[8,2048]{1,0:T(8,128)S(1)}, u32[]{:S(2)}, u32[]{:S(2)}) %collective-permute-start.28) | collective-permute-done | bytes 65568 | tf_op jit(solution)/shard_map/ppermute | solution.py:106
  (116 shorter events, 29.5 us)
Async XLA Ops:
  0.9 14.6 %collective-permute-start.2 = (f32[8]{0:T(128)S(1)}, f32[8]{0:T(128)S(1)}, u32[]{:S(2)}, u32[]{:S(2)}) collective-permute-start(f32[8]{0:T(128)S(1)} %fusion.28), channel_id=1, source_target_pairs={{0,12},{4,0},{8,4},{12,8},{1,13},{5,1},{9,5},{13,9},{2,14},{6,2},{... | collective-permute-start | bytes 104 | tf_op jit(solution)/shard_map/ppermute | solution.py:113
  6.0 9.5 %collective-permute-start.1 = (f32[8]{0:T(128)S(1)}, f32[8]{0:T(128)S(1)}, u32[]{:S(2)}, u32[]{:S(2)}) collective-permute-start(f32[8]{0:T(128)S(1)} %fusion.28), channel_id=1, source_target_pairs={{0,8},{4,12},{8,0},{12,4},{1,9},{5,13},{9,1},{13,5},{2,10},{6,14},... | collective-permute-start | bytes 104 | tf_op jit(solution)/shard_map/ppermute | solution.py:113
  6.0 9.6 %collective-permute-start = (f32[8]{0:T(128)S(1)}, f32[8]{0:T(128)S(1)}, u32[]{:S(2)}, u32[]{:S(2)}) collective-permute-start(f32[8]{0:T(128)S(1)} %fusion.28), channel_id=1, source_target_pairs={{0,4},{4,8},{8,12},{12,0},{1,5},{5,9},{9,13},{13,1},{2,6},{6,10},{... | collective-permute-start | bytes 104 | tf_op jit(solution)/shard_map/ppermute | solution.py:113
  16.4 4.2 %collective-permute-start.4 = (bf16[8,2048]{1,0:T(8,128)(2,1)S(1)}, bf16[8,2048]{1,0:T(8,128)(2,1)S(1)}, u32[]{:S(2)}, u32[]{:S(2)}) collective-permute-start(bf16[8,2048]{1,0:T(8,128)(2,1)S(1)} %fusion.30), channel_id=1, source_target_pairs={{0,2},{1,3},{2,0},{3,1},{4,6},{5,7},{6,4},{7,5},{8,10},{9,11},{10,... | collective-permute-start | bytes 98312 | tf_op jit(solution)/shard_map/ppermute | solution.py:96
  18.0 3.3 %collective-permute-start.3 = (bf16[8,2048]{1,0:T(8,128)(2,1)S(1)}, bf16[8,2048]{1,0:T(8,128)(2,1)S(1)}, u32[]{:S(2)}, u32[]{:S(2)}) collective-permute-start(bf16[8,2048]{1,0:T(8,128)(2,1)S(1)} %fusion.30), channel_id=1, source_target_pairs={{0,1},{1,2},{2,3},{3,0},{4,5},{5,6},{6,7},{7,4},{8,9},{9,10},{10,1... | collective-permute-start | bytes 98312 | tf_op jit(solution)/shard_map/ppermute | solution.py:96
  18.0 3.3 %collective-permute-start.5 = (bf16[8,2048]{1,0:T(8,128)(2,1)S(1)}, bf16[8,2048]{1,0:T(8,128)(2,1)S(1)}, u32[]{:S(2)}, u32[]{:S(2)}) collective-permute-start(bf16[8,2048]{1,0:T(8,128)(2,1)S(1)} %fusion.30), channel_id=1, source_target_pairs={{0,3},{1,0},{2,1},{3,2},{4,7},{5,4},{6,5},{7,6},{8,11},{9,8},{10,9... | collective-permute-start | bytes 98312 | tf_op jit(solution)/shard_map/ppermute | solution.py:96
  28.6 41.0 %copy-start.3 = (f32[2048]{0:T(1024)S(1)}, f32[2048]{0:T(1024)}, u32[]{:S(2)}) copy-start(f32[2048]{0:T(1024)} %param.28) | copy-start | bytes 24580
  29.2 7.2 %collective-permute-start.6 = (f32[8,2560]{1,0:T(8,128)S(1)}, f32[8,2560]{1,0:T(8,128)S(1)}, u32[]{:S(2)}, u32[]{:S(2)}) collective-permute-start(f32[8,2560]{1,0:T(8,128)S(1)} %get-tuple-element.57), channel_id=1, source_target_pairs={{0,4},{4,8},{8,12},{12,0},{1,5},{5,9},{9,13},{13,1},{2,6},{6,10},{... | collective-permute-start | bytes 245768 | tf_op jit(solution)/shard_map/ppermute | solution.py:106
  31.7 6.1 %collective-permute-start.8 = (f32[8,2560]{1,0:T(8,128)S(1)}, f32[8,2560]{1,0:T(8,128)S(1)}, u32[]{:S(2)}, u32[]{:S(2)}) collective-permute-start(f32[8,2560]{1,0:T(8,128)S(1)} %get-tuple-element.58), channel_id=1, source_target_pairs={{0,12},{4,0},{8,4},{12,8},{1,13},{5,1},{9,5},{13,9},{2,14},{6,2},{... | collective-permute-start | bytes 245768 | tf_op jit(solution)/shard_map/ppermute | solution.py:106
  33.1 8.2 %collective-permute-start.7 = (f32[8,2560]{1,0:T(8,128)S(1)}, f32[8,2560]{1,0:T(8,128)S(1)}, u32[]{:S(2)}, u32[]{:S(2)}) collective-permute-start(f32[8,2560]{1,0:T(8,128)S(1)} %get-tuple-element.59), channel_id=1, source_target_pairs={{0,8},{4,12},{8,0},{12,4},{1,9},{5,13},{9,1},{13,5},{2,10},{6,14},... | collective-permute-start | bytes 245768 | tf_op jit(solution)/shard_map/ppermute | solution.py:106
  42.7 4.0 %collective-permute-start.11 = (bf16[8,2048]{1,0:T(8,128)(2,1)S(1)}, bf16[8,2048]{1,0:T(8,128)(2,1)S(1)}, u32[]{:S(2)}, u32[]{:S(2)}) collective-permute-start(bf16[8,2048]{1,0:T(8,128)(2,1)S(1)} %bitcast.154), channel_id=1, source_target_pairs={{0,12},{4,0},{8,4},{12,8},{1,13},{5,1},{9,5},{13,9},{2,14},{6,2},{... | collective-permute-start | bytes 98312 | tf_op jit(solution)/shard_map/ppermute | solution.py:96
  44.4 5.0 %collective-permute-start.10 = (bf16[8,2048]{1,0:T(8,128)(2,1)S(1)}, bf16[8,2048]{1,0:T(8,128)(2,1)S(1)}, u32[]{:S(2)}, u32[]{:S(2)}) collective-permute-start(bf16[8,2048]{1,0:T(8,128)(2,1)S(1)} %bitcast.155), channel_id=1, source_target_pairs={{0,8},{4,12},{8,0},{12,4},{1,9},{5,13},{9,1},{13,5},{2,10},{6,14},... | collective-permute-start | bytes 98312 | tf_op jit(solution)/shard_map/ppermute | solution.py:96
  44.4 5.7 %collective-permute-start.9 = (bf16[8,2048]{1,0:T(8,128)(2,1)S(1)}, bf16[8,2048]{1,0:T(8,128)(2,1)S(1)}, u32[]{:S(2)}, u32[]{:S(2)}) collective-permute-start(bf16[8,2048]{1,0:T(8,128)(2,1)S(1)} %bitcast.156), channel_id=1, source_target_pairs={{0,4},{4,8},{8,12},{12,0},{1,5},{5,9},{9,13},{13,1},{2,6},{6,10},{... | collective-permute-start | bytes 98312 | tf_op jit(solution)/shard_map/ppermute | solution.py:96
  56.5 3.7 %collective-permute-start.12 = (f32[8,2048]{1,0:T(8,128)S(1)}, f32[8,2048]{1,0:T(8,128)S(1)}, u32[]{:S(2)}, u32[]{:S(2)}) collective-permute-start(f32[8,2048]{1,0:T(8,128)S(1)} %get-tuple-element.63), channel_id=1, source_target_pairs={{0,1},{1,2},{2,3},{3,0},{4,5},{5,6},{6,7},{7,4},{8,9},{9,10},{10,1... | collective-permute-start | bytes 196616 | tf_op jit(solution)/shard_map/ppermute | solution.py:106
  56.5 4.1 %collective-permute-start.14 = (f32[8,2048]{1,0:T(8,128)S(1)}, f32[8,2048]{1,0:T(8,128)S(1)}, u32[]{:S(2)}, u32[]{:S(2)}) collective-permute-start(f32[8,2048]{1,0:T(8,128)S(1)} %get-tuple-element.64), channel_id=1, source_target_pairs={{0,3},{1,0},{2,1},{3,2},{4,7},{5,4},{6,5},{7,6},{8,11},{9,8},{10,9... | collective-permute-start | bytes 196616 | tf_op jit(solution)/shard_map/ppermute | solution.py:106
  58.3 4.6 %collective-permute-start.13 = (f32[8,2048]{1,0:T(8,128)S(1)}, f32[8,2048]{1,0:T(8,128)S(1)}, u32[]{:S(2)}, u32[]{:S(2)}) collective-permute-start(f32[8,2048]{1,0:T(8,128)S(1)} %get-tuple-element.65), channel_id=1, source_target_pairs={{0,2},{1,3},{2,0},{3,1},{4,6},{5,7},{6,4},{7,5},{8,10},{9,11},{10,... | collective-permute-start | bytes 196616 | tf_op jit(solution)/shard_map/ppermute | solution.py:106
  63.0 3.6 %collective-permute-start.17 = (f32[8]{0:T(128)S(1)}, f32[8]{0:T(128)S(1)}, u32[]{:S(2)}, u32[]{:S(2)}) collective-permute-start(f32[8]{0:T(128)S(1)} %get-tuple-element.44), channel_id=1, source_target_pairs={{0,12},{4,0},{8,4},{12,8},{1,13},{5,1},{9,5},{13,9},{2,14},{6,2},{... | collective-permute-start | bytes 104 | tf_op jit(solution)/shard_map/ppermute | solution.py:113
  63.7 4.4 %collective-permute-start.16 = (f32[8]{0:T(128)S(1)}, f32[8]{0:T(128)S(1)}, u32[]{:S(2)}, u32[]{:S(2)}) collective-permute-start(f32[8]{0:T(128)S(1)} %get-tuple-element.44), channel_id=1, source_target_pairs={{0,8},{4,12},{8,0},{12,4},{1,9},{5,13},{9,1},{13,5},{2,10},{6,14},... | collective-permute-start | bytes 104 | tf_op jit(solution)/shard_map/ppermute | solution.py:113
  64.3 5.3 %collective-permute-start.15 = (f32[8]{0:T(128)S(1)}, f32[8]{0:T(128)S(1)}, u32[]{:S(2)}, u32[]{:S(2)}) collective-permute-start(f32[8]{0:T(128)S(1)} %get-tuple-element.44), channel_id=1, source_target_pairs={{0,4},{4,8},{8,12},{12,0},{1,5},{5,9},{9,13},{13,1},{2,6},{6,10},{... | collective-permute-start | bytes 104 | tf_op jit(solution)/shard_map/ppermute | solution.py:113
  69.7 4.0 %collective-permute-start.19 = (bf16[8,2048]{1,0:T(8,128)(2,1)S(1)}, bf16[8,2048]{1,0:T(8,128)(2,1)S(1)}, u32[]{:S(2)}, u32[]{:S(2)}) collective-permute-start(bf16[8,2048]{1,0:T(8,128)(2,1)S(1)} %multiply_convert_fusion), channel_id=1, source_target_pairs={{0,2},{1,3},{2,0},{3,1},{4,6},{5,7},{6,4},{7,5},{8,10},{9,11},{10,... | collective-permute-start | bytes 98312 | tf_op jit(solution)/shard_map/ppermute | solution.py:96
  70.9 3.3 %collective-permute-start.18 = (bf16[8,2048]{1,0:T(8,128)(2,1)S(1)}, bf16[8,2048]{1,0:T(8,128)(2,1)S(1)}, u32[]{:S(2)}, u32[]{:S(2)}) collective-permute-start(bf16[8,2048]{1,0:T(8,128)(2,1)S(1)} %multiply_convert_fusion), channel_id=1, source_target_pairs={{0,1},{1,2},{2,3},{3,0},{4,5},{5,6},{6,7},{7,4},{8,9},{9,10},{10,1... | collective-permute-start | bytes 98312 | tf_op jit(solution)/shard_map/ppermute | solution.py:96
  70.9 3.3 %collective-permute-start.20 = (bf16[8,2048]{1,0:T(8,128)(2,1)S(1)}, bf16[8,2048]{1,0:T(8,128)(2,1)S(1)}, u32[]{:S(2)}, u32[]{:S(2)}) collective-permute-start(bf16[8,2048]{1,0:T(8,128)(2,1)S(1)} %multiply_convert_fusion), channel_id=1, source_target_pairs={{0,3},{1,0},{2,1},{3,2},{4,7},{5,4},{6,5},{7,6},{8,11},{9,8},{10,9... | collective-permute-start | bytes 98312 | tf_op jit(solution)/shard_map/ppermute | solution.py:96
  82.7 44.9 %copy-start.1 = (s32[32]{0:T(128)S(1)}, s32[32]{0:T(128)}, u32[]{:S(2)}) copy-start(s32[32]{0:T(128)} %param.33) | copy-start | bytes 388
  90.7 8.2 %collective-permute-start.21 = (bf16[32,1792]{1,0:T(8,128)(2,1)S(1)}, bf16[32,1792]{1,0:T(8,128)(2,1)S(1)}, u32[]{:S(2)}, u32[]{:S(2)}) collective-permute-start(bf16[32,1792]{1,0:T(8,128)(2,1)S(1)} %get-tuple-element.54), channel_id=1, source_target_pairs={{0,4},{4,8},{8,12},{12,0},{1,5},{5,9},{9,13},{13,1},{2,6},{6,10},{... | collective-permute-start | bytes 344072 | tf_op jit(solution)/shard_map/ppermute | solution.py:106
  91.1 11.9 %collective-permute-start.22 = (bf16[32,1792]{1,0:T(8,128)(2,1)S(1)}, bf16[32,1792]{1,0:T(8,128)(2,1)S(1)}, u32[]{:S(2)}, u32[]{:S(2)}) collective-permute-start(bf16[32,1792]{1,0:T(8,128)(2,1)S(1)} %get-tuple-element.55), channel_id=1, source_target_pairs={{0,8},{4,12},{8,0},{12,4},{1,9},{5,13},{9,1},{13,5},{2,10},{6,14},... | collective-permute-start | bytes 344072 | tf_op jit(solution)/shard_map/ppermute | solution.py:106
  92.9 10.1 %collective-permute-start.23 = (bf16[32,1792]{1,0:T(8,128)(2,1)S(1)}, bf16[32,1792]{1,0:T(8,128)(2,1)S(1)}, u32[]{:S(2)}, u32[]{:S(2)}) collective-permute-start(bf16[32,1792]{1,0:T(8,128)(2,1)S(1)} %get-tuple-element.56), channel_id=1, source_target_pairs={{0,12},{4,0},{8,4},{12,8},{1,13},{5,1},{9,5},{13,9},{2,14},{6,2},{... | collective-permute-start | bytes 344072 | tf_op jit(solution)/shard_map/ppermute | solution.py:106
  103.1 5.9 %collective-permute-start.25 = (bf16[32,896]{1,0:T(8,128)(2,1)S(1)}, bf16[32,896]{1,0:T(8,128)(2,1)S(1)}, u32[]{:S(2)}, u32[]{:S(2)}) collective-permute-start(bf16[32,896]{1,0:T(8,128)(2,1)S(1)} %fusion.24), channel_id=1, source_target_pairs={{0,8},{4,12},{8,0},{12,4},{1,9},{5,13},{9,1},{13,5},{2,10},{6,14},... | collective-permute-start | bytes 172040 | tf_op jit(solution)/shard_map/ppermute | solution.py:96
  105.1 7.1 %collective-permute-start.24 = (bf16[32,896]{1,0:T(8,128)(2,1)S(1)}, bf16[32,896]{1,0:T(8,128)(2,1)S(1)}, u32[]{:S(2)}, u32[]{:S(2)}) collective-permute-start(bf16[32,896]{1,0:T(8,128)(2,1)S(1)} %fusion.24), channel_id=1, source_target_pairs={{0,4},{4,8},{8,12},{12,0},{1,5},{5,9},{9,13},{13,1},{2,6},{6,10},{... | collective-permute-start | bytes 172040 | tf_op jit(solution)/shard_map/ppermute | solution.py:96
  107.0 5.2 %collective-permute-start.26 = (bf16[32,896]{1,0:T(8,128)(2,1)S(1)}, bf16[32,896]{1,0:T(8,128)(2,1)S(1)}, u32[]{:S(2)}, u32[]{:S(2)}) collective-permute-start(bf16[32,896]{1,0:T(8,128)(2,1)S(1)} %fusion.24), channel_id=1, source_target_pairs={{0,12},{4,0},{8,4},{12,8},{1,13},{5,1},{9,5},{13,9},{2,14},{6,2},{... | collective-permute-start | bytes 172040 | tf_op jit(solution)/shard_map/ppermute | solution.py:96
  120.9 3.7 %collective-permute-start.27 = (f32[8,2048]{1,0:T(8,128)S(1)}, f32[8,2048]{1,0:T(8,128)S(1)}, u32[]{:S(2)}, u32[]{:S(2)}) collective-permute-start(f32[8,2048]{1,0:T(8,128)S(1)} %get-tuple-element.60), channel_id=1, source_target_pairs={{0,1},{1,2},{2,3},{3,0},{4,5},{5,6},{6,7},{7,4},{8,9},{9,10},{10,1... | collective-permute-start | bytes 196616 | tf_op jit(solution)/shard_map/ppermute | solution.py:106
  120.9 3.7 %collective-permute-start.29 = (f32[8,2048]{1,0:T(8,128)S(1)}, f32[8,2048]{1,0:T(8,128)S(1)}, u32[]{:S(2)}, u32[]{:S(2)}) collective-permute-start(f32[8,2048]{1,0:T(8,128)S(1)} %get-tuple-element.61), channel_id=1, source_target_pairs={{0,3},{1,0},{2,1},{3,2},{4,7},{5,4},{6,5},{7,6},{8,11},{9,8},{10,9... | collective-permute-start | bytes 196616 | tf_op jit(solution)/shard_map/ppermute | solution.py:106
  122.7 4.3 %collective-permute-start.28 = (f32[8,2048]{1,0:T(8,128)S(1)}, f32[8,2048]{1,0:T(8,128)S(1)}, u32[]{:S(2)}, u32[]{:S(2)}) collective-permute-start(f32[8,2048]{1,0:T(8,128)S(1)} %get-tuple-element.62), channel_id=1, source_target_pairs={{0,2},{1,3},{2,0},{3,1},{4,6},{5,7},{6,4},{7,5},{8,10},{9,11},{10,... | collective-permute-start | bytes 196616 | tf_op jit(solution)/shard_map/ppermute | solution.py:106
  (2 other events, 42.0 us)

commit v3 on v2

--- a/solution.py
+++ b/solution.py
@@ -112,6 +112,42 @@
     for k in range(1, n):
         total = total + lax.ppermute(x, axis, shift_pairs(n, k))
     return total
+
+
+def scatter_matmul(x, weights, axis, n):
+    idx = lax.axis_index(axis)
+    chunk = weights[0].shape[1] // n
+
+    def block(j):
+        parts = [
+            jnp.dot(
+                x,
+                lax.dynamic_slice_in_dim(w, j * chunk, chunk, 1),
+                preferred_element_type=jnp.float32,
+            ).astype(jnp.bfloat16)
+            for w in weights
+        ]
+        return jnp.concatenate(parts, axis=1)
+
+    total = None
+    for k in range(1, n):
+        got = lax.ppermute(block((idx + k) % n), axis, shift_pairs(n, k)).astype(jnp.float32)
+        total = got if total is None else total + got
+    own = block(idx).astype(jnp.float32)
+    return own if total is None else own + total
+
+
+def gather_matmul(x, w, axis, n):
+    idx = lax.axis_index(axis)
+    chunk = x.shape[1]
+    acc = jnp.dot(
+        x, lax.dynamic_slice_in_dim(w, idx * chunk, chunk, 0), preferred_element_type=jnp.float32
+    )
+    for k in range(1, n):
+        got = lax.ppermute(x, axis, shift_pairs(n, k))
+        rows = lax.dynamic_slice_in_dim(w, ((idx - k) % n) * chunk, chunk, 0)
+        acc = acc + jnp.dot(got, rows, preferred_element_type=jnp.float32)
+    return acc
 
 
 def local(
@@ -167,18 +203,12 @@
         residual * lax.rsqrt(squares_mid / D + epsilon)[:, None] * ffn_gain[None, :]
     ).astype(jnp.bfloat16)
     ffn_all = gather_blocks(ffn_normed, CS, n_cs).reshape(rows_total, -1)
-    gate_part = jnp.dot(ffn_all, w_gate, preferred_element_type=jnp.float32).astype(jnp.bfloat16)
-    up_part = jnp.dot(ffn_all, w_up, preferred_element_type=jnp.float32).astype(jnp.bfloat16)
-    hidden_cols = w_gate.shape[1]
-    chunk = hidden_cols // n_pool
-    gate_blocks = gate_part.reshape(rows_total, n_pool, chunk).transpose(1, 0, 2)
-    up_blocks = up_part.reshape(rows_total, n_pool, chunk).transpose(1, 0, 2)
-    both = scatter_sum(jnp.concatenate([gate_blocks, up_blocks], axis=2), "pool", n_pool)
+    both = scatter_matmul(ffn_all, (w_gate, w_up), "pool", n_pool)
+    chunk = w_gate.shape[1] // n_pool
     gate_total = both[:, :chunk]
     up_total = both[:, chunk:]
     hidden = (jax.nn.silu(gate_total) * up_total).astype(jnp.bfloat16)
-    hidden_all = gather_blocks(hidden, "pool", n_pool).transpose(1, 0, 2).reshape(rows_total, -1)
-    down_part = jnp.dot(hidden_all, w_down, preferred_element_type=jnp.float32)
+    down_part = gather_matmul(hidden, w_down, "pool", n_pool)
     return residual + scatter_sum(down_part.reshape(n_cs, rows_here, -1), CS, n_cs)
 
 

time: 128 us -> 127 us (level)
  matrix products: 35.2 us -> 37.8 us
  waiting for transfers between devices: 36.6 us -> 34.9 us
  starting transfers between devices: 37.8 us -> 36.5 us
    ppermute x0 -> x6, waiting for transfers between devices: none -> 9.75 us  [the longest x3 5.31 us: scatter_matmul(): lax.ppermute(block((idx + k) % n), axis, shift_pairs(n, k))]
    ppermute x0 -> x6, starting transfers between devices: none -> 8.62 us  [the longest x3 4.41 us: gather_matmul(): got = lax.ppermute(x, axis, shift_pairs(n, k))]
    ppermute x12 -> x9, waiting for transfers between devices: 22.7 us -> 14.5 us  [scatter_sum(): lax.ppermute(piece, axis, shift_pairs(n, k)).astype(jnp.float32)]
    ppermute x12 -> x9, starting transfers between devices: 14.4 us -> 8.56 us  [gather_blocks(): got = [x] + [lax.ppermute(x, axis, shift_pairs(n, k)) for k in range(1, n)]]
    ppermute x12 -> x9, starting transfers between devices: 14.1 us -> 10.1 us  [scatter_sum(): lax.ppermute(piece, axis, shift_pairs(n, k)).astype(jnp.float32)]
    ppermute x12 -> x9, waiting for transfers between devices: 10.5 us -> 7.31 us  [gather_blocks(): got = [x] + [lax.ppermute(x, axis, shift_pairs(n, k)) for k in range(1, n)]]
    dot_general x3 -> x12, matrix products: 23.4 us -> 25.9 us  [the longest x8 22.9 us: block(): jnp.dot(x, lax.dynamic_slice_in_dim(w, j * chunk, chunk, 1), preferred_el...]
  transfers between devices with their start and end apart: 30 -> 30, of which waited for: 20 -> 20; matrix products, arithmetic and copies ran while one was open for 7% -> 11% of each run, Pallas kernels for 0% -> 0%
where the time goes in v3:
time: 127 us; the launch traced here: 126 us
  matrix products  37.8 us (30%)
  starting transfers between devices  36.5 us (29%)
  waiting for transfers between devices  34.9 us (27%)
  local copies, waits for them, and re-layouts  9.71 us (8%)
  other arithmetic  6.76 us (5%)
    dot_general x8, matrix products, block(): jnp.dot(x, lax.dynamic_slice_in_dim(w, j * chunk, chunk, 1), preferred_el...  22.9 us
    ppermute x9, waiting for transfers between devices, scatter_sum(): lax.ppermute(piece, axis, shift_pairs(n, k)).astype(jnp.float32)  14.5 us
    ppermute x9, starting transfers between devices, scatter_sum(): lax.ppermute(piece, axis, shift_pairs(n, k)).astype(jnp.float32)  10.1 us
    ppermute x6, starting transfers between devices, all_sum(): total = total + lax.ppermute(x, axis, shift_pairs(n, k))  9.3 us
    ppermute x9, starting transfers between devices, gather_blocks(): got = [x] + [lax.ppermute(x, axis, shift_pairs(n, k)) for k in range(1, n)]  8.56 us
    ppermute x9, waiting for transfers between devices, gather_blocks(): got = [x] + [lax.ppermute(x, axis, shift_pairs(n, k)) for k in range(1, n)]  7.31 us
    dot_general x1, matrix products, local(): jnp.einsum('rf,fgc->rgc', by_slot, w_qkv, preferred_element_type=jnp.floa...  5.94 us
    ppermute x3, waiting for transfers between devices, scatter_matmul(): lax.ppermute(block((idx + k) % n), axis, shift_pairs(n, k))  5.31 us
  transfers between devices with their start and end apart: 30, of which 20 were waited for; matrix products, arithmetic and copies ran while one was open for 11% of the time, Pallas kernels for 0%

profile of v3, /device:TPU:0, one launch (start us, length us, event | category | flops | bytes accessed | tf_op | source)
XLA Modules:
  0.0 126.2 jit_solution(11597332882300659461)
XLA Ops:
  0.9 5.1 %collective-permute-start.2 = (f32[8]{0:T(128)S(1)}, f32[8]{0:T(128)S(1)}, u32[]{:S(2)}, u32[]{:S(2)}) collective-permute-start(f32[8]{0:T(128)S(1)} %fusion.80), channel_id=1, source_target_pairs={{0,12},{4,0},{8,4},{12,8},{1,13},{5,1},{9,5},{13,9},{2,14},{6,2},{... | collective-permute-start | bytes 104 | tf_op jit(solution)/shard_map/ppermute | solution.py:113
  12.7 2.7 %fusion.122 = (bf16[8,256,1,2,128]{4,3,2,1,0:T(2,128)(2,1)S(1)}, bf16[8,256,1,2,128]{4,3,2,1,0:T(2,128)(2,1)S(1)}) fusion(bf16[8,256,2,2,128]{4,3,2,1,0:T(2,128)(2,1)} %param.30), kind=kLoop, calls=%fused_computation.181 | loop fusion | bytes 4194304 | tf_op jit(solution)/shard_map/slice | solution.py:56
  16.4 1.6 %collective-permute-start.4 = (bf16[8,2048]{1,0:T(8,128)(2,1)S(1)}, bf16[8,2048]{1,0:T(8,128)(2,1)S(1)}, u32[]{:S(2)}, u32[]{:S(2)}) collective-permute-start(bf16[8,2048]{1,0:T(8,128)(2,1)S(1)} %fusion.82), channel_id=1, source_target_pairs={{0,2},{1,3},{2,0},{3,1},{4,6},{5,7},{6,4},{7,5},{8,10},{9,11},{10,... | collective-permute-start | bytes 98312 | tf_op jit(solution)/shard_map/ppermute | solution.py:96
  18.0 1.7 %collective-permute-start.5 = (bf16[8,2048]{1,0:T(8,128)(2,1)S(1)}, bf16[8,2048]{1,0:T(8,128)(2,1)S(1)}, u32[]{:S(2)}, u32[]{:S(2)}) collective-permute-start(bf16[8,2048]{1,0:T(8,128)(2,1)S(1)} %fusion.82), channel_id=1, source_target_pairs={{0,3},{1,0},{2,1},{3,2},{4,7},{5,4},{6,5},{7,6},{8,11},{9,8},{10,9... | collective-permute-start | bytes 98312 | tf_op jit(solution)/shard_map/ppermute | solution.py:96
  22.6 5.9 %fusion = f32[32,2,1280]{2,0,1:T(8,128)S(1)} fusion(bf16[2048,2,1280]{2,1,0:T(2,128)(2,1)} %param.24, bf16[32,2048]{1,0:T(8,128)(2,1)S(1)} %gather_fusion.4, pred[32]{0:T(512)(128)(4,1)S(1)} %get-tuple-element.39), kind=kOutput, calls=%fused_computation.9 | convolution fusion | flops 335609856 | bytes 10944544 | tf_op jit(solution)/shard_map/rf,fgc->rgc/dot_general | solution.py:189
  29.2 2.5 %collective-permute-start.6 = (f32[8,2560]{1,0:T(8,128)S(1)}, f32[8,2560]{1,0:T(8,128)S(1)}, u32[]{:S(2)}, u32[]{:S(2)}) collective-permute-start(f32[8,2560]{1,0:T(8,128)S(1)} %get-tuple-element.42), channel_id=1, source_target_pairs={{0,4},{4,8},{8,12},{12,0},{1,5},{5,9},{9,13},{13,1},{2,6},{6,10},{... | collective-permute-start | bytes 245768 | tf_op jit(solution)/shard_map/ppermute | solution.py:106
  33.2 3.1 %collective-permute-done.6 = f32[8,2560]{1,0:T(8,128)S(1)} collective-permute-done((f32[8,2560]{1,0:T(8,128)S(1)}, f32[8,2560]{1,0:T(8,128)S(1)}, u32[]{:S(2)}, u32[]{:S(2)}) %collective-permute-start.6) | collective-permute-done | bytes 81952 | tf_op jit(solution)/shard_map/ppermute | solution.py:106
  37.8 3.5 %collective-permute-done.7 = f32[8,2560]{1,0:T(8,128)S(1)} collective-permute-done((f32[8,2560]{1,0:T(8,128)S(1)}, f32[8,2560]{1,0:T(8,128)S(1)}, u32[]{:S(2)}, u32[]{:S(2)}) %collective-permute-start.7) | collective-permute-done | bytes 81952 | tf_op jit(solution)/shard_map/ppermute | solution.py:106
  42.7 1.7 %collective-permute-start.11 = (bf16[8,2048]{1,0:T(8,128)(2,1)S(1)}, bf16[8,2048]{1,0:T(8,128)(2,1)S(1)}, u32[]{:S(2)}, u32[]{:S(2)}) collective-permute-start(bf16[8,2048]{1,0:T(8,128)(2,1)S(1)} %bitcast.126), channel_id=1, source_target_pairs={{0,12},{4,0},{8,4},{12,8},{1,13},{5,1},{9,5},{13,9},{2,14},{6,2},{... | collective-permute-start | bytes 98312 | tf_op jit(solution)/shard_map/ppermute | solution.py:96
  45.1 1.6 %collective-permute-done.11 = bf16[8,2048]{1,0:T(8,128)(2,1)S(1)} collective-permute-done((bf16[8,2048]{1,0:T(8,128)(2,1)S(1)}, bf16[8,2048]{1,0:T(8,128)(2,1)S(1)}, u32[]{:S(2)}, u32[]{:S(2)}) %collective-permute-start.11) | collective-permute-done | bytes 32800 | tf_op jit(solution)/shard_map/ppermute | solution.py:96
  46.7 2.7 %collective-permute-done.10 = bf16[8,2048]{1,0:T(8,128)(2,1)S(1)} collective-permute-done((bf16[8,2048]{1,0:T(8,128)(2,1)S(1)}, bf16[8,2048]{1,0:T(8,128)(2,1)S(1)}, u32[]{:S(2)}, u32[]{:S(2)}) %collective-permute-start.10) | collective-permute-done | bytes 32800 | tf_op jit(solution)/shard_map/ppermute | solution.py:96
  51.5 5.0 %convolution_bitcast_fusion = f32[4,8,2048]{2,1,0:T(8,128)S(1)} fusion(bf16[2048,2048]{1,0:T(8,128)(2,1)} %param.25, bf16[32,2048]{1,0:T(8,128)(2,1)S(1)} %gather_fusion.6, pred[32]{0:T(512)(128)(4,1)S(1)} %get-tuple-element.34), kind=kOutput, calls=%fused_computation.39 | convolution fusion | flops 268500992 | bytes 8781856 | tf_op jit(solution)/shard_map/dot_general | solution.py:198
  56.5 1.7 %collective-permute-start.14 = (f32[8,2048]{1,0:T(8,128)S(1)}, f32[8,2048]{1,0:T(8,128)S(1)}, u32[]{:S(2)}, u32[]{:S(2)}) collective-permute-start(f32[8,2048]{1,0:T(8,128)S(1)} %get-tuple-element.49), channel_id=1, source_target_pairs={{0,3},{1,0},{2,1},{3,2},{4,7},{5,4},{6,5},{7,6},{8,11},{9,8},{10,9... | collective-permute-start | bytes 196616 | tf_op jit(solution)/shard_map/ppermute | solution.py:106
  60.6 2.2 %collective-permute-done.13 = f32[8,2048]{1,0:T(8,128)S(1)} collective-permute-done((f32[8,2048]{1,0:T(8,128)S(1)}, f32[8,2048]{1,0:T(8,128)S(1)}, u32[]{:S(2)}, u32[]{:S(2)}) %collective-permute-start.13) | collective-permute-done | bytes 65568 | tf_op jit(solution)/shard_map/ppermute | solution.py:106
  64.3 1.9 %collective-permute-start.15 = (f32[8]{0:T(128)S(1)}, f32[8]{0:T(128)S(1)}, u32[]{:S(2)}, u32[]{:S(2)}) collective-permute-start(f32[8]{0:T(128)S(1)} %get-tuple-element.32), channel_id=1, source_target_pairs={{0,4},{4,8},{8,12},{12,0},{1,5},{5,9},{9,13},{13,1},{2,6},{6,10},{... | collective-permute-start | bytes 104 | tf_op jit(solution)/shard_map/ppermute | solution.py:113
  66.6 1.6 %collective-permute-done.16 = f32[8]{0:T(128)S(1)} collective-permute-done((f32[8]{0:T(128)S(1)}, f32[8]{0:T(128)S(1)}, u32[]{:S(2)}, u32[]{:S(2)}) %collective-permute-start.16) | collective-permute-done | bytes 64 | tf_op jit(solution)/shard_map/ppermute | solution.py:113
  70.9 1.7 %collective-permute-start.20 = (bf16[8,2048]{1,0:T(8,128)(2,1)S(1)}, bf16[8,2048]{1,0:T(8,128)(2,1)S(1)}, u32[]{:S(2)}, u32[]{:S(2)}) collective-permute-start(bf16[8,2048]{1,0:T(8,128)(2,1)S(1)} %multiply_convert_fusion), channel_id=1, source_target_pairs={{0,3},{1,0},{2,1},{3,2},{4,7},{5,4},{6,5},{7,6},{8,11},{9,8},{10,9... | collective-permute-start | bytes 98312 | tf_op jit(solution)/shard_map/ppermute | solution.py:96
  74.8 2.8 %fusion.59 = bf16[32,896]{1,0:T(8,128)(2,1)S(1)} fusion(bf16[2048,3584]{1,0:T(8,128)(2,1)} %param.28, s32[]{:T(128)S(6)} %select_n.149, bf16[4,8,2048]{2,1,0:T(8,128)(2,1)S(1)} %gather_fusion.7, pred[4]{0:T(512)(128)(4,1)S(1)} %get-tuple-element.62), kind=kOutput, calls=%fused_computation.48 | convolution fusion | flops 117534720 | bytes 3858440 | tf_op jit(solution)/shard_map/dot_general | solution.py:123
  77.6 2.9 %fusion.56 = bf16[32,896]{1,0:T(8,128)(2,1)S(1)} fusion(bf16[2048,3584]{1,0:T(8,128)(2,1)} %param.27, s32[]{:T(128)S(6)} %select_n.149, bf16[4,8,2048]{2,1,0:T(8,128)(2,1)S(1)} %gather_fusion.7, pred[4]{0:T(512)(128)(4,1)S(1)} %get-tuple-element.62), kind=kOutput, calls=%fused_computation.47 | convolution fusion | flops 117534720 | bytes 3858440 | tf_op jit(solution)/shard_map/dot_general | solution.py:123
  80.6 2.9 %fusion.53 = bf16[32,896]{1,0:T(8,128)(2,1)S(1)} fusion(bf16[2048,3584]{1,0:T(8,128)(2,1)} %param.28, s32[]{:T(128)S(6)} %select_n.148, bf16[4,8,2048]{2,1,0:T(8,128)(2,1)S(1)} %gather_fusion.7, pred[4]{0:T(512)(128)(4,1)S(1)} %get-tuple-element.62), kind=kOutput, calls=%fused_computation.46 | convolution fusion | flops 117534720 | bytes 3858440 | tf_op jit(solution)/shard_map/dot_general | solution.py:123
  83.5 2.8 %fusion.50 = bf16[32,896]{1,0:T(8,128)(2,1)S(1)} fusion(bf16[2048,3584]{1,0:T(8,128)(2,1)} %param.27, s32[]{:T(128)S(6)} %select_n.148, bf16[4,8,2048]{2,1,0:T(8,128)(2,1)S(1)} %gather_fusion.7, pred[4]{0:T(512)(128)(4,1)S(1)} %get-tuple-element.62), kind=kOutput, calls=%fused_computation.45 | convolution fusion | flops 117534720 | bytes 3858440 | tf_op jit(solution)/shard_map/dot_general | solution.py:123
  86.4 2.9 %fusion.47 = bf16[32,896]{1,0:T(8,128)(2,1)S(1)} fusion(bf16[2048,3584]{1,0:T(8,128)(2,1)} %param.28, s32[]{:T(128)S(6)} %select_n.147, bf16[4,8,2048]{2,1,0:T(8,128)(2,1)S(1)} %gather_fusion.7, pred[4]{0:T(512)(128)(4,1)S(1)} %get-tuple-element.62), kind=kOutput, calls=%fused_computation.44 | convolution fusion | flops 117534720 | bytes 3858440 | tf_op jit(solution)/shard_map/dot_general | solution.py:123
  89.3 2.8 %fusion.44 = bf16[32,896]{1,0:T(8,128)(2,1)S(1)} fusion(bf16[2048,3584]{1,0:T(8,128)(2,1)} %param.27, s32[]{:T(128)S(6)} %select_n.147, bf16[4,8,2048]{2,1,0:T(8,128)(2,1)S(1)} %gather_fusion.7, pred[4]{0:T(512)(128)(4,1)S(1)} %get-tuple-element.62), kind=kOutput, calls=%fused_computation.43 | convolution fusion | flops 117534720 | bytes 3858440 | tf_op jit(solution)/shard_map/dot_general | solution.py:123
  92.1 2.9 %fusion.41 = bf16[32,896]{1,0:T(8,128)(2,1)S(1)} fusion(bf16[2048,3584]{1,0:T(8,128)(2,1)} %param.28, s32[]{:T(128)S(6)} %select_n.146, bf16[4,8,2048]{2,1,0:T(8,128)(2,1)S(1)} %gather_fusion.7, pred[4]{0:T(512)(128)(4,1)S(1)} %get-tuple-element.62), kind=kOutput, calls=%fused_computation.42 | convolution fusion | flops 117534720 | bytes 3858440 | tf_op jit(solution)/shard_map/dot_general | solution.py:123
  95.5 1.9 %collective-permute-start.22 = (bf16[32,1792]{1,0:T(8,128)(2,1)S(1)}, bf16[32,1792]{1,0:T(8,128)(2,1)S(1)}, u32[]{:S(2)}, u32[]{:S(2)}) collective-permute-start(bf16[32,1792]{1,0:T(8,128)(2,1)S(1)} %pad_maximum_fusion.4), channel_id=1, source_target_pairs={{0,8},{4,12},{8,0},{12,4},{1,9},{5,13},{9,1},{13,5},{2,10},{6,14},... | collective-permute-start | bytes 344072 | tf_op jit(solution)/shard_map/ppermute | solution.py:134
  97.4 2.0 %collective-permute-start.23 = (bf16[32,1792]{1,0:T(8,128)(2,1)S(1)}, bf16[32,1792]{1,0:T(8,128)(2,1)S(1)}, u32[]{:S(2)}, u32[]{:S(2)}) collective-permute-start(bf16[32,1792]{1,0:T(8,128)(2,1)S(1)} %pad_maximum_fusion.5), channel_id=1, source_target_pairs={{0,12},{4,0},{8,4},{12,8},{1,13},{5,1},{9,5},{13,9},{2,14},{6,2},{... | collective-permute-start | bytes 344072 | tf_op jit(solution)/shard_map/ppermute | solution.py:134
  99.3 2.8 %fusion.38 = bf16[32,896]{1,0:T(8,128)(2,1)S(1)} fusion(bf16[2048,3584]{1,0:T(8,128)(2,1)} %param.27, s32[]{:T(128)S(6)} %select_n.146, bf16[4,8,2048]{2,1,0:T(8,128)(2,1)S(1)} %gather_fusion.7, pred[4]{0:T(512)(128)(4,1)S(1)} %get-tuple-element.62), kind=kOutput, calls=%fused_computation.41 | convolution fusion | flops 117534720 | bytes 3858440 | tf_op jit(solution)/shard_map/dot_general | solution.py:123
  103.3 4.1 %collective-permute-done.22 = bf16[32,1792]{1,0:T(8,128)(2,1)S(1)} collective-permute-done((bf16[32,1792]{1,0:T(8,128)(2,1)S(1)}, bf16[32,1792]{1,0:T(8,128)(2,1)S(1)}, u32[]{:S(2)}, u32[]{:S(2)}) %collective-permute-start.22) | collective-permute-done | bytes 114720 | tf_op jit(solution)/shard_map/ppermute | solution.py:134
  107.5 3.3 %collective-permute-start.26 = (bf16[32,896]{1,0:T(8,128)(2,1)S(1)}, bf16[32,896]{1,0:T(8,128)(2,1)S(1)}, u32[]{:S(2)}, u32[]{:S(2)}) collective-permute-start(bf16[32,896]{1,0:T(8,128)(2,1)S(1)} %fusion.76), channel_id=1, source_target_pairs={{0,12},{4,0},{8,4},{12,8},{1,13},{5,1},{9,5},{13,9},{2,14},{6,2},{... | collective-permute-start | bytes 172040 | tf_op jit(solution)/shard_map/ppermute | solution.py:147
  112.7 4.4 %collective-permute-done.25 = bf16[32,896]{1,0:T(8,128)(2,1)S(1)} collective-permute-done((bf16[32,896]{1,0:T(8,128)(2,1)S(1)}, bf16[32,896]{1,0:T(8,128)(2,1)S(1)}, u32[]{:S(2)}, u32[]{:S(2)}) %collective-permute-start.25) | collective-permute-done | bytes 57376 | tf_op jit(solution)/shard_map/ppermute | solution.py:147
  119.6 1.7 %collective-permute-start.29 = (f32[8,2048]{1,0:T(8,128)S(1)}, f32[8,2048]{1,0:T(8,128)S(1)}, u32[]{:S(2)}, u32[]{:S(2)}) collective-permute-start(f32[8,2048]{1,0:T(8,128)S(1)} %get-tuple-element.46), channel_id=1, source_target_pairs={{0,3},{1,0},{2,1},{3,2},{4,7},{5,4},{6,5},{7,6},{8,11},{9,8},{10,9... | collective-permute-start | bytes 196616 | tf_op jit(solution)/shard_map/ppermute | solution.py:106
  123.3 2.3 %collective-permute-done.28 = f32[8,2048]{1,0:T(8,128)S(1)} collective-permute-done((f32[8,2048]{1,0:T(8,128)S(1)}, f32[8,2048]{1,0:T(8,128)S(1)}, u32[]{:S(2)}, u32[]{:S(2)}) %collective-permute-start.28) | collective-permute-done | bytes 65568 | tf_op jit(solution)/shard_map/ppermute | solution.py:106
  (126 shorter events, 36.8 us)
Async XLA Ops:
  0.9 14.6 %collective-permute-start.2 = (f32[8]{0:T(128)S(1)}, f32[8]{0:T(128)S(1)}, u32[]{:S(2)}, u32[]{:S(2)}) collective-permute-start(f32[8]{0:T(128)S(1)} %fusion.80), channel_id=1, source_target_pairs={{0,12},{4,0},{8,4},{12,8},{1,13},{5,1},{9,5},{13,9},{2,14},{6,2},{... | collective-permute-start | bytes 104 | tf_op jit(solution)/shard_map/ppermute | solution.py:113
  6.0 9.5 %collective-permute-start.1 = (f32[8]{0:T(128)S(1)}, f32[8]{0:T(128)S(1)}, u32[]{:S(2)}, u32[]{:S(2)}) collective-permute-start(f32[8]{0:T(128)S(1)} %fusion.80), channel_id=1, source_target_pairs={{0,8},{4,12},{8,0},{12,4},{1,9},{5,13},{9,1},{13,5},{2,10},{6,14},... | collective-permute-start | bytes 104 | tf_op jit(solution)/shard_map/ppermute | solution.py:113
  6.0 9.6 %collective-permute-start = (f32[8]{0:T(128)S(1)}, f32[8]{0:T(128)S(1)}, u32[]{:S(2)}, u32[]{:S(2)}) collective-permute-start(f32[8]{0:T(128)S(1)} %fusion.80), channel_id=1, source_target_pairs={{0,4},{4,8},{8,12},{12,0},{1,5},{5,9},{9,13},{13,1},{2,6},{6,10},{... | collective-permute-start | bytes 104 | tf_op jit(solution)/shard_map/ppermute | solution.py:113
  16.4 4.2 %collective-permute-start.4 = (bf16[8,2048]{1,0:T(8,128)(2,1)S(1)}, bf16[8,2048]{1,0:T(8,128)(2,1)S(1)}, u32[]{:S(2)}, u32[]{:S(2)}) collective-permute-start(bf16[8,2048]{1,0:T(8,128)(2,1)S(1)} %fusion.82), channel_id=1, source_target_pairs={{0,2},{1,3},{2,0},{3,1},{4,6},{5,7},{6,4},{7,5},{8,10},{9,11},{10,... | collective-permute-start | bytes 98312 | tf_op jit(solution)/shard_map/ppermute | solution.py:96
  18.0 3.3 %collective-permute-start.3 = (bf16[8,2048]{1,0:T(8,128)(2,1)S(1)}, bf16[8,2048]{1,0:T(8,128)(2,1)S(1)}, u32[]{:S(2)}, u32[]{:S(2)}) collective-permute-start(bf16[8,2048]{1,0:T(8,128)(2,1)S(1)} %fusion.82), channel_id=1, source_target_pairs={{0,1},{1,2},{2,3},{3,0},{4,5},{5,6},{6,7},{7,4},{8,9},{9,10},{10,1... | collective-permute-start | bytes 98312 | tf_op jit(solution)/shard_map/ppermute | solution.py:96
  18.0 3.3 %collective-permute-start.5 = (bf16[8,2048]{1,0:T(8,128)(2,1)S(1)}, bf16[8,2048]{1,0:T(8,128)(2,1)S(1)}, u32[]{:S(2)}, u32[]{:S(2)}) collective-permute-start(bf16[8,2048]{1,0:T(8,128)(2,1)S(1)} %fusion.82), channel_id=1, source_target_pairs={{0,3},{1,0},{2,1},{3,2},{4,7},{5,4},{6,5},{7,6},{8,11},{9,8},{10,9... | collective-permute-start | bytes 98312 | tf_op jit(solution)/shard_map/ppermute | solution.py:96
  29.2 7.2 %collective-permute-start.6 = (f32[8,2560]{1,0:T(8,128)S(1)}, f32[8,2560]{1,0:T(8,128)S(1)}, u32[]{:S(2)}, u32[]{:S(2)}) collective-permute-start(f32[8,2560]{1,0:T(8,128)S(1)} %get-tuple-element.42), channel_id=1, source_target_pairs={{0,4},{4,8},{8,12},{12,0},{1,5},{5,9},{9,13},{13,1},{2,6},{6,10},{... | collective-permute-start | bytes 245768 | tf_op jit(solution)/shard_map/ppermute | solution.py:106
  31.7 6.1 %collective-permute-start.8 = (f32[8,2560]{1,0:T(8,128)S(1)}, f32[8,2560]{1,0:T(8,128)S(1)}, u32[]{:S(2)}, u32[]{:S(2)}) collective-permute-start(f32[8,2560]{1,0:T(8,128)S(1)} %get-tuple-element.43), channel_id=1, source_target_pairs={{0,12},{4,0},{8,4},{12,8},{1,13},{5,1},{9,5},{13,9},{2,14},{6,2},{... | collective-permute-start | bytes 245768 | tf_op jit(solution)/shard_map/ppermute | solution.py:106
  33.0 8.2 %collective-permute-start.7 = (f32[8,2560]{1,0:T(8,128)S(1)}, f32[8,2560]{1,0:T(8,128)S(1)}, u32[]{:S(2)}, u32[]{:S(2)}) collective-permute-start(f32[8,2560]{1,0:T(8,128)S(1)} %get-tuple-element.44), channel_id=1, source_target_pairs={{0,8},{4,12},{8,0},{12,4},{1,9},{5,13},{9,1},{13,5},{2,10},{6,14},... | collective-permute-start | bytes 245768 | tf_op jit(solution)/shard_map/ppermute | solution.py:106
  42.7 4.0 %collective-permute-start.11 = (bf16[8,2048]{1,0:T(8,128)(2,1)S(1)}, bf16[8,2048]{1,0:T(8,128)(2,1)S(1)}, u32[]{:S(2)}, u32[]{:S(2)}) collective-permute-start(bf16[8,2048]{1,0:T(8,128)(2,1)S(1)} %bitcast.126), channel_id=1, source_target_pairs={{0,12},{4,0},{8,4},{12,8},{1,13},{5,1},{9,5},{13,9},{2,14},{6,2},{... | collective-permute-start | bytes 98312 | tf_op jit(solution)/shard_map/ppermute | solution.py:96
  44.4 5.0 %collective-permute-start.10 = (bf16[8,2048]{1,0:T(8,128)(2,1)S(1)}, bf16[8,2048]{1,0:T(8,128)(2,1)S(1)}, u32[]{:S(2)}, u32[]{:S(2)}) collective-permute-start(bf16[8,2048]{1,0:T(8,128)(2,1)S(1)} %bitcast.127), channel_id=1, source_target_pairs={{0,8},{4,12},{8,0},{12,4},{1,9},{5,13},{9,1},{13,5},{2,10},{6,14},... | collective-permute-start | bytes 98312 | tf_op jit(solution)/shard_map/ppermute | solution.py:96
  44.4 5.7 %collective-permute-start.9 = (bf16[8,2048]{1,0:T(8,128)(2,1)S(1)}, bf16[8,2048]{1,0:T(8,128)(2,1)S(1)}, u32[]{:S(2)}, u32[]{:S(2)}) collective-permute-start(bf16[8,2048]{1,0:T(8,128)(2,1)S(1)} %bitcast.128), channel_id=1, source_target_pairs={{0,4},{4,8},{8,12},{12,0},{1,5},{5,9},{9,13},{13,1},{2,6},{6,10},{... | collective-permute-start | bytes 98312 | tf_op jit(solution)/shard_map/ppermute | solution.py:96
  56.5 3.7 %collective-permute-start.12 = (f32[8,2048]{1,0:T(8,128)S(1)}, f32[8,2048]{1,0:T(8,128)S(1)}, u32[]{:S(2)}, u32[]{:S(2)}) collective-permute-start(f32[8,2048]{1,0:T(8,128)S(1)} %get-tuple-element.48), channel_id=1, source_target_pairs={{0,1},{1,2},{2,3},{3,0},{4,5},{5,6},{6,7},{7,4},{8,9},{9,10},{10,1... | collective-permute-start | bytes 196616 | tf_op jit(solution)/shard_map/ppermute | solution.py:106
  56.5 4.1 %collective-permute-start.14 = (f32[8,2048]{1,0:T(8,128)S(1)}, f32[8,2048]{1,0:T(8,128)S(1)}, u32[]{:S(2)}, u32[]{:S(2)}) collective-permute-start(f32[8,2048]{1,0:T(8,128)S(1)} %get-tuple-element.49), channel_id=1, source_target_pairs={{0,3},{1,0},{2,1},{3,2},{4,7},{5,4},{6,5},{7,6},{8,11},{9,8},{10,9... | collective-permute-start | bytes 196616 | tf_op jit(solution)/shard_map/ppermute | solution.py:106
  58.3 4.6 %collective-permute-start.13 = (f32[8,2048]{1,0:T(8,128)S(1)}, f32[8,2048]{1,0:T(8,128)S(1)}, u32[]{:S(2)}, u32[]{:S(2)}) collective-permute-start(f32[8,2048]{1,0:T(8,128)S(1)} %get-tuple-element.50), channel_id=1, source_target_pairs={{0,2},{1,3},{2,0},{3,1},{4,6},{5,7},{6,4},{7,5},{8,10},{9,11},{10,... | collective-permute-start | bytes 196616 | tf_op jit(solution)/shard_map/ppermute | solution.py:106
  63.0 3.6 %collective-permute-start.17 = (f32[8]{0:T(128)S(1)}, f32[8]{0:T(128)S(1)}, u32[]{:S(2)}, u32[]{:S(2)}) collective-permute-start(f32[8]{0:T(128)S(1)} %get-tuple-element.32), channel_id=1, source_target_pairs={{0,12},{4,0},{8,4},{12,8},{1,13},{5,1},{9,5},{13,9},{2,14},{6,2},{... | collective-permute-start | bytes 104 | tf_op jit(solution)/shard_map/ppermute | solution.py:113
  63.7 4.4 %collective-permute-start.16 = (f32[8]{0:T(128)S(1)}, f32[8]{0:T(128)S(1)}, u32[]{:S(2)}, u32[]{:S(2)}) collective-permute-start(f32[8]{0:T(128)S(1)} %get-tuple-element.32), channel_id=1, source_target_pairs={{0,8},{4,12},{8,0},{12,4},{1,9},{5,13},{9,1},{13,5},{2,10},{6,14},... | collective-permute-start | bytes 104 | tf_op jit(solution)/shard_map/ppermute | solution.py:113
  64.3 5.3 %collective-permute-start.15 = (f32[8]{0:T(128)S(1)}, f32[8]{0:T(128)S(1)}, u32[]{:S(2)}, u32[]{:S(2)}) collective-permute-start(f32[8]{0:T(128)S(1)} %get-tuple-element.32), channel_id=1, source_target_pairs={{0,4},{4,8},{8,12},{12,0},{1,5},{5,9},{9,13},{13,1},{2,6},{6,10},{... | collective-permute-start | bytes 104 | tf_op jit(solution)/shard_map/ppermute | solution.py:113
  69.7 4.0 %collective-permute-start.19 = (bf16[8,2048]{1,0:T(8,128)(2,1)S(1)}, bf16[8,2048]{1,0:T(8,128)(2,1)S(1)}, u32[]{:S(2)}, u32[]{:S(2)}) collective-permute-start(bf16[8,2048]{1,0:T(8,128)(2,1)S(1)} %multiply_convert_fusion), channel_id=1, source_target_pairs={{0,2},{1,3},{2,0},{3,1},{4,6},{5,7},{6,4},{7,5},{8,10},{9,11},{10,... | collective-permute-start | bytes 98312 | tf_op jit(solution)/shard_map/ppermute | solution.py:96
  70.9 3.3 %collective-permute-start.18 = (bf16[8,2048]{1,0:T(8,128)(2,1)S(1)}, bf16[8,2048]{1,0:T(8,128)(2,1)S(1)}, u32[]{:S(2)}, u32[]{:S(2)}) collective-permute-start(bf16[8,2048]{1,0:T(8,128)(2,1)S(1)} %multiply_convert_fusion), channel_id=1, source_target_pairs={{0,1},{1,2},{2,3},{3,0},{4,5},{5,6},{6,7},{7,4},{8,9},{9,10},{10,1... | collective-permute-start | bytes 98312 | tf_op jit(solution)/shard_map/ppermute | solution.py:96
  70.9 3.3 %collective-permute-start.20 = (bf16[8,2048]{1,0:T(8,128)(2,1)S(1)}, bf16[8,2048]{1,0:T(8,128)(2,1)S(1)}, u32[]{:S(2)}, u32[]{:S(2)}) collective-permute-start(bf16[8,2048]{1,0:T(8,128)(2,1)S(1)} %multiply_convert_fusion), channel_id=1, source_target_pairs={{0,3},{1,0},{2,1},{3,2},{4,7},{5,4},{6,5},{7,6},{8,11},{9,8},{10,9... | collective-permute-start | bytes 98312 | tf_op jit(solution)/shard_map/ppermute | solution.py:96
  77.6 34.4 %slice-start = ((s8[14680064]{0:T(1024)(128)(4,1)}), s8[4194304]{0:T(1024)(128)(4,1)S(1)}, s32[]{:S(2)}) async-start(s8[14680064]{0:T(1024)(128)(4,1)} %bitcast.116), calls=%async_computation | async-start | bytes 8388608
  80.6 31.4 %slice-start.1 = ((s8[14680064]{0:T(1024)(128)(4,1)}), s8[4194304]{0:T(1024)(128)(4,1)S(1)}, s32[]{:S(2)}) async-start(s8[14680064]{0:T(1024)(128)(4,1)} %bitcast.116), calls=%async_computation.1 | async-start | bytes 8388608
  95.1 8.2 %collective-permute-start.21 = (bf16[32,1792]{1,0:T(8,128)(2,1)S(1)}, bf16[32,1792]{1,0:T(8,128)(2,1)S(1)}, u32[]{:S(2)}, u32[]{:S(2)}) collective-permute-start(bf16[32,1792]{1,0:T(8,128)(2,1)S(1)} %pad_maximum_fusion.3), channel_id=1, source_target_pairs={{0,4},{4,8},{8,12},{12,0},{1,5},{5,9},{9,13},{13,1},{2,6},{6,10},{... | collective-permute-start | bytes 344072 | tf_op jit(solution)/shard_map/ppermute | solution.py:134
  95.5 11.9 %collective-permute-start.22 = (bf16[32,1792]{1,0:T(8,128)(2,1)S(1)}, bf16[32,1792]{1,0:T(8,128)(2,1)S(1)}, u32[]{:S(2)}, u32[]{:S(2)}) collective-permute-start(bf16[32,1792]{1,0:T(8,128)(2,1)S(1)} %pad_maximum_fusion.4), channel_id=1, source_target_pairs={{0,8},{4,12},{8,0},{12,4},{1,9},{5,13},{9,1},{13,5},{2,10},{6,14},... | collective-permute-start | bytes 344072 | tf_op jit(solution)/shard_map/ppermute | solution.py:134
  97.4 10.1 %collective-permute-start.23 = (bf16[32,1792]{1,0:T(8,128)(2,1)S(1)}, bf16[32,1792]{1,0:T(8,128)(2,1)S(1)}, u32[]{:S(2)}, u32[]{:S(2)}) collective-permute-start(bf16[32,1792]{1,0:T(8,128)(2,1)S(1)} %pad_maximum_fusion.5), channel_id=1, source_target_pairs={{0,12},{4,0},{8,4},{12,8},{1,13},{5,1},{9,5},{13,9},{2,14},{6,2},{... | collective-permute-start | bytes 344072 | tf_op jit(solution)/shard_map/ppermute | solution.py:134
  107.5 10.4 %collective-permute-start.26 = (bf16[32,896]{1,0:T(8,128)(2,1)S(1)}, bf16[32,896]{1,0:T(8,128)(2,1)S(1)}, u32[]{:S(2)}, u32[]{:S(2)}) collective-permute-start(bf16[32,896]{1,0:T(8,128)(2,1)S(1)} %fusion.76), channel_id=1, source_target_pairs={{0,12},{4,0},{8,4},{12,8},{1,13},{5,1},{9,5},{13,9},{2,14},{6,2},{... | collective-permute-start | bytes 172040 | tf_op jit(solution)/shard_map/ppermute | solution.py:147
  110.8 6.4 %collective-permute-start.25 = (bf16[32,896]{1,0:T(8,128)(2,1)S(1)}, bf16[32,896]{1,0:T(8,128)(2,1)S(1)}, u32[]{:S(2)}, u32[]{:S(2)}) collective-permute-start(bf16[32,896]{1,0:T(8,128)(2,1)S(1)} %fusion.76), channel_id=1, source_target_pairs={{0,8},{4,12},{8,0},{12,4},{1,9},{5,13},{9,1},{13,5},{2,10},{6,14},... | collective-permute-start | bytes 172040 | tf_op jit(solution)/shard_map/ppermute | solution.py:147
  112.0 6.7 %collective-permute-start.24 = (bf16[32,896]{1,0:T(8,128)(2,1)S(1)}, bf16[32,896]{1,0:T(8,128)(2,1)S(1)}, u32[]{:S(2)}, u32[]{:S(2)}) collective-permute-start(bf16[32,896]{1,0:T(8,128)(2,1)S(1)} %fusion.76), channel_id=1, source_target_pairs={{0,4},{4,8},{8,12},{12,0},{1,5},{5,9},{9,13},{13,1},{2,6},{6,10},{... | collective-permute-start | bytes 172040 | tf_op jit(solution)/shard_map/ppermute | solution.py:147
  119.5 3.7 %collective-permute-start.27 = (f32[8,2048]{1,0:T(8,128)S(1)}, f32[8,2048]{1,0:T(8,128)S(1)}, u32[]{:S(2)}, u32[]{:S(2)}) collective-permute-start(f32[8,2048]{1,0:T(8,128)S(1)} %get-tuple-element.45), channel_id=1, source_target_pairs={{0,1},{1,2},{2,3},{3,0},{4,5},{5,6},{6,7},{7,4},{8,9},{9,10},{10,1... | collective-permute-start | bytes 196616 | tf_op jit(solution)/shard_map/ppermute | solution.py:106
  119.6 3.7 %collective-permute-start.29 = (f32[8,2048]{1,0:T(8,128)S(1)}, f32[8,2048]{1,0:T(8,128)S(1)}, u32[]{:S(2)}, u32[]{:S(2)}) collective-permute-start(f32[8,2048]{1,0:T(8,128)S(1)} %get-tuple-element.46), channel_id=1, source_target_pairs={{0,3},{1,0},{2,1},{3,2},{4,7},{5,4},{6,5},{7,6},{8,11},{9,8},{10,9... | collective-permute-start | bytes 196616 | tf_op jit(solution)/shard_map/ppermute | solution.py:106
  121.3 4.3 %collective-permute-start.28 = (f32[8,2048]{1,0:T(8,128)S(1)}, f32[8,2048]{1,0:T(8,128)S(1)}, u32[]{:S(2)}, u32[]{:S(2)}) collective-permute-start(f32[8,2048]{1,0:T(8,128)S(1)} %get-tuple-element.47), channel_id=1, source_target_pairs={{0,2},{1,3},{2,0},{3,1},{4,6},{5,7},{6,4},{7,5},{8,10},{9,11},{10,... | collective-permute-start | bytes 196616 | tf_op jit(solution)/shard_map/ppermute | solution.py:106
  (6 other events, 130.7 us)

commit v4 on v2

--- a/solution.py
+++ b/solution.py
@@ -112,6 +112,19 @@
     for k in range(1, n):
         total = total + lax.ppermute(x, axis, shift_pairs(n, k))
     return total
+
+
+def gather_matmul(x, w, axis, n):
+    idx = lax.axis_index(axis)
+    chunk = x.shape[1]
+    acc = jnp.dot(
+        x, lax.dynamic_slice_in_dim(w, idx * chunk, chunk, 0), preferred_element_type=jnp.float32
+    )
+    for k in range(1, n):
+        got = lax.ppermute(x, axis, shift_pairs(n, k))
+        rows = lax.dynamic_slice_in_dim(w, ((idx - k) % n) * chunk, chunk, 0)
+        acc = acc + jnp.dot(got, rows, preferred_element_type=jnp.float32)
+    return acc
 
 
 def local(
@@ -167,18 +180,16 @@
         residual * lax.rsqrt(squares_mid / D + epsilon)[:, None] * ffn_gain[None, :]
     ).astype(jnp.bfloat16)
     ffn_all = gather_blocks(ffn_normed, CS, n_cs).reshape(rows_total, -1)
+    chunk = w_gate.shape[1] // n_pool
     gate_part = jnp.dot(ffn_all, w_gate, preferred_element_type=jnp.float32).astype(jnp.bfloat16)
     up_part = jnp.dot(ffn_all, w_up, preferred_element_type=jnp.float32).astype(jnp.bfloat16)
-    hidden_cols = w_gate.shape[1]
-    chunk = hidden_cols // n_pool
     gate_blocks = gate_part.reshape(rows_total, n_pool, chunk).transpose(1, 0, 2)
     up_blocks = up_part.reshape(rows_total, n_pool, chunk).transpose(1, 0, 2)
     both = scatter_sum(jnp.concatenate([gate_blocks, up_blocks], axis=2), "pool", n_pool)
     gate_total = both[:, :chunk]
     up_total = both[:, chunk:]
     hidden = (jax.nn.silu(gate_total) * up_total).astype(jnp.bfloat16)
-    hidden_all = gather_blocks(hidden, "pool", n_pool).transpose(1, 0, 2).reshape(rows_total, -1)
-    down_part = jnp.dot(hidden_all, w_down, preferred_element_type=jnp.float32)
+    down_part = gather_matmul(hidden, w_down, "pool", n_pool)
     return residual + scatter_sum(down_part.reshape(n_cs, rows_here, -1), CS, n_cs)
 
 

time: 128 us -> 129 us (level)
  matrix products: 35.2 us -> 38.7 us
  starting transfers between devices: 37.8 us -> 36.3 us
    ppermute x12 -> x9, starting transfers between devices: 14.4 us -> 8.56 us  [gather_blocks(): got = [x] + [lax.ppermute(x, axis, shift_pairs(n, k)) for k in range(1, n)]]
    ppermute x0 -> x3, starting transfers between devices: none -> 4.48 us  [gather_matmul(): got = lax.ppermute(x, axis, shift_pairs(n, k))]
    dot_general x1 -> x4, matrix products: 7.7 us -> 11.1 us  [the longest x3 8.35 us: gather_matmul(): acc = acc + jnp.dot(got, rows, preferred_element_type=jnp.float32)]
    ppermute x12 -> x9, waiting for transfers between devices: 10.5 us -> 7.31 us  [gather_blocks(): got = [x] + [lax.ppermute(x, axis, shift_pairs(n, k)) for k in range(1, n)]]
    ppermute x0 -> x3, waiting for transfers between devices: none -> 2.48 us  [gather_matmul(): got = lax.ppermute(x, axis, shift_pairs(n, k))]
  transfers between devices with their start and end apart: 30 -> 30, of which waited for: 20 -> 20; matrix products, arithmetic and copies ran while one was open for 7% -> 14% of each run, Pallas kernels for 0% -> 0%
where the time goes in v4:
time: 129 us; the launch traced here: 128 us
  matrix products  38.7 us (30%)
  starting transfers between devices  36.3 us (28%)
  waiting for transfers between devices  36 us (28%)
  local copies, waits for them, and re-layouts  9.73 us (8%)
  other arithmetic  6.8 us (5%)
    ppermute x12, waiting for transfers between devices, scatter_sum(): lax.ppermute(piece, axis, shift_pairs(n, k)).astype(jnp.float32)  22.8 us
    ppermute x12, starting transfers between devices, scatter_sum(): lax.ppermute(piece, axis, shift_pairs(n, k)).astype(jnp.float32)  14 us
    ppermute x6, starting transfers between devices, all_sum(): total = total + lax.ppermute(x, axis, shift_pairs(n, k))  9.3 us
    ppermute x9, starting transfers between devices, gather_blocks(): got = [x] + [lax.ppermute(x, axis, shift_pairs(n, k)) for k in range(1, n)]  8.56 us
    dot_general x3, matrix products, gather_matmul(): acc = acc + jnp.dot(got, rows, preferred_element_type=jnp.float32)  8.35 us
    dot_general x1, matrix products, local(): jnp.dot(ffn_all, w_gate, preferred_element_type=jnp.float32)  7.85 us
    dot_general x1, matrix products, local(): jnp.dot(ffn_all, w_up, preferred_element_type=jnp.float32)  7.85 us
    ppermute x9, waiting for transfers between devices, gather_blocks(): got = [x] + [lax.ppermute(x, axis, shift_pairs(n, k)) for k in range(1, n)]  7.31 us
  transfers between devices with their start and end apart: 30, of which 20 were waited for; matrix products, arithmetic and copies ran while one was open for 14% of the time, Pallas kernels for 0%

profile of v4, /device:TPU:0, one launch (start us, length us, event | category | flops | bytes accessed | tf_op | source)
XLA Modules:
  0.0 127.9 jit_solution(6256072651183829192)
XLA Ops:
  0.9 5.1 %collective-permute-start.2 = (f32[8]{0:T(128)S(1)}, f32[8]{0:T(128)S(1)}, u32[]{:S(2)}, u32[]{:S(2)}) collective-permute-start(f32[8]{0:T(128)S(1)} %fusion.46), channel_id=1, source_target_pairs={{0,12},{4,0},{8,4},{12,8},{1,13},{5,1},{9,5},{13,9},{2,14},{6,2},{... | collective-permute-start | bytes 104 | tf_op jit(solution)/shard_map/ppermute | solution.py:113
  12.7 2.7 %fusion.82 = (bf16[8,256,1,2,128]{4,3,2,1,0:T(2,128)(2,1)S(1)}, bf16[8,256,1,2,128]{4,3,2,1,0:T(2,128)(2,1)S(1)}) fusion(bf16[8,256,2,2,128]{4,3,2,1,0:T(2,128)(2,1)} %param.32), kind=kLoop, calls=%fused_computation.166 | loop fusion | bytes 4194304 | tf_op jit(solution)/shard_map/slice | solution.py:56
  16.4 1.6 %collective-permute-start.4 = (bf16[8,2048]{1,0:T(8,128)(2,1)S(1)}, bf16[8,2048]{1,0:T(8,128)(2,1)S(1)}, u32[]{:S(2)}, u32[]{:S(2)}) collective-permute-start(bf16[8,2048]{1,0:T(8,128)(2,1)S(1)} %fusion.48), channel_id=1, source_target_pairs={{0,2},{1,3},{2,0},{3,1},{4,6},{5,7},{6,4},{7,5},{8,10},{9,11},{10,... | collective-permute-start | bytes 98312 | tf_op jit(solution)/shard_map/ppermute | solution.py:96
  18.0 1.7 %collective-permute-start.5 = (bf16[8,2048]{1,0:T(8,128)(2,1)S(1)}, bf16[8,2048]{1,0:T(8,128)(2,1)S(1)}, u32[]{:S(2)}, u32[]{:S(2)}) collective-permute-start(bf16[8,2048]{1,0:T(8,128)(2,1)S(1)} %fusion.48), channel_id=1, source_target_pairs={{0,3},{1,0},{2,1},{3,2},{4,7},{5,4},{6,5},{7,6},{8,11},{9,8},{10,9... | collective-permute-start | bytes 98312 | tf_op jit(solution)/shard_map/ppermute | solution.py:96
  22.6 5.9 %fusion = f32[32,2,1280]{2,0,1:T(8,128)S(1)} fusion(bf16[2048,2,1280]{2,1,0:T(2,128)(2,1)} %param.26, bf16[32,2048]{1,0:T(8,128)(2,1)S(1)} %gather_fusion.4, pred[32]{0:T(512)(128)(4,1)S(1)} %get-tuple-element.51), kind=kOutput, calls=%fused_computation.9 | convolution fusion | flops 335609856 | bytes 10944544 | tf_op jit(solution)/shard_map/rf,fgc->rgc/dot_general | solution.py:166
  29.2 2.5 %collective-permute-start.6 = (f32[8,2560]{1,0:T(8,128)S(1)}, f32[8,2560]{1,0:T(8,128)S(1)}, u32[]{:S(2)}, u32[]{:S(2)}) collective-permute-start(f32[8,2560]{1,0:T(8,128)S(1)} %get-tuple-element.57), channel_id=1, source_target_pairs={{0,4},{4,8},{8,12},{12,0},{1,5},{5,9},{9,13},{13,1},{2,6},{6,10},{... | collective-permute-start | bytes 245768 | tf_op jit(solution)/shard_map/ppermute | solution.py:106
  33.2 3.1 %collective-permute-done.6 = f32[8,2560]{1,0:T(8,128)S(1)} collective-permute-done((f32[8,2560]{1,0:T(8,128)S(1)}, f32[8,2560]{1,0:T(8,128)S(1)}, u32[]{:S(2)}, u32[]{:S(2)}) %collective-permute-start.6) | collective-permute-done | bytes 81952 | tf_op jit(solution)/shard_map/ppermute | solution.py:106
  37.8 3.5 %collective-permute-done.7 = f32[8,2560]{1,0:T(8,128)S(1)} collective-permute-done((f32[8,2560]{1,0:T(8,128)S(1)}, f32[8,2560]{1,0:T(8,128)S(1)}, u32[]{:S(2)}, u32[]{:S(2)}) %collective-permute-start.7) | collective-permute-done | bytes 81952 | tf_op jit(solution)/shard_map/ppermute | solution.py:106
  42.7 1.7 %collective-permute-start.11 = (bf16[8,2048]{1,0:T(8,128)(2,1)S(1)}, bf16[8,2048]{1,0:T(8,128)(2,1)S(1)}, u32[]{:S(2)}, u32[]{:S(2)}) collective-permute-start(bf16[8,2048]{1,0:T(8,128)(2,1)S(1)} %bitcast.144), channel_id=1, source_target_pairs={{0,12},{4,0},{8,4},{12,8},{1,13},{5,1},{9,5},{13,9},{2,14},{6,2},{... | collective-permute-start | bytes 98312 | tf_op jit(solution)/shard_map/ppermute | solution.py:96
  45.1 1.6 %collective-permute-done.11 = bf16[8,2048]{1,0:T(8,128)(2,1)S(1)} collective-permute-done((bf16[8,2048]{1,0:T(8,128)(2,1)S(1)}, bf16[8,2048]{1,0:T(8,128)(2,1)S(1)}, u32[]{:S(2)}, u32[]{:S(2)}) %collective-permute-start.11) | collective-permute-done | bytes 32800 | tf_op jit(solution)/shard_map/ppermute | solution.py:96
  46.7 2.7 %collective-permute-done.10 = bf16[8,2048]{1,0:T(8,128)(2,1)S(1)} collective-permute-done((bf16[8,2048]{1,0:T(8,128)(2,1)S(1)}, bf16[8,2048]{1,0:T(8,128)(2,1)S(1)}, u32[]{:S(2)}, u32[]{:S(2)}) %collective-permute-start.10) | collective-permute-done | bytes 32800 | tf_op jit(solution)/shard_map/ppermute | solution.py:96
  51.5 5.0 %convolution_bitcast_fusion = f32[4,8,2048]{2,1,0:T(8,128)S(1)} fusion(bf16[2048,2048]{1,0:T(8,128)(2,1)} %param.27, bf16[32,2048]{1,0:T(8,128)(2,1)S(1)} %gather_fusion.6, pred[32]{0:T(512)(128)(4,1)S(1)} %get-tuple-element.46), kind=kOutput, calls=%fused_computation.25 | convolution fusion | flops 268500992 | bytes 8781856 | tf_op jit(solution)/shard_map/dot_general | solution.py:175
  56.5 1.7 %collective-permute-start.14 = (f32[8,2048]{1,0:T(8,128)S(1)}, f32[8,2048]{1,0:T(8,128)S(1)}, u32[]{:S(2)}, u32[]{:S(2)}) collective-permute-start(f32[8,2048]{1,0:T(8,128)S(1)} %get-tuple-element.64), channel_id=1, source_target_pairs={{0,3},{1,0},{2,1},{3,2},{4,7},{5,4},{6,5},{7,6},{8,11},{9,8},{10,9... | collective-permute-start | bytes 196616 | tf_op jit(solution)/shard_map/ppermute | solution.py:106
  58.3 1.5 %collective-permute-start.13 = (f32[8,2048]{1,0:T(8,128)S(1)}, f32[8,2048]{1,0:T(8,128)S(1)}, u32[]{:S(2)}, u32[]{:S(2)}) collective-permute-start(f32[8,2048]{1,0:T(8,128)S(1)} %get-tuple-element.65), channel_id=1, source_target_pairs={{0,2},{1,3},{2,0},{3,1},{4,6},{5,7},{6,4},{7,5},{8,10},{9,11},{10,... | collective-permute-start | bytes 196616 | tf_op jit(solution)/shard_map/ppermute | solution.py:106
  60.6 2.2 %collective-permute-done.13 = f32[8,2048]{1,0:T(8,128)S(1)} collective-permute-done((f32[8,2048]{1,0:T(8,128)S(1)}, f32[8,2048]{1,0:T(8,128)S(1)}, u32[]{:S(2)}, u32[]{:S(2)}) %collective-permute-start.13) | collective-permute-done | bytes 65568 | tf_op jit(solution)/shard_map/ppermute | solution.py:106
  64.2 1.9 %collective-permute-start.15 = (f32[8]{0:T(128)S(1)}, f32[8]{0:T(128)S(1)}, u32[]{:S(2)}, u32[]{:S(2)}) collective-permute-start(f32[8]{0:T(128)S(1)} %get-tuple-element.44), channel_id=1, source_target_pairs={{0,4},{4,8},{8,12},{12,0},{1,5},{5,9},{9,13},{13,1},{2,6},{6,10},{... | collective-permute-start | bytes 104 | tf_op jit(solution)/shard_map/ppermute | solution.py:113
  66.6 1.6 %collective-permute-done.16 = f32[8]{0:T(128)S(1)} collective-permute-done((f32[8]{0:T(128)S(1)}, f32[8]{0:T(128)S(1)}, u32[]{:S(2)}, u32[]{:S(2)}) %collective-permute-start.16) | collective-permute-done | bytes 64 | tf_op jit(solution)/shard_map/ppermute | solution.py:113
  70.9 1.7 %collective-permute-start.20 = (bf16[8,2048]{1,0:T(8,128)(2,1)S(1)}, bf16[8,2048]{1,0:T(8,128)(2,1)S(1)}, u32[]{:S(2)}, u32[]{:S(2)}) collective-permute-start(bf16[8,2048]{1,0:T(8,128)(2,1)S(1)} %multiply_convert_fusion), channel_id=1, source_target_pairs={{0,3},{1,0},{2,1},{3,2},{4,7},{5,4},{6,5},{7,6},{8,11},{9,8},{10,9... | collective-permute-start | bytes 98312 | tf_op jit(solution)/shard_map/ppermute | solution.py:96
  74.8 7.8 %convolution_convert_fusion = bf16[32,3584]{1,0:T(8,128)(2,1)S(1)} fusion(bf16[2048,3584]{1,0:T(8,128)(2,1)} %param.30, bf16[4,8,2048]{2,1,0:T(8,128)(2,1)S(1)} %gather_fusion.7, pred[4]{0:T(512)(128)(4,1)S(1)} %get-tuple-element.77), kind=kOutput, calls=%fused_computation.11 | convolution fusion | flops 469942272 | bytes 15040516 | tf_op jit(solution)/shard_map/dot_general | solution.py:185
  82.7 7.9 %convolution_convert_fusion.1 = bf16[32,3584]{1,0:T(8,128)(2,1)S(1)} fusion(bf16[2048,3584]{1,0:T(8,128)(2,1)} %param.29, bf16[4,8,2048]{2,1,0:T(8,128)(2,1)S(1)} %gather_fusion.7, pred[4]{0:T(512)(128)(4,1)S(1)} %get-tuple-element.77), kind=kOutput, calls=%fused_computation.12 | convolution fusion | flops 469942272 | bytes 15040516 | tf_op jit(solution)/shard_map/dot_general | solution.py:184
  91.1 1.8 %collective-permute-start.22 = (bf16[32,1792]{1,0:T(8,128)(2,1)S(1)}, bf16[32,1792]{1,0:T(8,128)(2,1)S(1)}, u32[]{:S(2)}, u32[]{:S(2)}) collective-permute-start(bf16[32,1792]{1,0:T(8,128)(2,1)S(1)} %get-tuple-element.55), channel_id=1, source_target_pairs={{0,8},{4,12},{8,0},{12,4},{1,9},{5,13},{9,1},{13,5},{2,10},{6,14},... | collective-permute-start | bytes 344072 | tf_op jit(solution)/shard_map/ppermute | solution.py:106
  92.9 1.9 %collective-permute-start.23 = (bf16[32,1792]{1,0:T(8,128)(2,1)S(1)}, bf16[32,1792]{1,0:T(8,128)(2,1)S(1)}, u32[]{:S(2)}, u32[]{:S(2)}) collective-permute-start(bf16[32,1792]{1,0:T(8,128)(2,1)S(1)} %get-tuple-element.56), channel_id=1, source_target_pairs={{0,12},{4,0},{8,4},{12,8},{1,13},{5,1},{9,5},{13,9},{2,14},{6,2},{... | collective-permute-start | bytes 344072 | tf_op jit(solution)/shard_map/ppermute | solution.py:106
  94.7 4.2 %collective-permute-done.21 = bf16[32,1792]{1,0:T(8,128)(2,1)S(1)} collective-permute-done((bf16[32,1792]{1,0:T(8,128)(2,1)S(1)}, bf16[32,1792]{1,0:T(8,128)(2,1)S(1)}, u32[]{:S(2)}, u32[]{:S(2)}) %collective-permute-start.21) | collective-permute-done | bytes 114720 | tf_op jit(solution)/shard_map/ppermute | solution.py:106
  98.9 4.0 %collective-permute-done.22 = bf16[32,1792]{1,0:T(8,128)(2,1)S(1)} collective-permute-done((bf16[32,1792]{1,0:T(8,128)(2,1)S(1)}, bf16[32,1792]{1,0:T(8,128)(2,1)S(1)}, u32[]{:S(2)}, u32[]{:S(2)}) %collective-permute-start.22) | collective-permute-done | bytes 114720 | tf_op jit(solution)/shard_map/ppermute | solution.py:106
  103.1 3.3 %collective-permute-start.26 = (bf16[32,896]{1,0:T(8,128)(2,1)S(1)}, bf16[32,896]{1,0:T(8,128)(2,1)S(1)}, u32[]{:S(2)}, u32[]{:S(2)}) collective-permute-start(bf16[32,896]{1,0:T(8,128)(2,1)S(1)} %fusion.42), channel_id=1, source_target_pairs={{0,12},{4,0},{8,4},{12,8},{1,13},{5,1},{9,5},{13,9},{2,14},{6,2},{... | collective-permute-start | bytes 172040 | tf_op jit(solution)/shard_map/ppermute | solution.py:124
  107.5 2.8 %fusion.8 = f32[32,2048]{1,0:T(8,128)S(1)} fusion(bf16[32,896]{1,0:T(8,128)(2,1)S(1)} %fusion.42, bf16[3584,2048]{1,0:T(8,128)(2,1)} %param.31, s32[]{:T(128)S(6)} %select_n.138), kind=kOutput, calls=%fused_computation.19 | convolution fusion | flops 117440512 | bytes 3989508 | tf_op jit(solution)/shard_map/dot_general | solution.py:120
  110.3 2.5 %collective-permute-done.25 = bf16[32,896]{1,0:T(8,128)(2,1)S(1)} collective-permute-done((bf16[32,896]{1,0:T(8,128)(2,1)S(1)}, bf16[32,896]{1,0:T(8,128)(2,1)S(1)}, u32[]{:S(2)}, u32[]{:S(2)}) %collective-permute-start.25) | collective-permute-done | bytes 57376 | tf_op jit(solution)/shard_map/ppermute | solution.py:124
  112.8 2.8 %fusion.4 = f32[32,2048]{1,0:T(8,128)S(1)} fusion(bf16[32,896]{1,0:T(8,128)(2,1)S(1)} %collective-permute-done.25, bf16[3584,2048]{1,0:T(8,128)(2,1)} %param.31, s32[]{:T(128)S(6)} %select_n.142), kind=kOutput, calls=%fused_computation.15 | convolution fusion | flops 117440512 | bytes 3989508 | tf_op jit(solution)/shard_map/dot_general | solution.py:126
  115.5 2.8 %fusion.2 = f32[32,2048]{1,0:T(8,128)S(1)} fusion(bf16[32,896]{1,0:T(8,128)(2,1)S(1)} %collective-permute-done.26, bf16[3584,2048]{1,0:T(8,128)(2,1)} %param.31, s32[]{:T(128)S(6)} %select_n.144), kind=kOutput, calls=%fused_computation.13 | convolution fusion | flops 117440512 | bytes 3989508 | tf_op jit(solution)/shard_map/dot_general | solution.py:126
  118.4 2.8 %fusion.19 = f32[4,8,2048]{2,1,0:T(8,128)S(1)} fusion(f32[32,2048]{1,0:T(8,128)S(1)} %fusion.2, f32[32,2048]{1,0:T(8,128)S(1)} %fusion.4, f32[32,2048]{1,0:T(8,128)S(1)} %fusion.8, bf16[32,896]{1,0:T(8,128)(2,1)S(1)} %collective-permute-done.24, bf16[3584,2048]{1,0:T(8,128)(2,1)} %param.31, s32[]{:T(128)S(6)} %select_n.140), kind=kOutput, calls=%fused_computation.24 | convolution fusion | flops 117637120 | bytes 4775940 | tf_op jit(solution)/shard_map/dot_general | solution.py:126
  121.3 1.7 %collective-permute-start.29 = (f32[8,2048]{1,0:T(8,128)S(1)}, f32[8,2048]{1,0:T(8,128)S(1)}, u32[]{:S(2)}, u32[]{:S(2)}) collective-permute-start(f32[8,2048]{1,0:T(8,128)S(1)} %get-tuple-element.61), channel_id=1, source_target_pairs={{0,3},{1,0},{2,1},{3,2},{4,7},{5,4},{6,5},{7,6},{8,11},{9,8},{10,9... | collective-permute-start | bytes 196616 | tf_op jit(solution)/shard_map/ppermute | solution.py:106
  124.9 2.3 %collective-permute-done.28 = f32[8,2048]{1,0:T(8,128)S(1)} collective-permute-done((f32[8,2048]{1,0:T(8,128)S(1)}, f32[8,2048]{1,0:T(8,128)S(1)}, u32[]{:S(2)}, u32[]{:S(2)}) %collective-permute-start.28) | collective-permute-done | bytes 65568 | tf_op jit(solution)/shard_map/ppermute | solution.py:106
  (111 shorter events, 31.2 us)
Async XLA Ops:
  0.9 14.6 %collective-permute-start.2 = (f32[8]{0:T(128)S(1)}, f32[8]{0:T(128)S(1)}, u32[]{:S(2)}, u32[]{:S(2)}) collective-permute-start(f32[8]{0:T(128)S(1)} %fusion.46), channel_id=1, source_target_pairs={{0,12},{4,0},{8,4},{12,8},{1,13},{5,1},{9,5},{13,9},{2,14},{6,2},{... | collective-permute-start | bytes 104 | tf_op jit(solution)/shard_map/ppermute | solution.py:113
  6.0 9.5 %collective-permute-start.1 = (f32[8]{0:T(128)S(1)}, f32[8]{0:T(128)S(1)}, u32[]{:S(2)}, u32[]{:S(2)}) collective-permute-start(f32[8]{0:T(128)S(1)} %fusion.46), channel_id=1, source_target_pairs={{0,8},{4,12},{8,0},{12,4},{1,9},{5,13},{9,1},{13,5},{2,10},{6,14},... | collective-permute-start | bytes 104 | tf_op jit(solution)/shard_map/ppermute | solution.py:113
  6.0 9.6 %collective-permute-start = (f32[8]{0:T(128)S(1)}, f32[8]{0:T(128)S(1)}, u32[]{:S(2)}, u32[]{:S(2)}) collective-permute-start(f32[8]{0:T(128)S(1)} %fusion.46), channel_id=1, source_target_pairs={{0,4},{4,8},{8,12},{12,0},{1,5},{5,9},{9,13},{13,1},{2,6},{6,10},{... | collective-permute-start | bytes 104 | tf_op jit(solution)/shard_map/ppermute | solution.py:113
  16.4 4.2 %collective-permute-start.4 = (bf16[8,2048]{1,0:T(8,128)(2,1)S(1)}, bf16[8,2048]{1,0:T(8,128)(2,1)S(1)}, u32[]{:S(2)}, u32[]{:S(2)}) collective-permute-start(bf16[8,2048]{1,0:T(8,128)(2,1)S(1)} %fusion.48), channel_id=1, source_target_pairs={{0,2},{1,3},{2,0},{3,1},{4,6},{5,7},{6,4},{7,5},{8,10},{9,11},{10,... | collective-permute-start | bytes 98312 | tf_op jit(solution)/shard_map/ppermute | solution.py:96
  18.0 3.3 %collective-permute-start.3 = (bf16[8,2048]{1,0:T(8,128)(2,1)S(1)}, bf16[8,2048]{1,0:T(8,128)(2,1)S(1)}, u32[]{:S(2)}, u32[]{:S(2)}) collective-permute-start(bf16[8,2048]{1,0:T(8,128)(2,1)S(1)} %fusion.48), channel_id=1, source_target_pairs={{0,1},{1,2},{2,3},{3,0},{4,5},{5,6},{6,7},{7,4},{8,9},{9,10},{10,1... | collective-permute-start | bytes 98312 | tf_op jit(solution)/shard_map/ppermute | solution.py:96
  18.0 3.3 %collective-permute-start.5 = (bf16[8,2048]{1,0:T(8,128)(2,1)S(1)}, bf16[8,2048]{1,0:T(8,128)(2,1)S(1)}, u32[]{:S(2)}, u32[]{:S(2)}) collective-permute-start(bf16[8,2048]{1,0:T(8,128)(2,1)S(1)} %fusion.48), channel_id=1, source_target_pairs={{0,3},{1,0},{2,1},{3,2},{4,7},{5,4},{6,5},{7,6},{8,11},{9,8},{10,9... | collective-permute-start | bytes 98312 | tf_op jit(solution)/shard_map/ppermute | solution.py:96
  29.2 7.2 %collective-permute-start.6 = (f32[8,2560]{1,0:T(8,128)S(1)}, f32[8,2560]{1,0:T(8,128)S(1)}, u32[]{:S(2)}, u32[]{:S(2)}) collective-permute-start(f32[8,2560]{1,0:T(8,128)S(1)} %get-tuple-element.57), channel_id=1, source_target_pairs={{0,4},{4,8},{8,12},{12,0},{1,5},{5,9},{9,13},{13,1},{2,6},{6,10},{... | collective-permute-start | bytes 245768 | tf_op jit(solution)/shard_map/ppermute | solution.py:106
  31.7 6.1 %collective-permute-start.8 = (f32[8,2560]{1,0:T(8,128)S(1)}, f32[8,2560]{1,0:T(8,128)S(1)}, u32[]{:S(2)}, u32[]{:S(2)}) collective-permute-start(f32[8,2560]{1,0:T(8,128)S(1)} %get-tuple-element.58), channel_id=1, source_target_pairs={{0,12},{4,0},{8,4},{12,8},{1,13},{5,1},{9,5},{13,9},{2,14},{6,2},{... | collective-permute-start | bytes 245768 | tf_op jit(solution)/shard_map/ppermute | solution.py:106
  33.0 8.2 %collective-permute-start.7 = (f32[8,2560]{1,0:T(8,128)S(1)}, f32[8,2560]{1,0:T(8,128)S(1)}, u32[]{:S(2)}, u32[]{:S(2)}) collective-permute-start(f32[8,2560]{1,0:T(8,128)S(1)} %get-tuple-element.59), channel_id=1, source_target_pairs={{0,8},{4,12},{8,0},{12,4},{1,9},{5,13},{9,1},{13,5},{2,10},{6,14},... | collective-permute-start | bytes 245768 | tf_op jit(solution)/shard_map/ppermute | solution.py:106
  42.2 27.4 %copy-start.3 = (f32[2048]{0:T(1024)S(1)}, f32[2048]{0:T(1024)}, u32[]{:S(2)}) copy-start(f32[2048]{0:T(1024)} %param.28) | copy-start | bytes 24580
  42.7 4.0 %collective-permute-start.11 = (bf16[8,2048]{1,0:T(8,128)(2,1)S(1)}, bf16[8,2048]{1,0:T(8,128)(2,1)S(1)}, u32[]{:S(2)}, u32[]{:S(2)}) collective-permute-start(bf16[8,2048]{1,0:T(8,128)(2,1)S(1)} %bitcast.144), channel_id=1, source_target_pairs={{0,12},{4,0},{8,4},{12,8},{1,13},{5,1},{9,5},{13,9},{2,14},{6,2},{... | collective-permute-start | bytes 98312 | tf_op jit(solution)/shard_map/ppermute | solution.py:96
  44.4 5.0 %collective-permute-start.10 = (bf16[8,2048]{1,0:T(8,128)(2,1)S(1)}, bf16[8,2048]{1,0:T(8,128)(2,1)S(1)}, u32[]{:S(2)}, u32[]{:S(2)}) collective-permute-start(bf16[8,2048]{1,0:T(8,128)(2,1)S(1)} %bitcast.145), channel_id=1, source_target_pairs={{0,8},{4,12},{8,0},{12,4},{1,9},{5,13},{9,1},{13,5},{2,10},{6,14},... | collective-permute-start | bytes 98312 | tf_op jit(solution)/shard_map/ppermute | solution.py:96
  44.4 5.7 %collective-permute-start.9 = (bf16[8,2048]{1,0:T(8,128)(2,1)S(1)}, bf16[8,2048]{1,0:T(8,128)(2,1)S(1)}, u32[]{:S(2)}, u32[]{:S(2)}) collective-permute-start(bf16[8,2048]{1,0:T(8,128)(2,1)S(1)} %bitcast.146), channel_id=1, source_target_pairs={{0,4},{4,8},{8,12},{12,0},{1,5},{5,9},{9,13},{13,1},{2,6},{6,10},{... | collective-permute-start | bytes 98312 | tf_op jit(solution)/shard_map/ppermute | solution.py:96
  56.5 3.7 %collective-permute-start.12 = (f32[8,2048]{1,0:T(8,128)S(1)}, f32[8,2048]{1,0:T(8,128)S(1)}, u32[]{:S(2)}, u32[]{:S(2)}) collective-permute-start(f32[8,2048]{1,0:T(8,128)S(1)} %get-tuple-element.63), channel_id=1, source_target_pairs={{0,1},{1,2},{2,3},{3,0},{4,5},{5,6},{6,7},{7,4},{8,9},{9,10},{10,1... | collective-permute-start | bytes 196616 | tf_op jit(solution)/shard_map/ppermute | solution.py:106
  56.5 4.1 %collective-permute-start.14 = (f32[8,2048]{1,0:T(8,128)S(1)}, f32[8,2048]{1,0:T(8,128)S(1)}, u32[]{:S(2)}, u32[]{:S(2)}) collective-permute-start(f32[8,2048]{1,0:T(8,128)S(1)} %get-tuple-element.64), channel_id=1, source_target_pairs={{0,3},{1,0},{2,1},{3,2},{4,7},{5,4},{6,5},{7,6},{8,11},{9,8},{10,9... | collective-permute-start | bytes 196616 | tf_op jit(solution)/shard_map/ppermute | solution.py:106
  58.3 4.6 %collective-permute-start.13 = (f32[8,2048]{1,0:T(8,128)S(1)}, f32[8,2048]{1,0:T(8,128)S(1)}, u32[]{:S(2)}, u32[]{:S(2)}) collective-permute-start(f32[8,2048]{1,0:T(8,128)S(1)} %get-tuple-element.65), channel_id=1, source_target_pairs={{0,2},{1,3},{2,0},{3,1},{4,6},{5,7},{6,4},{7,5},{8,10},{9,11},{10,... | collective-permute-start | bytes 196616 | tf_op jit(solution)/shard_map/ppermute | solution.py:106
  63.0 3.6 %collective-permute-start.17 = (f32[8]{0:T(128)S(1)}, f32[8]{0:T(128)S(1)}, u32[]{:S(2)}, u32[]{:S(2)}) collective-permute-start(f32[8]{0:T(128)S(1)} %get-tuple-element.44), channel_id=1, source_target_pairs={{0,12},{4,0},{8,4},{12,8},{1,13},{5,1},{9,5},{13,9},{2,14},{6,2},{... | collective-permute-start | bytes 104 | tf_op jit(solution)/shard_map/ppermute | solution.py:113
  63.7 4.4 %collective-permute-start.16 = (f32[8]{0:T(128)S(1)}, f32[8]{0:T(128)S(1)}, u32[]{:S(2)}, u32[]{:S(2)}) collective-permute-start(f32[8]{0:T(128)S(1)} %get-tuple-element.44), channel_id=1, source_target_pairs={{0,8},{4,12},{8,0},{12,4},{1,9},{5,13},{9,1},{13,5},{2,10},{6,14},... | collective-permute-start | bytes 104 | tf_op jit(solution)/shard_map/ppermute | solution.py:113
  64.2 5.3 %collective-permute-start.15 = (f32[8]{0:T(128)S(1)}, f32[8]{0:T(128)S(1)}, u32[]{:S(2)}, u32[]{:S(2)}) collective-permute-start(f32[8]{0:T(128)S(1)} %get-tuple-element.44), channel_id=1, source_target_pairs={{0,4},{4,8},{8,12},{12,0},{1,5},{5,9},{9,13},{13,1},{2,6},{6,10},{... | collective-permute-start | bytes 104 | tf_op jit(solution)/shard_map/ppermute | solution.py:113
  69.7 4.0 %collective-permute-start.19 = (bf16[8,2048]{1,0:T(8,128)(2,1)S(1)}, bf16[8,2048]{1,0:T(8,128)(2,1)S(1)}, u32[]{:S(2)}, u32[]{:S(2)}) collective-permute-start(bf16[8,2048]{1,0:T(8,128)(2,1)S(1)} %multiply_convert_fusion), channel_id=1, source_target_pairs={{0,2},{1,3},{2,0},{3,1},{4,6},{5,7},{6,4},{7,5},{8,10},{9,11},{10,... | collective-permute-start | bytes 98312 | tf_op jit(solution)/shard_map/ppermute | solution.py:96
  70.9 3.3 %collective-permute-start.18 = (bf16[8,2048]{1,0:T(8,128)(2,1)S(1)}, bf16[8,2048]{1,0:T(8,128)(2,1)S(1)}, u32[]{:S(2)}, u32[]{:S(2)}) collective-permute-start(bf16[8,2048]{1,0:T(8,128)(2,1)S(1)} %multiply_convert_fusion), channel_id=1, source_target_pairs={{0,1},{1,2},{2,3},{3,0},{4,5},{5,6},{6,7},{7,4},{8,9},{9,10},{10,1... | collective-permute-start | bytes 98312 | tf_op jit(solution)/shard_map/ppermute | solution.py:96
  70.9 3.3 %collective-permute-start.20 = (bf16[8,2048]{1,0:T(8,128)(2,1)S(1)}, bf16[8,2048]{1,0:T(8,128)(2,1)S(1)}, u32[]{:S(2)}, u32[]{:S(2)}) collective-permute-start(bf16[8,2048]{1,0:T(8,128)(2,1)S(1)} %multiply_convert_fusion), channel_id=1, source_target_pairs={{0,3},{1,0},{2,1},{3,2},{4,7},{5,4},{6,5},{7,6},{8,11},{9,8},{10,9... | collective-permute-start | bytes 98312 | tf_op jit(solution)/shard_map/ppermute | solution.py:96
  82.7 45.2 %copy-start.1 = (s32[32]{0:T(128)S(1)}, s32[32]{0:T(128)}, u32[]{:S(2)}) copy-start(s32[32]{0:T(128)} %param.33) | copy-start | bytes 388
  90.7 8.2 %collective-permute-start.21 = (bf16[32,1792]{1,0:T(8,128)(2,1)S(1)}, bf16[32,1792]{1,0:T(8,128)(2,1)S(1)}, u32[]{:S(2)}, u32[]{:S(2)}) collective-permute-start(bf16[32,1792]{1,0:T(8,128)(2,1)S(1)} %get-tuple-element.54), channel_id=1, source_target_pairs={{0,4},{4,8},{8,12},{12,0},{1,5},{5,9},{9,13},{13,1},{2,6},{6,10},{... | collective-permute-start | bytes 344072 | tf_op jit(solution)/shard_map/ppermute | solution.py:106
  91.1 11.9 %collective-permute-start.22 = (bf16[32,1792]{1,0:T(8,128)(2,1)S(1)}, bf16[32,1792]{1,0:T(8,128)(2,1)S(1)}, u32[]{:S(2)}, u32[]{:S(2)}) collective-permute-start(bf16[32,1792]{1,0:T(8,128)(2,1)S(1)} %get-tuple-element.55), channel_id=1, source_target_pairs={{0,8},{4,12},{8,0},{12,4},{1,9},{5,13},{9,1},{13,5},{2,10},{6,14},... | collective-permute-start | bytes 344072 | tf_op jit(solution)/shard_map/ppermute | solution.py:106
  92.9 10.1 %collective-permute-start.23 = (bf16[32,1792]{1,0:T(8,128)(2,1)S(1)}, bf16[32,1792]{1,0:T(8,128)(2,1)S(1)}, u32[]{:S(2)}, u32[]{:S(2)}) collective-permute-start(bf16[32,1792]{1,0:T(8,128)(2,1)S(1)} %get-tuple-element.56), channel_id=1, source_target_pairs={{0,12},{4,0},{8,4},{12,8},{1,13},{5,1},{9,5},{13,9},{2,14},{6,2},{... | collective-permute-start | bytes 344072 | tf_op jit(solution)/shard_map/ppermute | solution.py:106
  103.1 12.5 %collective-permute-start.26 = (bf16[32,896]{1,0:T(8,128)(2,1)S(1)}, bf16[32,896]{1,0:T(8,128)(2,1)S(1)}, u32[]{:S(2)}, u32[]{:S(2)}) collective-permute-start(bf16[32,896]{1,0:T(8,128)(2,1)S(1)} %fusion.42), channel_id=1, source_target_pairs={{0,12},{4,0},{8,4},{12,8},{1,13},{5,1},{9,5},{13,9},{2,14},{6,2},{... | collective-permute-start | bytes 172040 | tf_op jit(solution)/shard_map/ppermute | solution.py:124
  106.4 6.4 %collective-permute-start.25 = (bf16[32,896]{1,0:T(8,128)(2,1)S(1)}, bf16[32,896]{1,0:T(8,128)(2,1)S(1)}, u32[]{:S(2)}, u32[]{:S(2)}) collective-permute-start(bf16[32,896]{1,0:T(8,128)(2,1)S(1)} %fusion.42), channel_id=1, source_target_pairs={{0,8},{4,12},{8,0},{12,4},{1,9},{5,13},{9,1},{13,5},{2,10},{6,14},... | collective-permute-start | bytes 172040 | tf_op jit(solution)/shard_map/ppermute | solution.py:124
  107.5 10.8 %collective-permute-start.24 = (bf16[32,896]{1,0:T(8,128)(2,1)S(1)}, bf16[32,896]{1,0:T(8,128)(2,1)S(1)}, u32[]{:S(2)}, u32[]{:S(2)}) collective-permute-start(bf16[32,896]{1,0:T(8,128)(2,1)S(1)} %fusion.42), channel_id=1, source_target_pairs={{0,4},{4,8},{8,12},{12,0},{1,5},{5,9},{9,13},{13,1},{2,6},{6,10},{... | collective-permute-start | bytes 172040 | tf_op jit(solution)/shard_map/ppermute | solution.py:124
  121.2 3.7 %collective-permute-start.27 = (f32[8,2048]{1,0:T(8,128)S(1)}, f32[8,2048]{1,0:T(8,128)S(1)}, u32[]{:S(2)}, u32[]{:S(2)}) collective-permute-start(f32[8,2048]{1,0:T(8,128)S(1)} %get-tuple-element.60), channel_id=1, source_target_pairs={{0,1},{1,2},{2,3},{3,0},{4,5},{5,6},{6,7},{7,4},{8,9},{9,10},{10,1... | collective-permute-start | bytes 196616 | tf_op jit(solution)/shard_map/ppermute | solution.py:106
  121.3 3.7 %collective-permute-start.29 = (f32[8,2048]{1,0:T(8,128)S(1)}, f32[8,2048]{1,0:T(8,128)S(1)}, u32[]{:S(2)}, u32[]{:S(2)}) collective-permute-start(f32[8,2048]{1,0:T(8,128)S(1)} %get-tuple-element.61), channel_id=1, source_target_pairs={{0,3},{1,0},{2,1},{3,2},{4,7},{5,4},{6,5},{7,6},{8,11},{9,8},{10,9... | collective-permute-start | bytes 196616 | tf_op jit(solution)/shard_map/ppermute | solution.py:106
  123.0 4.3 %collective-permute-start.28 = (f32[8,2048]{1,0:T(8,128)S(1)}, f32[8,2048]{1,0:T(8,128)S(1)}, u32[]{:S(2)}, u32[]{:S(2)}) collective-permute-start(f32[8,2048]{1,0:T(8,128)S(1)} %get-tuple-element.62), channel_id=1, source_target_pairs={{0,2},{1,3},{2,0},{3,1},{4,6},{5,7},{6,4},{7,5},{8,10},{9,11},{10,... | collective-permute-start | bytes 196616 | tf_op jit(solution)/shard_map/ppermute | solution.py:106
  (2 other events, 28.9 us)

commit v5 on v4

--- a/solution.py
+++ b/solution.py
@@ -91,11 +91,18 @@
     return [(i, (i + k) % n) for i in range(n)]
 
 
-def gather_blocks(x, axis, n):
+def gather_rows(x, axis, n, want):
     idx = lax.axis_index(axis)
+    per = x.shape[0]
     got = [x] + [lax.ppermute(x, axis, shift_pairs(n, k)) for k in range(1, n)]
-    stacked = jnp.stack(got)
-    return jnp.take(stacked, (idx - jnp.arange(n)) % n, axis=0)
+    stacked = jnp.concatenate(got, axis=0)
+    arrival = ((idx - want // per) % n) * per + want % per
+    return jnp.take(stacked, arrival, axis=0)
+
+
+def pick(keys, wanted, values):
+    hit = keys[None, :] == wanted[:, None]
+    return jnp.sum(jnp.where(hit, values[None, :], 0), axis=1)
 
 
 def scatter_sum(blocks, axis, n):
@@ -149,29 +156,24 @@
     rows_here = tokens.shape[0]
     rows_total = rows_here * n_cs
     my_start = pool_index * per_owner
-    slot_of_row = jnp.take(request_slot, row_request)
-    row_of_slot = jnp.zeros_like(slot_of_row).at[slot_of_row].set(
-        jnp.arange(rows_total, dtype=slot_of_row.dtype)
-    )
-    length_of_row = jnp.take(lengths, row_request)
-    length_of_slot = jnp.take(length_of_row, row_of_slot)
+    every = jnp.arange(rows_total, dtype=row_request.dtype)
+    slot_of_row = pick(every, row_request, request_slot)
+    row_of_slot = pick(slot_of_row, every, every)
+    positions = pick(request_slot, my_start + jnp.arange(per_owner, dtype=row_request.dtype), lengths)
 
     residual = tokens.astype(jnp.float32)
     squares = all_sum(jnp.sum(residual * residual, axis=1), "pool", n_pool)
     normed = (residual * lax.rsqrt(squares / D + epsilon)[:, None] * attn_gain[None, :]).astype(
         jnp.bfloat16
     )
-    normed_all = gather_blocks(normed, CS, n_cs).reshape(rows_total, -1)
-    by_slot = jnp.take(normed_all, row_of_slot, axis=0)
+    by_slot = gather_rows(normed, CS, n_cs, row_of_slot)
     qkv_part = jnp.einsum(
         "rf,fgc->rgc", by_slot, w_qkv, preferred_element_type=jnp.float32
     ).reshape(rows_total, -1)
     summed = scatter_sum(qkv_part.reshape(n_pool, per_owner, -1), "pool", n_pool)
-    positions = lax.dynamic_slice_in_dim(length_of_slot, my_start, per_owner, 0)
     rotated = rope_rows(summed, positions, per_group, HD)
     attended = attend(rotated, kv_cache, positions, per_group, HD)
-    gathered = gather_blocks(attended, "pool", n_pool).reshape(rows_total, -1)
-    by_row = jnp.take(gathered, slot_of_row, axis=0)
+    by_row = gather_rows(attended, "pool", n_pool, slot_of_row)
     out_part = jnp.dot(by_row, w_out, preferred_element_type=jnp.float32)
     residual = residual + scatter_sum(out_part.reshape(n_cs, rows_here, -1), CS, n_cs)
 
@@ -179,7 +181,7 @@
     ffn_normed = (
         residual * lax.rsqrt(squares_mid / D + epsilon)[:, None] * ffn_gain[None, :]
     ).astype(jnp.bfloat16)
-    ffn_all = gather_blocks(ffn_normed, CS, n_cs).reshape(rows_total, -1)
+    ffn_all = gather_rows(ffn_normed, CS, n_cs, every)
     chunk = w_gate.shape[1] // n_pool
     gate_part = jnp.dot(ffn_all, w_gate, preferred_element_type=jnp.float32).astype(jnp.bfloat16)
     up_part = jnp.dot(ffn_all, w_up, preferred_element_type=jnp.float32).astype(jnp.bfloat16)

time: 129 us -> 119 us (0.922)
  starting transfers between devices: 36.3 us -> 31.7 us
  local copies, waits for them, and re-layouts: 9.73 us -> 5.25 us
  other arithmetic: 6.8 us -> 5.45 us
    ppermute x9, waiting for transfers between devices: 7.31 us -> 11.3 us  [gather_rows(): got = [x] + [lax.ppermute(x, axis, shift_pairs(n, k)) for k in range(1, n)]]
    gather x8 -> x3, local copies, waits for them, and re-layouts: 5.72 us -> 1.95 us  [gather_rows(): return jnp.take(stacked, arrival, axis=0)]
    ppermute x9, starting transfers between devices: 8.56 us -> 5.56 us  [gather_rows(): got = [x] + [lax.ppermute(x, axis, shift_pairs(n, k)) for k in range(1, n)]]
    ppermute x12, waiting for transfers between devices: 22.8 us -> 20.5 us  [scatter_sum(): lax.ppermute(piece, axis, shift_pairs(n, k)).astype(jnp.float32)]
    reduce_sum x0 -> x3, other arithmetic: none -> 1.82 us  [pick(): return jnp.sum(jnp.where(hit, values[None, :], 0), axis=1)]
    select_n x5 -> x1, other arithmetic: 1.36 us -> 0.01 us  [gather_rows(): return jnp.take(stacked, arrival, axis=0)]
  transfers between devices with their start and end apart: 30 -> 30, of which waited for: 20 -> 21; matrix products, arithmetic and copies ran while one was open for 14% -> 11% of each run, Pallas kernels for 0% -> 0%
where the time goes in v5:
time: 119 us
  matrix products  38.7 us (33%)
  waiting for transfers between devices  37.2 us (31%)
  starting transfers between devices  31.7 us (27%)
  other arithmetic  5.45 us (5%)
  local copies, waits for them, and re-layouts  5.25 us (4%)
    ppermute x12, waiting for transfers between devices, scatter_sum(): lax.ppermute(piece, axis, shift_pairs(n, k)).astype(jnp.float32)  20.5 us
    ppermute x12, starting transfers between devices, scatter_sum(): lax.ppermute(piece, axis, shift_pairs(n, k)).astype(jnp.float32)  13.3 us
    ppermute x9, waiting for transfers between devices, gather_rows(): got = [x] + [lax.ppermute(x, axis, shift_pairs(n, k)) for k in range(1, n)]  11.3 us
    ppermute x6, starting transfers between devices, all_sum(): total = total + lax.ppermute(x, axis, shift_pairs(n, k))  9.3 us
    dot_general x3, matrix products, gather_matmul(): acc = acc + jnp.dot(got, rows, preferred_element_type=jnp.float32)  8.39 us
    dot_general x1, matrix products, local(): jnp.dot(ffn_all, w_gate, preferred_element_type=jnp.float32)  7.86 us
    dot_general x1, matrix products, local(): jnp.dot(ffn_all, w_up, preferred_element_type=jnp.float32)  7.85 us
    dot_general x1, matrix products, local(): jnp.einsum('rf,fgc->rgc', by_slot, w_qkv, preferred_element_type=jnp.floa...  5.94 us
  transfers between devices with their start and end apart: 30, of which 21 were waited for; matrix products, arithmetic and copies ran while one was open for 11% of the time, Pallas kernels for 0%

profile of v5, /device:TPU:0, one launch (start us, length us, event | category | flops | bytes accessed | tf_op | source)
XLA Modules:
  0.0 118.7 jit_solution(18145756937953196641)
XLA Ops:
  0.9 5.1 %collective-permute-start.2 = (f32[8]{0:T(128)S(1)}, f32[8]{0:T(128)S(1)}, u32[]{:S(2)}, u32[]{:S(2)}) collective-permute-start(f32[8]{0:T(128)S(1)} %fusion.45), channel_id=1, source_target_pairs={{0,12},{4,0},{8,4},{12,8},{1,13},{5,1},{9,5},{13,9},{2,14},{6,2},{... | collective-permute-start | bytes 104 | tf_op jit(solution)/shard_map/ppermute | solution.py:120
  9.0 2.7 %fusion.86 = (bf16[8,256,1,2,128]{4,3,2,1,0:T(2,128)(2,1)S(1)}, bf16[8,256,1,2,128]{4,3,2,1,0:T(2,128)(2,1)S(1)}) fusion(bf16[8,256,2,2,128]{4,3,2,1,0:T(2,128)(2,1)} %param.28), kind=kLoop, calls=%fused_computation.178 | loop fusion | bytes 4194304 | tf_op jit(solution)/shard_map/slice | solution.py:56
  12.8 1.5 %collective-permute-start.4 = (bf16[8,2048]{1,0:T(8,128)(2,1)S(1)}, bf16[8,2048]{1,0:T(8,128)(2,1)S(1)}, u32[]{:S(2)}, u32[]{:S(2)}) collective-permute-start(bf16[8,2048]{1,0:T(8,128)(2,1)S(1)} %fusion.47), channel_id=1, source_target_pairs={{0,2},{1,3},{2,0},{3,1},{4,6},{5,7},{6,4},{7,5},{8,10},{9,11},{10,... | collective-permute-start | bytes 98312 | tf_op jit(solution)/shard_map/ppermute | solution.py:97
  14.5 2.3 %collective-permute-done.4 = bf16[8,2048]{1,0:T(8,128)(2,1)S(1)} collective-permute-done((bf16[8,2048]{1,0:T(8,128)(2,1)S(1)}, bf16[8,2048]{1,0:T(8,128)(2,1)S(1)}, u32[]{:S(2)}, u32[]{:S(2)}) %collective-permute-start.4) | collective-permute-done | bytes 32800 | tf_op jit(solution)/shard_map/ppermute | solution.py:97
  18.3 5.9 %fusion = f32[32,2,1280]{2,0,1:T(8,128)S(1)} fusion(bf16[2048,2,1280]{2,1,0:T(2,128)(2,1)} %param.22, bf16[32,2048]{1,0:T(8,128)(2,1)S(1)} %gather_fusion, pred[32]{0:T(512)(128)(4,1)S(1)} %get-tuple-element.46), kind=kOutput, calls=%fused_computation.3 | convolution fusion | flops 335609856 | bytes 10944544 | tf_op jit(solution)/shard_map/rf,fgc->rgc/dot_general | solution.py:170
  24.8 2.5 %collective-permute-start.6 = (f32[8,2560]{1,0:T(8,128)S(1)}, f32[8,2560]{1,0:T(8,128)S(1)}, u32[]{:S(2)}, u32[]{:S(2)}) collective-permute-start(f32[8,2560]{1,0:T(8,128)S(1)} %get-tuple-element.53), channel_id=1, source_target_pairs={{0,4},{4,8},{8,12},{12,0},{1,5},{5,9},{9,13},{13,1},{2,6},{6,10},{... | collective-permute-start | bytes 245768 | tf_op jit(solution)/shard_map/ppermute | solution.py:113
  27.4 1.3 %collective-permute-start.8 = (f32[8,2560]{1,0:T(8,128)S(1)}, f32[8,2560]{1,0:T(8,128)S(1)}, u32[]{:S(2)}, u32[]{:S(2)}) collective-permute-start(f32[8,2560]{1,0:T(8,128)S(1)} %get-tuple-element.54), channel_id=1, source_target_pairs={{0,12},{4,0},{8,4},{12,8},{1,13},{5,1},{9,5},{13,9},{2,14},{6,2},{... | collective-permute-start | bytes 245768 | tf_op jit(solution)/shard_map/ppermute | solution.py:113
  28.9 2.7 %collective-permute-done.6 = f32[8,2560]{1,0:T(8,128)S(1)} collective-permute-done((f32[8,2560]{1,0:T(8,128)S(1)}, f32[8,2560]{1,0:T(8,128)S(1)}, u32[]{:S(2)}, u32[]{:S(2)}) %collective-permute-start.6) | collective-permute-done | bytes 81952 | tf_op jit(solution)/shard_map/ppermute | solution.py:113
  32.3 3.2 %collective-permute-done.7 = f32[8,2560]{1,0:T(8,128)S(1)} collective-permute-done((f32[8,2560]{1,0:T(8,128)S(1)}, f32[8,2560]{1,0:T(8,128)S(1)}, u32[]{:S(2)}, u32[]{:S(2)}) %collective-permute-start.7) | collective-permute-done | bytes 81952 | tf_op jit(solution)/shard_map/ppermute | solution.py:113
  37.0 1.9 %collective-permute-start.11 = (bf16[8,2048]{1,0:T(8,128)(2,1)S(1)}, bf16[8,2048]{1,0:T(8,128)(2,1)S(1)}, u32[]{:S(2)}, u32[]{:S(2)}) collective-permute-start(bf16[8,2048]{1,0:T(8,128)(2,1)S(1)} %bitcast.109), channel_id=1, source_target_pairs={{0,12},{4,0},{8,4},{12,8},{1,13},{5,1},{9,5},{13,9},{2,14},{6,2},{... | collective-permute-start | bytes 98312 | tf_op jit(solution)/shard_map/ppermute | solution.py:97
  40.9 2.8 %collective-permute-done.10 = bf16[8,2048]{1,0:T(8,128)(2,1)S(1)} collective-permute-done((bf16[8,2048]{1,0:T(8,128)(2,1)S(1)}, bf16[8,2048]{1,0:T(8,128)(2,1)S(1)}, u32[]{:S(2)}, u32[]{:S(2)}) %collective-permute-start.10) | collective-permute-done | bytes 32800 | tf_op jit(solution)/shard_map/ppermute | solution.py:97
  45.3 5.0 %convolution_bitcast_fusion = f32[4,8,2048]{2,1,0:T(8,128)S(1)} fusion(bf16[2048,2048]{1,0:T(8,128)(2,1)} %param.23, bf16[32,2048]{1,0:T(8,128)(2,1)S(1)} %gather_fusion.1, pred[32]{0:T(512)(128)(4,1)S(1)} %get-tuple-element.44), kind=kOutput, calls=%fused_computation.19 | convolution fusion | flops 268500992 | bytes 8781856 | tf_op jit(solution)/shard_map/dot_general | solution.py:177
  50.4 1.7 %collective-permute-start.14 = (f32[8,2048]{1,0:T(8,128)S(1)}, f32[8,2048]{1,0:T(8,128)S(1)}, u32[]{:S(2)}, u32[]{:S(2)}) collective-permute-start(f32[8,2048]{1,0:T(8,128)S(1)} %get-tuple-element.60), channel_id=1, source_target_pairs={{0,3},{1,0},{2,1},{3,2},{4,7},{5,4},{6,5},{7,6},{8,11},{9,8},{10,9... | collective-permute-start | bytes 196616 | tf_op jit(solution)/shard_map/ppermute | solution.py:113
  54.1 2.3 %collective-permute-done.13 = f32[8,2048]{1,0:T(8,128)S(1)} collective-permute-done((f32[8,2048]{1,0:T(8,128)S(1)}, f32[8,2048]{1,0:T(8,128)S(1)}, u32[]{:S(2)}, u32[]{:S(2)}) %collective-permute-start.13) | collective-permute-done | bytes 65568 | tf_op jit(solution)/shard_map/ppermute | solution.py:113
  57.8 1.9 %collective-permute-start.15 = (f32[8]{0:T(128)S(1)}, f32[8]{0:T(128)S(1)}, u32[]{:S(2)}, u32[]{:S(2)}) collective-permute-start(f32[8]{0:T(128)S(1)} %get-tuple-element.42), channel_id=1, source_target_pairs={{0,4},{4,8},{8,12},{12,0},{1,5},{5,9},{9,13},{13,1},{2,6},{6,10},{... | collective-permute-start | bytes 104 | tf_op jit(solution)/shard_map/ppermute | solution.py:120
  60.1 1.6 %collective-permute-done.16 = f32[8]{0:T(128)S(1)} collective-permute-done((f32[8]{0:T(128)S(1)}, f32[8]{0:T(128)S(1)}, u32[]{:S(2)}, u32[]{:S(2)}) %collective-permute-start.16) | collective-permute-done | bytes 64 | tf_op jit(solution)/shard_map/ppermute | solution.py:120
  61.7 1.4 %collective-permute-done.15 = f32[8]{0:T(128)S(1)} collective-permute-done((f32[8]{0:T(128)S(1)}, f32[8]{0:T(128)S(1)}, u32[]{:S(2)}, u32[]{:S(2)}) %collective-permute-start.15) | collective-permute-done | bytes 64 | tf_op jit(solution)/shard_map/ppermute | solution.py:120
  64.8 2.4 %collective-permute-done.19 = bf16[8,2048]{1,0:T(8,128)(2,1)S(1)} collective-permute-done((bf16[8,2048]{1,0:T(8,128)(2,1)S(1)}, bf16[8,2048]{1,0:T(8,128)(2,1)S(1)}, u32[]{:S(2)}, u32[]{:S(2)}) %collective-permute-start.19) | collective-permute-done | bytes 32800 | tf_op jit(solution)/shard_map/ppermute | solution.py:97
  68.2 7.9 %convolution_convert_fusion = bf16[32,3584]{1,0:T(8,128)(2,1)S(1)} fusion(bf16[2048,3584]{1,0:T(8,128)(2,1)} %param.26, bf16[32,2048]{1,0:T(8,128)(2,1)S(1)} %gather_fusion.2, pred[32]{0:T(512)(128)(4,1)S(1)} %compare_and_fusion), kind=kOutput, calls=%fused_computation.5 | convolution fusion | flops 469942272 | bytes 15040544 | tf_op jit(solution)/shard_map/dot_general | solution.py:187
  76.1 7.9 %convolution_convert_fusion.1 = bf16[32,3584]{1,0:T(8,128)(2,1)S(1)} fusion(bf16[2048,3584]{1,0:T(8,128)(2,1)} %param.25, bf16[32,2048]{1,0:T(8,128)(2,1)S(1)} %gather_fusion.2, pred[32]{0:T(512)(128)(4,1)S(1)} %compare_and_fusion), kind=kOutput, calls=%fused_computation.6 | convolution fusion | flops 469942272 | bytes 15040544 | tf_op jit(solution)/shard_map/dot_general | solution.py:186
  84.3 1.8 %collective-permute-start.22 = (bf16[32,1792]{1,0:T(8,128)(2,1)S(1)}, bf16[32,1792]{1,0:T(8,128)(2,1)S(1)}, u32[]{:S(2)}, u32[]{:S(2)}) collective-permute-start(bf16[32,1792]{1,0:T(8,128)(2,1)S(1)} %get-tuple-element.51), channel_id=1, source_target_pairs={{0,8},{4,12},{8,0},{12,4},{1,9},{5,13},{9,1},{13,5},{2,10},{6,14},... | collective-permute-start | bytes 344072 | tf_op jit(solution)/shard_map/ppermute | solution.py:113
  86.1 1.9 %collective-permute-start.23 = (bf16[32,1792]{1,0:T(8,128)(2,1)S(1)}, bf16[32,1792]{1,0:T(8,128)(2,1)S(1)}, u32[]{:S(2)}, u32[]{:S(2)}) collective-permute-start(bf16[32,1792]{1,0:T(8,128)(2,1)S(1)} %get-tuple-element.52), channel_id=1, source_target_pairs={{0,12},{4,0},{8,4},{12,8},{1,13},{5,1},{9,5},{13,9},{2,14},{6,2},{... | collective-permute-start | bytes 344072 | tf_op jit(solution)/shard_map/ppermute | solution.py:113
  88.0 4.1 %collective-permute-done.21 = bf16[32,1792]{1,0:T(8,128)(2,1)S(1)} collective-permute-done((bf16[32,1792]{1,0:T(8,128)(2,1)S(1)}, bf16[32,1792]{1,0:T(8,128)(2,1)S(1)}, u32[]{:S(2)}, u32[]{:S(2)}) %collective-permute-start.21) | collective-permute-done | bytes 114720 | tf_op jit(solution)/shard_map/ppermute | solution.py:113
  92.0 3.0 %collective-permute-done.22 = bf16[32,1792]{1,0:T(8,128)(2,1)S(1)} collective-permute-done((bf16[32,1792]{1,0:T(8,128)(2,1)S(1)}, bf16[32,1792]{1,0:T(8,128)(2,1)S(1)}, u32[]{:S(2)}, u32[]{:S(2)}) %collective-permute-start.22) | collective-permute-done | bytes 114720 | tf_op jit(solution)/shard_map/ppermute | solution.py:113
  95.2 2.7 %collective-permute-start.26 = (bf16[32,896]{1,0:T(8,128)(2,1)S(1)}, bf16[32,896]{1,0:T(8,128)(2,1)S(1)}, u32[]{:S(2)}, u32[]{:S(2)}) collective-permute-start(bf16[32,896]{1,0:T(8,128)(2,1)S(1)} %fusion.41), channel_id=1, source_target_pairs={{0,12},{4,0},{8,4},{12,8},{1,13},{5,1},{9,5},{13,9},{2,14},{6,2},{... | collective-permute-start | bytes 172040 | tf_op jit(solution)/shard_map/ppermute | solution.py:131
  98.7 2.8 %fusion.8 = f32[32,2048]{1,0:T(8,128)S(1)} fusion(bf16[32,896]{1,0:T(8,128)(2,1)S(1)} %fusion.41, bf16[3584,2048]{1,0:T(8,128)(2,1)} %param.27, s32[]{:T(128)S(6)} %select_n.162), kind=kOutput, calls=%fused_computation.13 | convolution fusion | flops 117440512 | bytes 3989508 | tf_op jit(solution)/shard_map/dot_general | solution.py:127
  101.5 2.0 %collective-permute-done.25 = bf16[32,896]{1,0:T(8,128)(2,1)S(1)} collective-permute-done((bf16[32,896]{1,0:T(8,128)(2,1)S(1)}, bf16[32,896]{1,0:T(8,128)(2,1)S(1)}, u32[]{:S(2)}, u32[]{:S(2)}) %collective-permute-start.25) | collective-permute-done | bytes 57376 | tf_op jit(solution)/shard_map/ppermute | solution.py:131
  103.5 2.8 %fusion.4 = f32[32,2048]{1,0:T(8,128)S(1)} fusion(bf16[32,896]{1,0:T(8,128)(2,1)S(1)} %collective-permute-done.25, bf16[3584,2048]{1,0:T(8,128)(2,1)} %param.27, s32[]{:T(128)S(6)} %select_n.166), kind=kOutput, calls=%fused_computation.9 | convolution fusion | flops 117440512 | bytes 3989508 | tf_op jit(solution)/shard_map/dot_general | solution.py:133
  106.3 2.8 %fusion.2 = f32[32,2048]{1,0:T(8,128)S(1)} fusion(bf16[32,896]{1,0:T(8,128)(2,1)S(1)} %collective-permute-done.26, bf16[3584,2048]{1,0:T(8,128)(2,1)} %param.27, s32[]{:T(128)S(6)} %select_n.168), kind=kOutput, calls=%fused_computation.7 | convolution fusion | flops 117440512 | bytes 3989508 | tf_op jit(solution)/shard_map/dot_general | solution.py:133
  109.1 2.8 %fusion.19 = f32[4,8,2048]{2,1,0:T(8,128)S(1)} fusion(f32[32,2048]{1,0:T(8,128)S(1)} %fusion.2, f32[32,2048]{1,0:T(8,128)S(1)} %fusion.4, f32[32,2048]{1,0:T(8,128)S(1)} %fusion.8, bf16[32,896]{1,0:T(8,128)(2,1)S(1)} %collective-permute-done.24, bf16[3584,2048]{1,0:T(8,128)(2,1)} %param.27, s32[]{:T(128)S(6)} %select_n.164), kind=kOutput, calls=%fused_computation.18 | convolution fusion | flops 117637120 | bytes 4775940 | tf_op jit(solution)/shard_map/dot_general | solution.py:133
  112.0 1.7 %collective-permute-start.29 = (f32[8,2048]{1,0:T(8,128)S(1)}, f32[8,2048]{1,0:T(8,128)S(1)}, u32[]{:S(2)}, u32[]{:S(2)}) collective-permute-start(f32[8,2048]{1,0:T(8,128)S(1)} %get-tuple-element.57), channel_id=1, source_target_pairs={{0,3},{1,0},{2,1},{3,2},{4,7},{5,4},{6,5},{7,6},{8,11},{9,8},{10,9... | collective-permute-start | bytes 196616 | tf_op jit(solution)/shard_map/ppermute | solution.py:113
  115.7 2.3 %collective-permute-done.28 = f32[8,2048]{1,0:T(8,128)S(1)} collective-permute-done((f32[8,2048]{1,0:T(8,128)S(1)}, f32[8,2048]{1,0:T(8,128)S(1)}, u32[]{:S(2)}, u32[]{:S(2)}) %collective-permute-start.28) | collective-permute-done | bytes 65568 | tf_op jit(solution)/shard_map/ppermute | solution.py:113
  (93 shorter events, 23.4 us)
Async XLA Ops:
  0.9 10.9 %collective-permute-start.2 = (f32[8]{0:T(128)S(1)}, f32[8]{0:T(128)S(1)}, u32[]{:S(2)}, u32[]{:S(2)}) collective-permute-start(f32[8]{0:T(128)S(1)} %fusion.45), channel_id=1, source_target_pairs={{0,12},{4,0},{8,4},{12,8},{1,13},{5,1},{9,5},{13,9},{2,14},{6,2},{... | collective-permute-start | bytes 104 | tf_op jit(solution)/shard_map/ppermute | solution.py:120
  6.0 5.8 %collective-permute-start.1 = (f32[8]{0:T(128)S(1)}, f32[8]{0:T(128)S(1)}, u32[]{:S(2)}, u32[]{:S(2)}) collective-permute-start(f32[8]{0:T(128)S(1)} %fusion.45), channel_id=1, source_target_pairs={{0,8},{4,12},{8,0},{12,4},{1,9},{5,13},{9,1},{13,5},{2,10},{6,14},... | collective-permute-start | bytes 104 | tf_op jit(solution)/shard_map/ppermute | solution.py:120
  6.0 5.8 %collective-permute-start = (f32[8]{0:T(128)S(1)}, f32[8]{0:T(128)S(1)}, u32[]{:S(2)}, u32[]{:S(2)}) collective-permute-start(f32[8]{0:T(128)S(1)} %fusion.45), channel_id=1, source_target_pairs={{0,4},{4,8},{8,12},{12,0},{1,5},{5,9},{9,13},{13,1},{2,6},{6,10},{... | collective-permute-start | bytes 104 | tf_op jit(solution)/shard_map/ppermute | solution.py:120
  12.7 1.8 %collective-permute-start.5 = (bf16[8,2048]{1,0:T(8,128)(2,1)S(1)}, bf16[8,2048]{1,0:T(8,128)(2,1)S(1)}, u32[]{:S(2)}, u32[]{:S(2)}) collective-permute-start(bf16[8,2048]{1,0:T(8,128)(2,1)S(1)} %fusion.47), channel_id=1, source_target_pairs={{0,3},{1,0},{2,1},{3,2},{4,7},{5,4},{6,5},{7,6},{8,11},{9,8},{10,9... | collective-permute-start | bytes 98312 | tf_op jit(solution)/shard_map/ppermute | solution.py:97
  12.8 4.0 %collective-permute-start.4 = (bf16[8,2048]{1,0:T(8,128)(2,1)S(1)}, bf16[8,2048]{1,0:T(8,128)(2,1)S(1)}, u32[]{:S(2)}, u32[]{:S(2)}) collective-permute-start(bf16[8,2048]{1,0:T(8,128)(2,1)S(1)} %fusion.47), channel_id=1, source_target_pairs={{0,2},{1,3},{2,0},{3,1},{4,6},{5,7},{6,4},{7,5},{8,10},{9,11},{10,... | collective-permute-start | bytes 98312 | tf_op jit(solution)/shard_map/ppermute | solution.py:97
  14.3 3.3 %collective-permute-start.3 = (bf16[8,2048]{1,0:T(8,128)(2,1)S(1)}, bf16[8,2048]{1,0:T(8,128)(2,1)S(1)}, u32[]{:S(2)}, u32[]{:S(2)}) collective-permute-start(bf16[8,2048]{1,0:T(8,128)(2,1)S(1)} %fusion.47), channel_id=1, source_target_pairs={{0,1},{1,2},{2,3},{3,0},{4,5},{5,6},{6,7},{7,4},{8,9},{9,10},{10,1... | collective-permute-start | bytes 98312 | tf_op jit(solution)/shard_map/ppermute | solution.py:97
  24.8 6.8 %collective-permute-start.6 = (f32[8,2560]{1,0:T(8,128)S(1)}, f32[8,2560]{1,0:T(8,128)S(1)}, u32[]{:S(2)}, u32[]{:S(2)}) collective-permute-start(f32[8,2560]{1,0:T(8,128)S(1)} %get-tuple-element.53), channel_id=1, source_target_pairs={{0,4},{4,8},{8,12},{12,0},{1,5},{5,9},{9,13},{13,1},{2,6},{6,10},{... | collective-permute-start | bytes 245768 | tf_op jit(solution)/shard_map/ppermute | solution.py:113
  27.4 4.9 %collective-permute-start.8 = (f32[8,2560]{1,0:T(8,128)S(1)}, f32[8,2560]{1,0:T(8,128)S(1)}, u32[]{:S(2)}, u32[]{:S(2)}) collective-permute-start(f32[8,2560]{1,0:T(8,128)S(1)} %get-tuple-element.54), channel_id=1, source_target_pairs={{0,12},{4,0},{8,4},{12,8},{1,13},{5,1},{9,5},{13,9},{2,14},{6,2},{... | collective-permute-start | bytes 245768 | tf_op jit(solution)/shard_map/ppermute | solution.py:113
  28.7 6.8 %collective-permute-start.7 = (f32[8,2560]{1,0:T(8,128)S(1)}, f32[8,2560]{1,0:T(8,128)S(1)}, u32[]{:S(2)}, u32[]{:S(2)}) collective-permute-start(f32[8,2560]{1,0:T(8,128)S(1)} %get-tuple-element.55), channel_id=1, source_target_pairs={{0,8},{4,12},{8,0},{12,4},{1,9},{5,13},{9,1},{13,5},{2,10},{6,14},... | collective-permute-start | bytes 245768 | tf_op jit(solution)/shard_map/ppermute | solution.py:113
  35.6 20.7 %copy-start = (bf16[8,2048]{1,0:T(8,128)(2,1)S(1)}, bf16[8,2048]{1,0:T(8,128)(2,1)}, u32[]{:S(2)}) copy-start(bf16[8,2048]{1,0:T(8,128)(2,1)} %param.20) | copy-start | bytes 98308
  35.9 27.2 %copy-start.1 = (f32[2048]{0:T(1024)S(1)}, f32[2048]{0:T(1024)}, u32[]{:S(2)}) copy-start(f32[2048]{0:T(1024)} %param.24) | copy-start | bytes 24580
  37.0 4.0 %collective-permute-start.11 = (bf16[8,2048]{1,0:T(8,128)(2,1)S(1)}, bf16[8,2048]{1,0:T(8,128)(2,1)S(1)}, u32[]{:S(2)}, u32[]{:S(2)}) collective-permute-start(bf16[8,2048]{1,0:T(8,128)(2,1)S(1)} %bitcast.109), channel_id=1, source_target_pairs={{0,12},{4,0},{8,4},{12,8},{1,13},{5,1},{9,5},{13,9},{2,14},{6,2},{... | collective-permute-start | bytes 98312 | tf_op jit(solution)/shard_map/ppermute | solution.py:97
  38.9 4.8 %collective-permute-start.10 = (bf16[8,2048]{1,0:T(8,128)(2,1)S(1)}, bf16[8,2048]{1,0:T(8,128)(2,1)S(1)}, u32[]{:S(2)}, u32[]{:S(2)}) collective-permute-start(bf16[8,2048]{1,0:T(8,128)(2,1)S(1)} %bitcast.110), channel_id=1, source_target_pairs={{0,8},{4,12},{8,0},{12,4},{1,9},{5,13},{9,1},{13,5},{2,10},{6,14},... | collective-permute-start | bytes 98312 | tf_op jit(solution)/shard_map/ppermute | solution.py:97
  38.9 5.7 %collective-permute-start.9 = (bf16[8,2048]{1,0:T(8,128)(2,1)S(1)}, bf16[8,2048]{1,0:T(8,128)(2,1)S(1)}, u32[]{:S(2)}, u32[]{:S(2)}) collective-permute-start(bf16[8,2048]{1,0:T(8,128)(2,1)S(1)} %bitcast.111), channel_id=1, source_target_pairs={{0,4},{4,8},{8,12},{12,0},{1,5},{5,9},{9,13},{13,1},{2,6},{6,10},{... | collective-permute-start | bytes 98312 | tf_op jit(solution)/shard_map/ppermute | solution.py:97
  50.3 3.7 %collective-permute-start.12 = (f32[8,2048]{1,0:T(8,128)S(1)}, f32[8,2048]{1,0:T(8,128)S(1)}, u32[]{:S(2)}, u32[]{:S(2)}) collective-permute-start(f32[8,2048]{1,0:T(8,128)S(1)} %get-tuple-element.59), channel_id=1, source_target_pairs={{0,1},{1,2},{2,3},{3,0},{4,5},{5,6},{6,7},{7,4},{8,9},{9,10},{10,1... | collective-permute-start | bytes 196616 | tf_op jit(solution)/shard_map/ppermute | solution.py:113
  50.4 3.7 %collective-permute-start.14 = (f32[8,2048]{1,0:T(8,128)S(1)}, f32[8,2048]{1,0:T(8,128)S(1)}, u32[]{:S(2)}, u32[]{:S(2)}) collective-permute-start(f32[8,2048]{1,0:T(8,128)S(1)} %get-tuple-element.60), channel_id=1, source_target_pairs={{0,3},{1,0},{2,1},{3,2},{4,7},{5,4},{6,5},{7,6},{8,11},{9,8},{10,9... | collective-permute-start | bytes 196616 | tf_op jit(solution)/shard_map/ppermute | solution.py:113
  52.1 4.3 %collective-permute-start.13 = (f32[8,2048]{1,0:T(8,128)S(1)}, f32[8,2048]{1,0:T(8,128)S(1)}, u32[]{:S(2)}, u32[]{:S(2)}) collective-permute-start(f32[8,2048]{1,0:T(8,128)S(1)} %get-tuple-element.61), channel_id=1, source_target_pairs={{0,2},{1,3},{2,0},{3,1},{4,6},{5,7},{6,4},{7,5},{8,10},{9,11},{10,... | collective-permute-start | bytes 196616 | tf_op jit(solution)/shard_map/ppermute | solution.py:113
  56.5 3.6 %collective-permute-start.17 = (f32[8]{0:T(128)S(1)}, f32[8]{0:T(128)S(1)}, u32[]{:S(2)}, u32[]{:S(2)}) collective-permute-start(f32[8]{0:T(128)S(1)} %get-tuple-element.42), channel_id=1, source_target_pairs={{0,12},{4,0},{8,4},{12,8},{1,13},{5,1},{9,5},{13,9},{2,14},{6,2},{... | collective-permute-start | bytes 104 | tf_op jit(solution)/shard_map/ppermute | solution.py:120
  57.3 4.4 %collective-permute-start.16 = (f32[8]{0:T(128)S(1)}, f32[8]{0:T(128)S(1)}, u32[]{:S(2)}, u32[]{:S(2)}) collective-permute-start(f32[8]{0:T(128)S(1)} %get-tuple-element.42), channel_id=1, source_target_pairs={{0,8},{4,12},{8,0},{12,4},{1,9},{5,13},{9,1},{13,5},{2,10},{6,14},... | collective-permute-start | bytes 104 | tf_op jit(solution)/shard_map/ppermute | solution.py:120
  57.8 5.3 %collective-permute-start.15 = (f32[8]{0:T(128)S(1)}, f32[8]{0:T(128)S(1)}, u32[]{:S(2)}, u32[]{:S(2)}) collective-permute-start(f32[8]{0:T(128)S(1)} %get-tuple-element.42), channel_id=1, source_target_pairs={{0,4},{4,8},{8,12},{12,0},{1,5},{5,9},{9,13},{13,1},{2,6},{6,10},{... | collective-permute-start | bytes 104 | tf_op jit(solution)/shard_map/ppermute | solution.py:120
  63.2 1.6 %collective-permute-start.20 = (bf16[8,2048]{1,0:T(8,128)(2,1)S(1)}, bf16[8,2048]{1,0:T(8,128)(2,1)S(1)}, u32[]{:S(2)}, u32[]{:S(2)}) collective-permute-start(bf16[8,2048]{1,0:T(8,128)(2,1)S(1)} %multiply_convert_fusion), channel_id=1, source_target_pairs={{0,3},{1,0},{2,1},{3,2},{4,7},{5,4},{6,5},{7,6},{8,11},{9,8},{10,9... | collective-permute-start | bytes 98312 | tf_op jit(solution)/shard_map/ppermute | solution.py:97
  63.2 4.0 %collective-permute-start.19 = (bf16[8,2048]{1,0:T(8,128)(2,1)S(1)}, bf16[8,2048]{1,0:T(8,128)(2,1)S(1)}, u32[]{:S(2)}, u32[]{:S(2)}) collective-permute-start(bf16[8,2048]{1,0:T(8,128)(2,1)S(1)} %multiply_convert_fusion), channel_id=1, source_target_pairs={{0,2},{1,3},{2,0},{3,1},{4,6},{5,7},{6,4},{7,5},{8,10},{9,11},{10,... | collective-permute-start | bytes 98312 | tf_op jit(solution)/shard_map/ppermute | solution.py:97
  64.2 3.3 %collective-permute-start.18 = (bf16[8,2048]{1,0:T(8,128)(2,1)S(1)}, bf16[8,2048]{1,0:T(8,128)(2,1)S(1)}, u32[]{:S(2)}, u32[]{:S(2)}) collective-permute-start(bf16[8,2048]{1,0:T(8,128)(2,1)S(1)} %multiply_convert_fusion), channel_id=1, source_target_pairs={{0,1},{1,2},{2,3},{3,0},{4,5},{5,6},{6,7},{7,4},{8,9},{9,10},{10,1... | collective-permute-start | bytes 98312 | tf_op jit(solution)/shard_map/ppermute | solution.py:97
  84.1 7.9 %collective-permute-start.21 = (bf16[32,1792]{1,0:T(8,128)(2,1)S(1)}, bf16[32,1792]{1,0:T(8,128)(2,1)S(1)}, u32[]{:S(2)}, u32[]{:S(2)}) collective-permute-start(bf16[32,1792]{1,0:T(8,128)(2,1)S(1)} %get-tuple-element.50), channel_id=1, source_target_pairs={{0,4},{4,8},{8,12},{12,0},{1,5},{5,9},{9,13},{13,1},{2,6},{6,10},{... | collective-permute-start | bytes 344072 | tf_op jit(solution)/shard_map/ppermute | solution.py:113
  84.3 10.8 %collective-permute-start.22 = (bf16[32,1792]{1,0:T(8,128)(2,1)S(1)}, bf16[32,1792]{1,0:T(8,128)(2,1)S(1)}, u32[]{:S(2)}, u32[]{:S(2)}) collective-permute-start(bf16[32,1792]{1,0:T(8,128)(2,1)S(1)} %get-tuple-element.51), channel_id=1, source_target_pairs={{0,8},{4,12},{8,0},{12,4},{1,9},{5,13},{9,1},{13,5},{2,10},{6,14},... | collective-permute-start | bytes 344072 | tf_op jit(solution)/shard_map/ppermute | solution.py:113
  86.1 9.0 %collective-permute-start.23 = (bf16[32,1792]{1,0:T(8,128)(2,1)S(1)}, bf16[32,1792]{1,0:T(8,128)(2,1)S(1)}, u32[]{:S(2)}, u32[]{:S(2)}) collective-permute-start(bf16[32,1792]{1,0:T(8,128)(2,1)S(1)} %get-tuple-element.52), channel_id=1, source_target_pairs={{0,12},{4,0},{8,4},{12,8},{1,13},{5,1},{9,5},{13,9},{2,14},{6,2},{... | collective-permute-start | bytes 344072 | tf_op jit(solution)/shard_map/ppermute | solution.py:113
  95.2 11.1 %collective-permute-start.26 = (bf16[32,896]{1,0:T(8,128)(2,1)S(1)}, bf16[32,896]{1,0:T(8,128)(2,1)S(1)}, u32[]{:S(2)}, u32[]{:S(2)}) collective-permute-start(bf16[32,896]{1,0:T(8,128)(2,1)S(1)} %fusion.41), channel_id=1, source_target_pairs={{0,12},{4,0},{8,4},{12,8},{1,13},{5,1},{9,5},{13,9},{2,14},{6,2},{... | collective-permute-start | bytes 172040 | tf_op jit(solution)/shard_map/ppermute | solution.py:131
  97.9 5.6 %collective-permute-start.25 = (bf16[32,896]{1,0:T(8,128)(2,1)S(1)}, bf16[32,896]{1,0:T(8,128)(2,1)S(1)}, u32[]{:S(2)}, u32[]{:S(2)}) collective-permute-start(bf16[32,896]{1,0:T(8,128)(2,1)S(1)} %fusion.41), channel_id=1, source_target_pairs={{0,8},{4,12},{8,0},{12,4},{1,9},{5,13},{9,1},{13,5},{2,10},{6,14},... | collective-permute-start | bytes 172040 | tf_op jit(solution)/shard_map/ppermute | solution.py:131
  98.7 10.4 %collective-permute-start.24 = (bf16[32,896]{1,0:T(8,128)(2,1)S(1)}, bf16[32,896]{1,0:T(8,128)(2,1)S(1)}, u32[]{:S(2)}, u32[]{:S(2)}) collective-permute-start(bf16[32,896]{1,0:T(8,128)(2,1)S(1)} %fusion.41), channel_id=1, source_target_pairs={{0,4},{4,8},{8,12},{12,0},{1,5},{5,9},{9,13},{13,1},{2,6},{6,10},{... | collective-permute-start | bytes 172040 | tf_op jit(solution)/shard_map/ppermute | solution.py:131
  112.0 3.7 %collective-permute-start.27 = (f32[8,2048]{1,0:T(8,128)S(1)}, f32[8,2048]{1,0:T(8,128)S(1)}, u32[]{:S(2)}, u32[]{:S(2)}) collective-permute-start(f32[8,2048]{1,0:T(8,128)S(1)} %get-tuple-element.56), channel_id=1, source_target_pairs={{0,1},{1,2},{2,3},{3,0},{4,5},{5,6},{6,7},{7,4},{8,9},{9,10},{10,1... | collective-permute-start | bytes 196616 | tf_op jit(solution)/shard_map/ppermute | solution.py:113
  112.0 3.7 %collective-permute-start.29 = (f32[8,2048]{1,0:T(8,128)S(1)}, f32[8,2048]{1,0:T(8,128)S(1)}, u32[]{:S(2)}, u32[]{:S(2)}) collective-permute-start(f32[8,2048]{1,0:T(8,128)S(1)} %get-tuple-element.57), channel_id=1, source_target_pairs={{0,3},{1,0},{2,1},{3,2},{4,7},{5,4},{6,5},{7,6},{8,11},{9,8},{10,9... | collective-permute-start | bytes 196616 | tf_op jit(solution)/shard_map/ppermute | solution.py:113
  113.8 4.3 %collective-permute-start.28 = (f32[8,2048]{1,0:T(8,128)S(1)}, f32[8,2048]{1,0:T(8,128)S(1)}, u32[]{:S(2)}, u32[]{:S(2)}) collective-permute-start(f32[8,2048]{1,0:T(8,128)S(1)} %get-tuple-element.58), channel_id=1, source_target_pairs={{0,2},{1,3},{2,0},{3,1},{4,6},{5,7},{6,4},{7,5},{8,10},{9,11},{10,... | collective-permute-start | bytes 196616 | tf_op jit(solution)/shard_map/ppermute | solution.py:113

commit v6 on v5

--- a/solution.py
+++ b/solution.py
@@ -170,6 +170,7 @@
     qkv_part = jnp.einsum(
         "rf,fgc->rgc", by_slot, w_qkv, preferred_element_type=jnp.float32
     ).reshape(rows_total, -1)
+    qkv_part, kv_cache = lax.optimization_barrier((qkv_part, kv_cache))
     summed = scatter_sum(qkv_part.reshape(n_pool, per_owner, -1), "pool", n_pool)
     rotated = rope_rows(summed, positions, per_group, HD)
     attended = attend(rotated, kv_cache, positions, per_group, HD)

time: 119 us -> 118 us (level)
  local copies, waits for them, and re-layouts: 5.25 us -> 2.58 us
  waiting for transfers between devices: 37.2 us -> 38.5 us
    slice x1 -> x0, local copies, waits for them, and re-layouts: 2.68 us -> none  [attend(): cache_keys = kv_block[:, :, 0]]
    ppermute x6, waiting for transfers between devices: 3.4 us -> 5.61 us  [all_sum(): total = total + lax.ppermute(x, axis, shift_pairs(n, k))]
  transfers between devices with their start and end apart: 30 -> 30, of which waited for: 21 -> 22; matrix products, arithmetic and copies ran while one was open for 11% -> 9% of each run, Pallas kernels for 0% -> 0%
where the time goes in v6:
time: 118 us; the launch traced here: 117 us
  matrix products  38.7 us (33%)
  waiting for transfers between devices  38.5 us (33%)
  starting transfers between devices  31.3 us (27%)
  other arithmetic  5.6 us (5%)
  local copies, waits for them, and re-layouts  2.58 us (2%)
    ppermute x12, waiting for transfers between devices, scatter_sum(): lax.ppermute(piece, axis, shift_pairs(n, k)).astype(jnp.float32)  19.5 us
    ppermute x12, starting transfers between devices, scatter_sum(): lax.ppermute(piece, axis, shift_pairs(n, k)).astype(jnp.float32)  13 us
    ppermute x9, waiting for transfers between devices, gather_rows(): got = [x] + [lax.ppermute(x, axis, shift_pairs(n, k)) for k in range(1, n)]  11.3 us
    ppermute x6, starting transfers between devices, all_sum(): total = total + lax.ppermute(x, axis, shift_pairs(n, k))  9.3 us
    dot_general x3, matrix products, gather_matmul(): acc = acc + jnp.dot(got, rows, preferred_element_type=jnp.float32)  8.39 us
    dot_general x1, matrix products, local(): jnp.dot(ffn_all, w_gate, preferred_element_type=jnp.float32)  7.86 us
    dot_general x1, matrix products, local(): jnp.dot(ffn_all, w_up, preferred_element_type=jnp.float32)  7.85 us
    dot_general x1, matrix products, local(): jnp.einsum('rf,fgc->rgc', by_slot, w_qkv, preferred_element_type=jnp.floa...  5.94 us
  transfers between devices with their start and end apart: 30, of which 22 were waited for; matrix products, arithmetic and copies ran while one was open for 9% of the time, Pallas kernels for 0%

profile of v6, /device:TPU:0, one launch (start us, length us, event | category | flops | bytes accessed | tf_op | source)
XLA Modules:
  0.0 117.1 jit_solution(2183143345806301868)
XLA Ops:
  1.0 5.1 %collective-permute-start.2 = (f32[8]{0:T(128)S(1)}, f32[8]{0:T(128)S(1)}, u32[]{:S(2)}, u32[]{:S(2)}) collective-permute-start(f32[8]{0:T(128)S(1)} %fusion.48), channel_id=1, source_target_pairs={{0,12},{4,0},{8,4},{12,8},{1,13},{5,1},{9,5},{13,9},{2,14},{6,2},{... | collective-permute-start | bytes 104 | tf_op jit(solution)/shard_map/ppermute | solution.py:120
  9.3 1.3 %collective-permute-done.1 = f32[8]{0:T(128)S(1)} collective-permute-done((f32[8]{0:T(128)S(1)}, f32[8]{0:T(128)S(1)}, u32[]{:S(2)}, u32[]{:S(2)}) %collective-permute-start.1) | collective-permute-done | bytes 64 | tf_op jit(solution)/shard_map/ppermute | solution.py:120
  12.4 1.6 %collective-permute-start.4 = (bf16[8,2048]{1,0:T(8,128)(2,1)S(1)}, bf16[8,2048]{1,0:T(8,128)(2,1)S(1)}, u32[]{:S(2)}, u32[]{:S(2)}) collective-permute-start(bf16[8,2048]{1,0:T(8,128)(2,1)S(1)} %fusion.50), channel_id=1, source_target_pairs={{0,2},{1,3},{2,0},{3,1},{4,6},{5,7},{6,4},{7,5},{8,10},{9,11},{10,... | collective-permute-start | bytes 98312 | tf_op jit(solution)/shard_map/ppermute | solution.py:97
  14.1 2.3 %collective-permute-done.4 = bf16[8,2048]{1,0:T(8,128)(2,1)S(1)} collective-permute-done((bf16[8,2048]{1,0:T(8,128)(2,1)S(1)}, bf16[8,2048]{1,0:T(8,128)(2,1)S(1)}, u32[]{:S(2)}, u32[]{:S(2)}) %collective-permute-start.4) | collective-permute-done | bytes 32800 | tf_op jit(solution)/shard_map/ppermute | solution.py:97
  18.0 5.9 %fusion.10 = f32[2,4,8,1280]{3,2,1,0:T(8,128)S(1)} fusion(bf16[2048,2,1280]{2,1,0:T(2,128)(2,1)} %param.22, bf16[32,2048]{1,0:T(8,128)(2,1)S(1)} %gather_fusion, pred[32]{0:T(512)(128)(4,1)S(1)} %get-tuple-element.50), kind=kOutput, calls=%fused_computation.15 | convolution fusion | flops 335609856 | bytes 10944544 | tf_op jit(solution)/shard_map/rf,fgc->rgc/dot_general | solution.py:170
  24.3 3.5 %collective-permute-start.8 = (f32[8,2560]{1,0:T(8,128)S(1)}, f32[8,2560]{1,0:T(8,128)S(1)}, u32[]{:S(2)}, u32[]{:S(2)}) collective-permute-start(f32[8,2560]{1,0:T(8,128)S(1)} %get-tuple-element.56), channel_id=1, source_target_pairs={{0,12},{4,0},{8,4},{12,8},{1,13},{5,1},{9,5},{13,9},{2,14},{6,2},{... | collective-permute-start | bytes 245768 | tf_op jit(solution)/shard_map/ppermute | solution.py:113
  28.4 2.7 %collective-permute-done.6 = f32[8,2560]{1,0:T(8,128)S(1)} collective-permute-done((f32[8,2560]{1,0:T(8,128)S(1)}, f32[8,2560]{1,0:T(8,128)S(1)}, u32[]{:S(2)}, u32[]{:S(2)}) %collective-permute-start.6) | collective-permute-done | bytes 81952 | tf_op jit(solution)/shard_map/ppermute | solution.py:113
  31.1 2.9 %collective-permute-done.7 = f32[8,2560]{1,0:T(8,128)S(1)} collective-permute-done((f32[8,2560]{1,0:T(8,128)S(1)}, f32[8,2560]{1,0:T(8,128)S(1)}, u32[]{:S(2)}, u32[]{:S(2)}) %collective-permute-start.7) | collective-permute-done | bytes 81952 | tf_op jit(solution)/shard_map/ppermute | solution.py:113
  35.4 1.8 %collective-permute-start.11 = (bf16[8,2048]{1,0:T(8,128)(2,1)S(1)}, bf16[8,2048]{1,0:T(8,128)(2,1)S(1)}, u32[]{:S(2)}, u32[]{:S(2)}) collective-permute-start(bf16[8,2048]{1,0:T(8,128)(2,1)S(1)} %bitcast.115), channel_id=1, source_target_pairs={{0,12},{4,0},{8,4},{12,8},{1,13},{5,1},{9,5},{13,9},{2,14},{6,2},{... | collective-permute-start | bytes 98312 | tf_op jit(solution)/shard_map/ppermute | solution.py:97
  38.0 1.4 %collective-permute-done.11 = bf16[8,2048]{1,0:T(8,128)(2,1)S(1)} collective-permute-done((bf16[8,2048]{1,0:T(8,128)(2,1)S(1)}, bf16[8,2048]{1,0:T(8,128)(2,1)S(1)}, u32[]{:S(2)}, u32[]{:S(2)}) %collective-permute-start.11) | collective-permute-done | bytes 32800 | tf_op jit(solution)/shard_map/ppermute | solution.py:97
  39.4 2.7 %collective-permute-done.10 = bf16[8,2048]{1,0:T(8,128)(2,1)S(1)} collective-permute-done((bf16[8,2048]{1,0:T(8,128)(2,1)S(1)}, bf16[8,2048]{1,0:T(8,128)(2,1)S(1)}, u32[]{:S(2)}, u32[]{:S(2)}) %collective-permute-start.10) | collective-permute-done | bytes 32800 | tf_op jit(solution)/shard_map/ppermute | solution.py:97
  43.7 5.0 %convolution_bitcast_fusion = f32[4,8,2048]{2,1,0:T(8,128)S(1)} fusion(bf16[2048,2048]{1,0:T(8,128)(2,1)} %param.23, bf16[32,2048]{1,0:T(8,128)(2,1)S(1)} %gather_fusion.1, pred[32]{0:T(512)(128)(4,1)S(1)} %get-tuple-element.48), kind=kOutput, calls=%fused_computation.20 | convolution fusion | flops 268500992 | bytes 8781856 | tf_op jit(solution)/shard_map/dot_general | solution.py:178
  48.7 1.7 %collective-permute-start.14 = (f32[8,2048]{1,0:T(8,128)S(1)}, f32[8,2048]{1,0:T(8,128)S(1)}, u32[]{:S(2)}, u32[]{:S(2)}) collective-permute-start(f32[8,2048]{1,0:T(8,128)S(1)} %get-tuple-element.62), channel_id=1, source_target_pairs={{0,3},{1,0},{2,1},{3,2},{4,7},{5,4},{6,5},{7,6},{8,11},{9,8},{10,9... | collective-permute-start | bytes 196616 | tf_op jit(solution)/shard_map/ppermute | solution.py:113
  52.4 2.3 %collective-permute-done.13 = f32[8,2048]{1,0:T(8,128)S(1)} collective-permute-done((f32[8,2048]{1,0:T(8,128)S(1)}, f32[8,2048]{1,0:T(8,128)S(1)}, u32[]{:S(2)}, u32[]{:S(2)}) %collective-permute-start.13) | collective-permute-done | bytes 65568 | tf_op jit(solution)/shard_map/ppermute | solution.py:113
  56.1 1.9 %collective-permute-start.15 = (f32[8]{0:T(128)S(1)}, f32[8]{0:T(128)S(1)}, u32[]{:S(2)}, u32[]{:S(2)}) collective-permute-start(f32[8]{0:T(128)S(1)} %get-tuple-element.46), channel_id=1, source_target_pairs={{0,4},{4,8},{8,12},{12,0},{1,5},{5,9},{9,13},{13,1},{2,6},{6,10},{... | collective-permute-start | bytes 104 | tf_op jit(solution)/shard_map/ppermute | solution.py:120
  58.5 1.7 %collective-permute-done.16 = f32[8]{0:T(128)S(1)} collective-permute-done((f32[8]{0:T(128)S(1)}, f32[8]{0:T(128)S(1)}, u32[]{:S(2)}, u32[]{:S(2)}) %collective-permute-start.16) | collective-permute-done | bytes 64 | tf_op jit(solution)/shard_map/ppermute | solution.py:120
  60.2 1.3 %collective-permute-done.15 = f32[8]{0:T(128)S(1)} collective-permute-done((f32[8]{0:T(128)S(1)}, f32[8]{0:T(128)S(1)}, u32[]{:S(2)}, u32[]{:S(2)}) %collective-permute-start.15) | collective-permute-done | bytes 64 | tf_op jit(solution)/shard_map/ppermute | solution.py:120
  63.2 2.4 %collective-permute-done.19 = bf16[8,2048]{1,0:T(8,128)(2,1)S(1)} collective-permute-done((bf16[8,2048]{1,0:T(8,128)(2,1)S(1)}, bf16[8,2048]{1,0:T(8,128)(2,1)S(1)}, u32[]{:S(2)}, u32[]{:S(2)}) %collective-permute-start.19) | collective-permute-done | bytes 32800 | tf_op jit(solution)/shard_map/ppermute | solution.py:97
  66.6 7.9 %convolution_convert_fusion = bf16[32,3584]{1,0:T(8,128)(2,1)S(1)} fusion(bf16[2048,3584]{1,0:T(8,128)(2,1)} %param.26, bf16[32,2048]{1,0:T(8,128)(2,1)S(1)} %gather_fusion.2, pred[32]{0:T(512)(128)(4,1)S(1)} %compare_and_fusion), kind=kOutput, calls=%fused_computation.5 | convolution fusion | flops 469942272 | bytes 15040544 | tf_op jit(solution)/shard_map/dot_general | solution.py:188
  74.4 7.9 %convolution_convert_fusion.1 = bf16[32,3584]{1,0:T(8,128)(2,1)S(1)} fusion(bf16[2048,3584]{1,0:T(8,128)(2,1)} %param.25, bf16[32,2048]{1,0:T(8,128)(2,1)S(1)} %gather_fusion.2, pred[32]{0:T(512)(128)(4,1)S(1)} %compare_and_fusion), kind=kOutput, calls=%fused_computation.6 | convolution fusion | flops 469942272 | bytes 15040544 | tf_op jit(solution)/shard_map/dot_general | solution.py:187
  82.6 1.8 %collective-permute-start.22 = (bf16[32,1792]{1,0:T(8,128)(2,1)S(1)}, bf16[32,1792]{1,0:T(8,128)(2,1)S(1)}, u32[]{:S(2)}, u32[]{:S(2)}) collective-permute-start(bf16[32,1792]{1,0:T(8,128)(2,1)S(1)} %get-tuple-element.53), channel_id=1, source_target_pairs={{0,8},{4,12},{8,0},{12,4},{1,9},{5,13},{9,1},{13,5},{2,10},{6,14},... | collective-permute-start | bytes 344072 | tf_op jit(solution)/shard_map/ppermute | solution.py:113
  84.4 1.9 %collective-permute-start.23 = (bf16[32,1792]{1,0:T(8,128)(2,1)S(1)}, bf16[32,1792]{1,0:T(8,128)(2,1)S(1)}, u32[]{:S(2)}, u32[]{:S(2)}) collective-permute-start(bf16[32,1792]{1,0:T(8,128)(2,1)S(1)} %get-tuple-element.54), channel_id=1, source_target_pairs={{0,12},{4,0},{8,4},{12,8},{1,13},{5,1},{9,5},{13,9},{2,14},{6,2},{... | collective-permute-start | bytes 344072 | tf_op jit(solution)/shard_map/ppermute | solution.py:113
  86.3 4.1 %collective-permute-done.21 = bf16[32,1792]{1,0:T(8,128)(2,1)S(1)} collective-permute-done((bf16[32,1792]{1,0:T(8,128)(2,1)S(1)}, bf16[32,1792]{1,0:T(8,128)(2,1)S(1)}, u32[]{:S(2)}, u32[]{:S(2)}) %collective-permute-start.21) | collective-permute-done | bytes 114720 | tf_op jit(solution)/shard_map/ppermute | solution.py:113
  90.4 3.0 %collective-permute-done.22 = bf16[32,1792]{1,0:T(8,128)(2,1)S(1)} collective-permute-done((bf16[32,1792]{1,0:T(8,128)(2,1)S(1)}, bf16[32,1792]{1,0:T(8,128)(2,1)S(1)}, u32[]{:S(2)}, u32[]{:S(2)}) %collective-permute-start.22) | collective-permute-done | bytes 114720 | tf_op jit(solution)/shard_map/ppermute | solution.py:113
  93.5 2.7 %collective-permute-start.26 = (bf16[32,896]{1,0:T(8,128)(2,1)S(1)}, bf16[32,896]{1,0:T(8,128)(2,1)S(1)}, u32[]{:S(2)}, u32[]{:S(2)}) collective-permute-start(bf16[32,896]{1,0:T(8,128)(2,1)S(1)} %fusion.44), channel_id=1, source_target_pairs={{0,12},{4,0},{8,4},{12,8},{1,13},{5,1},{9,5},{13,9},{2,14},{6,2},{... | collective-permute-start | bytes 172040 | tf_op jit(solution)/shard_map/ppermute | solution.py:131
  97.1 2.8 %fusion.8 = f32[32,2048]{1,0:T(8,128)S(1)} fusion(bf16[32,896]{1,0:T(8,128)(2,1)S(1)} %fusion.44, bf16[3584,2048]{1,0:T(8,128)(2,1)} %param.27, s32[]{:T(128)S(6)} %select_n.162), kind=kOutput, calls=%fused_computation.13 | convolution fusion | flops 117440512 | bytes 3989508 | tf_op jit(solution)/shard_map/dot_general | solution.py:127
  99.9 2.0 %collective-permute-done.25 = bf16[32,896]{1,0:T(8,128)(2,1)S(1)} collective-permute-done((bf16[32,896]{1,0:T(8,128)(2,1)S(1)}, bf16[32,896]{1,0:T(8,128)(2,1)S(1)}, u32[]{:S(2)}, u32[]{:S(2)}) %collective-permute-start.25) | collective-permute-done | bytes 57376 | tf_op jit(solution)/shard_map/ppermute | solution.py:131
  101.9 2.8 %fusion.4 = f32[32,2048]{1,0:T(8,128)S(1)} fusion(bf16[32,896]{1,0:T(8,128)(2,1)S(1)} %collective-permute-done.25, bf16[3584,2048]{1,0:T(8,128)(2,1)} %param.27, s32[]{:T(128)S(6)} %select_n.166), kind=kOutput, calls=%fused_computation.9 | convolution fusion | flops 117440512 | bytes 3989508 | tf_op jit(solution)/shard_map/dot_general | solution.py:133
  104.7 2.8 %fusion.2 = f32[32,2048]{1,0:T(8,128)S(1)} fusion(bf16[32,896]{1,0:T(8,128)(2,1)S(1)} %collective-permute-done.26, bf16[3584,2048]{1,0:T(8,128)(2,1)} %param.27, s32[]{:T(128)S(6)} %select_n.168), kind=kOutput, calls=%fused_computation.7 | convolution fusion | flops 117440512 | bytes 3989508 | tf_op jit(solution)/shard_map/dot_general | solution.py:133
  107.5 2.8 %fusion.22 = f32[4,8,2048]{2,1,0:T(8,128)S(1)} fusion(f32[32,2048]{1,0:T(8,128)S(1)} %fusion.2, f32[32,2048]{1,0:T(8,128)S(1)} %fusion.4, f32[32,2048]{1,0:T(8,128)S(1)} %fusion.8, bf16[32,896]{1,0:T(8,128)(2,1)S(1)} %collective-permute-done.24, bf16[3584,2048]{1,0:T(8,128)(2,1)} %param.27, s32[]{:T(128)S(6)} %select_n.164), kind=kOutput, calls=%fused_computation.19 | convolution fusion | flops 117637120 | bytes 4775940 | tf_op jit(solution)/shard_map/dot_general | solution.py:133
  110.4 1.7 %collective-permute-start.29 = (f32[8,2048]{1,0:T(8,128)S(1)}, f32[8,2048]{1,0:T(8,128)S(1)}, u32[]{:S(2)}, u32[]{:S(2)}) collective-permute-start(f32[8,2048]{1,0:T(8,128)S(1)} %get-tuple-element.59), channel_id=1, source_target_pairs={{0,3},{1,0},{2,1},{3,2},{4,7},{5,4},{6,5},{7,6},{8,11},{9,8},{10,9... | collective-permute-start | bytes 196616 | tf_op jit(solution)/shard_map/ppermute | solution.py:113
  114.1 2.3 %collective-permute-done.28 = f32[8,2048]{1,0:T(8,128)S(1)} collective-permute-done((f32[8,2048]{1,0:T(8,128)S(1)}, f32[8,2048]{1,0:T(8,128)S(1)}, u32[]{:S(2)}, u32[]{:S(2)}) %collective-permute-start.28) | collective-permute-done | bytes 65568 | tf_op jit(solution)/shard_map/ppermute | solution.py:113
  (94 shorter events, 22.5 us)
Async XLA Ops:
  0.0 27.9 %copy-start = (bf16[8,256,2,2,128]{4,3,2,1,0:T(2,128)(2,1)S(1)}, bf16[8,256,2,2,128]{4,3,2,1,0:T(2,128)(2,1)}, u32[]{:S(2)}) copy-start(bf16[8,256,2,2,128]{4,3,2,1,0:T(2,128)(2,1)} %param.28) | copy-start | bytes 6291460
  1.0 8.2 %collective-permute-start.2 = (f32[8]{0:T(128)S(1)}, f32[8]{0:T(128)S(1)}, u32[]{:S(2)}, u32[]{:S(2)}) collective-permute-start(f32[8]{0:T(128)S(1)} %fusion.48), channel_id=1, source_target_pairs={{0,12},{4,0},{8,4},{12,8},{1,13},{5,1},{9,5},{13,9},{2,14},{6,2},{... | collective-permute-start | bytes 104 | tf_op jit(solution)/shard_map/ppermute | solution.py:120
  6.1 4.4 %collective-permute-start.1 = (f32[8]{0:T(128)S(1)}, f32[8]{0:T(128)S(1)}, u32[]{:S(2)}, u32[]{:S(2)}) collective-permute-start(f32[8]{0:T(128)S(1)} %fusion.48), channel_id=1, source_target_pairs={{0,8},{4,12},{8,0},{12,4},{1,9},{5,13},{9,1},{13,5},{2,10},{6,14},... | collective-permute-start | bytes 104 | tf_op jit(solution)/shard_map/ppermute | solution.py:120
  6.1 5.3 %collective-permute-start = (f32[8]{0:T(128)S(1)}, f32[8]{0:T(128)S(1)}, u32[]{:S(2)}, u32[]{:S(2)}) collective-permute-start(f32[8]{0:T(128)S(1)} %fusion.48), channel_id=1, source_target_pairs={{0,4},{4,8},{8,12},{12,0},{1,5},{5,9},{9,13},{13,1},{2,6},{6,10},{... | collective-permute-start | bytes 104 | tf_op jit(solution)/shard_map/ppermute | solution.py:120
  12.3 1.8 %collective-permute-start.5 = (bf16[8,2048]{1,0:T(8,128)(2,1)S(1)}, bf16[8,2048]{1,0:T(8,128)(2,1)S(1)}, u32[]{:S(2)}, u32[]{:S(2)}) collective-permute-start(bf16[8,2048]{1,0:T(8,128)(2,1)S(1)} %fusion.50), channel_id=1, source_target_pairs={{0,3},{1,0},{2,1},{3,2},{4,7},{5,4},{6,5},{7,6},{8,11},{9,8},{10,9... | collective-permute-start | bytes 98312 | tf_op jit(solution)/shard_map/ppermute | solution.py:97
  12.4 4.1 %collective-permute-start.4 = (bf16[8,2048]{1,0:T(8,128)(2,1)S(1)}, bf16[8,2048]{1,0:T(8,128)(2,1)S(1)}, u32[]{:S(2)}, u32[]{:S(2)}) collective-permute-start(bf16[8,2048]{1,0:T(8,128)(2,1)S(1)} %fusion.50), channel_id=1, source_target_pairs={{0,2},{1,3},{2,0},{3,1},{4,6},{5,7},{6,4},{7,5},{8,10},{9,11},{10,... | collective-permute-start | bytes 98312 | tf_op jit(solution)/shard_map/ppermute | solution.py:97
  13.9 3.3 %collective-permute-start.3 = (bf16[8,2048]{1,0:T(8,128)(2,1)S(1)}, bf16[8,2048]{1,0:T(8,128)(2,1)S(1)}, u32[]{:S(2)}, u32[]{:S(2)}) collective-permute-start(bf16[8,2048]{1,0:T(8,128)(2,1)S(1)} %fusion.50), channel_id=1, source_target_pairs={{0,1},{1,2},{2,3},{3,0},{4,5},{5,6},{6,7},{7,4},{8,9},{9,10},{10,1... | collective-permute-start | bytes 98312 | tf_op jit(solution)/shard_map/ppermute | solution.py:97
  24.0 7.1 %collective-permute-start.6 = (f32[8,2560]{1,0:T(8,128)S(1)}, f32[8,2560]{1,0:T(8,128)S(1)}, u32[]{:S(2)}, u32[]{:S(2)}) collective-permute-start(f32[8,2560]{1,0:T(8,128)S(1)} %get-tuple-element.55), channel_id=1, source_target_pairs={{0,4},{4,8},{8,12},{12,0},{1,5},{5,9},{9,13},{13,1},{2,6},{6,10},{... | collective-permute-start | bytes 245768 | tf_op jit(solution)/shard_map/ppermute | solution.py:113
  24.3 6.7 %collective-permute-start.8 = (f32[8,2560]{1,0:T(8,128)S(1)}, f32[8,2560]{1,0:T(8,128)S(1)}, u32[]{:S(2)}, u32[]{:S(2)}) collective-permute-start(f32[8,2560]{1,0:T(8,128)S(1)} %get-tuple-element.56), channel_id=1, source_target_pairs={{0,12},{4,0},{8,4},{12,8},{1,13},{5,1},{9,5},{13,9},{2,14},{6,2},{... | collective-permute-start | bytes 245768 | tf_op jit(solution)/shard_map/ppermute | solution.py:113
  27.8 6.1 %collective-permute-start.7 = (f32[8,2560]{1,0:T(8,128)S(1)}, f32[8,2560]{1,0:T(8,128)S(1)}, u32[]{:S(2)}, u32[]{:S(2)}) collective-permute-start(f32[8,2560]{1,0:T(8,128)S(1)} %get-tuple-element.57), channel_id=1, source_target_pairs={{0,8},{4,12},{8,0},{12,4},{1,9},{5,13},{9,1},{13,5},{2,10},{6,14},... | collective-permute-start | bytes 245768 | tf_op jit(solution)/shard_map/ppermute | solution.py:113
  34.4 27.1 %copy-start.2 = (f32[2048]{0:T(1024)S(1)}, f32[2048]{0:T(1024)}, u32[]{:S(2)}) copy-start(f32[2048]{0:T(1024)} %param.24) | copy-start | bytes 24580
  35.4 4.0 %collective-permute-start.11 = (bf16[8,2048]{1,0:T(8,128)(2,1)S(1)}, bf16[8,2048]{1,0:T(8,128)(2,1)S(1)}, u32[]{:S(2)}, u32[]{:S(2)}) collective-permute-start(bf16[8,2048]{1,0:T(8,128)(2,1)S(1)} %bitcast.115), channel_id=1, source_target_pairs={{0,12},{4,0},{8,4},{12,8},{1,13},{5,1},{9,5},{13,9},{2,14},{6,2},{... | collective-permute-start | bytes 98312 | tf_op jit(solution)/shard_map/ppermute | solution.py:97
  37.3 4.9 %collective-permute-start.10 = (bf16[8,2048]{1,0:T(8,128)(2,1)S(1)}, bf16[8,2048]{1,0:T(8,128)(2,1)S(1)}, u32[]{:S(2)}, u32[]{:S(2)}) collective-permute-start(bf16[8,2048]{1,0:T(8,128)(2,1)S(1)} %bitcast.116), channel_id=1, source_target_pairs={{0,8},{4,12},{8,0},{12,4},{1,9},{5,13},{9,1},{13,5},{2,10},{6,14},... | collective-permute-start | bytes 98312 | tf_op jit(solution)/shard_map/ppermute | solution.py:97
  37.3 5.7 %collective-permute-start.9 = (bf16[8,2048]{1,0:T(8,128)(2,1)S(1)}, bf16[8,2048]{1,0:T(8,128)(2,1)S(1)}, u32[]{:S(2)}, u32[]{:S(2)}) collective-permute-start(bf16[8,2048]{1,0:T(8,128)(2,1)S(1)} %bitcast.117), channel_id=1, source_target_pairs={{0,4},{4,8},{8,12},{12,0},{1,5},{5,9},{9,13},{13,1},{2,6},{6,10},{... | collective-permute-start | bytes 98312 | tf_op jit(solution)/shard_map/ppermute | solution.py:97
  48.7 3.7 %collective-permute-start.12 = (f32[8,2048]{1,0:T(8,128)S(1)}, f32[8,2048]{1,0:T(8,128)S(1)}, u32[]{:S(2)}, u32[]{:S(2)}) collective-permute-start(f32[8,2048]{1,0:T(8,128)S(1)} %get-tuple-element.61), channel_id=1, source_target_pairs={{0,1},{1,2},{2,3},{3,0},{4,5},{5,6},{6,7},{7,4},{8,9},{9,10},{10,1... | collective-permute-start | bytes 196616 | tf_op jit(solution)/shard_map/ppermute | solution.py:113
  48.7 3.7 %collective-permute-start.14 = (f32[8,2048]{1,0:T(8,128)S(1)}, f32[8,2048]{1,0:T(8,128)S(1)}, u32[]{:S(2)}, u32[]{:S(2)}) collective-permute-start(f32[8,2048]{1,0:T(8,128)S(1)} %get-tuple-element.62), channel_id=1, source_target_pairs={{0,3},{1,0},{2,1},{3,2},{4,7},{5,4},{6,5},{7,6},{8,11},{9,8},{10,9... | collective-permute-start | bytes 196616 | tf_op jit(solution)/shard_map/ppermute | solution.py:113
  50.5 4.3 %collective-permute-start.13 = (f32[8,2048]{1,0:T(8,128)S(1)}, f32[8,2048]{1,0:T(8,128)S(1)}, u32[]{:S(2)}, u32[]{:S(2)}) collective-permute-start(f32[8,2048]{1,0:T(8,128)S(1)} %get-tuple-element.63), channel_id=1, source_target_pairs={{0,2},{1,3},{2,0},{3,1},{4,6},{5,7},{6,4},{7,5},{8,10},{9,11},{10,... | collective-permute-start | bytes 196616 | tf_op jit(solution)/shard_map/ppermute | solution.py:113
  54.9 3.6 %collective-permute-start.17 = (f32[8]{0:T(128)S(1)}, f32[8]{0:T(128)S(1)}, u32[]{:S(2)}, u32[]{:S(2)}) collective-permute-start(f32[8]{0:T(128)S(1)} %get-tuple-element.46), channel_id=1, source_target_pairs={{0,12},{4,0},{8,4},{12,8},{1,13},{5,1},{9,5},{13,9},{2,14},{6,2},{... | collective-permute-start | bytes 104 | tf_op jit(solution)/shard_map/ppermute | solution.py:120
  55.7 4.4 %collective-permute-start.16 = (f32[8]{0:T(128)S(1)}, f32[8]{0:T(128)S(1)}, u32[]{:S(2)}, u32[]{:S(2)}) collective-permute-start(f32[8]{0:T(128)S(1)} %get-tuple-element.46), channel_id=1, source_target_pairs={{0,8},{4,12},{8,0},{12,4},{1,9},{5,13},{9,1},{13,5},{2,10},{6,14},... | collective-permute-start | bytes 104 | tf_op jit(solution)/shard_map/ppermute | solution.py:120
  56.1 5.3 %collective-permute-start.15 = (f32[8]{0:T(128)S(1)}, f32[8]{0:T(128)S(1)}, u32[]{:S(2)}, u32[]{:S(2)}) collective-permute-start(f32[8]{0:T(128)S(1)} %get-tuple-element.46), channel_id=1, source_target_pairs={{0,4},{4,8},{8,12},{12,0},{1,5},{5,9},{9,13},{13,1},{2,6},{6,10},{... | collective-permute-start | bytes 104 | tf_op jit(solution)/shard_map/ppermute | solution.py:120
  61.6 1.6 %collective-permute-start.20 = (bf16[8,2048]{1,0:T(8,128)(2,1)S(1)}, bf16[8,2048]{1,0:T(8,128)(2,1)S(1)}, u32[]{:S(2)}, u32[]{:S(2)}) collective-permute-start(bf16[8,2048]{1,0:T(8,128)(2,1)S(1)} %multiply_convert_fusion), channel_id=1, source_target_pairs={{0,3},{1,0},{2,1},{3,2},{4,7},{5,4},{6,5},{7,6},{8,11},{9,8},{10,9... | collective-permute-start | bytes 98312 | tf_op jit(solution)/shard_map/ppermute | solution.py:97
  61.6 4.0 %collective-permute-start.19 = (bf16[8,2048]{1,0:T(8,128)(2,1)S(1)}, bf16[8,2048]{1,0:T(8,128)(2,1)S(1)}, u32[]{:S(2)}, u32[]{:S(2)}) collective-permute-start(bf16[8,2048]{1,0:T(8,128)(2,1)S(1)} %multiply_convert_fusion), channel_id=1, source_target_pairs={{0,2},{1,3},{2,0},{3,1},{4,6},{5,7},{6,4},{7,5},{8,10},{9,11},{10,... | collective-permute-start | bytes 98312 | tf_op jit(solution)/shard_map/ppermute | solution.py:97
  62.6 3.4 %collective-permute-start.18 = (bf16[8,2048]{1,0:T(8,128)(2,1)S(1)}, bf16[8,2048]{1,0:T(8,128)(2,1)S(1)}, u32[]{:S(2)}, u32[]{:S(2)}) collective-permute-start(bf16[8,2048]{1,0:T(8,128)(2,1)S(1)} %multiply_convert_fusion), channel_id=1, source_target_pairs={{0,1},{1,2},{2,3},{3,0},{4,5},{5,6},{6,7},{7,4},{8,9},{9,10},{10,1... | collective-permute-start | bytes 98312 | tf_op jit(solution)/shard_map/ppermute | solution.py:97
  82.4 7.9 %collective-permute-start.21 = (bf16[32,1792]{1,0:T(8,128)(2,1)S(1)}, bf16[32,1792]{1,0:T(8,128)(2,1)S(1)}, u32[]{:S(2)}, u32[]{:S(2)}) collective-permute-start(bf16[32,1792]{1,0:T(8,128)(2,1)S(1)} %get-tuple-element.52), channel_id=1, source_target_pairs={{0,4},{4,8},{8,12},{12,0},{1,5},{5,9},{9,13},{13,1},{2,6},{6,10},{... | collective-permute-start | bytes 344072 | tf_op jit(solution)/shard_map/ppermute | solution.py:113
  82.6 10.8 %collective-permute-start.22 = (bf16[32,1792]{1,0:T(8,128)(2,1)S(1)}, bf16[32,1792]{1,0:T(8,128)(2,1)S(1)}, u32[]{:S(2)}, u32[]{:S(2)}) collective-permute-start(bf16[32,1792]{1,0:T(8,128)(2,1)S(1)} %get-tuple-element.53), channel_id=1, source_target_pairs={{0,8},{4,12},{8,0},{12,4},{1,9},{5,13},{9,1},{13,5},{2,10},{6,14},... | collective-permute-start | bytes 344072 | tf_op jit(solution)/shard_map/ppermute | solution.py:113
  84.4 9.0 %collective-permute-start.23 = (bf16[32,1792]{1,0:T(8,128)(2,1)S(1)}, bf16[32,1792]{1,0:T(8,128)(2,1)S(1)}, u32[]{:S(2)}, u32[]{:S(2)}) collective-permute-start(bf16[32,1792]{1,0:T(8,128)(2,1)S(1)} %get-tuple-element.54), channel_id=1, source_target_pairs={{0,12},{4,0},{8,4},{12,8},{1,13},{5,1},{9,5},{13,9},{2,14},{6,2},{... | collective-permute-start | bytes 344072 | tf_op jit(solution)/shard_map/ppermute | solution.py:113
  93.5 11.1 %collective-permute-start.26 = (bf16[32,896]{1,0:T(8,128)(2,1)S(1)}, bf16[32,896]{1,0:T(8,128)(2,1)S(1)}, u32[]{:S(2)}, u32[]{:S(2)}) collective-permute-start(bf16[32,896]{1,0:T(8,128)(2,1)S(1)} %fusion.44), channel_id=1, source_target_pairs={{0,12},{4,0},{8,4},{12,8},{1,13},{5,1},{9,5},{13,9},{2,14},{6,2},{... | collective-permute-start | bytes 172040 | tf_op jit(solution)/shard_map/ppermute | solution.py:131
  96.3 5.6 %collective-permute-start.25 = (bf16[32,896]{1,0:T(8,128)(2,1)S(1)}, bf16[32,896]{1,0:T(8,128)(2,1)S(1)}, u32[]{:S(2)}, u32[]{:S(2)}) collective-permute-start(bf16[32,896]{1,0:T(8,128)(2,1)S(1)} %fusion.44), channel_id=1, source_target_pairs={{0,8},{4,12},{8,0},{12,4},{1,9},{5,13},{9,1},{13,5},{2,10},{6,14},... | collective-permute-start | bytes 172040 | tf_op jit(solution)/shard_map/ppermute | solution.py:131
  97.1 10.4 %collective-permute-start.24 = (bf16[32,896]{1,0:T(8,128)(2,1)S(1)}, bf16[32,896]{1,0:T(8,128)(2,1)S(1)}, u32[]{:S(2)}, u32[]{:S(2)}) collective-permute-start(bf16[32,896]{1,0:T(8,128)(2,1)S(1)} %fusion.44), channel_id=1, source_target_pairs={{0,4},{4,8},{8,12},{12,0},{1,5},{5,9},{9,13},{13,1},{2,6},{6,10},{... | collective-permute-start | bytes 172040 | tf_op jit(solution)/shard_map/ppermute | solution.py:131
  110.3 3.7 %collective-permute-start.27 = (f32[8,2048]{1,0:T(8,128)S(1)}, f32[8,2048]{1,0:T(8,128)S(1)}, u32[]{:S(2)}, u32[]{:S(2)}) collective-permute-start(f32[8,2048]{1,0:T(8,128)S(1)} %get-tuple-element.58), channel_id=1, source_target_pairs={{0,1},{1,2},{2,3},{3,0},{4,5},{5,6},{6,7},{7,4},{8,9},{9,10},{10,1... | collective-permute-start | bytes 196616 | tf_op jit(solution)/shard_map/ppermute | solution.py:113
  110.4 3.7 %collective-permute-start.29 = (f32[8,2048]{1,0:T(8,128)S(1)}, f32[8,2048]{1,0:T(8,128)S(1)}, u32[]{:S(2)}, u32[]{:S(2)}) collective-permute-start(f32[8,2048]{1,0:T(8,128)S(1)} %get-tuple-element.59), channel_id=1, source_target_pairs={{0,3},{1,0},{2,1},{3,2},{4,7},{5,4},{6,5},{7,6},{8,11},{9,8},{10,9... | collective-permute-start | bytes 196616 | tf_op jit(solution)/shard_map/ppermute | solution.py:113
  112.1 4.3 %collective-permute-start.28 = (f32[8,2048]{1,0:T(8,128)S(1)}, f32[8,2048]{1,0:T(8,128)S(1)}, u32[]{:S(2)}, u32[]{:S(2)}) collective-permute-start(f32[8,2048]{1,0:T(8,128)S(1)} %get-tuple-element.60), channel_id=1, source_target_pairs={{0,2},{1,3},{2,0},{3,1},{4,6},{5,7},{6,4},{7,5},{8,10},{9,11},{10,... | collective-permute-start | bytes 196616 | tf_op jit(solution)/shard_map/ppermute | solution.py:113
  (1 other events, 20.6 us)

commit v7 on v6

--- a/solution.py
+++ b/solution.py
@@ -131,6 +131,18 @@
         got = lax.ppermute(x, axis, shift_pairs(n, k))
         rows = lax.dynamic_slice_in_dim(w, ((idx - k) % n) * chunk, chunk, 0)
         acc = acc + jnp.dot(got, rows, preferred_element_type=jnp.float32)
+    return acc
+
+
+def staged_matmul(x, w, axis, n):
+    idx = lax.axis_index(axis)
+    size = w.shape[0] // n
+    turned = jnp.roll(x, -idx * size, axis=1)
+    acc = None
+    for k in range(n):
+        rows = lax.dynamic_slice_in_dim(w, ((idx + k) % n) * size, size, 0)
+        part = jnp.dot(turned[:, k * size : (k + 1) * size], rows, preferred_element_type=jnp.float32)
+        acc = part if acc is None else acc + part
     return acc
 
 
@@ -175,7 +187,7 @@
     rotated = rope_rows(summed, positions, per_group, HD)
     attended = attend(rotated, kv_cache, positions, per_group, HD)
     by_row = gather_rows(attended, "pool", n_pool, slot_of_row)
-    out_part = jnp.dot(by_row, w_out, preferred_element_type=jnp.float32)
+    out_part = staged_matmul(by_row, w_out, "pool", n_pool)
     residual = residual + scatter_sum(out_part.reshape(n_cs, rows_here, -1), CS, n_cs)
 
     squares_mid = all_sum(jnp.sum(residual * residual, axis=1), "pool", n_pool)
@@ -184,8 +196,8 @@
     ).astype(jnp.bfloat16)
     ffn_all = gather_rows(ffn_normed, CS, n_cs, every)
     chunk = w_gate.shape[1] // n_pool
-    gate_part = jnp.dot(ffn_all, w_gate, preferred_element_type=jnp.float32).astype(jnp.bfloat16)
-    up_part = jnp.dot(ffn_all, w_up, preferred_element_type=jnp.float32).astype(jnp.bfloat16)
+    gate_part = staged_matmul(ffn_all, w_gate, "pool", n_pool).astype(jnp.bfloat16)
+    up_part = staged_matmul(ffn_all, w_up, "pool", n_pool).astype(jnp.bfloat16)
     gate_blocks = gate_part.reshape(rows_total, n_pool, chunk).transpose(1, 0, 2)
     up_blocks = up_part.reshape(rows_total, n_pool, chunk).transpose(1, 0, 2)
     both = scatter_sum(jnp.concatenate([gate_blocks, up_blocks], axis=2), "pool", n_pool)

time: 118 us -> 124 us (1.051)
  matrix products: 38.7 us -> 45 us
    dot_general x3 -> x12, matrix products: 20.7 us -> 27 us  [staged_matmul(): jnp.dot(turned[:, k * size:(k + 1) * size], rows, preferred_element_type=...]
where the time goes in v7:
time: 124 us
  matrix products  45 us (36%)
  waiting for transfers between devices  38.4 us (31%)
  starting transfers between devices  31.3 us (25%)
  other arithmetic  6.03 us (5%)
  local copies, waits for them, and re-layouts  2.63 us (2%)
    dot_general x12, matrix products, staged_matmul(): jnp.dot(turned[:, k * size:(k + 1) * size], rows, preferred_element_type=...  27 us
    ppermute x12, waiting for transfers between devices, scatter_sum(): lax.ppermute(piece, axis, shift_pairs(n, k)).astype(jnp.float32)  19.5 us
    ppermute x12, starting transfers between devices, scatter_sum(): lax.ppermute(piece, axis, shift_pairs(n, k)).astype(jnp.float32)  13 us
    ppermute x9, waiting for transfers between devices, gather_rows(): got = [x] + [lax.ppermute(x, axis, shift_pairs(n, k)) for k in range(1, n)]  11.3 us
    ppermute x6, starting transfers between devices, all_sum(): total = total + lax.ppermute(x, axis, shift_pairs(n, k))  9.3 us
    dot_general x3, matrix products, gather_matmul(): acc = acc + jnp.dot(got, rows, preferred_element_type=jnp.float32)  8.39 us
    dot_general x1, matrix products, local(): jnp.einsum('rf,fgc->rgc', by_slot, w_qkv, preferred_element_type=jnp.floa...  5.94 us
    ppermute x6, waiting for transfers between devices, all_sum(): total = total + lax.ppermute(x, axis, shift_pairs(n, k))  5.61 us
  transfers between devices with their start and end apart: 30, of which 22 were waited for; matrix products, arithmetic and copies ran while one was open for 9% of the time, Pallas kernels for 0%

profile of v7, /device:TPU:0, one launch (start us, length us, event | category | flops | bytes accessed | tf_op | source)
XLA Modules:
  0.0 123.9 jit_solution(10862564008792924129)
XLA Ops:
  1.0 5.1 %collective-permute-start.2 = (f32[8]{0:T(128)S(1)}, f32[8]{0:T(128)S(1)}, u32[]{:S(2)}, u32[]{:S(2)}) collective-permute-start(f32[8]{0:T(128)S(1)} %fusion.66), channel_id=1, source_target_pairs={{0,12},{4,0},{8,4},{12,8},{1,13},{5,1},{9,5},{13,9},{2,14},{6,2},{... | collective-permute-start | bytes 104 | tf_op jit(solution)/shard_map/ppermute | solution.py:120
  14.1 2.3 %collective-permute-done.4 = bf16[8,2048]{1,0:T(8,128)(2,1)S(1)} collective-permute-done((bf16[8,2048]{1,0:T(8,128)(2,1)S(1)}, bf16[8,2048]{1,0:T(8,128)(2,1)S(1)}, u32[]{:S(2)}, u32[]{:S(2)}) %collective-permute-start.4) | collective-permute-done | bytes 32800 | tf_op jit(solution)/shard_map/ppermute | solution.py:97
  18.0 5.9 %fusion.22 = f32[2,4,8,1280]{3,2,1,0:T(8,128)S(1)} fusion(bf16[2048,2,1280]{2,1,0:T(2,128)(2,1)} %param.24, bf16[32,2048]{1,0:T(8,128)(2,1)S(1)} %gather_fusion, pred[32]{0:T(512)(128)(4,1)S(1)} %get-tuple-element.51), kind=kOutput, calls=%fused_computation.31 | convolution fusion | flops 335609856 | bytes 10944544 | tf_op jit(solution)/shard_map/rf,fgc->rgc/dot_general | solution.py:182
  24.3 3.5 %collective-permute-start.8 = (f32[8,2560]{1,0:T(8,128)S(1)}, f32[8,2560]{1,0:T(8,128)S(1)}, u32[]{:S(2)}, u32[]{:S(2)}) collective-permute-start(f32[8,2560]{1,0:T(8,128)S(1)} %get-tuple-element.57), channel_id=1, source_target_pairs={{0,12},{4,0},{8,4},{12,8},{1,13},{5,1},{9,5},{13,9},{2,14},{6,2},{... | collective-permute-start | bytes 245768 | tf_op jit(solution)/shard_map/ppermute | solution.py:113
  28.4 2.7 %collective-permute-done.6 = f32[8,2560]{1,0:T(8,128)S(1)} collective-permute-done((f32[8,2560]{1,0:T(8,128)S(1)}, f32[8,2560]{1,0:T(8,128)S(1)}, u32[]{:S(2)}, u32[]{:S(2)}) %collective-permute-start.6) | collective-permute-done | bytes 81952 | tf_op jit(solution)/shard_map/ppermute | solution.py:113
  31.1 2.9 %collective-permute-done.7 = f32[8,2560]{1,0:T(8,128)S(1)} collective-permute-done((f32[8,2560]{1,0:T(8,128)S(1)}, f32[8,2560]{1,0:T(8,128)S(1)}, u32[]{:S(2)}, u32[]{:S(2)}) %collective-permute-start.7) | collective-permute-done | bytes 81952 | tf_op jit(solution)/shard_map/ppermute | solution.py:113
  35.4 1.8 %collective-permute-start.11 = (bf16[8,2048]{1,0:T(8,128)(2,1)S(1)}, bf16[8,2048]{1,0:T(8,128)(2,1)S(1)}, u32[]{:S(2)}, u32[]{:S(2)}) collective-permute-start(bf16[8,2048]{1,0:T(8,128)(2,1)S(1)} %bitcast.114), channel_id=1, source_target_pairs={{0,12},{4,0},{8,4},{12,8},{1,13},{5,1},{9,5},{13,9},{2,14},{6,2},{... | collective-permute-start | bytes 98312 | tf_op jit(solution)/shard_map/ppermute | solution.py:97
  39.4 2.7 %collective-permute-done.10 = bf16[8,2048]{1,0:T(8,128)(2,1)S(1)} collective-permute-done((bf16[8,2048]{1,0:T(8,128)(2,1)S(1)}, bf16[8,2048]{1,0:T(8,128)(2,1)S(1)}, u32[]{:S(2)}, u32[]{:S(2)}) %collective-permute-start.10) | collective-permute-done | bytes 32800 | tf_op jit(solution)/shard_map/ppermute | solution.py:97
  43.9 2.1 %fusion.41 = f32[32,2048]{1,0:T(8,128)S(1)} fusion(bf16[2048,2048]{1,0:T(8,128)(2,1)} %param.25, s32[]{:T(128)S(6)} %select_n.212, bf16[32,2048]{1,0:T(8,128)(2,1)S(1)} %fusion.46), kind=kOutput, calls=%fused_computation.43 | convolution fusion | flops 67108864 | bytes 2392068 | tf_op jit(solution)/shard_map/dot_general | solution.py:144
  45.9 2.1 %convolution_add_fusion.8 = f32[32,2048]{1,0:T(8,128)S(1)} fusion(f32[32,2048]{1,0:T(8,128)S(1)} %fusion.41, bf16[2048,2048]{1,0:T(8,128)(2,1)} %param.25, s32[]{:T(128)S(6)} %select_n.213, bf16[32,2048]{1,0:T(8,128)(2,1)S(1)} %fusion.46), kind=kOutput, calls=%fused_computation.39 | convolution fusion | flops 67174400 | bytes 2654212 | tf_op jit(solution)/shard_map/dot_general | solution.py:144
  48.0 2.1 %convolution_add_fusion.7 = f32[32,2048]{1,0:T(8,128)S(1)} fusion(f32[32,2048]{1,0:T(8,128)S(1)} %convolution_add_fusion.8, bf16[2048,2048]{1,0:T(8,128)(2,1)} %param.25, s32[]{:T(128)S(6)} %select_n.214, bf16[32,2048]{1,0:T(8,128)(2,1)S(1)} %fusion.46), kind=kOutput, calls=%fused_computation.38 | convolution fusion | flops 67174400 | bytes 2654212 | tf_op jit(solution)/shard_map/dot_general | solution.py:144
  50.1 2.2 %fusion.37 = f32[4,8,2048]{2,1,0:T(8,128)S(1)} fusion(f32[32,2048]{1,0:T(8,128)S(1)} %convolution_add_fusion.7, bf16[2048,2048]{1,0:T(8,128)(2,1)} %param.25, s32[]{:T(128)S(6)} %select_n.215, bf16[32,2048]{1,0:T(8,128)(2,1)S(1)} %fusion.46), kind=kOutput, calls=%fused_computation.37 | convolution fusion | flops 67174400 | bytes 2654212 | tf_op jit(solution)/shard_map/dot_general | solution.py:144
  56.1 2.3 %collective-permute-done.13 = f32[8,2048]{1,0:T(8,128)S(1)} collective-permute-done((f32[8,2048]{1,0:T(8,128)S(1)}, f32[8,2048]{1,0:T(8,128)S(1)}, u32[]{:S(2)}, u32[]{:S(2)}) %collective-permute-start.13) | collective-permute-done | bytes 65568 | tf_op jit(solution)/shard_map/ppermute | solution.py:113
  59.8 1.9 %collective-permute-start.15 = (f32[8]{0:T(128)S(1)}, f32[8]{0:T(128)S(1)}, u32[]{:S(2)}, u32[]{:S(2)}) collective-permute-start(f32[8]{0:T(128)S(1)} %get-tuple-element.47), channel_id=1, source_target_pairs={{0,4},{4,8},{8,12},{12,0},{1,5},{5,9},{9,13},{13,1},{2,6},{6,10},{... | collective-permute-start | bytes 104 | tf_op jit(solution)/shard_map/ppermute | solution.py:120
  66.8 2.4 %collective-permute-done.19 = bf16[8,2048]{1,0:T(8,128)(2,1)S(1)} collective-permute-done((bf16[8,2048]{1,0:T(8,128)(2,1)S(1)}, bf16[8,2048]{1,0:T(8,128)(2,1)S(1)}, u32[]{:S(2)}, u32[]{:S(2)}) %collective-permute-start.19) | collective-permute-done | bytes 32800 | tf_op jit(solution)/shard_map/ppermute | solution.py:97
  70.5 2.9 %fusion.15 = f32[32,3584]{1,0:T(8,128)S(1)} fusion(bf16[2048,3584]{1,0:T(8,128)(2,1)} %param.28, s32[]{:T(128)S(6)} %select_n.212, bf16[32,2048]{1,0:T(8,128)(2,1)S(1)} %fusion.45), kind=kOutput, calls=%fused_computation.24 | convolution fusion | flops 117440512 | bytes 4161540 | tf_op jit(solution)/shard_map/dot_general | solution.py:144
  73.4 2.8 %convolution_add_fusion.2 = f32[32,3584]{1,0:T(8,128)S(1)} fusion(f32[32,3584]{1,0:T(8,128)S(1)} %fusion.15, bf16[2048,3584]{1,0:T(8,128)(2,1)} %param.28, s32[]{:T(128)S(6)} %select_n.213, bf16[32,2048]{1,0:T(8,128)(2,1)S(1)} %fusion.45), kind=kOutput, calls=%fused_computation.7 | convolution fusion | flops 117555200 | bytes 4620292 | tf_op jit(solution)/shard_map/dot_general | solution.py:144
  76.2 2.9 %convolution_add_fusion.1 = f32[32,3584]{1,0:T(8,128)S(1)} fusion(f32[32,3584]{1,0:T(8,128)S(1)} %convolution_add_fusion.2, bf16[2048,3584]{1,0:T(8,128)(2,1)} %param.28, s32[]{:T(128)S(6)} %select_n.214, bf16[32,2048]{1,0:T(8,128)(2,1)S(1)} %fusion.45), kind=kOutput, calls=%fused_computation.6 | convolution fusion | flops 117555200 | bytes 4620292 | tf_op jit(solution)/shard_map/dot_general | solution.py:144
  79.1 2.8 %fusion.3 = bf16[32,3584]{1,0:T(8,128)(2,1)S(1)} fusion(f32[32,3584]{1,0:T(8,128)S(1)} %convolution_add_fusion.1, bf16[2048,3584]{1,0:T(8,128)(2,1)} %param.28, s32[]{:T(128)S(6)} %select_n.215, bf16[32,2048]{1,0:T(8,128)(2,1)S(1)} %fusion.45), kind=kOutput, calls=%fused_computation.12 | convolution fusion | flops 117669888 | bytes 4390916 | tf_op jit(solution)/shard_map/dot_general | solution.py:144
  81.9 2.9 %fusion.20 = f32[32,3584]{1,0:T(8,128)S(1)} fusion(bf16[2048,3584]{1,0:T(8,128)(2,1)} %param.27, s32[]{:T(128)S(6)} %select_n.212, bf16[32,2048]{1,0:T(8,128)(2,1)S(1)} %fusion.45), kind=kOutput, calls=%fused_computation.29 | convolution fusion | flops 117440512 | bytes 4161540 | tf_op jit(solution)/shard_map/dot_general | solution.py:144
  84.8 2.8 %convolution_add_fusion.5 = f32[32,3584]{1,0:T(8,128)S(1)} fusion(f32[32,3584]{1,0:T(8,128)S(1)} %fusion.20, bf16[2048,3584]{1,0:T(8,128)(2,1)} %param.27, s32[]{:T(128)S(6)} %select_n.213, bf16[32,2048]{1,0:T(8,128)(2,1)S(1)} %fusion.45), kind=kOutput, calls=%fused_computation.10 | convolution fusion | flops 117555200 | bytes 4620292 | tf_op jit(solution)/shard_map/dot_general | solution.py:144
  89.5 1.8 %collective-permute-start.22 = (bf16[32,1792]{1,0:T(8,128)(2,1)S(1)}, bf16[32,1792]{1,0:T(8,128)(2,1)S(1)}, u32[]{:S(2)}, u32[]{:S(2)}) collective-permute-start(bf16[32,1792]{1,0:T(8,128)(2,1)S(1)} %get-tuple-element.54), channel_id=1, source_target_pairs={{0,8},{4,12},{8,0},{12,4},{1,9},{5,13},{9,1},{13,5},{2,10},{6,14},... | collective-permute-start | bytes 344072 | tf_op jit(solution)/shard_map/ppermute | solution.py:113
  91.3 1.9 %collective-permute-start.23 = (bf16[32,1792]{1,0:T(8,128)(2,1)S(1)}, bf16[32,1792]{1,0:T(8,128)(2,1)S(1)}, u32[]{:S(2)}, u32[]{:S(2)}) collective-permute-start(bf16[32,1792]{1,0:T(8,128)(2,1)S(1)} %get-tuple-element.55), channel_id=1, source_target_pairs={{0,12},{4,0},{8,4},{12,8},{1,13},{5,1},{9,5},{13,9},{2,14},{6,2},{... | collective-permute-start | bytes 344072 | tf_op jit(solution)/shard_map/ppermute | solution.py:113
  93.2 4.1 %collective-permute-done.21 = bf16[32,1792]{1,0:T(8,128)(2,1)S(1)} collective-permute-done((bf16[32,1792]{1,0:T(8,128)(2,1)S(1)}, bf16[32,1792]{1,0:T(8,128)(2,1)S(1)}, u32[]{:S(2)}, u32[]{:S(2)}) %collective-permute-start.21) | collective-permute-done | bytes 114720 | tf_op jit(solution)/shard_map/ppermute | solution.py:113
  97.2 3.0 %collective-permute-done.22 = bf16[32,1792]{1,0:T(8,128)(2,1)S(1)} collective-permute-done((bf16[32,1792]{1,0:T(8,128)(2,1)S(1)}, bf16[32,1792]{1,0:T(8,128)(2,1)S(1)}, u32[]{:S(2)}, u32[]{:S(2)}) %collective-permute-start.22) | collective-permute-done | bytes 114720 | tf_op jit(solution)/shard_map/ppermute | solution.py:113
  100.4 2.8 %collective-permute-start.26 = (bf16[32,896]{1,0:T(8,128)(2,1)S(1)}, bf16[32,896]{1,0:T(8,128)(2,1)S(1)}, u32[]{:S(2)}, u32[]{:S(2)}) collective-permute-start(bf16[32,896]{1,0:T(8,128)(2,1)S(1)} %fusion.62), channel_id=1, source_target_pairs={{0,12},{4,0},{8,4},{12,8},{1,13},{5,1},{9,5},{13,9},{2,14},{6,2},{... | collective-permute-start | bytes 172040 | tf_op jit(solution)/shard_map/ppermute | solution.py:131
  104.0 2.8 %fusion.10 = f32[32,2048]{1,0:T(8,128)S(1)} fusion(bf16[32,896]{1,0:T(8,128)(2,1)S(1)} %fusion.62, bf16[3584,2048]{1,0:T(8,128)(2,1)} %param.29, s32[]{:T(128)S(6)} %select_n.222), kind=kOutput, calls=%fused_computation.19 | convolution fusion | flops 117440512 | bytes 3989508 | tf_op jit(solution)/shard_map/dot_general | solution.py:127
  106.7 2.0 %collective-permute-done.25 = bf16[32,896]{1,0:T(8,128)(2,1)S(1)} collective-permute-done((bf16[32,896]{1,0:T(8,128)(2,1)S(1)}, bf16[32,896]{1,0:T(8,128)(2,1)S(1)}, u32[]{:S(2)}, u32[]{:S(2)}) %collective-permute-start.25) | collective-permute-done | bytes 57376 | tf_op jit(solution)/shard_map/ppermute | solution.py:131
  108.7 2.8 %fusion.6 = f32[32,2048]{1,0:T(8,128)S(1)} fusion(bf16[32,896]{1,0:T(8,128)(2,1)S(1)} %collective-permute-done.25, bf16[3584,2048]{1,0:T(8,128)(2,1)} %param.29, s32[]{:T(128)S(6)} %select_n.226), kind=kOutput, calls=%fused_computation.15 | convolution fusion | flops 117440512 | bytes 3989508 | tf_op jit(solution)/shard_map/dot_general | solution.py:133
  111.5 2.8 %fusion.4 = f32[32,2048]{1,0:T(8,128)S(1)} fusion(bf16[32,896]{1,0:T(8,128)(2,1)S(1)} %collective-permute-done.26, bf16[3584,2048]{1,0:T(8,128)(2,1)} %param.29, s32[]{:T(128)S(6)} %select_n.228), kind=kOutput, calls=%fused_computation.13 | convolution fusion | flops 117440512 | bytes 3989508 | tf_op jit(solution)/shard_map/dot_general | solution.py:133
  114.3 2.8 %fusion.34 = f32[4,8,2048]{2,1,0:T(8,128)S(1)} fusion(f32[32,2048]{1,0:T(8,128)S(1)} %fusion.4, f32[32,2048]{1,0:T(8,128)S(1)} %fusion.6, f32[32,2048]{1,0:T(8,128)S(1)} %fusion.10, bf16[32,896]{1,0:T(8,128)(2,1)S(1)} %collective-permute-done.24, bf16[3584,2048]{1,0:T(8,128)(2,1)} %param.29, s32[]{:T(128)S(6)} %select_n.224), kind=kOutput, calls=%fused_computation.35 | convolution fusion | flops 117637120 | bytes 4775940 | tf_op jit(solution)/shard_map/dot_general | solution.py:133
  120.9 2.3 %collective-permute-done.28 = f32[8,2048]{1,0:T(8,128)S(1)} collective-permute-done((f32[8,2048]{1,0:T(8,128)S(1)}, f32[8,2048]{1,0:T(8,128)S(1)}, u32[]{:S(2)}, u32[]{:S(2)}) %collective-permute-start.28) | collective-permute-done | bytes 65568 | tf_op jit(solution)/shard_map/ppermute | solution.py:113
  (116 shorter events, 35.1 us)
Async XLA Ops:
  1.0 8.2 %collective-permute-start.2 = (f32[8]{0:T(128)S(1)}, f32[8]{0:T(128)S(1)}, u32[]{:S(2)}, u32[]{:S(2)}) collective-permute-start(f32[8]{0:T(128)S(1)} %fusion.66), channel_id=1, source_target_pairs={{0,12},{4,0},{8,4},{12,8},{1,13},{5,1},{9,5},{13,9},{2,14},{6,2},{... | collective-permute-start | bytes 104 | tf_op jit(solution)/shard_map/ppermute | solution.py:120
  6.1 4.4 %collective-permute-start.1 = (f32[8]{0:T(128)S(1)}, f32[8]{0:T(128)S(1)}, u32[]{:S(2)}, u32[]{:S(2)}) collective-permute-start(f32[8]{0:T(128)S(1)} %fusion.66), channel_id=1, source_target_pairs={{0,8},{4,12},{8,0},{12,4},{1,9},{5,13},{9,1},{13,5},{2,10},{6,14},... | collective-permute-start | bytes 104 | tf_op jit(solution)/shard_map/ppermute | solution.py:120
  6.1 5.3 %collective-permute-start = (f32[8]{0:T(128)S(1)}, f32[8]{0:T(128)S(1)}, u32[]{:S(2)}, u32[]{:S(2)}) collective-permute-start(f32[8]{0:T(128)S(1)} %fusion.66), channel_id=1, source_target_pairs={{0,4},{4,8},{8,12},{12,0},{1,5},{5,9},{9,13},{13,1},{2,6},{6,10},{... | collective-permute-start | bytes 104 | tf_op jit(solution)/shard_map/ppermute | solution.py:120
  12.3 1.8 %collective-permute-start.5 = (bf16[8,2048]{1,0:T(8,128)(2,1)S(1)}, bf16[8,2048]{1,0:T(8,128)(2,1)S(1)}, u32[]{:S(2)}, u32[]{:S(2)}) collective-permute-start(bf16[8,2048]{1,0:T(8,128)(2,1)S(1)} %fusion.68), channel_id=1, source_target_pairs={{0,3},{1,0},{2,1},{3,2},{4,7},{5,4},{6,5},{7,6},{8,11},{9,8},{10,9... | collective-permute-start | bytes 98312 | tf_op jit(solution)/shard_map/ppermute | solution.py:97
  12.4 4.1 %collective-permute-start.4 = (bf16[8,2048]{1,0:T(8,128)(2,1)S(1)}, bf16[8,2048]{1,0:T(8,128)(2,1)S(1)}, u32[]{:S(2)}, u32[]{:S(2)}) collective-permute-start(bf16[8,2048]{1,0:T(8,128)(2,1)S(1)} %fusion.68), channel_id=1, source_target_pairs={{0,2},{1,3},{2,0},{3,1},{4,6},{5,7},{6,4},{7,5},{8,10},{9,11},{10,... | collective-permute-start | bytes 98312 | tf_op jit(solution)/shard_map/ppermute | solution.py:97
  13.9 3.3 %collective-permute-start.3 = (bf16[8,2048]{1,0:T(8,128)(2,1)S(1)}, bf16[8,2048]{1,0:T(8,128)(2,1)S(1)}, u32[]{:S(2)}, u32[]{:S(2)}) collective-permute-start(bf16[8,2048]{1,0:T(8,128)(2,1)S(1)} %fusion.68), channel_id=1, source_target_pairs={{0,1},{1,2},{2,3},{3,0},{4,5},{5,6},{6,7},{7,4},{8,9},{9,10},{10,1... | collective-permute-start | bytes 98312 | tf_op jit(solution)/shard_map/ppermute | solution.py:97
  24.0 7.1 %collective-permute-start.6 = (f32[8,2560]{1,0:T(8,128)S(1)}, f32[8,2560]{1,0:T(8,128)S(1)}, u32[]{:S(2)}, u32[]{:S(2)}) collective-permute-start(f32[8,2560]{1,0:T(8,128)S(1)} %get-tuple-element.56), channel_id=1, source_target_pairs={{0,4},{4,8},{8,12},{12,0},{1,5},{5,9},{9,13},{13,1},{2,6},{6,10},{... | collective-permute-start | bytes 245768 | tf_op jit(solution)/shard_map/ppermute | solution.py:113
  24.3 6.7 %collective-permute-start.8 = (f32[8,2560]{1,0:T(8,128)S(1)}, f32[8,2560]{1,0:T(8,128)S(1)}, u32[]{:S(2)}, u32[]{:S(2)}) collective-permute-start(f32[8,2560]{1,0:T(8,128)S(1)} %get-tuple-element.57), channel_id=1, source_target_pairs={{0,12},{4,0},{8,4},{12,8},{1,13},{5,1},{9,5},{13,9},{2,14},{6,2},{... | collective-permute-start | bytes 245768 | tf_op jit(solution)/shard_map/ppermute | solution.py:113
  27.8 6.1 %collective-permute-start.7 = (f32[8,2560]{1,0:T(8,128)S(1)}, f32[8,2560]{1,0:T(8,128)S(1)}, u32[]{:S(2)}, u32[]{:S(2)}) collective-permute-start(f32[8,2560]{1,0:T(8,128)S(1)} %get-tuple-element.58), channel_id=1, source_target_pairs={{0,8},{4,12},{8,0},{12,4},{1,9},{5,13},{9,1},{13,5},{2,10},{6,14},... | collective-permute-start | bytes 245768 | tf_op jit(solution)/shard_map/ppermute | solution.py:113
  34.4 30.7 %copy-start.2 = (f32[2048]{0:T(1024)S(1)}, f32[2048]{0:T(1024)}, u32[]{:S(2)}) copy-start(f32[2048]{0:T(1024)} %param.26) | copy-start | bytes 24580
  35.4 4.0 %collective-permute-start.11 = (bf16[8,2048]{1,0:T(8,128)(2,1)S(1)}, bf16[8,2048]{1,0:T(8,128)(2,1)S(1)}, u32[]{:S(2)}, u32[]{:S(2)}) collective-permute-start(bf16[8,2048]{1,0:T(8,128)(2,1)S(1)} %bitcast.114), channel_id=1, source_target_pairs={{0,12},{4,0},{8,4},{12,8},{1,13},{5,1},{9,5},{13,9},{2,14},{6,2},{... | collective-permute-start | bytes 98312 | tf_op jit(solution)/shard_map/ppermute | solution.py:97
  37.3 4.9 %collective-permute-start.10 = (bf16[8,2048]{1,0:T(8,128)(2,1)S(1)}, bf16[8,2048]{1,0:T(8,128)(2,1)S(1)}, u32[]{:S(2)}, u32[]{:S(2)}) collective-permute-start(bf16[8,2048]{1,0:T(8,128)(2,1)S(1)} %bitcast.115), channel_id=1, source_target_pairs={{0,8},{4,12},{8,0},{12,4},{1,9},{5,13},{9,1},{13,5},{2,10},{6,14},... | collective-permute-start | bytes 98312 | tf_op jit(solution)/shard_map/ppermute | solution.py:97
  37.3 5.7 %collective-permute-start.9 = (bf16[8,2048]{1,0:T(8,128)(2,1)S(1)}, bf16[8,2048]{1,0:T(8,128)(2,1)S(1)}, u32[]{:S(2)}, u32[]{:S(2)}) collective-permute-start(bf16[8,2048]{1,0:T(8,128)(2,1)S(1)} %bitcast.116), channel_id=1, source_target_pairs={{0,4},{4,8},{8,12},{12,0},{1,5},{5,9},{9,13},{13,1},{2,6},{6,10},{... | collective-permute-start | bytes 98312 | tf_op jit(solution)/shard_map/ppermute | solution.py:97
  50.1 37.6 %slice-start = ((s8[14680064]{0:T(1024)(128)(4,1)}), s8[2097152]{0:T(1024)(128)(4,1)S(1)}, s32[]{:S(2)}) async-start(s8[14680064]{0:T(1024)(128)(4,1)} %bitcast.103), calls=%async_computation | async-start | bytes 4194304
  52.3 3.7 %collective-permute-start.12 = (f32[8,2048]{1,0:T(8,128)S(1)}, f32[8,2048]{1,0:T(8,128)S(1)}, u32[]{:S(2)}, u32[]{:S(2)}) collective-permute-start(f32[8,2048]{1,0:T(8,128)S(1)} %get-tuple-element.62), channel_id=1, source_target_pairs={{0,1},{1,2},{2,3},{3,0},{4,5},{5,6},{6,7},{7,4},{8,9},{9,10},{10,1... | collective-permute-start | bytes 196616 | tf_op jit(solution)/shard_map/ppermute | solution.py:113
  52.4 3.7 %collective-permute-start.14 = (f32[8,2048]{1,0:T(8,128)S(1)}, f32[8,2048]{1,0:T(8,128)S(1)}, u32[]{:S(2)}, u32[]{:S(2)}) collective-permute-start(f32[8,2048]{1,0:T(8,128)S(1)} %get-tuple-element.63), channel_id=1, source_target_pairs={{0,3},{1,0},{2,1},{3,2},{4,7},{5,4},{6,5},{7,6},{8,11},{9,8},{10,9... | collective-permute-start | bytes 196616 | tf_op jit(solution)/shard_map/ppermute | solution.py:113
  54.1 4.3 %collective-permute-start.13 = (f32[8,2048]{1,0:T(8,128)S(1)}, f32[8,2048]{1,0:T(8,128)S(1)}, u32[]{:S(2)}, u32[]{:S(2)}) collective-permute-start(f32[8,2048]{1,0:T(8,128)S(1)} %get-tuple-element.64), channel_id=1, source_target_pairs={{0,2},{1,3},{2,0},{3,1},{4,6},{5,7},{6,4},{7,5},{8,10},{9,11},{10,... | collective-permute-start | bytes 196616 | tf_op jit(solution)/shard_map/ppermute | solution.py:113
  58.5 3.6 %collective-permute-start.17 = (f32[8]{0:T(128)S(1)}, f32[8]{0:T(128)S(1)}, u32[]{:S(2)}, u32[]{:S(2)}) collective-permute-start(f32[8]{0:T(128)S(1)} %get-tuple-element.47), channel_id=1, source_target_pairs={{0,12},{4,0},{8,4},{12,8},{1,13},{5,1},{9,5},{13,9},{2,14},{6,2},{... | collective-permute-start | bytes 104 | tf_op jit(solution)/shard_map/ppermute | solution.py:120
  59.4 4.4 %collective-permute-start.16 = (f32[8]{0:T(128)S(1)}, f32[8]{0:T(128)S(1)}, u32[]{:S(2)}, u32[]{:S(2)}) collective-permute-start(f32[8]{0:T(128)S(1)} %get-tuple-element.47), channel_id=1, source_target_pairs={{0,8},{4,12},{8,0},{12,4},{1,9},{5,13},{9,1},{13,5},{2,10},{6,14},... | collective-permute-start | bytes 104 | tf_op jit(solution)/shard_map/ppermute | solution.py:120
  59.8 5.3 %collective-permute-start.15 = (f32[8]{0:T(128)S(1)}, f32[8]{0:T(128)S(1)}, u32[]{:S(2)}, u32[]{:S(2)}) collective-permute-start(f32[8]{0:T(128)S(1)} %get-tuple-element.47), channel_id=1, source_target_pairs={{0,4},{4,8},{8,12},{12,0},{1,5},{5,9},{9,13},{13,1},{2,6},{6,10},{... | collective-permute-start | bytes 104 | tf_op jit(solution)/shard_map/ppermute | solution.py:120
  65.2 1.6 %collective-permute-start.20 = (bf16[8,2048]{1,0:T(8,128)(2,1)S(1)}, bf16[8,2048]{1,0:T(8,128)(2,1)S(1)}, u32[]{:S(2)}, u32[]{:S(2)}) collective-permute-start(bf16[8,2048]{1,0:T(8,128)(2,1)S(1)} %multiply_convert_fusion), channel_id=1, source_target_pairs={{0,3},{1,0},{2,1},{3,2},{4,7},{5,4},{6,5},{7,6},{8,11},{9,8},{10,9... | collective-permute-start | bytes 98312 | tf_op jit(solution)/shard_map/ppermute | solution.py:97
  65.3 4.0 %collective-permute-start.19 = (bf16[8,2048]{1,0:T(8,128)(2,1)S(1)}, bf16[8,2048]{1,0:T(8,128)(2,1)S(1)}, u32[]{:S(2)}, u32[]{:S(2)}) collective-permute-start(bf16[8,2048]{1,0:T(8,128)(2,1)S(1)} %multiply_convert_fusion), channel_id=1, source_target_pairs={{0,2},{1,3},{2,0},{3,1},{4,6},{5,7},{6,4},{7,5},{8,10},{9,11},{10,... | collective-permute-start | bytes 98312 | tf_op jit(solution)/shard_map/ppermute | solution.py:97
  66.2 3.4 %collective-permute-start.18 = (bf16[8,2048]{1,0:T(8,128)(2,1)S(1)}, bf16[8,2048]{1,0:T(8,128)(2,1)S(1)}, u32[]{:S(2)}, u32[]{:S(2)}) collective-permute-start(bf16[8,2048]{1,0:T(8,128)(2,1)S(1)} %multiply_convert_fusion), channel_id=1, source_target_pairs={{0,1},{1,2},{2,3},{3,0},{4,5},{5,6},{6,7},{7,4},{8,9},{9,10},{10,1... | collective-permute-start | bytes 98312 | tf_op jit(solution)/shard_map/ppermute | solution.py:97
  89.3 7.9 %collective-permute-start.21 = (bf16[32,1792]{1,0:T(8,128)(2,1)S(1)}, bf16[32,1792]{1,0:T(8,128)(2,1)S(1)}, u32[]{:S(2)}, u32[]{:S(2)}) collective-permute-start(bf16[32,1792]{1,0:T(8,128)(2,1)S(1)} %get-tuple-element.53), channel_id=1, source_target_pairs={{0,4},{4,8},{8,12},{12,0},{1,5},{5,9},{9,13},{13,1},{2,6},{6,10},{... | collective-permute-start | bytes 344072 | tf_op jit(solution)/shard_map/ppermute | solution.py:113
  89.5 10.8 %collective-permute-start.22 = (bf16[32,1792]{1,0:T(8,128)(2,1)S(1)}, bf16[32,1792]{1,0:T(8,128)(2,1)S(1)}, u32[]{:S(2)}, u32[]{:S(2)}) collective-permute-start(bf16[32,1792]{1,0:T(8,128)(2,1)S(1)} %get-tuple-element.54), channel_id=1, source_target_pairs={{0,8},{4,12},{8,0},{12,4},{1,9},{5,13},{9,1},{13,5},{2,10},{6,14},... | collective-permute-start | bytes 344072 | tf_op jit(solution)/shard_map/ppermute | solution.py:113
  91.3 9.0 %collective-permute-start.23 = (bf16[32,1792]{1,0:T(8,128)(2,1)S(1)}, bf16[32,1792]{1,0:T(8,128)(2,1)S(1)}, u32[]{:S(2)}, u32[]{:S(2)}) collective-permute-start(bf16[32,1792]{1,0:T(8,128)(2,1)S(1)} %get-tuple-element.55), channel_id=1, source_target_pairs={{0,12},{4,0},{8,4},{12,8},{1,13},{5,1},{9,5},{13,9},{2,14},{6,2},{... | collective-permute-start | bytes 344072 | tf_op jit(solution)/shard_map/ppermute | solution.py:113
  100.4 11.1 %collective-permute-start.26 = (bf16[32,896]{1,0:T(8,128)(2,1)S(1)}, bf16[32,896]{1,0:T(8,128)(2,1)S(1)}, u32[]{:S(2)}, u32[]{:S(2)}) collective-permute-start(bf16[32,896]{1,0:T(8,128)(2,1)S(1)} %fusion.62), channel_id=1, source_target_pairs={{0,12},{4,0},{8,4},{12,8},{1,13},{5,1},{9,5},{13,9},{2,14},{6,2},{... | collective-permute-start | bytes 172040 | tf_op jit(solution)/shard_map/ppermute | solution.py:131
  103.1 5.6 %collective-permute-start.25 = (bf16[32,896]{1,0:T(8,128)(2,1)S(1)}, bf16[32,896]{1,0:T(8,128)(2,1)S(1)}, u32[]{:S(2)}, u32[]{:S(2)}) collective-permute-start(bf16[32,896]{1,0:T(8,128)(2,1)S(1)} %fusion.62), channel_id=1, source_target_pairs={{0,8},{4,12},{8,0},{12,4},{1,9},{5,13},{9,1},{13,5},{2,10},{6,14},... | collective-permute-start | bytes 172040 | tf_op jit(solution)/shard_map/ppermute | solution.py:131
  103.9 10.4 %collective-permute-start.24 = (bf16[32,896]{1,0:T(8,128)(2,1)S(1)}, bf16[32,896]{1,0:T(8,128)(2,1)S(1)}, u32[]{:S(2)}, u32[]{:S(2)}) collective-permute-start(bf16[32,896]{1,0:T(8,128)(2,1)S(1)} %fusion.62), channel_id=1, source_target_pairs={{0,4},{4,8},{8,12},{12,0},{1,5},{5,9},{9,13},{13,1},{2,6},{6,10},{... | collective-permute-start | bytes 172040 | tf_op jit(solution)/shard_map/ppermute | solution.py:131
  117.2 3.7 %collective-permute-start.27 = (f32[8,2048]{1,0:T(8,128)S(1)}, f32[8,2048]{1,0:T(8,128)S(1)}, u32[]{:S(2)}, u32[]{:S(2)}) collective-permute-start(f32[8,2048]{1,0:T(8,128)S(1)} %get-tuple-element.59), channel_id=1, source_target_pairs={{0,1},{1,2},{2,3},{3,0},{4,5},{5,6},{6,7},{7,4},{8,9},{9,10},{10,1... | collective-permute-start | bytes 196616 | tf_op jit(solution)/shard_map/ppermute | solution.py:113
  117.2 3.7 %collective-permute-start.29 = (f32[8,2048]{1,0:T(8,128)S(1)}, f32[8,2048]{1,0:T(8,128)S(1)}, u32[]{:S(2)}, u32[]{:S(2)}) collective-permute-start(f32[8,2048]{1,0:T(8,128)S(1)} %get-tuple-element.60), channel_id=1, source_target_pairs={{0,3},{1,0},{2,1},{3,2},{4,7},{5,4},{6,5},{7,6},{8,11},{9,8},{10,9... | collective-permute-start | bytes 196616 | tf_op jit(solution)/shard_map/ppermute | solution.py:113
  119.0 4.3 %collective-permute-start.28 = (f32[8,2048]{1,0:T(8,128)S(1)}, f32[8,2048]{1,0:T(8,128)S(1)}, u32[]{:S(2)}, u32[]{:S(2)}) collective-permute-start(f32[8,2048]{1,0:T(8,128)S(1)} %get-tuple-element.61), channel_id=1, source_target_pairs={{0,2},{1,3},{2,0},{3,1},{4,6},{5,7},{6,4},{7,5},{8,10},{9,11},{10,... | collective-permute-start | bytes 196616 | tf_op jit(solution)/shard_map/ppermute | solution.py:113
  (5 other events, 86.5 us)

commit v8 on v6

--- a/solution.py
+++ b/solution.py
@@ -112,6 +112,14 @@
         piece = jnp.take(blocks, (idx + k) % n, axis=0)
         total = total + lax.ppermute(piece, axis, shift_pairs(n, k)).astype(jnp.float32)
     return total
+
+
+def scatter_sum_cs(blocks):
+    n_col = lax.axis_size("col")
+    n_side = lax.axis_size("side")
+    shaped = blocks.reshape((n_col, n_side) + blocks.shape[1:])
+    per_col = scatter_sum(jnp.swapaxes(shaped, 0, 1), "side", n_side)
+    return scatter_sum(per_col, "col", n_col)
 
 
 def all_sum(x, axis, n):
@@ -176,7 +184,7 @@
     attended = attend(rotated, kv_cache, positions, per_group, HD)
     by_row = gather_rows(attended, "pool", n_pool, slot_of_row)
     out_part = jnp.dot(by_row, w_out, preferred_element_type=jnp.float32)
-    residual = residual + scatter_sum(out_part.reshape(n_cs, rows_here, -1), CS, n_cs)
+    residual = residual + scatter_sum_cs(out_part.reshape(n_cs, rows_here, -1))
 
     squares_mid = all_sum(jnp.sum(residual * residual, axis=1), "pool", n_pool)
     ffn_normed = (
@@ -193,7 +201,7 @@
     up_total = both[:, chunk:]
     hidden = (jax.nn.silu(gate_total) * up_total).astype(jnp.bfloat16)
     down_part = gather_matmul(hidden, w_down, "pool", n_pool)
-    return residual + scatter_sum(down_part.reshape(n_cs, rows_here, -1), CS, n_cs)
+    return residual + scatter_sum_cs(down_part.reshape(n_cs, rows_here, -1))
 
 
 def solution(mesh):

time: 118 us -> 117 us (level)
  starting transfers between devices: 31.3 us -> 28 us
  waiting for transfers between devices: 38.5 us -> 41.2 us
    ppermute x12 -> x10, starting transfers between devices: 13 us -> 9.72 us  [scatter_sum(): lax.ppermute(piece, axis, shift_pairs(n, k)).astype(jnp.float32)]
    ppermute x12 -> x10, waiting for transfers between devices: 19.5 us -> 22.1 us  [scatter_sum(): lax.ppermute(piece, axis, shift_pairs(n, k)).astype(jnp.float32)]
  transfers between devices with their start and end apart: 30 -> 28, of which waited for: 22 -> 22; matrix products, arithmetic and copies ran while one was open for 9% -> 9% of each run, Pallas kernels for 0% -> 0%
where the time goes in v8:
time: 117 us
  waiting for transfers between devices  41.2 us (35%)
  matrix products  38.7 us (33%)
  starting transfers between devices  28 us (24%)
  other arithmetic  5.64 us (5%)
  local copies, waits for them, and re-layouts  2.62 us (2%)
    ppermute x10, waiting for transfers between devices, scatter_sum(): lax.ppermute(piece, axis, shift_pairs(n, k)).astype(jnp.float32)  22.1 us
    ppermute x9, waiting for transfers between devices, gather_rows(): got = [x] + [lax.ppermute(x, axis, shift_pairs(n, k)) for k in range(1, n)]  11.4 us
    ppermute x10, starting transfers between devices, scatter_sum(): lax.ppermute(piece, axis, shift_pairs(n, k)).astype(jnp.float32)  9.72 us
    ppermute x6, starting transfers between devices, all_sum(): total = total + lax.ppermute(x, axis, shift_pairs(n, k))  9.3 us
    dot_general x3, matrix products, gather_matmul(): acc = acc + jnp.dot(got, rows, preferred_element_type=jnp.float32)  8.39 us
    dot_general x1, matrix products, local(): jnp.dot(ffn_all, w_gate, preferred_element_type=jnp.float32)  7.86 us
    dot_general x1, matrix products, local(): jnp.dot(ffn_all, w_up, preferred_element_type=jnp.float32)  7.85 us
    dot_general x1, matrix products, local(): jnp.einsum('rf,fgc->rgc', by_slot, w_qkv, preferred_element_type=jnp.floa...  5.94 us
  transfers between devices with their start and end apart: 28, of which 22 were waited for; matrix products, arithmetic and copies ran while one was open for 9% of the time, Pallas kernels for 0%

profile of v8, /device:TPU:0, one launch (start us, length us, event | category | flops | bytes accessed | tf_op | source)
XLA Modules:
  0.0 116.5 jit_solution(1808722764360812147)
XLA Ops:
  1.0 5.1 %collective-permute-start.2 = (f32[8]{0:T(128)S(1)}, f32[8]{0:T(128)S(1)}, u32[]{:S(2)}, u32[]{:S(2)}) collective-permute-start(f32[8]{0:T(128)S(1)} %fusion.46), channel_id=1, source_target_pairs={{0,12},{4,0},{8,4},{12,8},{1,13},{5,1},{9,5},{13,9},{2,14},{6,2},{... | collective-permute-start | bytes 104 | tf_op jit(solution)/shard_map/ppermute | solution.py:128
  9.2 1.3 %collective-permute-done.1 = f32[8]{0:T(128)S(1)} collective-permute-done((f32[8]{0:T(128)S(1)}, f32[8]{0:T(128)S(1)}, u32[]{:S(2)}, u32[]{:S(2)}) %collective-permute-start.1) | collective-permute-done | bytes 64 | tf_op jit(solution)/shard_map/ppermute | solution.py:128
  12.4 1.6 %collective-permute-start.4 = (bf16[8,2048]{1,0:T(8,128)(2,1)S(1)}, bf16[8,2048]{1,0:T(8,128)(2,1)S(1)}, u32[]{:S(2)}, u32[]{:S(2)}) collective-permute-start(bf16[8,2048]{1,0:T(8,128)(2,1)S(1)} %fusion.48), channel_id=1, source_target_pairs={{0,2},{1,3},{2,0},{3,1},{4,6},{5,7},{6,4},{7,5},{8,10},{9,11},{10,... | collective-permute-start | bytes 98312 | tf_op jit(solution)/shard_map/ppermute | solution.py:97
  14.1 2.3 %collective-permute-done.4 = bf16[8,2048]{1,0:T(8,128)(2,1)S(1)} collective-permute-done((bf16[8,2048]{1,0:T(8,128)(2,1)S(1)}, bf16[8,2048]{1,0:T(8,128)(2,1)S(1)}, u32[]{:S(2)}, u32[]{:S(2)}) %collective-permute-start.4) | collective-permute-done | bytes 32800 | tf_op jit(solution)/shard_map/ppermute | solution.py:97
  18.0 5.9 %fusion.10 = f32[2,4,8,1280]{3,2,1,0:T(8,128)S(1)} fusion(bf16[2048,2,1280]{2,1,0:T(2,128)(2,1)} %param.24, bf16[32,2048]{1,0:T(8,128)(2,1)S(1)} %gather_fusion, pred[32]{0:T(512)(128)(4,1)S(1)} %get-tuple-element.62), kind=kOutput, calls=%fused_computation.15 | convolution fusion | flops 335609856 | bytes 10944544 | tf_op jit(solution)/shard_map/rf,fgc->rgc/dot_general | solution.py:178
  24.3 3.6 %collective-permute-start.8 = (f32[8,2560]{1,0:T(8,128)S(1)}, f32[8,2560]{1,0:T(8,128)S(1)}, u32[]{:S(2)}, u32[]{:S(2)}) collective-permute-start(f32[8,2560]{1,0:T(8,128)S(1)} %get-tuple-element.68), channel_id=1, source_target_pairs={{0,12},{4,0},{8,4},{12,8},{1,13},{5,1},{9,5},{13,9},{2,14},{6,2},{... | collective-permute-start | bytes 245768 | tf_op jit(solution)/shard_map/ppermute | solution.py:113
  28.4 2.7 %collective-permute-done.6 = f32[8,2560]{1,0:T(8,128)S(1)} collective-permute-done((f32[8,2560]{1,0:T(8,128)S(1)}, f32[8,2560]{1,0:T(8,128)S(1)}, u32[]{:S(2)}, u32[]{:S(2)}) %collective-permute-start.6) | collective-permute-done | bytes 81952 | tf_op jit(solution)/shard_map/ppermute | solution.py:113
  31.1 2.9 %collective-permute-done.7 = f32[8,2560]{1,0:T(8,128)S(1)} collective-permute-done((f32[8,2560]{1,0:T(8,128)S(1)}, f32[8,2560]{1,0:T(8,128)S(1)}, u32[]{:S(2)}, u32[]{:S(2)}) %collective-permute-start.7) | collective-permute-done | bytes 81952 | tf_op jit(solution)/shard_map/ppermute | solution.py:113
  35.4 1.8 %collective-permute-start.11 = (bf16[8,2048]{1,0:T(8,128)(2,1)S(1)}, bf16[8,2048]{1,0:T(8,128)(2,1)S(1)}, u32[]{:S(2)}, u32[]{:S(2)}) collective-permute-start(bf16[8,2048]{1,0:T(8,128)(2,1)S(1)} %bitcast.117), channel_id=1, source_target_pairs={{0,12},{4,0},{8,4},{12,8},{1,13},{5,1},{9,5},{13,9},{2,14},{6,2},{... | collective-permute-start | bytes 98312 | tf_op jit(solution)/shard_map/ppermute | solution.py:97
  37.9 1.5 %collective-permute-done.11 = bf16[8,2048]{1,0:T(8,128)(2,1)S(1)} collective-permute-done((bf16[8,2048]{1,0:T(8,128)(2,1)S(1)}, bf16[8,2048]{1,0:T(8,128)(2,1)S(1)}, u32[]{:S(2)}, u32[]{:S(2)}) %collective-permute-start.11) | collective-permute-done | bytes 32800 | tf_op jit(solution)/shard_map/ppermute | solution.py:97
  39.4 2.7 %collective-permute-done.10 = bf16[8,2048]{1,0:T(8,128)(2,1)S(1)} collective-permute-done((bf16[8,2048]{1,0:T(8,128)(2,1)S(1)}, bf16[8,2048]{1,0:T(8,128)(2,1)S(1)}, u32[]{:S(2)}, u32[]{:S(2)}) %collective-permute-start.10) | collective-permute-done | bytes 32800 | tf_op jit(solution)/shard_map/ppermute | solution.py:97
  43.6 5.0 %fusion.25 = f32[32,2048]{1,0:T(8,128)S(1)} fusion(bf16[2048,2048]{1,0:T(8,128)(2,1)} %param.25, bf16[32,2048]{1,0:T(8,128)(2,1)S(1)} %gather_fusion.1, pred[32]{0:T(512)(128)(4,1)S(1)} %get-tuple-element.60), kind=kOutput, calls=%fused_computation.46 | convolution fusion | flops 268500992 | bytes 8781856 | tf_op jit(solution)/shard_map/dot_general | solution.py:186
  48.8 1.3 %collective-permute-done.12 = f32[2,8,2048]{2,1,0:T(8,128)S(1)} collective-permute-done((f32[2,8,2048]{2,1,0:T(8,128)S(1)}, f32[2,8,2048]{2,1,0:T(8,128)S(1)}, u32[]{:S(2)}, u32[]{:S(2)}) %collective-permute-start.12) | collective-permute-done | bytes 131104 | tf_op jit(solution)/shard_map/ppermute | solution.py:113
  51.1 3.4 %collective-permute-done.13 = f32[8,2048]{1,0:T(8,128)S(1)} collective-permute-done((f32[8,2048]{1,0:T(8,128)S(1)}, f32[8,2048]{1,0:T(8,128)S(1)}, u32[]{:S(2)}, u32[]{:S(2)}) %collective-permute-start.13) | collective-permute-done | bytes 65568 | tf_op jit(solution)/shard_map/ppermute | solution.py:113
  55.9 1.9 %collective-permute-start.14 = (f32[8]{0:T(128)S(1)}, f32[8]{0:T(128)S(1)}, u32[]{:S(2)}, u32[]{:S(2)}) collective-permute-start(f32[8]{0:T(128)S(1)} %get-tuple-element.58), channel_id=1, source_target_pairs={{0,4},{4,8},{8,12},{12,0},{1,5},{5,9},{9,13},{13,1},{2,6},{6,10},{... | collective-permute-start | bytes 104 | tf_op jit(solution)/shard_map/ppermute | solution.py:128
  58.2 1.7 %collective-permute-done.15 = f32[8]{0:T(128)S(1)} collective-permute-done((f32[8]{0:T(128)S(1)}, f32[8]{0:T(128)S(1)}, u32[]{:S(2)}, u32[]{:S(2)}) %collective-permute-start.15) | collective-permute-done | bytes 64 | tf_op jit(solution)/shard_map/ppermute | solution.py:128
  59.9 1.3 %collective-permute-done.14 = f32[8]{0:T(128)S(1)} collective-permute-done((f32[8]{0:T(128)S(1)}, f32[8]{0:T(128)S(1)}, u32[]{:S(2)}, u32[]{:S(2)}) %collective-permute-start.14) | collective-permute-done | bytes 64 | tf_op jit(solution)/shard_map/ppermute | solution.py:128
  62.9 2.4 %collective-permute-done.18 = bf16[8,2048]{1,0:T(8,128)(2,1)S(1)} collective-permute-done((bf16[8,2048]{1,0:T(8,128)(2,1)S(1)}, bf16[8,2048]{1,0:T(8,128)(2,1)S(1)}, u32[]{:S(2)}, u32[]{:S(2)}) %collective-permute-start.18) | collective-permute-done | bytes 32800 | tf_op jit(solution)/shard_map/ppermute | solution.py:97
  66.3 7.8 %convolution_convert_fusion = bf16[32,3584]{1,0:T(8,128)(2,1)S(1)} fusion(bf16[2048,3584]{1,0:T(8,128)(2,1)} %param.28, bf16[32,2048]{1,0:T(8,128)(2,1)S(1)} %gather_fusion.2, pred[32]{0:T(512)(128)(4,1)S(1)} %compare_and_fusion), kind=kOutput, calls=%fused_computation.5 | convolution fusion | flops 469942272 | bytes 15040544 | tf_op jit(solution)/shard_map/dot_general | solution.py:196
  74.2 7.9 %convolution_convert_fusion.1 = bf16[32,3584]{1,0:T(8,128)(2,1)S(1)} fusion(bf16[2048,3584]{1,0:T(8,128)(2,1)} %param.27, bf16[32,2048]{1,0:T(8,128)(2,1)S(1)} %gather_fusion.2, pred[32]{0:T(512)(128)(4,1)S(1)} %compare_and_fusion), kind=kOutput, calls=%fused_computation.6 | convolution fusion | flops 469942272 | bytes 15040544 | tf_op jit(solution)/shard_map/dot_general | solution.py:195
  82.4 1.8 %collective-permute-start.21 = (bf16[32,1792]{1,0:T(8,128)(2,1)S(1)}, bf16[32,1792]{1,0:T(8,128)(2,1)S(1)}, u32[]{:S(2)}, u32[]{:S(2)}) collective-permute-start(bf16[32,1792]{1,0:T(8,128)(2,1)S(1)} %get-tuple-element.65), channel_id=1, source_target_pairs={{0,8},{4,12},{8,0},{12,4},{1,9},{5,13},{9,1},{13,5},{2,10},{6,14},... | collective-permute-start | bytes 344072 | tf_op jit(solution)/shard_map/ppermute | solution.py:113
  84.2 1.9 %collective-permute-start.22 = (bf16[32,1792]{1,0:T(8,128)(2,1)S(1)}, bf16[32,1792]{1,0:T(8,128)(2,1)S(1)}, u32[]{:S(2)}, u32[]{:S(2)}) collective-permute-start(bf16[32,1792]{1,0:T(8,128)(2,1)S(1)} %get-tuple-element.66), channel_id=1, source_target_pairs={{0,12},{4,0},{8,4},{12,8},{1,13},{5,1},{9,5},{13,9},{2,14},{6,2},{... | collective-permute-start | bytes 344072 | tf_op jit(solution)/shard_map/ppermute | solution.py:113
  86.1 4.1 %collective-permute-done.20 = bf16[32,1792]{1,0:T(8,128)(2,1)S(1)} collective-permute-done((bf16[32,1792]{1,0:T(8,128)(2,1)S(1)}, bf16[32,1792]{1,0:T(8,128)(2,1)S(1)}, u32[]{:S(2)}, u32[]{:S(2)}) %collective-permute-start.20) | collective-permute-done | bytes 114720 | tf_op jit(solution)/shard_map/ppermute | solution.py:113
  90.1 3.0 %collective-permute-done.21 = bf16[32,1792]{1,0:T(8,128)(2,1)S(1)} collective-permute-done((bf16[32,1792]{1,0:T(8,128)(2,1)S(1)}, bf16[32,1792]{1,0:T(8,128)(2,1)S(1)}, u32[]{:S(2)}, u32[]{:S(2)}) %collective-permute-start.21) | collective-permute-done | bytes 114720 | tf_op jit(solution)/shard_map/ppermute | solution.py:113
  93.3 2.8 %collective-permute-start.25 = (bf16[32,896]{1,0:T(8,128)(2,1)S(1)}, bf16[32,896]{1,0:T(8,128)(2,1)S(1)}, u32[]{:S(2)}, u32[]{:S(2)}) collective-permute-start(bf16[32,896]{1,0:T(8,128)(2,1)S(1)} %fusion.42), channel_id=1, source_target_pairs={{0,12},{4,0},{8,4},{12,8},{1,13},{5,1},{9,5},{13,9},{2,14},{6,2},{... | collective-permute-start | bytes 172040 | tf_op jit(solution)/shard_map/ppermute | solution.py:139
  96.8 2.8 %fusion.8 = f32[32,2048]{1,0:T(8,128)S(1)} fusion(bf16[32,896]{1,0:T(8,128)(2,1)S(1)} %fusion.42, bf16[3584,2048]{1,0:T(8,128)(2,1)} %param.29, s32[]{:T(128)S(6)} %select_n.161), kind=kOutput, calls=%fused_computation.13 | convolution fusion | flops 117440512 | bytes 3989508 | tf_op jit(solution)/shard_map/dot_general | solution.py:135
  99.6 2.0 %collective-permute-done.24 = bf16[32,896]{1,0:T(8,128)(2,1)S(1)} collective-permute-done((bf16[32,896]{1,0:T(8,128)(2,1)S(1)}, bf16[32,896]{1,0:T(8,128)(2,1)S(1)}, u32[]{:S(2)}, u32[]{:S(2)}) %collective-permute-start.24) | collective-permute-done | bytes 57376 | tf_op jit(solution)/shard_map/ppermute | solution.py:139
  101.6 2.8 %fusion.4 = f32[32,2048]{1,0:T(8,128)S(1)} fusion(bf16[32,896]{1,0:T(8,128)(2,1)S(1)} %collective-permute-done.24, bf16[3584,2048]{1,0:T(8,128)(2,1)} %param.29, s32[]{:T(128)S(6)} %select_n.165), kind=kOutput, calls=%fused_computation.9 | convolution fusion | flops 117440512 | bytes 3989508 | tf_op jit(solution)/shard_map/dot_general | solution.py:141
  104.4 2.8 %fusion.2 = f32[32,2048]{1,0:T(8,128)S(1)} fusion(bf16[32,896]{1,0:T(8,128)(2,1)S(1)} %collective-permute-done.25, bf16[3584,2048]{1,0:T(8,128)(2,1)} %param.29, s32[]{:T(128)S(6)} %select_n.167), kind=kOutput, calls=%fused_computation.7 | convolution fusion | flops 117440512 | bytes 3989508 | tf_op jit(solution)/shard_map/dot_general | solution.py:141
  107.2 2.8 %fusion.19 = f32[32,2048]{1,0:T(8,128)S(1)} fusion(f32[32,2048]{1,0:T(8,128)S(1)} %fusion.2, f32[32,2048]{1,0:T(8,128)S(1)} %fusion.4, f32[32,2048]{1,0:T(8,128)S(1)} %fusion.8, bf16[32,896]{1,0:T(8,128)(2,1)S(1)} %collective-permute-done.23, bf16[3584,2048]{1,0:T(8,128)(2,1)} %param.29, s32[]{:T(128)S(6)} %select_n.163), kind=kOutput, calls=%fused_computation.18 | convolution fusion | flops 117637120 | bytes 4775940 | tf_op jit(solution)/shard_map/dot_general | solution.py:141
  110.2 1.3 %collective-permute-done.26 = f32[2,8,2048]{2,1,0:T(8,128)S(1)} collective-permute-done((f32[2,8,2048]{2,1,0:T(8,128)S(1)}, f32[2,8,2048]{2,1,0:T(8,128)S(1)}, u32[]{:S(2)}, u32[]{:S(2)}) %collective-permute-start.26) | collective-permute-done | bytes 131104 | tf_op jit(solution)/shard_map/ppermute | solution.py:113
  112.4 3.5 %collective-permute-done.27 = f32[8,2048]{1,0:T(8,128)S(1)} collective-permute-done((f32[8,2048]{1,0:T(8,128)S(1)}, f32[8,2048]{1,0:T(8,128)S(1)}, u32[]{:S(2)}, u32[]{:S(2)}) %collective-permute-start.27) | collective-permute-done | bytes 65568 | tf_op jit(solution)/shard_map/ppermute | solution.py:113
  (96 shorter events, 20.5 us)
Async XLA Ops:
  0.0 27.9 %copy-start = (bf16[8,256,2,2,128]{4,3,2,1,0:T(2,128)(2,1)S(1)}, bf16[8,256,2,2,128]{4,3,2,1,0:T(2,128)(2,1)}, u32[]{:S(2)}) copy-start(bf16[8,256,2,2,128]{4,3,2,1,0:T(2,128)(2,1)} %param.30) | copy-start | bytes 6291460
  1.0 8.2 %collective-permute-start.2 = (f32[8]{0:T(128)S(1)}, f32[8]{0:T(128)S(1)}, u32[]{:S(2)}, u32[]{:S(2)}) collective-permute-start(f32[8]{0:T(128)S(1)} %fusion.46), channel_id=1, source_target_pairs={{0,12},{4,0},{8,4},{12,8},{1,13},{5,1},{9,5},{13,9},{2,14},{6,2},{... | collective-permute-start | bytes 104 | tf_op jit(solution)/shard_map/ppermute | solution.py:128
  6.1 4.4 %collective-permute-start.1 = (f32[8]{0:T(128)S(1)}, f32[8]{0:T(128)S(1)}, u32[]{:S(2)}, u32[]{:S(2)}) collective-permute-start(f32[8]{0:T(128)S(1)} %fusion.46), channel_id=1, source_target_pairs={{0,8},{4,12},{8,0},{12,4},{1,9},{5,13},{9,1},{13,5},{2,10},{6,14},... | collective-permute-start | bytes 104 | tf_op jit(solution)/shard_map/ppermute | solution.py:128
  6.1 5.3 %collective-permute-start = (f32[8]{0:T(128)S(1)}, f32[8]{0:T(128)S(1)}, u32[]{:S(2)}, u32[]{:S(2)}) collective-permute-start(f32[8]{0:T(128)S(1)} %fusion.46), channel_id=1, source_target_pairs={{0,4},{4,8},{8,12},{12,0},{1,5},{5,9},{9,13},{13,1},{2,6},{6,10},{... | collective-permute-start | bytes 104 | tf_op jit(solution)/shard_map/ppermute | solution.py:128
  12.3 1.8 %collective-permute-start.5 = (bf16[8,2048]{1,0:T(8,128)(2,1)S(1)}, bf16[8,2048]{1,0:T(8,128)(2,1)S(1)}, u32[]{:S(2)}, u32[]{:S(2)}) collective-permute-start(bf16[8,2048]{1,0:T(8,128)(2,1)S(1)} %fusion.48), channel_id=1, source_target_pairs={{0,3},{1,0},{2,1},{3,2},{4,7},{5,4},{6,5},{7,6},{8,11},{9,8},{10,9... | collective-permute-start | bytes 98312 | tf_op jit(solution)/shard_map/ppermute | solution.py:97
  12.4 4.1 %collective-permute-start.4 = (bf16[8,2048]{1,0:T(8,128)(2,1)S(1)}, bf16[8,2048]{1,0:T(8,128)(2,1)S(1)}, u32[]{:S(2)}, u32[]{:S(2)}) collective-permute-start(bf16[8,2048]{1,0:T(8,128)(2,1)S(1)} %fusion.48), channel_id=1, source_target_pairs={{0,2},{1,3},{2,0},{3,1},{4,6},{5,7},{6,4},{7,5},{8,10},{9,11},{10,... | collective-permute-start | bytes 98312 | tf_op jit(solution)/shard_map/ppermute | solution.py:97
  13.9 3.3 %collective-permute-start.3 = (bf16[8,2048]{1,0:T(8,128)(2,1)S(1)}, bf16[8,2048]{1,0:T(8,128)(2,1)S(1)}, u32[]{:S(2)}, u32[]{:S(2)}) collective-permute-start(bf16[8,2048]{1,0:T(8,128)(2,1)S(1)} %fusion.48), channel_id=1, source_target_pairs={{0,1},{1,2},{2,3},{3,0},{4,5},{5,6},{6,7},{7,4},{8,9},{9,10},{10,1... | collective-permute-start | bytes 98312 | tf_op jit(solution)/shard_map/ppermute | solution.py:97
  24.0 7.1 %collective-permute-start.6 = (f32[8,2560]{1,0:T(8,128)S(1)}, f32[8,2560]{1,0:T(8,128)S(1)}, u32[]{:S(2)}, u32[]{:S(2)}) collective-permute-start(f32[8,2560]{1,0:T(8,128)S(1)} %get-tuple-element.67), channel_id=1, source_target_pairs={{0,4},{4,8},{8,12},{12,0},{1,5},{5,9},{9,13},{13,1},{2,6},{6,10},{... | collective-permute-start | bytes 245768 | tf_op jit(solution)/shard_map/ppermute | solution.py:113
  24.3 6.8 %collective-permute-start.8 = (f32[8,2560]{1,0:T(8,128)S(1)}, f32[8,2560]{1,0:T(8,128)S(1)}, u32[]{:S(2)}, u32[]{:S(2)}) collective-permute-start(f32[8,2560]{1,0:T(8,128)S(1)} %get-tuple-element.68), channel_id=1, source_target_pairs={{0,12},{4,0},{8,4},{12,8},{1,13},{5,1},{9,5},{13,9},{2,14},{6,2},{... | collective-permute-start | bytes 245768 | tf_op jit(solution)/shard_map/ppermute | solution.py:113
  27.8 6.1 %collective-permute-start.7 = (f32[8,2560]{1,0:T(8,128)S(1)}, f32[8,2560]{1,0:T(8,128)S(1)}, u32[]{:S(2)}, u32[]{:S(2)}) collective-permute-start(f32[8,2560]{1,0:T(8,128)S(1)} %get-tuple-element.69), channel_id=1, source_target_pairs={{0,8},{4,12},{8,0},{12,4},{1,9},{5,13},{9,1},{13,5},{2,10},{6,14},... | collective-permute-start | bytes 245768 | tf_op jit(solution)/shard_map/ppermute | solution.py:113
  34.4 20.1 %copy-start.1 = (bf16[8,2048]{1,0:T(8,128)(2,1)S(1)}, bf16[8,2048]{1,0:T(8,128)(2,1)}, u32[]{:S(2)}) copy-start(bf16[8,2048]{1,0:T(8,128)(2,1)} %param.22) | copy-start | bytes 98308
  34.9 26.4 %copy-start.2 = (f32[2048]{0:T(1024)S(1)}, f32[2048]{0:T(1024)}, u32[]{:S(2)}) copy-start(f32[2048]{0:T(1024)} %param.26) | copy-start | bytes 24580
  35.4 4.0 %collective-permute-start.11 = (bf16[8,2048]{1,0:T(8,128)(2,1)S(1)}, bf16[8,2048]{1,0:T(8,128)(2,1)S(1)}, u32[]{:S(2)}, u32[]{:S(2)}) collective-permute-start(bf16[8,2048]{1,0:T(8,128)(2,1)S(1)} %bitcast.117), channel_id=1, source_target_pairs={{0,12},{4,0},{8,4},{12,8},{1,13},{5,1},{9,5},{13,9},{2,14},{6,2},{... | collective-permute-start | bytes 98312 | tf_op jit(solution)/shard_map/ppermute | solution.py:97
  37.3 4.9 %collective-permute-start.10 = (bf16[8,2048]{1,0:T(8,128)(2,1)S(1)}, bf16[8,2048]{1,0:T(8,128)(2,1)S(1)}, u32[]{:S(2)}, u32[]{:S(2)}) collective-permute-start(bf16[8,2048]{1,0:T(8,128)(2,1)S(1)} %bitcast.118), channel_id=1, source_target_pairs={{0,8},{4,12},{8,0},{12,4},{1,9},{5,13},{9,1},{13,5},{2,10},{6,14},... | collective-permute-start | bytes 98312 | tf_op jit(solution)/shard_map/ppermute | solution.py:97
  37.3 5.7 %collective-permute-start.9 = (bf16[8,2048]{1,0:T(8,128)(2,1)S(1)}, bf16[8,2048]{1,0:T(8,128)(2,1)S(1)}, u32[]{:S(2)}, u32[]{:S(2)}) collective-permute-start(bf16[8,2048]{1,0:T(8,128)(2,1)S(1)} %bitcast.119), channel_id=1, source_target_pairs={{0,4},{4,8},{8,12},{12,0},{1,5},{5,9},{9,13},{13,1},{2,6},{6,10},{... | collective-permute-start | bytes 98312 | tf_op jit(solution)/shard_map/ppermute | solution.py:97
  48.7 1.4 %collective-permute-start.12 = (f32[2,8,2048]{2,1,0:T(8,128)S(1)}, f32[2,8,2048]{2,1,0:T(8,128)S(1)}, u32[]{:S(2)}, u32[]{:S(2)}) collective-permute-start(f32[2,8,2048]{2,1,0:T(8,128)S(1)} %select_bitcast_fusion.1), channel_id=1, source_target_pairs={{0,1},{1,0},{2,3},{3,2},{4,5},{5,4},{6,7},{7,6},{8,9},{9,8},{10,11... | collective-permute-start | bytes 393224 | tf_op jit(solution)/shard_map/ppermute | solution.py:113
  50.1 4.3 %collective-permute-start.13 = (f32[8,2048]{1,0:T(8,128)S(1)}, f32[8,2048]{1,0:T(8,128)S(1)}, u32[]{:S(2)}, u32[]{:S(2)}) collective-permute-start(f32[8,2048]{1,0:T(8,128)S(1)} %select_bitcast_fusion.6), channel_id=1, source_target_pairs={{0,2},{2,0},{1,3},{3,1},{4,6},{6,4},{5,7},{7,5},{8,10},{10,8},{9,1... | collective-permute-start | bytes 196616 | tf_op jit(solution)/shard_map/ppermute | solution.py:113
  54.6 3.6 %collective-permute-start.16 = (f32[8]{0:T(128)S(1)}, f32[8]{0:T(128)S(1)}, u32[]{:S(2)}, u32[]{:S(2)}) collective-permute-start(f32[8]{0:T(128)S(1)} %get-tuple-element.58), channel_id=1, source_target_pairs={{0,12},{4,0},{8,4},{12,8},{1,13},{5,1},{9,5},{13,9},{2,14},{6,2},{... | collective-permute-start | bytes 104 | tf_op jit(solution)/shard_map/ppermute | solution.py:128
  55.5 4.4 %collective-permute-start.15 = (f32[8]{0:T(128)S(1)}, f32[8]{0:T(128)S(1)}, u32[]{:S(2)}, u32[]{:S(2)}) collective-permute-start(f32[8]{0:T(128)S(1)} %get-tuple-element.58), channel_id=1, source_target_pairs={{0,8},{4,12},{8,0},{12,4},{1,9},{5,13},{9,1},{13,5},{2,10},{6,14},... | collective-permute-start | bytes 104 | tf_op jit(solution)/shard_map/ppermute | solution.py:128
  55.9 5.3 %collective-permute-start.14 = (f32[8]{0:T(128)S(1)}, f32[8]{0:T(128)S(1)}, u32[]{:S(2)}, u32[]{:S(2)}) collective-permute-start(f32[8]{0:T(128)S(1)} %get-tuple-element.58), channel_id=1, source_target_pairs={{0,4},{4,8},{8,12},{12,0},{1,5},{5,9},{9,13},{13,1},{2,6},{6,10},{... | collective-permute-start | bytes 104 | tf_op jit(solution)/shard_map/ppermute | solution.py:128
  61.3 1.6 %collective-permute-start.19 = (bf16[8,2048]{1,0:T(8,128)(2,1)S(1)}, bf16[8,2048]{1,0:T(8,128)(2,1)S(1)}, u32[]{:S(2)}, u32[]{:S(2)}) collective-permute-start(bf16[8,2048]{1,0:T(8,128)(2,1)S(1)} %multiply_convert_fusion), channel_id=1, source_target_pairs={{0,3},{1,0},{2,1},{3,2},{4,7},{5,4},{6,5},{7,6},{8,11},{9,8},{10,9... | collective-permute-start | bytes 98312 | tf_op jit(solution)/shard_map/ppermute | solution.py:97
  61.3 4.0 %collective-permute-start.18 = (bf16[8,2048]{1,0:T(8,128)(2,1)S(1)}, bf16[8,2048]{1,0:T(8,128)(2,1)S(1)}, u32[]{:S(2)}, u32[]{:S(2)}) collective-permute-start(bf16[8,2048]{1,0:T(8,128)(2,1)S(1)} %multiply_convert_fusion), channel_id=1, source_target_pairs={{0,2},{1,3},{2,0},{3,1},{4,6},{5,7},{6,4},{7,5},{8,10},{9,11},{10,... | collective-permute-start | bytes 98312 | tf_op jit(solution)/shard_map/ppermute | solution.py:97
  62.3 3.4 %collective-permute-start.17 = (bf16[8,2048]{1,0:T(8,128)(2,1)S(1)}, bf16[8,2048]{1,0:T(8,128)(2,1)S(1)}, u32[]{:S(2)}, u32[]{:S(2)}) collective-permute-start(bf16[8,2048]{1,0:T(8,128)(2,1)S(1)} %multiply_convert_fusion), channel_id=1, source_target_pairs={{0,1},{1,2},{2,3},{3,0},{4,5},{5,6},{6,7},{7,4},{8,9},{9,10},{10,1... | collective-permute-start | bytes 98312 | tf_op jit(solution)/shard_map/ppermute | solution.py:97
  82.2 7.9 %collective-permute-start.20 = (bf16[32,1792]{1,0:T(8,128)(2,1)S(1)}, bf16[32,1792]{1,0:T(8,128)(2,1)S(1)}, u32[]{:S(2)}, u32[]{:S(2)}) collective-permute-start(bf16[32,1792]{1,0:T(8,128)(2,1)S(1)} %get-tuple-element.64), channel_id=1, source_target_pairs={{0,4},{4,8},{8,12},{12,0},{1,5},{5,9},{9,13},{13,1},{2,6},{6,10},{... | collective-permute-start | bytes 344072 | tf_op jit(solution)/shard_map/ppermute | solution.py:113
  82.4 10.8 %collective-permute-start.21 = (bf16[32,1792]{1,0:T(8,128)(2,1)S(1)}, bf16[32,1792]{1,0:T(8,128)(2,1)S(1)}, u32[]{:S(2)}, u32[]{:S(2)}) collective-permute-start(bf16[32,1792]{1,0:T(8,128)(2,1)S(1)} %get-tuple-element.65), channel_id=1, source_target_pairs={{0,8},{4,12},{8,0},{12,4},{1,9},{5,13},{9,1},{13,5},{2,10},{6,14},... | collective-permute-start | bytes 344072 | tf_op jit(solution)/shard_map/ppermute | solution.py:113
  84.2 9.0 %collective-permute-start.22 = (bf16[32,1792]{1,0:T(8,128)(2,1)S(1)}, bf16[32,1792]{1,0:T(8,128)(2,1)S(1)}, u32[]{:S(2)}, u32[]{:S(2)}) collective-permute-start(bf16[32,1792]{1,0:T(8,128)(2,1)S(1)} %get-tuple-element.66), channel_id=1, source_target_pairs={{0,12},{4,0},{8,4},{12,8},{1,13},{5,1},{9,5},{13,9},{2,14},{6,2},{... | collective-permute-start | bytes 344072 | tf_op jit(solution)/shard_map/ppermute | solution.py:113
  93.3 11.1 %collective-permute-start.25 = (bf16[32,896]{1,0:T(8,128)(2,1)S(1)}, bf16[32,896]{1,0:T(8,128)(2,1)S(1)}, u32[]{:S(2)}, u32[]{:S(2)}) collective-permute-start(bf16[32,896]{1,0:T(8,128)(2,1)S(1)} %fusion.42), channel_id=1, source_target_pairs={{0,12},{4,0},{8,4},{12,8},{1,13},{5,1},{9,5},{13,9},{2,14},{6,2},{... | collective-permute-start | bytes 172040 | tf_op jit(solution)/shard_map/ppermute | solution.py:139
  96.0 5.6 %collective-permute-start.24 = (bf16[32,896]{1,0:T(8,128)(2,1)S(1)}, bf16[32,896]{1,0:T(8,128)(2,1)S(1)}, u32[]{:S(2)}, u32[]{:S(2)}) collective-permute-start(bf16[32,896]{1,0:T(8,128)(2,1)S(1)} %fusion.42), channel_id=1, source_target_pairs={{0,8},{4,12},{8,0},{12,4},{1,9},{5,13},{9,1},{13,5},{2,10},{6,14},... | collective-permute-start | bytes 172040 | tf_op jit(solution)/shard_map/ppermute | solution.py:139
  96.8 10.4 %collective-permute-start.23 = (bf16[32,896]{1,0:T(8,128)(2,1)S(1)}, bf16[32,896]{1,0:T(8,128)(2,1)S(1)}, u32[]{:S(2)}, u32[]{:S(2)}) collective-permute-start(bf16[32,896]{1,0:T(8,128)(2,1)S(1)} %fusion.42), channel_id=1, source_target_pairs={{0,4},{4,8},{8,12},{12,0},{1,5},{5,9},{9,13},{13,1},{2,6},{6,10},{... | collective-permute-start | bytes 172040 | tf_op jit(solution)/shard_map/ppermute | solution.py:139
  110.1 1.4 %collective-permute-start.26 = (f32[2,8,2048]{2,1,0:T(8,128)S(1)}, f32[2,8,2048]{2,1,0:T(8,128)S(1)}, u32[]{:S(2)}, u32[]{:S(2)}) collective-permute-start(f32[2,8,2048]{2,1,0:T(8,128)S(1)} %select_bitcast_fusion), channel_id=1, source_target_pairs={{0,1},{1,0},{2,3},{3,2},{4,5},{5,4},{6,7},{7,6},{8,9},{9,8},{10,11... | collective-permute-start | bytes 393224 | tf_op jit(solution)/shard_map/ppermute | solution.py:113
  111.5 4.3 %collective-permute-start.27 = (f32[8,2048]{1,0:T(8,128)S(1)}, f32[8,2048]{1,0:T(8,128)S(1)}, u32[]{:S(2)}, u32[]{:S(2)}) collective-permute-start(f32[8,2048]{1,0:T(8,128)S(1)} %select_bitcast_fusion.5), channel_id=1, source_target_pairs={{0,2},{2,0},{1,3},{3,1},{4,6},{6,4},{5,7},{7,5},{8,10},{10,8},{9,1... | collective-permute-start | bytes 196616 | tf_op jit(solution)/shard_map/ppermute | solution.py:113

commit v9 on v8

--- a/solution.py
+++ b/solution.py
@@ -127,6 +127,29 @@
     for k in range(1, n):
         total = total + lax.ppermute(x, axis, shift_pairs(n, k))
     return total
+
+
+def scatter_matmul(x, weights, axis, n):
+    idx = lax.axis_index(axis)
+    chunk = weights[0].shape[1] // n
+
+    def block(j):
+        parts = [
+            jnp.dot(
+                x,
+                lax.dynamic_slice_in_dim(w, j * chunk, chunk, 1),
+                preferred_element_type=jnp.float32,
+            ).astype(jnp.bfloat16)
+            for w in weights
+        ]
+        return jnp.concatenate(parts, axis=1)
+
+    total = None
+    for k in range(1, n):
+        got = lax.ppermute(block((idx + k) % n), axis, shift_pairs(n, k)).astype(jnp.float32)
+        total = got if total is None else total + got
+    own = block(idx).astype(jnp.float32)
+    return own if total is None else own + total
 
 
 def gather_matmul(x, w, axis, n):
@@ -191,12 +214,8 @@
         residual * lax.rsqrt(squares_mid / D + epsilon)[:, None] * ffn_gain[None, :]
     ).astype(jnp.bfloat16)
     ffn_all = gather_rows(ffn_normed, CS, n_cs, every)
+    both = scatter_matmul(ffn_all, (w_gate, w_up), "pool", n_pool)
     chunk = w_gate.shape[1] // n_pool
-    gate_part = jnp.dot(ffn_all, w_gate, preferred_element_type=jnp.float32).astype(jnp.bfloat16)
-    up_part = jnp.dot(ffn_all, w_up, preferred_element_type=jnp.float32).astype(jnp.bfloat16)
-    gate_blocks = gate_part.reshape(rows_total, n_pool, chunk).transpose(1, 0, 2)
-    up_blocks = up_part.reshape(rows_total, n_pool, chunk).transpose(1, 0, 2)
-    both = scatter_sum(jnp.concatenate([gate_blocks, up_blocks], axis=2), "pool", n_pool)
     gate_total = both[:, :chunk]
     up_total = both[:, chunk:]
     hidden = (jax.nn.silu(gate_total) * up_total).astype(jnp.bfloat16)

time: 117 us -> 115 us (0.983)
    dot_general x2 -> x8, matrix products: 15.7 us -> 22.9 us  [block(): jnp.dot(x, lax.dynamic_slice_in_dim(w, j * chunk, chunk, 1), preferred_el...]
    ppermute x10 -> x7, waiting for transfers between devices: 22.1 us -> 15 us  [scatter_sum(): lax.ppermute(piece, axis, shift_pairs(n, k)).astype(jnp.float32)]
    dot_general x3, matrix products: 8.39 us -> 2.26 us  [gather_matmul(): acc = acc + jnp.dot(got, rows, preferred_element_type=jnp.float32)]
    ppermute x0 -> x3, waiting for transfers between devices: none -> 6.05 us  [scatter_matmul(): lax.ppermute(block((idx + k) % n), axis, shift_pairs(n, k))]
    ppermute x10 -> x7, starting transfers between devices: 9.72 us -> 5.92 us  [scatter_sum(): lax.ppermute(piece, axis, shift_pairs(n, k)).astype(jnp.float32)]
    ppermute x0 -> x3, starting transfers between devices: none -> 2.93 us  [scatter_matmul(): lax.ppermute(block((idx + k) % n), axis, shift_pairs(n, k))]
    dot_general x1, matrix products: 2.78 us -> 0.74 us  [gather_matmul(): jnp.dot(x, lax.dynamic_slice_in_dim(w, idx * chunk, chunk, 0), preferred_...]
  transfers between devices with their start and end apart: 28 -> 28, of which waited for: 22 -> 21; matrix products, arithmetic and copies ran while one was open for 9% -> 7% of each run, Pallas kernels for 0% -> 0%
where the time goes in v9:
time: 115 us; the launch traced here: 114 us
  waiting for transfers between devices  40.4 us (35%)
  matrix products  37.8 us (33%)
  starting transfers between devices  27.2 us (24%)
  other arithmetic  5.59 us (5%)
  local copies, waits for them, and re-layouts  2.6 us (2%)
    dot_general x8, matrix products, block(): jnp.dot(x, lax.dynamic_slice_in_dim(w, j * chunk, chunk, 1), preferred_el...  22.9 us
    ppermute x7, waiting for transfers between devices, scatter_sum(): lax.ppermute(piece, axis, shift_pairs(n, k)).astype(jnp.float32)  15 us
    ppermute x9, waiting for transfers between devices, gather_rows(): got = [x] + [lax.ppermute(x, axis, shift_pairs(n, k)) for k in range(1, n)]  11.3 us
    ppermute x6, starting transfers between devices, all_sum(): total = total + lax.ppermute(x, axis, shift_pairs(n, k))  9.3 us
    ppermute x3, waiting for transfers between devices, scatter_matmul(): lax.ppermute(block((idx + k) % n), axis, shift_pairs(n, k))  6.05 us
    dot_general x1, matrix products, local(): jnp.einsum('rf,fgc->rgc', by_slot, w_qkv, preferred_element_type=jnp.floa...  5.94 us
    ppermute x7, starting transfers between devices, scatter_sum(): lax.ppermute(piece, axis, shift_pairs(n, k)).astype(jnp.float32)  5.92 us
    ppermute x6, waiting for transfers between devices, all_sum(): total = total + lax.ppermute(x, axis, shift_pairs(n, k))  5.64 us
  transfers between devices with their start and end apart: 28, of which 21 were waited for; matrix products, arithmetic and copies ran while one was open for 7% of the time, Pallas kernels for 0%

profile of v9, /device:TPU:0, one launch (start us, length us, event | category | flops | bytes accessed | tf_op | source)
XLA Modules:
  0.0 114.2 jit_solution(9333977319190994318)
XLA Ops:
  1.0 5.1 %collective-permute-start.2 = (f32[8]{0:T(128)S(1)}, f32[8]{0:T(128)S(1)}, u32[]{:S(2)}, u32[]{:S(2)}) collective-permute-start(f32[8]{0:T(128)S(1)} %fusion.74), channel_id=1, source_target_pairs={{0,12},{4,0},{8,4},{12,8},{1,13},{5,1},{9,5},{13,9},{2,14},{6,2},{... | collective-permute-start | bytes 104 | tf_op jit(solution)/shard_map/ppermute | solution.py:128
  9.2 1.3 %collective-permute-done.1 = f32[8]{0:T(128)S(1)} collective-permute-done((f32[8]{0:T(128)S(1)}, f32[8]{0:T(128)S(1)}, u32[]{:S(2)}, u32[]{:S(2)}) %collective-permute-start.1) | collective-permute-done | bytes 64 | tf_op jit(solution)/shard_map/ppermute | solution.py:128
  12.4 1.6 %collective-permute-start.4 = (bf16[8,2048]{1,0:T(8,128)(2,1)S(1)}, bf16[8,2048]{1,0:T(8,128)(2,1)S(1)}, u32[]{:S(2)}, u32[]{:S(2)}) collective-permute-start(bf16[8,2048]{1,0:T(8,128)(2,1)S(1)} %fusion.76), channel_id=1, source_target_pairs={{0,2},{1,3},{2,0},{3,1},{4,6},{5,7},{6,4},{7,5},{8,10},{9,11},{10,... | collective-permute-start | bytes 98312 | tf_op jit(solution)/shard_map/ppermute | solution.py:97
  14.1 2.3 %collective-permute-done.4 = bf16[8,2048]{1,0:T(8,128)(2,1)S(1)} collective-permute-done((bf16[8,2048]{1,0:T(8,128)(2,1)S(1)}, bf16[8,2048]{1,0:T(8,128)(2,1)S(1)}, u32[]{:S(2)}, u32[]{:S(2)}) %collective-permute-start.4) | collective-permute-done | bytes 32800 | tf_op jit(solution)/shard_map/ppermute | solution.py:97
  18.0 5.9 %fusion.26 = f32[2,4,8,1280]{3,2,1,0:T(8,128)S(1)} fusion(bf16[2048,2,1280]{2,1,0:T(2,128)(2,1)} %param.22, bf16[32,2048]{1,0:T(8,128)(2,1)S(1)} %gather_fusion, pred[32]{0:T(512)(128)(4,1)S(1)} %get-tuple-element.50), kind=kOutput, calls=%fused_computation.29 | convolution fusion | flops 335609856 | bytes 10944544 | tf_op jit(solution)/shard_map/rf,fgc->rgc/dot_general | solution.py:201
  24.3 3.6 %collective-permute-start.8 = (f32[8,2560]{1,0:T(8,128)S(1)}, f32[8,2560]{1,0:T(8,128)S(1)}, u32[]{:S(2)}, u32[]{:S(2)}) collective-permute-start(f32[8,2560]{1,0:T(8,128)S(1)} %get-tuple-element.53), channel_id=1, source_target_pairs={{0,12},{4,0},{8,4},{12,8},{1,13},{5,1},{9,5},{13,9},{2,14},{6,2},{... | collective-permute-start | bytes 245768 | tf_op jit(solution)/shard_map/ppermute | solution.py:113
  28.4 2.7 %collective-permute-done.6 = f32[8,2560]{1,0:T(8,128)S(1)} collective-permute-done((f32[8,2560]{1,0:T(8,128)S(1)}, f32[8,2560]{1,0:T(8,128)S(1)}, u32[]{:S(2)}, u32[]{:S(2)}) %collective-permute-start.6) | collective-permute-done | bytes 81952 | tf_op jit(solution)/shard_map/ppermute | solution.py:113
  31.1 2.9 %collective-permute-done.7 = f32[8,2560]{1,0:T(8,128)S(1)} collective-permute-done((f32[8,2560]{1,0:T(8,128)S(1)}, f32[8,2560]{1,0:T(8,128)S(1)}, u32[]{:S(2)}, u32[]{:S(2)}) %collective-permute-start.7) | collective-permute-done | bytes 81952 | tf_op jit(solution)/shard_map/ppermute | solution.py:113
  35.4 1.8 %collective-permute-start.11 = (bf16[8,2048]{1,0:T(8,128)(2,1)S(1)}, bf16[8,2048]{1,0:T(8,128)(2,1)S(1)}, u32[]{:S(2)}, u32[]{:S(2)}) collective-permute-start(bf16[8,2048]{1,0:T(8,128)(2,1)S(1)} %bitcast.95), channel_id=1, source_target_pairs={{0,12},{4,0},{8,4},{12,8},{1,13},{5,1},{9,5},{13,9},{2,14},{6,2},{... | collective-permute-start | bytes 98312 | tf_op jit(solution)/shard_map/ppermute | solution.py:97
  37.9 1.5 %collective-permute-done.11 = bf16[8,2048]{1,0:T(8,128)(2,1)S(1)} collective-permute-done((bf16[8,2048]{1,0:T(8,128)(2,1)S(1)}, bf16[8,2048]{1,0:T(8,128)(2,1)S(1)}, u32[]{:S(2)}, u32[]{:S(2)}) %collective-permute-start.11) | collective-permute-done | bytes 32800 | tf_op jit(solution)/shard_map/ppermute | solution.py:97
  39.4 2.7 %collective-permute-done.10 = bf16[8,2048]{1,0:T(8,128)(2,1)S(1)} collective-permute-done((bf16[8,2048]{1,0:T(8,128)(2,1)S(1)}, bf16[8,2048]{1,0:T(8,128)(2,1)S(1)}, u32[]{:S(2)}, u32[]{:S(2)}) %collective-permute-start.10) | collective-permute-done | bytes 32800 | tf_op jit(solution)/shard_map/ppermute | solution.py:97
  43.7 5.0 %fusion.65 = f32[32,2048]{1,0:T(8,128)S(1)} fusion(bf16[2048,2048]{1,0:T(8,128)(2,1)} %param.23, bf16[32,2048]{1,0:T(8,128)(2,1)S(1)} %gather_fusion.1, pred[32]{0:T(512)(128)(4,1)S(1)} %get-tuple-element.48), kind=kOutput, calls=%fused_computation.58 | convolution fusion | flops 268500992 | bytes 8781856 | tf_op jit(solution)/shard_map/dot_general | solution.py:209
  48.8 1.3 %collective-permute-done.12 = f32[2,8,2048]{2,1,0:T(8,128)S(1)} collective-permute-done((f32[2,8,2048]{2,1,0:T(8,128)S(1)}, f32[2,8,2048]{2,1,0:T(8,128)S(1)}, u32[]{:S(2)}, u32[]{:S(2)}) %collective-permute-start.12) | collective-permute-done | bytes 131104 | tf_op jit(solution)/shard_map/ppermute | solution.py:113
  51.1 3.4 %collective-permute-done.13 = f32[8,2048]{1,0:T(8,128)S(1)} collective-permute-done((f32[8,2048]{1,0:T(8,128)S(1)}, f32[8,2048]{1,0:T(8,128)S(1)}, u32[]{:S(2)}, u32[]{:S(2)}) %collective-permute-start.13) | collective-permute-done | bytes 65568 | tf_op jit(solution)/shard_map/ppermute | solution.py:113
  55.9 1.9 %collective-permute-start.14 = (f32[8]{0:T(128)S(1)}, f32[8]{0:T(128)S(1)}, u32[]{:S(2)}, u32[]{:S(2)}) collective-permute-start(f32[8]{0:T(128)S(1)} %get-tuple-element.46), channel_id=1, source_target_pairs={{0,4},{4,8},{8,12},{12,0},{1,5},{5,9},{9,13},{13,1},{2,6},{6,10},{... | collective-permute-start | bytes 104 | tf_op jit(solution)/shard_map/ppermute | solution.py:128
  58.2 1.7 %collective-permute-done.15 = f32[8]{0:T(128)S(1)} collective-permute-done((f32[8]{0:T(128)S(1)}, f32[8]{0:T(128)S(1)}, u32[]{:S(2)}, u32[]{:S(2)}) %collective-permute-start.15) | collective-permute-done | bytes 64 | tf_op jit(solution)/shard_map/ppermute | solution.py:128
  59.9 1.3 %collective-permute-done.14 = f32[8]{0:T(128)S(1)} collective-permute-done((f32[8]{0:T(128)S(1)}, f32[8]{0:T(128)S(1)}, u32[]{:S(2)}, u32[]{:S(2)}) %collective-permute-start.14) | collective-permute-done | bytes 64 | tf_op jit(solution)/shard_map/ppermute | solution.py:128
  62.9 2.4 %collective-permute-done.18 = bf16[8,2048]{1,0:T(8,128)(2,1)S(1)} collective-permute-done((bf16[8,2048]{1,0:T(8,128)(2,1)S(1)}, bf16[8,2048]{1,0:T(8,128)(2,1)S(1)}, u32[]{:S(2)}, u32[]{:S(2)}) %collective-permute-start.18) | collective-permute-done | bytes 32800 | tf_op jit(solution)/shard_map/ppermute | solution.py:97
  66.4 2.8 %fusion.44 = bf16[32,896]{1,0:T(8,128)(2,1)S(1)} fusion(bf16[2048,3584]{1,0:T(8,128)(2,1)} %param.25, s32[]{:T(128)S(6)} %select_n.170, bf16[32,2048]{1,0:T(8,128)(2,1)S(1)} %gather_fusion.2, pred[32]{0:T(512)(128)(4,1)S(1)} %compare_and_fusion), kind=kOutput, calls=%fused_computation.36 | convolution fusion | flops 117534720 | bytes 3858468 | tf_op jit(solution)/shard_map/dot_general | solution.py:138
  69.2 2.9 %fusion.47 = bf16[32,896]{1,0:T(8,128)(2,1)S(1)} fusion(bf16[2048,3584]{1,0:T(8,128)(2,1)} %param.26, s32[]{:T(128)S(6)} %select_n.170, bf16[32,2048]{1,0:T(8,128)(2,1)S(1)} %gather_fusion.2, pred[32]{0:T(512)(128)(4,1)S(1)} %compare_and_fusion), kind=kOutput, calls=%fused_computation.37 | convolution fusion | flops 117534720 | bytes 3858468 | tf_op jit(solution)/shard_map/dot_general | solution.py:138
  72.1 2.9 %fusion.50 = bf16[32,896]{1,0:T(8,128)(2,1)S(1)} fusion(bf16[2048,3584]{1,0:T(8,128)(2,1)} %param.25, s32[]{:T(128)S(6)} %select_n.171, bf16[32,2048]{1,0:T(8,128)(2,1)S(1)} %gather_fusion.2, pred[32]{0:T(512)(128)(4,1)S(1)} %compare_and_fusion), kind=kOutput, calls=%fused_computation.38 | convolution fusion | flops 117534720 | bytes 3858468 | tf_op jit(solution)/shard_map/dot_general | solution.py:138
  75.1 2.8 %fusion.53 = bf16[32,896]{1,0:T(8,128)(2,1)S(1)} fusion(bf16[2048,3584]{1,0:T(8,128)(2,1)} %param.26, s32[]{:T(128)S(6)} %select_n.171, bf16[32,2048]{1,0:T(8,128)(2,1)S(1)} %gather_fusion.2, pred[32]{0:T(512)(128)(4,1)S(1)} %compare_and_fusion), kind=kOutput, calls=%fused_computation.39 | convolution fusion | flops 117534720 | bytes 3858468 | tf_op jit(solution)/shard_map/dot_general | solution.py:138
  77.9 2.9 %fusion.56 = bf16[32,896]{1,0:T(8,128)(2,1)S(1)} fusion(bf16[2048,3584]{1,0:T(8,128)(2,1)} %param.25, s32[]{:T(128)S(6)} %select_n.172, bf16[32,2048]{1,0:T(8,128)(2,1)S(1)} %gather_fusion.2, pred[32]{0:T(512)(128)(4,1)S(1)} %compare_and_fusion), kind=kOutput, calls=%fused_computation.40 | convolution fusion | flops 117534720 | bytes 3858468 | tf_op jit(solution)/shard_map/dot_general | solution.py:138
  80.9 2.8 %fusion.59 = bf16[32,896]{1,0:T(8,128)(2,1)S(1)} fusion(bf16[2048,3584]{1,0:T(8,128)(2,1)} %param.26, s32[]{:T(128)S(6)} %select_n.172, bf16[32,2048]{1,0:T(8,128)(2,1)S(1)} %gather_fusion.2, pred[32]{0:T(512)(128)(4,1)S(1)} %compare_and_fusion), kind=kOutput, calls=%fused_computation.41 | convolution fusion | flops 117534720 | bytes 3858468 | tf_op jit(solution)/shard_map/dot_general | solution.py:138
  83.7 2.9 %fusion.41 = bf16[32,896]{1,0:T(8,128)(2,1)S(1)} fusion(bf16[2048,3584]{1,0:T(8,128)(2,1)} %param.26, s32[]{:T(128)S(6)} %select_n.169, bf16[32,2048]{1,0:T(8,128)(2,1)S(1)} %gather_fusion.2, pred[32]{0:T(512)(128)(4,1)S(1)} %compare_and_fusion), kind=kOutput, calls=%fused_computation.35 | convolution fusion | flops 117534720 | bytes 3858468 | tf_op jit(solution)/shard_map/dot_general | solution.py:138
  86.6 1.4 %collective-permute-start.22 = (bf16[32,1792]{1,0:T(8,128)(2,1)S(1)}, bf16[32,1792]{1,0:T(8,128)(2,1)S(1)}, u32[]{:S(2)}, u32[]{:S(2)}) collective-permute-start(bf16[32,1792]{1,0:T(8,128)(2,1)S(1)} %pad_maximum_fusion.5), channel_id=1, source_target_pairs={{0,12},{4,0},{8,4},{12,8},{1,13},{5,1},{9,5},{13,9},{2,14},{6,2},{... | collective-permute-start | bytes 344072 | tf_op jit(solution)/shard_map/ppermute | solution.py:149
  89.6 2.8 %fusion.38 = bf16[32,896]{1,0:T(8,128)(2,1)S(1)} fusion(bf16[2048,3584]{1,0:T(8,128)(2,1)} %param.25, s32[]{:T(128)S(6)} %select_n.169, bf16[32,2048]{1,0:T(8,128)(2,1)S(1)} %gather_fusion.2, pred[32]{0:T(512)(128)(4,1)S(1)} %compare_and_fusion), kind=kOutput, calls=%fused_computation.34 | convolution fusion | flops 117534720 | bytes 3858468 | tf_op jit(solution)/shard_map/dot_general | solution.py:138
  92.4 6.0 %collective-permute-done.21 = bf16[32,1792]{1,0:T(8,128)(2,1)S(1)} collective-permute-done((bf16[32,1792]{1,0:T(8,128)(2,1)S(1)}, bf16[32,1792]{1,0:T(8,128)(2,1)S(1)}, u32[]{:S(2)}, u32[]{:S(2)}) %collective-permute-start.21) | collective-permute-done | bytes 114720 | tf_op jit(solution)/shard_map/ppermute | solution.py:149
  100.3 1.9 %collective-permute-start.23 = (bf16[32,896]{1,0:T(8,128)(2,1)S(1)}, bf16[32,896]{1,0:T(8,128)(2,1)S(1)}, u32[]{:S(2)}, u32[]{:S(2)}) collective-permute-start(bf16[32,896]{1,0:T(8,128)(2,1)S(1)} %fusion.70), channel_id=1, source_target_pairs={{0,4},{4,8},{8,12},{12,0},{1,5},{5,9},{9,13},{13,1},{2,6},{6,10},{... | collective-permute-start | bytes 172040 | tf_op jit(solution)/shard_map/ppermute | solution.py:162
  103.0 2.4 %collective-permute-done.24 = bf16[32,896]{1,0:T(8,128)(2,1)S(1)} collective-permute-done((bf16[32,896]{1,0:T(8,128)(2,1)S(1)}, bf16[32,896]{1,0:T(8,128)(2,1)S(1)}, u32[]{:S(2)}, u32[]{:S(2)}) %collective-permute-start.24) | collective-permute-done | bytes 57376 | tf_op jit(solution)/shard_map/ppermute | solution.py:162
  107.9 1.3 %collective-permute-done.26 = f32[2,8,2048]{2,1,0:T(8,128)S(1)} collective-permute-done((f32[2,8,2048]{2,1,0:T(8,128)S(1)}, f32[2,8,2048]{2,1,0:T(8,128)S(1)}, u32[]{:S(2)}, u32[]{:S(2)}) %collective-permute-start.26) | collective-permute-done | bytes 131104 | tf_op jit(solution)/shard_map/ppermute | solution.py:113
  110.2 3.4 %collective-permute-done.27 = f32[8,2048]{1,0:T(8,128)S(1)} collective-permute-done((f32[8,2048]{1,0:T(8,128)S(1)}, f32[8,2048]{1,0:T(8,128)S(1)}, u32[]{:S(2)}, u32[]{:S(2)}) %collective-permute-start.27) | collective-permute-done | bytes 65568 | tf_op jit(solution)/shard_map/ppermute | solution.py:113
  (112 shorter events, 25.6 us)
Async XLA Ops:
  0.0 27.9 %copy-start = (bf16[8,256,2,2,128]{4,3,2,1,0:T(2,128)(2,1)S(1)}, bf16[8,256,2,2,128]{4,3,2,1,0:T(2,128)(2,1)}, u32[]{:S(2)}) copy-start(bf16[8,256,2,2,128]{4,3,2,1,0:T(2,128)(2,1)} %param.28) | copy-start | bytes 6291460
  1.0 8.2 %collective-permute-start.2 = (f32[8]{0:T(128)S(1)}, f32[8]{0:T(128)S(1)}, u32[]{:S(2)}, u32[]{:S(2)}) collective-permute-start(f32[8]{0:T(128)S(1)} %fusion.74), channel_id=1, source_target_pairs={{0,12},{4,0},{8,4},{12,8},{1,13},{5,1},{9,5},{13,9},{2,14},{6,2},{... | collective-permute-start | bytes 104 | tf_op jit(solution)/shard_map/ppermute | solution.py:128
  6.1 4.4 %collective-permute-start.1 = (f32[8]{0:T(128)S(1)}, f32[8]{0:T(128)S(1)}, u32[]{:S(2)}, u32[]{:S(2)}) collective-permute-start(f32[8]{0:T(128)S(1)} %fusion.74), channel_id=1, source_target_pairs={{0,8},{4,12},{8,0},{12,4},{1,9},{5,13},{9,1},{13,5},{2,10},{6,14},... | collective-permute-start | bytes 104 | tf_op jit(solution)/shard_map/ppermute | solution.py:128
  6.1 5.3 %collective-permute-start = (f32[8]{0:T(128)S(1)}, f32[8]{0:T(128)S(1)}, u32[]{:S(2)}, u32[]{:S(2)}) collective-permute-start(f32[8]{0:T(128)S(1)} %fusion.74), channel_id=1, source_target_pairs={{0,4},{4,8},{8,12},{12,0},{1,5},{5,9},{9,13},{13,1},{2,6},{6,10},{... | collective-permute-start | bytes 104 | tf_op jit(solution)/shard_map/ppermute | solution.py:128
  12.3 1.8 %collective-permute-start.5 = (bf16[8,2048]{1,0:T(8,128)(2,1)S(1)}, bf16[8,2048]{1,0:T(8,128)(2,1)S(1)}, u32[]{:S(2)}, u32[]{:S(2)}) collective-permute-start(bf16[8,2048]{1,0:T(8,128)(2,1)S(1)} %fusion.76), channel_id=1, source_target_pairs={{0,3},{1,0},{2,1},{3,2},{4,7},{5,4},{6,5},{7,6},{8,11},{9,8},{10,9... | collective-permute-start | bytes 98312 | tf_op jit(solution)/shard_map/ppermute | solution.py:97
  12.4 4.1 %collective-permute-start.4 = (bf16[8,2048]{1,0:T(8,128)(2,1)S(1)}, bf16[8,2048]{1,0:T(8,128)(2,1)S(1)}, u32[]{:S(2)}, u32[]{:S(2)}) collective-permute-start(bf16[8,2048]{1,0:T(8,128)(2,1)S(1)} %fusion.76), channel_id=1, source_target_pairs={{0,2},{1,3},{2,0},{3,1},{4,6},{5,7},{6,4},{7,5},{8,10},{9,11},{10,... | collective-permute-start | bytes 98312 | tf_op jit(solution)/shard_map/ppermute | solution.py:97
  13.9 3.3 %collective-permute-start.3 = (bf16[8,2048]{1,0:T(8,128)(2,1)S(1)}, bf16[8,2048]{1,0:T(8,128)(2,1)S(1)}, u32[]{:S(2)}, u32[]{:S(2)}) collective-permute-start(bf16[8,2048]{1,0:T(8,128)(2,1)S(1)} %fusion.76), channel_id=1, source_target_pairs={{0,1},{1,2},{2,3},{3,0},{4,5},{5,6},{6,7},{7,4},{8,9},{9,10},{10,1... | collective-permute-start | bytes 98312 | tf_op jit(solution)/shard_map/ppermute | solution.py:97
  24.0 7.1 %collective-permute-start.6 = (f32[8,2560]{1,0:T(8,128)S(1)}, f32[8,2560]{1,0:T(8,128)S(1)}, u32[]{:S(2)}, u32[]{:S(2)}) collective-permute-start(f32[8,2560]{1,0:T(8,128)S(1)} %get-tuple-element.52), channel_id=1, source_target_pairs={{0,4},{4,8},{8,12},{12,0},{1,5},{5,9},{9,13},{13,1},{2,6},{6,10},{... | collective-permute-start | bytes 245768 | tf_op jit(solution)/shard_map/ppermute | solution.py:113
  24.3 6.8 %collective-permute-start.8 = (f32[8,2560]{1,0:T(8,128)S(1)}, f32[8,2560]{1,0:T(8,128)S(1)}, u32[]{:S(2)}, u32[]{:S(2)}) collective-permute-start(f32[8,2560]{1,0:T(8,128)S(1)} %get-tuple-element.53), channel_id=1, source_target_pairs={{0,12},{4,0},{8,4},{12,8},{1,13},{5,1},{9,5},{13,9},{2,14},{6,2},{... | collective-permute-start | bytes 245768 | tf_op jit(solution)/shard_map/ppermute | solution.py:113
  27.8 6.1 %collective-permute-start.7 = (f32[8,2560]{1,0:T(8,128)S(1)}, f32[8,2560]{1,0:T(8,128)S(1)}, u32[]{:S(2)}, u32[]{:S(2)}) collective-permute-start(f32[8,2560]{1,0:T(8,128)S(1)} %get-tuple-element.54), channel_id=1, source_target_pairs={{0,8},{4,12},{8,0},{12,4},{1,9},{5,13},{9,1},{13,5},{2,10},{6,14},... | collective-permute-start | bytes 245768 | tf_op jit(solution)/shard_map/ppermute | solution.py:113
  35.4 4.0 %collective-permute-start.11 = (bf16[8,2048]{1,0:T(8,128)(2,1)S(1)}, bf16[8,2048]{1,0:T(8,128)(2,1)S(1)}, u32[]{:S(2)}, u32[]{:S(2)}) collective-permute-start(bf16[8,2048]{1,0:T(8,128)(2,1)S(1)} %bitcast.95), channel_id=1, source_target_pairs={{0,12},{4,0},{8,4},{12,8},{1,13},{5,1},{9,5},{13,9},{2,14},{6,2},{... | collective-permute-start | bytes 98312 | tf_op jit(solution)/shard_map/ppermute | solution.py:97
  37.3 4.9 %collective-permute-start.10 = (bf16[8,2048]{1,0:T(8,128)(2,1)S(1)}, bf16[8,2048]{1,0:T(8,128)(2,1)S(1)}, u32[]{:S(2)}, u32[]{:S(2)}) collective-permute-start(bf16[8,2048]{1,0:T(8,128)(2,1)S(1)} %bitcast.96), channel_id=1, source_target_pairs={{0,8},{4,12},{8,0},{12,4},{1,9},{5,13},{9,1},{13,5},{2,10},{6,14},... | collective-permute-start | bytes 98312 | tf_op jit(solution)/shard_map/ppermute | solution.py:97
  37.3 5.7 %collective-permute-start.9 = (bf16[8,2048]{1,0:T(8,128)(2,1)S(1)}, bf16[8,2048]{1,0:T(8,128)(2,1)S(1)}, u32[]{:S(2)}, u32[]{:S(2)}) collective-permute-start(bf16[8,2048]{1,0:T(8,128)(2,1)S(1)} %bitcast.97), channel_id=1, source_target_pairs={{0,4},{4,8},{8,12},{12,0},{1,5},{5,9},{9,13},{13,1},{2,6},{6,10},{... | collective-permute-start | bytes 98312 | tf_op jit(solution)/shard_map/ppermute | solution.py:97
  48.7 1.4 %collective-permute-start.12 = (f32[2,8,2048]{2,1,0:T(8,128)S(1)}, f32[2,8,2048]{2,1,0:T(8,128)S(1)}, u32[]{:S(2)}, u32[]{:S(2)}) collective-permute-start(f32[2,8,2048]{2,1,0:T(8,128)S(1)} %select_bitcast_fusion.1), channel_id=1, source_target_pairs={{0,1},{1,0},{2,3},{3,2},{4,5},{5,4},{6,7},{7,6},{8,9},{9,8},{10,11... | collective-permute-start | bytes 393224 | tf_op jit(solution)/shard_map/ppermute | solution.py:113
  50.2 4.3 %collective-permute-start.13 = (f32[8,2048]{1,0:T(8,128)S(1)}, f32[8,2048]{1,0:T(8,128)S(1)}, u32[]{:S(2)}, u32[]{:S(2)}) collective-permute-start(f32[8,2048]{1,0:T(8,128)S(1)} %select_bitcast_fusion.6), channel_id=1, source_target_pairs={{0,2},{2,0},{1,3},{3,1},{4,6},{6,4},{5,7},{7,5},{8,10},{10,8},{9,1... | collective-permute-start | bytes 196616 | tf_op jit(solution)/shard_map/ppermute | solution.py:113
  54.6 3.6 %collective-permute-start.16 = (f32[8]{0:T(128)S(1)}, f32[8]{0:T(128)S(1)}, u32[]{:S(2)}, u32[]{:S(2)}) collective-permute-start(f32[8]{0:T(128)S(1)} %get-tuple-element.46), channel_id=1, source_target_pairs={{0,12},{4,0},{8,4},{12,8},{1,13},{5,1},{9,5},{13,9},{2,14},{6,2},{... | collective-permute-start | bytes 104 | tf_op jit(solution)/shard_map/ppermute | solution.py:128
  55.5 4.4 %collective-permute-start.15 = (f32[8]{0:T(128)S(1)}, f32[8]{0:T(128)S(1)}, u32[]{:S(2)}, u32[]{:S(2)}) collective-permute-start(f32[8]{0:T(128)S(1)} %get-tuple-element.46), channel_id=1, source_target_pairs={{0,8},{4,12},{8,0},{12,4},{1,9},{5,13},{9,1},{13,5},{2,10},{6,14},... | collective-permute-start | bytes 104 | tf_op jit(solution)/shard_map/ppermute | solution.py:128
  55.9 5.3 %collective-permute-start.14 = (f32[8]{0:T(128)S(1)}, f32[8]{0:T(128)S(1)}, u32[]{:S(2)}, u32[]{:S(2)}) collective-permute-start(f32[8]{0:T(128)S(1)} %get-tuple-element.46), channel_id=1, source_target_pairs={{0,4},{4,8},{8,12},{12,0},{1,5},{5,9},{9,13},{13,1},{2,6},{6,10},{... | collective-permute-start | bytes 104 | tf_op jit(solution)/shard_map/ppermute | solution.py:128
  61.3 1.6 %collective-permute-start.19 = (bf16[8,2048]{1,0:T(8,128)(2,1)S(1)}, bf16[8,2048]{1,0:T(8,128)(2,1)S(1)}, u32[]{:S(2)}, u32[]{:S(2)}) collective-permute-start(bf16[8,2048]{1,0:T(8,128)(2,1)S(1)} %multiply_convert_fusion), channel_id=1, source_target_pairs={{0,3},{1,0},{2,1},{3,2},{4,7},{5,4},{6,5},{7,6},{8,11},{9,8},{10,9... | collective-permute-start | bytes 98312 | tf_op jit(solution)/shard_map/ppermute | solution.py:97
  61.4 4.0 %collective-permute-start.18 = (bf16[8,2048]{1,0:T(8,128)(2,1)S(1)}, bf16[8,2048]{1,0:T(8,128)(2,1)S(1)}, u32[]{:S(2)}, u32[]{:S(2)}) collective-permute-start(bf16[8,2048]{1,0:T(8,128)(2,1)S(1)} %multiply_convert_fusion), channel_id=1, source_target_pairs={{0,2},{1,3},{2,0},{3,1},{4,6},{5,7},{6,4},{7,5},{8,10},{9,11},{10,... | collective-permute-start | bytes 98312 | tf_op jit(solution)/shard_map/ppermute | solution.py:97
  62.3 3.4 %collective-permute-start.17 = (bf16[8,2048]{1,0:T(8,128)(2,1)S(1)}, bf16[8,2048]{1,0:T(8,128)(2,1)S(1)}, u32[]{:S(2)}, u32[]{:S(2)}) collective-permute-start(bf16[8,2048]{1,0:T(8,128)(2,1)S(1)} %multiply_convert_fusion), channel_id=1, source_target_pairs={{0,1},{1,2},{2,3},{3,0},{4,5},{5,6},{6,7},{7,4},{8,9},{9,10},{10,1... | collective-permute-start | bytes 98312 | tf_op jit(solution)/shard_map/ppermute | solution.py:97
  69.2 33.1 %slice-start = ((s8[14680064]{0:T(1024)(128)(4,1)}), s8[4194304]{0:T(1024)(128)(4,1)S(1)}, s32[]{:S(2)}) async-start(s8[14680064]{0:T(1024)(128)(4,1)} %bitcast.80), calls=%async_computation | async-start | bytes 8388608
  72.1 30.1 %slice-start.1 = ((s8[14680064]{0:T(1024)(128)(4,1)}), s8[4194304]{0:T(1024)(128)(4,1)S(1)}, s32[]{:S(2)}) async-start(s8[14680064]{0:T(1024)(128)(4,1)} %bitcast.80), calls=%async_computation.1 | async-start | bytes 8388608
  77.9 24.4 %slice-start.2 = ((s8[14680064]{0:T(1024)(128)(4,1)}), s8[4194304]{0:T(1024)(128)(4,1)S(1)}, s32[]{:S(2)}) async-start(s8[14680064]{0:T(1024)(128)(4,1)} %bitcast.80), calls=%async_computation.2 | async-start | bytes 8388608
  86.6 5.8 %collective-permute-start.22 = (bf16[32,1792]{1,0:T(8,128)(2,1)S(1)}, bf16[32,1792]{1,0:T(8,128)(2,1)S(1)}, u32[]{:S(2)}, u32[]{:S(2)}) collective-permute-start(bf16[32,1792]{1,0:T(8,128)(2,1)S(1)} %pad_maximum_fusion.5), channel_id=1, source_target_pairs={{0,12},{4,0},{8,4},{12,8},{1,13},{5,1},{9,5},{13,9},{2,14},{6,2},{... | collective-permute-start | bytes 344072 | tf_op jit(solution)/shard_map/ppermute | solution.py:149
  88.1 10.4 %collective-permute-start.21 = (bf16[32,1792]{1,0:T(8,128)(2,1)S(1)}, bf16[32,1792]{1,0:T(8,128)(2,1)S(1)}, u32[]{:S(2)}, u32[]{:S(2)}) collective-permute-start(bf16[32,1792]{1,0:T(8,128)(2,1)S(1)} %pad_maximum_fusion.4), channel_id=1, source_target_pairs={{0,8},{4,12},{8,0},{12,4},{1,9},{5,13},{9,1},{13,5},{2,10},{6,14},... | collective-permute-start | bytes 344072 | tf_op jit(solution)/shard_map/ppermute | solution.py:149
  88.4 10.1 %collective-permute-start.20 = (bf16[32,1792]{1,0:T(8,128)(2,1)S(1)}, bf16[32,1792]{1,0:T(8,128)(2,1)S(1)}, u32[]{:S(2)}, u32[]{:S(2)}) collective-permute-start(bf16[32,1792]{1,0:T(8,128)(2,1)S(1)} %pad_maximum_fusion.3), channel_id=1, source_target_pairs={{0,4},{4,8},{8,12},{12,0},{1,5},{5,9},{9,13},{13,1},{2,6},{6,10},{... | collective-permute-start | bytes 344072 | tf_op jit(solution)/shard_map/ppermute | solution.py:149
  98.6 7.6 %collective-permute-start.25 = (bf16[32,896]{1,0:T(8,128)(2,1)S(1)}, bf16[32,896]{1,0:T(8,128)(2,1)S(1)}, u32[]{:S(2)}, u32[]{:S(2)}) collective-permute-start(bf16[32,896]{1,0:T(8,128)(2,1)S(1)} %fusion.70), channel_id=1, source_target_pairs={{0,12},{4,0},{8,4},{12,8},{1,13},{5,1},{9,5},{13,9},{2,14},{6,2},{... | collective-permute-start | bytes 172040 | tf_op jit(solution)/shard_map/ppermute | solution.py:162
  99.1 6.3 %collective-permute-start.24 = (bf16[32,896]{1,0:T(8,128)(2,1)S(1)}, bf16[32,896]{1,0:T(8,128)(2,1)S(1)}, u32[]{:S(2)}, u32[]{:S(2)}) collective-permute-start(bf16[32,896]{1,0:T(8,128)(2,1)S(1)} %fusion.70), channel_id=1, source_target_pairs={{0,8},{4,12},{8,0},{12,4},{1,9},{5,13},{9,1},{13,5},{2,10},{6,14},... | collective-permute-start | bytes 172040 | tf_op jit(solution)/shard_map/ppermute | solution.py:162
  100.3 6.6 %collective-permute-start.23 = (bf16[32,896]{1,0:T(8,128)(2,1)S(1)}, bf16[32,896]{1,0:T(8,128)(2,1)S(1)}, u32[]{:S(2)}, u32[]{:S(2)}) collective-permute-start(bf16[32,896]{1,0:T(8,128)(2,1)S(1)} %fusion.70), channel_id=1, source_target_pairs={{0,4},{4,8},{8,12},{12,0},{1,5},{5,9},{9,13},{13,1},{2,6},{6,10},{... | collective-permute-start | bytes 172040 | tf_op jit(solution)/shard_map/ppermute | solution.py:162
  107.8 1.4 %collective-permute-start.26 = (f32[2,8,2048]{2,1,0:T(8,128)S(1)}, f32[2,8,2048]{2,1,0:T(8,128)S(1)}, u32[]{:S(2)}, u32[]{:S(2)}) collective-permute-start(f32[2,8,2048]{2,1,0:T(8,128)S(1)} %select_bitcast_fusion), channel_id=1, source_target_pairs={{0,1},{1,0},{2,3},{3,2},{4,5},{5,4},{6,7},{7,6},{8,9},{9,8},{10,11... | collective-permute-start | bytes 393224 | tf_op jit(solution)/shard_map/ppermute | solution.py:113
  109.3 4.3 %collective-permute-start.27 = (f32[8,2048]{1,0:T(8,128)S(1)}, f32[8,2048]{1,0:T(8,128)S(1)}, u32[]{:S(2)}, u32[]{:S(2)}) collective-permute-start(f32[8,2048]{1,0:T(8,128)S(1)} %select_bitcast_fusion.5), channel_id=1, source_target_pairs={{0,2},{2,0},{1,3},{3,1},{4,6},{6,4},{5,7},{7,5},{8,10},{10,8},{9,1... | collective-permute-start | bytes 196616 | tf_op jit(solution)/shard_map/ppermute | solution.py:113
  (3 other events, 47.1 us)

commit v10 on v9

--- a/solution.py
+++ b/solution.py
@@ -198,11 +198,18 @@
         jnp.bfloat16
     )
     by_slot = gather_rows(normed, CS, n_cs, row_of_slot)
-    qkv_part = jnp.einsum(
-        "rf,fgc->rgc", by_slot, w_qkv, preferred_element_type=jnp.float32
-    ).reshape(rows_total, -1)
-    qkv_part, kv_cache = lax.optimization_barrier((qkv_part, kv_cache))
-    summed = scatter_sum(qkv_part.reshape(n_pool, per_owner, -1), "pool", n_pool)
+    cut = w_qkv.shape[2] // 2
+    sums = []
+    for cols in (slice(0, cut), slice(cut, w_qkv.shape[2])):
+        qkv_part = jnp.einsum(
+            "rf,fgc->rgc", by_slot, w_qkv[:, :, cols], preferred_element_type=jnp.float32
+        )
+        if not sums:
+            qkv_part, kv_cache = lax.optimization_barrier((qkv_part, kv_cache))
+        sums.append(
+            scatter_sum(qkv_part.reshape((n_pool, per_owner) + qkv_part.shape[1:]), "pool", n_pool)
+        )
+    summed = jnp.concatenate(sums, axis=2).reshape(per_owner, -1)
     rotated = rope_rows(summed, positions, per_group, HD)
     attended = attend(rotated, kv_cache, positions, per_group, HD)
     by_row = gather_rows(attended, "pool", n_pool, slot_of_row)

time: 115 us -> 121 us (1.052)
  local copies, waits for them, and re-layouts: 2.6 us -> 13 us
  waiting for transfers between devices: 40.4 us -> 33 us
  starting transfers between devices: 27.2 us -> 32.8 us
  matrix products: 37.8 us -> 36.4 us
    slice x0 -> x1, local copies, waits for them, and re-layouts: none -> 10.1 us  [local(): w_qkv[:, :, cols]]
    ppermute x7 -> x10, starting transfers between devices: 5.92 us -> 10.6 us  [scatter_sum(): lax.ppermute(piece, axis, shift_pairs(n, k)).astype(jnp.float32)]
    ppermute x3, waiting for transfers between devices: 6.05 us -> 2.25 us  [scatter_matmul(): lax.ppermute(block((idx + k) % n), axis, shift_pairs(n, k))]
    ppermute x9, waiting for transfers between devices: 11.3 us -> 10 us  [gather_rows(): got = [x] + [lax.ppermute(x, axis, shift_pairs(n, k)) for k in range(1, n)]]
    dot_general x1 -> x2, matrix products: 5.94 us -> 4.74 us  [local(): jnp.einsum('rf,fgc->rgc', by_slot, w_qkv[:, :, cols], preferred_element_t...]
    ppermute x7 -> x10, waiting for transfers between devices: 15 us -> 14.5 us  [scatter_sum(): lax.ppermute(piece, axis, shift_pairs(n, k)).astype(jnp.float32)]
  transfers between devices with their start and end apart: 28 -> 31, of which waited for: 21 -> 22; matrix products, arithmetic and copies ran while one was open for 7% -> 17% of each run, Pallas kernels for 0% -> 0%
where the time goes in v10:
time: 121 us
  matrix products  36.4 us (30%)
  waiting for transfers between devices  33 us (27%)
  starting transfers between devices  32.8 us (27%)
  local copies, waits for them, and re-layouts  13 us (11%)
  other arithmetic  4.71 us (4%)
    dot_general x8, matrix products, block(): jnp.dot(x, lax.dynamic_slice_in_dim(w, j * chunk, chunk, 1), preferred_el...  22.8 us
    ppermute x10, waiting for transfers between devices, scatter_sum(): lax.ppermute(piece, axis, shift_pairs(n, k)).astype(jnp.float32)  14.5 us
    ppermute x10, starting transfers between devices, scatter_sum(): lax.ppermute(piece, axis, shift_pairs(n, k)).astype(jnp.float32)  10.6 us
    slice x1, local copies, waits for them, and re-layouts, local(): w_qkv[:, :, cols]  10.1 us
    ppermute x9, waiting for transfers between devices, gather_rows(): got = [x] + [lax.ppermute(x, axis, shift_pairs(n, k)) for k in range(1, n)]  10 us
    ppermute x6, starting transfers between devices, all_sum(): total = total + lax.ppermute(x, axis, shift_pairs(n, k))  8.67 us
    ppermute x9, starting transfers between devices, gather_rows(): got = [x] + [lax.ppermute(x, axis, shift_pairs(n, k)) for k in range(1, n)]  6.12 us
    dot_general x1, matrix products, local(): out_part = jnp.dot(by_row, w_out, preferred_element_type=jnp.float32)  4.98 us
  transfers between devices with their start and end apart: 31, of which 22 were waited for; matrix products, arithmetic and copies ran while one was open for 17% of the time, Pallas kernels for 0%

profile of v10, /device:TPU:0, one launch (start us, length us, event | category | flops | bytes accessed | tf_op | source)
XLA Modules:
  0.0 120.6 jit_solution(17624276322449327683)
XLA Ops:
  0.9 5.1 %collective-permute-start.2 = (f32[8]{0:T(128)S(1)}, f32[8]{0:T(128)S(1)}, u32[]{:S(2)}, u32[]{:S(2)}) collective-permute-start(f32[8]{0:T(128)S(1)} %fusion.73), channel_id=1, source_target_pairs={{0,12},{4,0},{8,4},{12,8},{1,13},{5,1},{9,5},{13,9},{2,14},{6,2},{... | collective-permute-start | bytes 104 | tf_op jit(solution)/shard_map/ppermute | solution.py:128
  9.0 10.1 %fusion.129 = (bf16[2048,2,640]{2,1,0:T(2,128)(2,1)}, bf16[2048,2,640]{2,1,0:T(2,128)(2,1)}) fusion(bf16[2048,2,1280]{2,1,0:T(2,128)(2,1)} %param.22), kind=kLoop, calls=%fused_computation.203 | loop fusion | bytes 20971520 | tf_op jit(solution)/shard_map/slice | solution.py:205
  19.5 1.5 %collective-permute-start.4 = (bf16[8,2048]{1,0:T(8,128)(2,1)S(1)}, bf16[8,2048]{1,0:T(8,128)(2,1)S(1)}, u32[]{:S(2)}, u32[]{:S(2)}) collective-permute-start(bf16[8,2048]{1,0:T(8,128)(2,1)S(1)} %fusion.75), channel_id=1, source_target_pairs={{0,2},{1,3},{2,0},{3,1},{4,6},{5,7},{6,4},{7,5},{8,10},{9,11},{10,... | collective-permute-start | bytes 98312 | tf_op jit(solution)/shard_map/ppermute | solution.py:97
  21.1 2.3 %collective-permute-done.4 = bf16[8,2048]{1,0:T(8,128)(2,1)S(1)} collective-permute-done((bf16[8,2048]{1,0:T(8,128)(2,1)S(1)}, bf16[8,2048]{1,0:T(8,128)(2,1)S(1)}, u32[]{:S(2)}, u32[]{:S(2)}) %collective-permute-start.4) | collective-permute-done | bytes 32800 | tf_op jit(solution)/shard_map/ppermute | solution.py:97
  25.0 3.7 %fusion.2 = f32[32,2,640]{2,0,1:T(8,128)S(1)} fusion(bf16[2048,2,640]{2,1,0:T(2,128)(2,1)} %get-tuple-element.53, bf16[32,2048]{1,0:T(8,128)(2,1)S(1)} %gather_fusion, pred[32]{0:T(512)(128)(4,1)S(1)} %get-tuple-element.50), kind=kOutput, calls=%fused_computation.5 | convolution fusion | flops 167837696 | bytes 5537824 | tf_op jit(solution)/shard_map/rf,fgc->rgc/dot_general | solution.py:204
  30.1 2.9 %collective-permute-start.11 = (f32[8,2,640]{2,0,1:T(8,128)S(1)}, f32[8,2,640]{2,0,1:T(8,128)S(1)}, u32[]{:S(2)}, u32[]{:S(2)}) collective-permute-start(f32[8,2,640]{2,0,1:T(8,128)S(1)} %get-tuple-element.58), channel_id=1, source_target_pairs={{0,12},{4,0},{8,4},{12,8},{1,13},{5,1},{9,5},{13,9},{2,14},{6,2},{... | collective-permute-start | bytes 122888 | tf_op jit(solution)/shard_map/ppermute | solution.py:113
  34.6 3.9 %collective-permute-start.8 = (f32[8,2,640]{2,0,1:T(8,128)S(1)}, f32[8,2,640]{2,0,1:T(8,128)S(1)}, u32[]{:S(2)}, u32[]{:S(2)}) collective-permute-start(f32[8,2,640]{2,0,1:T(8,128)S(1)} %select_bitcast_fusion.4), channel_id=1, source_target_pairs={{0,12},{4,0},{8,4},{12,8},{1,13},{5,1},{9,5},{13,9},{2,14},{6,2},{... | collective-permute-start | bytes 122888 | tf_op jit(solution)/shard_map/ppermute | solution.py:113
  40.1 3.2 %collective-permute-done.7 = f32[8,2,640]{2,0,1:T(8,128)S(1)} collective-permute-done((f32[8,2,640]{2,0,1:T(8,128)S(1)}, f32[8,2,640]{2,0,1:T(8,128)S(1)}, u32[]{:S(2)}, u32[]{:S(2)}) %collective-permute-start.7) | collective-permute-done | bytes 40992 | tf_op jit(solution)/shard_map/ppermute | solution.py:113
  47.0 1.9 %collective-permute-start.12 = (bf16[8,2048]{1,0:T(8,128)(2,1)S(1)}, bf16[8,2048]{1,0:T(8,128)(2,1)S(1)}, u32[]{:S(2)}, u32[]{:S(2)}) collective-permute-start(bf16[8,2048]{1,0:T(8,128)(2,1)S(1)} %bitcast.154), channel_id=1, source_target_pairs={{0,4},{4,8},{8,12},{12,0},{1,5},{5,9},{9,13},{13,1},{2,6},{6,10},{... | collective-permute-start | bytes 98312 | tf_op jit(solution)/shard_map/ppermute | solution.py:97
  49.7 1.5 %collective-permute-done.13 = bf16[8,2048]{1,0:T(8,128)(2,1)S(1)} collective-permute-done((bf16[8,2048]{1,0:T(8,128)(2,1)S(1)}, bf16[8,2048]{1,0:T(8,128)(2,1)S(1)}, u32[]{:S(2)}, u32[]{:S(2)}) %collective-permute-start.13) | collective-permute-done | bytes 32800 | tf_op jit(solution)/shard_map/ppermute | solution.py:97
  51.2 1.5 %collective-permute-done.12 = bf16[8,2048]{1,0:T(8,128)(2,1)S(1)} collective-permute-done((bf16[8,2048]{1,0:T(8,128)(2,1)S(1)}, bf16[8,2048]{1,0:T(8,128)(2,1)S(1)}, u32[]{:S(2)}, u32[]{:S(2)}) %collective-permute-start.12) | collective-permute-done | bytes 32800 | tf_op jit(solution)/shard_map/ppermute | solution.py:97
  53.4 5.0 %fusion.68 = f32[32,2048]{1,0:T(8,128)S(1)} fusion(bf16[2048,2048]{1,0:T(8,128)(2,1)} %param.23, bf16[32,2048]{1,0:T(8,128)(2,1)S(1)} %gather_fusion.1, pred[32]{0:T(512)(128)(4,1)S(1)} %get-tuple-element.48), kind=kOutput, calls=%fused_computation.61 | convolution fusion | flops 268500992 | bytes 8781856 | tf_op jit(solution)/shard_map/dot_general | solution.py:216
  58.6 1.3 %collective-permute-done.15 = f32[2,8,2048]{2,1,0:T(8,128)S(1)} collective-permute-done((f32[2,8,2048]{2,1,0:T(8,128)S(1)}, f32[2,8,2048]{2,1,0:T(8,128)S(1)}, u32[]{:S(2)}, u32[]{:S(2)}) %collective-permute-start.15) | collective-permute-done | bytes 131104 | tf_op jit(solution)/shard_map/ppermute | solution.py:113
  60.9 3.4 %collective-permute-done.16 = f32[8,2048]{1,0:T(8,128)S(1)} collective-permute-done((f32[8,2048]{1,0:T(8,128)S(1)}, f32[8,2048]{1,0:T(8,128)S(1)}, u32[]{:S(2)}, u32[]{:S(2)}) %collective-permute-start.16) | collective-permute-done | bytes 65568 | tf_op jit(solution)/shard_map/ppermute | solution.py:113
  64.4 1.4 %collective-permute-start.19 = (f32[8]{0:T(128)S(1)}, f32[8]{0:T(128)S(1)}, u32[]{:S(2)}, u32[]{:S(2)}) collective-permute-start(f32[8]{0:T(128)S(1)} %get-tuple-element.46), channel_id=1, source_target_pairs={{0,12},{4,0},{8,4},{12,8},{1,13},{5,1},{9,5},{13,9},{2,14},{6,2},{... | collective-permute-start | bytes 104 | tf_op jit(solution)/shard_map/ppermute | solution.py:128
  68.0 2.3 %collective-permute-done.18 = f32[8]{0:T(128)S(1)} collective-permute-done((f32[8]{0:T(128)S(1)}, f32[8]{0:T(128)S(1)}, u32[]{:S(2)}, u32[]{:S(2)}) %collective-permute-start.18) | collective-permute-done | bytes 64 | tf_op jit(solution)/shard_map/ppermute | solution.py:128
  73.1 2.4 %collective-permute-done.21 = bf16[8,2048]{1,0:T(8,128)(2,1)S(1)} collective-permute-done((bf16[8,2048]{1,0:T(8,128)(2,1)S(1)}, bf16[8,2048]{1,0:T(8,128)(2,1)S(1)}, u32[]{:S(2)}, u32[]{:S(2)}) %collective-permute-start.21) | collective-permute-done | bytes 32800 | tf_op jit(solution)/shard_map/ppermute | solution.py:97
  76.5 2.8 %fusion.61 = bf16[32,896]{1,0:T(8,128)(2,1)S(1)} fusion(bf16[2048,3584]{1,0:T(8,128)(2,1)} %param.26, s32[]{:T(128)S(6)} %select_n.178, bf16[32,2048]{1,0:T(8,128)(2,1)S(1)} %gather_fusion.2, pred[32]{0:T(512)(128)(4,1)S(1)} %compare_and_fusion), kind=kOutput, calls=%fused_computation.43 | convolution fusion | flops 117534720 | bytes 3858468 | tf_op jit(solution)/shard_map/dot_general | solution.py:138
  79.3 2.9 %fusion.58 = bf16[32,896]{1,0:T(8,128)(2,1)S(1)} fusion(bf16[2048,3584]{1,0:T(8,128)(2,1)} %param.25, s32[]{:T(128)S(6)} %select_n.178, bf16[32,2048]{1,0:T(8,128)(2,1)S(1)} %gather_fusion.2, pred[32]{0:T(512)(128)(4,1)S(1)} %compare_and_fusion), kind=kOutput, calls=%fused_computation.42 | convolution fusion | flops 117534720 | bytes 3858468 | tf_op jit(solution)/shard_map/dot_general | solution.py:138
  82.3 2.9 %fusion.55 = bf16[32,896]{1,0:T(8,128)(2,1)S(1)} fusion(bf16[2048,3584]{1,0:T(8,128)(2,1)} %param.26, s32[]{:T(128)S(6)} %select_n.177, bf16[32,2048]{1,0:T(8,128)(2,1)S(1)} %gather_fusion.2, pred[32]{0:T(512)(128)(4,1)S(1)} %compare_and_fusion), kind=kOutput, calls=%fused_computation.41 | convolution fusion | flops 117534720 | bytes 3858468 | tf_op jit(solution)/shard_map/dot_general | solution.py:138
  85.2 2.8 %fusion.52 = bf16[32,896]{1,0:T(8,128)(2,1)S(1)} fusion(bf16[2048,3584]{1,0:T(8,128)(2,1)} %param.25, s32[]{:T(128)S(6)} %select_n.177, bf16[32,2048]{1,0:T(8,128)(2,1)S(1)} %gather_fusion.2, pred[32]{0:T(512)(128)(4,1)S(1)} %compare_and_fusion), kind=kOutput, calls=%fused_computation.40 | convolution fusion | flops 117534720 | bytes 3858468 | tf_op jit(solution)/shard_map/dot_general | solution.py:138
  88.0 2.9 %fusion.49 = bf16[32,896]{1,0:T(8,128)(2,1)S(1)} fusion(bf16[2048,3584]{1,0:T(8,128)(2,1)} %param.26, s32[]{:T(128)S(6)} %select_n.176, bf16[32,2048]{1,0:T(8,128)(2,1)S(1)} %gather_fusion.2, pred[32]{0:T(512)(128)(4,1)S(1)} %compare_and_fusion), kind=kOutput, calls=%fused_computation.39 | convolution fusion | flops 117534720 | bytes 3858468 | tf_op jit(solution)/shard_map/dot_general | solution.py:138
  91.0 2.8 %fusion.46 = bf16[32,896]{1,0:T(8,128)(2,1)S(1)} fusion(bf16[2048,3584]{1,0:T(8,128)(2,1)} %param.25, s32[]{:T(128)S(6)} %select_n.176, bf16[32,2048]{1,0:T(8,128)(2,1)S(1)} %gather_fusion.2, pred[32]{0:T(512)(128)(4,1)S(1)} %compare_and_fusion), kind=kOutput, calls=%fused_computation.38 | convolution fusion | flops 117534720 | bytes 3858468 | tf_op jit(solution)/shard_map/dot_general | solution.py:138
  95.0 2.2 %collective-permute-start.23 = (bf16[32,1792]{1,0:T(8,128)(2,1)S(1)}, bf16[32,1792]{1,0:T(8,128)(2,1)S(1)}, u32[]{:S(2)}, u32[]{:S(2)}) collective-permute-start(bf16[32,1792]{1,0:T(8,128)(2,1)S(1)} %pad_maximum_fusion.3), channel_id=1, source_target_pairs={{0,4},{4,8},{8,12},{12,0},{1,5},{5,9},{9,13},{13,1},{2,6},{6,10},{... | collective-permute-start | bytes 344072 | tf_op jit(solution)/shard_map/ppermute | solution.py:149
  97.1 2.8 %fusion.43 = bf16[32,896]{1,0:T(8,128)(2,1)S(1)} fusion(bf16[2048,3584]{1,0:T(8,128)(2,1)} %param.26, s32[]{:T(128)S(6)} %select_n.175, bf16[32,2048]{1,0:T(8,128)(2,1)S(1)} %gather_fusion.2, pred[32]{0:T(512)(128)(4,1)S(1)} %compare_and_fusion), kind=kOutput, calls=%fused_computation.37 | convolution fusion | flops 117534720 | bytes 3858468 | tf_op jit(solution)/shard_map/dot_general | solution.py:138
  99.9 2.8 %fusion.40 = bf16[32,896]{1,0:T(8,128)(2,1)S(1)} fusion(bf16[2048,3584]{1,0:T(8,128)(2,1)} %param.25, s32[]{:T(128)S(6)} %select_n.175, bf16[32,2048]{1,0:T(8,128)(2,1)S(1)} %gather_fusion.2, pred[32]{0:T(512)(128)(4,1)S(1)} %compare_and_fusion), kind=kOutput, calls=%fused_computation.36 | convolution fusion | flops 117534720 | bytes 3858468 | tf_op jit(solution)/shard_map/dot_general | solution.py:138
  102.8 2.2 %collective-permute-done.24 = bf16[32,1792]{1,0:T(8,128)(2,1)S(1)} collective-permute-done((bf16[32,1792]{1,0:T(8,128)(2,1)S(1)}, bf16[32,1792]{1,0:T(8,128)(2,1)S(1)}, u32[]{:S(2)}, u32[]{:S(2)}) %collective-permute-start.24) | collective-permute-done | bytes 114720 | tf_op jit(solution)/shard_map/ppermute | solution.py:149
  105.8 1.5 %collective-permute-start.27 = (bf16[32,896]{1,0:T(8,128)(2,1)S(1)}, bf16[32,896]{1,0:T(8,128)(2,1)S(1)}, u32[]{:S(2)}, u32[]{:S(2)}) collective-permute-start(bf16[32,896]{1,0:T(8,128)(2,1)S(1)} %fusion.71), channel_id=1, source_target_pairs={{0,8},{4,12},{8,0},{12,4},{1,9},{5,13},{9,1},{13,5},{2,10},{6,14},... | collective-permute-start | bytes 172040 | tf_op jit(solution)/shard_map/ppermute | solution.py:162
  107.4 1.9 %collective-permute-start.26 = (bf16[32,896]{1,0:T(8,128)(2,1)S(1)}, bf16[32,896]{1,0:T(8,128)(2,1)S(1)}, u32[]{:S(2)}, u32[]{:S(2)}) collective-permute-start(bf16[32,896]{1,0:T(8,128)(2,1)S(1)} %fusion.71), channel_id=1, source_target_pairs={{0,4},{4,8},{8,12},{12,0},{1,5},{5,9},{9,13},{13,1},{2,6},{6,10},{... | collective-permute-start | bytes 172040 | tf_op jit(solution)/shard_map/ppermute | solution.py:162
  110.8 1.7 %collective-permute-done.27 = bf16[32,896]{1,0:T(8,128)(2,1)S(1)} collective-permute-done((bf16[32,896]{1,0:T(8,128)(2,1)S(1)}, bf16[32,896]{1,0:T(8,128)(2,1)S(1)}, u32[]{:S(2)}, u32[]{:S(2)}) %collective-permute-start.27) | collective-permute-done | bytes 57376 | tf_op jit(solution)/shard_map/ppermute | solution.py:162
  114.2 1.3 %collective-permute-done.29 = f32[2,8,2048]{2,1,0:T(8,128)S(1)} collective-permute-done((f32[2,8,2048]{2,1,0:T(8,128)S(1)}, f32[2,8,2048]{2,1,0:T(8,128)S(1)}, u32[]{:S(2)}, u32[]{:S(2)}) %collective-permute-start.29) | collective-permute-done | bytes 131104 | tf_op jit(solution)/shard_map/ppermute | solution.py:113
  116.6 3.4 %collective-permute-done.30 = f32[8,2048]{1,0:T(8,128)S(1)} collective-permute-done((f32[8,2048]{1,0:T(8,128)S(1)}, f32[8,2048]{1,0:T(8,128)S(1)}, u32[]{:S(2)}, u32[]{:S(2)}) %collective-permute-start.30) | collective-permute-done | bytes 65568 | tf_op jit(solution)/shard_map/ppermute | solution.py:113
  (127 shorter events, 29.5 us)
Async XLA Ops:
  0.9 18.3 %collective-permute-start.2 = (f32[8]{0:T(128)S(1)}, f32[8]{0:T(128)S(1)}, u32[]{:S(2)}, u32[]{:S(2)}) collective-permute-start(f32[8]{0:T(128)S(1)} %fusion.73), channel_id=1, source_target_pairs={{0,12},{4,0},{8,4},{12,8},{1,13},{5,1},{9,5},{13,9},{2,14},{6,2},{... | collective-permute-start | bytes 104 | tf_op jit(solution)/shard_map/ppermute | solution.py:128
  6.0 13.2 %collective-permute-start.1 = (f32[8]{0:T(128)S(1)}, f32[8]{0:T(128)S(1)}, u32[]{:S(2)}, u32[]{:S(2)}) collective-permute-start(f32[8]{0:T(128)S(1)} %fusion.73), channel_id=1, source_target_pairs={{0,8},{4,12},{8,0},{12,4},{1,9},{5,13},{9,1},{13,5},{2,10},{6,14},... | collective-permute-start | bytes 104 | tf_op jit(solution)/shard_map/ppermute | solution.py:128
  6.0 13.2 %collective-permute-start = (f32[8]{0:T(128)S(1)}, f32[8]{0:T(128)S(1)}, u32[]{:S(2)}, u32[]{:S(2)}) collective-permute-start(f32[8]{0:T(128)S(1)} %fusion.73), channel_id=1, source_target_pairs={{0,4},{4,8},{8,12},{12,0},{1,5},{5,9},{9,13},{13,1},{2,6},{6,10},{... | collective-permute-start | bytes 104 | tf_op jit(solution)/shard_map/ppermute | solution.py:128
  19.3 1.8 %collective-permute-start.5 = (bf16[8,2048]{1,0:T(8,128)(2,1)S(1)}, bf16[8,2048]{1,0:T(8,128)(2,1)S(1)}, u32[]{:S(2)}, u32[]{:S(2)}) collective-permute-start(bf16[8,2048]{1,0:T(8,128)(2,1)S(1)} %fusion.75), channel_id=1, source_target_pairs={{0,3},{1,0},{2,1},{3,2},{4,7},{5,4},{6,5},{7,6},{8,11},{9,8},{10,9... | collective-permute-start | bytes 98312 | tf_op jit(solution)/shard_map/ppermute | solution.py:97
  19.5 4.0 %collective-permute-start.4 = (bf16[8,2048]{1,0:T(8,128)(2,1)S(1)}, bf16[8,2048]{1,0:T(8,128)(2,1)S(1)}, u32[]{:S(2)}, u32[]{:S(2)}) collective-permute-start(bf16[8,2048]{1,0:T(8,128)(2,1)S(1)} %fusion.75), channel_id=1, source_target_pairs={{0,2},{1,3},{2,0},{3,1},{4,6},{5,7},{6,4},{7,5},{8,10},{9,11},{10,... | collective-permute-start | bytes 98312 | tf_op jit(solution)/shard_map/ppermute | solution.py:97
  20.9 3.3 %collective-permute-start.3 = (bf16[8,2048]{1,0:T(8,128)(2,1)S(1)}, bf16[8,2048]{1,0:T(8,128)(2,1)S(1)}, u32[]{:S(2)}, u32[]{:S(2)}) collective-permute-start(bf16[8,2048]{1,0:T(8,128)(2,1)S(1)} %fusion.75), channel_id=1, source_target_pairs={{0,1},{1,2},{2,3},{3,0},{4,5},{5,6},{6,7},{7,4},{8,9},{9,10},{10,1... | collective-permute-start | bytes 98312 | tf_op jit(solution)/shard_map/ppermute | solution.py:97
  30.1 8.4 %collective-permute-start.11 = (f32[8,2,640]{2,0,1:T(8,128)S(1)}, f32[8,2,640]{2,0,1:T(8,128)S(1)}, u32[]{:S(2)}, u32[]{:S(2)}) collective-permute-start(f32[8,2,640]{2,0,1:T(8,128)S(1)} %get-tuple-element.58), channel_id=1, source_target_pairs={{0,12},{4,0},{8,4},{12,8},{1,13},{5,1},{9,5},{13,9},{2,14},{6,2},{... | collective-permute-start | bytes 122888 | tf_op jit(solution)/shard_map/ppermute | solution.py:113
  32.9 6.2 %collective-permute-start.10 = (f32[8,2,640]{2,0,1:T(8,128)S(1)}, f32[8,2,640]{2,0,1:T(8,128)S(1)}, u32[]{:S(2)}, u32[]{:S(2)}) collective-permute-start(f32[8,2,640]{2,0,1:T(8,128)S(1)} %get-tuple-element.57), channel_id=1, source_target_pairs={{0,8},{4,12},{8,0},{12,4},{1,9},{5,13},{9,1},{13,5},{2,10},{6,14},... | collective-permute-start | bytes 122888 | tf_op jit(solution)/shard_map/ppermute | solution.py:113
  34.0 5.8 %collective-permute-start.9 = (f32[8,2,640]{2,0,1:T(8,128)S(1)}, f32[8,2,640]{2,0,1:T(8,128)S(1)}, u32[]{:S(2)}, u32[]{:S(2)}) collective-permute-start(f32[8,2,640]{2,0,1:T(8,128)S(1)} %get-tuple-element.56), channel_id=1, source_target_pairs={{0,4},{4,8},{8,12},{12,0},{1,5},{5,9},{9,13},{13,1},{2,6},{6,10},{... | collective-permute-start | bytes 122888 | tf_op jit(solution)/shard_map/ppermute | solution.py:113
  34.6 5.5 %collective-permute-start.8 = (f32[8,2,640]{2,0,1:T(8,128)S(1)}, f32[8,2,640]{2,0,1:T(8,128)S(1)}, u32[]{:S(2)}, u32[]{:S(2)}) collective-permute-start(f32[8,2,640]{2,0,1:T(8,128)S(1)} %select_bitcast_fusion.4), channel_id=1, source_target_pairs={{0,12},{4,0},{8,4},{12,8},{1,13},{5,1},{9,5},{13,9},{2,14},{6,2},{... | collective-permute-start | bytes 122888 | tf_op jit(solution)/shard_map/ppermute | solution.py:113
  38.5 4.9 %collective-permute-start.7 = (f32[8,2,640]{2,0,1:T(8,128)S(1)}, f32[8,2,640]{2,0,1:T(8,128)S(1)}, u32[]{:S(2)}, u32[]{:S(2)}) collective-permute-start(f32[8,2,640]{2,0,1:T(8,128)S(1)} %get-tuple-element.55), channel_id=1, source_target_pairs={{0,8},{4,12},{8,0},{12,4},{1,9},{5,13},{9,1},{13,5},{2,10},{6,14},... | collective-permute-start | bytes 122888 | tf_op jit(solution)/shard_map/ppermute | solution.py:113
  38.5 5.8 %collective-permute-start.6 = (f32[8,2,640]{2,0,1:T(8,128)S(1)}, f32[8,2,640]{2,0,1:T(8,128)S(1)}, u32[]{:S(2)}, u32[]{:S(2)}) collective-permute-start(f32[8,2,640]{2,0,1:T(8,128)S(1)} %get-tuple-element.54), channel_id=1, source_target_pairs={{0,4},{4,8},{8,12},{12,0},{1,5},{5,9},{9,13},{13,1},{2,6},{6,10},{... | collective-permute-start | bytes 122888 | tf_op jit(solution)/shard_map/ppermute | solution.py:113
  45.8 4.0 %collective-permute-start.14 = (bf16[8,2048]{1,0:T(8,128)(2,1)S(1)}, bf16[8,2048]{1,0:T(8,128)(2,1)S(1)}, u32[]{:S(2)}, u32[]{:S(2)}) collective-permute-start(bf16[8,2048]{1,0:T(8,128)(2,1)S(1)} %bitcast.152), channel_id=1, source_target_pairs={{0,12},{4,0},{8,4},{12,8},{1,13},{5,1},{9,5},{13,9},{2,14},{6,2},{... | collective-permute-start | bytes 98312 | tf_op jit(solution)/shard_map/ppermute | solution.py:97
  46.4 4.8 %collective-permute-start.13 = (bf16[8,2048]{1,0:T(8,128)(2,1)S(1)}, bf16[8,2048]{1,0:T(8,128)(2,1)S(1)}, u32[]{:S(2)}, u32[]{:S(2)}) collective-permute-start(bf16[8,2048]{1,0:T(8,128)(2,1)S(1)} %bitcast.153), channel_id=1, source_target_pairs={{0,8},{4,12},{8,0},{12,4},{1,9},{5,13},{9,1},{13,5},{2,10},{6,14},... | collective-permute-start | bytes 98312 | tf_op jit(solution)/shard_map/ppermute | solution.py:97
  47.0 5.7 %collective-permute-start.12 = (bf16[8,2048]{1,0:T(8,128)(2,1)S(1)}, bf16[8,2048]{1,0:T(8,128)(2,1)S(1)}, u32[]{:S(2)}, u32[]{:S(2)}) collective-permute-start(bf16[8,2048]{1,0:T(8,128)(2,1)S(1)} %bitcast.154), channel_id=1, source_target_pairs={{0,4},{4,8},{8,12},{12,0},{1,5},{5,9},{9,13},{13,1},{2,6},{6,10},{... | collective-permute-start | bytes 98312 | tf_op jit(solution)/shard_map/ppermute | solution.py:97
  58.4 1.4 %collective-permute-start.15 = (f32[2,8,2048]{2,1,0:T(8,128)S(1)}, f32[2,8,2048]{2,1,0:T(8,128)S(1)}, u32[]{:S(2)}, u32[]{:S(2)}) collective-permute-start(f32[2,8,2048]{2,1,0:T(8,128)S(1)} %select_bitcast_fusion.1), channel_id=1, source_target_pairs={{0,1},{1,0},{2,3},{3,2},{4,5},{5,4},{6,7},{7,6},{8,9},{9,8},{10,11... | collective-permute-start | bytes 393224 | tf_op jit(solution)/shard_map/ppermute | solution.py:113
  59.9 4.3 %collective-permute-start.16 = (f32[8,2048]{1,0:T(8,128)S(1)}, f32[8,2048]{1,0:T(8,128)S(1)}, u32[]{:S(2)}, u32[]{:S(2)}) collective-permute-start(f32[8,2048]{1,0:T(8,128)S(1)} %select_bitcast_fusion.3), channel_id=1, source_target_pairs={{0,2},{2,0},{1,3},{3,1},{4,6},{6,4},{5,7},{7,5},{8,10},{10,8},{9,1... | collective-permute-start | bytes 196616 | tf_op jit(solution)/shard_map/ppermute | solution.py:113
  64.4 3.6 %collective-permute-start.19 = (f32[8]{0:T(128)S(1)}, f32[8]{0:T(128)S(1)}, u32[]{:S(2)}, u32[]{:S(2)}) collective-permute-start(f32[8]{0:T(128)S(1)} %get-tuple-element.46), channel_id=1, source_target_pairs={{0,12},{4,0},{8,4},{12,8},{1,13},{5,1},{9,5},{13,9},{2,14},{6,2},{... | collective-permute-start | bytes 104 | tf_op jit(solution)/shard_map/ppermute | solution.py:128
  65.8 4.4 %collective-permute-start.18 = (f32[8]{0:T(128)S(1)}, f32[8]{0:T(128)S(1)}, u32[]{:S(2)}, u32[]{:S(2)}) collective-permute-start(f32[8]{0:T(128)S(1)} %get-tuple-element.46), channel_id=1, source_target_pairs={{0,8},{4,12},{8,0},{12,4},{1,9},{5,13},{9,1},{13,5},{2,10},{6,14},... | collective-permute-start | bytes 104 | tf_op jit(solution)/shard_map/ppermute | solution.py:128
  66.0 5.3 %collective-permute-start.17 = (f32[8]{0:T(128)S(1)}, f32[8]{0:T(128)S(1)}, u32[]{:S(2)}, u32[]{:S(2)}) collective-permute-start(f32[8]{0:T(128)S(1)} %get-tuple-element.46), channel_id=1, source_target_pairs={{0,4},{4,8},{8,12},{12,0},{1,5},{5,9},{9,13},{13,1},{2,6},{6,10},{... | collective-permute-start | bytes 104 | tf_op jit(solution)/shard_map/ppermute | solution.py:128
  71.5 1.6 %collective-permute-start.22 = (bf16[8,2048]{1,0:T(8,128)(2,1)S(1)}, bf16[8,2048]{1,0:T(8,128)(2,1)S(1)}, u32[]{:S(2)}, u32[]{:S(2)}) collective-permute-start(bf16[8,2048]{1,0:T(8,128)(2,1)S(1)} %multiply_convert_fusion), channel_id=1, source_target_pairs={{0,3},{1,0},{2,1},{3,2},{4,7},{5,4},{6,5},{7,6},{8,11},{9,8},{10,9... | collective-permute-start | bytes 98312 | tf_op jit(solution)/shard_map/ppermute | solution.py:97
  71.5 4.0 %collective-permute-start.21 = (bf16[8,2048]{1,0:T(8,128)(2,1)S(1)}, bf16[8,2048]{1,0:T(8,128)(2,1)S(1)}, u32[]{:S(2)}, u32[]{:S(2)}) collective-permute-start(bf16[8,2048]{1,0:T(8,128)(2,1)S(1)} %multiply_convert_fusion), channel_id=1, source_target_pairs={{0,2},{1,3},{2,0},{3,1},{4,6},{5,7},{6,4},{7,5},{8,10},{9,11},{10,... | collective-permute-start | bytes 98312 | tf_op jit(solution)/shard_map/ppermute | solution.py:97
  72.5 3.4 %collective-permute-start.20 = (bf16[8,2048]{1,0:T(8,128)(2,1)S(1)}, bf16[8,2048]{1,0:T(8,128)(2,1)S(1)}, u32[]{:S(2)}, u32[]{:S(2)}) collective-permute-start(bf16[8,2048]{1,0:T(8,128)(2,1)S(1)} %multiply_convert_fusion), channel_id=1, source_target_pairs={{0,1},{1,2},{2,3},{3,0},{4,5},{5,6},{6,7},{7,4},{8,9},{9,10},{10,1... | collective-permute-start | bytes 98312 | tf_op jit(solution)/shard_map/ppermute | solution.py:97
  79.3 30.0 %slice-start = ((s8[14680064]{0:T(1024)(128)(4,1)}), s8[4194304]{0:T(1024)(128)(4,1)S(1)}, s32[]{:S(2)}) async-start(s8[14680064]{0:T(1024)(128)(4,1)} %bitcast.138), calls=%async_computation | async-start | bytes 8388608
  93.8 8.9 %collective-permute-start.25 = (bf16[32,1792]{1,0:T(8,128)(2,1)S(1)}, bf16[32,1792]{1,0:T(8,128)(2,1)S(1)}, u32[]{:S(2)}, u32[]{:S(2)}) collective-permute-start(bf16[32,1792]{1,0:T(8,128)(2,1)S(1)} %pad_maximum_fusion.5), channel_id=1, source_target_pairs={{0,12},{4,0},{8,4},{12,8},{1,13},{5,1},{9,5},{13,9},{2,14},{6,2},{... | collective-permute-start | bytes 344072 | tf_op jit(solution)/shard_map/ppermute | solution.py:149
  94.9 10.1 %collective-permute-start.24 = (bf16[32,1792]{1,0:T(8,128)(2,1)S(1)}, bf16[32,1792]{1,0:T(8,128)(2,1)S(1)}, u32[]{:S(2)}, u32[]{:S(2)}) collective-permute-start(bf16[32,1792]{1,0:T(8,128)(2,1)S(1)} %pad_maximum_fusion.4), channel_id=1, source_target_pairs={{0,8},{4,12},{8,0},{12,4},{1,9},{5,13},{9,1},{13,5},{2,10},{6,14},... | collective-permute-start | bytes 344072 | tf_op jit(solution)/shard_map/ppermute | solution.py:149
  95.0 10.0 %collective-permute-start.23 = (bf16[32,1792]{1,0:T(8,128)(2,1)S(1)}, bf16[32,1792]{1,0:T(8,128)(2,1)S(1)}, u32[]{:S(2)}, u32[]{:S(2)}) collective-permute-start(bf16[32,1792]{1,0:T(8,128)(2,1)S(1)} %pad_maximum_fusion.3), channel_id=1, source_target_pairs={{0,4},{4,8},{8,12},{12,0},{1,5},{5,9},{9,13},{13,1},{2,6},{6,10},{... | collective-permute-start | bytes 344072 | tf_op jit(solution)/shard_map/ppermute | solution.py:149
  105.1 5.0 %collective-permute-start.28 = (bf16[32,896]{1,0:T(8,128)(2,1)S(1)}, bf16[32,896]{1,0:T(8,128)(2,1)S(1)}, u32[]{:S(2)}, u32[]{:S(2)}) collective-permute-start(bf16[32,896]{1,0:T(8,128)(2,1)S(1)} %fusion.71), channel_id=1, source_target_pairs={{0,12},{4,0},{8,4},{12,8},{1,13},{5,1},{9,5},{13,9},{2,14},{6,2},{... | collective-permute-start | bytes 172040 | tf_op jit(solution)/shard_map/ppermute | solution.py:162
  105.8 6.7 %collective-permute-start.27 = (bf16[32,896]{1,0:T(8,128)(2,1)S(1)}, bf16[32,896]{1,0:T(8,128)(2,1)S(1)}, u32[]{:S(2)}, u32[]{:S(2)}) collective-permute-start(bf16[32,896]{1,0:T(8,128)(2,1)S(1)} %fusion.71), channel_id=1, source_target_pairs={{0,8},{4,12},{8,0},{12,4},{1,9},{5,13},{9,1},{13,5},{2,10},{6,14},... | collective-permute-start | bytes 172040 | tf_op jit(solution)/shard_map/ppermute | solution.py:162
  107.4 6.0 %collective-permute-start.26 = (bf16[32,896]{1,0:T(8,128)(2,1)S(1)}, bf16[32,896]{1,0:T(8,128)(2,1)S(1)}, u32[]{:S(2)}, u32[]{:S(2)}) collective-permute-start(bf16[32,896]{1,0:T(8,128)(2,1)S(1)} %fusion.71), channel_id=1, source_target_pairs={{0,4},{4,8},{8,12},{12,0},{1,5},{5,9},{9,13},{13,1},{2,6},{6,10},{... | collective-permute-start | bytes 172040 | tf_op jit(solution)/shard_map/ppermute | solution.py:162
  114.2 1.4 %collective-permute-start.29 = (f32[2,8,2048]{2,1,0:T(8,128)S(1)}, f32[2,8,2048]{2,1,0:T(8,128)S(1)}, u32[]{:S(2)}, u32[]{:S(2)}) collective-permute-start(f32[2,8,2048]{2,1,0:T(8,128)S(1)} %select_bitcast_fusion), channel_id=1, source_target_pairs={{0,1},{1,0},{2,3},{3,2},{4,5},{5,4},{6,7},{7,6},{8,9},{9,8},{10,11... | collective-permute-start | bytes 393224 | tf_op jit(solution)/shard_map/ppermute | solution.py:113
  115.6 4.3 %collective-permute-start.30 = (f32[8,2048]{1,0:T(8,128)S(1)}, f32[8,2048]{1,0:T(8,128)S(1)}, u32[]{:S(2)}, u32[]{:S(2)}) collective-permute-start(f32[8,2048]{1,0:T(8,128)S(1)} %select_bitcast_fusion.2), channel_id=1, source_target_pairs={{0,2},{2,0},{1,3},{3,1},{4,6},{6,4},{5,7},{7,5},{8,10},{10,8},{9,1... | collective-permute-start | bytes 196616 | tf_op jit(solution)/shard_map/ppermute | solution.py:113
  (8 other events, 114.5 us)

commit v11 on v9

--- a/solution.py
+++ b/solution.py
@@ -120,6 +120,18 @@
     shaped = blocks.reshape((n_col, n_side) + blocks.shape[1:])
     per_col = scatter_sum(jnp.swapaxes(shaped, 0, 1), "side", n_side)
     return scatter_sum(per_col, "col", n_col)
+
+
+def all_sum_cs(parts):
+    n_col = lax.axis_size("col")
+    n_side = lax.axis_size("side")
+    side = lax.axis_index("side")
+    mine = scatter_sum(parts.reshape((n_side, -1) + parts.shape[1:]), "side", n_side)
+    mine = all_sum(mine, "col", n_col)
+    got = [mine] + [lax.ppermute(mine, "side", shift_pairs(n_side, k)) for k in range(1, n_side)]
+    stacked = jnp.stack(got)
+    ordered = jnp.take(stacked, (side - jnp.arange(n_side)) % n_side, axis=0)
+    return ordered.reshape(parts.shape)
 
 
 def all_sum(x, axis, n):
@@ -207,13 +219,20 @@
     attended = attend(rotated, kv_cache, positions, per_group, HD)
     by_row = gather_rows(attended, "pool", n_pool, slot_of_row)
     out_part = jnp.dot(by_row, w_out, preferred_element_type=jnp.float32)
-    residual = residual + scatter_sum_cs(out_part.reshape(n_cs, rows_here, -1))
-
-    squares_mid = all_sum(jnp.sum(residual * residual, axis=1), "pool", n_pool)
-    ffn_normed = (
-        residual * lax.rsqrt(squares_mid / D + epsilon)[:, None] * ffn_gain[None, :]
+    cs_index = lax.axis_index(CS)
+    out_part = lax.dynamic_update_slice_in_dim(
+        out_part,
+        lax.dynamic_slice_in_dim(out_part, cs_index * rows_here, rows_here, 0) + residual,
+        cs_index * rows_here,
+        0,
+    )
+    resid_all = all_sum_cs(out_part)
+    residual = lax.dynamic_slice_in_dim(resid_all, cs_index * rows_here, rows_here, 0)
+
+    squares_mid = all_sum(jnp.sum(resid_all * resid_all, axis=1), "pool", n_pool)
+    ffn_all = (
+        resid_all * lax.rsqrt(squares_mid / D + epsilon)[:, None] * ffn_gain[None, :]
     ).astype(jnp.bfloat16)
-    ffn_all = gather_rows(ffn_normed, CS, n_cs, every)
     both = scatter_matmul(ffn_all, (w_gate, w_up), "pool", n_pool)
     chunk = w_gate.shape[1] // n_pool
     gate_total = both[:, :chunk]

time: 115 us -> 113 us (0.983)
  waiting for transfers between devices: 40.4 us -> 39 us
    ppermute x6 -> x7, waiting for transfers between devices: 5.64 us -> 10.3 us  [all_sum(): total = total + lax.ppermute(x, axis, shift_pairs(n, k))]
    ppermute x7 -> x6, waiting for transfers between devices: 15 us -> 11.6 us  [scatter_sum(): lax.ppermute(piece, axis, shift_pairs(n, k)).astype(jnp.float32)]
    ppermute x9 -> x6, waiting for transfers between devices: 11.3 us -> 8.23 us  [gather_rows(): got = [x] + [lax.ppermute(x, axis, shift_pairs(n, k)) for k in range(1, n)]]
    ppermute x3, waiting for transfers between devices: 6.05 us -> 3.94 us  [scatter_matmul(): lax.ppermute(block((idx + k) % n), axis, shift_pairs(n, k))]
    ppermute x3, waiting for transfers between devices: 2.42 us -> 3.89 us  [gather_matmul(): got = lax.ppermute(x, axis, shift_pairs(n, k))]
    ppermute x9 -> x6, starting transfers between devices: 5.39 us -> 4.25 us  [gather_rows(): got = [x] + [lax.ppermute(x, axis, shift_pairs(n, k)) for k in range(1, n)]]
    ppermute x7 -> x6, starting transfers between devices: 5.92 us -> 4.99 us  [scatter_sum(): lax.ppermute(piece, axis, shift_pairs(n, k)).astype(jnp.float32)]
    ppermute x6 -> x7, starting transfers between devices: 9.3 us -> 10.2 us  [all_sum(): total = total + lax.ppermute(x, axis, shift_pairs(n, k))]
  transfers between devices with their start and end apart: 28 -> 26, of which waited for: 21 -> 20; matrix products, arithmetic and copies ran while one was open for 7% -> 7% of each run, Pallas kernels for 0% -> 0%
where the time goes in v11:
time: 113 us; the launch traced here: 112 us
  waiting for transfers between devices  39 us (35%)
  matrix products  37.1 us (33%)
  starting transfers between devices  27.1 us (24%)
  other arithmetic  5.69 us (5%)
  local copies, waits for them, and re-layouts  2.73 us (2%)
    dot_general x8, matrix products, block(): jnp.dot(x, lax.dynamic_slice_in_dim(w, j * chunk, chunk, 1), preferred_el...  22.3 us
    ppermute x6, waiting for transfers between devices, scatter_sum(): lax.ppermute(piece, axis, shift_pairs(n, k)).astype(jnp.float32)  11.6 us
    ppermute x7, waiting for transfers between devices, all_sum(): total = total + lax.ppermute(x, axis, shift_pairs(n, k))  10.3 us
    ppermute x7, starting transfers between devices, all_sum(): total = total + lax.ppermute(x, axis, shift_pairs(n, k))  10.2 us
    ppermute x6, waiting for transfers between devices, gather_rows(): got = [x] + [lax.ppermute(x, axis, shift_pairs(n, k)) for k in range(1, n)]  8.23 us
    dot_general x1, matrix products, local(): jnp.einsum('rf,fgc->rgc', by_slot, w_qkv, preferred_element_type=jnp.floa...  5.94 us
    ppermute x6, starting transfers between devices, scatter_sum(): lax.ppermute(piece, axis, shift_pairs(n, k)).astype(jnp.float32)  4.99 us
    dot_general x1, matrix products, local(): out_part = jnp.dot(by_row, w_out, preferred_element_type=jnp.float32)  4.99 us
  transfers between devices with their start and end apart: 26, of which 20 were waited for; matrix products, arithmetic and copies ran while one was open for 7% of the time, Pallas kernels for 0%

profile of v11, /device:TPU:0, one launch (start us, length us, event | category | flops | bytes accessed | tf_op | source)
XLA Modules:
  0.0 112.2 jit_solution(1527038314561797655)
XLA Ops:
  1.0 5.1 %collective-permute-start.2 = (f32[8]{0:T(128)S(1)}, f32[8]{0:T(128)S(1)}, u32[]{:S(2)}, u32[]{:S(2)}) collective-permute-start(f32[8]{0:T(128)S(1)} %fusion.74), channel_id=1, source_target_pairs={{0,12},{4,0},{8,4},{12,8},{1,13},{5,1},{9,5},{13,9},{2,14},{6,2},{... | collective-permute-start | bytes 104 | tf_op jit(solution)/shard_map/ppermute | solution.py:140
  9.2 1.3 %collective-permute-done.1 = f32[8]{0:T(128)S(1)} collective-permute-done((f32[8]{0:T(128)S(1)}, f32[8]{0:T(128)S(1)}, u32[]{:S(2)}, u32[]{:S(2)}) %collective-permute-start.1) | collective-permute-done | bytes 64 | tf_op jit(solution)/shard_map/ppermute | solution.py:140
  12.4 1.6 %collective-permute-start.4 = (bf16[8,2048]{1,0:T(8,128)(2,1)S(1)}, bf16[8,2048]{1,0:T(8,128)(2,1)S(1)}, u32[]{:S(2)}, u32[]{:S(2)}) collective-permute-start(bf16[8,2048]{1,0:T(8,128)(2,1)S(1)} %fusion.76), channel_id=1, source_target_pairs={{0,2},{1,3},{2,0},{3,1},{4,6},{5,7},{6,4},{7,5},{8,10},{9,11},{10,... | collective-permute-start | bytes 98312 | tf_op jit(solution)/shard_map/ppermute | solution.py:97
  14.1 2.3 %collective-permute-done.4 = bf16[8,2048]{1,0:T(8,128)(2,1)S(1)} collective-permute-done((bf16[8,2048]{1,0:T(8,128)(2,1)S(1)}, bf16[8,2048]{1,0:T(8,128)(2,1)S(1)}, u32[]{:S(2)}, u32[]{:S(2)}) %collective-permute-start.4) | collective-permute-done | bytes 32800 | tf_op jit(solution)/shard_map/ppermute | solution.py:97
  18.0 5.9 %fusion.26 = f32[2,4,8,1280]{3,2,1,0:T(8,128)S(1)} fusion(bf16[2048,2,1280]{2,1,0:T(2,128)(2,1)} %param.24, bf16[32,2048]{1,0:T(8,128)(2,1)S(1)} %gather_fusion.1, pred[32]{0:T(512)(128)(4,1)S(1)} %get-tuple-element.62), kind=kOutput, calls=%fused_computation.29 | convolution fusion | flops 335609856 | bytes 10944544 | tf_op jit(solution)/shard_map/rf,fgc->rgc/dot_general | solution.py:213
  24.3 3.6 %collective-permute-start.8 = (f32[8,2560]{1,0:T(8,128)S(1)}, f32[8,2560]{1,0:T(8,128)S(1)}, u32[]{:S(2)}, u32[]{:S(2)}) collective-permute-start(f32[8,2560]{1,0:T(8,128)S(1)} %get-tuple-element.65), channel_id=1, source_target_pairs={{0,12},{4,0},{8,4},{12,8},{1,13},{5,1},{9,5},{13,9},{2,14},{6,2},{... | collective-permute-start | bytes 245768 | tf_op jit(solution)/shard_map/ppermute | solution.py:113
  28.4 2.7 %collective-permute-done.6 = f32[8,2560]{1,0:T(8,128)S(1)} collective-permute-done((f32[8,2560]{1,0:T(8,128)S(1)}, f32[8,2560]{1,0:T(8,128)S(1)}, u32[]{:S(2)}, u32[]{:S(2)}) %collective-permute-start.6) | collective-permute-done | bytes 81952 | tf_op jit(solution)/shard_map/ppermute | solution.py:113
  31.1 2.9 %collective-permute-done.7 = f32[8,2560]{1,0:T(8,128)S(1)} collective-permute-done((f32[8,2560]{1,0:T(8,128)S(1)}, f32[8,2560]{1,0:T(8,128)S(1)}, u32[]{:S(2)}, u32[]{:S(2)}) %collective-permute-start.7) | collective-permute-done | bytes 81952 | tf_op jit(solution)/shard_map/ppermute | solution.py:113
  35.4 1.8 %collective-permute-start.11 = (bf16[8,2048]{1,0:T(8,128)(2,1)S(1)}, bf16[8,2048]{1,0:T(8,128)(2,1)S(1)}, u32[]{:S(2)}, u32[]{:S(2)}) collective-permute-start(bf16[8,2048]{1,0:T(8,128)(2,1)S(1)} %bitcast.101), channel_id=1, source_target_pairs={{0,12},{4,0},{8,4},{12,8},{1,13},{5,1},{9,5},{13,9},{2,14},{6,2},{... | collective-permute-start | bytes 98312 | tf_op jit(solution)/shard_map/ppermute | solution.py:97
  37.9 1.5 %collective-permute-done.11 = bf16[8,2048]{1,0:T(8,128)(2,1)S(1)} collective-permute-done((bf16[8,2048]{1,0:T(8,128)(2,1)S(1)}, bf16[8,2048]{1,0:T(8,128)(2,1)S(1)}, u32[]{:S(2)}, u32[]{:S(2)}) %collective-permute-start.11) | collective-permute-done | bytes 32800 | tf_op jit(solution)/shard_map/ppermute | solution.py:97
  39.4 2.7 %collective-permute-done.10 = bf16[8,2048]{1,0:T(8,128)(2,1)S(1)} collective-permute-done((bf16[8,2048]{1,0:T(8,128)(2,1)S(1)}, bf16[8,2048]{1,0:T(8,128)(2,1)S(1)}, u32[]{:S(2)}, u32[]{:S(2)}) %collective-permute-start.10) | collective-permute-done | bytes 32800 | tf_op jit(solution)/shard_map/ppermute | solution.py:97
  43.7 5.0 %fusion.65 = f32[32,2048]{1,0:T(8,128)S(1)} fusion(bf16[2048,2048]{1,0:T(8,128)(2,1)} %param.25, bf16[32,2048]{1,0:T(8,128)(2,1)S(1)} %gather_fusion.2, pred[32]{0:T(512)(128)(4,1)S(1)} %get-tuple-element.60), kind=kOutput, calls=%fused_computation.60 | convolution fusion | flops 268500992 | bytes 8781856 | tf_op jit(solution)/shard_map/dot_general | solution.py:221
  48.8 1.3 %collective-permute-done.12 = f32[16,2048]{1,0:T(8,128)S(1)} collective-permute-done((f32[16,2048]{1,0:T(8,128)S(1)}, f32[16,2048]{1,0:T(8,128)S(1)}, u32[]{:S(2)}, u32[]{:S(2)}) %collective-permute-start.12) | collective-permute-done | bytes 131104 | tf_op jit(solution)/shard_map/ppermute | solution.py:113
  51.1 4.6 %collective-permute-done.13 = f32[16,2048]{1,0:T(8,128)S(1)} collective-permute-done((f32[16,2048]{1,0:T(8,128)S(1)}, f32[16,2048]{1,0:T(8,128)S(1)}, u32[]{:S(2)}, u32[]{:S(2)}) %collective-permute-start.13) | collective-permute-done | bytes 131104 | tf_op jit(solution)/shard_map/ppermute | solution.py:140
  59.2 2.0 %collective-permute-start.15 = (f32[32]{0:T(128)S(1)}, f32[32]{0:T(128)S(1)}, u32[]{:S(2)}, u32[]{:S(2)}) collective-permute-start(f32[32]{0:T(128)S(1)} %reduce_sum.62), channel_id=1, source_target_pairs={{0,4},{4,8},{8,12},{12,0},{1,5},{5,9},{9,13},{13,1},{2,6},{6,10},{... | collective-permute-start | bytes 392 | tf_op jit(solution)/shard_map/ppermute | solution.py:140
  61.6 1.7 %collective-permute-done.16 = f32[32]{0:T(128)S(1)} collective-permute-done((f32[32]{0:T(128)S(1)}, f32[32]{0:T(128)S(1)}, u32[]{:S(2)}, u32[]{:S(2)}) %collective-permute-start.16) | collective-permute-done | bytes 160 | tf_op jit(solution)/shard_map/ppermute | solution.py:140
  63.3 1.3 %collective-permute-done.15 = f32[32]{0:T(128)S(1)} collective-permute-done((f32[32]{0:T(128)S(1)}, f32[32]{0:T(128)S(1)}, u32[]{:S(2)}, u32[]{:S(2)}) %collective-permute-start.15) | collective-permute-done | bytes 160 | tf_op jit(solution)/shard_map/ppermute | solution.py:140
  64.7 2.7 %fusion.59 = bf16[32,896]{1,0:T(8,128)(2,1)S(1)} fusion(bf16[32,2048]{1,0:T(8,128)(2,1)S(1)} %get-tuple-element.58, bf16[2048,3584]{1,0:T(8,128)(2,1)} %param.28, s32[]{:T(128)S(6)} %select_n.214), kind=kOutput, calls=%fused_computation.41 | convolution fusion | flops 117469184 | bytes 3858436 | tf_op jit(solution)/shard_map/dot_general | solution.py:150
  67.4 2.9 %fusion.56 = bf16[32,896]{1,0:T(8,128)(2,1)S(1)} fusion(bf16[32,2048]{1,0:T(8,128)(2,1)S(1)} %get-tuple-element.58, bf16[2048,3584]{1,0:T(8,128)(2,1)} %param.27, s32[]{:T(128)S(6)} %select_n.214), kind=kOutput, calls=%fused_computation.40 | convolution fusion | flops 117469184 | bytes 3858436 | tf_op jit(solution)/shard_map/dot_general | solution.py:150
  70.3 2.9 %fusion.53 = bf16[32,896]{1,0:T(8,128)(2,1)S(1)} fusion(bf16[32,2048]{1,0:T(8,128)(2,1)S(1)} %get-tuple-element.58, bf16[2048,3584]{1,0:T(8,128)(2,1)} %param.28, s32[]{:T(128)S(6)} %select_n.213), kind=kOutput, calls=%fused_computation.39 | convolution fusion | flops 117469184 | bytes 3858436 | tf_op jit(solution)/shard_map/dot_general | solution.py:150
  73.2 2.7 %fusion.50 = bf16[32,896]{1,0:T(8,128)(2,1)S(1)} fusion(bf16[32,2048]{1,0:T(8,128)(2,1)S(1)} %get-tuple-element.58, bf16[2048,3584]{1,0:T(8,128)(2,1)} %param.27, s32[]{:T(128)S(6)} %select_n.213), kind=kOutput, calls=%fused_computation.38 | convolution fusion | flops 117469184 | bytes 3858436 | tf_op jit(solution)/shard_map/dot_general | solution.py:150
  75.9 2.9 %fusion.47 = bf16[32,896]{1,0:T(8,128)(2,1)S(1)} fusion(bf16[32,2048]{1,0:T(8,128)(2,1)S(1)} %get-tuple-element.58, bf16[2048,3584]{1,0:T(8,128)(2,1)} %param.28, s32[]{:T(128)S(6)} %select_n.212), kind=kOutput, calls=%fused_computation.37 | convolution fusion | flops 117469184 | bytes 3858436 | tf_op jit(solution)/shard_map/dot_general | solution.py:150
  78.8 2.7 %fusion.44 = bf16[32,896]{1,0:T(8,128)(2,1)S(1)} fusion(bf16[32,2048]{1,0:T(8,128)(2,1)S(1)} %get-tuple-element.58, bf16[2048,3584]{1,0:T(8,128)(2,1)} %param.27, s32[]{:T(128)S(6)} %select_n.212), kind=kOutput, calls=%fused_computation.36 | convolution fusion | flops 117469184 | bytes 3858436 | tf_op jit(solution)/shard_map/dot_general | solution.py:150
  81.5 2.9 %fusion.41 = bf16[32,896]{1,0:T(8,128)(2,1)S(1)} fusion(bf16[32,2048]{1,0:T(8,128)(2,1)S(1)} %get-tuple-element.58, bf16[2048,3584]{1,0:T(8,128)(2,1)} %param.28, s32[]{:T(128)S(6)} %select_n.211), kind=kOutput, calls=%fused_computation.35 | convolution fusion | flops 117469184 | bytes 3858436 | tf_op jit(solution)/shard_map/dot_general | solution.py:150
  84.7 1.9 %collective-permute-start.19 = (bf16[32,1792]{1,0:T(8,128)(2,1)S(1)}, bf16[32,1792]{1,0:T(8,128)(2,1)S(1)}, u32[]{:S(2)}, u32[]{:S(2)}) collective-permute-start(bf16[32,1792]{1,0:T(8,128)(2,1)S(1)} %pad_maximum_fusion.4), channel_id=1, source_target_pairs={{0,8},{4,12},{8,0},{12,4},{1,9},{5,13},{9,1},{13,5},{2,10},{6,14},... | collective-permute-start | bytes 344072 | tf_op jit(solution)/shard_map/ppermute | solution.py:161
  86.5 1.9 %collective-permute-start.20 = (bf16[32,1792]{1,0:T(8,128)(2,1)S(1)}, bf16[32,1792]{1,0:T(8,128)(2,1)S(1)}, u32[]{:S(2)}, u32[]{:S(2)}) collective-permute-start(bf16[32,1792]{1,0:T(8,128)(2,1)S(1)} %pad_maximum_fusion.5), channel_id=1, source_target_pairs={{0,12},{4,0},{8,4},{12,8},{1,13},{5,1},{9,5},{13,9},{2,14},{6,2},{... | collective-permute-start | bytes 344072 | tf_op jit(solution)/shard_map/ppermute | solution.py:161
  88.4 2.7 %fusion.38 = bf16[32,896]{1,0:T(8,128)(2,1)S(1)} fusion(bf16[32,2048]{1,0:T(8,128)(2,1)S(1)} %get-tuple-element.58, bf16[2048,3584]{1,0:T(8,128)(2,1)} %param.27, s32[]{:T(128)S(6)} %select_n.211), kind=kOutput, calls=%fused_computation.34 | convolution fusion | flops 117469184 | bytes 3858436 | tf_op jit(solution)/shard_map/dot_general | solution.py:150
  92.3 2.8 %collective-permute-done.19 = bf16[32,1792]{1,0:T(8,128)(2,1)S(1)} collective-permute-done((bf16[32,1792]{1,0:T(8,128)(2,1)S(1)}, bf16[32,1792]{1,0:T(8,128)(2,1)S(1)}, u32[]{:S(2)}, u32[]{:S(2)}) %collective-permute-start.19) | collective-permute-done | bytes 114720 | tf_op jit(solution)/shard_map/ppermute | solution.py:161
  95.2 2.6 %collective-permute-start.23 = (bf16[32,896]{1,0:T(8,128)(2,1)S(1)}, bf16[32,896]{1,0:T(8,128)(2,1)S(1)}, u32[]{:S(2)}, u32[]{:S(2)}) collective-permute-start(bf16[32,896]{1,0:T(8,128)(2,1)S(1)} %fusion.70), channel_id=1, source_target_pairs={{0,12},{4,0},{8,4},{12,8},{1,13},{5,1},{9,5},{13,9},{2,14},{6,2},{... | collective-permute-start | bytes 172040 | tf_op jit(solution)/shard_map/ppermute | solution.py:174
  99.6 3.9 %collective-permute-done.22 = bf16[32,896]{1,0:T(8,128)(2,1)S(1)} collective-permute-done((bf16[32,896]{1,0:T(8,128)(2,1)S(1)}, bf16[32,896]{1,0:T(8,128)(2,1)S(1)}, u32[]{:S(2)}, u32[]{:S(2)}) %collective-permute-start.22) | collective-permute-done | bytes 57376 | tf_op jit(solution)/shard_map/ppermute | solution.py:174
  105.9 1.3 %collective-permute-done.24 = f32[2,8,2048]{2,1,0:T(8,128)S(1)} collective-permute-done((f32[2,8,2048]{2,1,0:T(8,128)S(1)}, f32[2,8,2048]{2,1,0:T(8,128)S(1)}, u32[]{:S(2)}, u32[]{:S(2)}) %collective-permute-start.24) | collective-permute-done | bytes 131104 | tf_op jit(solution)/shard_map/ppermute | solution.py:113
  108.2 3.4 %collective-permute-done.25 = f32[8,2048]{1,0:T(8,128)S(1)} collective-permute-done((f32[8,2048]{1,0:T(8,128)S(1)}, f32[8,2048]{1,0:T(8,128)S(1)}, u32[]{:S(2)}, u32[]{:S(2)}) %collective-permute-start.25) | collective-permute-done | bytes 65568 | tf_op jit(solution)/shard_map/ppermute | solution.py:113
  (111 shorter events, 24.2 us)
Async XLA Ops:
  0.0 27.9 %copy-start = (bf16[8,256,2,2,128]{4,3,2,1,0:T(2,128)(2,1)S(1)}, bf16[8,256,2,2,128]{4,3,2,1,0:T(2,128)(2,1)}, u32[]{:S(2)}) copy-start(bf16[8,256,2,2,128]{4,3,2,1,0:T(2,128)(2,1)} %param.30) | copy-start | bytes 6291460
  1.0 8.2 %collective-permute-start.2 = (f32[8]{0:T(128)S(1)}, f32[8]{0:T(128)S(1)}, u32[]{:S(2)}, u32[]{:S(2)}) collective-permute-start(f32[8]{0:T(128)S(1)} %fusion.74), channel_id=1, source_target_pairs={{0,12},{4,0},{8,4},{12,8},{1,13},{5,1},{9,5},{13,9},{2,14},{6,2},{... | collective-permute-start | bytes 104 | tf_op jit(solution)/shard_map/ppermute | solution.py:140
  6.1 4.4 %collective-permute-start.1 = (f32[8]{0:T(128)S(1)}, f32[8]{0:T(128)S(1)}, u32[]{:S(2)}, u32[]{:S(2)}) collective-permute-start(f32[8]{0:T(128)S(1)} %fusion.74), channel_id=1, source_target_pairs={{0,8},{4,12},{8,0},{12,4},{1,9},{5,13},{9,1},{13,5},{2,10},{6,14},... | collective-permute-start | bytes 104 | tf_op jit(solution)/shard_map/ppermute | solution.py:140
  6.1 5.3 %collective-permute-start = (f32[8]{0:T(128)S(1)}, f32[8]{0:T(128)S(1)}, u32[]{:S(2)}, u32[]{:S(2)}) collective-permute-start(f32[8]{0:T(128)S(1)} %fusion.74), channel_id=1, source_target_pairs={{0,4},{4,8},{8,12},{12,0},{1,5},{5,9},{9,13},{13,1},{2,6},{6,10},{... | collective-permute-start | bytes 104 | tf_op jit(solution)/shard_map/ppermute | solution.py:140
  12.3 1.8 %collective-permute-start.5 = (bf16[8,2048]{1,0:T(8,128)(2,1)S(1)}, bf16[8,2048]{1,0:T(8,128)(2,1)S(1)}, u32[]{:S(2)}, u32[]{:S(2)}) collective-permute-start(bf16[8,2048]{1,0:T(8,128)(2,1)S(1)} %fusion.76), channel_id=1, source_target_pairs={{0,3},{1,0},{2,1},{3,2},{4,7},{5,4},{6,5},{7,6},{8,11},{9,8},{10,9... | collective-permute-start | bytes 98312 | tf_op jit(solution)/shard_map/ppermute | solution.py:97
  12.4 4.1 %collective-permute-start.4 = (bf16[8,2048]{1,0:T(8,128)(2,1)S(1)}, bf16[8,2048]{1,0:T(8,128)(2,1)S(1)}, u32[]{:S(2)}, u32[]{:S(2)}) collective-permute-start(bf16[8,2048]{1,0:T(8,128)(2,1)S(1)} %fusion.76), channel_id=1, source_target_pairs={{0,2},{1,3},{2,0},{3,1},{4,6},{5,7},{6,4},{7,5},{8,10},{9,11},{10,... | collective-permute-start | bytes 98312 | tf_op jit(solution)/shard_map/ppermute | solution.py:97
  13.9 3.3 %collective-permute-start.3 = (bf16[8,2048]{1,0:T(8,128)(2,1)S(1)}, bf16[8,2048]{1,0:T(8,128)(2,1)S(1)}, u32[]{:S(2)}, u32[]{:S(2)}) collective-permute-start(bf16[8,2048]{1,0:T(8,128)(2,1)S(1)} %fusion.76), channel_id=1, source_target_pairs={{0,1},{1,2},{2,3},{3,0},{4,5},{5,6},{6,7},{7,4},{8,9},{9,10},{10,1... | collective-permute-start | bytes 98312 | tf_op jit(solution)/shard_map/ppermute | solution.py:97
  24.0 7.1 %collective-permute-start.6 = (f32[8,2560]{1,0:T(8,128)S(1)}, f32[8,2560]{1,0:T(8,128)S(1)}, u32[]{:S(2)}, u32[]{:S(2)}) collective-permute-start(f32[8,2560]{1,0:T(8,128)S(1)} %get-tuple-element.64), channel_id=1, source_target_pairs={{0,4},{4,8},{8,12},{12,0},{1,5},{5,9},{9,13},{13,1},{2,6},{6,10},{... | collective-permute-start | bytes 245768 | tf_op jit(solution)/shard_map/ppermute | solution.py:113
  24.3 6.8 %collective-permute-start.8 = (f32[8,2560]{1,0:T(8,128)S(1)}, f32[8,2560]{1,0:T(8,128)S(1)}, u32[]{:S(2)}, u32[]{:S(2)}) collective-permute-start(f32[8,2560]{1,0:T(8,128)S(1)} %get-tuple-element.65), channel_id=1, source_target_pairs={{0,12},{4,0},{8,4},{12,8},{1,13},{5,1},{9,5},{13,9},{2,14},{6,2},{... | collective-permute-start | bytes 245768 | tf_op jit(solution)/shard_map/ppermute | solution.py:113
  27.8 6.1 %collective-permute-start.7 = (f32[8,2560]{1,0:T(8,128)S(1)}, f32[8,2560]{1,0:T(8,128)S(1)}, u32[]{:S(2)}, u32[]{:S(2)}) collective-permute-start(f32[8,2560]{1,0:T(8,128)S(1)} %get-tuple-element.66), channel_id=1, source_target_pairs={{0,8},{4,12},{8,0},{12,4},{1,9},{5,13},{9,1},{13,5},{2,10},{6,14},... | collective-permute-start | bytes 245768 | tf_op jit(solution)/shard_map/ppermute | solution.py:113
  35.4 4.0 %collective-permute-start.11 = (bf16[8,2048]{1,0:T(8,128)(2,1)S(1)}, bf16[8,2048]{1,0:T(8,128)(2,1)S(1)}, u32[]{:S(2)}, u32[]{:S(2)}) collective-permute-start(bf16[8,2048]{1,0:T(8,128)(2,1)S(1)} %bitcast.101), channel_id=1, source_target_pairs={{0,12},{4,0},{8,4},{12,8},{1,13},{5,1},{9,5},{13,9},{2,14},{6,2},{... | collective-permute-start | bytes 98312 | tf_op jit(solution)/shard_map/ppermute | solution.py:97
  37.3 4.9 %collective-permute-start.10 = (bf16[8,2048]{1,0:T(8,128)(2,1)S(1)}, bf16[8,2048]{1,0:T(8,128)(2,1)S(1)}, u32[]{:S(2)}, u32[]{:S(2)}) collective-permute-start(bf16[8,2048]{1,0:T(8,128)(2,1)S(1)} %bitcast.102), channel_id=1, source_target_pairs={{0,8},{4,12},{8,0},{12,4},{1,9},{5,13},{9,1},{13,5},{2,10},{6,14},... | collective-permute-start | bytes 98312 | tf_op jit(solution)/shard_map/ppermute | solution.py:97
  37.3 5.7 %collective-permute-start.9 = (bf16[8,2048]{1,0:T(8,128)(2,1)S(1)}, bf16[8,2048]{1,0:T(8,128)(2,1)S(1)}, u32[]{:S(2)}, u32[]{:S(2)}) collective-permute-start(bf16[8,2048]{1,0:T(8,128)(2,1)S(1)} %bitcast.103), channel_id=1, source_target_pairs={{0,4},{4,8},{8,12},{12,0},{1,5},{5,9},{9,13},{13,1},{2,6},{6,10},{... | collective-permute-start | bytes 98312 | tf_op jit(solution)/shard_map/ppermute | solution.py:97
  43.6 20.9 %copy-start.2 = (f32[2048]{0:T(1024)S(1)}, f32[2048]{0:T(1024)}, u32[]{:S(2)}) copy-start(f32[2048]{0:T(1024)} %param.26) | copy-start | bytes 24580
  48.7 1.4 %collective-permute-start.12 = (f32[16,2048]{1,0:T(8,128)S(1)}, f32[16,2048]{1,0:T(8,128)S(1)}, u32[]{:S(2)}, u32[]{:S(2)}) collective-permute-start(f32[16,2048]{1,0:T(8,128)S(1)} %select_bitcast_fusion.1), channel_id=1, source_target_pairs={{0,1},{1,0},{2,3},{3,2},{4,5},{5,4},{6,7},{7,6},{8,9},{9,8},{10,11... | collective-permute-start | bytes 393224 | tf_op jit(solution)/shard_map/ppermute | solution.py:113
  50.1 5.6 %collective-permute-start.13 = (f32[16,2048]{1,0:T(8,128)S(1)}, f32[16,2048]{1,0:T(8,128)S(1)}, u32[]{:S(2)}, u32[]{:S(2)}) collective-permute-start(f32[16,2048]{1,0:T(8,128)S(1)} %bitcast_add_fusion.1), channel_id=1, source_target_pairs={{0,2},{2,0},{1,3},{3,1},{4,6},{6,4},{5,7},{7,5},{8,10},{10,8},{9,1... | collective-permute-start | bytes 393224 | tf_op jit(solution)/shard_map/ppermute | solution.py:140
  55.8 1.4 %collective-permute-start.14 = (f32[16,2048]{1,0:T(8,128)S(1)}, f32[16,2048]{1,0:T(8,128)S(1)}, u32[]{:S(2)}, u32[]{:S(2)}) collective-permute-start(f32[16,2048]{1,0:T(8,128)S(1)} %add.289), channel_id=1, source_target_pairs={{0,1},{1,0},{2,3},{3,2},{4,5},{5,4},{6,7},{7,6},{8,9},{9,8},{10,11... | collective-permute-start | bytes 393224 | tf_op jit(solution)/shard_map/ppermute | solution.py:131
  58.0 3.5 %collective-permute-start.17 = (f32[32]{0:T(128)S(1)}, f32[32]{0:T(128)S(1)}, u32[]{:S(2)}, u32[]{:S(2)}) collective-permute-start(f32[32]{0:T(128)S(1)} %reduce_sum.62), channel_id=1, source_target_pairs={{0,12},{4,0},{8,4},{12,8},{1,13},{5,1},{9,5},{13,9},{2,14},{6,2},{... | collective-permute-start | bytes 392 | tf_op jit(solution)/shard_map/ppermute | solution.py:140
  58.9 4.4 %collective-permute-start.16 = (f32[32]{0:T(128)S(1)}, f32[32]{0:T(128)S(1)}, u32[]{:S(2)}, u32[]{:S(2)}) collective-permute-start(f32[32]{0:T(128)S(1)} %reduce_sum.62), channel_id=1, source_target_pairs={{0,8},{4,12},{8,0},{12,4},{1,9},{5,13},{9,1},{13,5},{2,10},{6,14},... | collective-permute-start | bytes 392 | tf_op jit(solution)/shard_map/ppermute | solution.py:140
  59.2 5.3 %collective-permute-start.15 = (f32[32]{0:T(128)S(1)}, f32[32]{0:T(128)S(1)}, u32[]{:S(2)}, u32[]{:S(2)}) collective-permute-start(f32[32]{0:T(128)S(1)} %reduce_sum.62), channel_id=1, source_target_pairs={{0,4},{4,8},{8,12},{12,0},{1,5},{5,9},{9,13},{13,1},{2,6},{6,10},{... | collective-permute-start | bytes 392 | tf_op jit(solution)/shard_map/ppermute | solution.py:140
  67.4 31.4 %slice-start = ((s8[14680064]{0:T(1024)(128)(4,1)}), s8[4194304]{0:T(1024)(128)(4,1)S(1)}, s32[]{:S(2)}) async-start(s8[14680064]{0:T(1024)(128)(4,1)} %bitcast.85), calls=%async_computation | async-start | bytes 8388608
  70.3 28.5 %slice-start.1 = ((s8[14680064]{0:T(1024)(128)(4,1)}), s8[4194304]{0:T(1024)(128)(4,1)S(1)}, s32[]{:S(2)}) async-start(s8[14680064]{0:T(1024)(128)(4,1)} %bitcast.85), calls=%async_computation.1 | async-start | bytes 8388608
  75.9 22.9 %slice-start.2 = ((s8[14680064]{0:T(1024)(128)(4,1)}), s8[4194304]{0:T(1024)(128)(4,1)S(1)}, s32[]{:S(2)}) async-start(s8[14680064]{0:T(1024)(128)(4,1)} %bitcast.85), calls=%async_computation.2 | async-start | bytes 8388608
  81.5 17.3 %slice-start.3 = ((s8[14680064]{0:T(1024)(128)(4,1)}), s8[2097152]{0:T(1024)(128)(4,1)S(1)}, s32[]{:S(2)}) async-start(s8[14680064]{0:T(1024)(128)(4,1)} %bitcast.85), calls=%async_computation.3 | async-start | bytes 4194304
  84.4 7.9 %collective-permute-start.18 = (bf16[32,1792]{1,0:T(8,128)(2,1)S(1)}, bf16[32,1792]{1,0:T(8,128)(2,1)S(1)}, u32[]{:S(2)}, u32[]{:S(2)}) collective-permute-start(bf16[32,1792]{1,0:T(8,128)(2,1)S(1)} %pad_maximum_fusion.3), channel_id=1, source_target_pairs={{0,4},{4,8},{8,12},{12,0},{1,5},{5,9},{9,13},{13,1},{2,6},{6,10},{... | collective-permute-start | bytes 344072 | tf_op jit(solution)/shard_map/ppermute | solution.py:161
  84.7 10.4 %collective-permute-start.19 = (bf16[32,1792]{1,0:T(8,128)(2,1)S(1)}, bf16[32,1792]{1,0:T(8,128)(2,1)S(1)}, u32[]{:S(2)}, u32[]{:S(2)}) collective-permute-start(bf16[32,1792]{1,0:T(8,128)(2,1)S(1)} %pad_maximum_fusion.4), channel_id=1, source_target_pairs={{0,8},{4,12},{8,0},{12,4},{1,9},{5,13},{9,1},{13,5},{2,10},{6,14},... | collective-permute-start | bytes 344072 | tf_op jit(solution)/shard_map/ppermute | solution.py:161
  86.5 8.6 %collective-permute-start.20 = (bf16[32,1792]{1,0:T(8,128)(2,1)S(1)}, bf16[32,1792]{1,0:T(8,128)(2,1)S(1)}, u32[]{:S(2)}, u32[]{:S(2)}) collective-permute-start(bf16[32,1792]{1,0:T(8,128)(2,1)S(1)} %pad_maximum_fusion.5), channel_id=1, source_target_pairs={{0,12},{4,0},{8,4},{12,8},{1,13},{5,1},{9,5},{13,9},{2,14},{6,2},{... | collective-permute-start | bytes 344072 | tf_op jit(solution)/shard_map/ppermute | solution.py:161
  95.2 9.0 %collective-permute-start.23 = (bf16[32,896]{1,0:T(8,128)(2,1)S(1)}, bf16[32,896]{1,0:T(8,128)(2,1)S(1)}, u32[]{:S(2)}, u32[]{:S(2)}) collective-permute-start(bf16[32,896]{1,0:T(8,128)(2,1)S(1)} %fusion.70), channel_id=1, source_target_pairs={{0,12},{4,0},{8,4},{12,8},{1,13},{5,1},{9,5},{13,9},{2,14},{6,2},{... | collective-permute-start | bytes 172040 | tf_op jit(solution)/shard_map/ppermute | solution.py:174
  97.8 5.6 %collective-permute-start.22 = (bf16[32,896]{1,0:T(8,128)(2,1)S(1)}, bf16[32,896]{1,0:T(8,128)(2,1)S(1)}, u32[]{:S(2)}, u32[]{:S(2)}) collective-permute-start(bf16[32,896]{1,0:T(8,128)(2,1)S(1)} %fusion.70), channel_id=1, source_target_pairs={{0,8},{4,12},{8,0},{12,4},{1,9},{5,13},{9,1},{13,5},{2,10},{6,14},... | collective-permute-start | bytes 172040 | tf_op jit(solution)/shard_map/ppermute | solution.py:174
  98.8 6.2 %collective-permute-start.21 = (bf16[32,896]{1,0:T(8,128)(2,1)S(1)}, bf16[32,896]{1,0:T(8,128)(2,1)S(1)}, u32[]{:S(2)}, u32[]{:S(2)}) collective-permute-start(bf16[32,896]{1,0:T(8,128)(2,1)S(1)} %fusion.70), channel_id=1, source_target_pairs={{0,4},{4,8},{8,12},{12,0},{1,5},{5,9},{9,13},{13,1},{2,6},{6,10},{... | collective-permute-start | bytes 172040 | tf_op jit(solution)/shard_map/ppermute | solution.py:174
  105.8 1.4 %collective-permute-start.24 = (f32[2,8,2048]{2,1,0:T(8,128)S(1)}, f32[2,8,2048]{2,1,0:T(8,128)S(1)}, u32[]{:S(2)}, u32[]{:S(2)}) collective-permute-start(f32[2,8,2048]{2,1,0:T(8,128)S(1)} %select_bitcast_fusion), channel_id=1, source_target_pairs={{0,1},{1,0},{2,3},{3,2},{4,5},{5,4},{6,7},{7,6},{8,9},{9,8},{10,11... | collective-permute-start | bytes 393224 | tf_op jit(solution)/shard_map/ppermute | solution.py:113
  107.3 4.3 %collective-permute-start.25 = (f32[8,2048]{1,0:T(8,128)S(1)}, f32[8,2048]{1,0:T(8,128)S(1)}, u32[]{:S(2)}, u32[]{:S(2)}) collective-permute-start(f32[8,2048]{1,0:T(8,128)S(1)} %select_bitcast_fusion.5), channel_id=1, source_target_pairs={{0,2},{2,0},{1,3},{3,1},{4,6},{6,4},{5,7},{7,5},{8,10},{10,8},{9,1... | collective-permute-start | bytes 196616 | tf_op jit(solution)/shard_map/ppermute | solution.py:113
  (1 other events, 13.2 us)

commit v12 on v11

--- a/solution.py
+++ b/solution.py
@@ -135,6 +135,12 @@
 
 
 def all_sum(x, axis, n):
+    if n & (n - 1) == 0:
+        step = 1
+        while step < n:
+            x = x + lax.ppermute(x, axis, [(i, i ^ step) for i in range(n)])
+            step *= 2
+        return x
     total = x
     for k in range(1, n):
         total = total + lax.ppermute(x, axis, shift_pairs(n, k))

time: 113 us -> 114 us (level)
  waiting for transfers between devices: 39 us -> 40.9 us
    ppermute x7 -> x5, waiting for transfers between devices: 10.3 us -> 13.4 us  [all_sum(): x = x + lax.ppermute(x, axis, [(i, i ^ step) for i in range(n)])]
    ppermute x7 -> x5, starting transfers between devices: 10.2 us -> 7.8 us  [all_sum(): x = x + lax.ppermute(x, axis, [(i, i ^ step) for i in range(n)])]
  transfers between devices with their start and end apart: 26 -> 24, of which waited for: 20 -> 19; matrix products, arithmetic and copies ran while one was open for 7% -> 7% of each run, Pallas kernels for 0% -> 0%
where the time goes in v12:
time: 114 us; the launch traced here: 113 us
  waiting for transfers between devices  40.9 us (36%)
  matrix products  37.1 us (33%)
  starting transfers between devices  26.2 us (23%)
  other arithmetic  5.69 us (5%)
  local copies, waits for them, and re-layouts  2.73 us (2%)
    dot_general x8, matrix products, block(): jnp.dot(x, lax.dynamic_slice_in_dim(w, j * chunk, chunk, 1), preferred_el...  22.3 us
    ppermute x5, waiting for transfers between devices, all_sum(): x = x + lax.ppermute(x, axis, [(i, i ^ step) for i in range(n)])  13.4 us
    ppermute x6, waiting for transfers between devices, scatter_sum(): lax.ppermute(piece, axis, shift_pairs(n, k)).astype(jnp.float32)  11.7 us
    ppermute x6, waiting for transfers between devices, gather_rows(): got = [x] + [lax.ppermute(x, axis, shift_pairs(n, k)) for k in range(1, n)]  8.23 us
    ppermute x5, starting transfers between devices, all_sum(): x = x + lax.ppermute(x, axis, [(i, i ^ step) for i in range(n)])  7.8 us
    dot_general x1, matrix products, local(): jnp.einsum('rf,fgc->rgc', by_slot, w_qkv, preferred_element_type=jnp.floa...  5.94 us
    ppermute x6, starting transfers between devices, scatter_sum(): lax.ppermute(piece, axis, shift_pairs(n, k)).astype(jnp.float32)  5.75 us
    dot_general x1, matrix products, local(): out_part = jnp.dot(by_row, w_out, preferred_element_type=jnp.float32)  4.98 us
  transfers between devices with their start and end apart: 24, of which 19 were waited for; matrix products, arithmetic and copies ran while one was open for 7% of the time, Pallas kernels for 0%

profile of v12, /device:TPU:0, one launch (start us, length us, event | category | flops | bytes accessed | tf_op | source)
XLA Modules:
  0.0 113.3 jit_solution(13189056802530014656)
XLA Ops:
  1.0 3.1 %collective-permute-start = (f32[8]{0:T(128)S(1)}, f32[8]{0:T(128)S(1)}, u32[]{:S(2)}, u32[]{:S(2)}) collective-permute-start(f32[8]{0:T(128)S(1)} %fusion.74), channel_id=1, source_target_pairs={{0,4},{4,0},{8,12},{12,8},{1,5},{5,1},{9,13},{13,9},{2,6},{6,2},{1... | collective-permute-start | bytes 104 | tf_op jit(solution)/shard_map/ppermute | solution.py:141
  6.2 2.7 %collective-permute-start.1 = (f32[8]{0:T(128)S(1)}, f32[8]{0:T(128)S(1)}, u32[]{:S(2)}, u32[]{:S(2)}) collective-permute-start(f32[8]{0:T(128)S(1)} %add.255), channel_id=1, source_target_pairs={{0,8},{4,12},{8,0},{12,4},{1,9},{5,13},{9,1},{13,5},{2,10},{6,14},... | collective-permute-start | bytes 104 | tf_op jit(solution)/shard_map/ppermute | solution.py:141
  8.9 1.9 %collective-permute-done.1 = f32[8]{0:T(128)S(1)} collective-permute-done((f32[8]{0:T(128)S(1)}, f32[8]{0:T(128)S(1)}, u32[]{:S(2)}, u32[]{:S(2)}) %collective-permute-start.1) | collective-permute-done | bytes 64 | tf_op jit(solution)/shard_map/ppermute | solution.py:141
  11.6 1.6 %collective-permute-start.3 = (bf16[8,2048]{1,0:T(8,128)(2,1)S(1)}, bf16[8,2048]{1,0:T(8,128)(2,1)S(1)}, u32[]{:S(2)}, u32[]{:S(2)}) collective-permute-start(bf16[8,2048]{1,0:T(8,128)(2,1)S(1)} %fusion.76), channel_id=1, source_target_pairs={{0,2},{1,3},{2,0},{3,1},{4,6},{5,7},{6,4},{7,5},{8,10},{9,11},{10,... | collective-permute-start | bytes 98312 | tf_op jit(solution)/shard_map/ppermute | solution.py:97
  13.4 2.3 %collective-permute-done.3 = bf16[8,2048]{1,0:T(8,128)(2,1)S(1)} collective-permute-done((bf16[8,2048]{1,0:T(8,128)(2,1)S(1)}, bf16[8,2048]{1,0:T(8,128)(2,1)S(1)}, u32[]{:S(2)}, u32[]{:S(2)}) %collective-permute-start.3) | collective-permute-done | bytes 32800 | tf_op jit(solution)/shard_map/ppermute | solution.py:97
  17.2 5.9 %fusion.26 = f32[2,4,8,1280]{3,2,1,0:T(8,128)S(1)} fusion(bf16[2048,2,1280]{2,1,0:T(2,128)(2,1)} %param.24, bf16[32,2048]{1,0:T(8,128)(2,1)S(1)} %gather_fusion.1, pred[32]{0:T(512)(128)(4,1)S(1)} %get-tuple-element.62), kind=kOutput, calls=%fused_computation.29 | convolution fusion | flops 335609856 | bytes 10944544 | tf_op jit(solution)/shard_map/rf,fgc->rgc/dot_general | solution.py:219
  23.2 1.4 %collective-permute-start.5 = (f32[8,2560]{1,0:T(8,128)S(1)}, f32[8,2560]{1,0:T(8,128)S(1)}, u32[]{:S(2)}, u32[]{:S(2)}) collective-permute-start(f32[8,2560]{1,0:T(8,128)S(1)} %get-tuple-element.64), channel_id=1, source_target_pairs={{0,4},{4,8},{8,12},{12,0},{1,5},{5,9},{9,13},{13,1},{2,6},{6,10},{... | collective-permute-start | bytes 245768 | tf_op jit(solution)/shard_map/ppermute | solution.py:113
  24.6 2.4 %collective-permute-start.7 = (f32[8,2560]{1,0:T(8,128)S(1)}, f32[8,2560]{1,0:T(8,128)S(1)}, u32[]{:S(2)}, u32[]{:S(2)}) collective-permute-start(f32[8,2560]{1,0:T(8,128)S(1)} %get-tuple-element.65), channel_id=1, source_target_pairs={{0,12},{4,0},{8,4},{12,8},{1,13},{5,1},{9,5},{13,9},{2,14},{6,2},{... | collective-permute-start | bytes 245768 | tf_op jit(solution)/shard_map/ppermute | solution.py:113
  28.4 2.0 %collective-permute-done.5 = f32[8,2560]{1,0:T(8,128)S(1)} collective-permute-done((f32[8,2560]{1,0:T(8,128)S(1)}, f32[8,2560]{1,0:T(8,128)S(1)}, u32[]{:S(2)}, u32[]{:S(2)}) %collective-permute-start.5) | collective-permute-done | bytes 81952 | tf_op jit(solution)/shard_map/ppermute | solution.py:113
  30.4 3.7 %collective-permute-done.6 = f32[8,2560]{1,0:T(8,128)S(1)} collective-permute-done((f32[8,2560]{1,0:T(8,128)S(1)}, f32[8,2560]{1,0:T(8,128)S(1)}, u32[]{:S(2)}, u32[]{:S(2)}) %collective-permute-start.6) | collective-permute-done | bytes 81952 | tf_op jit(solution)/shard_map/ppermute | solution.py:113
  35.5 2.4 %collective-permute-start.10 = (bf16[8,2048]{1,0:T(8,128)(2,1)S(1)}, bf16[8,2048]{1,0:T(8,128)(2,1)S(1)}, u32[]{:S(2)}, u32[]{:S(2)}) collective-permute-start(bf16[8,2048]{1,0:T(8,128)(2,1)S(1)} %bitcast.101), channel_id=1, source_target_pairs={{0,12},{4,0},{8,4},{12,8},{1,13},{5,1},{9,5},{13,9},{2,14},{6,2},{... | collective-permute-start | bytes 98312 | tf_op jit(solution)/shard_map/ppermute | solution.py:97
  39.5 3.2 %collective-permute-done.9 = bf16[8,2048]{1,0:T(8,128)(2,1)S(1)} collective-permute-done((bf16[8,2048]{1,0:T(8,128)(2,1)S(1)}, bf16[8,2048]{1,0:T(8,128)(2,1)S(1)}, u32[]{:S(2)}, u32[]{:S(2)}) %collective-permute-start.9) | collective-permute-done | bytes 32800 | tf_op jit(solution)/shard_map/ppermute | solution.py:97
  44.3 5.0 %fusion.65 = f32[32,2048]{1,0:T(8,128)S(1)} fusion(bf16[2048,2048]{1,0:T(8,128)(2,1)} %param.25, bf16[32,2048]{1,0:T(8,128)(2,1)S(1)} %gather_fusion.2, pred[32]{0:T(512)(128)(4,1)S(1)} %get-tuple-element.60), kind=kOutput, calls=%fused_computation.60 | convolution fusion | flops 268500992 | bytes 8781856 | tf_op jit(solution)/shard_map/dot_general | solution.py:227
  49.4 1.3 %collective-permute-done.11 = f32[16,2048]{1,0:T(8,128)S(1)} collective-permute-done((f32[16,2048]{1,0:T(8,128)S(1)}, f32[16,2048]{1,0:T(8,128)S(1)}, u32[]{:S(2)}, u32[]{:S(2)}) %collective-permute-start.11) | collective-permute-done | bytes 131104 | tf_op jit(solution)/shard_map/ppermute | solution.py:113
  51.7 4.7 %collective-permute-done.12 = f32[16,2048]{1,0:T(8,128)S(1)} collective-permute-done((f32[16,2048]{1,0:T(8,128)S(1)}, f32[16,2048]{1,0:T(8,128)S(1)}, u32[]{:S(2)}, u32[]{:S(2)}) %collective-permute-start.12) | collective-permute-done | bytes 131104 | tf_op jit(solution)/shard_map/ppermute | solution.py:141
  58.7 3.5 %collective-permute-done.14 = f32[32]{0:T(128)S(1)} collective-permute-done((f32[32]{0:T(128)S(1)}, f32[32]{0:T(128)S(1)}, u32[]{:S(2)}, u32[]{:S(2)}) %collective-permute-start.14) | collective-permute-done | bytes 160 | tf_op jit(solution)/shard_map/ppermute | solution.py:141
  63.4 3.3 %collective-permute-done.15 = f32[32]{0:T(128)S(1)} collective-permute-done((f32[32]{0:T(128)S(1)}, f32[32]{0:T(128)S(1)}, u32[]{:S(2)}, u32[]{:S(2)}) %collective-permute-start.15) | collective-permute-done | bytes 160 | tf_op jit(solution)/shard_map/ppermute | solution.py:141
  66.8 2.7 %fusion.59 = bf16[32,896]{1,0:T(8,128)(2,1)S(1)} fusion(bf16[32,2048]{1,0:T(8,128)(2,1)S(1)} %get-tuple-element.58, bf16[2048,3584]{1,0:T(8,128)(2,1)} %param.28, s32[]{:T(128)S(6)} %select_n.214), kind=kOutput, calls=%fused_computation.41 | convolution fusion | flops 117469184 | bytes 3858436 | tf_op jit(solution)/shard_map/dot_general | solution.py:156
  69.6 2.9 %fusion.56 = bf16[32,896]{1,0:T(8,128)(2,1)S(1)} fusion(bf16[32,2048]{1,0:T(8,128)(2,1)S(1)} %get-tuple-element.58, bf16[2048,3584]{1,0:T(8,128)(2,1)} %param.27, s32[]{:T(128)S(6)} %select_n.214), kind=kOutput, calls=%fused_computation.40 | convolution fusion | flops 117469184 | bytes 3858436 | tf_op jit(solution)/shard_map/dot_general | solution.py:156
  72.4 2.9 %fusion.53 = bf16[32,896]{1,0:T(8,128)(2,1)S(1)} fusion(bf16[32,2048]{1,0:T(8,128)(2,1)S(1)} %get-tuple-element.58, bf16[2048,3584]{1,0:T(8,128)(2,1)} %param.28, s32[]{:T(128)S(6)} %select_n.213), kind=kOutput, calls=%fused_computation.39 | convolution fusion | flops 117469184 | bytes 3858436 | tf_op jit(solution)/shard_map/dot_general | solution.py:156
  75.3 2.7 %fusion.50 = bf16[32,896]{1,0:T(8,128)(2,1)S(1)} fusion(bf16[32,2048]{1,0:T(8,128)(2,1)S(1)} %get-tuple-element.58, bf16[2048,3584]{1,0:T(8,128)(2,1)} %param.27, s32[]{:T(128)S(6)} %select_n.213), kind=kOutput, calls=%fused_computation.38 | convolution fusion | flops 117469184 | bytes 3858436 | tf_op jit(solution)/shard_map/dot_general | solution.py:156
  78.0 2.9 %fusion.47 = bf16[32,896]{1,0:T(8,128)(2,1)S(1)} fusion(bf16[32,2048]{1,0:T(8,128)(2,1)S(1)} %get-tuple-element.58, bf16[2048,3584]{1,0:T(8,128)(2,1)} %param.28, s32[]{:T(128)S(6)} %select_n.212), kind=kOutput, calls=%fused_computation.37 | convolution fusion | flops 117469184 | bytes 3858436 | tf_op jit(solution)/shard_map/dot_general | solution.py:156
  80.9 2.7 %fusion.44 = bf16[32,896]{1,0:T(8,128)(2,1)S(1)} fusion(bf16[32,2048]{1,0:T(8,128)(2,1)S(1)} %get-tuple-element.58, bf16[2048,3584]{1,0:T(8,128)(2,1)} %param.27, s32[]{:T(128)S(6)} %select_n.212), kind=kOutput, calls=%fused_computation.36 | convolution fusion | flops 117469184 | bytes 3858436 | tf_op jit(solution)/shard_map/dot_general | solution.py:156
  83.6 2.9 %fusion.41 = bf16[32,896]{1,0:T(8,128)(2,1)S(1)} fusion(bf16[32,2048]{1,0:T(8,128)(2,1)S(1)} %get-tuple-element.58, bf16[2048,3584]{1,0:T(8,128)(2,1)} %param.28, s32[]{:T(128)S(6)} %select_n.211), kind=kOutput, calls=%fused_computation.35 | convolution fusion | flops 117469184 | bytes 3858436 | tf_op jit(solution)/shard_map/dot_general | solution.py:156
  86.6 1.2 %collective-permute-start.17 = (bf16[32,1792]{1,0:T(8,128)(2,1)S(1)}, bf16[32,1792]{1,0:T(8,128)(2,1)S(1)}, u32[]{:S(2)}, u32[]{:S(2)}) collective-permute-start(bf16[32,1792]{1,0:T(8,128)(2,1)S(1)} %pad_maximum_fusion.4), channel_id=1, source_target_pairs={{0,8},{4,12},{8,0},{12,4},{1,9},{5,13},{9,1},{13,5},{2,10},{6,14},... | collective-permute-start | bytes 344072 | tf_op jit(solution)/shard_map/ppermute | solution.py:167
  87.8 3.0 %collective-permute-start.18 = (bf16[32,1792]{1,0:T(8,128)(2,1)S(1)}, bf16[32,1792]{1,0:T(8,128)(2,1)S(1)}, u32[]{:S(2)}, u32[]{:S(2)}) collective-permute-start(bf16[32,1792]{1,0:T(8,128)(2,1)S(1)} %pad_maximum_fusion.5), channel_id=1, source_target_pairs={{0,12},{4,0},{8,4},{12,8},{1,13},{5,1},{9,5},{13,9},{2,14},{6,2},{... | collective-permute-start | bytes 344072 | tf_op jit(solution)/shard_map/ppermute | solution.py:167
  90.8 2.7 %fusion.38 = bf16[32,896]{1,0:T(8,128)(2,1)S(1)} fusion(bf16[32,2048]{1,0:T(8,128)(2,1)S(1)} %get-tuple-element.58, bf16[2048,3584]{1,0:T(8,128)(2,1)} %param.27, s32[]{:T(128)S(6)} %select_n.211), kind=kOutput, calls=%fused_computation.34 | convolution fusion | flops 117469184 | bytes 3858436 | tf_op jit(solution)/shard_map/dot_general | solution.py:156
  93.9 2.4 %collective-permute-done.17 = bf16[32,1792]{1,0:T(8,128)(2,1)S(1)} collective-permute-done((bf16[32,1792]{1,0:T(8,128)(2,1)S(1)}, bf16[32,1792]{1,0:T(8,128)(2,1)S(1)}, u32[]{:S(2)}, u32[]{:S(2)}) %collective-permute-start.17) | collective-permute-done | bytes 114720 | tf_op jit(solution)/shard_map/ppermute | solution.py:167
  96.5 2.6 %collective-permute-start.21 = (bf16[32,896]{1,0:T(8,128)(2,1)S(1)}, bf16[32,896]{1,0:T(8,128)(2,1)S(1)}, u32[]{:S(2)}, u32[]{:S(2)}) collective-permute-start(bf16[32,896]{1,0:T(8,128)(2,1)S(1)} %fusion.70), channel_id=1, source_target_pairs={{0,12},{4,0},{8,4},{12,8},{1,13},{5,1},{9,5},{13,9},{2,14},{6,2},{... | collective-permute-start | bytes 172040 | tf_op jit(solution)/shard_map/ppermute | solution.py:180
  100.8 3.6 %collective-permute-done.20 = bf16[32,896]{1,0:T(8,128)(2,1)S(1)} collective-permute-done((bf16[32,896]{1,0:T(8,128)(2,1)S(1)}, bf16[32,896]{1,0:T(8,128)(2,1)S(1)}, u32[]{:S(2)}, u32[]{:S(2)}) %collective-permute-start.20) | collective-permute-done | bytes 57376 | tf_op jit(solution)/shard_map/ppermute | solution.py:180
  107.0 1.3 %collective-permute-done.22 = f32[2,8,2048]{2,1,0:T(8,128)S(1)} collective-permute-done((f32[2,8,2048]{2,1,0:T(8,128)S(1)}, f32[2,8,2048]{2,1,0:T(8,128)S(1)}, u32[]{:S(2)}, u32[]{:S(2)}) %collective-permute-start.22) | collective-permute-done | bytes 131104 | tf_op jit(solution)/shard_map/ppermute | solution.py:113
  109.3 3.4 %collective-permute-done.23 = f32[8,2048]{1,0:T(8,128)S(1)} collective-permute-done((f32[8,2048]{1,0:T(8,128)S(1)}, f32[8,2048]{1,0:T(8,128)S(1)}, u32[]{:S(2)}, u32[]{:S(2)}) %collective-permute-start.23) | collective-permute-done | bytes 65568 | tf_op jit(solution)/shard_map/ppermute | solution.py:113
  (109 shorter events, 22.5 us)
Async XLA Ops:
  0.0 27.9 %copy-start = (bf16[8,256,2,2,128]{4,3,2,1,0:T(2,128)(2,1)S(1)}, bf16[8,256,2,2,128]{4,3,2,1,0:T(2,128)(2,1)}, u32[]{:S(2)}) copy-start(bf16[8,256,2,2,128]{4,3,2,1,0:T(2,128)(2,1)} %param.30) | copy-start | bytes 6291460
  1.0 5.2 %collective-permute-start = (f32[8]{0:T(128)S(1)}, f32[8]{0:T(128)S(1)}, u32[]{:S(2)}, u32[]{:S(2)}) collective-permute-start(f32[8]{0:T(128)S(1)} %fusion.74), channel_id=1, source_target_pairs={{0,4},{4,0},{8,12},{12,8},{1,5},{5,1},{9,13},{13,9},{2,6},{6,2},{1... | collective-permute-start | bytes 104 | tf_op jit(solution)/shard_map/ppermute | solution.py:141
  6.2 4.5 %collective-permute-start.1 = (f32[8]{0:T(128)S(1)}, f32[8]{0:T(128)S(1)}, u32[]{:S(2)}, u32[]{:S(2)}) collective-permute-start(f32[8]{0:T(128)S(1)} %add.255), channel_id=1, source_target_pairs={{0,8},{4,12},{8,0},{12,4},{1,9},{5,13},{9,1},{13,5},{2,10},{6,14},... | collective-permute-start | bytes 104 | tf_op jit(solution)/shard_map/ppermute | solution.py:141
  11.6 1.8 %collective-permute-start.4 = (bf16[8,2048]{1,0:T(8,128)(2,1)S(1)}, bf16[8,2048]{1,0:T(8,128)(2,1)S(1)}, u32[]{:S(2)}, u32[]{:S(2)}) collective-permute-start(bf16[8,2048]{1,0:T(8,128)(2,1)S(1)} %fusion.76), channel_id=1, source_target_pairs={{0,3},{1,0},{2,1},{3,2},{4,7},{5,4},{6,5},{7,6},{8,11},{9,8},{10,9... | collective-permute-start | bytes 98312 | tf_op jit(solution)/shard_map/ppermute | solution.py:97
  11.6 4.1 %collective-permute-start.3 = (bf16[8,2048]{1,0:T(8,128)(2,1)S(1)}, bf16[8,2048]{1,0:T(8,128)(2,1)S(1)}, u32[]{:S(2)}, u32[]{:S(2)}) collective-permute-start(bf16[8,2048]{1,0:T(8,128)(2,1)S(1)} %fusion.76), channel_id=1, source_target_pairs={{0,2},{1,3},{2,0},{3,1},{4,6},{5,7},{6,4},{7,5},{8,10},{9,11},{10,... | collective-permute-start | bytes 98312 | tf_op jit(solution)/shard_map/ppermute | solution.py:97
  13.2 3.3 %collective-permute-start.2 = (bf16[8,2048]{1,0:T(8,128)(2,1)S(1)}, bf16[8,2048]{1,0:T(8,128)(2,1)S(1)}, u32[]{:S(2)}, u32[]{:S(2)}) collective-permute-start(bf16[8,2048]{1,0:T(8,128)(2,1)S(1)} %fusion.76), channel_id=1, source_target_pairs={{0,1},{1,2},{2,3},{3,0},{4,5},{5,6},{6,7},{7,4},{8,9},{9,10},{10,1... | collective-permute-start | bytes 98312 | tf_op jit(solution)/shard_map/ppermute | solution.py:97
  23.2 7.2 %collective-permute-start.5 = (f32[8,2560]{1,0:T(8,128)S(1)}, f32[8,2560]{1,0:T(8,128)S(1)}, u32[]{:S(2)}, u32[]{:S(2)}) collective-permute-start(f32[8,2560]{1,0:T(8,128)S(1)} %get-tuple-element.64), channel_id=1, source_target_pairs={{0,4},{4,8},{8,12},{12,0},{1,5},{5,9},{9,13},{13,1},{2,6},{6,10},{... | collective-permute-start | bytes 245768 | tf_op jit(solution)/shard_map/ppermute | solution.py:113
  24.6 5.8 %collective-permute-start.7 = (f32[8,2560]{1,0:T(8,128)S(1)}, f32[8,2560]{1,0:T(8,128)S(1)}, u32[]{:S(2)}, u32[]{:S(2)}) collective-permute-start(f32[8,2560]{1,0:T(8,128)S(1)} %get-tuple-element.65), channel_id=1, source_target_pairs={{0,12},{4,0},{8,4},{12,8},{1,13},{5,1},{9,5},{13,9},{2,14},{6,2},{... | collective-permute-start | bytes 245768 | tf_op jit(solution)/shard_map/ppermute | solution.py:113
  27.1 7.0 %collective-permute-start.6 = (f32[8,2560]{1,0:T(8,128)S(1)}, f32[8,2560]{1,0:T(8,128)S(1)}, u32[]{:S(2)}, u32[]{:S(2)}) collective-permute-start(f32[8,2560]{1,0:T(8,128)S(1)} %get-tuple-element.66), channel_id=1, source_target_pairs={{0,8},{4,12},{8,0},{12,4},{1,9},{5,13},{9,1},{13,5},{2,10},{6,14},... | collective-permute-start | bytes 245768 | tf_op jit(solution)/shard_map/ppermute | solution.py:113
  35.5 13.8 %copy-start.1 = (bf16[8,2048]{1,0:T(8,128)(2,1)S(1)}, bf16[8,2048]{1,0:T(8,128)(2,1)}, u32[]{:S(2)}) copy-start(bf16[8,2048]{1,0:T(8,128)(2,1)} %param.22) | copy-start | bytes 98308
  35.5 4.0 %collective-permute-start.10 = (bf16[8,2048]{1,0:T(8,128)(2,1)S(1)}, bf16[8,2048]{1,0:T(8,128)(2,1)S(1)}, u32[]{:S(2)}, u32[]{:S(2)}) collective-permute-start(bf16[8,2048]{1,0:T(8,128)(2,1)S(1)} %bitcast.101), channel_id=1, source_target_pairs={{0,12},{4,0},{8,4},{12,8},{1,13},{5,1},{9,5},{13,9},{2,14},{6,2},{... | collective-permute-start | bytes 98312 | tf_op jit(solution)/shard_map/ppermute | solution.py:97
  37.9 4.8 %collective-permute-start.9 = (bf16[8,2048]{1,0:T(8,128)(2,1)S(1)}, bf16[8,2048]{1,0:T(8,128)(2,1)S(1)}, u32[]{:S(2)}, u32[]{:S(2)}) collective-permute-start(bf16[8,2048]{1,0:T(8,128)(2,1)S(1)} %bitcast.102), channel_id=1, source_target_pairs={{0,8},{4,12},{8,0},{12,4},{1,9},{5,13},{9,1},{13,5},{2,10},{6,14},... | collective-permute-start | bytes 98312 | tf_op jit(solution)/shard_map/ppermute | solution.py:97
  37.9 5.7 %collective-permute-start.8 = (bf16[8,2048]{1,0:T(8,128)(2,1)S(1)}, bf16[8,2048]{1,0:T(8,128)(2,1)S(1)}, u32[]{:S(2)}, u32[]{:S(2)}) collective-permute-start(bf16[8,2048]{1,0:T(8,128)(2,1)S(1)} %bitcast.103), channel_id=1, source_target_pairs={{0,4},{4,8},{8,12},{12,0},{1,5},{5,9},{9,13},{13,1},{2,6},{6,10},{... | collective-permute-start | bytes 98312 | tf_op jit(solution)/shard_map/ppermute | solution.py:97
  44.3 22.4 %copy-start.2 = (f32[2048]{0:T(1024)S(1)}, f32[2048]{0:T(1024)}, u32[]{:S(2)}) copy-start(f32[2048]{0:T(1024)} %param.26) | copy-start | bytes 24580
  49.4 1.4 %collective-permute-start.11 = (f32[16,2048]{1,0:T(8,128)S(1)}, f32[16,2048]{1,0:T(8,128)S(1)}, u32[]{:S(2)}, u32[]{:S(2)}) collective-permute-start(f32[16,2048]{1,0:T(8,128)S(1)} %select_bitcast_fusion.1), channel_id=1, source_target_pairs={{0,1},{1,0},{2,3},{3,2},{4,5},{5,4},{6,7},{7,6},{8,9},{9,8},{10,11... | collective-permute-start | bytes 393224 | tf_op jit(solution)/shard_map/ppermute | solution.py:113
  50.8 5.6 %collective-permute-start.12 = (f32[16,2048]{1,0:T(8,128)S(1)}, f32[16,2048]{1,0:T(8,128)S(1)}, u32[]{:S(2)}, u32[]{:S(2)}) collective-permute-start(f32[16,2048]{1,0:T(8,128)S(1)} %bitcast_add_fusion.1), channel_id=1, source_target_pairs={{0,2},{2,0},{1,3},{3,1},{4,6},{6,4},{5,7},{7,5},{8,10},{10,8},{9,1... | collective-permute-start | bytes 393224 | tf_op jit(solution)/shard_map/ppermute | solution.py:141
  56.4 1.4 %collective-permute-start.13 = (f32[16,2048]{1,0:T(8,128)S(1)}, f32[16,2048]{1,0:T(8,128)S(1)}, u32[]{:S(2)}, u32[]{:S(2)}) collective-permute-start(f32[16,2048]{1,0:T(8,128)S(1)} %add.282), channel_id=1, source_target_pairs={{0,1},{1,0},{2,3},{3,2},{4,5},{5,4},{6,7},{7,6},{8,9},{9,8},{10,11... | collective-permute-start | bytes 393224 | tf_op jit(solution)/shard_map/ppermute | solution.py:131
  58.7 3.5 %collective-permute-start.14 = (f32[32]{0:T(128)S(1)}, f32[32]{0:T(128)S(1)}, u32[]{:S(2)}, u32[]{:S(2)}) collective-permute-start(f32[32]{0:T(128)S(1)} %reduce_sum.62), channel_id=1, source_target_pairs={{0,4},{4,0},{8,12},{12,8},{1,5},{5,1},{9,13},{13,9},{2,6},{6,2},{1... | collective-permute-start | bytes 392 | tf_op jit(solution)/shard_map/ppermute | solution.py:141
  62.3 4.4 %collective-permute-start.15 = (f32[32]{0:T(128)S(1)}, f32[32]{0:T(128)S(1)}, u32[]{:S(2)}, u32[]{:S(2)}) collective-permute-start(f32[32]{0:T(128)S(1)} %add.285), channel_id=1, source_target_pairs={{0,8},{4,12},{8,0},{12,4},{1,9},{5,13},{9,1},{13,5},{2,10},{6,14},... | collective-permute-start | bytes 392 | tf_op jit(solution)/shard_map/ppermute | solution.py:141
  69.5 30.5 %slice-start = ((s8[14680064]{0:T(1024)(128)(4,1)}), s8[4194304]{0:T(1024)(128)(4,1)S(1)}, s32[]{:S(2)}) async-start(s8[14680064]{0:T(1024)(128)(4,1)} %bitcast.85), calls=%async_computation | async-start | bytes 8388608
  72.4 27.6 %slice-start.1 = ((s8[14680064]{0:T(1024)(128)(4,1)}), s8[4194304]{0:T(1024)(128)(4,1)S(1)}, s32[]{:S(2)}) async-start(s8[14680064]{0:T(1024)(128)(4,1)} %bitcast.85), calls=%async_computation.1 | async-start | bytes 8388608
  78.0 22.0 %slice-start.2 = ((s8[14680064]{0:T(1024)(128)(4,1)}), s8[4194304]{0:T(1024)(128)(4,1)S(1)}, s32[]{:S(2)}) async-start(s8[14680064]{0:T(1024)(128)(4,1)} %bitcast.85), calls=%async_computation.2 | async-start | bytes 8388608
  83.6 16.4 %slice-start.3 = ((s8[14680064]{0:T(1024)(128)(4,1)}), s8[2097152]{0:T(1024)(128)(4,1)S(1)}, s32[]{:S(2)}) async-start(s8[14680064]{0:T(1024)(128)(4,1)} %bitcast.85), calls=%async_computation.3 | async-start | bytes 4194304
  86.5 7.4 %collective-permute-start.16 = (bf16[32,1792]{1,0:T(8,128)(2,1)S(1)}, bf16[32,1792]{1,0:T(8,128)(2,1)S(1)}, u32[]{:S(2)}, u32[]{:S(2)}) collective-permute-start(bf16[32,1792]{1,0:T(8,128)(2,1)S(1)} %pad_maximum_fusion.3), channel_id=1, source_target_pairs={{0,4},{4,8},{8,12},{12,0},{1,5},{5,9},{9,13},{13,1},{2,6},{6,10},{... | collective-permute-start | bytes 344072 | tf_op jit(solution)/shard_map/ppermute | solution.py:167
  86.6 9.7 %collective-permute-start.17 = (bf16[32,1792]{1,0:T(8,128)(2,1)S(1)}, bf16[32,1792]{1,0:T(8,128)(2,1)S(1)}, u32[]{:S(2)}, u32[]{:S(2)}) collective-permute-start(bf16[32,1792]{1,0:T(8,128)(2,1)S(1)} %pad_maximum_fusion.4), channel_id=1, source_target_pairs={{0,8},{4,12},{8,0},{12,4},{1,9},{5,13},{9,1},{13,5},{2,10},{6,14},... | collective-permute-start | bytes 344072 | tf_op jit(solution)/shard_map/ppermute | solution.py:167
  87.8 8.5 %collective-permute-start.18 = (bf16[32,1792]{1,0:T(8,128)(2,1)S(1)}, bf16[32,1792]{1,0:T(8,128)(2,1)S(1)}, u32[]{:S(2)}, u32[]{:S(2)}) collective-permute-start(bf16[32,1792]{1,0:T(8,128)(2,1)S(1)} %pad_maximum_fusion.5), channel_id=1, source_target_pairs={{0,12},{4,0},{8,4},{12,8},{1,13},{5,1},{9,5},{13,9},{2,14},{6,2},{... | collective-permute-start | bytes 344072 | tf_op jit(solution)/shard_map/ppermute | solution.py:167
  96.5 8.7 %collective-permute-start.21 = (bf16[32,896]{1,0:T(8,128)(2,1)S(1)}, bf16[32,896]{1,0:T(8,128)(2,1)S(1)}, u32[]{:S(2)}, u32[]{:S(2)}) collective-permute-start(bf16[32,896]{1,0:T(8,128)(2,1)S(1)} %fusion.70), channel_id=1, source_target_pairs={{0,12},{4,0},{8,4},{12,8},{1,13},{5,1},{9,5},{13,9},{2,14},{6,2},{... | collective-permute-start | bytes 172040 | tf_op jit(solution)/shard_map/ppermute | solution.py:180
  99.1 5.3 %collective-permute-start.20 = (bf16[32,896]{1,0:T(8,128)(2,1)S(1)}, bf16[32,896]{1,0:T(8,128)(2,1)S(1)}, u32[]{:S(2)}, u32[]{:S(2)}) collective-permute-start(bf16[32,896]{1,0:T(8,128)(2,1)S(1)} %fusion.70), channel_id=1, source_target_pairs={{0,8},{4,12},{8,0},{12,4},{1,9},{5,13},{9,1},{13,5},{2,10},{6,14},... | collective-permute-start | bytes 172040 | tf_op jit(solution)/shard_map/ppermute | solution.py:180
  100.0 6.0 %collective-permute-start.19 = (bf16[32,896]{1,0:T(8,128)(2,1)S(1)}, bf16[32,896]{1,0:T(8,128)(2,1)S(1)}, u32[]{:S(2)}, u32[]{:S(2)}) collective-permute-start(bf16[32,896]{1,0:T(8,128)(2,1)S(1)} %fusion.70), channel_id=1, source_target_pairs={{0,4},{4,8},{8,12},{12,0},{1,5},{5,9},{9,13},{13,1},{2,6},{6,10},{... | collective-permute-start | bytes 172040 | tf_op jit(solution)/shard_map/ppermute | solution.py:180
  106.9 1.4 %collective-permute-start.22 = (f32[2,8,2048]{2,1,0:T(8,128)S(1)}, f32[2,8,2048]{2,1,0:T(8,128)S(1)}, u32[]{:S(2)}, u32[]{:S(2)}) collective-permute-start(f32[2,8,2048]{2,1,0:T(8,128)S(1)} %select_bitcast_fusion), channel_id=1, source_target_pairs={{0,1},{1,0},{2,3},{3,2},{4,5},{5,4},{6,7},{7,6},{8,9},{9,8},{10,11... | collective-permute-start | bytes 393224 | tf_op jit(solution)/shard_map/ppermute | solution.py:113
  108.3 4.3 %collective-permute-start.23 = (f32[8,2048]{1,0:T(8,128)S(1)}, f32[8,2048]{1,0:T(8,128)S(1)}, u32[]{:S(2)}, u32[]{:S(2)}) collective-permute-start(f32[8,2048]{1,0:T(8,128)S(1)} %select_bitcast_fusion.5), channel_id=1, source_target_pairs={{0,2},{2,0},{1,3},{3,1},{4,6},{6,4},{5,7},{7,5},{8,10},{10,8},{9,1... | collective-permute-start | bytes 196616 | tf_op jit(solution)/shard_map/ppermute | solution.py:113

commit v13 on v11

--- a/solution.py
+++ b/solution.py
@@ -156,9 +156,11 @@
         ]
         return jnp.concatenate(parts, axis=1)
 
+    pieces = [block((idx + k) % n) for k in range(1, n)]
+    pieces, x = lax.optimization_barrier((pieces, x))
     total = None
     for k in range(1, n):
-        got = lax.ppermute(block((idx + k) % n), axis, shift_pairs(n, k)).astype(jnp.float32)
+        got = lax.ppermute(pieces[k - 1], axis, shift_pairs(n, k)).astype(jnp.float32)
         total = got if total is None else total + got
     own = block(idx).astype(jnp.float32)
     return own if total is None else own + total

time: 113 us -> 110 us (0.973)
  waiting for transfers between devices: 39 us -> 36.4 us
    ppermute x3, waiting for transfers between devices: 3.94 us -> 1.38 us  [scatter_matmul(): lax.ppermute(pieces[k - 1], axis, shift_pairs(n, k)).astype(jnp.float32)]
  transfers between devices with their start and end apart: 26 -> 26, of which waited for: 20 -> 19; matrix products, arithmetic and copies ran while one was open for 7% -> 10% of each run, Pallas kernels for 0% -> 0%
where the time goes in v13:
time: 110 us; the launch traced here: 109 us
  matrix products  37 us (34%)
  waiting for transfers between devices  36.4 us (33%)
  starting transfers between devices  26.9 us (24%)
  other arithmetic  5.69 us (5%)
  local copies, waits for them, and re-layouts  2.73 us (2%)
    dot_general x8, matrix products, block(): jnp.dot(x, lax.dynamic_slice_in_dim(w, j * chunk, chunk, 1), preferred_el...  22.1 us
    ppermute x6, waiting for transfers between devices, scatter_sum(): lax.ppermute(piece, axis, shift_pairs(n, k)).astype(jnp.float32)  11.6 us
    ppermute x7, waiting for transfers between devices, all_sum(): total = total + lax.ppermute(x, axis, shift_pairs(n, k))  10.3 us
    ppermute x7, starting transfers between devices, all_sum(): total = total + lax.ppermute(x, axis, shift_pairs(n, k))  10.2 us
    ppermute x6, waiting for transfers between devices, gather_rows(): got = [x] + [lax.ppermute(x, axis, shift_pairs(n, k)) for k in range(1, n)]  8.23 us
    dot_general x1, matrix products, local(): jnp.einsum('rf,fgc->rgc', by_slot, w_qkv, preferred_element_type=jnp.floa...  5.94 us
    dot_general x1, matrix products, local(): out_part = jnp.dot(by_row, w_out, preferred_element_type=jnp.float32)  4.99 us
    ppermute x6, starting transfers between devices, scatter_sum(): lax.ppermute(piece, axis, shift_pairs(n, k)).astype(jnp.float32)  4.98 us
  transfers between devices with their start and end apart: 26, of which 19 were waited for; matrix products, arithmetic and copies ran while one was open for 10% of the time, Pallas kernels for 0%

profile of v13, /device:TPU:0, one launch (start us, length us, event | category | flops | bytes accessed | tf_op | source)
XLA Modules:
  0.0 109.4 jit_solution(17210523760346057761)
XLA Ops:
  1.0 5.1 %collective-permute-start.2 = (f32[8]{0:T(128)S(1)}, f32[8]{0:T(128)S(1)}, u32[]{:S(2)}, u32[]{:S(2)}) collective-permute-start(f32[8]{0:T(128)S(1)} %fusion.74), channel_id=1, source_target_pairs={{0,12},{4,0},{8,4},{12,8},{1,13},{5,1},{9,5},{13,9},{2,14},{6,2},{... | collective-permute-start | bytes 104 | tf_op jit(solution)/shard_map/ppermute | solution.py:140
  9.2 1.3 %collective-permute-done.1 = f32[8]{0:T(128)S(1)} collective-permute-done((f32[8]{0:T(128)S(1)}, f32[8]{0:T(128)S(1)}, u32[]{:S(2)}, u32[]{:S(2)}) %collective-permute-start.1) | collective-permute-done | bytes 64 | tf_op jit(solution)/shard_map/ppermute | solution.py:140
  12.4 1.6 %collective-permute-start.4 = (bf16[8,2048]{1,0:T(8,128)(2,1)S(1)}, bf16[8,2048]{1,0:T(8,128)(2,1)S(1)}, u32[]{:S(2)}, u32[]{:S(2)}) collective-permute-start(bf16[8,2048]{1,0:T(8,128)(2,1)S(1)} %fusion.76), channel_id=1, source_target_pairs={{0,2},{1,3},{2,0},{3,1},{4,6},{5,7},{6,4},{7,5},{8,10},{9,11},{10,... | collective-permute-start | bytes 98312 | tf_op jit(solution)/shard_map/ppermute | solution.py:97
  14.1 2.3 %collective-permute-done.4 = bf16[8,2048]{1,0:T(8,128)(2,1)S(1)} collective-permute-done((bf16[8,2048]{1,0:T(8,128)(2,1)S(1)}, bf16[8,2048]{1,0:T(8,128)(2,1)S(1)}, u32[]{:S(2)}, u32[]{:S(2)}) %collective-permute-start.4) | collective-permute-done | bytes 32800 | tf_op jit(solution)/shard_map/ppermute | solution.py:97
  18.0 5.9 %fusion.26 = f32[2,4,8,1280]{3,2,1,0:T(8,128)S(1)} fusion(bf16[2048,2,1280]{2,1,0:T(2,128)(2,1)} %param.24, bf16[32,2048]{1,0:T(8,128)(2,1)S(1)} %gather_fusion.1, pred[32]{0:T(512)(128)(4,1)S(1)} %get-tuple-element.70), kind=kOutput, calls=%fused_computation.29 | convolution fusion | flops 335609856 | bytes 10944544 | tf_op jit(solution)/shard_map/rf,fgc->rgc/dot_general | solution.py:215
  24.3 3.6 %collective-permute-start.8 = (f32[8,2560]{1,0:T(8,128)S(1)}, f32[8,2560]{1,0:T(8,128)S(1)}, u32[]{:S(2)}, u32[]{:S(2)}) collective-permute-start(f32[8,2560]{1,0:T(8,128)S(1)} %get-tuple-element.73), channel_id=1, source_target_pairs={{0,12},{4,0},{8,4},{12,8},{1,13},{5,1},{9,5},{13,9},{2,14},{6,2},{... | collective-permute-start | bytes 245768 | tf_op jit(solution)/shard_map/ppermute | solution.py:113
  28.4 2.7 %collective-permute-done.6 = f32[8,2560]{1,0:T(8,128)S(1)} collective-permute-done((f32[8,2560]{1,0:T(8,128)S(1)}, f32[8,2560]{1,0:T(8,128)S(1)}, u32[]{:S(2)}, u32[]{:S(2)}) %collective-permute-start.6) | collective-permute-done | bytes 81952 | tf_op jit(solution)/shard_map/ppermute | solution.py:113
  31.1 2.9 %collective-permute-done.7 = f32[8,2560]{1,0:T(8,128)S(1)} collective-permute-done((f32[8,2560]{1,0:T(8,128)S(1)}, f32[8,2560]{1,0:T(8,128)S(1)}, u32[]{:S(2)}, u32[]{:S(2)}) %collective-permute-start.7) | collective-permute-done | bytes 81952 | tf_op jit(solution)/shard_map/ppermute | solution.py:113
  35.4 1.8 %collective-permute-start.11 = (bf16[8,2048]{1,0:T(8,128)(2,1)S(1)}, bf16[8,2048]{1,0:T(8,128)(2,1)S(1)}, u32[]{:S(2)}, u32[]{:S(2)}) collective-permute-start(bf16[8,2048]{1,0:T(8,128)(2,1)S(1)} %bitcast.101), channel_id=1, source_target_pairs={{0,12},{4,0},{8,4},{12,8},{1,13},{5,1},{9,5},{13,9},{2,14},{6,2},{... | collective-permute-start | bytes 98312 | tf_op jit(solution)/shard_map/ppermute | solution.py:97
  37.9 1.5 %collective-permute-done.11 = bf16[8,2048]{1,0:T(8,128)(2,1)S(1)} collective-permute-done((bf16[8,2048]{1,0:T(8,128)(2,1)S(1)}, bf16[8,2048]{1,0:T(8,128)(2,1)S(1)}, u32[]{:S(2)}, u32[]{:S(2)}) %collective-permute-start.11) | collective-permute-done | bytes 32800 | tf_op jit(solution)/shard_map/ppermute | solution.py:97
  39.4 2.7 %collective-permute-done.10 = bf16[8,2048]{1,0:T(8,128)(2,1)S(1)} collective-permute-done((bf16[8,2048]{1,0:T(8,128)(2,1)S(1)}, bf16[8,2048]{1,0:T(8,128)(2,1)S(1)}, u32[]{:S(2)}, u32[]{:S(2)}) %collective-permute-start.10) | collective-permute-done | bytes 32800 | tf_op jit(solution)/shard_map/ppermute | solution.py:97
  43.7 5.0 %fusion.65 = f32[32,2048]{1,0:T(8,128)S(1)} fusion(bf16[2048,2048]{1,0:T(8,128)(2,1)} %param.25, bf16[32,2048]{1,0:T(8,128)(2,1)S(1)} %gather_fusion.2, pred[32]{0:T(512)(128)(4,1)S(1)} %get-tuple-element.68), kind=kOutput, calls=%fused_computation.60 | convolution fusion | flops 268500992 | bytes 8781856 | tf_op jit(solution)/shard_map/dot_general | solution.py:223
  48.8 1.3 %collective-permute-done.12 = f32[16,2048]{1,0:T(8,128)S(1)} collective-permute-done((f32[16,2048]{1,0:T(8,128)S(1)}, f32[16,2048]{1,0:T(8,128)S(1)}, u32[]{:S(2)}, u32[]{:S(2)}) %collective-permute-start.12) | collective-permute-done | bytes 131104 | tf_op jit(solution)/shard_map/ppermute | solution.py:113
  51.1 4.6 %collective-permute-done.13 = f32[16,2048]{1,0:T(8,128)S(1)} collective-permute-done((f32[16,2048]{1,0:T(8,128)S(1)}, f32[16,2048]{1,0:T(8,128)S(1)}, u32[]{:S(2)}, u32[]{:S(2)}) %collective-permute-start.13) | collective-permute-done | bytes 131104 | tf_op jit(solution)/shard_map/ppermute | solution.py:140
  59.2 2.0 %collective-permute-start.15 = (f32[32]{0:T(128)S(1)}, f32[32]{0:T(128)S(1)}, u32[]{:S(2)}, u32[]{:S(2)}) collective-permute-start(f32[32]{0:T(128)S(1)} %reduce_sum.62), channel_id=1, source_target_pairs={{0,4},{4,8},{8,12},{12,0},{1,5},{5,9},{9,13},{13,1},{2,6},{6,10},{... | collective-permute-start | bytes 392 | tf_op jit(solution)/shard_map/ppermute | solution.py:140
  61.6 1.7 %collective-permute-done.16 = f32[32]{0:T(128)S(1)} collective-permute-done((f32[32]{0:T(128)S(1)}, f32[32]{0:T(128)S(1)}, u32[]{:S(2)}, u32[]{:S(2)}) %collective-permute-start.16) | collective-permute-done | bytes 160 | tf_op jit(solution)/shard_map/ppermute | solution.py:140
  63.3 1.3 %collective-permute-done.15 = f32[32]{0:T(128)S(1)} collective-permute-done((f32[32]{0:T(128)S(1)}, f32[32]{0:T(128)S(1)}, u32[]{:S(2)}, u32[]{:S(2)}) %collective-permute-start.15) | collective-permute-done | bytes 160 | tf_op jit(solution)/shard_map/ppermute | solution.py:140
  64.7 2.7 %fusion.53 = bf16[32,896]{1,0:T(8,128)(2,1)S(1)} fusion(bf16[32,2048]{1,0:T(8,128)(2,1)S(1)} %get-tuple-element.18, bf16[2048,3584]{1,0:T(8,128)(2,1)} %param.28, s32[]{:T(128)S(6)} %select_n.213), kind=kOutput, calls=%fused_computation.39 | convolution fusion | flops 117469184 | bytes 3858436 | tf_op jit(solution)/shard_map/dot_general | solution.py:150
  67.4 2.9 %fusion.50 = bf16[32,896]{1,0:T(8,128)(2,1)S(1)} fusion(bf16[32,2048]{1,0:T(8,128)(2,1)S(1)} %get-tuple-element.18, bf16[2048,3584]{1,0:T(8,128)(2,1)} %param.27, s32[]{:T(128)S(6)} %select_n.213), kind=kOutput, calls=%fused_computation.38 | convolution fusion | flops 117469184 | bytes 3858436 | tf_op jit(solution)/shard_map/dot_general | solution.py:150
  70.3 2.9 %fusion.47 = bf16[32,896]{1,0:T(8,128)(2,1)S(1)} fusion(bf16[32,2048]{1,0:T(8,128)(2,1)S(1)} %get-tuple-element.18, bf16[2048,3584]{1,0:T(8,128)(2,1)} %param.28, s32[]{:T(128)S(6)} %select_n.212), kind=kOutput, calls=%fused_computation.37 | convolution fusion | flops 117469184 | bytes 3858436 | tf_op jit(solution)/shard_map/dot_general | solution.py:150
  73.2 2.7 %fusion.44 = bf16[32,896]{1,0:T(8,128)(2,1)S(1)} fusion(bf16[32,2048]{1,0:T(8,128)(2,1)S(1)} %get-tuple-element.18, bf16[2048,3584]{1,0:T(8,128)(2,1)} %param.27, s32[]{:T(128)S(6)} %select_n.212), kind=kOutput, calls=%fused_computation.36 | convolution fusion | flops 117469184 | bytes 3858436 | tf_op jit(solution)/shard_map/dot_general | solution.py:150
  75.9 2.9 %fusion.41 = bf16[32,896]{1,0:T(8,128)(2,1)S(1)} fusion(bf16[32,2048]{1,0:T(8,128)(2,1)S(1)} %get-tuple-element.18, bf16[2048,3584]{1,0:T(8,128)(2,1)} %param.28, s32[]{:T(128)S(6)} %select_n.211), kind=kOutput, calls=%fused_computation.35 | convolution fusion | flops 117469184 | bytes 3858436 | tf_op jit(solution)/shard_map/dot_general | solution.py:150
  78.8 2.7 %fusion.38 = bf16[32,896]{1,0:T(8,128)(2,1)S(1)} fusion(bf16[32,2048]{1,0:T(8,128)(2,1)S(1)} %get-tuple-element.18, bf16[2048,3584]{1,0:T(8,128)(2,1)} %param.27, s32[]{:T(128)S(6)} %select_n.211), kind=kOutput, calls=%fused_computation.34 | convolution fusion | flops 117469184 | bytes 3858436 | tf_op jit(solution)/shard_map/dot_general | solution.py:150
  81.8 1.8 %collective-permute-start.19 = (bf16[32,1792]{1,0:T(8,128)(2,1)S(1)}, bf16[32,1792]{1,0:T(8,128)(2,1)S(1)}, u32[]{:S(2)}, u32[]{:S(2)}) collective-permute-start(bf16[32,1792]{1,0:T(8,128)(2,1)S(1)} %get-tuple-element.20), channel_id=1, source_target_pairs={{0,8},{4,12},{8,0},{12,4},{1,9},{5,13},{9,1},{13,5},{2,10},{6,14},... | collective-permute-start | bytes 344072 | tf_op jit(solution)/shard_map/ppermute | solution.py:163
  83.6 1.8 %collective-permute-start.20 = (bf16[32,1792]{1,0:T(8,128)(2,1)S(1)}, bf16[32,1792]{1,0:T(8,128)(2,1)S(1)}, u32[]{:S(2)}, u32[]{:S(2)}) collective-permute-start(bf16[32,1792]{1,0:T(8,128)(2,1)S(1)} %pad_maximum_fusion.5), channel_id=1, source_target_pairs={{0,12},{4,0},{8,4},{12,8},{1,13},{5,1},{9,5},{13,9},{2,14},{6,2},{... | collective-permute-start | bytes 344072 | tf_op jit(solution)/shard_map/ppermute | solution.py:163
  85.4 2.7 %fusion.59 = bf16[32,896]{1,0:T(8,128)(2,1)S(1)} fusion(bf16[32,2048]{1,0:T(8,128)(2,1)S(1)} %get-tuple-element.18, bf16[2048,3584]{1,0:T(8,128)(2,1)} %param.28, s32[]{:T(128)S(6)} %select_n.214), kind=kOutput, calls=%fused_computation.41 | convolution fusion | flops 117469184 | bytes 3858436 | tf_op jit(solution)/shard_map/dot_general | solution.py:150
  88.2 2.7 %fusion.56 = bf16[32,896]{1,0:T(8,128)(2,1)S(1)} fusion(bf16[32,2048]{1,0:T(8,128)(2,1)S(1)} %get-tuple-element.18, bf16[2048,3584]{1,0:T(8,128)(2,1)} %param.27, s32[]{:T(128)S(6)} %select_n.214), kind=kOutput, calls=%fused_computation.40 | convolution fusion | flops 117469184 | bytes 3858436 | tf_op jit(solution)/shard_map/dot_general | solution.py:150
  90.9 1.4 %collective-permute-done.19 = bf16[32,1792]{1,0:T(8,128)(2,1)S(1)} collective-permute-done((bf16[32,1792]{1,0:T(8,128)(2,1)S(1)}, bf16[32,1792]{1,0:T(8,128)(2,1)S(1)}, u32[]{:S(2)}, u32[]{:S(2)}) %collective-permute-start.19) | collective-permute-done | bytes 114720 | tf_op jit(solution)/shard_map/ppermute | solution.py:163
  92.4 2.6 %collective-permute-start.23 = (bf16[32,896]{1,0:T(8,128)(2,1)S(1)}, bf16[32,896]{1,0:T(8,128)(2,1)S(1)}, u32[]{:S(2)}, u32[]{:S(2)}) collective-permute-start(bf16[32,896]{1,0:T(8,128)(2,1)S(1)} %fusion.70), channel_id=1, source_target_pairs={{0,12},{4,0},{8,4},{12,8},{1,13},{5,1},{9,5},{13,9},{2,14},{6,2},{... | collective-permute-start | bytes 172040 | tf_op jit(solution)/shard_map/ppermute | solution.py:176
  96.7 3.9 %collective-permute-done.22 = bf16[32,896]{1,0:T(8,128)(2,1)S(1)} collective-permute-done((bf16[32,896]{1,0:T(8,128)(2,1)S(1)}, bf16[32,896]{1,0:T(8,128)(2,1)S(1)}, u32[]{:S(2)}, u32[]{:S(2)}) %collective-permute-start.22) | collective-permute-done | bytes 57376 | tf_op jit(solution)/shard_map/ppermute | solution.py:176
  103.0 1.3 %collective-permute-done.24 = f32[2,8,2048]{2,1,0:T(8,128)S(1)} collective-permute-done((f32[2,8,2048]{2,1,0:T(8,128)S(1)}, f32[2,8,2048]{2,1,0:T(8,128)S(1)}, u32[]{:S(2)}, u32[]{:S(2)}) %collective-permute-start.24) | collective-permute-done | bytes 131104 | tf_op jit(solution)/shard_map/ppermute | solution.py:113
  105.3 3.4 %collective-permute-done.25 = f32[8,2048]{1,0:T(8,128)S(1)} collective-permute-done((f32[8,2048]{1,0:T(8,128)S(1)}, f32[8,2048]{1,0:T(8,128)S(1)}, u32[]{:S(2)}, u32[]{:S(2)}) %collective-permute-start.25) | collective-permute-done | bytes 65568 | tf_op jit(solution)/shard_map/ppermute | solution.py:113
  (110 shorter events, 23.0 us)
Async XLA Ops:
  0.0 27.9 %copy-start = (bf16[8,256,2,2,128]{4,3,2,1,0:T(2,128)(2,1)S(1)}, bf16[8,256,2,2,128]{4,3,2,1,0:T(2,128)(2,1)}, u32[]{:S(2)}) copy-start(bf16[8,256,2,2,128]{4,3,2,1,0:T(2,128)(2,1)} %param.30) | copy-start | bytes 6291460
  1.0 8.2 %collective-permute-start.2 = (f32[8]{0:T(128)S(1)}, f32[8]{0:T(128)S(1)}, u32[]{:S(2)}, u32[]{:S(2)}) collective-permute-start(f32[8]{0:T(128)S(1)} %fusion.74), channel_id=1, source_target_pairs={{0,12},{4,0},{8,4},{12,8},{1,13},{5,1},{9,5},{13,9},{2,14},{6,2},{... | collective-permute-start | bytes 104 | tf_op jit(solution)/shard_map/ppermute | solution.py:140
  6.1 4.4 %collective-permute-start.1 = (f32[8]{0:T(128)S(1)}, f32[8]{0:T(128)S(1)}, u32[]{:S(2)}, u32[]{:S(2)}) collective-permute-start(f32[8]{0:T(128)S(1)} %fusion.74), channel_id=1, source_target_pairs={{0,8},{4,12},{8,0},{12,4},{1,9},{5,13},{9,1},{13,5},{2,10},{6,14},... | collective-permute-start | bytes 104 | tf_op jit(solution)/shard_map/ppermute | solution.py:140
  6.1 5.3 %collective-permute-start = (f32[8]{0:T(128)S(1)}, f32[8]{0:T(128)S(1)}, u32[]{:S(2)}, u32[]{:S(2)}) collective-permute-start(f32[8]{0:T(128)S(1)} %fusion.74), channel_id=1, source_target_pairs={{0,4},{4,8},{8,12},{12,0},{1,5},{5,9},{9,13},{13,1},{2,6},{6,10},{... | collective-permute-start | bytes 104 | tf_op jit(solution)/shard_map/ppermute | solution.py:140
  12.3 1.8 %collective-permute-start.5 = (bf16[8,2048]{1,0:T(8,128)(2,1)S(1)}, bf16[8,2048]{1,0:T(8,128)(2,1)S(1)}, u32[]{:S(2)}, u32[]{:S(2)}) collective-permute-start(bf16[8,2048]{1,0:T(8,128)(2,1)S(1)} %fusion.76), channel_id=1, source_target_pairs={{0,3},{1,0},{2,1},{3,2},{4,7},{5,4},{6,5},{7,6},{8,11},{9,8},{10,9... | collective-permute-start | bytes 98312 | tf_op jit(solution)/shard_map/ppermute | solution.py:97
  12.4 4.1 %collective-permute-start.4 = (bf16[8,2048]{1,0:T(8,128)(2,1)S(1)}, bf16[8,2048]{1,0:T(8,128)(2,1)S(1)}, u32[]{:S(2)}, u32[]{:S(2)}) collective-permute-start(bf16[8,2048]{1,0:T(8,128)(2,1)S(1)} %fusion.76), channel_id=1, source_target_pairs={{0,2},{1,3},{2,0},{3,1},{4,6},{5,7},{6,4},{7,5},{8,10},{9,11},{10,... | collective-permute-start | bytes 98312 | tf_op jit(solution)/shard_map/ppermute | solution.py:97
  13.9 3.3 %collective-permute-start.3 = (bf16[8,2048]{1,0:T(8,128)(2,1)S(1)}, bf16[8,2048]{1,0:T(8,128)(2,1)S(1)}, u32[]{:S(2)}, u32[]{:S(2)}) collective-permute-start(bf16[8,2048]{1,0:T(8,128)(2,1)S(1)} %fusion.76), channel_id=1, source_target_pairs={{0,1},{1,2},{2,3},{3,0},{4,5},{5,6},{6,7},{7,4},{8,9},{9,10},{10,1... | collective-permute-start | bytes 98312 | tf_op jit(solution)/shard_map/ppermute | solution.py:97
  24.0 7.1 %collective-permute-start.6 = (f32[8,2560]{1,0:T(8,128)S(1)}, f32[8,2560]{1,0:T(8,128)S(1)}, u32[]{:S(2)}, u32[]{:S(2)}) collective-permute-start(f32[8,2560]{1,0:T(8,128)S(1)} %get-tuple-element.72), channel_id=1, source_target_pairs={{0,4},{4,8},{8,12},{12,0},{1,5},{5,9},{9,13},{13,1},{2,6},{6,10},{... | collective-permute-start | bytes 245768 | tf_op jit(solution)/shard_map/ppermute | solution.py:113
  24.3 6.8 %collective-permute-start.8 = (f32[8,2560]{1,0:T(8,128)S(1)}, f32[8,2560]{1,0:T(8,128)S(1)}, u32[]{:S(2)}, u32[]{:S(2)}) collective-permute-start(f32[8,2560]{1,0:T(8,128)S(1)} %get-tuple-element.73), channel_id=1, source_target_pairs={{0,12},{4,0},{8,4},{12,8},{1,13},{5,1},{9,5},{13,9},{2,14},{6,2},{... | collective-permute-start | bytes 245768 | tf_op jit(solution)/shard_map/ppermute | solution.py:113
  27.8 6.1 %collective-permute-start.7 = (f32[8,2560]{1,0:T(8,128)S(1)}, f32[8,2560]{1,0:T(8,128)S(1)}, u32[]{:S(2)}, u32[]{:S(2)}) collective-permute-start(f32[8,2560]{1,0:T(8,128)S(1)} %get-tuple-element.74), channel_id=1, source_target_pairs={{0,8},{4,12},{8,0},{12,4},{1,9},{5,13},{9,1},{13,5},{2,10},{6,14},... | collective-permute-start | bytes 245768 | tf_op jit(solution)/shard_map/ppermute | solution.py:113
  35.4 4.0 %collective-permute-start.11 = (bf16[8,2048]{1,0:T(8,128)(2,1)S(1)}, bf16[8,2048]{1,0:T(8,128)(2,1)S(1)}, u32[]{:S(2)}, u32[]{:S(2)}) collective-permute-start(bf16[8,2048]{1,0:T(8,128)(2,1)S(1)} %bitcast.101), channel_id=1, source_target_pairs={{0,12},{4,0},{8,4},{12,8},{1,13},{5,1},{9,5},{13,9},{2,14},{6,2},{... | collective-permute-start | bytes 98312 | tf_op jit(solution)/shard_map/ppermute | solution.py:97
  37.3 4.9 %collective-permute-start.10 = (bf16[8,2048]{1,0:T(8,128)(2,1)S(1)}, bf16[8,2048]{1,0:T(8,128)(2,1)S(1)}, u32[]{:S(2)}, u32[]{:S(2)}) collective-permute-start(bf16[8,2048]{1,0:T(8,128)(2,1)S(1)} %bitcast.102), channel_id=1, source_target_pairs={{0,8},{4,12},{8,0},{12,4},{1,9},{5,13},{9,1},{13,5},{2,10},{6,14},... | collective-permute-start | bytes 98312 | tf_op jit(solution)/shard_map/ppermute | solution.py:97
  37.3 5.7 %collective-permute-start.9 = (bf16[8,2048]{1,0:T(8,128)(2,1)S(1)}, bf16[8,2048]{1,0:T(8,128)(2,1)S(1)}, u32[]{:S(2)}, u32[]{:S(2)}) collective-permute-start(bf16[8,2048]{1,0:T(8,128)(2,1)S(1)} %bitcast.103), channel_id=1, source_target_pairs={{0,4},{4,8},{8,12},{12,0},{1,5},{5,9},{9,13},{13,1},{2,6},{6,10},{... | collective-permute-start | bytes 98312 | tf_op jit(solution)/shard_map/ppermute | solution.py:97
  43.6 20.9 %copy-start.2 = (f32[2048]{0:T(1024)S(1)}, f32[2048]{0:T(1024)}, u32[]{:S(2)}) copy-start(f32[2048]{0:T(1024)} %param.26) | copy-start | bytes 24580
  48.7 1.4 %collective-permute-start.12 = (f32[16,2048]{1,0:T(8,128)S(1)}, f32[16,2048]{1,0:T(8,128)S(1)}, u32[]{:S(2)}, u32[]{:S(2)}) collective-permute-start(f32[16,2048]{1,0:T(8,128)S(1)} %select_bitcast_fusion.1), channel_id=1, source_target_pairs={{0,1},{1,0},{2,3},{3,2},{4,5},{5,4},{6,7},{7,6},{8,9},{9,8},{10,11... | collective-permute-start | bytes 393224 | tf_op jit(solution)/shard_map/ppermute | solution.py:113
  50.1 5.6 %collective-permute-start.13 = (f32[16,2048]{1,0:T(8,128)S(1)}, f32[16,2048]{1,0:T(8,128)S(1)}, u32[]{:S(2)}, u32[]{:S(2)}) collective-permute-start(f32[16,2048]{1,0:T(8,128)S(1)} %bitcast_add_fusion.1), channel_id=1, source_target_pairs={{0,2},{2,0},{1,3},{3,1},{4,6},{6,4},{5,7},{7,5},{8,10},{10,8},{9,1... | collective-permute-start | bytes 393224 | tf_op jit(solution)/shard_map/ppermute | solution.py:140
  55.8 1.4 %collective-permute-start.14 = (f32[16,2048]{1,0:T(8,128)S(1)}, f32[16,2048]{1,0:T(8,128)S(1)}, u32[]{:S(2)}, u32[]{:S(2)}) collective-permute-start(f32[16,2048]{1,0:T(8,128)S(1)} %add.289), channel_id=1, source_target_pairs={{0,1},{1,0},{2,3},{3,2},{4,5},{5,4},{6,7},{7,6},{8,9},{9,8},{10,11... | collective-permute-start | bytes 393224 | tf_op jit(solution)/shard_map/ppermute | solution.py:131
  58.0 3.5 %collective-permute-start.17 = (f32[32]{0:T(128)S(1)}, f32[32]{0:T(128)S(1)}, u32[]{:S(2)}, u32[]{:S(2)}) collective-permute-start(f32[32]{0:T(128)S(1)} %reduce_sum.62), channel_id=1, source_target_pairs={{0,12},{4,0},{8,4},{12,8},{1,13},{5,1},{9,5},{13,9},{2,14},{6,2},{... | collective-permute-start | bytes 392 | tf_op jit(solution)/shard_map/ppermute | solution.py:140
  58.9 4.4 %collective-permute-start.16 = (f32[32]{0:T(128)S(1)}, f32[32]{0:T(128)S(1)}, u32[]{:S(2)}, u32[]{:S(2)}) collective-permute-start(f32[32]{0:T(128)S(1)} %reduce_sum.62), channel_id=1, source_target_pairs={{0,8},{4,12},{8,0},{12,4},{1,9},{5,13},{9,1},{13,5},{2,10},{6,14},... | collective-permute-start | bytes 392 | tf_op jit(solution)/shard_map/ppermute | solution.py:140
  59.2 5.3 %collective-permute-start.15 = (f32[32]{0:T(128)S(1)}, f32[32]{0:T(128)S(1)}, u32[]{:S(2)}, u32[]{:S(2)}) collective-permute-start(f32[32]{0:T(128)S(1)} %reduce_sum.62), channel_id=1, source_target_pairs={{0,4},{4,8},{8,12},{12,0},{1,5},{5,9},{9,13},{13,1},{2,6},{6,10},{... | collective-permute-start | bytes 392 | tf_op jit(solution)/shard_map/ppermute | solution.py:140
  67.4 28.5 %slice-start = ((s8[14680064]{0:T(1024)(128)(4,1)}), s8[4194304]{0:T(1024)(128)(4,1)S(1)}, s32[]{:S(2)}) async-start(s8[14680064]{0:T(1024)(128)(4,1)} %bitcast.85), calls=%async_computation | async-start | bytes 8388608
  70.3 25.6 %slice-start.1 = ((s8[14680064]{0:T(1024)(128)(4,1)}), s8[4194304]{0:T(1024)(128)(4,1)S(1)}, s32[]{:S(2)}) async-start(s8[14680064]{0:T(1024)(128)(4,1)} %bitcast.85), calls=%async_computation.1 | async-start | bytes 8388608
  75.9 20.0 %slice-start.2 = ((s8[14680064]{0:T(1024)(128)(4,1)}), s8[4194304]{0:T(1024)(128)(4,1)S(1)}, s32[]{:S(2)}) async-start(s8[14680064]{0:T(1024)(128)(4,1)} %bitcast.85), calls=%async_computation.2 | async-start | bytes 8388608
  81.5 14.4 %slice-start.3 = ((s8[14680064]{0:T(1024)(128)(4,1)}), s8[2097152]{0:T(1024)(128)(4,1)S(1)}, s32[]{:S(2)}) async-start(s8[14680064]{0:T(1024)(128)(4,1)} %bitcast.85), calls=%async_computation.3 | async-start | bytes 4194304
  81.6 9.3 %collective-permute-start.18 = (bf16[32,1792]{1,0:T(8,128)(2,1)S(1)}, bf16[32,1792]{1,0:T(8,128)(2,1)S(1)}, u32[]{:S(2)}, u32[]{:S(2)}) collective-permute-start(bf16[32,1792]{1,0:T(8,128)(2,1)S(1)} %get-tuple-element.19), channel_id=1, source_target_pairs={{0,4},{4,8},{8,12},{12,0},{1,5},{5,9},{9,13},{13,1},{2,6},{6,10},{... | collective-permute-start | bytes 344072 | tf_op jit(solution)/shard_map/ppermute | solution.py:163
  81.8 10.5 %collective-permute-start.19 = (bf16[32,1792]{1,0:T(8,128)(2,1)S(1)}, bf16[32,1792]{1,0:T(8,128)(2,1)S(1)}, u32[]{:S(2)}, u32[]{:S(2)}) collective-permute-start(bf16[32,1792]{1,0:T(8,128)(2,1)S(1)} %get-tuple-element.20), channel_id=1, source_target_pairs={{0,8},{4,12},{8,0},{12,4},{1,9},{5,13},{9,1},{13,5},{2,10},{6,14},... | collective-permute-start | bytes 344072 | tf_op jit(solution)/shard_map/ppermute | solution.py:163
  83.6 8.7 %collective-permute-start.20 = (bf16[32,1792]{1,0:T(8,128)(2,1)S(1)}, bf16[32,1792]{1,0:T(8,128)(2,1)S(1)}, u32[]{:S(2)}, u32[]{:S(2)}) collective-permute-start(bf16[32,1792]{1,0:T(8,128)(2,1)S(1)} %pad_maximum_fusion.5), channel_id=1, source_target_pairs={{0,12},{4,0},{8,4},{12,8},{1,13},{5,1},{9,5},{13,9},{2,14},{6,2},{... | collective-permute-start | bytes 344072 | tf_op jit(solution)/shard_map/ppermute | solution.py:163
  92.4 8.9 %collective-permute-start.23 = (bf16[32,896]{1,0:T(8,128)(2,1)S(1)}, bf16[32,896]{1,0:T(8,128)(2,1)S(1)}, u32[]{:S(2)}, u32[]{:S(2)}) collective-permute-start(bf16[32,896]{1,0:T(8,128)(2,1)S(1)} %fusion.70), channel_id=1, source_target_pairs={{0,12},{4,0},{8,4},{12,8},{1,13},{5,1},{9,5},{13,9},{2,14},{6,2},{... | collective-permute-start | bytes 172040 | tf_op jit(solution)/shard_map/ppermute | solution.py:176
  95.0 5.6 %collective-permute-start.22 = (bf16[32,896]{1,0:T(8,128)(2,1)S(1)}, bf16[32,896]{1,0:T(8,128)(2,1)S(1)}, u32[]{:S(2)}, u32[]{:S(2)}) collective-permute-start(bf16[32,896]{1,0:T(8,128)(2,1)S(1)} %fusion.70), channel_id=1, source_target_pairs={{0,8},{4,12},{8,0},{12,4},{1,9},{5,13},{9,1},{13,5},{2,10},{6,14},... | collective-permute-start | bytes 172040 | tf_op jit(solution)/shard_map/ppermute | solution.py:176
  95.9 6.1 %collective-permute-start.21 = (bf16[32,896]{1,0:T(8,128)(2,1)S(1)}, bf16[32,896]{1,0:T(8,128)(2,1)S(1)}, u32[]{:S(2)}, u32[]{:S(2)}) collective-permute-start(bf16[32,896]{1,0:T(8,128)(2,1)S(1)} %fusion.70), channel_id=1, source_target_pairs={{0,4},{4,8},{8,12},{12,0},{1,5},{5,9},{9,13},{13,1},{2,6},{6,10},{... | collective-permute-start | bytes 172040 | tf_op jit(solution)/shard_map/ppermute | solution.py:176
  102.9 1.4 %collective-permute-start.24 = (f32[2,8,2048]{2,1,0:T(8,128)S(1)}, f32[2,8,2048]{2,1,0:T(8,128)S(1)}, u32[]{:S(2)}, u32[]{:S(2)}) collective-permute-start(f32[2,8,2048]{2,1,0:T(8,128)S(1)} %select_bitcast_fusion), channel_id=1, source_target_pairs={{0,1},{1,0},{2,3},{3,2},{4,5},{5,4},{6,7},{7,6},{8,9},{9,8},{10,11... | collective-permute-start | bytes 393224 | tf_op jit(solution)/shard_map/ppermute | solution.py:113
  104.4 4.3 %collective-permute-start.25 = (f32[8,2048]{1,0:T(8,128)S(1)}, f32[8,2048]{1,0:T(8,128)S(1)}, u32[]{:S(2)}, u32[]{:S(2)}) collective-permute-start(f32[8,2048]{1,0:T(8,128)S(1)} %select_bitcast_fusion.5), channel_id=1, source_target_pairs={{0,2},{2,0},{1,3},{3,1},{4,6},{6,4},{5,7},{7,5},{8,10},{10,8},{9,1... | collective-permute-start | bytes 196616 | tf_op jit(solution)/shard_map/ppermute | solution.py:113
  (1 other events, 13.2 us)

commit v14 on v13

--- a/solution.py
+++ b/solution.py
@@ -97,7 +97,8 @@
     got = [x] + [lax.ppermute(x, axis, shift_pairs(n, k)) for k in range(1, n)]
     stacked = jnp.concatenate(got, axis=0)
     arrival = ((idx - want // per) % n) * per + want % per
-    return jnp.take(stacked, arrival, axis=0)
+    chooser = (arrival[:, None] == jnp.arange(n * per, dtype=arrival.dtype)[None, :]).astype(x.dtype)
+    return jnp.dot(chooser, stacked, preferred_element_type=jnp.float32).astype(x.dtype)
 
 
 def pick(keys, wanted, values):
@@ -129,9 +130,8 @@
     mine = scatter_sum(parts.reshape((n_side, -1) + parts.shape[1:]), "side", n_side)
     mine = all_sum(mine, "col", n_col)
     got = [mine] + [lax.ppermute(mine, "side", shift_pairs(n_side, k)) for k in range(1, n_side)]
-    stacked = jnp.stack(got)
-    ordered = jnp.take(stacked, (side - jnp.arange(n_side)) % n_side, axis=0)
-    return ordered.reshape(parts.shape)
+    ordered = [lax.select_n((side - j) % n_side, *got) for j in range(n_side)]
+    return jnp.stack(ordered).reshape(parts.shape)
 
 
 def all_sum(x, axis, n):

time: 110 us -> 109 us (level)
  local copies, waits for them, and re-layouts: 2.73 us -> 0.71 us
    gather x3 -> x0, local copies, waits for them, and re-layouts: 1.87 us -> none  [the longest x2 1.3 us: gather_rows(): return jnp.take(stacked, arrival, axis=0)]
  transfers between devices with their start and end apart: 26 -> 26, of which waited for: 19 -> 19; matrix products, arithmetic and copies ran while one was open for 10% -> 9% of each run, Pallas kernels for 0% -> 0%
where the time goes in v14:
time: 109 us; the launch traced here: 108 us
  matrix products  38 us (35%)
  waiting for transfers between devices  36.5 us (33%)
  starting transfers between devices  26.9 us (25%)
  other arithmetic  5.54 us (5%)
    dot_general x8, matrix products, block(): jnp.dot(x, lax.dynamic_slice_in_dim(w, j * chunk, chunk, 1), preferred_el...  22.1 us
    ppermute x6, waiting for transfers between devices, scatter_sum(): lax.ppermute(piece, axis, shift_pairs(n, k)).astype(jnp.float32)  11.6 us
    ppermute x7, waiting for transfers between devices, all_sum(): total = total + lax.ppermute(x, axis, shift_pairs(n, k))  10.4 us
    ppermute x7, starting transfers between devices, all_sum(): total = total + lax.ppermute(x, axis, shift_pairs(n, k))  10.2 us
    ppermute x6, waiting for transfers between devices, gather_rows(): got = [x] + [lax.ppermute(x, axis, shift_pairs(n, k)) for k in range(1, n)]  8.12 us
    dot_general x1, matrix products, local(): jnp.einsum('rf,fgc->rgc', by_slot, w_qkv, preferred_element_type=jnp.floa...  6.85 us
    dot_general x1, matrix products, local(): out_part = jnp.dot(by_row, w_out, preferred_element_type=jnp.float32)  5.09 us
    ppermute x6, starting transfers between devices, scatter_sum(): lax.ppermute(piece, axis, shift_pairs(n, k)).astype(jnp.float32)  4.97 us
  transfers between devices with their start and end apart: 26, of which 19 were waited for; matrix products, arithmetic and copies ran while one was open for 9% of the time, Pallas kernels for 0%

profile of v14, /device:TPU:0, one launch (start us, length us, event | category | flops | bytes accessed | tf_op | source)
XLA Modules:
  0.0 108.4 jit_solution(4942116183760041855)
XLA Ops:
  1.0 5.1 %collective-permute-start.2 = (f32[8]{0:T(128)S(1)}, f32[8]{0:T(128)S(1)}, u32[]{:S(2)}, u32[]{:S(2)}) collective-permute-start(f32[8]{0:T(128)S(1)} %fusion.98), channel_id=1, source_target_pairs={{0,12},{4,0},{8,4},{12,8},{1,13},{5,1},{9,5},{13,9},{2,14},{6,2},{... | collective-permute-start | bytes 104 | tf_op jit(solution)/shard_map/ppermute | solution.py:140
  9.1 1.4 %collective-permute-done.1 = f32[8]{0:T(128)S(1)} collective-permute-done((f32[8]{0:T(128)S(1)}, f32[8]{0:T(128)S(1)}, u32[]{:S(2)}, u32[]{:S(2)}) %collective-permute-start.1) | collective-permute-done | bytes 64 | tf_op jit(solution)/shard_map/ppermute | solution.py:140
  12.4 1.6 %collective-permute-start.4 = (bf16[8,2048]{1,0:T(8,128)(2,1)S(1)}, bf16[8,2048]{1,0:T(8,128)(2,1)S(1)}, u32[]{:S(2)}, u32[]{:S(2)}) collective-permute-start(bf16[8,2048]{1,0:T(8,128)(2,1)S(1)} %fusion.100), channel_id=1, source_target_pairs={{0,2},{1,3},{2,0},{3,1},{4,6},{5,7},{6,4},{7,5},{8,10},{9,11},{10,... | collective-permute-start | bytes 98312 | tf_op jit(solution)/shard_map/ppermute | solution.py:97
  14.2 2.3 %collective-permute-done.4 = bf16[8,2048]{1,0:T(8,128)(2,1)S(1)} collective-permute-done((bf16[8,2048]{1,0:T(8,128)(2,1)S(1)}, bf16[8,2048]{1,0:T(8,128)(2,1)S(1)}, u32[]{:S(2)}, u32[]{:S(2)}) %collective-permute-start.4) | collective-permute-done | bytes 32800 | tf_op jit(solution)/shard_map/ppermute | solution.py:97
  17.3 6.9 %fusion.26 = f32[2,4,8,1280]{3,2,1,0:T(8,128)S(1)} fusion(bf16[2048,2,1280]{2,1,0:T(2,128)(2,1)} %param.22, bf16[8,2048]{1,0:T(8,128)(2,1)S(1)} %collective-permute-done.5, bf16[8,2048]{1,0:T(8,128)(2,1)S(1)} %collective-permute-done.4, bf16[8,2048]{1,0:T(8,128)(2,1)S(1)} %collective-permute-done.3, bf16[8,2048]{1,0:T(8,128)(2,1)S(1)} %fusion.100, ...), kind=kOutput, calls=%fused_computation.26 | convolution fusion | flops 340329472 | bytes 10944640 | tf_op jit(solution)/shard_map/rf,fgc->rgc/dot_general | solution.py:215
  24.4 3.7 %collective-permute-start.8 = (f32[8,2560]{1,0:T(8,128)S(1)}, f32[8,2560]{1,0:T(8,128)S(1)}, u32[]{:S(2)}, u32[]{:S(2)}) collective-permute-start(f32[8,2560]{1,0:T(8,128)S(1)} %get-tuple-element.66), channel_id=1, source_target_pairs={{0,12},{4,0},{8,4},{12,8},{1,13},{5,1},{9,5},{13,9},{2,14},{6,2},{... | collective-permute-start | bytes 245768 | tf_op jit(solution)/shard_map/ppermute | solution.py:114
  28.7 2.6 %collective-permute-done.6 = f32[8,2560]{1,0:T(8,128)S(1)} collective-permute-done((f32[8,2560]{1,0:T(8,128)S(1)}, f32[8,2560]{1,0:T(8,128)S(1)}, u32[]{:S(2)}, u32[]{:S(2)}) %collective-permute-start.6) | collective-permute-done | bytes 81952 | tf_op jit(solution)/shard_map/ppermute | solution.py:114
  31.3 2.9 %collective-permute-done.7 = f32[8,2560]{1,0:T(8,128)S(1)} collective-permute-done((f32[8,2560]{1,0:T(8,128)S(1)}, f32[8,2560]{1,0:T(8,128)S(1)}, u32[]{:S(2)}, u32[]{:S(2)}) %collective-permute-start.7) | collective-permute-done | bytes 81952 | tf_op jit(solution)/shard_map/ppermute | solution.py:114
  35.7 1.8 %collective-permute-start.11 = (bf16[8,2048]{1,0:T(8,128)(2,1)S(1)}, bf16[8,2048]{1,0:T(8,128)(2,1)S(1)}, u32[]{:S(2)}, u32[]{:S(2)}) collective-permute-start(bf16[8,2048]{1,0:T(8,128)(2,1)S(1)} %bitcast.100), channel_id=1, source_target_pairs={{0,12},{4,0},{8,4},{12,8},{1,13},{5,1},{9,5},{13,9},{2,14},{6,2},{... | collective-permute-start | bytes 98312 | tf_op jit(solution)/shard_map/ppermute | solution.py:97
  38.2 1.5 %collective-permute-done.11 = bf16[8,2048]{1,0:T(8,128)(2,1)S(1)} collective-permute-done((bf16[8,2048]{1,0:T(8,128)(2,1)S(1)}, bf16[8,2048]{1,0:T(8,128)(2,1)S(1)}, u32[]{:S(2)}, u32[]{:S(2)}) %collective-permute-start.11) | collective-permute-done | bytes 32800 | tf_op jit(solution)/shard_map/ppermute | solution.py:97
  39.6 2.7 %collective-permute-done.10 = bf16[8,2048]{1,0:T(8,128)(2,1)S(1)} collective-permute-done((bf16[8,2048]{1,0:T(8,128)(2,1)S(1)}, bf16[8,2048]{1,0:T(8,128)(2,1)S(1)}, u32[]{:S(2)}, u32[]{:S(2)}) %collective-permute-start.10) | collective-permute-done | bytes 32800 | tf_op jit(solution)/shard_map/ppermute | solution.py:97
  43.2 5.1 %fusion.39 = f32[32,2048]{1,0:T(8,128)S(1)} fusion(bf16[2048,2048]{1,0:T(8,128)(2,1)} %param.23, bf16[8,2048]{1,0:T(8,128)(2,1)S(1)} %collective-permute-done.11, bf16[8,2048]{1,0:T(8,128)(2,1)S(1)} %collective-permute-done.10, bf16[8,2048]{1,0:T(8,128)(2,1)S(1)} %collective-permute-done.9, bf16[8,2048]{1,0:T(8,128)(2,1)S(1)} %bitcast.103, s32[32]{0:T(128)S(1)} %fusion.130), kind=kOutput, calls=%fused_computation.33 | convolution fusion | flops 273220608 | bytes 8781952 | tf_op jit(solution)/shard_map/dot_general | solution.py:223
  48.5 1.3 %collective-permute-done.12 = f32[16,2048]{1,0:T(8,128)S(1)} collective-permute-done((f32[16,2048]{1,0:T(8,128)S(1)}, f32[16,2048]{1,0:T(8,128)S(1)}, u32[]{:S(2)}, u32[]{:S(2)}) %collective-permute-start.12) | collective-permute-done | bytes 131104 | tf_op jit(solution)/shard_map/ppermute | solution.py:114
  50.8 4.7 %collective-permute-done.13 = f32[16,2048]{1,0:T(8,128)S(1)} collective-permute-done((f32[16,2048]{1,0:T(8,128)S(1)}, f32[16,2048]{1,0:T(8,128)S(1)}, u32[]{:S(2)}, u32[]{:S(2)}) %collective-permute-start.13) | collective-permute-done | bytes 131104 | tf_op jit(solution)/shard_map/ppermute | solution.py:140
  58.3 2.0 %collective-permute-start.15 = (f32[32]{0:T(128)S(1)}, f32[32]{0:T(128)S(1)}, u32[]{:S(2)}, u32[]{:S(2)}) collective-permute-start(f32[32]{0:T(128)S(1)} %reduce_sum.62), channel_id=1, source_target_pairs={{0,4},{4,8},{8,12},{12,0},{1,5},{5,9},{9,13},{13,1},{2,6},{6,10},{... | collective-permute-start | bytes 392 | tf_op jit(solution)/shard_map/ppermute | solution.py:140
  60.6 1.7 %collective-permute-done.16 = f32[32]{0:T(128)S(1)} collective-permute-done((f32[32]{0:T(128)S(1)}, f32[32]{0:T(128)S(1)}, u32[]{:S(2)}, u32[]{:S(2)}) %collective-permute-start.16) | collective-permute-done | bytes 160 | tf_op jit(solution)/shard_map/ppermute | solution.py:140
  62.3 1.3 %collective-permute-done.15 = f32[32]{0:T(128)S(1)} collective-permute-done((f32[32]{0:T(128)S(1)}, f32[32]{0:T(128)S(1)}, u32[]{:S(2)}, u32[]{:S(2)}) %collective-permute-start.15) | collective-permute-done | bytes 160 | tf_op jit(solution)/shard_map/ppermute | solution.py:140
  63.7 2.7 %fusion.55 = bf16[32,896]{1,0:T(8,128)(2,1)S(1)} fusion(bf16[32,2048]{1,0:T(8,128)(2,1)S(1)} %multiply_convert_fusion, bf16[2048,3584]{1,0:T(8,128)(2,1)} %param.26, s32[]{:T(128)S(6)} %select_n.218), kind=kOutput, calls=%fused_computation.40 | convolution fusion | flops 117469184 | bytes 3858436 | tf_op jit(solution)/shard_map/dot_general | solution.py:150
  66.4 2.9 %fusion.52 = bf16[32,896]{1,0:T(8,128)(2,1)S(1)} fusion(bf16[32,2048]{1,0:T(8,128)(2,1)S(1)} %multiply_convert_fusion, bf16[2048,3584]{1,0:T(8,128)(2,1)} %param.25, s32[]{:T(128)S(6)} %select_n.218), kind=kOutput, calls=%fused_computation.39 | convolution fusion | flops 117469184 | bytes 3858436 | tf_op jit(solution)/shard_map/dot_general | solution.py:150
  69.3 2.9 %fusion.49 = bf16[32,896]{1,0:T(8,128)(2,1)S(1)} fusion(bf16[32,2048]{1,0:T(8,128)(2,1)S(1)} %multiply_convert_fusion, bf16[2048,3584]{1,0:T(8,128)(2,1)} %param.26, s32[]{:T(128)S(6)} %select_n.217), kind=kOutput, calls=%fused_computation.38 | convolution fusion | flops 117469184 | bytes 3858436 | tf_op jit(solution)/shard_map/dot_general | solution.py:150
  72.2 2.7 %fusion.46 = bf16[32,896]{1,0:T(8,128)(2,1)S(1)} fusion(bf16[32,2048]{1,0:T(8,128)(2,1)S(1)} %multiply_convert_fusion, bf16[2048,3584]{1,0:T(8,128)(2,1)} %param.25, s32[]{:T(128)S(6)} %select_n.217), kind=kOutput, calls=%fused_computation.37 | convolution fusion | flops 117469184 | bytes 3858436 | tf_op jit(solution)/shard_map/dot_general | solution.py:150
  74.9 2.9 %fusion.43 = bf16[32,896]{1,0:T(8,128)(2,1)S(1)} fusion(bf16[32,2048]{1,0:T(8,128)(2,1)S(1)} %multiply_convert_fusion, bf16[2048,3584]{1,0:T(8,128)(2,1)} %param.26, s32[]{:T(128)S(6)} %select_n.216), kind=kOutput, calls=%fused_computation.36 | convolution fusion | flops 117469184 | bytes 3858436 | tf_op jit(solution)/shard_map/dot_general | solution.py:150
  77.8 2.7 %fusion.40 = bf16[32,896]{1,0:T(8,128)(2,1)S(1)} fusion(bf16[32,2048]{1,0:T(8,128)(2,1)S(1)} %multiply_convert_fusion, bf16[2048,3584]{1,0:T(8,128)(2,1)} %param.25, s32[]{:T(128)S(6)} %select_n.216), kind=kOutput, calls=%fused_computation.35 | convolution fusion | flops 117469184 | bytes 3858436 | tf_op jit(solution)/shard_map/dot_general | solution.py:150
  80.8 1.8 %collective-permute-start.19 = (bf16[32,1792]{1,0:T(8,128)(2,1)S(1)}, bf16[32,1792]{1,0:T(8,128)(2,1)S(1)}, u32[]{:S(2)}, u32[]{:S(2)}) collective-permute-start(bf16[32,1792]{1,0:T(8,128)(2,1)S(1)} %get-tuple-element.19), channel_id=1, source_target_pairs={{0,8},{4,12},{8,0},{12,4},{1,9},{5,13},{9,1},{13,5},{2,10},{6,14},... | collective-permute-start | bytes 344072 | tf_op jit(solution)/shard_map/ppermute | solution.py:163
  82.6 1.8 %collective-permute-start.20 = (bf16[32,1792]{1,0:T(8,128)(2,1)S(1)}, bf16[32,1792]{1,0:T(8,128)(2,1)S(1)}, u32[]{:S(2)}, u32[]{:S(2)}) collective-permute-start(bf16[32,1792]{1,0:T(8,128)(2,1)S(1)} %pad_maximum_fusion.3), channel_id=1, source_target_pairs={{0,12},{4,0},{8,4},{12,8},{1,13},{5,1},{9,5},{13,9},{2,14},{6,2},{... | collective-permute-start | bytes 344072 | tf_op jit(solution)/shard_map/ppermute | solution.py:163
  84.5 2.7 %fusion.61 = bf16[32,896]{1,0:T(8,128)(2,1)S(1)} fusion(bf16[32,2048]{1,0:T(8,128)(2,1)S(1)} %multiply_convert_fusion, bf16[2048,3584]{1,0:T(8,128)(2,1)} %param.26, s32[]{:T(128)S(6)} %select_n.219), kind=kOutput, calls=%fused_computation.42 | convolution fusion | flops 117469184 | bytes 3858436 | tf_op jit(solution)/shard_map/dot_general | solution.py:150
  87.2 2.7 %fusion.58 = bf16[32,896]{1,0:T(8,128)(2,1)S(1)} fusion(bf16[32,2048]{1,0:T(8,128)(2,1)S(1)} %multiply_convert_fusion, bf16[2048,3584]{1,0:T(8,128)(2,1)} %param.25, s32[]{:T(128)S(6)} %select_n.219), kind=kOutput, calls=%fused_computation.41 | convolution fusion | flops 117469184 | bytes 3858436 | tf_op jit(solution)/shard_map/dot_general | solution.py:150
  89.9 1.4 %collective-permute-done.19 = bf16[32,1792]{1,0:T(8,128)(2,1)S(1)} collective-permute-done((bf16[32,1792]{1,0:T(8,128)(2,1)S(1)}, bf16[32,1792]{1,0:T(8,128)(2,1)S(1)}, u32[]{:S(2)}, u32[]{:S(2)}) %collective-permute-start.19) | collective-permute-done | bytes 114720 | tf_op jit(solution)/shard_map/ppermute | solution.py:163
  91.4 2.6 %collective-permute-start.23 = (bf16[32,896]{1,0:T(8,128)(2,1)S(1)}, bf16[32,896]{1,0:T(8,128)(2,1)S(1)}, u32[]{:S(2)}, u32[]{:S(2)}) collective-permute-start(bf16[32,896]{1,0:T(8,128)(2,1)S(1)} %fusion.94), channel_id=1, source_target_pairs={{0,12},{4,0},{8,4},{12,8},{1,13},{5,1},{9,5},{13,9},{2,14},{6,2},{... | collective-permute-start | bytes 172040 | tf_op jit(solution)/shard_map/ppermute | solution.py:176
  95.7 3.9 %collective-permute-done.22 = bf16[32,896]{1,0:T(8,128)(2,1)S(1)} collective-permute-done((bf16[32,896]{1,0:T(8,128)(2,1)S(1)}, bf16[32,896]{1,0:T(8,128)(2,1)S(1)}, u32[]{:S(2)}, u32[]{:S(2)}) %collective-permute-start.22) | collective-permute-done | bytes 57376 | tf_op jit(solution)/shard_map/ppermute | solution.py:176
  102.1 1.3 %collective-permute-done.24 = f32[2,8,2048]{2,1,0:T(8,128)S(1)} collective-permute-done((f32[2,8,2048]{2,1,0:T(8,128)S(1)}, f32[2,8,2048]{2,1,0:T(8,128)S(1)}, u32[]{:S(2)}, u32[]{:S(2)}) %collective-permute-start.24) | collective-permute-done | bytes 131104 | tf_op jit(solution)/shard_map/ppermute | solution.py:114
  104.4 3.4 %collective-permute-done.25 = f32[8,2048]{1,0:T(8,128)S(1)} collective-permute-done((f32[8,2048]{1,0:T(8,128)S(1)}, f32[8,2048]{1,0:T(8,128)S(1)}, u32[]{:S(2)}, u32[]{:S(2)}) %collective-permute-start.25) | collective-permute-done | bytes 65568 | tf_op jit(solution)/shard_map/ppermute | solution.py:114
  (98 shorter events, 20.9 us)
Async XLA Ops:
  0.0 28.2 %copy-start = (bf16[8,256,2,2,128]{4,3,2,1,0:T(2,128)(2,1)S(1)}, bf16[8,256,2,2,128]{4,3,2,1,0:T(2,128)(2,1)}, u32[]{:S(2)}) copy-start(bf16[8,256,2,2,128]{4,3,2,1,0:T(2,128)(2,1)} %param.28) | copy-start | bytes 6291460
  1.0 8.1 %collective-permute-start.2 = (f32[8]{0:T(128)S(1)}, f32[8]{0:T(128)S(1)}, u32[]{:S(2)}, u32[]{:S(2)}) collective-permute-start(f32[8]{0:T(128)S(1)} %fusion.98), channel_id=1, source_target_pairs={{0,12},{4,0},{8,4},{12,8},{1,13},{5,1},{9,5},{13,9},{2,14},{6,2},{... | collective-permute-start | bytes 104 | tf_op jit(solution)/shard_map/ppermute | solution.py:140
  6.1 4.4 %collective-permute-start.1 = (f32[8]{0:T(128)S(1)}, f32[8]{0:T(128)S(1)}, u32[]{:S(2)}, u32[]{:S(2)}) collective-permute-start(f32[8]{0:T(128)S(1)} %fusion.98), channel_id=1, source_target_pairs={{0,8},{4,12},{8,0},{12,4},{1,9},{5,13},{9,1},{13,5},{2,10},{6,14},... | collective-permute-start | bytes 104 | tf_op jit(solution)/shard_map/ppermute | solution.py:140
  6.1 5.3 %collective-permute-start = (f32[8]{0:T(128)S(1)}, f32[8]{0:T(128)S(1)}, u32[]{:S(2)}, u32[]{:S(2)}) collective-permute-start(f32[8]{0:T(128)S(1)} %fusion.98), channel_id=1, source_target_pairs={{0,4},{4,8},{8,12},{12,0},{1,5},{5,9},{9,13},{13,1},{2,6},{6,10},{... | collective-permute-start | bytes 104 | tf_op jit(solution)/shard_map/ppermute | solution.py:140
  12.3 1.9 %collective-permute-start.5 = (bf16[8,2048]{1,0:T(8,128)(2,1)S(1)}, bf16[8,2048]{1,0:T(8,128)(2,1)S(1)}, u32[]{:S(2)}, u32[]{:S(2)}) collective-permute-start(bf16[8,2048]{1,0:T(8,128)(2,1)S(1)} %fusion.100), channel_id=1, source_target_pairs={{0,3},{1,0},{2,1},{3,2},{4,7},{5,4},{6,5},{7,6},{8,11},{9,8},{10,9... | collective-permute-start | bytes 98312 | tf_op jit(solution)/shard_map/ppermute | solution.py:97
  12.4 4.1 %collective-permute-start.4 = (bf16[8,2048]{1,0:T(8,128)(2,1)S(1)}, bf16[8,2048]{1,0:T(8,128)(2,1)S(1)}, u32[]{:S(2)}, u32[]{:S(2)}) collective-permute-start(bf16[8,2048]{1,0:T(8,128)(2,1)S(1)} %fusion.100), channel_id=1, source_target_pairs={{0,2},{1,3},{2,0},{3,1},{4,6},{5,7},{6,4},{7,5},{8,10},{9,11},{10,... | collective-permute-start | bytes 98312 | tf_op jit(solution)/shard_map/ppermute | solution.py:97
  13.9 3.3 %collective-permute-start.3 = (bf16[8,2048]{1,0:T(8,128)(2,1)S(1)}, bf16[8,2048]{1,0:T(8,128)(2,1)S(1)}, u32[]{:S(2)}, u32[]{:S(2)}) collective-permute-start(bf16[8,2048]{1,0:T(8,128)(2,1)S(1)} %fusion.100), channel_id=1, source_target_pairs={{0,1},{1,2},{2,3},{3,0},{4,5},{5,6},{6,7},{7,4},{8,9},{9,10},{10,1... | collective-permute-start | bytes 98312 | tf_op jit(solution)/shard_map/ppermute | solution.py:97
  24.2 7.1 %collective-permute-start.6 = (f32[8,2560]{1,0:T(8,128)S(1)}, f32[8,2560]{1,0:T(8,128)S(1)}, u32[]{:S(2)}, u32[]{:S(2)}) collective-permute-start(f32[8,2560]{1,0:T(8,128)S(1)} %get-tuple-element.65), channel_id=1, source_target_pairs={{0,4},{4,8},{8,12},{12,0},{1,5},{5,9},{9,13},{13,1},{2,6},{6,10},{... | collective-permute-start | bytes 245768 | tf_op jit(solution)/shard_map/ppermute | solution.py:114
  24.4 6.9 %collective-permute-start.8 = (f32[8,2560]{1,0:T(8,128)S(1)}, f32[8,2560]{1,0:T(8,128)S(1)}, u32[]{:S(2)}, u32[]{:S(2)}) collective-permute-start(f32[8,2560]{1,0:T(8,128)S(1)} %get-tuple-element.66), channel_id=1, source_target_pairs={{0,12},{4,0},{8,4},{12,8},{1,13},{5,1},{9,5},{13,9},{2,14},{6,2},{... | collective-permute-start | bytes 245768 | tf_op jit(solution)/shard_map/ppermute | solution.py:114
  28.1 6.1 %collective-permute-start.7 = (f32[8,2560]{1,0:T(8,128)S(1)}, f32[8,2560]{1,0:T(8,128)S(1)}, u32[]{:S(2)}, u32[]{:S(2)}) collective-permute-start(f32[8,2560]{1,0:T(8,128)S(1)} %get-tuple-element.67), channel_id=1, source_target_pairs={{0,8},{4,12},{8,0},{12,4},{1,9},{5,13},{9,1},{13,5},{2,10},{6,14},... | collective-permute-start | bytes 245768 | tf_op jit(solution)/shard_map/ppermute | solution.py:114
  28.2 20.1 %copy-start.1 = (bf16[8,2048]{1,0:T(8,128)(2,1)S(1)}, bf16[8,2048]{1,0:T(8,128)(2,1)}, u32[]{:S(2)}) copy-start(bf16[8,2048]{1,0:T(8,128)(2,1)} %param.20) | copy-start | bytes 98308
  28.7 34.9 %copy-start.2 = (f32[2048]{0:T(1024)S(1)}, f32[2048]{0:T(1024)}, u32[]{:S(2)}) copy-start(f32[2048]{0:T(1024)} %param.24) | copy-start | bytes 24580
  35.7 4.0 %collective-permute-start.11 = (bf16[8,2048]{1,0:T(8,128)(2,1)S(1)}, bf16[8,2048]{1,0:T(8,128)(2,1)S(1)}, u32[]{:S(2)}, u32[]{:S(2)}) collective-permute-start(bf16[8,2048]{1,0:T(8,128)(2,1)S(1)} %bitcast.100), channel_id=1, source_target_pairs={{0,12},{4,0},{8,4},{12,8},{1,13},{5,1},{9,5},{13,9},{2,14},{6,2},{... | collective-permute-start | bytes 98312 | tf_op jit(solution)/shard_map/ppermute | solution.py:97
  37.5 4.9 %collective-permute-start.10 = (bf16[8,2048]{1,0:T(8,128)(2,1)S(1)}, bf16[8,2048]{1,0:T(8,128)(2,1)S(1)}, u32[]{:S(2)}, u32[]{:S(2)}) collective-permute-start(bf16[8,2048]{1,0:T(8,128)(2,1)S(1)} %bitcast.101), channel_id=1, source_target_pairs={{0,8},{4,12},{8,0},{12,4},{1,9},{5,13},{9,1},{13,5},{2,10},{6,14},... | collective-permute-start | bytes 98312 | tf_op jit(solution)/shard_map/ppermute | solution.py:97
  37.5 5.7 %collective-permute-start.9 = (bf16[8,2048]{1,0:T(8,128)(2,1)S(1)}, bf16[8,2048]{1,0:T(8,128)(2,1)S(1)}, u32[]{:S(2)}, u32[]{:S(2)}) collective-permute-start(bf16[8,2048]{1,0:T(8,128)(2,1)S(1)} %bitcast.102), channel_id=1, source_target_pairs={{0,4},{4,8},{8,12},{12,0},{1,5},{5,9},{9,13},{13,1},{2,6},{6,10},{... | collective-permute-start | bytes 98312 | tf_op jit(solution)/shard_map/ppermute | solution.py:97
  48.4 1.4 %collective-permute-start.12 = (f32[16,2048]{1,0:T(8,128)S(1)}, f32[16,2048]{1,0:T(8,128)S(1)}, u32[]{:S(2)}, u32[]{:S(2)}) collective-permute-start(f32[16,2048]{1,0:T(8,128)S(1)} %select_bitcast_fusion.1), channel_id=1, source_target_pairs={{0,1},{1,0},{2,3},{3,2},{4,5},{5,4},{6,7},{7,6},{8,9},{9,8},{10,11... | collective-permute-start | bytes 393224 | tf_op jit(solution)/shard_map/ppermute | solution.py:114
  49.8 5.6 %collective-permute-start.13 = (f32[16,2048]{1,0:T(8,128)S(1)}, f32[16,2048]{1,0:T(8,128)S(1)}, u32[]{:S(2)}, u32[]{:S(2)}) collective-permute-start(f32[16,2048]{1,0:T(8,128)S(1)} %bitcast_add_fusion.1), channel_id=1, source_target_pairs={{0,2},{2,0},{1,3},{3,1},{4,6},{6,4},{5,7},{7,5},{8,10},{10,8},{9,1... | collective-permute-start | bytes 393224 | tf_op jit(solution)/shard_map/ppermute | solution.py:140
  55.4 1.4 %collective-permute-start.14 = (f32[16,2048]{1,0:T(8,128)S(1)}, f32[16,2048]{1,0:T(8,128)S(1)}, u32[]{:S(2)}, u32[]{:S(2)}) collective-permute-start(f32[16,2048]{1,0:T(8,128)S(1)} %add.289), channel_id=1, source_target_pairs={{0,1},{1,0},{2,3},{3,2},{4,5},{5,4},{6,7},{7,6},{8,9},{9,8},{10,11... | collective-permute-start | bytes 393224 | tf_op jit(solution)/shard_map/ppermute | solution.py:132
  57.1 3.5 %collective-permute-start.17 = (f32[32]{0:T(128)S(1)}, f32[32]{0:T(128)S(1)}, u32[]{:S(2)}, u32[]{:S(2)}) collective-permute-start(f32[32]{0:T(128)S(1)} %reduce_sum.62), channel_id=1, source_target_pairs={{0,12},{4,0},{8,4},{12,8},{1,13},{5,1},{9,5},{13,9},{2,14},{6,2},{... | collective-permute-start | bytes 392 | tf_op jit(solution)/shard_map/ppermute | solution.py:140
  57.9 4.4 %collective-permute-start.16 = (f32[32]{0:T(128)S(1)}, f32[32]{0:T(128)S(1)}, u32[]{:S(2)}, u32[]{:S(2)}) collective-permute-start(f32[32]{0:T(128)S(1)} %reduce_sum.62), channel_id=1, source_target_pairs={{0,8},{4,12},{8,0},{12,4},{1,9},{5,13},{9,1},{13,5},{2,10},{6,14},... | collective-permute-start | bytes 392 | tf_op jit(solution)/shard_map/ppermute | solution.py:140
  58.3 5.3 %collective-permute-start.15 = (f32[32]{0:T(128)S(1)}, f32[32]{0:T(128)S(1)}, u32[]{:S(2)}, u32[]{:S(2)}) collective-permute-start(f32[32]{0:T(128)S(1)} %reduce_sum.62), channel_id=1, source_target_pairs={{0,4},{4,8},{8,12},{12,0},{1,5},{5,9},{9,13},{13,1},{2,6},{6,10},{... | collective-permute-start | bytes 392 | tf_op jit(solution)/shard_map/ppermute | solution.py:140
  66.4 28.5 %slice-start = ((s8[14680064]{0:T(1024)(128)(4,1)}), s8[4194304]{0:T(1024)(128)(4,1)S(1)}, s32[]{:S(2)}) async-start(s8[14680064]{0:T(1024)(128)(4,1)} %bitcast.85), calls=%async_computation | async-start | bytes 8388608
  69.3 25.6 %slice-start.1 = ((s8[14680064]{0:T(1024)(128)(4,1)}), s8[4194304]{0:T(1024)(128)(4,1)S(1)}, s32[]{:S(2)}) async-start(s8[14680064]{0:T(1024)(128)(4,1)} %bitcast.85), calls=%async_computation.1 | async-start | bytes 8388608
  74.9 20.0 %slice-start.2 = ((s8[14680064]{0:T(1024)(128)(4,1)}), s8[4194304]{0:T(1024)(128)(4,1)S(1)}, s32[]{:S(2)}) async-start(s8[14680064]{0:T(1024)(128)(4,1)} %bitcast.85), calls=%async_computation.2 | async-start | bytes 8388608
  80.6 9.3 %collective-permute-start.18 = (bf16[32,1792]{1,0:T(8,128)(2,1)S(1)}, bf16[32,1792]{1,0:T(8,128)(2,1)S(1)}, u32[]{:S(2)}, u32[]{:S(2)}) collective-permute-start(bf16[32,1792]{1,0:T(8,128)(2,1)S(1)} %get-tuple-element.18), channel_id=1, source_target_pairs={{0,4},{4,8},{8,12},{12,0},{1,5},{5,9},{9,13},{13,1},{2,6},{6,10},{... | collective-permute-start | bytes 344072 | tf_op jit(solution)/shard_map/ppermute | solution.py:163
  80.8 10.5 %collective-permute-start.19 = (bf16[32,1792]{1,0:T(8,128)(2,1)S(1)}, bf16[32,1792]{1,0:T(8,128)(2,1)S(1)}, u32[]{:S(2)}, u32[]{:S(2)}) collective-permute-start(bf16[32,1792]{1,0:T(8,128)(2,1)S(1)} %get-tuple-element.19), channel_id=1, source_target_pairs={{0,8},{4,12},{8,0},{12,4},{1,9},{5,13},{9,1},{13,5},{2,10},{6,14},... | collective-permute-start | bytes 344072 | tf_op jit(solution)/shard_map/ppermute | solution.py:163
  82.6 8.7 %collective-permute-start.20 = (bf16[32,1792]{1,0:T(8,128)(2,1)S(1)}, bf16[32,1792]{1,0:T(8,128)(2,1)S(1)}, u32[]{:S(2)}, u32[]{:S(2)}) collective-permute-start(bf16[32,1792]{1,0:T(8,128)(2,1)S(1)} %pad_maximum_fusion.3), channel_id=1, source_target_pairs={{0,12},{4,0},{8,4},{12,8},{1,13},{5,1},{9,5},{13,9},{2,14},{6,2},{... | collective-permute-start | bytes 344072 | tf_op jit(solution)/shard_map/ppermute | solution.py:163
  91.4 8.9 %collective-permute-start.23 = (bf16[32,896]{1,0:T(8,128)(2,1)S(1)}, bf16[32,896]{1,0:T(8,128)(2,1)S(1)}, u32[]{:S(2)}, u32[]{:S(2)}) collective-permute-start(bf16[32,896]{1,0:T(8,128)(2,1)S(1)} %fusion.94), channel_id=1, source_target_pairs={{0,12},{4,0},{8,4},{12,8},{1,13},{5,1},{9,5},{13,9},{2,14},{6,2},{... | collective-permute-start | bytes 172040 | tf_op jit(solution)/shard_map/ppermute | solution.py:176
  94.0 5.6 %collective-permute-start.22 = (bf16[32,896]{1,0:T(8,128)(2,1)S(1)}, bf16[32,896]{1,0:T(8,128)(2,1)S(1)}, u32[]{:S(2)}, u32[]{:S(2)}) collective-permute-start(bf16[32,896]{1,0:T(8,128)(2,1)S(1)} %fusion.94), channel_id=1, source_target_pairs={{0,8},{4,12},{8,0},{12,4},{1,9},{5,13},{9,1},{13,5},{2,10},{6,14},... | collective-permute-start | bytes 172040 | tf_op jit(solution)/shard_map/ppermute | solution.py:176
  94.9 6.2 %collective-permute-start.21 = (bf16[32,896]{1,0:T(8,128)(2,1)S(1)}, bf16[32,896]{1,0:T(8,128)(2,1)S(1)}, u32[]{:S(2)}, u32[]{:S(2)}) collective-permute-start(bf16[32,896]{1,0:T(8,128)(2,1)S(1)} %fusion.94), channel_id=1, source_target_pairs={{0,4},{4,8},{8,12},{12,0},{1,5},{5,9},{9,13},{13,1},{2,6},{6,10},{... | collective-permute-start | bytes 172040 | tf_op jit(solution)/shard_map/ppermute | solution.py:176
  102.0 1.4 %collective-permute-start.24 = (f32[2,8,2048]{2,1,0:T(8,128)S(1)}, f32[2,8,2048]{2,1,0:T(8,128)S(1)}, u32[]{:S(2)}, u32[]{:S(2)}) collective-permute-start(f32[2,8,2048]{2,1,0:T(8,128)S(1)} %select_bitcast_fusion), channel_id=1, source_target_pairs={{0,1},{1,0},{2,3},{3,2},{4,5},{5,4},{6,7},{7,6},{8,9},{9,8},{10,11... | collective-permute-start | bytes 393224 | tf_op jit(solution)/shard_map/ppermute | solution.py:114
  103.4 4.3 %collective-permute-start.25 = (f32[8,2048]{1,0:T(8,128)S(1)}, f32[8,2048]{1,0:T(8,128)S(1)}, u32[]{:S(2)}, u32[]{:S(2)}) collective-permute-start(f32[8,2048]{1,0:T(8,128)S(1)} %select_bitcast_fusion.7), channel_id=1, source_target_pairs={{0,2},{2,0},{1,3},{3,1},{4,6},{6,4},{5,7},{7,5},{8,10},{10,8},{9,1... | collective-permute-start | bytes 196616 | tf_op jit(solution)/shard_map/ppermute | solution.py:114
  (1 other events, 14.4 us)

commit v15 on v14

--- a/solution.py
+++ b/solution.py
@@ -126,12 +126,18 @@
 def all_sum_cs(parts):
     n_col = lax.axis_size("col")
     n_side = lax.axis_size("side")
+    n_pool = lax.axis_size("pool")
     side = lax.axis_index("side")
     mine = scatter_sum(parts.reshape((n_side, -1) + parts.shape[1:]), "side", n_side)
     mine = all_sum(mine, "col", n_col)
+    squares = all_sum(jnp.sum(mine * mine, axis=1), "pool", n_pool)
     got = [mine] + [lax.ppermute(mine, "side", shift_pairs(n_side, k)) for k in range(1, n_side)]
+    got_sq = [squares] + [
+        lax.ppermute(squares, "side", shift_pairs(n_side, k)) for k in range(1, n_side)
+    ]
     ordered = [lax.select_n((side - j) % n_side, *got) for j in range(n_side)]
-    return jnp.stack(ordered).reshape(parts.shape)
+    ordered_sq = [lax.select_n((side - j) % n_side, *got_sq) for j in range(n_side)]
+    return jnp.stack(ordered).reshape(parts.shape), jnp.concatenate(ordered_sq)
 
 
 def all_sum(x, axis, n):
@@ -228,10 +234,9 @@
         cs_index * rows_here,
         0,
     )
-    resid_all = all_sum_cs(out_part)
+    resid_all, squares_mid = all_sum_cs(out_part)
     residual = lax.dynamic_slice_in_dim(resid_all, cs_index * rows_here, rows_here, 0)
 
-    squares_mid = all_sum(jnp.sum(resid_all * resid_all, axis=1), "pool", n_pool)
     ffn_all = (
         resid_all * lax.rsqrt(squares_mid / D + epsilon)[:, None] * ffn_gain[None, :]
     ).astype(jnp.bfloat16)

time: 109 us -> 111 us (1.018)
  waiting for transfers between devices: 36.5 us -> 37.7 us
    ppermute x3, waiting for transfers between devices: 1.38 us -> 2.7 us  [scatter_matmul(): lax.ppermute(pieces[k - 1], axis, shift_pairs(n, k)).astype(jnp.float32)]
  transfers between devices with their start and end apart: 26 -> 27, of which waited for: 19 -> 20; matrix products, arithmetic and copies ran while one was open for 9% -> 9% of each run, Pallas kernels for 0% -> 0%
where the time goes in v15:
time: 111 us; the launch traced here: 110 us
  matrix products  38 us (34%)
  waiting for transfers between devices  37.7 us (34%)
  starting transfers between devices  27.8 us (25%)
  other arithmetic  5.65 us (5%)
    dot_general x8, matrix products, block(): jnp.dot(x, lax.dynamic_slice_in_dim(w, j * chunk, chunk, 1), preferred_el...  22.1 us
    ppermute x6, waiting for transfers between devices, scatter_sum(): lax.ppermute(piece, axis, shift_pairs(n, k)).astype(jnp.float32)  11.5 us
    ppermute x7, waiting for transfers between devices, all_sum(): total = total + lax.ppermute(x, axis, shift_pairs(n, k))  10.4 us
    ppermute x7, starting transfers between devices, all_sum(): total = total + lax.ppermute(x, axis, shift_pairs(n, k))  10.3 us
    ppermute x6, waiting for transfers between devices, gather_rows(): got = [x] + [lax.ppermute(x, axis, shift_pairs(n, k)) for k in range(1, n)]  8.12 us
    dot_general x1, matrix products, local(): jnp.einsum('rf,fgc->rgc', by_slot, w_qkv, preferred_element_type=jnp.floa...  6.85 us
    dot_general x1, matrix products, local(): out_part = jnp.dot(by_row, w_out, preferred_element_type=jnp.float32)  5.09 us
    ppermute x6, starting transfers between devices, scatter_sum(): lax.ppermute(piece, axis, shift_pairs(n, k)).astype(jnp.float32)  4.98 us
  transfers between devices with their start and end apart: 27, of which 20 were waited for; matrix products, arithmetic and copies ran while one was open for 9% of the time, Pallas kernels for 0%

profile of v15, /device:TPU:0, one launch (start us, length us, event | category | flops | bytes accessed | tf_op | source)
XLA Modules:
  0.0 110.3 jit_solution(17152298315400763146)
XLA Ops:
  1.0 5.1 %collective-permute-start.2 = (f32[8]{0:T(128)S(1)}, f32[8]{0:T(128)S(1)}, u32[]{:S(2)}, u32[]{:S(2)}) collective-permute-start(f32[8]{0:T(128)S(1)} %fusion.98), channel_id=1, source_target_pairs={{0,12},{4,0},{8,4},{12,8},{1,13},{5,1},{9,5},{13,9},{2,14},{6,2},{... | collective-permute-start | bytes 104 | tf_op jit(solution)/shard_map/ppermute | solution.py:146
  9.1 1.4 %collective-permute-done.1 = f32[8]{0:T(128)S(1)} collective-permute-done((f32[8]{0:T(128)S(1)}, f32[8]{0:T(128)S(1)}, u32[]{:S(2)}, u32[]{:S(2)}) %collective-permute-start.1) | collective-permute-done | bytes 64 | tf_op jit(solution)/shard_map/ppermute | solution.py:146
  12.4 1.6 %collective-permute-start.4 = (bf16[8,2048]{1,0:T(8,128)(2,1)S(1)}, bf16[8,2048]{1,0:T(8,128)(2,1)S(1)}, u32[]{:S(2)}, u32[]{:S(2)}) collective-permute-start(bf16[8,2048]{1,0:T(8,128)(2,1)S(1)} %fusion.100), channel_id=1, source_target_pairs={{0,2},{1,3},{2,0},{3,1},{4,6},{5,7},{6,4},{7,5},{8,10},{9,11},{10,... | collective-permute-start | bytes 98312 | tf_op jit(solution)/shard_map/ppermute | solution.py:97
  14.2 2.3 %collective-permute-done.4 = bf16[8,2048]{1,0:T(8,128)(2,1)S(1)} collective-permute-done((bf16[8,2048]{1,0:T(8,128)(2,1)S(1)}, bf16[8,2048]{1,0:T(8,128)(2,1)S(1)}, u32[]{:S(2)}, u32[]{:S(2)}) %collective-permute-start.4) | collective-permute-done | bytes 32800 | tf_op jit(solution)/shard_map/ppermute | solution.py:97
  17.3 6.9 %fusion.26 = f32[2,4,8,1280]{3,2,1,0:T(8,128)S(1)} fusion(bf16[2048,2,1280]{2,1,0:T(2,128)(2,1)} %param.22, bf16[8,2048]{1,0:T(8,128)(2,1)S(1)} %collective-permute-done.5, bf16[8,2048]{1,0:T(8,128)(2,1)S(1)} %collective-permute-done.4, bf16[8,2048]{1,0:T(8,128)(2,1)S(1)} %collective-permute-done.3, bf16[8,2048]{1,0:T(8,128)(2,1)S(1)} %fusion.100, ...), kind=kOutput, calls=%fused_computation.26 | convolution fusion | flops 340329472 | bytes 10944640 | tf_op jit(solution)/shard_map/rf,fgc->rgc/dot_general | solution.py:221
  24.4 3.7 %collective-permute-start.8 = (f32[8,2560]{1,0:T(8,128)S(1)}, f32[8,2560]{1,0:T(8,128)S(1)}, u32[]{:S(2)}, u32[]{:S(2)}) collective-permute-start(f32[8,2560]{1,0:T(8,128)S(1)} %get-tuple-element.68), channel_id=1, source_target_pairs={{0,12},{4,0},{8,4},{12,8},{1,13},{5,1},{9,5},{13,9},{2,14},{6,2},{... | collective-permute-start | bytes 245768 | tf_op jit(solution)/shard_map/ppermute | solution.py:114
  28.7 2.6 %collective-permute-done.6 = f32[8,2560]{1,0:T(8,128)S(1)} collective-permute-done((f32[8,2560]{1,0:T(8,128)S(1)}, f32[8,2560]{1,0:T(8,128)S(1)}, u32[]{:S(2)}, u32[]{:S(2)}) %collective-permute-start.6) | collective-permute-done | bytes 81952 | tf_op jit(solution)/shard_map/ppermute | solution.py:114
  31.3 2.9 %collective-permute-done.7 = f32[8,2560]{1,0:T(8,128)S(1)} collective-permute-done((f32[8,2560]{1,0:T(8,128)S(1)}, f32[8,2560]{1,0:T(8,128)S(1)}, u32[]{:S(2)}, u32[]{:S(2)}) %collective-permute-start.7) | collective-permute-done | bytes 81952 | tf_op jit(solution)/shard_map/ppermute | solution.py:114
  35.7 1.8 %collective-permute-start.11 = (bf16[8,2048]{1,0:T(8,128)(2,1)S(1)}, bf16[8,2048]{1,0:T(8,128)(2,1)S(1)}, u32[]{:S(2)}, u32[]{:S(2)}) collective-permute-start(bf16[8,2048]{1,0:T(8,128)(2,1)S(1)} %bitcast.100), channel_id=1, source_target_pairs={{0,12},{4,0},{8,4},{12,8},{1,13},{5,1},{9,5},{13,9},{2,14},{6,2},{... | collective-permute-start | bytes 98312 | tf_op jit(solution)/shard_map/ppermute | solution.py:97
  38.2 1.5 %collective-permute-done.11 = bf16[8,2048]{1,0:T(8,128)(2,1)S(1)} collective-permute-done((bf16[8,2048]{1,0:T(8,128)(2,1)S(1)}, bf16[8,2048]{1,0:T(8,128)(2,1)S(1)}, u32[]{:S(2)}, u32[]{:S(2)}) %collective-permute-start.11) | collective-permute-done | bytes 32800 | tf_op jit(solution)/shard_map/ppermute | solution.py:97
  39.6 2.7 %collective-permute-done.10 = bf16[8,2048]{1,0:T(8,128)(2,1)S(1)} collective-permute-done((bf16[8,2048]{1,0:T(8,128)(2,1)S(1)}, bf16[8,2048]{1,0:T(8,128)(2,1)S(1)}, u32[]{:S(2)}, u32[]{:S(2)}) %collective-permute-start.10) | collective-permute-done | bytes 32800 | tf_op jit(solution)/shard_map/ppermute | solution.py:97
  43.2 5.1 %fusion.39 = f32[32,2048]{1,0:T(8,128)S(1)} fusion(bf16[2048,2048]{1,0:T(8,128)(2,1)} %param.23, bf16[8,2048]{1,0:T(8,128)(2,1)S(1)} %collective-permute-done.11, bf16[8,2048]{1,0:T(8,128)(2,1)S(1)} %collective-permute-done.10, bf16[8,2048]{1,0:T(8,128)(2,1)S(1)} %collective-permute-done.9, bf16[8,2048]{1,0:T(8,128)(2,1)S(1)} %bitcast.103, s32[32]{0:T(128)S(1)} %fusion.130), kind=kOutput, calls=%fused_computation.33 | convolution fusion | flops 273220608 | bytes 8781952 | tf_op jit(solution)/shard_map/dot_general | solution.py:229
  48.5 1.3 %collective-permute-done.12 = f32[16,2048]{1,0:T(8,128)S(1)} collective-permute-done((f32[16,2048]{1,0:T(8,128)S(1)}, f32[16,2048]{1,0:T(8,128)S(1)}, u32[]{:S(2)}, u32[]{:S(2)}) %collective-permute-start.12) | collective-permute-done | bytes 131104 | tf_op jit(solution)/shard_map/ppermute | solution.py:114
  50.8 4.7 %collective-permute-done.13 = f32[16,2048]{1,0:T(8,128)S(1)} collective-permute-done((f32[16,2048]{1,0:T(8,128)S(1)}, f32[16,2048]{1,0:T(8,128)S(1)}, u32[]{:S(2)}, u32[]{:S(2)}) %collective-permute-start.13) | collective-permute-done | bytes 131104 | tf_op jit(solution)/shard_map/ppermute | solution.py:146
  56.8 1.9 %collective-permute-start.15 = (f32[16]{0:T(128)S(1)}, f32[16]{0:T(128)S(1)}, u32[]{:S(2)}, u32[]{:S(2)}) collective-permute-start(f32[16]{0:T(128)S(1)} %get-tuple-element.65), channel_id=1, source_target_pairs={{0,4},{4,8},{8,12},{12,0},{1,5},{5,9},{9,13},{13,1},{2,6},{6,10},{... | collective-permute-start | bytes 200 | tf_op jit(solution)/shard_map/ppermute | solution.py:146
  59.1 1.7 %collective-permute-done.16 = f32[16]{0:T(128)S(1)} collective-permute-done((f32[16]{0:T(128)S(1)}, f32[16]{0:T(128)S(1)}, u32[]{:S(2)}, u32[]{:S(2)}) %collective-permute-start.16) | collective-permute-done | bytes 96 | tf_op jit(solution)/shard_map/ppermute | solution.py:146
  60.9 1.3 %collective-permute-done.15 = f32[16]{0:T(128)S(1)} collective-permute-done((f32[16]{0:T(128)S(1)}, f32[16]{0:T(128)S(1)}, u32[]{:S(2)}, u32[]{:S(2)}) %collective-permute-start.15) | collective-permute-done | bytes 96 | tf_op jit(solution)/shard_map/ppermute | solution.py:146
  63.8 2.7 %fusion.55 = bf16[32,896]{1,0:T(8,128)(2,1)S(1)} fusion(bf16[32,2048]{1,0:T(8,128)(2,1)S(1)} %multiply_convert_fusion, bf16[2048,3584]{1,0:T(8,128)(2,1)} %param.26, s32[]{:T(128)S(6)} %select_n.240), kind=kOutput, calls=%fused_computation.40 | convolution fusion | flops 117469184 | bytes 3858436 | tf_op jit(solution)/shard_map/dot_general | solution.py:156
  66.5 2.9 %fusion.52 = bf16[32,896]{1,0:T(8,128)(2,1)S(1)} fusion(bf16[32,2048]{1,0:T(8,128)(2,1)S(1)} %multiply_convert_fusion, bf16[2048,3584]{1,0:T(8,128)(2,1)} %param.25, s32[]{:T(128)S(6)} %select_n.240), kind=kOutput, calls=%fused_computation.39 | convolution fusion | flops 117469184 | bytes 3858436 | tf_op jit(solution)/shard_map/dot_general | solution.py:156
  69.4 2.9 %fusion.49 = bf16[32,896]{1,0:T(8,128)(2,1)S(1)} fusion(bf16[32,2048]{1,0:T(8,128)(2,1)S(1)} %multiply_convert_fusion, bf16[2048,3584]{1,0:T(8,128)(2,1)} %param.26, s32[]{:T(128)S(6)} %select_n.239), kind=kOutput, calls=%fused_computation.38 | convolution fusion | flops 117469184 | bytes 3858436 | tf_op jit(solution)/shard_map/dot_general | solution.py:156
  72.3 2.7 %fusion.46 = bf16[32,896]{1,0:T(8,128)(2,1)S(1)} fusion(bf16[32,2048]{1,0:T(8,128)(2,1)S(1)} %multiply_convert_fusion, bf16[2048,3584]{1,0:T(8,128)(2,1)} %param.25, s32[]{:T(128)S(6)} %select_n.239), kind=kOutput, calls=%fused_computation.37 | convolution fusion | flops 117469184 | bytes 3858436 | tf_op jit(solution)/shard_map/dot_general | solution.py:156
  75.0 2.9 %fusion.43 = bf16[32,896]{1,0:T(8,128)(2,1)S(1)} fusion(bf16[32,2048]{1,0:T(8,128)(2,1)S(1)} %multiply_convert_fusion, bf16[2048,3584]{1,0:T(8,128)(2,1)} %param.26, s32[]{:T(128)S(6)} %select_n.238), kind=kOutput, calls=%fused_computation.36 | convolution fusion | flops 117469184 | bytes 3858436 | tf_op jit(solution)/shard_map/dot_general | solution.py:156
  77.9 2.7 %fusion.40 = bf16[32,896]{1,0:T(8,128)(2,1)S(1)} fusion(bf16[32,2048]{1,0:T(8,128)(2,1)S(1)} %multiply_convert_fusion, bf16[2048,3584]{1,0:T(8,128)(2,1)} %param.25, s32[]{:T(128)S(6)} %select_n.238), kind=kOutput, calls=%fused_computation.35 | convolution fusion | flops 117469184 | bytes 3858436 | tf_op jit(solution)/shard_map/dot_general | solution.py:156
  80.9 1.8 %collective-permute-start.20 = (bf16[32,1792]{1,0:T(8,128)(2,1)S(1)}, bf16[32,1792]{1,0:T(8,128)(2,1)S(1)}, u32[]{:S(2)}, u32[]{:S(2)}) collective-permute-start(bf16[32,1792]{1,0:T(8,128)(2,1)S(1)} %get-tuple-element.19), channel_id=1, source_target_pairs={{0,8},{4,12},{8,0},{12,4},{1,9},{5,13},{9,1},{13,5},{2,10},{6,14},... | collective-permute-start | bytes 344072 | tf_op jit(solution)/shard_map/ppermute | solution.py:169
  82.7 1.9 %collective-permute-start.21 = (bf16[32,1792]{1,0:T(8,128)(2,1)S(1)}, bf16[32,1792]{1,0:T(8,128)(2,1)S(1)}, u32[]{:S(2)}, u32[]{:S(2)}) collective-permute-start(bf16[32,1792]{1,0:T(8,128)(2,1)S(1)} %pad_maximum_fusion.3), channel_id=1, source_target_pairs={{0,12},{4,0},{8,4},{12,8},{1,13},{5,1},{9,5},{13,9},{2,14},{6,2},{... | collective-permute-start | bytes 344072 | tf_op jit(solution)/shard_map/ppermute | solution.py:169
  84.6 2.7 %fusion.61 = bf16[32,896]{1,0:T(8,128)(2,1)S(1)} fusion(bf16[32,2048]{1,0:T(8,128)(2,1)S(1)} %multiply_convert_fusion, bf16[2048,3584]{1,0:T(8,128)(2,1)} %param.26, s32[]{:T(128)S(6)} %select_n.241), kind=kOutput, calls=%fused_computation.42 | convolution fusion | flops 117469184 | bytes 3858436 | tf_op jit(solution)/shard_map/dot_general | solution.py:156
  87.3 2.7 %fusion.58 = bf16[32,896]{1,0:T(8,128)(2,1)S(1)} fusion(bf16[32,2048]{1,0:T(8,128)(2,1)S(1)} %multiply_convert_fusion, bf16[2048,3584]{1,0:T(8,128)(2,1)} %param.25, s32[]{:T(128)S(6)} %select_n.241), kind=kOutput, calls=%fused_computation.41 | convolution fusion | flops 117469184 | bytes 3858436 | tf_op jit(solution)/shard_map/dot_general | solution.py:156
  90.0 2.7 %collective-permute-done.20 = bf16[32,1792]{1,0:T(8,128)(2,1)S(1)} collective-permute-done((bf16[32,1792]{1,0:T(8,128)(2,1)S(1)}, bf16[32,1792]{1,0:T(8,128)(2,1)S(1)}, u32[]{:S(2)}, u32[]{:S(2)}) %collective-permute-start.20) | collective-permute-done | bytes 114720 | tf_op jit(solution)/shard_map/ppermute | solution.py:169
  92.8 2.7 %collective-permute-start.24 = (bf16[32,896]{1,0:T(8,128)(2,1)S(1)}, bf16[32,896]{1,0:T(8,128)(2,1)S(1)}, u32[]{:S(2)}, u32[]{:S(2)}) collective-permute-start(bf16[32,896]{1,0:T(8,128)(2,1)S(1)} %fusion.94), channel_id=1, source_target_pairs={{0,12},{4,0},{8,4},{12,8},{1,13},{5,1},{9,5},{13,9},{2,14},{6,2},{... | collective-permute-start | bytes 172040 | tf_op jit(solution)/shard_map/ppermute | solution.py:182
  97.5 4.0 %collective-permute-done.23 = bf16[32,896]{1,0:T(8,128)(2,1)S(1)} collective-permute-done((bf16[32,896]{1,0:T(8,128)(2,1)S(1)}, bf16[32,896]{1,0:T(8,128)(2,1)S(1)}, u32[]{:S(2)}, u32[]{:S(2)}) %collective-permute-start.23) | collective-permute-done | bytes 57376 | tf_op jit(solution)/shard_map/ppermute | solution.py:182
  104.0 1.3 %collective-permute-done.25 = f32[2,8,2048]{2,1,0:T(8,128)S(1)} collective-permute-done((f32[2,8,2048]{2,1,0:T(8,128)S(1)}, f32[2,8,2048]{2,1,0:T(8,128)S(1)}, u32[]{:S(2)}, u32[]{:S(2)}) %collective-permute-start.25) | collective-permute-done | bytes 131104 | tf_op jit(solution)/shard_map/ppermute | solution.py:114
  106.3 3.4 %collective-permute-done.26 = f32[8,2048]{1,0:T(8,128)S(1)} collective-permute-done((f32[8,2048]{1,0:T(8,128)S(1)}, f32[8,2048]{1,0:T(8,128)S(1)}, u32[]{:S(2)}, u32[]{:S(2)}) %collective-permute-start.26) | collective-permute-done | bytes 65568 | tf_op jit(solution)/shard_map/ppermute | solution.py:114
  (101 shorter events, 21.4 us)
Async XLA Ops:
  0.0 28.2 %copy-start = (bf16[8,256,2,2,128]{4,3,2,1,0:T(2,128)(2,1)S(1)}, bf16[8,256,2,2,128]{4,3,2,1,0:T(2,128)(2,1)}, u32[]{:S(2)}) copy-start(bf16[8,256,2,2,128]{4,3,2,1,0:T(2,128)(2,1)} %param.28) | copy-start | bytes 6291460
  1.0 8.1 %collective-permute-start.2 = (f32[8]{0:T(128)S(1)}, f32[8]{0:T(128)S(1)}, u32[]{:S(2)}, u32[]{:S(2)}) collective-permute-start(f32[8]{0:T(128)S(1)} %fusion.98), channel_id=1, source_target_pairs={{0,12},{4,0},{8,4},{12,8},{1,13},{5,1},{9,5},{13,9},{2,14},{6,2},{... | collective-permute-start | bytes 104 | tf_op jit(solution)/shard_map/ppermute | solution.py:146
  6.1 4.4 %collective-permute-start.1 = (f32[8]{0:T(128)S(1)}, f32[8]{0:T(128)S(1)}, u32[]{:S(2)}, u32[]{:S(2)}) collective-permute-start(f32[8]{0:T(128)S(1)} %fusion.98), channel_id=1, source_target_pairs={{0,8},{4,12},{8,0},{12,4},{1,9},{5,13},{9,1},{13,5},{2,10},{6,14},... | collective-permute-start | bytes 104 | tf_op jit(solution)/shard_map/ppermute | solution.py:146
  6.1 5.3 %collective-permute-start = (f32[8]{0:T(128)S(1)}, f32[8]{0:T(128)S(1)}, u32[]{:S(2)}, u32[]{:S(2)}) collective-permute-start(f32[8]{0:T(128)S(1)} %fusion.98), channel_id=1, source_target_pairs={{0,4},{4,8},{8,12},{12,0},{1,5},{5,9},{9,13},{13,1},{2,6},{6,10},{... | collective-permute-start | bytes 104 | tf_op jit(solution)/shard_map/ppermute | solution.py:146
  12.3 1.9 %collective-permute-start.5 = (bf16[8,2048]{1,0:T(8,128)(2,1)S(1)}, bf16[8,2048]{1,0:T(8,128)(2,1)S(1)}, u32[]{:S(2)}, u32[]{:S(2)}) collective-permute-start(bf16[8,2048]{1,0:T(8,128)(2,1)S(1)} %fusion.100), channel_id=1, source_target_pairs={{0,3},{1,0},{2,1},{3,2},{4,7},{5,4},{6,5},{7,6},{8,11},{9,8},{10,9... | collective-permute-start | bytes 98312 | tf_op jit(solution)/shard_map/ppermute | solution.py:97
  12.4 4.1 %collective-permute-start.4 = (bf16[8,2048]{1,0:T(8,128)(2,1)S(1)}, bf16[8,2048]{1,0:T(8,128)(2,1)S(1)}, u32[]{:S(2)}, u32[]{:S(2)}) collective-permute-start(bf16[8,2048]{1,0:T(8,128)(2,1)S(1)} %fusion.100), channel_id=1, source_target_pairs={{0,2},{1,3},{2,0},{3,1},{4,6},{5,7},{6,4},{7,5},{8,10},{9,11},{10,... | collective-permute-start | bytes 98312 | tf_op jit(solution)/shard_map/ppermute | solution.py:97
  13.9 3.3 %collective-permute-start.3 = (bf16[8,2048]{1,0:T(8,128)(2,1)S(1)}, bf16[8,2048]{1,0:T(8,128)(2,1)S(1)}, u32[]{:S(2)}, u32[]{:S(2)}) collective-permute-start(bf16[8,2048]{1,0:T(8,128)(2,1)S(1)} %fusion.100), channel_id=1, source_target_pairs={{0,1},{1,2},{2,3},{3,0},{4,5},{5,6},{6,7},{7,4},{8,9},{9,10},{10,1... | collective-permute-start | bytes 98312 | tf_op jit(solution)/shard_map/ppermute | solution.py:97
  24.2 7.1 %collective-permute-start.6 = (f32[8,2560]{1,0:T(8,128)S(1)}, f32[8,2560]{1,0:T(8,128)S(1)}, u32[]{:S(2)}, u32[]{:S(2)}) collective-permute-start(f32[8,2560]{1,0:T(8,128)S(1)} %get-tuple-element.67), channel_id=1, source_target_pairs={{0,4},{4,8},{8,12},{12,0},{1,5},{5,9},{9,13},{13,1},{2,6},{6,10},{... | collective-permute-start | bytes 245768 | tf_op jit(solution)/shard_map/ppermute | solution.py:114
  24.4 6.9 %collective-permute-start.8 = (f32[8,2560]{1,0:T(8,128)S(1)}, f32[8,2560]{1,0:T(8,128)S(1)}, u32[]{:S(2)}, u32[]{:S(2)}) collective-permute-start(f32[8,2560]{1,0:T(8,128)S(1)} %get-tuple-element.68), channel_id=1, source_target_pairs={{0,12},{4,0},{8,4},{12,8},{1,13},{5,1},{9,5},{13,9},{2,14},{6,2},{... | collective-permute-start | bytes 245768 | tf_op jit(solution)/shard_map/ppermute | solution.py:114
  28.1 6.1 %collective-permute-start.7 = (f32[8,2560]{1,0:T(8,128)S(1)}, f32[8,2560]{1,0:T(8,128)S(1)}, u32[]{:S(2)}, u32[]{:S(2)}) collective-permute-start(f32[8,2560]{1,0:T(8,128)S(1)} %get-tuple-element.69), channel_id=1, source_target_pairs={{0,8},{4,12},{8,0},{12,4},{1,9},{5,13},{9,1},{13,5},{2,10},{6,14},... | collective-permute-start | bytes 245768 | tf_op jit(solution)/shard_map/ppermute | solution.py:114
  28.7 35.0 %copy-start.2 = (f32[2048]{0:T(1024)S(1)}, f32[2048]{0:T(1024)}, u32[]{:S(2)}) copy-start(f32[2048]{0:T(1024)} %param.24) | copy-start | bytes 24580
  35.7 4.0 %collective-permute-start.11 = (bf16[8,2048]{1,0:T(8,128)(2,1)S(1)}, bf16[8,2048]{1,0:T(8,128)(2,1)S(1)}, u32[]{:S(2)}, u32[]{:S(2)}) collective-permute-start(bf16[8,2048]{1,0:T(8,128)(2,1)S(1)} %bitcast.100), channel_id=1, source_target_pairs={{0,12},{4,0},{8,4},{12,8},{1,13},{5,1},{9,5},{13,9},{2,14},{6,2},{... | collective-permute-start | bytes 98312 | tf_op jit(solution)/shard_map/ppermute | solution.py:97
  37.5 4.9 %collective-permute-start.10 = (bf16[8,2048]{1,0:T(8,128)(2,1)S(1)}, bf16[8,2048]{1,0:T(8,128)(2,1)S(1)}, u32[]{:S(2)}, u32[]{:S(2)}) collective-permute-start(bf16[8,2048]{1,0:T(8,128)(2,1)S(1)} %bitcast.101), channel_id=1, source_target_pairs={{0,8},{4,12},{8,0},{12,4},{1,9},{5,13},{9,1},{13,5},{2,10},{6,14},... | collective-permute-start | bytes 98312 | tf_op jit(solution)/shard_map/ppermute | solution.py:97
  37.5 5.7 %collective-permute-start.9 = (bf16[8,2048]{1,0:T(8,128)(2,1)S(1)}, bf16[8,2048]{1,0:T(8,128)(2,1)S(1)}, u32[]{:S(2)}, u32[]{:S(2)}) collective-permute-start(bf16[8,2048]{1,0:T(8,128)(2,1)S(1)} %bitcast.102), channel_id=1, source_target_pairs={{0,4},{4,8},{8,12},{12,0},{1,5},{5,9},{9,13},{13,1},{2,6},{6,10},{... | collective-permute-start | bytes 98312 | tf_op jit(solution)/shard_map/ppermute | solution.py:97
  48.4 1.4 %collective-permute-start.12 = (f32[16,2048]{1,0:T(8,128)S(1)}, f32[16,2048]{1,0:T(8,128)S(1)}, u32[]{:S(2)}, u32[]{:S(2)}) collective-permute-start(f32[16,2048]{1,0:T(8,128)S(1)} %select_bitcast_fusion.1), channel_id=1, source_target_pairs={{0,1},{1,0},{2,3},{3,2},{4,5},{5,4},{6,7},{7,6},{8,9},{9,8},{10,11... | collective-permute-start | bytes 393224 | tf_op jit(solution)/shard_map/ppermute | solution.py:114
  49.8 5.6 %collective-permute-start.13 = (f32[16,2048]{1,0:T(8,128)S(1)}, f32[16,2048]{1,0:T(8,128)S(1)}, u32[]{:S(2)}, u32[]{:S(2)}) collective-permute-start(f32[16,2048]{1,0:T(8,128)S(1)} %bitcast_add_fusion.1), channel_id=1, source_target_pairs={{0,2},{2,0},{1,3},{3,1},{4,6},{6,4},{5,7},{7,5},{8,10},{10,8},{9,1... | collective-permute-start | bytes 393224 | tf_op jit(solution)/shard_map/ppermute | solution.py:146
  55.6 3.6 %collective-permute-start.17 = (f32[16]{0:T(128)S(1)}, f32[16]{0:T(128)S(1)}, u32[]{:S(2)}, u32[]{:S(2)}) collective-permute-start(f32[16]{0:T(128)S(1)} %get-tuple-element.65), channel_id=1, source_target_pairs={{0,12},{4,0},{8,4},{12,8},{1,13},{5,1},{9,5},{13,9},{2,14},{6,2},{... | collective-permute-start | bytes 200 | tf_op jit(solution)/shard_map/ppermute | solution.py:146
  56.4 4.4 %collective-permute-start.16 = (f32[16]{0:T(128)S(1)}, f32[16]{0:T(128)S(1)}, u32[]{:S(2)}, u32[]{:S(2)}) collective-permute-start(f32[16]{0:T(128)S(1)} %get-tuple-element.65), channel_id=1, source_target_pairs={{0,8},{4,12},{8,0},{12,4},{1,9},{5,13},{9,1},{13,5},{2,10},{6,14},... | collective-permute-start | bytes 200 | tf_op jit(solution)/shard_map/ppermute | solution.py:146
  56.8 5.3 %collective-permute-start.15 = (f32[16]{0:T(128)S(1)}, f32[16]{0:T(128)S(1)}, u32[]{:S(2)}, u32[]{:S(2)}) collective-permute-start(f32[16]{0:T(128)S(1)} %get-tuple-element.65), channel_id=1, source_target_pairs={{0,4},{4,8},{8,12},{12,0},{1,5},{5,9},{9,13},{13,1},{2,6},{6,10},{... | collective-permute-start | bytes 200 | tf_op jit(solution)/shard_map/ppermute | solution.py:146
  62.2 1.1 %collective-permute-start.18 = (f32[16]{0:T(128)S(1)}, f32[16]{0:T(128)S(1)}, u32[]{:S(2)}, u32[]{:S(2)}) collective-permute-start(f32[16]{0:T(128)S(1)} %add_add_fusion.1), channel_id=1, source_target_pairs={{0,1},{1,0},{2,3},{3,2},{4,5},{5,4},{6,7},{7,6},{8,9},{9,8},{10,11... | collective-permute-start | bytes 200 | tf_op jit(solution)/shard_map/ppermute | solution.py:136
  62.2 1.5 %collective-permute-start.14 = (f32[16,2048]{1,0:T(8,128)S(1)}, f32[16,2048]{1,0:T(8,128)S(1)}, u32[]{:S(2)}, u32[]{:S(2)}) collective-permute-start(f32[16,2048]{1,0:T(8,128)S(1)} %get-tuple-element.66), channel_id=1, source_target_pairs={{0,1},{1,0},{2,3},{3,2},{4,5},{5,4},{6,7},{7,6},{8,9},{9,8},{10,11... | collective-permute-start | bytes 393224 | tf_op jit(solution)/shard_map/ppermute | solution.py:134
  66.5 30.2 %slice-start = ((s8[14680064]{0:T(1024)(128)(4,1)}), s8[4194304]{0:T(1024)(128)(4,1)S(1)}, s32[]{:S(2)}) async-start(s8[14680064]{0:T(1024)(128)(4,1)} %bitcast.85), calls=%async_computation | async-start | bytes 8388608
  69.4 27.3 %slice-start.1 = ((s8[14680064]{0:T(1024)(128)(4,1)}), s8[4194304]{0:T(1024)(128)(4,1)S(1)}, s32[]{:S(2)}) async-start(s8[14680064]{0:T(1024)(128)(4,1)} %bitcast.85), calls=%async_computation.1 | async-start | bytes 8388608
  75.0 21.7 %slice-start.2 = ((s8[14680064]{0:T(1024)(128)(4,1)}), s8[4194304]{0:T(1024)(128)(4,1)S(1)}, s32[]{:S(2)}) async-start(s8[14680064]{0:T(1024)(128)(4,1)} %bitcast.85), calls=%async_computation.2 | async-start | bytes 8388608
  80.7 9.3 %collective-permute-start.19 = (bf16[32,1792]{1,0:T(8,128)(2,1)S(1)}, bf16[32,1792]{1,0:T(8,128)(2,1)S(1)}, u32[]{:S(2)}, u32[]{:S(2)}) collective-permute-start(bf16[32,1792]{1,0:T(8,128)(2,1)S(1)} %get-tuple-element.18), channel_id=1, source_target_pairs={{0,4},{4,8},{8,12},{12,0},{1,5},{5,9},{9,13},{13,1},{2,6},{6,10},{... | collective-permute-start | bytes 344072 | tf_op jit(solution)/shard_map/ppermute | solution.py:169
  80.9 11.8 %collective-permute-start.20 = (bf16[32,1792]{1,0:T(8,128)(2,1)S(1)}, bf16[32,1792]{1,0:T(8,128)(2,1)S(1)}, u32[]{:S(2)}, u32[]{:S(2)}) collective-permute-start(bf16[32,1792]{1,0:T(8,128)(2,1)S(1)} %get-tuple-element.19), channel_id=1, source_target_pairs={{0,8},{4,12},{8,0},{12,4},{1,9},{5,13},{9,1},{13,5},{2,10},{6,14},... | collective-permute-start | bytes 344072 | tf_op jit(solution)/shard_map/ppermute | solution.py:169
  82.7 10.0 %collective-permute-start.21 = (bf16[32,1792]{1,0:T(8,128)(2,1)S(1)}, bf16[32,1792]{1,0:T(8,128)(2,1)S(1)}, u32[]{:S(2)}, u32[]{:S(2)}) collective-permute-start(bf16[32,1792]{1,0:T(8,128)(2,1)S(1)} %pad_maximum_fusion.3), channel_id=1, source_target_pairs={{0,12},{4,0},{8,4},{12,8},{1,13},{5,1},{9,5},{13,9},{2,14},{6,2},{... | collective-permute-start | bytes 344072 | tf_op jit(solution)/shard_map/ppermute | solution.py:169
  92.8 9.4 %collective-permute-start.24 = (bf16[32,896]{1,0:T(8,128)(2,1)S(1)}, bf16[32,896]{1,0:T(8,128)(2,1)S(1)}, u32[]{:S(2)}, u32[]{:S(2)}) collective-permute-start(bf16[32,896]{1,0:T(8,128)(2,1)S(1)} %fusion.94), channel_id=1, source_target_pairs={{0,12},{4,0},{8,4},{12,8},{1,13},{5,1},{9,5},{13,9},{2,14},{6,2},{... | collective-permute-start | bytes 172040 | tf_op jit(solution)/shard_map/ppermute | solution.py:182
  95.5 6.0 %collective-permute-start.23 = (bf16[32,896]{1,0:T(8,128)(2,1)S(1)}, bf16[32,896]{1,0:T(8,128)(2,1)S(1)}, u32[]{:S(2)}, u32[]{:S(2)}) collective-permute-start(bf16[32,896]{1,0:T(8,128)(2,1)S(1)} %fusion.94), channel_id=1, source_target_pairs={{0,8},{4,12},{8,0},{12,4},{1,9},{5,13},{9,1},{13,5},{2,10},{6,14},... | collective-permute-start | bytes 172040 | tf_op jit(solution)/shard_map/ppermute | solution.py:182
  96.7 6.3 %collective-permute-start.22 = (bf16[32,896]{1,0:T(8,128)(2,1)S(1)}, bf16[32,896]{1,0:T(8,128)(2,1)S(1)}, u32[]{:S(2)}, u32[]{:S(2)}) collective-permute-start(bf16[32,896]{1,0:T(8,128)(2,1)S(1)} %fusion.94), channel_id=1, source_target_pairs={{0,4},{4,8},{8,12},{12,0},{1,5},{5,9},{9,13},{13,1},{2,6},{6,10},{... | collective-permute-start | bytes 172040 | tf_op jit(solution)/shard_map/ppermute | solution.py:182
  103.9 1.4 %collective-permute-start.25 = (f32[2,8,2048]{2,1,0:T(8,128)S(1)}, f32[2,8,2048]{2,1,0:T(8,128)S(1)}, u32[]{:S(2)}, u32[]{:S(2)}) collective-permute-start(f32[2,8,2048]{2,1,0:T(8,128)S(1)} %select_bitcast_fusion), channel_id=1, source_target_pairs={{0,1},{1,0},{2,3},{3,2},{4,5},{5,4},{6,7},{7,6},{8,9},{9,8},{10,11... | collective-permute-start | bytes 393224 | tf_op jit(solution)/shard_map/ppermute | solution.py:114
  105.3 4.3 %collective-permute-start.26 = (f32[8,2048]{1,0:T(8,128)S(1)}, f32[8,2048]{1,0:T(8,128)S(1)}, u32[]{:S(2)}, u32[]{:S(2)}) collective-permute-start(f32[8,2048]{1,0:T(8,128)S(1)} %select_bitcast_fusion.7), channel_id=1, source_target_pairs={{0,2},{2,0},{1,3},{3,1},{4,6},{6,4},{5,7},{7,5},{8,10},{10,8},{9,1... | collective-permute-start | bytes 196616 | tf_op jit(solution)/shard_map/ppermute | solution.py:114
  (2 other events, 36.2 us)

commit v16 on v14

--- a/solution.py
+++ b/solution.py
@@ -208,10 +208,20 @@
 
     residual = tokens.astype(jnp.float32)
     squares = all_sum(jnp.sum(residual * residual, axis=1), "pool", n_pool)
-    normed = (residual * lax.rsqrt(squares / D + epsilon)[:, None] * attn_gain[None, :]).astype(
-        jnp.bfloat16
-    )
-    by_slot = gather_rows(normed, CS, n_cs, row_of_slot)
+    tokens_by_slot = gather_rows(tokens, CS, n_cs, row_of_slot)
+    cs_index = lax.axis_index(CS)
+    squares_got = jnp.concatenate(
+        [squares] + [lax.ppermute(squares, CS, shift_pairs(n_cs, k)) for k in range(1, n_cs)]
+    )
+    squares_by_slot = jnp.take(
+        squares_got,
+        ((cs_index - row_of_slot // rows_here) % n_cs) * rows_here + row_of_slot % rows_here,
+    )[:, None]
+    by_slot = (
+        tokens_by_slot.astype(jnp.float32)
+        * lax.rsqrt(squares_by_slot / D + epsilon)
+        * attn_gain[None, :]
+    ).astype(jnp.bfloat16)
     qkv_part = jnp.einsum(
         "rf,fgc->rgc", by_slot, w_qkv, preferred_element_type=jnp.float32
     ).reshape(rows_total, -1)
@@ -221,7 +231,6 @@
     attended = attend(rotated, kv_cache, positions, per_group, HD)
     by_row = gather_rows(attended, "pool", n_pool, slot_of_row)
     out_part = jnp.dot(by_row, w_out, preferred_element_type=jnp.float32)
-    cs_index = lax.axis_index(CS)
     out_part = lax.dynamic_update_slice_in_dim(
         out_part,
         lax.dynamic_slice_in_dim(out_part, cs_index * rows_here, rows_here, 0) + residual,

time: 109 us -> 110 us (level)
  starting transfers between devices: 26.9 us -> 29.6 us
  waiting for transfers between devices: 36.5 us -> 35.1 us
    ppermute x6, waiting for transfers between devices: 8.12 us -> 5.04 us  [gather_rows(): got = [x] + [lax.ppermute(x, axis, shift_pairs(n, k)) for k in range(1, n)]]
    ppermute x0 -> x3, waiting for transfers between devices: none -> 2.97 us  [local(): lax.ppermute(squares, CS, shift_pairs(n_cs, k))]
    ppermute x0 -> x3, starting transfers between devices: none -> 2.34 us  [local(): lax.ppermute(squares, CS, shift_pairs(n_cs, k))]
    ppermute x7, waiting for transfers between devices: 10.4 us -> 8.53 us  [all_sum(): total = total + lax.ppermute(x, axis, shift_pairs(n, k))]
  transfers between devices with their start and end apart: 26 -> 29, of which waited for: 19 -> 20; matrix products, arithmetic and copies ran while one was open for 9% -> 10% of each run, Pallas kernels for 0% -> 0%
where the time goes in v16:
time: 110 us
  matrix products  38 us (35%)
  waiting for transfers between devices  35.1 us (32%)
  starting transfers between devices  29.6 us (27%)
  other arithmetic  4.81 us (4%)
  local copies, waits for them, and re-layouts  1.4 us (1%)
    dot_general x8, matrix products, block(): jnp.dot(x, lax.dynamic_slice_in_dim(w, j * chunk, chunk, 1), preferred_el...  22.1 us
    ppermute x6, waiting for transfers between devices, scatter_sum(): lax.ppermute(piece, axis, shift_pairs(n, k)).astype(jnp.float32)  12 us
    ppermute x7, starting transfers between devices, all_sum(): total = total + lax.ppermute(x, axis, shift_pairs(n, k))  10.2 us
    ppermute x7, waiting for transfers between devices, all_sum(): total = total + lax.ppermute(x, axis, shift_pairs(n, k))  8.53 us
    dot_general x1, matrix products, local(): jnp.einsum('rf,fgc->rgc', by_slot, w_qkv, preferred_element_type=jnp.floa...  6.89 us
    ppermute x6, starting transfers between devices, scatter_sum(): lax.ppermute(piece, axis, shift_pairs(n, k)).astype(jnp.float32)  5.16 us
    dot_general x1, matrix products, local(): out_part = jnp.dot(by_row, w_out, preferred_element_type=jnp.float32)  5.09 us
    ppermute x6, waiting for transfers between devices, gather_rows(): got = [x] + [lax.ppermute(x, axis, shift_pairs(n, k)) for k in range(1, n)]  5.04 us
  transfers between devices with their start and end apart: 29, of which 20 were waited for; matrix products, arithmetic and copies ran while one was open for 10% of the time, Pallas kernels for 0%

profile of v16, /device:TPU:0, one launch (start us, length us, event | category | flops | bytes accessed | tf_op | source)
XLA Modules:
  0.0 109.6 jit_solution(11968475633461790644)
XLA Ops:
  1.0 5.1 %collective-permute-start.5 = (f32[8]{0:T(128)S(1)}, f32[8]{0:T(128)S(1)}, u32[]{:S(2)}, u32[]{:S(2)}) collective-permute-start(f32[8]{0:T(128)S(1)} %fusion.104), channel_id=1, source_target_pairs={{0,12},{4,0},{8,4},{12,8},{1,13},{5,1},{9,5},{13,9},{2,14},{6,2},{... | collective-permute-start | bytes 104 | tf_op jit(solution)/shard_map/ppermute | solution.py:140
  7.2 1.4 %collective-permute-start.1 = (bf16[8,2048]{1,0:T(8,128)(2,1)}, bf16[8,2048]{1,0:T(8,128)(2,1)S(1)}, u32[]{:S(2)}, u32[]{:S(2)}) collective-permute-start(bf16[8,2048]{1,0:T(8,128)(2,1)} %param.20), channel_id=1, source_target_pairs={{0,2},{1,3},{2,0},{3,1},{4,6},{5,7},{6,4},{7,5},{8,10},{9,11},{10,... | collective-permute-start | bytes 98312 | tf_op jit(solution)/shard_map/ppermute | solution.py:97
  14.5 1.6 %collective-permute-done.7 = f32[8]{0:T(128)S(1)} collective-permute-done((f32[8]{0:T(128)S(1)}, f32[8]{0:T(128)S(1)}, u32[]{:S(2)}, u32[]{:S(2)}) %collective-permute-start.7) | collective-permute-done | bytes 64 | tf_op jit(solution)/shard_map/ppermute | solution.py:214
  17.6 6.9 %fusion.26 = f32[2,4,8,1280]{3,2,1,0:T(8,128)S(1)} fusion(bf16[2048,2,1280]{2,1,0:T(2,128)(2,1)} %param.22, bf16[8,2048]{1,0:T(8,128)(2,1)S(1)} %collective-permute-done.2, bf16[8,2048]{1,0:T(8,128)(2,1)S(1)} %collective-permute-done.1, bf16[8,2048]{1,0:T(8,128)(2,1)S(1)} %collective-permute-done, bf16[8,2048]{1,0:T(8,128)(2,1)} %param.20, ...), kind=kOutput, calls=%fused_computation.27 | convolution fusion | flops 340591616 | bytes 10952960 | tf_op jit(solution)/shard_map/rf,fgc->rgc/dot_general | solution.py:225
  24.6 2.5 %collective-permute-start.9 = (f32[8,2560]{1,0:T(8,128)S(1)}, f32[8,2560]{1,0:T(8,128)S(1)}, u32[]{:S(2)}, u32[]{:S(2)}) collective-permute-start(f32[8,2560]{1,0:T(8,128)S(1)} %get-tuple-element.67), channel_id=1, source_target_pairs={{0,4},{4,8},{8,12},{12,0},{1,5},{5,9},{9,13},{13,1},{2,6},{6,10},{... | collective-permute-start | bytes 245768 | tf_op jit(solution)/shard_map/ppermute | solution.py:114
  27.1 1.3 %collective-permute-start.11 = (f32[8,2560]{1,0:T(8,128)S(1)}, f32[8,2560]{1,0:T(8,128)S(1)}, u32[]{:S(2)}, u32[]{:S(2)}) collective-permute-start(f32[8,2560]{1,0:T(8,128)S(1)} %get-tuple-element.68), channel_id=1, source_target_pairs={{0,12},{4,0},{8,4},{12,8},{1,13},{5,1},{9,5},{13,9},{2,14},{6,2},{... | collective-permute-start | bytes 245768 | tf_op jit(solution)/shard_map/ppermute | solution.py:114
  29.3 2.3 %collective-permute-done.9 = f32[8,2560]{1,0:T(8,128)S(1)} collective-permute-done((f32[8,2560]{1,0:T(8,128)S(1)}, f32[8,2560]{1,0:T(8,128)S(1)}, u32[]{:S(2)}, u32[]{:S(2)}) %collective-permute-start.9) | collective-permute-done | bytes 81952 | tf_op jit(solution)/shard_map/ppermute | solution.py:114
  32.1 3.2 %collective-permute-done.10 = f32[8,2560]{1,0:T(8,128)S(1)} collective-permute-done((f32[8,2560]{1,0:T(8,128)S(1)}, f32[8,2560]{1,0:T(8,128)S(1)}, u32[]{:S(2)}, u32[]{:S(2)}) %collective-permute-start.10) | collective-permute-done | bytes 81952 | tf_op jit(solution)/shard_map/ppermute | solution.py:114
  36.7 2.0 %collective-permute-start.14 = (bf16[8,2048]{1,0:T(8,128)(2,1)S(1)}, bf16[8,2048]{1,0:T(8,128)(2,1)S(1)}, u32[]{:S(2)}, u32[]{:S(2)}) collective-permute-start(bf16[8,2048]{1,0:T(8,128)(2,1)S(1)} %bitcast.117), channel_id=1, source_target_pairs={{0,12},{4,0},{8,4},{12,8},{1,13},{5,1},{9,5},{13,9},{2,14},{6,2},{... | collective-permute-start | bytes 98312 | tf_op jit(solution)/shard_map/ppermute | solution.py:97
  39.4 1.3 %collective-permute-done.14 = bf16[8,2048]{1,0:T(8,128)(2,1)S(1)} collective-permute-done((bf16[8,2048]{1,0:T(8,128)(2,1)S(1)}, bf16[8,2048]{1,0:T(8,128)(2,1)S(1)}, u32[]{:S(2)}, u32[]{:S(2)}) %collective-permute-start.14) | collective-permute-done | bytes 32800 | tf_op jit(solution)/shard_map/ppermute | solution.py:97
  40.7 2.8 %collective-permute-done.13 = bf16[8,2048]{1,0:T(8,128)(2,1)S(1)} collective-permute-done((bf16[8,2048]{1,0:T(8,128)(2,1)S(1)}, bf16[8,2048]{1,0:T(8,128)(2,1)S(1)}, u32[]{:S(2)}, u32[]{:S(2)}) %collective-permute-start.13) | collective-permute-done | bytes 32800 | tf_op jit(solution)/shard_map/ppermute | solution.py:97
  44.4 5.1 %fusion.43 = f32[32,2048]{1,0:T(8,128)S(1)} fusion(bf16[2048,2048]{1,0:T(8,128)(2,1)} %param.23, bf16[8,2048]{1,0:T(8,128)(2,1)S(1)} %collective-permute-done.14, bf16[8,2048]{1,0:T(8,128)(2,1)S(1)} %collective-permute-done.13, bf16[8,2048]{1,0:T(8,128)(2,1)S(1)} %collective-permute-done.12, bf16[8,2048]{1,0:T(8,128)(2,1)S(1)} %bitcast.120, s32[32]{0:T(128)S(1)} %fusion.134), kind=kOutput, calls=%fused_computation.38 | convolution fusion | flops 273220608 | bytes 8781952 | tf_op jit(solution)/shard_map/dot_general | solution.py:233
  49.6 1.3 %collective-permute-done.15 = f32[16,2048]{1,0:T(8,128)S(1)} collective-permute-done((f32[16,2048]{1,0:T(8,128)S(1)}, f32[16,2048]{1,0:T(8,128)S(1)}, u32[]{:S(2)}, u32[]{:S(2)}) %collective-permute-start.15) | collective-permute-done | bytes 131104 | tf_op jit(solution)/shard_map/ppermute | solution.py:114
  52.0 4.6 %collective-permute-done.16 = f32[16,2048]{1,0:T(8,128)S(1)} collective-permute-done((f32[16,2048]{1,0:T(8,128)S(1)}, f32[16,2048]{1,0:T(8,128)S(1)}, u32[]{:S(2)}, u32[]{:S(2)}) %collective-permute-start.16) | collective-permute-done | bytes 131104 | tf_op jit(solution)/shard_map/ppermute | solution.py:140
  59.4 2.0 %collective-permute-start.18 = (f32[32]{0:T(128)S(1)}, f32[32]{0:T(128)S(1)}, u32[]{:S(2)}, u32[]{:S(2)}) collective-permute-start(f32[32]{0:T(128)S(1)} %reduce_sum.65), channel_id=1, source_target_pairs={{0,4},{4,8},{8,12},{12,0},{1,5},{5,9},{9,13},{13,1},{2,6},{6,10},{... | collective-permute-start | bytes 392 | tf_op jit(solution)/shard_map/ppermute | solution.py:140
  61.8 1.6 %collective-permute-done.19 = f32[32]{0:T(128)S(1)} collective-permute-done((f32[32]{0:T(128)S(1)}, f32[32]{0:T(128)S(1)}, u32[]{:S(2)}, u32[]{:S(2)}) %collective-permute-start.19) | collective-permute-done | bytes 160 | tf_op jit(solution)/shard_map/ppermute | solution.py:140
  63.4 1.4 %collective-permute-done.18 = f32[32]{0:T(128)S(1)} collective-permute-done((f32[32]{0:T(128)S(1)}, f32[32]{0:T(128)S(1)}, u32[]{:S(2)}, u32[]{:S(2)}) %collective-permute-start.18) | collective-permute-done | bytes 160 | tf_op jit(solution)/shard_map/ppermute | solution.py:140
  64.9 2.7 %fusion.59 = bf16[32,896]{1,0:T(8,128)(2,1)S(1)} fusion(bf16[32,2048]{1,0:T(8,128)(2,1)S(1)} %multiply_convert_fusion, bf16[2048,3584]{1,0:T(8,128)(2,1)} %param.26, s32[]{:T(128)S(6)} %select_n.294), kind=kOutput, calls=%fused_computation.45 | convolution fusion | flops 117469184 | bytes 3858436 | tf_op jit(solution)/shard_map/dot_general | solution.py:150
  67.6 2.9 %fusion.56 = bf16[32,896]{1,0:T(8,128)(2,1)S(1)} fusion(bf16[32,2048]{1,0:T(8,128)(2,1)S(1)} %multiply_convert_fusion, bf16[2048,3584]{1,0:T(8,128)(2,1)} %param.25, s32[]{:T(128)S(6)} %select_n.294), kind=kOutput, calls=%fused_computation.44 | convolution fusion | flops 117469184 | bytes 3858436 | tf_op jit(solution)/shard_map/dot_general | solution.py:150
  70.5 2.9 %fusion.53 = bf16[32,896]{1,0:T(8,128)(2,1)S(1)} fusion(bf16[32,2048]{1,0:T(8,128)(2,1)S(1)} %multiply_convert_fusion, bf16[2048,3584]{1,0:T(8,128)(2,1)} %param.26, s32[]{:T(128)S(6)} %select_n.293), kind=kOutput, calls=%fused_computation.43 | convolution fusion | flops 117469184 | bytes 3858436 | tf_op jit(solution)/shard_map/dot_general | solution.py:150
  73.4 2.7 %fusion.50 = bf16[32,896]{1,0:T(8,128)(2,1)S(1)} fusion(bf16[32,2048]{1,0:T(8,128)(2,1)S(1)} %multiply_convert_fusion, bf16[2048,3584]{1,0:T(8,128)(2,1)} %param.25, s32[]{:T(128)S(6)} %select_n.293), kind=kOutput, calls=%fused_computation.42 | convolution fusion | flops 117469184 | bytes 3858436 | tf_op jit(solution)/shard_map/dot_general | solution.py:150
  76.1 2.9 %fusion.47 = bf16[32,896]{1,0:T(8,128)(2,1)S(1)} fusion(bf16[32,2048]{1,0:T(8,128)(2,1)S(1)} %multiply_convert_fusion, bf16[2048,3584]{1,0:T(8,128)(2,1)} %param.26, s32[]{:T(128)S(6)} %select_n.292), kind=kOutput, calls=%fused_computation.41 | convolution fusion | flops 117469184 | bytes 3858436 | tf_op jit(solution)/shard_map/dot_general | solution.py:150
  79.0 2.7 %fusion.44 = bf16[32,896]{1,0:T(8,128)(2,1)S(1)} fusion(bf16[32,2048]{1,0:T(8,128)(2,1)S(1)} %multiply_convert_fusion, bf16[2048,3584]{1,0:T(8,128)(2,1)} %param.25, s32[]{:T(128)S(6)} %select_n.292), kind=kOutput, calls=%fused_computation.40 | convolution fusion | flops 117469184 | bytes 3858436 | tf_op jit(solution)/shard_map/dot_general | solution.py:150
  82.0 1.8 %collective-permute-start.22 = (bf16[32,1792]{1,0:T(8,128)(2,1)S(1)}, bf16[32,1792]{1,0:T(8,128)(2,1)S(1)}, u32[]{:S(2)}, u32[]{:S(2)}) collective-permute-start(bf16[32,1792]{1,0:T(8,128)(2,1)S(1)} %get-tuple-element.19), channel_id=1, source_target_pairs={{0,8},{4,12},{8,0},{12,4},{1,9},{5,13},{9,1},{13,5},{2,10},{6,14},... | collective-permute-start | bytes 344072 | tf_op jit(solution)/shard_map/ppermute | solution.py:163
  83.8 1.8 %collective-permute-start.23 = (bf16[32,1792]{1,0:T(8,128)(2,1)S(1)}, bf16[32,1792]{1,0:T(8,128)(2,1)S(1)}, u32[]{:S(2)}, u32[]{:S(2)}) collective-permute-start(bf16[32,1792]{1,0:T(8,128)(2,1)S(1)} %pad_maximum_fusion.3), channel_id=1, source_target_pairs={{0,12},{4,0},{8,4},{12,8},{1,13},{5,1},{9,5},{13,9},{2,14},{6,2},{... | collective-permute-start | bytes 344072 | tf_op jit(solution)/shard_map/ppermute | solution.py:163
  85.6 2.7 %fusion.65 = bf16[32,896]{1,0:T(8,128)(2,1)S(1)} fusion(bf16[32,2048]{1,0:T(8,128)(2,1)S(1)} %multiply_convert_fusion, bf16[2048,3584]{1,0:T(8,128)(2,1)} %param.26, s32[]{:T(128)S(6)} %select_n.295), kind=kOutput, calls=%fused_computation.47 | convolution fusion | flops 117469184 | bytes 3858436 | tf_op jit(solution)/shard_map/dot_general | solution.py:150
  88.3 2.7 %fusion.62 = bf16[32,896]{1,0:T(8,128)(2,1)S(1)} fusion(bf16[32,2048]{1,0:T(8,128)(2,1)S(1)} %multiply_convert_fusion, bf16[2048,3584]{1,0:T(8,128)(2,1)} %param.25, s32[]{:T(128)S(6)} %select_n.295), kind=kOutput, calls=%fused_computation.46 | convolution fusion | flops 117469184 | bytes 3858436 | tf_op jit(solution)/shard_map/dot_general | solution.py:150
  91.1 1.4 %collective-permute-done.22 = bf16[32,1792]{1,0:T(8,128)(2,1)S(1)} collective-permute-done((bf16[32,1792]{1,0:T(8,128)(2,1)S(1)}, bf16[32,1792]{1,0:T(8,128)(2,1)S(1)}, u32[]{:S(2)}, u32[]{:S(2)}) %collective-permute-start.22) | collective-permute-done | bytes 114720 | tf_op jit(solution)/shard_map/ppermute | solution.py:163
  92.6 2.6 %collective-permute-start.26 = (bf16[32,896]{1,0:T(8,128)(2,1)S(1)}, bf16[32,896]{1,0:T(8,128)(2,1)S(1)}, u32[]{:S(2)}, u32[]{:S(2)}) collective-permute-start(bf16[32,896]{1,0:T(8,128)(2,1)S(1)} %fusion.100), channel_id=1, source_target_pairs={{0,12},{4,0},{8,4},{12,8},{1,13},{5,1},{9,5},{13,9},{2,14},{6,2},{... | collective-permute-start | bytes 172040 | tf_op jit(solution)/shard_map/ppermute | solution.py:176
  96.9 3.9 %collective-permute-done.25 = bf16[32,896]{1,0:T(8,128)(2,1)S(1)} collective-permute-done((bf16[32,896]{1,0:T(8,128)(2,1)S(1)}, bf16[32,896]{1,0:T(8,128)(2,1)S(1)}, u32[]{:S(2)}, u32[]{:S(2)}) %collective-permute-start.25) | collective-permute-done | bytes 57376 | tf_op jit(solution)/shard_map/ppermute | solution.py:176
  103.2 1.3 %collective-permute-done.27 = f32[2,8,2048]{2,1,0:T(8,128)S(1)} collective-permute-done((f32[2,8,2048]{2,1,0:T(8,128)S(1)}, f32[2,8,2048]{2,1,0:T(8,128)S(1)}, u32[]{:S(2)}, u32[]{:S(2)}) %collective-permute-start.27) | collective-permute-done | bytes 131104 | tf_op jit(solution)/shard_map/ppermute | solution.py:114
  105.6 3.4 %collective-permute-done.28 = f32[8,2048]{1,0:T(8,128)S(1)} collective-permute-done((f32[8,2048]{1,0:T(8,128)S(1)}, f32[8,2048]{1,0:T(8,128)S(1)}, u32[]{:S(2)}, u32[]{:S(2)}) %collective-permute-start.28) | collective-permute-done | bytes 65568 | tf_op jit(solution)/shard_map/ppermute | solution.py:114
  (107 shorter events, 24.2 us)
Async XLA Ops:
  0.0 28.7 %copy-start = (bf16[8,256,2,2,128]{4,3,2,1,0:T(2,128)(2,1)S(1)}, bf16[8,256,2,2,128]{4,3,2,1,0:T(2,128)(2,1)}, u32[]{:S(2)}) copy-start(bf16[8,256,2,2,128]{4,3,2,1,0:T(2,128)(2,1)} %param.28) | copy-start | bytes 6291460
  1.0 9.6 %collective-permute-start.5 = (f32[8]{0:T(128)S(1)}, f32[8]{0:T(128)S(1)}, u32[]{:S(2)}, u32[]{:S(2)}) collective-permute-start(f32[8]{0:T(128)S(1)} %fusion.104), channel_id=1, source_target_pairs={{0,12},{4,0},{8,4},{12,8},{1,13},{5,1},{9,5},{13,9},{2,14},{6,2},{... | collective-permute-start | bytes 104 | tf_op jit(solution)/shard_map/ppermute | solution.py:140
  6.1 4.8 %collective-permute-start.4 = (f32[8]{0:T(128)S(1)}, f32[8]{0:T(128)S(1)}, u32[]{:S(2)}, u32[]{:S(2)}) collective-permute-start(f32[8]{0:T(128)S(1)} %fusion.104), channel_id=1, source_target_pairs={{0,8},{4,12},{8,0},{12,4},{1,9},{5,13},{9,1},{13,5},{2,10},{6,14},... | collective-permute-start | bytes 104 | tf_op jit(solution)/shard_map/ppermute | solution.py:140
  6.1 5.3 %collective-permute-start.3 = (f32[8]{0:T(128)S(1)}, f32[8]{0:T(128)S(1)}, u32[]{:S(2)}, u32[]{:S(2)}) collective-permute-start(f32[8]{0:T(128)S(1)} %fusion.104), channel_id=1, source_target_pairs={{0,4},{4,8},{8,12},{12,0},{1,5},{5,9},{9,13},{13,1},{2,6},{6,10},{... | collective-permute-start | bytes 104 | tf_op jit(solution)/shard_map/ppermute | solution.py:140
  7.1 10.5 %collective-permute-start.2 = (bf16[8,2048]{1,0:T(8,128)(2,1)}, bf16[8,2048]{1,0:T(8,128)(2,1)S(1)}, u32[]{:S(2)}, u32[]{:S(2)}) collective-permute-start(bf16[8,2048]{1,0:T(8,128)(2,1)} %param.20), channel_id=1, source_target_pairs={{0,3},{1,0},{2,1},{3,2},{4,7},{5,4},{6,5},{7,6},{8,11},{9,8},{10,9... | collective-permute-start | bytes 98312 | tf_op jit(solution)/shard_map/ppermute | solution.py:97
  7.2 10.4 %collective-permute-start.1 = (bf16[8,2048]{1,0:T(8,128)(2,1)}, bf16[8,2048]{1,0:T(8,128)(2,1)S(1)}, u32[]{:S(2)}, u32[]{:S(2)}) collective-permute-start(bf16[8,2048]{1,0:T(8,128)(2,1)} %param.20), channel_id=1, source_target_pairs={{0,2},{1,3},{2,0},{3,1},{4,6},{5,7},{6,4},{7,5},{8,10},{9,11},{10,... | collective-permute-start | bytes 98312 | tf_op jit(solution)/shard_map/ppermute | solution.py:97
  10.7 7.0 %collective-permute-start = (bf16[8,2048]{1,0:T(8,128)(2,1)}, bf16[8,2048]{1,0:T(8,128)(2,1)S(1)}, u32[]{:S(2)}, u32[]{:S(2)}) collective-permute-start(bf16[8,2048]{1,0:T(8,128)(2,1)} %param.20), channel_id=1, source_target_pairs={{0,1},{1,2},{2,3},{3,0},{4,5},{5,6},{6,7},{7,4},{8,9},{9,10},{10,1... | collective-permute-start | bytes 98312 | tf_op jit(solution)/shard_map/ppermute | solution.py:97
  11.5 2.3 %collective-permute-start.8 = (f32[8]{0:T(128)S(1)}, f32[8]{0:T(128)S(1)}, u32[]{:S(2)}, u32[]{:S(2)}) collective-permute-start(f32[8]{0:T(128)S(1)} %add_add_fusion.1), channel_id=1, source_target_pairs={{0,3},{1,0},{2,1},{3,2},{4,7},{5,4},{6,5},{7,6},{8,11},{9,8},{10,9... | collective-permute-start | bytes 104 | tf_op jit(solution)/shard_map/ppermute | solution.py:214
  12.5 3.5 %collective-permute-start.7 = (f32[8]{0:T(128)S(1)}, f32[8]{0:T(128)S(1)}, u32[]{:S(2)}, u32[]{:S(2)}) collective-permute-start(f32[8]{0:T(128)S(1)} %add_add_fusion.1), channel_id=1, source_target_pairs={{0,2},{1,3},{2,0},{3,1},{4,6},{5,7},{6,4},{7,5},{8,10},{9,11},{10,... | collective-permute-start | bytes 104 | tf_op jit(solution)/shard_map/ppermute | solution.py:214
  13.8 3.0 %collective-permute-start.6 = (f32[8]{0:T(128)S(1)}, f32[8]{0:T(128)S(1)}, u32[]{:S(2)}, u32[]{:S(2)}) collective-permute-start(f32[8]{0:T(128)S(1)} %add_add_fusion.1), channel_id=1, source_target_pairs={{0,1},{1,2},{2,3},{3,0},{4,5},{5,6},{6,7},{7,4},{8,9},{9,10},{10,1... | collective-permute-start | bytes 104 | tf_op jit(solution)/shard_map/ppermute | solution.py:214
  24.6 6.9 %collective-permute-start.9 = (f32[8,2560]{1,0:T(8,128)S(1)}, f32[8,2560]{1,0:T(8,128)S(1)}, u32[]{:S(2)}, u32[]{:S(2)}) collective-permute-start(f32[8,2560]{1,0:T(8,128)S(1)} %get-tuple-element.67), channel_id=1, source_target_pairs={{0,4},{4,8},{8,12},{12,0},{1,5},{5,9},{9,13},{13,1},{2,6},{6,10},{... | collective-permute-start | bytes 245768 | tf_op jit(solution)/shard_map/ppermute | solution.py:114
  27.1 5.0 %collective-permute-start.11 = (f32[8,2560]{1,0:T(8,128)S(1)}, f32[8,2560]{1,0:T(8,128)S(1)}, u32[]{:S(2)}, u32[]{:S(2)}) collective-permute-start(f32[8,2560]{1,0:T(8,128)S(1)} %get-tuple-element.68), channel_id=1, source_target_pairs={{0,12},{4,0},{8,4},{12,8},{1,13},{5,1},{9,5},{13,9},{2,14},{6,2},{... | collective-permute-start | bytes 245768 | tf_op jit(solution)/shard_map/ppermute | solution.py:114
  28.5 6.8 %collective-permute-start.10 = (f32[8,2560]{1,0:T(8,128)S(1)}, f32[8,2560]{1,0:T(8,128)S(1)}, u32[]{:S(2)}, u32[]{:S(2)}) collective-permute-start(f32[8,2560]{1,0:T(8,128)S(1)} %get-tuple-element.69), channel_id=1, source_target_pairs={{0,8},{4,12},{8,0},{12,4},{1,9},{5,13},{9,1},{13,5},{2,10},{6,14},... | collective-permute-start | bytes 245768 | tf_op jit(solution)/shard_map/ppermute | solution.py:114
  29.2 35.5 %copy-start.2 = (f32[2048]{0:T(1024)S(1)}, f32[2048]{0:T(1024)}, u32[]{:S(2)}) copy-start(f32[2048]{0:T(1024)} %param.24) | copy-start | bytes 24580
  36.7 4.0 %collective-permute-start.14 = (bf16[8,2048]{1,0:T(8,128)(2,1)S(1)}, bf16[8,2048]{1,0:T(8,128)(2,1)S(1)}, u32[]{:S(2)}, u32[]{:S(2)}) collective-permute-start(bf16[8,2048]{1,0:T(8,128)(2,1)S(1)} %bitcast.117), channel_id=1, source_target_pairs={{0,12},{4,0},{8,4},{12,8},{1,13},{5,1},{9,5},{13,9},{2,14},{6,2},{... | collective-permute-start | bytes 98312 | tf_op jit(solution)/shard_map/ppermute | solution.py:97
  38.7 4.8 %collective-permute-start.13 = (bf16[8,2048]{1,0:T(8,128)(2,1)S(1)}, bf16[8,2048]{1,0:T(8,128)(2,1)S(1)}, u32[]{:S(2)}, u32[]{:S(2)}) collective-permute-start(bf16[8,2048]{1,0:T(8,128)(2,1)S(1)} %bitcast.118), channel_id=1, source_target_pairs={{0,8},{4,12},{8,0},{12,4},{1,9},{5,13},{9,1},{13,5},{2,10},{6,14},... | collective-permute-start | bytes 98312 | tf_op jit(solution)/shard_map/ppermute | solution.py:97
  38.7 5.7 %collective-permute-start.12 = (bf16[8,2048]{1,0:T(8,128)(2,1)S(1)}, bf16[8,2048]{1,0:T(8,128)(2,1)S(1)}, u32[]{:S(2)}, u32[]{:S(2)}) collective-permute-start(bf16[8,2048]{1,0:T(8,128)(2,1)S(1)} %bitcast.119), channel_id=1, source_target_pairs={{0,4},{4,8},{8,12},{12,0},{1,5},{5,9},{9,13},{13,1},{2,6},{6,10},{... | collective-permute-start | bytes 98312 | tf_op jit(solution)/shard_map/ppermute | solution.py:97
  49.6 1.4 %collective-permute-start.15 = (f32[16,2048]{1,0:T(8,128)S(1)}, f32[16,2048]{1,0:T(8,128)S(1)}, u32[]{:S(2)}, u32[]{:S(2)}) collective-permute-start(f32[16,2048]{1,0:T(8,128)S(1)} %select_bitcast_fusion.1), channel_id=1, source_target_pairs={{0,1},{1,0},{2,3},{3,2},{4,5},{5,4},{6,7},{7,6},{8,9},{9,8},{10,11... | collective-permute-start | bytes 393224 | tf_op jit(solution)/shard_map/ppermute | solution.py:114
  51.0 5.6 %collective-permute-start.16 = (f32[16,2048]{1,0:T(8,128)S(1)}, f32[16,2048]{1,0:T(8,128)S(1)}, u32[]{:S(2)}, u32[]{:S(2)}) collective-permute-start(f32[16,2048]{1,0:T(8,128)S(1)} %bitcast_add_fusion.1), channel_id=1, source_target_pairs={{0,2},{2,0},{1,3},{3,1},{4,6},{6,4},{5,7},{7,5},{8,10},{10,8},{9,1... | collective-permute-start | bytes 393224 | tf_op jit(solution)/shard_map/ppermute | solution.py:140
  56.6 1.4 %collective-permute-start.17 = (f32[16,2048]{1,0:T(8,128)S(1)}, f32[16,2048]{1,0:T(8,128)S(1)}, u32[]{:S(2)}, u32[]{:S(2)}) collective-permute-start(f32[16,2048]{1,0:T(8,128)S(1)} %add.382), channel_id=1, source_target_pairs={{0,1},{1,0},{2,3},{3,2},{4,5},{5,4},{6,7},{7,6},{8,9},{9,8},{10,11... | collective-permute-start | bytes 393224 | tf_op jit(solution)/shard_map/ppermute | solution.py:132
  58.3 3.5 %collective-permute-start.20 = (f32[32]{0:T(128)S(1)}, f32[32]{0:T(128)S(1)}, u32[]{:S(2)}, u32[]{:S(2)}) collective-permute-start(f32[32]{0:T(128)S(1)} %reduce_sum.65), channel_id=1, source_target_pairs={{0,12},{4,0},{8,4},{12,8},{1,13},{5,1},{9,5},{13,9},{2,14},{6,2},{... | collective-permute-start | bytes 392 | tf_op jit(solution)/shard_map/ppermute | solution.py:140
  58.9 4.4 %collective-permute-start.19 = (f32[32]{0:T(128)S(1)}, f32[32]{0:T(128)S(1)}, u32[]{:S(2)}, u32[]{:S(2)}) collective-permute-start(f32[32]{0:T(128)S(1)} %reduce_sum.65), channel_id=1, source_target_pairs={{0,8},{4,12},{8,0},{12,4},{1,9},{5,13},{9,1},{13,5},{2,10},{6,14},... | collective-permute-start | bytes 392 | tf_op jit(solution)/shard_map/ppermute | solution.py:140
  59.4 5.3 %collective-permute-start.18 = (f32[32]{0:T(128)S(1)}, f32[32]{0:T(128)S(1)}, u32[]{:S(2)}, u32[]{:S(2)}) collective-permute-start(f32[32]{0:T(128)S(1)} %reduce_sum.65), channel_id=1, source_target_pairs={{0,4},{4,8},{8,12},{12,0},{1,5},{5,9},{9,13},{13,1},{2,6},{6,10},{... | collective-permute-start | bytes 392 | tf_op jit(solution)/shard_map/ppermute | solution.py:140
  67.6 28.5 %slice-start = ((s8[14680064]{0:T(1024)(128)(4,1)}), s8[4194304]{0:T(1024)(128)(4,1)S(1)}, s32[]{:S(2)}) async-start(s8[14680064]{0:T(1024)(128)(4,1)} %bitcast.102), calls=%async_computation | async-start | bytes 8388608
  81.8 9.3 %collective-permute-start.21 = (bf16[32,1792]{1,0:T(8,128)(2,1)S(1)}, bf16[32,1792]{1,0:T(8,128)(2,1)S(1)}, u32[]{:S(2)}, u32[]{:S(2)}) collective-permute-start(bf16[32,1792]{1,0:T(8,128)(2,1)S(1)} %get-tuple-element.18), channel_id=1, source_target_pairs={{0,4},{4,8},{8,12},{12,0},{1,5},{5,9},{9,13},{13,1},{2,6},{6,10},{... | collective-permute-start | bytes 344072 | tf_op jit(solution)/shard_map/ppermute | solution.py:163
  82.0 10.5 %collective-permute-start.22 = (bf16[32,1792]{1,0:T(8,128)(2,1)S(1)}, bf16[32,1792]{1,0:T(8,128)(2,1)S(1)}, u32[]{:S(2)}, u32[]{:S(2)}) collective-permute-start(bf16[32,1792]{1,0:T(8,128)(2,1)S(1)} %get-tuple-element.19), channel_id=1, source_target_pairs={{0,8},{4,12},{8,0},{12,4},{1,9},{5,13},{9,1},{13,5},{2,10},{6,14},... | collective-permute-start | bytes 344072 | tf_op jit(solution)/shard_map/ppermute | solution.py:163
  83.8 8.7 %collective-permute-start.23 = (bf16[32,1792]{1,0:T(8,128)(2,1)S(1)}, bf16[32,1792]{1,0:T(8,128)(2,1)S(1)}, u32[]{:S(2)}, u32[]{:S(2)}) collective-permute-start(bf16[32,1792]{1,0:T(8,128)(2,1)S(1)} %pad_maximum_fusion.3), channel_id=1, source_target_pairs={{0,12},{4,0},{8,4},{12,8},{1,13},{5,1},{9,5},{13,9},{2,14},{6,2},{... | collective-permute-start | bytes 344072 | tf_op jit(solution)/shard_map/ppermute | solution.py:163
  92.6 8.9 %collective-permute-start.26 = (bf16[32,896]{1,0:T(8,128)(2,1)S(1)}, bf16[32,896]{1,0:T(8,128)(2,1)S(1)}, u32[]{:S(2)}, u32[]{:S(2)}) collective-permute-start(bf16[32,896]{1,0:T(8,128)(2,1)S(1)} %fusion.100), channel_id=1, source_target_pairs={{0,12},{4,0},{8,4},{12,8},{1,13},{5,1},{9,5},{13,9},{2,14},{6,2},{... | collective-permute-start | bytes 172040 | tf_op jit(solution)/shard_map/ppermute | solution.py:176
  95.2 5.6 %collective-permute-start.25 = (bf16[32,896]{1,0:T(8,128)(2,1)S(1)}, bf16[32,896]{1,0:T(8,128)(2,1)S(1)}, u32[]{:S(2)}, u32[]{:S(2)}) collective-permute-start(bf16[32,896]{1,0:T(8,128)(2,1)S(1)} %fusion.100), channel_id=1, source_target_pairs={{0,8},{4,12},{8,0},{12,4},{1,9},{5,13},{9,1},{13,5},{2,10},{6,14},... | collective-permute-start | bytes 172040 | tf_op jit(solution)/shard_map/ppermute | solution.py:176
  96.1 6.1 %collective-permute-start.24 = (bf16[32,896]{1,0:T(8,128)(2,1)S(1)}, bf16[32,896]{1,0:T(8,128)(2,1)S(1)}, u32[]{:S(2)}, u32[]{:S(2)}) collective-permute-start(bf16[32,896]{1,0:T(8,128)(2,1)S(1)} %fusion.100), channel_id=1, source_target_pairs={{0,4},{4,8},{8,12},{12,0},{1,5},{5,9},{9,13},{13,1},{2,6},{6,10},{... | collective-permute-start | bytes 172040 | tf_op jit(solution)/shard_map/ppermute | solution.py:176
  103.1 1.4 %collective-permute-start.27 = (f32[2,8,2048]{2,1,0:T(8,128)S(1)}, f32[2,8,2048]{2,1,0:T(8,128)S(1)}, u32[]{:S(2)}, u32[]{:S(2)}) collective-permute-start(f32[2,8,2048]{2,1,0:T(8,128)S(1)} %select_bitcast_fusion), channel_id=1, source_target_pairs={{0,1},{1,0},{2,3},{3,2},{4,5},{5,4},{6,7},{7,6},{8,9},{9,8},{10,11... | collective-permute-start | bytes 393224 | tf_op jit(solution)/shard_map/ppermute | solution.py:114
  104.6 4.3 %collective-permute-start.28 = (f32[8,2048]{1,0:T(8,128)S(1)}, f32[8,2048]{1,0:T(8,128)S(1)}, u32[]{:S(2)}, u32[]{:S(2)}) collective-permute-start(f32[8,2048]{1,0:T(8,128)S(1)} %select_bitcast_fusion.7), channel_id=1, source_target_pairs={{0,2},{2,0},{1,3},{3,1},{4,6},{6,4},{5,7},{7,5},{8,10},{10,8},{9,1... | collective-permute-start | bytes 196616 | tf_op jit(solution)/shard_map/ppermute | solution.py:114
  (4 other events, 80.9 us)

commit v17 on v14

--- a/solution.py
+++ b/solution.py
@@ -87,6 +87,10 @@
     return mixture.reshape(slot_count, -1).astype(jnp.bfloat16)
 
 
+def send_order(n):
+    return sorted(range(1, n), key=lambda k: -min(k, n - k))
+
+
 def shift_pairs(n, k):
     return [(i, (i + k) % n) for i in range(n)]
 
@@ -94,8 +98,8 @@
 def gather_rows(x, axis, n, want):
     idx = lax.axis_index(axis)
     per = x.shape[0]
-    got = [x] + [lax.ppermute(x, axis, shift_pairs(n, k)) for k in range(1, n)]
-    stacked = jnp.concatenate(got, axis=0)
+    sent = {k: lax.ppermute(x, axis, shift_pairs(n, k)) for k in send_order(n)}
+    stacked = jnp.concatenate([x] + [sent[k] for k in range(1, n)], axis=0)
     arrival = ((idx - want // per) % n) * per + want % per
     chooser = (arrival[:, None] == jnp.arange(n * per, dtype=arrival.dtype)[None, :]).astype(x.dtype)
     return jnp.dot(chooser, stacked, preferred_element_type=jnp.float32).astype(x.dtype)
@@ -109,7 +113,7 @@
 def scatter_sum(blocks, axis, n):
     idx = lax.axis_index(axis)
     total = jnp.take(blocks, idx, axis=0).astype(jnp.float32)
-    for k in range(1, n):
+    for k in send_order(n):
         piece = jnp.take(blocks, (idx + k) % n, axis=0)
         total = total + lax.ppermute(piece, axis, shift_pairs(n, k)).astype(jnp.float32)
     return total
@@ -156,11 +160,12 @@
         ]
         return jnp.concatenate(parts, axis=1)
 
-    pieces = [block((idx + k) % n) for k in range(1, n)]
+    order = send_order(n)
+    pieces = [block((idx + k) % n) for k in order]
     pieces, x = lax.optimization_barrier((pieces, x))
     total = None
-    for k in range(1, n):
-        got = lax.ppermute(pieces[k - 1], axis, shift_pairs(n, k)).astype(jnp.float32)
+    for k, piece in zip(order, pieces):
+        got = lax.ppermute(piece, axis, shift_pairs(n, k)).astype(jnp.float32)
         total = got if total is None else total + got
     own = block(idx).astype(jnp.float32)
     return own if total is None else own + total
@@ -172,7 +177,7 @@
     acc = jnp.dot(
         x, lax.dynamic_slice_in_dim(w, idx * chunk, chunk, 0), preferred_element_type=jnp.float32
     )
-    for k in range(1, n):
+    for k in send_order(n):
         got = lax.ppermute(x, axis, shift_pairs(n, k))
         rows = lax.dynamic_slice_in_dim(w, ((idx - k) % n) * chunk, chunk, 0)
         acc = acc + jnp.dot(got, rows, preferred_element_type=jnp.float32)

time: 109 us -> 107 us (0.982)
  waiting for transfers between devices: 36.5 us -> 34.5 us
    ppermute x9, starting transfers between devices: 8.12 us -> 9.52 us  [the longest x6 4.78 us: gather_rows(): sent = {k: lax.ppermute(x, axis, shift_pairs(n, k)) for k in send_order(n)}]
  transfers between devices with their start and end apart: 26 -> 26, of which waited for: 19 -> 19; matrix products, arithmetic and copies ran while one was open for 9% -> 10% of each run, Pallas kernels for 0% -> 0%
where the time goes in v17:
time: 107 us
  matrix products  38 us (36%)
  waiting for transfers between devices  34.5 us (32%)
  starting transfers between devices  27.4 us (26%)
  other arithmetic  5.54 us (5%)
    dot_general x8, matrix products, block(): jnp.dot(x, lax.dynamic_slice_in_dim(w, j * chunk, chunk, 1), preferred_el...  22.1 us
    ppermute x6, waiting for transfers between devices, scatter_sum(): lax.ppermute(piece, axis, shift_pairs(n, k)).astype(jnp.float32)  11.2 us
    ppermute x7, waiting for transfers between devices, all_sum(): total = total + lax.ppermute(x, axis, shift_pairs(n, k))  10.8 us
    ppermute x7, starting transfers between devices, all_sum(): total = total + lax.ppermute(x, axis, shift_pairs(n, k))  9.16 us
    ppermute x6, waiting for transfers between devices, gather_rows(): sent = {k: lax.ppermute(x, axis, shift_pairs(n, k)) for k in send_order(n)}  8.1 us
    dot_general x1, matrix products, local(): jnp.einsum('rf,fgc->rgc', by_slot, w_qkv, preferred_element_type=jnp.floa...  6.85 us
    dot_general x1, matrix products, local(): out_part = jnp.dot(by_row, w_out, preferred_element_type=jnp.float32)  5.09 us
    ppermute x6, starting transfers between devices, gather_rows(): sent = {k: lax.ppermute(x, axis, shift_pairs(n, k)) for k in send_order(n)}  4.78 us
  transfers between devices with their start and end apart: 26, of which 19 were waited for; matrix products, arithmetic and copies ran while one was open for 10% of the time, Pallas kernels for 0%

profile of v17, /device:TPU:0, one launch (start us, length us, event | category | flops | bytes accessed | tf_op | source)
XLA Modules:
  0.0 106.8 jit_solution(222659958540135154)
XLA Ops:
  1.0 5.1 %collective-permute-start.2 = (f32[8]{0:T(128)S(1)}, f32[8]{0:T(128)S(1)}, u32[]{:S(2)}, u32[]{:S(2)}) collective-permute-start(f32[8]{0:T(128)S(1)} %fusion.98), channel_id=1, source_target_pairs={{0,12},{4,0},{8,4},{12,8},{1,13},{5,1},{9,5},{13,9},{2,14},{6,2},{... | collective-permute-start | bytes 104 | tf_op jit(solution)/shard_map/ppermute | solution.py:144
  9.1 1.4 %collective-permute-done.1 = f32[8]{0:T(128)S(1)} collective-permute-done((f32[8]{0:T(128)S(1)}, f32[8]{0:T(128)S(1)}, u32[]{:S(2)}, u32[]{:S(2)}) %collective-permute-start.1) | collective-permute-done | bytes 64 | tf_op jit(solution)/shard_map/ppermute | solution.py:144
  12.4 1.6 %collective-permute-start.4 = (bf16[8,2048]{1,0:T(8,128)(2,1)S(1)}, bf16[8,2048]{1,0:T(8,128)(2,1)S(1)}, u32[]{:S(2)}, u32[]{:S(2)}) collective-permute-start(bf16[8,2048]{1,0:T(8,128)(2,1)S(1)} %fusion.100), channel_id=1, source_target_pairs={{0,2},{1,3},{2,0},{3,1},{4,6},{5,7},{6,4},{7,5},{8,10},{9,11},{10,... | collective-permute-start | bytes 98312 | tf_op jit(solution)/shard_map/ppermute | solution.py:101
  14.2 2.3 %collective-permute-done.4 = bf16[8,2048]{1,0:T(8,128)(2,1)S(1)} collective-permute-done((bf16[8,2048]{1,0:T(8,128)(2,1)S(1)}, bf16[8,2048]{1,0:T(8,128)(2,1)S(1)}, u32[]{:S(2)}, u32[]{:S(2)}) %collective-permute-start.4) | collective-permute-done | bytes 32800 | tf_op jit(solution)/shard_map/ppermute | solution.py:101
  17.3 6.9 %fusion.26 = f32[2,4,8,1280]{3,2,1,0:T(8,128)S(1)} fusion(bf16[2048,2,1280]{2,1,0:T(2,128)(2,1)} %param.22, bf16[8,2048]{1,0:T(8,128)(2,1)S(1)} %collective-permute-done.5, bf16[8,2048]{1,0:T(8,128)(2,1)S(1)} %collective-permute-done.4, bf16[8,2048]{1,0:T(8,128)(2,1)S(1)} %collective-permute-done.3, bf16[8,2048]{1,0:T(8,128)(2,1)S(1)} %fusion.100, ...), kind=kOutput, calls=%fused_computation.26 | convolution fusion | flops 340329472 | bytes 10944640 | tf_op jit(solution)/shard_map/rf,fgc->rgc/dot_general | solution.py:220
  25.4 1.4 %collective-permute-start.8 = (f32[8,2560]{1,0:T(8,128)S(1)}, f32[8,2560]{1,0:T(8,128)S(1)}, u32[]{:S(2)}, u32[]{:S(2)}) collective-permute-start(f32[8,2560]{1,0:T(8,128)S(1)} %get-tuple-element.66), channel_id=1, source_target_pairs={{0,12},{4,0},{8,4},{12,8},{1,13},{5,1},{9,5},{13,9},{2,14},{6,2},{... | collective-permute-start | bytes 245768 | tf_op jit(solution)/shard_map/ppermute | solution.py:118
  28.0 3.6 %collective-permute-done.6 = f32[8,2560]{1,0:T(8,128)S(1)} collective-permute-done((f32[8,2560]{1,0:T(8,128)S(1)}, f32[8,2560]{1,0:T(8,128)S(1)}, u32[]{:S(2)}, u32[]{:S(2)}) %collective-permute-start.6) | collective-permute-done | bytes 81952 | tf_op jit(solution)/shard_map/ppermute | solution.py:118
  31.7 1.5 %collective-permute-done.7 = f32[8,2560]{1,0:T(8,128)S(1)} collective-permute-done((f32[8,2560]{1,0:T(8,128)S(1)}, f32[8,2560]{1,0:T(8,128)S(1)}, u32[]{:S(2)}, u32[]{:S(2)}) %collective-permute-start.7) | collective-permute-done | bytes 81952 | tf_op jit(solution)/shard_map/ppermute | solution.py:118
  34.6 1.3 %collective-permute-start.11 = (bf16[8,2048]{1,0:T(8,128)(2,1)S(1)}, bf16[8,2048]{1,0:T(8,128)(2,1)S(1)}, u32[]{:S(2)}, u32[]{:S(2)}) collective-permute-start(bf16[8,2048]{1,0:T(8,128)(2,1)S(1)} %bitcast.100), channel_id=1, source_target_pairs={{0,12},{4,0},{8,4},{12,8},{1,13},{5,1},{9,5},{13,9},{2,14},{6,2},{... | collective-permute-start | bytes 98312 | tf_op jit(solution)/shard_map/ppermute | solution.py:101
  38.6 2.5 %collective-permute-done.10 = bf16[8,2048]{1,0:T(8,128)(2,1)S(1)} collective-permute-done((bf16[8,2048]{1,0:T(8,128)(2,1)S(1)}, bf16[8,2048]{1,0:T(8,128)(2,1)S(1)}, u32[]{:S(2)}, u32[]{:S(2)}) %collective-permute-start.10) | collective-permute-done | bytes 32800 | tf_op jit(solution)/shard_map/ppermute | solution.py:101
  41.1 1.6 %collective-permute-done.9 = bf16[8,2048]{1,0:T(8,128)(2,1)S(1)} collective-permute-done((bf16[8,2048]{1,0:T(8,128)(2,1)S(1)}, bf16[8,2048]{1,0:T(8,128)(2,1)S(1)}, u32[]{:S(2)}, u32[]{:S(2)}) %collective-permute-start.9) | collective-permute-done | bytes 32800 | tf_op jit(solution)/shard_map/ppermute | solution.py:101
  42.7 5.1 %fusion.39 = f32[32,2048]{1,0:T(8,128)S(1)} fusion(bf16[2048,2048]{1,0:T(8,128)(2,1)} %param.23, bf16[8,2048]{1,0:T(8,128)(2,1)S(1)} %collective-permute-done.11, bf16[8,2048]{1,0:T(8,128)(2,1)S(1)} %collective-permute-done.10, bf16[8,2048]{1,0:T(8,128)(2,1)S(1)} %collective-permute-done.9, bf16[8,2048]{1,0:T(8,128)(2,1)S(1)} %bitcast.103, s32[32]{0:T(128)S(1)} %fusion.130), kind=kOutput, calls=%fused_computation.33 | convolution fusion | flops 273220608 | bytes 8781952 | tf_op jit(solution)/shard_map/dot_general | solution.py:228
  47.9 1.3 %collective-permute-done.12 = f32[16,2048]{1,0:T(8,128)S(1)} collective-permute-done((f32[16,2048]{1,0:T(8,128)S(1)}, f32[16,2048]{1,0:T(8,128)S(1)}, u32[]{:S(2)}, u32[]{:S(2)}) %collective-permute-start.12) | collective-permute-done | bytes 131104 | tf_op jit(solution)/shard_map/ppermute | solution.py:118
  50.2 4.7 %collective-permute-done.13 = f32[16,2048]{1,0:T(8,128)S(1)} collective-permute-done((f32[16,2048]{1,0:T(8,128)S(1)}, f32[16,2048]{1,0:T(8,128)S(1)}, u32[]{:S(2)}, u32[]{:S(2)}) %collective-permute-start.13) | collective-permute-done | bytes 131104 | tf_op jit(solution)/shard_map/ppermute | solution.py:144
  55.1 1.2 %collective-permute-done.14 = f32[16,2048]{1,0:T(8,128)S(1)} collective-permute-done((f32[16,2048]{1,0:T(8,128)S(1)}, f32[16,2048]{1,0:T(8,128)S(1)}, u32[]{:S(2)}, u32[]{:S(2)}) %collective-permute-start.14) | collective-permute-done | bytes 131104 | tf_op jit(solution)/shard_map/ppermute | solution.py:136
  56.9 1.7 %collective-permute-start.15 = (f32[32]{0:T(128)S(1)}, f32[32]{0:T(128)S(1)}, u32[]{:S(2)}, u32[]{:S(2)}) collective-permute-start(f32[32]{0:T(128)S(1)} %reduce_sum.62), channel_id=1, source_target_pairs={{0,4},{4,8},{8,12},{12,0},{1,5},{5,9},{9,13},{13,1},{2,6},{6,10},{... | collective-permute-start | bytes 392 | tf_op jit(solution)/shard_map/ppermute | solution.py:144
  58.6 1.4 %collective-permute-done.17 = f32[32]{0:T(128)S(1)} collective-permute-done((f32[32]{0:T(128)S(1)}, f32[32]{0:T(128)S(1)}, u32[]{:S(2)}, u32[]{:S(2)}) %collective-permute-start.17) | collective-permute-done | bytes 160 | tf_op jit(solution)/shard_map/ppermute | solution.py:144
  62.5 2.7 %fusion.55 = bf16[32,896]{1,0:T(8,128)(2,1)S(1)} fusion(bf16[32,2048]{1,0:T(8,128)(2,1)S(1)} %multiply_convert_fusion, bf16[2048,3584]{1,0:T(8,128)(2,1)} %param.26, s32[]{:T(128)S(6)} %select_n.218), kind=kOutput, calls=%fused_computation.40 | convolution fusion | flops 117469184 | bytes 3858436 | tf_op jit(solution)/shard_map/dot_general | solution.py:154
  65.3 2.9 %fusion.52 = bf16[32,896]{1,0:T(8,128)(2,1)S(1)} fusion(bf16[32,2048]{1,0:T(8,128)(2,1)S(1)} %multiply_convert_fusion, bf16[2048,3584]{1,0:T(8,128)(2,1)} %param.25, s32[]{:T(128)S(6)} %select_n.218), kind=kOutput, calls=%fused_computation.39 | convolution fusion | flops 117469184 | bytes 3858436 | tf_op jit(solution)/shard_map/dot_general | solution.py:154
  68.2 2.9 %fusion.49 = bf16[32,896]{1,0:T(8,128)(2,1)S(1)} fusion(bf16[32,2048]{1,0:T(8,128)(2,1)S(1)} %multiply_convert_fusion, bf16[2048,3584]{1,0:T(8,128)(2,1)} %param.26, s32[]{:T(128)S(6)} %select_n.217), kind=kOutput, calls=%fused_computation.38 | convolution fusion | flops 117469184 | bytes 3858436 | tf_op jit(solution)/shard_map/dot_general | solution.py:154
  71.0 2.7 %fusion.46 = bf16[32,896]{1,0:T(8,128)(2,1)S(1)} fusion(bf16[32,2048]{1,0:T(8,128)(2,1)S(1)} %multiply_convert_fusion, bf16[2048,3584]{1,0:T(8,128)(2,1)} %param.25, s32[]{:T(128)S(6)} %select_n.217), kind=kOutput, calls=%fused_computation.37 | convolution fusion | flops 117469184 | bytes 3858436 | tf_op jit(solution)/shard_map/dot_general | solution.py:154
  73.8 2.9 %fusion.43 = bf16[32,896]{1,0:T(8,128)(2,1)S(1)} fusion(bf16[32,2048]{1,0:T(8,128)(2,1)S(1)} %multiply_convert_fusion, bf16[2048,3584]{1,0:T(8,128)(2,1)} %param.26, s32[]{:T(128)S(6)} %select_n.216), kind=kOutput, calls=%fused_computation.36 | convolution fusion | flops 117469184 | bytes 3858436 | tf_op jit(solution)/shard_map/dot_general | solution.py:154
  76.6 2.7 %fusion.40 = bf16[32,896]{1,0:T(8,128)(2,1)S(1)} fusion(bf16[32,2048]{1,0:T(8,128)(2,1)S(1)} %multiply_convert_fusion, bf16[2048,3584]{1,0:T(8,128)(2,1)} %param.25, s32[]{:T(128)S(6)} %select_n.216), kind=kOutput, calls=%fused_computation.35 | convolution fusion | flops 117469184 | bytes 3858436 | tf_op jit(solution)/shard_map/dot_general | solution.py:154
  80.3 1.7 %collective-permute-start.19 = (bf16[32,1792]{1,0:T(8,128)(2,1)S(1)}, bf16[32,1792]{1,0:T(8,128)(2,1)S(1)}, u32[]{:S(2)}, u32[]{:S(2)}) collective-permute-start(bf16[32,1792]{1,0:T(8,128)(2,1)S(1)} %get-tuple-element.19), channel_id=1, source_target_pairs={{0,4},{4,8},{8,12},{12,0},{1,5},{5,9},{9,13},{13,1},{2,6},{6,10},{... | collective-permute-start | bytes 344072 | tf_op jit(solution)/shard_map/ppermute | solution.py:168
  82.1 2.1 %collective-permute-start.20 = (bf16[32,1792]{1,0:T(8,128)(2,1)S(1)}, bf16[32,1792]{1,0:T(8,128)(2,1)S(1)}, u32[]{:S(2)}, u32[]{:S(2)}) collective-permute-start(bf16[32,1792]{1,0:T(8,128)(2,1)S(1)} %pad_maximum_fusion.3), channel_id=1, source_target_pairs={{0,12},{4,0},{8,4},{12,8},{1,13},{5,1},{9,5},{13,9},{2,14},{6,2},{... | collective-permute-start | bytes 344072 | tf_op jit(solution)/shard_map/ppermute | solution.py:168
  84.2 2.7 %fusion.61 = bf16[32,896]{1,0:T(8,128)(2,1)S(1)} fusion(bf16[32,2048]{1,0:T(8,128)(2,1)S(1)} %multiply_convert_fusion, bf16[2048,3584]{1,0:T(8,128)(2,1)} %param.26, s32[]{:T(128)S(6)} %select_n.219), kind=kOutput, calls=%fused_computation.42 | convolution fusion | flops 117469184 | bytes 3858436 | tf_op jit(solution)/shard_map/dot_general | solution.py:154
  86.9 2.7 %fusion.58 = bf16[32,896]{1,0:T(8,128)(2,1)S(1)} fusion(bf16[32,2048]{1,0:T(8,128)(2,1)S(1)} %multiply_convert_fusion, bf16[2048,3584]{1,0:T(8,128)(2,1)} %param.25, s32[]{:T(128)S(6)} %select_n.219), kind=kOutput, calls=%fused_computation.41 | convolution fusion | flops 117469184 | bytes 3858436 | tf_op jit(solution)/shard_map/dot_general | solution.py:154
  90.0 2.0 %collective-permute-start.23 = (bf16[32,896]{1,0:T(8,128)(2,1)S(1)}, bf16[32,896]{1,0:T(8,128)(2,1)S(1)}, u32[]{:S(2)}, u32[]{:S(2)}) collective-permute-start(bf16[32,896]{1,0:T(8,128)(2,1)S(1)} %fusion.94), channel_id=1, source_target_pairs={{0,12},{4,0},{8,4},{12,8},{1,13},{5,1},{9,5},{13,9},{2,14},{6,2},{... | collective-permute-start | bytes 172040 | tf_op jit(solution)/shard_map/ppermute | solution.py:181
  92.5 1.8 %collective-permute-start.21 = (bf16[32,896]{1,0:T(8,128)(2,1)S(1)}, bf16[32,896]{1,0:T(8,128)(2,1)S(1)}, u32[]{:S(2)}, u32[]{:S(2)}) collective-permute-start(bf16[32,896]{1,0:T(8,128)(2,1)S(1)} %fusion.94), channel_id=1, source_target_pairs={{0,8},{4,12},{8,0},{12,4},{1,9},{5,13},{9,1},{13,5},{2,10},{6,14},... | collective-permute-start | bytes 172040 | tf_op jit(solution)/shard_map/ppermute | solution.py:181
  95.1 2.9 %collective-permute-done.22 = bf16[32,896]{1,0:T(8,128)(2,1)S(1)} collective-permute-done((bf16[32,896]{1,0:T(8,128)(2,1)S(1)}, bf16[32,896]{1,0:T(8,128)(2,1)S(1)}, u32[]{:S(2)}, u32[]{:S(2)}) %collective-permute-start.22) | collective-permute-done | bytes 57376 | tf_op jit(solution)/shard_map/ppermute | solution.py:181
  100.5 1.3 %collective-permute-done.24 = f32[2,8,2048]{2,1,0:T(8,128)S(1)} collective-permute-done((f32[2,8,2048]{2,1,0:T(8,128)S(1)}, f32[2,8,2048]{2,1,0:T(8,128)S(1)}, u32[]{:S(2)}, u32[]{:S(2)}) %collective-permute-start.24) | collective-permute-done | bytes 131104 | tf_op jit(solution)/shard_map/ppermute | solution.py:118
  102.8 3.4 %collective-permute-done.25 = f32[8,2048]{1,0:T(8,128)S(1)} collective-permute-done((f32[8,2048]{1,0:T(8,128)S(1)}, f32[8,2048]{1,0:T(8,128)S(1)}, u32[]{:S(2)}, u32[]{:S(2)}) %collective-permute-start.25) | collective-permute-done | bytes 65568 | tf_op jit(solution)/shard_map/ppermute | solution.py:118
  (98 shorter events, 24.1 us)
Async XLA Ops:
  0.0 27.5 %copy-start = (bf16[8,256,2,2,128]{4,3,2,1,0:T(2,128)(2,1)S(1)}, bf16[8,256,2,2,128]{4,3,2,1,0:T(2,128)(2,1)}, u32[]{:S(2)}) copy-start(bf16[8,256,2,2,128]{4,3,2,1,0:T(2,128)(2,1)} %param.28) | copy-start | bytes 6291460
  1.0 8.1 %collective-permute-start.2 = (f32[8]{0:T(128)S(1)}, f32[8]{0:T(128)S(1)}, u32[]{:S(2)}, u32[]{:S(2)}) collective-permute-start(f32[8]{0:T(128)S(1)} %fusion.98), channel_id=1, source_target_pairs={{0,12},{4,0},{8,4},{12,8},{1,13},{5,1},{9,5},{13,9},{2,14},{6,2},{... | collective-permute-start | bytes 104 | tf_op jit(solution)/shard_map/ppermute | solution.py:144
  6.1 4.4 %collective-permute-start.1 = (f32[8]{0:T(128)S(1)}, f32[8]{0:T(128)S(1)}, u32[]{:S(2)}, u32[]{:S(2)}) collective-permute-start(f32[8]{0:T(128)S(1)} %fusion.98), channel_id=1, source_target_pairs={{0,8},{4,12},{8,0},{12,4},{1,9},{5,13},{9,1},{13,5},{2,10},{6,14},... | collective-permute-start | bytes 104 | tf_op jit(solution)/shard_map/ppermute | solution.py:144
  6.1 5.3 %collective-permute-start = (f32[8]{0:T(128)S(1)}, f32[8]{0:T(128)S(1)}, u32[]{:S(2)}, u32[]{:S(2)}) collective-permute-start(f32[8]{0:T(128)S(1)} %fusion.98), channel_id=1, source_target_pairs={{0,4},{4,8},{8,12},{12,0},{1,5},{5,9},{9,13},{13,1},{2,6},{6,10},{... | collective-permute-start | bytes 104 | tf_op jit(solution)/shard_map/ppermute | solution.py:144
  12.3 1.9 %collective-permute-start.5 = (bf16[8,2048]{1,0:T(8,128)(2,1)S(1)}, bf16[8,2048]{1,0:T(8,128)(2,1)S(1)}, u32[]{:S(2)}, u32[]{:S(2)}) collective-permute-start(bf16[8,2048]{1,0:T(8,128)(2,1)S(1)} %fusion.100), channel_id=1, source_target_pairs={{0,3},{1,0},{2,1},{3,2},{4,7},{5,4},{6,5},{7,6},{8,11},{9,8},{10,9... | collective-permute-start | bytes 98312 | tf_op jit(solution)/shard_map/ppermute | solution.py:101
  12.4 4.1 %collective-permute-start.4 = (bf16[8,2048]{1,0:T(8,128)(2,1)S(1)}, bf16[8,2048]{1,0:T(8,128)(2,1)S(1)}, u32[]{:S(2)}, u32[]{:S(2)}) collective-permute-start(bf16[8,2048]{1,0:T(8,128)(2,1)S(1)} %fusion.100), channel_id=1, source_target_pairs={{0,2},{1,3},{2,0},{3,1},{4,6},{5,7},{6,4},{7,5},{8,10},{9,11},{10,... | collective-permute-start | bytes 98312 | tf_op jit(solution)/shard_map/ppermute | solution.py:101
  13.9 3.3 %collective-permute-start.3 = (bf16[8,2048]{1,0:T(8,128)(2,1)S(1)}, bf16[8,2048]{1,0:T(8,128)(2,1)S(1)}, u32[]{:S(2)}, u32[]{:S(2)}) collective-permute-start(bf16[8,2048]{1,0:T(8,128)(2,1)S(1)} %fusion.100), channel_id=1, source_target_pairs={{0,1},{1,2},{2,3},{3,0},{4,5},{5,6},{6,7},{7,4},{8,9},{9,10},{10,1... | collective-permute-start | bytes 98312 | tf_op jit(solution)/shard_map/ppermute | solution.py:101
  24.2 7.4 %collective-permute-start.6 = (f32[8,2560]{1,0:T(8,128)S(1)}, f32[8,2560]{1,0:T(8,128)S(1)}, u32[]{:S(2)}, u32[]{:S(2)}) collective-permute-start(f32[8,2560]{1,0:T(8,128)S(1)} %get-tuple-element.65), channel_id=1, source_target_pairs={{0,8},{4,12},{8,0},{12,4},{1,9},{5,13},{9,1},{13,5},{2,10},{6,14},... | collective-permute-start | bytes 245768 | tf_op jit(solution)/shard_map/ppermute | solution.py:118
  25.4 6.2 %collective-permute-start.8 = (f32[8,2560]{1,0:T(8,128)S(1)}, f32[8,2560]{1,0:T(8,128)S(1)}, u32[]{:S(2)}, u32[]{:S(2)}) collective-permute-start(f32[8,2560]{1,0:T(8,128)S(1)} %get-tuple-element.66), channel_id=1, source_target_pairs={{0,12},{4,0},{8,4},{12,8},{1,13},{5,1},{9,5},{13,9},{2,14},{6,2},{... | collective-permute-start | bytes 245768 | tf_op jit(solution)/shard_map/ppermute | solution.py:118
  26.8 6.3 %collective-permute-start.7 = (f32[8,2560]{1,0:T(8,128)S(1)}, f32[8,2560]{1,0:T(8,128)S(1)}, u32[]{:S(2)}, u32[]{:S(2)}) collective-permute-start(f32[8,2560]{1,0:T(8,128)S(1)} %get-tuple-element.67), channel_id=1, source_target_pairs={{0,4},{4,8},{8,12},{12,0},{1,5},{5,9},{9,13},{13,1},{2,6},{6,10},{... | collective-permute-start | bytes 245768 | tf_op jit(solution)/shard_map/ppermute | solution.py:118
  27.5 20.2 %copy-start.1 = (bf16[8,2048]{1,0:T(8,128)(2,1)S(1)}, bf16[8,2048]{1,0:T(8,128)(2,1)}, u32[]{:S(2)}) copy-start(bf16[8,2048]{1,0:T(8,128)(2,1)} %param.20) | copy-start | bytes 98308
  28.0 34.4 %copy-start.2 = (f32[2048]{0:T(1024)S(1)}, f32[2048]{0:T(1024)}, u32[]{:S(2)}) copy-start(f32[2048]{0:T(1024)} %param.24) | copy-start | bytes 24580
  34.6 4.0 %collective-permute-start.11 = (bf16[8,2048]{1,0:T(8,128)(2,1)S(1)}, bf16[8,2048]{1,0:T(8,128)(2,1)S(1)}, u32[]{:S(2)}, u32[]{:S(2)}) collective-permute-start(bf16[8,2048]{1,0:T(8,128)(2,1)S(1)} %bitcast.100), channel_id=1, source_target_pairs={{0,12},{4,0},{8,4},{12,8},{1,13},{5,1},{9,5},{13,9},{2,14},{6,2},{... | collective-permute-start | bytes 98312 | tf_op jit(solution)/shard_map/ppermute | solution.py:101
  35.9 5.2 %collective-permute-start.10 = (bf16[8,2048]{1,0:T(8,128)(2,1)S(1)}, bf16[8,2048]{1,0:T(8,128)(2,1)S(1)}, u32[]{:S(2)}, u32[]{:S(2)}) collective-permute-start(bf16[8,2048]{1,0:T(8,128)(2,1)S(1)} %bitcast.101), channel_id=1, source_target_pairs={{0,8},{4,12},{8,0},{12,4},{1,9},{5,13},{9,1},{13,5},{2,10},{6,14},... | collective-permute-start | bytes 98312 | tf_op jit(solution)/shard_map/ppermute | solution.py:101
  36.9 5.7 %collective-permute-start.9 = (bf16[8,2048]{1,0:T(8,128)(2,1)S(1)}, bf16[8,2048]{1,0:T(8,128)(2,1)S(1)}, u32[]{:S(2)}, u32[]{:S(2)}) collective-permute-start(bf16[8,2048]{1,0:T(8,128)(2,1)S(1)} %bitcast.102), channel_id=1, source_target_pairs={{0,4},{4,8},{8,12},{12,0},{1,5},{5,9},{9,13},{13,1},{2,6},{6,10},{... | collective-permute-start | bytes 98312 | tf_op jit(solution)/shard_map/ppermute | solution.py:101
  47.8 1.4 %collective-permute-start.12 = (f32[16,2048]{1,0:T(8,128)S(1)}, f32[16,2048]{1,0:T(8,128)S(1)}, u32[]{:S(2)}, u32[]{:S(2)}) collective-permute-start(f32[16,2048]{1,0:T(8,128)S(1)} %select_bitcast_fusion.1), channel_id=1, source_target_pairs={{0,1},{1,0},{2,3},{3,2},{4,5},{5,4},{6,7},{7,6},{8,9},{9,8},{10,11... | collective-permute-start | bytes 393224 | tf_op jit(solution)/shard_map/ppermute | solution.py:118
  49.2 5.6 %collective-permute-start.13 = (f32[16,2048]{1,0:T(8,128)S(1)}, f32[16,2048]{1,0:T(8,128)S(1)}, u32[]{:S(2)}, u32[]{:S(2)}) collective-permute-start(f32[16,2048]{1,0:T(8,128)S(1)} %bitcast_add_fusion.1), channel_id=1, source_target_pairs={{0,2},{2,0},{1,3},{3,1},{4,6},{6,4},{5,7},{7,5},{8,10},{10,8},{9,1... | collective-permute-start | bytes 393224 | tf_op jit(solution)/shard_map/ppermute | solution.py:144
  54.9 1.4 %collective-permute-start.14 = (f32[16,2048]{1,0:T(8,128)S(1)}, f32[16,2048]{1,0:T(8,128)S(1)}, u32[]{:S(2)}, u32[]{:S(2)}) collective-permute-start(f32[16,2048]{1,0:T(8,128)S(1)} %add.289), channel_id=1, source_target_pairs={{0,1},{1,0},{2,3},{3,2},{4,5},{5,4},{6,7},{7,6},{8,9},{9,8},{10,11... | collective-permute-start | bytes 393224 | tf_op jit(solution)/shard_map/ppermute | solution.py:136
  56.5 3.5 %collective-permute-start.17 = (f32[32]{0:T(128)S(1)}, f32[32]{0:T(128)S(1)}, u32[]{:S(2)}, u32[]{:S(2)}) collective-permute-start(f32[32]{0:T(128)S(1)} %reduce_sum.62), channel_id=1, source_target_pairs={{0,12},{4,0},{8,4},{12,8},{1,13},{5,1},{9,5},{13,9},{2,14},{6,2},{... | collective-permute-start | bytes 392 | tf_op jit(solution)/shard_map/ppermute | solution.py:144
  56.8 4.4 %collective-permute-start.16 = (f32[32]{0:T(128)S(1)}, f32[32]{0:T(128)S(1)}, u32[]{:S(2)}, u32[]{:S(2)}) collective-permute-start(f32[32]{0:T(128)S(1)} %reduce_sum.62), channel_id=1, source_target_pairs={{0,8},{4,12},{8,0},{12,4},{1,9},{5,13},{9,1},{13,5},{2,10},{6,14},... | collective-permute-start | bytes 392 | tf_op jit(solution)/shard_map/ppermute | solution.py:144
  56.9 5.5 %collective-permute-start.15 = (f32[32]{0:T(128)S(1)}, f32[32]{0:T(128)S(1)}, u32[]{:S(2)}, u32[]{:S(2)}) collective-permute-start(f32[32]{0:T(128)S(1)} %reduce_sum.62), channel_id=1, source_target_pairs={{0,4},{4,8},{8,12},{12,0},{1,5},{5,9},{9,13},{13,1},{2,6},{6,10},{... | collective-permute-start | bytes 392 | tf_op jit(solution)/shard_map/ppermute | solution.py:144
  65.3 29.1 %slice-start = ((s8[14680064]{0:T(1024)(128)(4,1)}), s8[4194304]{0:T(1024)(128)(4,1)S(1)}, s32[]{:S(2)}) async-start(s8[14680064]{0:T(1024)(128)(4,1)} %bitcast.85), calls=%async_computation | async-start | bytes 8388608
  68.1 26.2 %slice-start.1 = ((s8[14680064]{0:T(1024)(128)(4,1)}), s8[4194304]{0:T(1024)(128)(4,1)S(1)}, s32[]{:S(2)}) async-start(s8[14680064]{0:T(1024)(128)(4,1)} %bitcast.85), calls=%async_computation.1 | async-start | bytes 8388608
  73.7 20.6 %slice-start.2 = ((s8[14680064]{0:T(1024)(128)(4,1)}), s8[4194304]{0:T(1024)(128)(4,1)S(1)}, s32[]{:S(2)}) async-start(s8[14680064]{0:T(1024)(128)(4,1)} %bitcast.85), calls=%async_computation.2 | async-start | bytes 8388608
  79.4 10.2 %collective-permute-start.18 = (bf16[32,1792]{1,0:T(8,128)(2,1)S(1)}, bf16[32,1792]{1,0:T(8,128)(2,1)S(1)}, u32[]{:S(2)}, u32[]{:S(2)}) collective-permute-start(bf16[32,1792]{1,0:T(8,128)(2,1)S(1)} %get-tuple-element.18), channel_id=1, source_target_pairs={{0,8},{4,12},{8,0},{12,4},{1,9},{5,13},{9,1},{13,5},{2,10},{6,14},... | collective-permute-start | bytes 344072 | tf_op jit(solution)/shard_map/ppermute | solution.py:168
  80.3 9.3 %collective-permute-start.19 = (bf16[32,1792]{1,0:T(8,128)(2,1)S(1)}, bf16[32,1792]{1,0:T(8,128)(2,1)S(1)}, u32[]{:S(2)}, u32[]{:S(2)}) collective-permute-start(bf16[32,1792]{1,0:T(8,128)(2,1)S(1)} %get-tuple-element.19), channel_id=1, source_target_pairs={{0,4},{4,8},{8,12},{12,0},{1,5},{5,9},{9,13},{13,1},{2,6},{6,10},{... | collective-permute-start | bytes 344072 | tf_op jit(solution)/shard_map/ppermute | solution.py:168
  82.1 7.9 %collective-permute-start.20 = (bf16[32,1792]{1,0:T(8,128)(2,1)S(1)}, bf16[32,1792]{1,0:T(8,128)(2,1)S(1)}, u32[]{:S(2)}, u32[]{:S(2)}) collective-permute-start(bf16[32,1792]{1,0:T(8,128)(2,1)S(1)} %pad_maximum_fusion.3), channel_id=1, source_target_pairs={{0,12},{4,0},{8,4},{12,8},{1,13},{5,1},{9,5},{13,9},{2,14},{6,2},{... | collective-permute-start | bytes 344072 | tf_op jit(solution)/shard_map/ppermute | solution.py:168
  90.0 8.7 %collective-permute-start.23 = (bf16[32,896]{1,0:T(8,128)(2,1)S(1)}, bf16[32,896]{1,0:T(8,128)(2,1)S(1)}, u32[]{:S(2)}, u32[]{:S(2)}) collective-permute-start(bf16[32,896]{1,0:T(8,128)(2,1)S(1)} %fusion.94), channel_id=1, source_target_pairs={{0,12},{4,0},{8,4},{12,8},{1,13},{5,1},{9,5},{13,9},{2,14},{6,2},{... | collective-permute-start | bytes 172040 | tf_op jit(solution)/shard_map/ppermute | solution.py:181
  92.0 6.0 %collective-permute-start.22 = (bf16[32,896]{1,0:T(8,128)(2,1)S(1)}, bf16[32,896]{1,0:T(8,128)(2,1)S(1)}, u32[]{:S(2)}, u32[]{:S(2)}) collective-permute-start(bf16[32,896]{1,0:T(8,128)(2,1)S(1)} %fusion.94), channel_id=1, source_target_pairs={{0,4},{4,8},{8,12},{12,0},{1,5},{5,9},{9,13},{13,1},{2,6},{6,10},{... | collective-permute-start | bytes 172040 | tf_op jit(solution)/shard_map/ppermute | solution.py:181
  92.5 7.0 %collective-permute-start.21 = (bf16[32,896]{1,0:T(8,128)(2,1)S(1)}, bf16[32,896]{1,0:T(8,128)(2,1)S(1)}, u32[]{:S(2)}, u32[]{:S(2)}) collective-permute-start(bf16[32,896]{1,0:T(8,128)(2,1)S(1)} %fusion.94), channel_id=1, source_target_pairs={{0,8},{4,12},{8,0},{12,4},{1,9},{5,13},{9,1},{13,5},{2,10},{6,14},... | collective-permute-start | bytes 172040 | tf_op jit(solution)/shard_map/ppermute | solution.py:181
  100.4 1.4 %collective-permute-start.24 = (f32[2,8,2048]{2,1,0:T(8,128)S(1)}, f32[2,8,2048]{2,1,0:T(8,128)S(1)}, u32[]{:S(2)}, u32[]{:S(2)}) collective-permute-start(f32[2,8,2048]{2,1,0:T(8,128)S(1)} %select_bitcast_fusion), channel_id=1, source_target_pairs={{0,1},{1,0},{2,3},{3,2},{4,5},{5,4},{6,7},{7,6},{8,9},{9,8},{10,11... | collective-permute-start | bytes 393224 | tf_op jit(solution)/shard_map/ppermute | solution.py:118
  101.8 4.3 %collective-permute-start.25 = (f32[8,2048]{1,0:T(8,128)S(1)}, f32[8,2048]{1,0:T(8,128)S(1)}, u32[]{:S(2)}, u32[]{:S(2)}) collective-permute-start(f32[8,2048]{1,0:T(8,128)S(1)} %select_bitcast_fusion.7), channel_id=1, source_target_pairs={{0,2},{2,0},{1,3},{3,1},{4,6},{6,4},{5,7},{7,5},{8,10},{10,8},{9,1... | collective-permute-start | bytes 196616 | tf_op jit(solution)/shard_map/ppermute | solution.py:118
  (1 other events, 15.0 us)

commit v18 on v17

--- a/solution.py
+++ b/solution.py
@@ -140,7 +140,7 @@
 
 def all_sum(x, axis, n):
     total = x
-    for k in range(1, n):
+    for k in send_order(n):
         total = total + lax.ppermute(x, axis, shift_pairs(n, k))
     return total
 

time: 107 us -> 108 us (level)
  starting transfers between devices: 27.4 us -> 28.5 us
    ppermute x6, waiting for transfers between devices: 8.1 us -> 6.86 us  [gather_rows(): sent = {k: lax.ppermute(x, axis, shift_pairs(n, k)) for k in send_order(n)}]
  transfers between devices with their start and end apart: 26 -> 26, of which waited for: 19 -> 17; matrix products, arithmetic and copies ran while one was open for 10% -> 10% of each run, Pallas kernels for 0% -> 0%
where the time goes in v18:
time: 108 us; the launch traced here: 107 us
  matrix products  38 us (35%)
  waiting for transfers between devices  33.9 us (31%)
  starting transfers between devices  28.5 us (26%)
  other arithmetic  5.54 us (5%)
    dot_general x8, matrix products, block(): jnp.dot(x, lax.dynamic_slice_in_dim(w, j * chunk, chunk, 1), preferred_el...  22.1 us
    ppermute x6, waiting for transfers between devices, scatter_sum(): lax.ppermute(piece, axis, shift_pairs(n, k)).astype(jnp.float32)  11.6 us
    ppermute x7, waiting for transfers between devices, all_sum(): total = total + lax.ppermute(x, axis, shift_pairs(n, k))  10.7 us
    ppermute x7, starting transfers between devices, all_sum(): total = total + lax.ppermute(x, axis, shift_pairs(n, k))  10.1 us
    ppermute x6, waiting for transfers between devices, gather_rows(): sent = {k: lax.ppermute(x, axis, shift_pairs(n, k)) for k in send_order(n)}  6.86 us
    dot_general x1, matrix products, local(): jnp.einsum('rf,fgc->rgc', by_slot, w_qkv, preferred_element_type=jnp.floa...  6.85 us
    dot_general x1, matrix products, local(): out_part = jnp.dot(by_row, w_out, preferred_element_type=jnp.float32)  5.09 us
    ppermute x6, starting transfers between devices, gather_rows(): sent = {k: lax.ppermute(x, axis, shift_pairs(n, k)) for k in send_order(n)}  4.93 us
  transfers between devices with their start and end apart: 26, of which 17 were waited for; matrix products, arithmetic and copies ran while one was open for 10% of the time, Pallas kernels for 0%

profile of v18, /device:TPU:0, one launch (start us, length us, event | category | flops | bytes accessed | tf_op | source)
XLA Modules:
  0.0 107.3 jit_solution(8693158183544965022)
XLA Ops:
  1.0 5.1 %collective-permute-start.2 = (f32[8]{0:T(128)S(1)}, f32[8]{0:T(128)S(1)}, u32[]{:S(2)}, u32[]{:S(2)}) collective-permute-start(f32[8]{0:T(128)S(1)} %fusion.98), channel_id=1, source_target_pairs={{0,12},{4,0},{8,4},{12,8},{1,13},{5,1},{9,5},{13,9},{2,14},{6,2},{... | collective-permute-start | bytes 104 | tf_op jit(solution)/shard_map/ppermute | solution.py:144
  9.1 2.3 %collective-permute-done.1 = f32[8]{0:T(128)S(1)} collective-permute-done((f32[8]{0:T(128)S(1)}, f32[8]{0:T(128)S(1)}, u32[]{:S(2)}, u32[]{:S(2)}) %collective-permute-start.1) | collective-permute-done | bytes 64 | tf_op jit(solution)/shard_map/ppermute | solution.py:144
  12.4 1.6 %collective-permute-start.4 = (bf16[8,2048]{1,0:T(8,128)(2,1)S(1)}, bf16[8,2048]{1,0:T(8,128)(2,1)S(1)}, u32[]{:S(2)}, u32[]{:S(2)}) collective-permute-start(bf16[8,2048]{1,0:T(8,128)(2,1)S(1)} %fusion.100), channel_id=1, source_target_pairs={{0,2},{1,3},{2,0},{3,1},{4,6},{5,7},{6,4},{7,5},{8,10},{9,11},{10,... | collective-permute-start | bytes 98312 | tf_op jit(solution)/shard_map/ppermute | solution.py:101
  14.2 2.3 %collective-permute-done.4 = bf16[8,2048]{1,0:T(8,128)(2,1)S(1)} collective-permute-done((bf16[8,2048]{1,0:T(8,128)(2,1)S(1)}, bf16[8,2048]{1,0:T(8,128)(2,1)S(1)}, u32[]{:S(2)}, u32[]{:S(2)}) %collective-permute-start.4) | collective-permute-done | bytes 32800 | tf_op jit(solution)/shard_map/ppermute | solution.py:101
  17.3 6.9 %fusion.26 = f32[2,4,8,1280]{3,2,1,0:T(8,128)S(1)} fusion(bf16[2048,2,1280]{2,1,0:T(2,128)(2,1)} %param.22, bf16[8,2048]{1,0:T(8,128)(2,1)S(1)} %collective-permute-done.5, bf16[8,2048]{1,0:T(8,128)(2,1)S(1)} %collective-permute-done.4, bf16[8,2048]{1,0:T(8,128)(2,1)S(1)} %collective-permute-done.3, bf16[8,2048]{1,0:T(8,128)(2,1)S(1)} %fusion.100, ...), kind=kOutput, calls=%fused_computation.26 | convolution fusion | flops 340329472 | bytes 10944640 | tf_op jit(solution)/shard_map/rf,fgc->rgc/dot_general | solution.py:220
  24.4 3.3 %collective-permute-start.8 = (f32[8,2560]{1,0:T(8,128)S(1)}, f32[8,2560]{1,0:T(8,128)S(1)}, u32[]{:S(2)}, u32[]{:S(2)}) collective-permute-start(f32[8,2560]{1,0:T(8,128)S(1)} %get-tuple-element.66), channel_id=1, source_target_pairs={{0,12},{4,0},{8,4},{12,8},{1,13},{5,1},{9,5},{13,9},{2,14},{6,2},{... | collective-permute-start | bytes 245768 | tf_op jit(solution)/shard_map/ppermute | solution.py:118
  28.4 3.7 %collective-permute-done.6 = f32[8,2560]{1,0:T(8,128)S(1)} collective-permute-done((f32[8,2560]{1,0:T(8,128)S(1)}, f32[8,2560]{1,0:T(8,128)S(1)}, u32[]{:S(2)}, u32[]{:S(2)}) %collective-permute-start.6) | collective-permute-done | bytes 81952 | tf_op jit(solution)/shard_map/ppermute | solution.py:118
  32.1 1.9 %collective-permute-done.7 = f32[8,2560]{1,0:T(8,128)S(1)} collective-permute-done((f32[8,2560]{1,0:T(8,128)S(1)}, f32[8,2560]{1,0:T(8,128)S(1)}, u32[]{:S(2)}, u32[]{:S(2)}) %collective-permute-start.7) | collective-permute-done | bytes 81952 | tf_op jit(solution)/shard_map/ppermute | solution.py:118
  35.4 1.3 %collective-permute-start.11 = (bf16[8,2048]{1,0:T(8,128)(2,1)S(1)}, bf16[8,2048]{1,0:T(8,128)(2,1)S(1)}, u32[]{:S(2)}, u32[]{:S(2)}) collective-permute-start(bf16[8,2048]{1,0:T(8,128)(2,1)S(1)} %bitcast.100), channel_id=1, source_target_pairs={{0,12},{4,0},{8,4},{12,8},{1,13},{5,1},{9,5},{13,9},{2,14},{6,2},{... | collective-permute-start | bytes 98312 | tf_op jit(solution)/shard_map/ppermute | solution.py:101
  36.7 1.9 %collective-permute-start.9 = (bf16[8,2048]{1,0:T(8,128)(2,1)S(1)}, bf16[8,2048]{1,0:T(8,128)(2,1)S(1)}, u32[]{:S(2)}, u32[]{:S(2)}) collective-permute-start(bf16[8,2048]{1,0:T(8,128)(2,1)S(1)} %bitcast.102), channel_id=1, source_target_pairs={{0,4},{4,8},{8,12},{12,0},{1,5},{5,9},{9,13},{13,1},{2,6},{6,10},{... | collective-permute-start | bytes 98312 | tf_op jit(solution)/shard_map/ppermute | solution.py:101
  39.7 1.8 %collective-permute-done.10 = bf16[8,2048]{1,0:T(8,128)(2,1)S(1)} collective-permute-done((bf16[8,2048]{1,0:T(8,128)(2,1)S(1)}, bf16[8,2048]{1,0:T(8,128)(2,1)S(1)}, u32[]{:S(2)}, u32[]{:S(2)}) %collective-permute-start.10) | collective-permute-done | bytes 32800 | tf_op jit(solution)/shard_map/ppermute | solution.py:101
  42.4 5.1 %fusion.39 = f32[32,2048]{1,0:T(8,128)S(1)} fusion(bf16[2048,2048]{1,0:T(8,128)(2,1)} %param.23, bf16[8,2048]{1,0:T(8,128)(2,1)S(1)} %collective-permute-done.11, bf16[8,2048]{1,0:T(8,128)(2,1)S(1)} %collective-permute-done.10, bf16[8,2048]{1,0:T(8,128)(2,1)S(1)} %collective-permute-done.9, bf16[8,2048]{1,0:T(8,128)(2,1)S(1)} %bitcast.103, s32[32]{0:T(128)S(1)} %fusion.130), kind=kOutput, calls=%fused_computation.33 | convolution fusion | flops 273220608 | bytes 8781952 | tf_op jit(solution)/shard_map/dot_general | solution.py:228
  47.6 1.3 %collective-permute-done.12 = f32[16,2048]{1,0:T(8,128)S(1)} collective-permute-done((f32[16,2048]{1,0:T(8,128)S(1)}, f32[16,2048]{1,0:T(8,128)S(1)}, u32[]{:S(2)}, u32[]{:S(2)}) %collective-permute-start.12) | collective-permute-done | bytes 131104 | tf_op jit(solution)/shard_map/ppermute | solution.py:118
  49.8 4.7 %collective-permute-done.13 = f32[16,2048]{1,0:T(8,128)S(1)} collective-permute-done((f32[16,2048]{1,0:T(8,128)S(1)}, f32[16,2048]{1,0:T(8,128)S(1)}, u32[]{:S(2)}, u32[]{:S(2)}) %collective-permute-start.13) | collective-permute-done | bytes 131104 | tf_op jit(solution)/shard_map/ppermute | solution.py:144
  54.8 1.2 %collective-permute-done.14 = f32[16,2048]{1,0:T(8,128)S(1)} collective-permute-done((f32[16,2048]{1,0:T(8,128)S(1)}, f32[16,2048]{1,0:T(8,128)S(1)}, u32[]{:S(2)}, u32[]{:S(2)}) %collective-permute-start.14) | collective-permute-done | bytes 131104 | tf_op jit(solution)/shard_map/ppermute | solution.py:136
  56.2 1.4 %collective-permute-start.17 = (f32[32]{0:T(128)S(1)}, f32[32]{0:T(128)S(1)}, u32[]{:S(2)}, u32[]{:S(2)}) collective-permute-start(f32[32]{0:T(128)S(1)} %reduce_sum.62), channel_id=1, source_target_pairs={{0,12},{4,0},{8,4},{12,8},{1,13},{5,1},{9,5},{13,9},{2,14},{6,2},{... | collective-permute-start | bytes 392 | tf_op jit(solution)/shard_map/ppermute | solution.py:144
  59.8 3.2 %collective-permute-done.16 = f32[32]{0:T(128)S(1)} collective-permute-done((f32[32]{0:T(128)S(1)}, f32[32]{0:T(128)S(1)}, u32[]{:S(2)}, u32[]{:S(2)}) %collective-permute-start.16) | collective-permute-done | bytes 160 | tf_op jit(solution)/shard_map/ppermute | solution.py:144
  63.1 2.7 %fusion.55 = bf16[32,896]{1,0:T(8,128)(2,1)S(1)} fusion(bf16[32,2048]{1,0:T(8,128)(2,1)S(1)} %multiply_convert_fusion, bf16[2048,3584]{1,0:T(8,128)(2,1)} %param.26, s32[]{:T(128)S(6)} %select_n.218), kind=kOutput, calls=%fused_computation.40 | convolution fusion | flops 117469184 | bytes 3858436 | tf_op jit(solution)/shard_map/dot_general | solution.py:154
  65.8 2.9 %fusion.52 = bf16[32,896]{1,0:T(8,128)(2,1)S(1)} fusion(bf16[32,2048]{1,0:T(8,128)(2,1)S(1)} %multiply_convert_fusion, bf16[2048,3584]{1,0:T(8,128)(2,1)} %param.25, s32[]{:T(128)S(6)} %select_n.218), kind=kOutput, calls=%fused_computation.39 | convolution fusion | flops 117469184 | bytes 3858436 | tf_op jit(solution)/shard_map/dot_general | solution.py:154
  68.7 2.9 %fusion.49 = bf16[32,896]{1,0:T(8,128)(2,1)S(1)} fusion(bf16[32,2048]{1,0:T(8,128)(2,1)S(1)} %multiply_convert_fusion, bf16[2048,3584]{1,0:T(8,128)(2,1)} %param.26, s32[]{:T(128)S(6)} %select_n.217), kind=kOutput, calls=%fused_computation.38 | convolution fusion | flops 117469184 | bytes 3858436 | tf_op jit(solution)/shard_map/dot_general | solution.py:154
  71.5 2.7 %fusion.46 = bf16[32,896]{1,0:T(8,128)(2,1)S(1)} fusion(bf16[32,2048]{1,0:T(8,128)(2,1)S(1)} %multiply_convert_fusion, bf16[2048,3584]{1,0:T(8,128)(2,1)} %param.25, s32[]{:T(128)S(6)} %select_n.217), kind=kOutput, calls=%fused_computation.37 | convolution fusion | flops 117469184 | bytes 3858436 | tf_op jit(solution)/shard_map/dot_general | solution.py:154
  74.3 2.9 %fusion.43 = bf16[32,896]{1,0:T(8,128)(2,1)S(1)} fusion(bf16[32,2048]{1,0:T(8,128)(2,1)S(1)} %multiply_convert_fusion, bf16[2048,3584]{1,0:T(8,128)(2,1)} %param.26, s32[]{:T(128)S(6)} %select_n.216), kind=kOutput, calls=%fused_computation.36 | convolution fusion | flops 117469184 | bytes 3858436 | tf_op jit(solution)/shard_map/dot_general | solution.py:154
  77.2 2.7 %fusion.40 = bf16[32,896]{1,0:T(8,128)(2,1)S(1)} fusion(bf16[32,2048]{1,0:T(8,128)(2,1)S(1)} %multiply_convert_fusion, bf16[2048,3584]{1,0:T(8,128)(2,1)} %param.25, s32[]{:T(128)S(6)} %select_n.216), kind=kOutput, calls=%fused_computation.35 | convolution fusion | flops 117469184 | bytes 3858436 | tf_op jit(solution)/shard_map/dot_general | solution.py:154
  80.9 2.6 %collective-permute-start.19 = (bf16[32,1792]{1,0:T(8,128)(2,1)S(1)}, bf16[32,1792]{1,0:T(8,128)(2,1)S(1)}, u32[]{:S(2)}, u32[]{:S(2)}) collective-permute-start(bf16[32,1792]{1,0:T(8,128)(2,1)S(1)} %get-tuple-element.19), channel_id=1, source_target_pairs={{0,4},{4,8},{8,12},{12,0},{1,5},{5,9},{9,13},{13,1},{2,6},{6,10},{... | collective-permute-start | bytes 344072 | tf_op jit(solution)/shard_map/ppermute | solution.py:168
  83.5 1.2 %collective-permute-start.20 = (bf16[32,1792]{1,0:T(8,128)(2,1)S(1)}, bf16[32,1792]{1,0:T(8,128)(2,1)S(1)}, u32[]{:S(2)}, u32[]{:S(2)}) collective-permute-start(bf16[32,1792]{1,0:T(8,128)(2,1)S(1)} %pad_maximum_fusion.3), channel_id=1, source_target_pairs={{0,12},{4,0},{8,4},{12,8},{1,13},{5,1},{9,5},{13,9},{2,14},{6,2},{... | collective-permute-start | bytes 344072 | tf_op jit(solution)/shard_map/ppermute | solution.py:168
  84.7 2.7 %fusion.61 = bf16[32,896]{1,0:T(8,128)(2,1)S(1)} fusion(bf16[32,2048]{1,0:T(8,128)(2,1)S(1)} %multiply_convert_fusion, bf16[2048,3584]{1,0:T(8,128)(2,1)} %param.26, s32[]{:T(128)S(6)} %select_n.219), kind=kOutput, calls=%fused_computation.42 | convolution fusion | flops 117469184 | bytes 3858436 | tf_op jit(solution)/shard_map/dot_general | solution.py:154
  87.4 2.7 %fusion.58 = bf16[32,896]{1,0:T(8,128)(2,1)S(1)} fusion(bf16[32,2048]{1,0:T(8,128)(2,1)S(1)} %multiply_convert_fusion, bf16[2048,3584]{1,0:T(8,128)(2,1)} %param.25, s32[]{:T(128)S(6)} %select_n.219), kind=kOutput, calls=%fused_computation.41 | convolution fusion | flops 117469184 | bytes 3858436 | tf_op jit(solution)/shard_map/dot_general | solution.py:154
  90.9 1.6 %collective-permute-start.23 = (bf16[32,896]{1,0:T(8,128)(2,1)S(1)}, bf16[32,896]{1,0:T(8,128)(2,1)S(1)}, u32[]{:S(2)}, u32[]{:S(2)}) collective-permute-start(bf16[32,896]{1,0:T(8,128)(2,1)S(1)} %fusion.94), channel_id=1, source_target_pairs={{0,12},{4,0},{8,4},{12,8},{1,13},{5,1},{9,5},{13,9},{2,14},{6,2},{... | collective-permute-start | bytes 172040 | tf_op jit(solution)/shard_map/ppermute | solution.py:181
  93.0 1.9 %collective-permute-start.21 = (bf16[32,896]{1,0:T(8,128)(2,1)S(1)}, bf16[32,896]{1,0:T(8,128)(2,1)S(1)}, u32[]{:S(2)}, u32[]{:S(2)}) collective-permute-start(bf16[32,896]{1,0:T(8,128)(2,1)S(1)} %fusion.94), channel_id=1, source_target_pairs={{0,8},{4,12},{8,0},{12,4},{1,9},{5,13},{9,1},{13,5},{2,10},{6,14},... | collective-permute-start | bytes 172040 | tf_op jit(solution)/shard_map/ppermute | solution.py:181
  95.6 2.9 %collective-permute-done.22 = bf16[32,896]{1,0:T(8,128)(2,1)S(1)} collective-permute-done((bf16[32,896]{1,0:T(8,128)(2,1)S(1)}, bf16[32,896]{1,0:T(8,128)(2,1)S(1)}, u32[]{:S(2)}, u32[]{:S(2)}) %collective-permute-start.22) | collective-permute-done | bytes 57376 | tf_op jit(solution)/shard_map/ppermute | solution.py:181
  101.0 1.3 %collective-permute-done.24 = f32[2,8,2048]{2,1,0:T(8,128)S(1)} collective-permute-done((f32[2,8,2048]{2,1,0:T(8,128)S(1)}, f32[2,8,2048]{2,1,0:T(8,128)S(1)}, u32[]{:S(2)}, u32[]{:S(2)}) %collective-permute-start.24) | collective-permute-done | bytes 131104 | tf_op jit(solution)/shard_map/ppermute | solution.py:118
  103.3 3.4 %collective-permute-done.25 = f32[8,2048]{1,0:T(8,128)S(1)} collective-permute-done((f32[8,2048]{1,0:T(8,128)S(1)}, f32[8,2048]{1,0:T(8,128)S(1)}, u32[]{:S(2)}, u32[]{:S(2)}) %collective-permute-start.25) | collective-permute-done | bytes 65568 | tf_op jit(solution)/shard_map/ppermute | solution.py:118
  (98 shorter events, 20.8 us)
Async XLA Ops:
  0.0 27.8 %copy-start = (bf16[8,256,2,2,128]{4,3,2,1,0:T(2,128)(2,1)S(1)}, bf16[8,256,2,2,128]{4,3,2,1,0:T(2,128)(2,1)}, u32[]{:S(2)}) copy-start(bf16[8,256,2,2,128]{4,3,2,1,0:T(2,128)(2,1)} %param.28) | copy-start | bytes 6291460
  1.0 8.1 %collective-permute-start.2 = (f32[8]{0:T(128)S(1)}, f32[8]{0:T(128)S(1)}, u32[]{:S(2)}, u32[]{:S(2)}) collective-permute-start(f32[8]{0:T(128)S(1)} %fusion.98), channel_id=1, source_target_pairs={{0,12},{4,0},{8,4},{12,8},{1,13},{5,1},{9,5},{13,9},{2,14},{6,2},{... | collective-permute-start | bytes 104 | tf_op jit(solution)/shard_map/ppermute | solution.py:144
  6.1 5.3 %collective-permute-start.1 = (f32[8]{0:T(128)S(1)}, f32[8]{0:T(128)S(1)}, u32[]{:S(2)}, u32[]{:S(2)}) collective-permute-start(f32[8]{0:T(128)S(1)} %fusion.98), channel_id=1, source_target_pairs={{0,4},{4,8},{8,12},{12,0},{1,5},{5,9},{9,13},{13,1},{2,6},{6,10},{... | collective-permute-start | bytes 104 | tf_op jit(solution)/shard_map/ppermute | solution.py:144
  6.1 5.3 %collective-permute-start = (f32[8]{0:T(128)S(1)}, f32[8]{0:T(128)S(1)}, u32[]{:S(2)}, u32[]{:S(2)}) collective-permute-start(f32[8]{0:T(128)S(1)} %fusion.98), channel_id=1, source_target_pairs={{0,8},{4,12},{8,0},{12,4},{1,9},{5,13},{9,1},{13,5},{2,10},{6,14},... | collective-permute-start | bytes 104 | tf_op jit(solution)/shard_map/ppermute | solution.py:144
  12.3 1.9 %collective-permute-start.5 = (bf16[8,2048]{1,0:T(8,128)(2,1)S(1)}, bf16[8,2048]{1,0:T(8,128)(2,1)S(1)}, u32[]{:S(2)}, u32[]{:S(2)}) collective-permute-start(bf16[8,2048]{1,0:T(8,128)(2,1)S(1)} %fusion.100), channel_id=1, source_target_pairs={{0,3},{1,0},{2,1},{3,2},{4,7},{5,4},{6,5},{7,6},{8,11},{9,8},{10,9... | collective-permute-start | bytes 98312 | tf_op jit(solution)/shard_map/ppermute | solution.py:101
  12.4 4.1 %collective-permute-start.4 = (bf16[8,2048]{1,0:T(8,128)(2,1)S(1)}, bf16[8,2048]{1,0:T(8,128)(2,1)S(1)}, u32[]{:S(2)}, u32[]{:S(2)}) collective-permute-start(bf16[8,2048]{1,0:T(8,128)(2,1)S(1)} %fusion.100), channel_id=1, source_target_pairs={{0,2},{1,3},{2,0},{3,1},{4,6},{5,7},{6,4},{7,5},{8,10},{9,11},{10,... | collective-permute-start | bytes 98312 | tf_op jit(solution)/shard_map/ppermute | solution.py:101
  13.9 3.3 %collective-permute-start.3 = (bf16[8,2048]{1,0:T(8,128)(2,1)S(1)}, bf16[8,2048]{1,0:T(8,128)(2,1)S(1)}, u32[]{:S(2)}, u32[]{:S(2)}) collective-permute-start(bf16[8,2048]{1,0:T(8,128)(2,1)S(1)} %fusion.100), channel_id=1, source_target_pairs={{0,1},{1,2},{2,3},{3,0},{4,5},{5,6},{6,7},{7,4},{8,9},{9,10},{10,1... | collective-permute-start | bytes 98312 | tf_op jit(solution)/shard_map/ppermute | solution.py:101
  24.2 7.9 %collective-permute-start.6 = (f32[8,2560]{1,0:T(8,128)S(1)}, f32[8,2560]{1,0:T(8,128)S(1)}, u32[]{:S(2)}, u32[]{:S(2)}) collective-permute-start(f32[8,2560]{1,0:T(8,128)S(1)} %get-tuple-element.65), channel_id=1, source_target_pairs={{0,8},{4,12},{8,0},{12,4},{1,9},{5,13},{9,1},{13,5},{2,10},{6,14},... | collective-permute-start | bytes 245768 | tf_op jit(solution)/shard_map/ppermute | solution.py:118
  24.4 7.7 %collective-permute-start.8 = (f32[8,2560]{1,0:T(8,128)S(1)}, f32[8,2560]{1,0:T(8,128)S(1)}, u32[]{:S(2)}, u32[]{:S(2)}) collective-permute-start(f32[8,2560]{1,0:T(8,128)S(1)} %get-tuple-element.66), channel_id=1, source_target_pairs={{0,12},{4,0},{8,4},{12,8},{1,13},{5,1},{9,5},{13,9},{2,14},{6,2},{... | collective-permute-start | bytes 245768 | tf_op jit(solution)/shard_map/ppermute | solution.py:118
  27.7 6.2 %collective-permute-start.7 = (f32[8,2560]{1,0:T(8,128)S(1)}, f32[8,2560]{1,0:T(8,128)S(1)}, u32[]{:S(2)}, u32[]{:S(2)}) collective-permute-start(f32[8,2560]{1,0:T(8,128)S(1)} %get-tuple-element.67), channel_id=1, source_target_pairs={{0,4},{4,8},{8,12},{12,0},{1,5},{5,9},{9,13},{13,1},{2,6},{6,10},{... | collective-permute-start | bytes 245768 | tf_op jit(solution)/shard_map/ppermute | solution.py:118
  27.8 19.6 %copy-start.1 = (bf16[8,2048]{1,0:T(8,128)(2,1)S(1)}, bf16[8,2048]{1,0:T(8,128)(2,1)}, u32[]{:S(2)}) copy-start(bf16[8,2048]{1,0:T(8,128)(2,1)} %param.20) | copy-start | bytes 98308
  28.4 34.6 %copy-start.2 = (f32[2048]{0:T(1024)S(1)}, f32[2048]{0:T(1024)}, u32[]{:S(2)}) copy-start(f32[2048]{0:T(1024)} %param.24) | copy-start | bytes 24580
  35.4 4.3 %collective-permute-start.11 = (bf16[8,2048]{1,0:T(8,128)(2,1)S(1)}, bf16[8,2048]{1,0:T(8,128)(2,1)S(1)}, u32[]{:S(2)}, u32[]{:S(2)}) collective-permute-start(bf16[8,2048]{1,0:T(8,128)(2,1)S(1)} %bitcast.100), channel_id=1, source_target_pairs={{0,12},{4,0},{8,4},{12,8},{1,13},{5,1},{9,5},{13,9},{2,14},{6,2},{... | collective-permute-start | bytes 98312 | tf_op jit(solution)/shard_map/ppermute | solution.py:101
  36.6 4.8 %collective-permute-start.10 = (bf16[8,2048]{1,0:T(8,128)(2,1)S(1)}, bf16[8,2048]{1,0:T(8,128)(2,1)S(1)}, u32[]{:S(2)}, u32[]{:S(2)}) collective-permute-start(bf16[8,2048]{1,0:T(8,128)(2,1)S(1)} %bitcast.101), channel_id=1, source_target_pairs={{0,8},{4,12},{8,0},{12,4},{1,9},{5,13},{9,1},{13,5},{2,10},{6,14},... | collective-permute-start | bytes 98312 | tf_op jit(solution)/shard_map/ppermute | solution.py:101
  36.7 5.7 %collective-permute-start.9 = (bf16[8,2048]{1,0:T(8,128)(2,1)S(1)}, bf16[8,2048]{1,0:T(8,128)(2,1)S(1)}, u32[]{:S(2)}, u32[]{:S(2)}) collective-permute-start(bf16[8,2048]{1,0:T(8,128)(2,1)S(1)} %bitcast.102), channel_id=1, source_target_pairs={{0,4},{4,8},{8,12},{12,0},{1,5},{5,9},{9,13},{13,1},{2,6},{6,10},{... | collective-permute-start | bytes 98312 | tf_op jit(solution)/shard_map/ppermute | solution.py:101
  47.5 1.4 %collective-permute-start.12 = (f32[16,2048]{1,0:T(8,128)S(1)}, f32[16,2048]{1,0:T(8,128)S(1)}, u32[]{:S(2)}, u32[]{:S(2)}) collective-permute-start(f32[16,2048]{1,0:T(8,128)S(1)} %select_bitcast_fusion.1), channel_id=1, source_target_pairs={{0,1},{1,0},{2,3},{3,2},{4,5},{5,4},{6,7},{7,6},{8,9},{9,8},{10,11... | collective-permute-start | bytes 393224 | tf_op jit(solution)/shard_map/ppermute | solution.py:118
  49.0 5.6 %collective-permute-start.13 = (f32[16,2048]{1,0:T(8,128)S(1)}, f32[16,2048]{1,0:T(8,128)S(1)}, u32[]{:S(2)}, u32[]{:S(2)}) collective-permute-start(f32[16,2048]{1,0:T(8,128)S(1)} %bitcast_add_fusion.1), channel_id=1, source_target_pairs={{0,2},{2,0},{1,3},{3,1},{4,6},{6,4},{5,7},{7,5},{8,10},{10,8},{9,1... | collective-permute-start | bytes 393224 | tf_op jit(solution)/shard_map/ppermute | solution.py:144
  54.6 1.4 %collective-permute-start.14 = (f32[16,2048]{1,0:T(8,128)S(1)}, f32[16,2048]{1,0:T(8,128)S(1)}, u32[]{:S(2)}, u32[]{:S(2)}) collective-permute-start(f32[16,2048]{1,0:T(8,128)S(1)} %add.289), channel_id=1, source_target_pairs={{0,1},{1,0},{2,3},{3,2},{4,5},{5,4},{6,7},{7,6},{8,9},{9,8},{10,11... | collective-permute-start | bytes 393224 | tf_op jit(solution)/shard_map/ppermute | solution.py:136
  56.2 3.5 %collective-permute-start.17 = (f32[32]{0:T(128)S(1)}, f32[32]{0:T(128)S(1)}, u32[]{:S(2)}, u32[]{:S(2)}) collective-permute-start(f32[32]{0:T(128)S(1)} %reduce_sum.62), channel_id=1, source_target_pairs={{0,12},{4,0},{8,4},{12,8},{1,13},{5,1},{9,5},{13,9},{2,14},{6,2},{... | collective-permute-start | bytes 392 | tf_op jit(solution)/shard_map/ppermute | solution.py:144
  57.6 5.3 %collective-permute-start.16 = (f32[32]{0:T(128)S(1)}, f32[32]{0:T(128)S(1)}, u32[]{:S(2)}, u32[]{:S(2)}) collective-permute-start(f32[32]{0:T(128)S(1)} %reduce_sum.62), channel_id=1, source_target_pairs={{0,4},{4,8},{8,12},{12,0},{1,5},{5,9},{9,13},{13,1},{2,6},{6,10},{... | collective-permute-start | bytes 392 | tf_op jit(solution)/shard_map/ppermute | solution.py:144
  58.3 4.7 %collective-permute-start.15 = (f32[32]{0:T(128)S(1)}, f32[32]{0:T(128)S(1)}, u32[]{:S(2)}, u32[]{:S(2)}) collective-permute-start(f32[32]{0:T(128)S(1)} %reduce_sum.62), channel_id=1, source_target_pairs={{0,8},{4,12},{8,0},{12,4},{1,9},{5,13},{9,1},{13,5},{2,10},{6,14},... | collective-permute-start | bytes 392 | tf_op jit(solution)/shard_map/ppermute | solution.py:144
  65.8 29.1 %slice-start = ((s8[14680064]{0:T(1024)(128)(4,1)}), s8[4194304]{0:T(1024)(128)(4,1)S(1)}, s32[]{:S(2)}) async-start(s8[14680064]{0:T(1024)(128)(4,1)} %bitcast.85), calls=%async_computation | async-start | bytes 8388608
  68.7 26.2 %slice-start.1 = ((s8[14680064]{0:T(1024)(128)(4,1)}), s8[4194304]{0:T(1024)(128)(4,1)S(1)}, s32[]{:S(2)}) async-start(s8[14680064]{0:T(1024)(128)(4,1)} %bitcast.85), calls=%async_computation.1 | async-start | bytes 8388608
  74.3 20.6 %slice-start.2 = ((s8[14680064]{0:T(1024)(128)(4,1)}), s8[4194304]{0:T(1024)(128)(4,1)S(1)}, s32[]{:S(2)}) async-start(s8[14680064]{0:T(1024)(128)(4,1)} %bitcast.85), calls=%async_computation.2 | async-start | bytes 8388608
  79.9 10.2 %collective-permute-start.18 = (bf16[32,1792]{1,0:T(8,128)(2,1)S(1)}, bf16[32,1792]{1,0:T(8,128)(2,1)S(1)}, u32[]{:S(2)}, u32[]{:S(2)}) collective-permute-start(bf16[32,1792]{1,0:T(8,128)(2,1)S(1)} %get-tuple-element.18), channel_id=1, source_target_pairs={{0,8},{4,12},{8,0},{12,4},{1,9},{5,13},{9,1},{13,5},{2,10},{6,14},... | collective-permute-start | bytes 344072 | tf_op jit(solution)/shard_map/ppermute | solution.py:168
  80.9 9.3 %collective-permute-start.19 = (bf16[32,1792]{1,0:T(8,128)(2,1)S(1)}, bf16[32,1792]{1,0:T(8,128)(2,1)S(1)}, u32[]{:S(2)}, u32[]{:S(2)}) collective-permute-start(bf16[32,1792]{1,0:T(8,128)(2,1)S(1)} %get-tuple-element.19), channel_id=1, source_target_pairs={{0,4},{4,8},{8,12},{12,0},{1,5},{5,9},{9,13},{13,1},{2,6},{6,10},{... | collective-permute-start | bytes 344072 | tf_op jit(solution)/shard_map/ppermute | solution.py:168
  83.5 7.3 %collective-permute-start.20 = (bf16[32,1792]{1,0:T(8,128)(2,1)S(1)}, bf16[32,1792]{1,0:T(8,128)(2,1)S(1)}, u32[]{:S(2)}, u32[]{:S(2)}) collective-permute-start(bf16[32,1792]{1,0:T(8,128)(2,1)S(1)} %pad_maximum_fusion.3), channel_id=1, source_target_pairs={{0,12},{4,0},{8,4},{12,8},{1,13},{5,1},{9,5},{13,9},{2,14},{6,2},{... | collective-permute-start | bytes 344072 | tf_op jit(solution)/shard_map/ppermute | solution.py:168
  90.9 8.3 %collective-permute-start.23 = (bf16[32,896]{1,0:T(8,128)(2,1)S(1)}, bf16[32,896]{1,0:T(8,128)(2,1)S(1)}, u32[]{:S(2)}, u32[]{:S(2)}) collective-permute-start(bf16[32,896]{1,0:T(8,128)(2,1)S(1)} %fusion.94), channel_id=1, source_target_pairs={{0,12},{4,0},{8,4},{12,8},{1,13},{5,1},{9,5},{13,9},{2,14},{6,2},{... | collective-permute-start | bytes 172040 | tf_op jit(solution)/shard_map/ppermute | solution.py:181
  92.5 6.0 %collective-permute-start.22 = (bf16[32,896]{1,0:T(8,128)(2,1)S(1)}, bf16[32,896]{1,0:T(8,128)(2,1)S(1)}, u32[]{:S(2)}, u32[]{:S(2)}) collective-permute-start(bf16[32,896]{1,0:T(8,128)(2,1)S(1)} %fusion.94), channel_id=1, source_target_pairs={{0,4},{4,8},{8,12},{12,0},{1,5},{5,9},{9,13},{13,1},{2,6},{6,10},{... | collective-permute-start | bytes 172040 | tf_op jit(solution)/shard_map/ppermute | solution.py:181
  93.0 7.0 %collective-permute-start.21 = (bf16[32,896]{1,0:T(8,128)(2,1)S(1)}, bf16[32,896]{1,0:T(8,128)(2,1)S(1)}, u32[]{:S(2)}, u32[]{:S(2)}) collective-permute-start(bf16[32,896]{1,0:T(8,128)(2,1)S(1)} %fusion.94), channel_id=1, source_target_pairs={{0,8},{4,12},{8,0},{12,4},{1,9},{5,13},{9,1},{13,5},{2,10},{6,14},... | collective-permute-start | bytes 172040 | tf_op jit(solution)/shard_map/ppermute | solution.py:181
  100.9 1.4 %collective-permute-start.24 = (f32[2,8,2048]{2,1,0:T(8,128)S(1)}, f32[2,8,2048]{2,1,0:T(8,128)S(1)}, u32[]{:S(2)}, u32[]{:S(2)}) collective-permute-start(f32[2,8,2048]{2,1,0:T(8,128)S(1)} %select_bitcast_fusion), channel_id=1, source_target_pairs={{0,1},{1,0},{2,3},{3,2},{4,5},{5,4},{6,7},{7,6},{8,9},{9,8},{10,11... | collective-permute-start | bytes 393224 | tf_op jit(solution)/shard_map/ppermute | solution.py:118
  102.3 4.3 %collective-permute-start.25 = (f32[8,2048]{1,0:T(8,128)S(1)}, f32[8,2048]{1,0:T(8,128)S(1)}, u32[]{:S(2)}, u32[]{:S(2)}) collective-permute-start(f32[8,2048]{1,0:T(8,128)S(1)} %select_bitcast_fusion.7), channel_id=1, source_target_pairs={{0,2},{2,0},{1,3},{3,1},{4,6},{6,4},{5,7},{7,5},{8,10},{10,8},{9,1... | collective-permute-start | bytes 196616 | tf_op jit(solution)/shard_map/ppermute | solution.py:118
  (1 other events, 15.0 us)

commit v19 on v17

--- a/solution.py
+++ b/solution.py
@@ -113,9 +113,12 @@
 def scatter_sum(blocks, axis, n):
     idx = lax.axis_index(axis)
     total = jnp.take(blocks, idx, axis=0).astype(jnp.float32)
-    for k in send_order(n):
-        piece = jnp.take(blocks, (idx + k) % n, axis=0)
-        total = total + lax.ppermute(piece, axis, shift_pairs(n, k)).astype(jnp.float32)
+    sent = {
+        k: lax.ppermute(jnp.take(blocks, (idx + k) % n, axis=0), axis, shift_pairs(n, k))
+        for k in send_order(n)
+    }
+    for k in reversed(send_order(n)):
+        total = total + sent[k].astype(jnp.float32)
     return total
 
 
@@ -177,10 +180,10 @@
     acc = jnp.dot(
         x, lax.dynamic_slice_in_dim(w, idx * chunk, chunk, 0), preferred_element_type=jnp.float32
     )
-    for k in send_order(n):
-        got = lax.ppermute(x, axis, shift_pairs(n, k))
+    sent = {k: lax.ppermute(x, axis, shift_pairs(n, k)) for k in send_order(n)}
+    for k in reversed(send_order(n)):
         rows = lax.dynamic_slice_in_dim(w, ((idx - k) % n) * chunk, chunk, 0)
-        acc = acc + jnp.dot(got, rows, preferred_element_type=jnp.float32)
+        acc = acc + jnp.dot(sent[k], rows, preferred_element_type=jnp.float32)
     return acc
 
 

time: 107 us -> 107 us (level)
  waiting for transfers between devices: 34.5 us -> 31.3 us
  starting transfers between devices: 27.4 us -> 30.1 us
    ppermute x9, waiting for transfers between devices: 14.1 us -> 12.5 us  [the longest x6 11 us: scatter_sum(): lax.ppermute(jnp.take(blocks, (idx + k) % n, axis=0), axis, shift_pairs(n...]
    ppermute x9, starting transfers between devices: 8.61 us -> 10 us  [the longest x3 5.7 us: gather_matmul(): sent = {k: lax.ppermute(x, axis, shift_pairs(n, k)) for k in send_order(n)}]
    ppermute x6, waiting for transfers between devices: 8.1 us -> 6.81 us  [gather_rows(): sent = {k: lax.ppermute(x, axis, shift_pairs(n, k)) for k in send_order(n)}]
  transfers between devices with their start and end apart: 26 -> 26, of which waited for: 19 -> 18; matrix products, arithmetic and copies ran while one was open for 10% -> 10% of each run, Pallas kernels for 0% -> 0%
where the time goes in v19:
time: 107 us; the launch traced here: 106 us
  matrix products  38 us (36%)
  waiting for transfers between devices  31.3 us (29%)
  starting transfers between devices  30.1 us (28%)
  other arithmetic  5.54 us (5%)
    dot_general x8, matrix products, block(): jnp.dot(x, lax.dynamic_slice_in_dim(w, j * chunk, chunk, 1), preferred_el...  22.1 us
    ppermute x6, waiting for transfers between devices, scatter_sum(): lax.ppermute(jnp.take(blocks, (idx + k) % n, axis=0), axis, shift_pairs(n...  11 us
    ppermute x7, waiting for transfers between devices, all_sum(): total = total + lax.ppermute(x, axis, shift_pairs(n, k))  10.8 us
    ppermute x7, starting transfers between devices, all_sum(): total = total + lax.ppermute(x, axis, shift_pairs(n, k))  10.2 us
    dot_general x1, matrix products, local(): jnp.einsum('rf,fgc->rgc', by_slot, w_qkv, preferred_element_type=jnp.floa...  6.85 us
    ppermute x6, waiting for transfers between devices, gather_rows(): sent = {k: lax.ppermute(x, axis, shift_pairs(n, k)) for k in send_order(n)}  6.81 us
    ppermute x3, starting transfers between devices, gather_matmul(): sent = {k: lax.ppermute(x, axis, shift_pairs(n, k)) for k in send_order(n)}  5.7 us
    ppermute x6, starting transfers between devices, gather_rows(): sent = {k: lax.ppermute(x, axis, shift_pairs(n, k)) for k in send_order(n)}  5.15 us
  transfers between devices with their start and end apart: 26, of which 18 were waited for; matrix products, arithmetic and copies ran while one was open for 10% of the time, Pallas kernels for 0%

profile of v19, /device:TPU:0, one launch (start us, length us, event | category | flops | bytes accessed | tf_op | source)
XLA Modules:
  0.0 106.3 jit_solution(4477689648316794360)
XLA Ops:
  1.0 5.1 %collective-permute-start.2 = (f32[8]{0:T(128)S(1)}, f32[8]{0:T(128)S(1)}, u32[]{:S(2)}, u32[]{:S(2)}) collective-permute-start(f32[8]{0:T(128)S(1)} %fusion.98), channel_id=1, source_target_pairs={{0,12},{4,0},{8,4},{12,8},{1,13},{5,1},{9,5},{13,9},{2,14},{6,2},{... | collective-permute-start | bytes 104 | tf_op jit(solution)/shard_map/ppermute | solution.py:147
  9.1 1.4 %collective-permute-done.1 = f32[8]{0:T(128)S(1)} collective-permute-done((f32[8]{0:T(128)S(1)}, f32[8]{0:T(128)S(1)}, u32[]{:S(2)}, u32[]{:S(2)}) %collective-permute-start.1) | collective-permute-done | bytes 64 | tf_op jit(solution)/shard_map/ppermute | solution.py:147
  12.4 1.6 %collective-permute-start.4 = (bf16[8,2048]{1,0:T(8,128)(2,1)S(1)}, bf16[8,2048]{1,0:T(8,128)(2,1)S(1)}, u32[]{:S(2)}, u32[]{:S(2)}) collective-permute-start(bf16[8,2048]{1,0:T(8,128)(2,1)S(1)} %fusion.100), channel_id=1, source_target_pairs={{0,2},{1,3},{2,0},{3,1},{4,6},{5,7},{6,4},{7,5},{8,10},{9,11},{10,... | collective-permute-start | bytes 98312 | tf_op jit(solution)/shard_map/ppermute | solution.py:101
  14.2 2.3 %collective-permute-done.4 = bf16[8,2048]{1,0:T(8,128)(2,1)S(1)} collective-permute-done((bf16[8,2048]{1,0:T(8,128)(2,1)S(1)}, bf16[8,2048]{1,0:T(8,128)(2,1)S(1)}, u32[]{:S(2)}, u32[]{:S(2)}) %collective-permute-start.4) | collective-permute-done | bytes 32800 | tf_op jit(solution)/shard_map/ppermute | solution.py:101
  17.3 6.9 %fusion.26 = f32[2,4,8,1280]{3,2,1,0:T(8,128)S(1)} fusion(bf16[2048,2,1280]{2,1,0:T(2,128)(2,1)} %param.22, bf16[8,2048]{1,0:T(8,128)(2,1)S(1)} %collective-permute-done.5, bf16[8,2048]{1,0:T(8,128)(2,1)S(1)} %collective-permute-done.4, bf16[8,2048]{1,0:T(8,128)(2,1)S(1)} %collective-permute-done.3, bf16[8,2048]{1,0:T(8,128)(2,1)S(1)} %fusion.100, ...), kind=kOutput, calls=%fused_computation.26 | convolution fusion | flops 340329472 | bytes 10944640 | tf_op jit(solution)/shard_map/rf,fgc->rgc/dot_general | solution.py:223
  25.9 1.5 %collective-permute-start.7 = (f32[8,2560]{1,0:T(8,128)S(1)}, f32[8,2560]{1,0:T(8,128)S(1)}, u32[]{:S(2)}, u32[]{:S(2)}) collective-permute-start(f32[8,2560]{1,0:T(8,128)S(1)} %get-tuple-element.67), channel_id=1, source_target_pairs={{0,4},{4,8},{8,12},{12,0},{1,5},{5,9},{9,13},{13,1},{2,6},{6,10},{... | collective-permute-start | bytes 245768 | tf_op jit(solution)/shard_map/ppermute | solution.py:117
  28.9 4.2 %collective-permute-done.8 = f32[8,2560]{1,0:T(8,128)S(1)} collective-permute-done((f32[8,2560]{1,0:T(8,128)S(1)}, f32[8,2560]{1,0:T(8,128)S(1)}, u32[]{:S(2)}, u32[]{:S(2)}) %collective-permute-start.8) | collective-permute-done | bytes 81952 | tf_op jit(solution)/shard_map/ppermute | solution.py:117
  34.5 1.3 %collective-permute-start.11 = (bf16[8,2048]{1,0:T(8,128)(2,1)S(1)}, bf16[8,2048]{1,0:T(8,128)(2,1)S(1)}, u32[]{:S(2)}, u32[]{:S(2)}) collective-permute-start(bf16[8,2048]{1,0:T(8,128)(2,1)S(1)} %bitcast.100), channel_id=1, source_target_pairs={{0,12},{4,0},{8,4},{12,8},{1,13},{5,1},{9,5},{13,9},{2,14},{6,2},{... | collective-permute-start | bytes 98312 | tf_op jit(solution)/shard_map/ppermute | solution.py:101
  35.9 1.9 %collective-permute-start.9 = (bf16[8,2048]{1,0:T(8,128)(2,1)S(1)}, bf16[8,2048]{1,0:T(8,128)(2,1)S(1)}, u32[]{:S(2)}, u32[]{:S(2)}) collective-permute-start(bf16[8,2048]{1,0:T(8,128)(2,1)S(1)} %bitcast.102), channel_id=1, source_target_pairs={{0,4},{4,8},{8,12},{12,0},{1,5},{5,9},{9,13},{13,1},{2,6},{6,10},{... | collective-permute-start | bytes 98312 | tf_op jit(solution)/shard_map/ppermute | solution.py:101
  38.6 2.3 %collective-permute-done.10 = bf16[8,2048]{1,0:T(8,128)(2,1)S(1)} collective-permute-done((bf16[8,2048]{1,0:T(8,128)(2,1)S(1)}, bf16[8,2048]{1,0:T(8,128)(2,1)S(1)}, u32[]{:S(2)}, u32[]{:S(2)}) %collective-permute-start.10) | collective-permute-done | bytes 32800 | tf_op jit(solution)/shard_map/ppermute | solution.py:101
  41.6 5.1 %fusion.39 = f32[32,2048]{1,0:T(8,128)S(1)} fusion(bf16[2048,2048]{1,0:T(8,128)(2,1)} %param.23, bf16[8,2048]{1,0:T(8,128)(2,1)S(1)} %collective-permute-done.11, bf16[8,2048]{1,0:T(8,128)(2,1)S(1)} %collective-permute-done.10, bf16[8,2048]{1,0:T(8,128)(2,1)S(1)} %collective-permute-done.9, bf16[8,2048]{1,0:T(8,128)(2,1)S(1)} %bitcast.103, s32[32]{0:T(128)S(1)} %fusion.130), kind=kOutput, calls=%fused_computation.33 | convolution fusion | flops 273220608 | bytes 8781952 | tf_op jit(solution)/shard_map/dot_general | solution.py:231
  46.8 1.3 %collective-permute-done.12 = f32[16,2048]{1,0:T(8,128)S(1)} collective-permute-done((f32[16,2048]{1,0:T(8,128)S(1)}, f32[16,2048]{1,0:T(8,128)S(1)}, u32[]{:S(2)}, u32[]{:S(2)}) %collective-permute-start.12) | collective-permute-done | bytes 131104 | tf_op jit(solution)/shard_map/ppermute | solution.py:117
  49.2 4.6 %collective-permute-done.13 = f32[16,2048]{1,0:T(8,128)S(1)} collective-permute-done((f32[16,2048]{1,0:T(8,128)S(1)}, f32[16,2048]{1,0:T(8,128)S(1)}, u32[]{:S(2)}, u32[]{:S(2)}) %collective-permute-start.13) | collective-permute-done | bytes 131104 | tf_op jit(solution)/shard_map/ppermute | solution.py:147
  54.0 1.2 %collective-permute-done.14 = f32[16,2048]{1,0:T(8,128)S(1)} collective-permute-done((f32[16,2048]{1,0:T(8,128)S(1)}, f32[16,2048]{1,0:T(8,128)S(1)}, u32[]{:S(2)}, u32[]{:S(2)}) %collective-permute-start.14) | collective-permute-done | bytes 131104 | tf_op jit(solution)/shard_map/ppermute | solution.py:139
  55.5 1.2 %collective-permute-start.17 = (f32[32]{0:T(128)S(1)}, f32[32]{0:T(128)S(1)}, u32[]{:S(2)}, u32[]{:S(2)}) collective-permute-start(f32[32]{0:T(128)S(1)} %reduce_sum.62), channel_id=1, source_target_pairs={{0,12},{4,0},{8,4},{12,8},{1,13},{5,1},{9,5},{13,9},{2,14},{6,2},{... | collective-permute-start | bytes 392 | tf_op jit(solution)/shard_map/ppermute | solution.py:147
  57.1 1.4 %collective-permute-start.15 = (f32[32]{0:T(128)S(1)}, f32[32]{0:T(128)S(1)}, u32[]{:S(2)}, u32[]{:S(2)}) collective-permute-start(f32[32]{0:T(128)S(1)} %reduce_sum.62), channel_id=1, source_target_pairs={{0,4},{4,8},{8,12},{12,0},{1,5},{5,9},{9,13},{13,1},{2,6},{6,10},{... | collective-permute-start | bytes 392 | tf_op jit(solution)/shard_map/ppermute | solution.py:147
  59.0 2.1 %collective-permute-done.16 = f32[32]{0:T(128)S(1)} collective-permute-done((f32[32]{0:T(128)S(1)}, f32[32]{0:T(128)S(1)}, u32[]{:S(2)}, u32[]{:S(2)}) %collective-permute-start.16) | collective-permute-done | bytes 160 | tf_op jit(solution)/shard_map/ppermute | solution.py:147
  61.1 1.3 %collective-permute-done.15 = f32[32]{0:T(128)S(1)} collective-permute-done((f32[32]{0:T(128)S(1)}, f32[32]{0:T(128)S(1)}, u32[]{:S(2)}, u32[]{:S(2)}) %collective-permute-start.15) | collective-permute-done | bytes 160 | tf_op jit(solution)/shard_map/ppermute | solution.py:147
  62.5 2.7 %fusion.55 = bf16[32,896]{1,0:T(8,128)(2,1)S(1)} fusion(bf16[32,2048]{1,0:T(8,128)(2,1)S(1)} %multiply_convert_fusion, bf16[2048,3584]{1,0:T(8,128)(2,1)} %param.26, s32[]{:T(128)S(6)} %select_n.218), kind=kOutput, calls=%fused_computation.40 | convolution fusion | flops 117469184 | bytes 3858436 | tf_op jit(solution)/shard_map/dot_general | solution.py:157
  65.3 2.9 %fusion.52 = bf16[32,896]{1,0:T(8,128)(2,1)S(1)} fusion(bf16[32,2048]{1,0:T(8,128)(2,1)S(1)} %multiply_convert_fusion, bf16[2048,3584]{1,0:T(8,128)(2,1)} %param.25, s32[]{:T(128)S(6)} %select_n.218), kind=kOutput, calls=%fused_computation.39 | convolution fusion | flops 117469184 | bytes 3858436 | tf_op jit(solution)/shard_map/dot_general | solution.py:157
  68.1 2.9 %fusion.49 = bf16[32,896]{1,0:T(8,128)(2,1)S(1)} fusion(bf16[32,2048]{1,0:T(8,128)(2,1)S(1)} %multiply_convert_fusion, bf16[2048,3584]{1,0:T(8,128)(2,1)} %param.26, s32[]{:T(128)S(6)} %select_n.217), kind=kOutput, calls=%fused_computation.38 | convolution fusion | flops 117469184 | bytes 3858436 | tf_op jit(solution)/shard_map/dot_general | solution.py:157
  71.0 2.7 %fusion.46 = bf16[32,896]{1,0:T(8,128)(2,1)S(1)} fusion(bf16[32,2048]{1,0:T(8,128)(2,1)S(1)} %multiply_convert_fusion, bf16[2048,3584]{1,0:T(8,128)(2,1)} %param.25, s32[]{:T(128)S(6)} %select_n.217), kind=kOutput, calls=%fused_computation.37 | convolution fusion | flops 117469184 | bytes 3858436 | tf_op jit(solution)/shard_map/dot_general | solution.py:157
  73.7 2.9 %fusion.43 = bf16[32,896]{1,0:T(8,128)(2,1)S(1)} fusion(bf16[32,2048]{1,0:T(8,128)(2,1)S(1)} %multiply_convert_fusion, bf16[2048,3584]{1,0:T(8,128)(2,1)} %param.26, s32[]{:T(128)S(6)} %select_n.216), kind=kOutput, calls=%fused_computation.36 | convolution fusion | flops 117469184 | bytes 3858436 | tf_op jit(solution)/shard_map/dot_general | solution.py:157
  76.6 2.7 %fusion.40 = bf16[32,896]{1,0:T(8,128)(2,1)S(1)} fusion(bf16[32,2048]{1,0:T(8,128)(2,1)S(1)} %multiply_convert_fusion, bf16[2048,3584]{1,0:T(8,128)(2,1)} %param.25, s32[]{:T(128)S(6)} %select_n.216), kind=kOutput, calls=%fused_computation.35 | convolution fusion | flops 117469184 | bytes 3858436 | tf_op jit(solution)/shard_map/dot_general | solution.py:157
  81.0 3.0 %collective-permute-start.20 = (bf16[32,1792]{1,0:T(8,128)(2,1)S(1)}, bf16[32,1792]{1,0:T(8,128)(2,1)S(1)}, u32[]{:S(2)}, u32[]{:S(2)}) collective-permute-start(bf16[32,1792]{1,0:T(8,128)(2,1)S(1)} %pad_maximum_fusion.3), channel_id=1, source_target_pairs={{0,12},{4,0},{8,4},{12,8},{1,13},{5,1},{9,5},{13,9},{2,14},{6,2},{... | collective-permute-start | bytes 344072 | tf_op jit(solution)/shard_map/ppermute | solution.py:171
  84.0 2.7 %fusion.61 = bf16[32,896]{1,0:T(8,128)(2,1)S(1)} fusion(bf16[32,2048]{1,0:T(8,128)(2,1)S(1)} %multiply_convert_fusion, bf16[2048,3584]{1,0:T(8,128)(2,1)} %param.26, s32[]{:T(128)S(6)} %select_n.219), kind=kOutput, calls=%fused_computation.42 | convolution fusion | flops 117469184 | bytes 3858436 | tf_op jit(solution)/shard_map/dot_general | solution.py:157
  86.7 2.7 %fusion.58 = bf16[32,896]{1,0:T(8,128)(2,1)S(1)} fusion(bf16[32,2048]{1,0:T(8,128)(2,1)S(1)} %multiply_convert_fusion, bf16[2048,3584]{1,0:T(8,128)(2,1)} %param.25, s32[]{:T(128)S(6)} %select_n.219), kind=kOutput, calls=%fused_computation.41 | convolution fusion | flops 117469184 | bytes 3858436 | tf_op jit(solution)/shard_map/dot_general | solution.py:157
  89.6 1.9 %collective-permute-start.23 = (bf16[32,896]{1,0:T(8,128)(2,1)S(1)}, bf16[32,896]{1,0:T(8,128)(2,1)S(1)}, u32[]{:S(2)}, u32[]{:S(2)}) collective-permute-start(bf16[32,896]{1,0:T(8,128)(2,1)S(1)} %fusion.94), channel_id=1, source_target_pairs={{0,8},{4,12},{8,0},{12,4},{1,9},{5,13},{9,1},{13,5},{2,10},{6,14},... | collective-permute-start | bytes 172040 | tf_op jit(solution)/shard_map/ppermute | solution.py:183
  91.7 3.6 %collective-permute-start.21 = (bf16[32,896]{1,0:T(8,128)(2,1)S(1)}, bf16[32,896]{1,0:T(8,128)(2,1)S(1)}, u32[]{:S(2)}, u32[]{:S(2)}) collective-permute-start(bf16[32,896]{1,0:T(8,128)(2,1)S(1)} %fusion.94), channel_id=1, source_target_pairs={{0,12},{4,0},{8,4},{12,8},{1,13},{5,1},{9,5},{13,9},{2,14},{6,2},{... | collective-permute-start | bytes 172040 | tf_op jit(solution)/shard_map/ppermute | solution.py:183
  96.1 1.5 %collective-permute-done.22 = bf16[32,896]{1,0:T(8,128)(2,1)S(1)} collective-permute-done((bf16[32,896]{1,0:T(8,128)(2,1)S(1)}, bf16[32,896]{1,0:T(8,128)(2,1)S(1)}, u32[]{:S(2)}, u32[]{:S(2)}) %collective-permute-start.22) | collective-permute-done | bytes 57376 | tf_op jit(solution)/shard_map/ppermute | solution.py:183
  100.0 1.3 %collective-permute-done.24 = f32[2,8,2048]{2,1,0:T(8,128)S(1)} collective-permute-done((f32[2,8,2048]{2,1,0:T(8,128)S(1)}, f32[2,8,2048]{2,1,0:T(8,128)S(1)}, u32[]{:S(2)}, u32[]{:S(2)}) %collective-permute-start.24) | collective-permute-done | bytes 131104 | tf_op jit(solution)/shard_map/ppermute | solution.py:117
  102.3 3.4 %collective-permute-done.25 = f32[8,2048]{1,0:T(8,128)S(1)} collective-permute-done((f32[8,2048]{1,0:T(8,128)S(1)}, f32[8,2048]{1,0:T(8,128)S(1)}, u32[]{:S(2)}, u32[]{:S(2)}) %collective-permute-start.25) | collective-permute-done | bytes 65568 | tf_op jit(solution)/shard_map/ppermute | solution.py:117
  (98 shorter events, 22.0 us)
Async XLA Ops:
  0.0 27.5 %copy-start = (bf16[8,256,2,2,128]{4,3,2,1,0:T(2,128)(2,1)S(1)}, bf16[8,256,2,2,128]{4,3,2,1,0:T(2,128)(2,1)}, u32[]{:S(2)}) copy-start(bf16[8,256,2,2,128]{4,3,2,1,0:T(2,128)(2,1)} %param.28) | copy-start | bytes 6291460
  1.0 8.1 %collective-permute-start.2 = (f32[8]{0:T(128)S(1)}, f32[8]{0:T(128)S(1)}, u32[]{:S(2)}, u32[]{:S(2)}) collective-permute-start(f32[8]{0:T(128)S(1)} %fusion.98), channel_id=1, source_target_pairs={{0,12},{4,0},{8,4},{12,8},{1,13},{5,1},{9,5},{13,9},{2,14},{6,2},{... | collective-permute-start | bytes 104 | tf_op jit(solution)/shard_map/ppermute | solution.py:147
  6.1 4.4 %collective-permute-start.1 = (f32[8]{0:T(128)S(1)}, f32[8]{0:T(128)S(1)}, u32[]{:S(2)}, u32[]{:S(2)}) collective-permute-start(f32[8]{0:T(128)S(1)} %fusion.98), channel_id=1, source_target_pairs={{0,8},{4,12},{8,0},{12,4},{1,9},{5,13},{9,1},{13,5},{2,10},{6,14},... | collective-permute-start | bytes 104 | tf_op jit(solution)/shard_map/ppermute | solution.py:147
  6.1 5.3 %collective-permute-start = (f32[8]{0:T(128)S(1)}, f32[8]{0:T(128)S(1)}, u32[]{:S(2)}, u32[]{:S(2)}) collective-permute-start(f32[8]{0:T(128)S(1)} %fusion.98), channel_id=1, source_target_pairs={{0,4},{4,8},{8,12},{12,0},{1,5},{5,9},{9,13},{13,1},{2,6},{6,10},{... | collective-permute-start | bytes 104 | tf_op jit(solution)/shard_map/ppermute | solution.py:147
  12.3 1.9 %collective-permute-start.5 = (bf16[8,2048]{1,0:T(8,128)(2,1)S(1)}, bf16[8,2048]{1,0:T(8,128)(2,1)S(1)}, u32[]{:S(2)}, u32[]{:S(2)}) collective-permute-start(bf16[8,2048]{1,0:T(8,128)(2,1)S(1)} %fusion.100), channel_id=1, source_target_pairs={{0,3},{1,0},{2,1},{3,2},{4,7},{5,4},{6,5},{7,6},{8,11},{9,8},{10,9... | collective-permute-start | bytes 98312 | tf_op jit(solution)/shard_map/ppermute | solution.py:101
  12.4 4.1 %collective-permute-start.4 = (bf16[8,2048]{1,0:T(8,128)(2,1)S(1)}, bf16[8,2048]{1,0:T(8,128)(2,1)S(1)}, u32[]{:S(2)}, u32[]{:S(2)}) collective-permute-start(bf16[8,2048]{1,0:T(8,128)(2,1)S(1)} %fusion.100), channel_id=1, source_target_pairs={{0,2},{1,3},{2,0},{3,1},{4,6},{5,7},{6,4},{7,5},{8,10},{9,11},{10,... | collective-permute-start | bytes 98312 | tf_op jit(solution)/shard_map/ppermute | solution.py:101
  13.9 3.3 %collective-permute-start.3 = (bf16[8,2048]{1,0:T(8,128)(2,1)S(1)}, bf16[8,2048]{1,0:T(8,128)(2,1)S(1)}, u32[]{:S(2)}, u32[]{:S(2)}) collective-permute-start(bf16[8,2048]{1,0:T(8,128)(2,1)S(1)} %fusion.100), channel_id=1, source_target_pairs={{0,1},{1,2},{2,3},{3,0},{4,5},{5,6},{6,7},{7,4},{8,9},{9,10},{10,1... | collective-permute-start | bytes 98312 | tf_op jit(solution)/shard_map/ppermute | solution.py:101
  24.2 4.6 %collective-permute-start.6 = (f32[8,2560]{1,0:T(8,128)S(1)}, f32[8,2560]{1,0:T(8,128)S(1)}, u32[]{:S(2)}, u32[]{:S(2)}) collective-permute-start(f32[8,2560]{1,0:T(8,128)S(1)} %get-tuple-element.65), channel_id=1, source_target_pairs={{0,12},{4,0},{8,4},{12,8},{1,13},{5,1},{9,5},{13,9},{2,14},{6,2},{... | collective-permute-start | bytes 245768 | tf_op jit(solution)/shard_map/ppermute | solution.py:117
  24.8 8.2 %collective-permute-start.8 = (f32[8,2560]{1,0:T(8,128)S(1)}, f32[8,2560]{1,0:T(8,128)S(1)}, u32[]{:S(2)}, u32[]{:S(2)}) collective-permute-start(f32[8,2560]{1,0:T(8,128)S(1)} %get-tuple-element.66), channel_id=1, source_target_pairs={{0,8},{4,12},{8,0},{12,4},{1,9},{5,13},{9,1},{13,5},{2,10},{6,14},... | collective-permute-start | bytes 245768 | tf_op jit(solution)/shard_map/ppermute | solution.py:117
  25.9 7.1 %collective-permute-start.7 = (f32[8,2560]{1,0:T(8,128)S(1)}, f32[8,2560]{1,0:T(8,128)S(1)}, u32[]{:S(2)}, u32[]{:S(2)}) collective-permute-start(f32[8,2560]{1,0:T(8,128)S(1)} %get-tuple-element.67), channel_id=1, source_target_pairs={{0,4},{4,8},{8,12},{12,0},{1,5},{5,9},{9,13},{13,1},{2,6},{6,10},{... | collective-permute-start | bytes 245768 | tf_op jit(solution)/shard_map/ppermute | solution.py:117
  27.5 19.2 %copy-start.1 = (bf16[8,2048]{1,0:T(8,128)(2,1)S(1)}, bf16[8,2048]{1,0:T(8,128)(2,1)}, u32[]{:S(2)}) copy-start(bf16[8,2048]{1,0:T(8,128)(2,1)} %param.20) | copy-start | bytes 98308
  28.0 34.4 %copy-start.2 = (f32[2048]{0:T(1024)S(1)}, f32[2048]{0:T(1024)}, u32[]{:S(2)}) copy-start(f32[2048]{0:T(1024)} %param.24) | copy-start | bytes 24580
  34.5 4.2 %collective-permute-start.11 = (bf16[8,2048]{1,0:T(8,128)(2,1)S(1)}, bf16[8,2048]{1,0:T(8,128)(2,1)S(1)}, u32[]{:S(2)}, u32[]{:S(2)}) collective-permute-start(bf16[8,2048]{1,0:T(8,128)(2,1)S(1)} %bitcast.100), channel_id=1, source_target_pairs={{0,12},{4,0},{8,4},{12,8},{1,13},{5,1},{9,5},{13,9},{2,14},{6,2},{... | collective-permute-start | bytes 98312 | tf_op jit(solution)/shard_map/ppermute | solution.py:101
  35.8 5.2 %collective-permute-start.10 = (bf16[8,2048]{1,0:T(8,128)(2,1)S(1)}, bf16[8,2048]{1,0:T(8,128)(2,1)S(1)}, u32[]{:S(2)}, u32[]{:S(2)}) collective-permute-start(bf16[8,2048]{1,0:T(8,128)(2,1)S(1)} %bitcast.101), channel_id=1, source_target_pairs={{0,8},{4,12},{8,0},{12,4},{1,9},{5,13},{9,1},{13,5},{2,10},{6,14},... | collective-permute-start | bytes 98312 | tf_op jit(solution)/shard_map/ppermute | solution.py:101
  35.9 5.7 %collective-permute-start.9 = (bf16[8,2048]{1,0:T(8,128)(2,1)S(1)}, bf16[8,2048]{1,0:T(8,128)(2,1)S(1)}, u32[]{:S(2)}, u32[]{:S(2)}) collective-permute-start(bf16[8,2048]{1,0:T(8,128)(2,1)S(1)} %bitcast.102), channel_id=1, source_target_pairs={{0,4},{4,8},{8,12},{12,0},{1,5},{5,9},{9,13},{13,1},{2,6},{6,10},{... | collective-permute-start | bytes 98312 | tf_op jit(solution)/shard_map/ppermute | solution.py:101
  46.8 1.4 %collective-permute-start.12 = (f32[16,2048]{1,0:T(8,128)S(1)}, f32[16,2048]{1,0:T(8,128)S(1)}, u32[]{:S(2)}, u32[]{:S(2)}) collective-permute-start(f32[16,2048]{1,0:T(8,128)S(1)} %select_bitcast_fusion.1), channel_id=1, source_target_pairs={{0,1},{1,0},{2,3},{3,2},{4,5},{5,4},{6,7},{7,6},{8,9},{9,8},{10,11... | collective-permute-start | bytes 393224 | tf_op jit(solution)/shard_map/ppermute | solution.py:117
  48.2 5.6 %collective-permute-start.13 = (f32[16,2048]{1,0:T(8,128)S(1)}, f32[16,2048]{1,0:T(8,128)S(1)}, u32[]{:S(2)}, u32[]{:S(2)}) collective-permute-start(f32[16,2048]{1,0:T(8,128)S(1)} %bitcast_add_fusion.1), channel_id=1, source_target_pairs={{0,2},{2,0},{1,3},{3,1},{4,6},{6,4},{5,7},{7,5},{8,10},{10,8},{9,1... | collective-permute-start | bytes 393224 | tf_op jit(solution)/shard_map/ppermute | solution.py:147
  53.8 1.4 %collective-permute-start.14 = (f32[16,2048]{1,0:T(8,128)S(1)}, f32[16,2048]{1,0:T(8,128)S(1)}, u32[]{:S(2)}, u32[]{:S(2)}) collective-permute-start(f32[16,2048]{1,0:T(8,128)S(1)} %add.289), channel_id=1, source_target_pairs={{0,1},{1,0},{2,3},{3,2},{4,5},{5,4},{6,7},{7,6},{8,9},{9,8},{10,11... | collective-permute-start | bytes 393224 | tf_op jit(solution)/shard_map/ppermute | solution.py:139
  55.5 3.5 %collective-permute-start.17 = (f32[32]{0:T(128)S(1)}, f32[32]{0:T(128)S(1)}, u32[]{:S(2)}, u32[]{:S(2)}) collective-permute-start(f32[32]{0:T(128)S(1)} %reduce_sum.62), channel_id=1, source_target_pairs={{0,12},{4,0},{8,4},{12,8},{1,13},{5,1},{9,5},{13,9},{2,14},{6,2},{... | collective-permute-start | bytes 392 | tf_op jit(solution)/shard_map/ppermute | solution.py:147
  56.7 4.4 %collective-permute-start.16 = (f32[32]{0:T(128)S(1)}, f32[32]{0:T(128)S(1)}, u32[]{:S(2)}, u32[]{:S(2)}) collective-permute-start(f32[32]{0:T(128)S(1)} %reduce_sum.62), channel_id=1, source_target_pairs={{0,8},{4,12},{8,0},{12,4},{1,9},{5,13},{9,1},{13,5},{2,10},{6,14},... | collective-permute-start | bytes 392 | tf_op jit(solution)/shard_map/ppermute | solution.py:147
  57.1 5.3 %collective-permute-start.15 = (f32[32]{0:T(128)S(1)}, f32[32]{0:T(128)S(1)}, u32[]{:S(2)}, u32[]{:S(2)}) collective-permute-start(f32[32]{0:T(128)S(1)} %reduce_sum.62), channel_id=1, source_target_pairs={{0,4},{4,8},{8,12},{12,0},{1,5},{5,9},{9,13},{13,1},{2,6},{6,10},{... | collective-permute-start | bytes 392 | tf_op jit(solution)/shard_map/ppermute | solution.py:147
  65.2 30.1 %slice-start = ((s8[14680064]{0:T(1024)(128)(4,1)}), s8[4194304]{0:T(1024)(128)(4,1)S(1)}, s32[]{:S(2)}) async-start(s8[14680064]{0:T(1024)(128)(4,1)} %bitcast.85), calls=%async_computation | async-start | bytes 8388608
  68.1 27.2 %slice-start.1 = ((s8[14680064]{0:T(1024)(128)(4,1)}), s8[4194304]{0:T(1024)(128)(4,1)S(1)}, s32[]{:S(2)}) async-start(s8[14680064]{0:T(1024)(128)(4,1)} %bitcast.85), calls=%async_computation.1 | async-start | bytes 8388608
  73.7 21.6 %slice-start.2 = ((s8[14680064]{0:T(1024)(128)(4,1)}), s8[4194304]{0:T(1024)(128)(4,1)S(1)}, s32[]{:S(2)}) async-start(s8[14680064]{0:T(1024)(128)(4,1)} %bitcast.85), calls=%async_computation.2 | async-start | bytes 8388608
  79.4 10.1 %collective-permute-start.18 = (bf16[32,1792]{1,0:T(8,128)(2,1)S(1)}, bf16[32,1792]{1,0:T(8,128)(2,1)S(1)}, u32[]{:S(2)}, u32[]{:S(2)}) collective-permute-start(bf16[32,1792]{1,0:T(8,128)(2,1)S(1)} %get-tuple-element.18), channel_id=1, source_target_pairs={{0,8},{4,12},{8,0},{12,4},{1,9},{5,13},{9,1},{13,5},{2,10},{6,14},... | collective-permute-start | bytes 344072 | tf_op jit(solution)/shard_map/ppermute | solution.py:171
  80.2 9.3 %collective-permute-start.19 = (bf16[32,1792]{1,0:T(8,128)(2,1)S(1)}, bf16[32,1792]{1,0:T(8,128)(2,1)S(1)}, u32[]{:S(2)}, u32[]{:S(2)}) collective-permute-start(bf16[32,1792]{1,0:T(8,128)(2,1)S(1)} %get-tuple-element.19), channel_id=1, source_target_pairs={{0,4},{4,8},{8,12},{12,0},{1,5},{5,9},{9,13},{13,1},{2,6},{6,10},{... | collective-permute-start | bytes 344072 | tf_op jit(solution)/shard_map/ppermute | solution.py:171
  81.0 8.5 %collective-permute-start.20 = (bf16[32,1792]{1,0:T(8,128)(2,1)S(1)}, bf16[32,1792]{1,0:T(8,128)(2,1)S(1)}, u32[]{:S(2)}, u32[]{:S(2)}) collective-permute-start(bf16[32,1792]{1,0:T(8,128)(2,1)S(1)} %pad_maximum_fusion.3), channel_id=1, source_target_pairs={{0,12},{4,0},{8,4},{12,8},{1,13},{5,1},{9,5},{13,9},{2,14},{6,2},{... | collective-permute-start | bytes 344072 | tf_op jit(solution)/shard_map/ppermute | solution.py:171
  89.6 8.7 %collective-permute-start.23 = (bf16[32,896]{1,0:T(8,128)(2,1)S(1)}, bf16[32,896]{1,0:T(8,128)(2,1)S(1)}, u32[]{:S(2)}, u32[]{:S(2)}) collective-permute-start(bf16[32,896]{1,0:T(8,128)(2,1)S(1)} %fusion.94), channel_id=1, source_target_pairs={{0,8},{4,12},{8,0},{12,4},{1,9},{5,13},{9,1},{13,5},{2,10},{6,14},... | collective-permute-start | bytes 172040 | tf_op jit(solution)/shard_map/ppermute | solution.py:183
  91.5 6.1 %collective-permute-start.22 = (bf16[32,896]{1,0:T(8,128)(2,1)S(1)}, bf16[32,896]{1,0:T(8,128)(2,1)S(1)}, u32[]{:S(2)}, u32[]{:S(2)}) collective-permute-start(bf16[32,896]{1,0:T(8,128)(2,1)S(1)} %fusion.94), channel_id=1, source_target_pairs={{0,4},{4,8},{8,12},{12,0},{1,5},{5,9},{9,13},{13,1},{2,6},{6,10},{... | collective-permute-start | bytes 172040 | tf_op jit(solution)/shard_map/ppermute | solution.py:183
  91.7 7.3 %collective-permute-start.21 = (bf16[32,896]{1,0:T(8,128)(2,1)S(1)}, bf16[32,896]{1,0:T(8,128)(2,1)S(1)}, u32[]{:S(2)}, u32[]{:S(2)}) collective-permute-start(bf16[32,896]{1,0:T(8,128)(2,1)S(1)} %fusion.94), channel_id=1, source_target_pairs={{0,12},{4,0},{8,4},{12,8},{1,13},{5,1},{9,5},{13,9},{2,14},{6,2},{... | collective-permute-start | bytes 172040 | tf_op jit(solution)/shard_map/ppermute | solution.py:183
  99.9 1.4 %collective-permute-start.24 = (f32[2,8,2048]{2,1,0:T(8,128)S(1)}, f32[2,8,2048]{2,1,0:T(8,128)S(1)}, u32[]{:S(2)}, u32[]{:S(2)}) collective-permute-start(f32[2,8,2048]{2,1,0:T(8,128)S(1)} %select_bitcast_fusion), channel_id=1, source_target_pairs={{0,1},{1,0},{2,3},{3,2},{4,5},{5,4},{6,7},{7,6},{8,9},{9,8},{10,11... | collective-permute-start | bytes 393224 | tf_op jit(solution)/shard_map/ppermute | solution.py:117
  101.4 4.3 %collective-permute-start.25 = (f32[8,2048]{1,0:T(8,128)S(1)}, f32[8,2048]{1,0:T(8,128)S(1)}, u32[]{:S(2)}, u32[]{:S(2)}) collective-permute-start(f32[8,2048]{1,0:T(8,128)S(1)} %select_bitcast_fusion.7), channel_id=1, source_target_pairs={{0,2},{2,0},{1,3},{3,1},{4,6},{6,4},{5,7},{7,5},{8,10},{10,8},{9,1... | collective-permute-start | bytes 196616 | tf_op jit(solution)/shard_map/ppermute | solution.py:117
  (1 other events, 15.9 us)

commit v20 on v19

--- a/solution.py
+++ b/solution.py
@@ -166,9 +166,10 @@
     order = send_order(n)
     pieces = [block((idx + k) % n) for k in order]
     pieces, x = lax.optimization_barrier((pieces, x))
+    sent = {k: lax.ppermute(piece, axis, shift_pairs(n, k)) for k, piece in zip(order, pieces)}
     total = None
-    for k, piece in zip(order, pieces):
-        got = lax.ppermute(piece, axis, shift_pairs(n, k)).astype(jnp.float32)
+    for k in reversed(order):
+        got = sent[k].astype(jnp.float32)
         total = got if total is None else total + got
     own = block(idx).astype(jnp.float32)
     return own if total is None else own + total

time: 107 us -> 106 us (level)
  starting transfers between devices: 30.1 us -> 26.5 us
  waiting for transfers between devices: 31.3 us -> 34.4 us
    ppermute x3, waiting for transfers between devices: 0.01 us -> 3.05 us  [scatter_matmul(): lax.ppermute(piece, axis, shift_pairs(n, k))]
    ppermute x3, starting transfers between devices: 4.62 us -> 2.81 us  [scatter_matmul(): lax.ppermute(piece, axis, shift_pairs(n, k))]
    ppermute x3, starting transfers between devices: 5.7 us -> 3.95 us  [gather_matmul(): sent = {k: lax.ppermute(x, axis, shift_pairs(n, k)) for k in send_order(n)}]
  transfers between devices with their start and end apart: 26 -> 26, of which waited for: 18 -> 20; matrix products, arithmetic and copies ran while one was open for 10% -> 10% of each run, Pallas kernels for 0% -> 0%
where the time goes in v20:
time: 106 us
  matrix products  38 us (36%)
  waiting for transfers between devices  34.4 us (32%)
  starting transfers between devices  26.5 us (25%)
  other arithmetic  5.54 us (5%)
    dot_general x8, matrix products, block(): jnp.dot(x, lax.dynamic_slice_in_dim(w, j * chunk, chunk, 1), preferred_el...  22.1 us
    ppermute x6, waiting for transfers between devices, scatter_sum(): lax.ppermute(jnp.take(blocks, (idx + k) % n, axis=0), axis, shift_pairs(n...  11 us
    ppermute x7, waiting for transfers between devices, all_sum(): total = total + lax.ppermute(x, axis, shift_pairs(n, k))  10.8 us
    ppermute x7, starting transfers between devices, all_sum(): total = total + lax.ppermute(x, axis, shift_pairs(n, k))  10.2 us
    dot_general x1, matrix products, local(): jnp.einsum('rf,fgc->rgc', by_slot, w_qkv, preferred_element_type=jnp.floa...  6.85 us
    ppermute x6, waiting for transfers between devices, gather_rows(): sent = {k: lax.ppermute(x, axis, shift_pairs(n, k)) for k in send_order(n)}  6.81 us
    ppermute x6, starting transfers between devices, gather_rows(): sent = {k: lax.ppermute(x, axis, shift_pairs(n, k)) for k in send_order(n)}  5.15 us
    dot_general x1, matrix products, local(): out_part = jnp.dot(by_row, w_out, preferred_element_type=jnp.float32)  5.09 us
  transfers between devices with their start and end apart: 26, of which 20 were waited for; matrix products, arithmetic and copies ran while one was open for 10% of the time, Pallas kernels for 0%

profile of v20, /device:TPU:0, one launch (start us, length us, event | category | flops | bytes accessed | tf_op | source)
XLA Modules:
  0.0 105.8 jit_solution(5760788242180117371)
XLA Ops:
  1.0 5.1 %collective-permute-start.2 = (f32[8]{0:T(128)S(1)}, f32[8]{0:T(128)S(1)}, u32[]{:S(2)}, u32[]{:S(2)}) collective-permute-start(f32[8]{0:T(128)S(1)} %fusion.98), channel_id=1, source_target_pairs={{0,12},{4,0},{8,4},{12,8},{1,13},{5,1},{9,5},{13,9},{2,14},{6,2},{... | collective-permute-start | bytes 104 | tf_op jit(solution)/shard_map/ppermute | solution.py:147
  9.1 1.4 %collective-permute-done.1 = f32[8]{0:T(128)S(1)} collective-permute-done((f32[8]{0:T(128)S(1)}, f32[8]{0:T(128)S(1)}, u32[]{:S(2)}, u32[]{:S(2)}) %collective-permute-start.1) | collective-permute-done | bytes 64 | tf_op jit(solution)/shard_map/ppermute | solution.py:147
  12.4 1.6 %collective-permute-start.4 = (bf16[8,2048]{1,0:T(8,128)(2,1)S(1)}, bf16[8,2048]{1,0:T(8,128)(2,1)S(1)}, u32[]{:S(2)}, u32[]{:S(2)}) collective-permute-start(bf16[8,2048]{1,0:T(8,128)(2,1)S(1)} %fusion.100), channel_id=1, source_target_pairs={{0,2},{1,3},{2,0},{3,1},{4,6},{5,7},{6,4},{7,5},{8,10},{9,11},{10,... | collective-permute-start | bytes 98312 | tf_op jit(solution)/shard_map/ppermute | solution.py:101
  14.2 2.3 %collective-permute-done.4 = bf16[8,2048]{1,0:T(8,128)(2,1)S(1)} collective-permute-done((bf16[8,2048]{1,0:T(8,128)(2,1)S(1)}, bf16[8,2048]{1,0:T(8,128)(2,1)S(1)}, u32[]{:S(2)}, u32[]{:S(2)}) %collective-permute-start.4) | collective-permute-done | bytes 32800 | tf_op jit(solution)/shard_map/ppermute | solution.py:101
  17.3 6.9 %fusion.26 = f32[2,4,8,1280]{3,2,1,0:T(8,128)S(1)} fusion(bf16[2048,2,1280]{2,1,0:T(2,128)(2,1)} %param.22, bf16[8,2048]{1,0:T(8,128)(2,1)S(1)} %collective-permute-done.5, bf16[8,2048]{1,0:T(8,128)(2,1)S(1)} %collective-permute-done.4, bf16[8,2048]{1,0:T(8,128)(2,1)S(1)} %collective-permute-done.3, bf16[8,2048]{1,0:T(8,128)(2,1)S(1)} %fusion.100, ...), kind=kOutput, calls=%fused_computation.26 | convolution fusion | flops 340329472 | bytes 10944640 | tf_op jit(solution)/shard_map/rf,fgc->rgc/dot_general | solution.py:224
  25.9 1.5 %collective-permute-start.7 = (f32[8,2560]{1,0:T(8,128)S(1)}, f32[8,2560]{1,0:T(8,128)S(1)}, u32[]{:S(2)}, u32[]{:S(2)}) collective-permute-start(f32[8,2560]{1,0:T(8,128)S(1)} %get-tuple-element.67), channel_id=1, source_target_pairs={{0,4},{4,8},{8,12},{12,0},{1,5},{5,9},{9,13},{13,1},{2,6},{6,10},{... | collective-permute-start | bytes 245768 | tf_op jit(solution)/shard_map/ppermute | solution.py:117
  28.9 4.2 %collective-permute-done.8 = f32[8,2560]{1,0:T(8,128)S(1)} collective-permute-done((f32[8,2560]{1,0:T(8,128)S(1)}, f32[8,2560]{1,0:T(8,128)S(1)}, u32[]{:S(2)}, u32[]{:S(2)}) %collective-permute-start.8) | collective-permute-done | bytes 81952 | tf_op jit(solution)/shard_map/ppermute | solution.py:117
  34.5 1.3 %collective-permute-start.11 = (bf16[8,2048]{1,0:T(8,128)(2,1)S(1)}, bf16[8,2048]{1,0:T(8,128)(2,1)S(1)}, u32[]{:S(2)}, u32[]{:S(2)}) collective-permute-start(bf16[8,2048]{1,0:T(8,128)(2,1)S(1)} %bitcast.100), channel_id=1, source_target_pairs={{0,12},{4,0},{8,4},{12,8},{1,13},{5,1},{9,5},{13,9},{2,14},{6,2},{... | collective-permute-start | bytes 98312 | tf_op jit(solution)/shard_map/ppermute | solution.py:101
  35.9 1.9 %collective-permute-start.9 = (bf16[8,2048]{1,0:T(8,128)(2,1)S(1)}, bf16[8,2048]{1,0:T(8,128)(2,1)S(1)}, u32[]{:S(2)}, u32[]{:S(2)}) collective-permute-start(bf16[8,2048]{1,0:T(8,128)(2,1)S(1)} %bitcast.102), channel_id=1, source_target_pairs={{0,4},{4,8},{8,12},{12,0},{1,5},{5,9},{9,13},{13,1},{2,6},{6,10},{... | collective-permute-start | bytes 98312 | tf_op jit(solution)/shard_map/ppermute | solution.py:101
  38.6 2.3 %collective-permute-done.10 = bf16[8,2048]{1,0:T(8,128)(2,1)S(1)} collective-permute-done((bf16[8,2048]{1,0:T(8,128)(2,1)S(1)}, bf16[8,2048]{1,0:T(8,128)(2,1)S(1)}, u32[]{:S(2)}, u32[]{:S(2)}) %collective-permute-start.10) | collective-permute-done | bytes 32800 | tf_op jit(solution)/shard_map/ppermute | solution.py:101
  41.6 5.1 %fusion.39 = f32[32,2048]{1,0:T(8,128)S(1)} fusion(bf16[2048,2048]{1,0:T(8,128)(2,1)} %param.23, bf16[8,2048]{1,0:T(8,128)(2,1)S(1)} %collective-permute-done.11, bf16[8,2048]{1,0:T(8,128)(2,1)S(1)} %collective-permute-done.10, bf16[8,2048]{1,0:T(8,128)(2,1)S(1)} %collective-permute-done.9, bf16[8,2048]{1,0:T(8,128)(2,1)S(1)} %bitcast.103, s32[32]{0:T(128)S(1)} %fusion.130), kind=kOutput, calls=%fused_computation.33 | convolution fusion | flops 273220608 | bytes 8781952 | tf_op jit(solution)/shard_map/dot_general | solution.py:232
  46.8 1.3 %collective-permute-done.12 = f32[16,2048]{1,0:T(8,128)S(1)} collective-permute-done((f32[16,2048]{1,0:T(8,128)S(1)}, f32[16,2048]{1,0:T(8,128)S(1)}, u32[]{:S(2)}, u32[]{:S(2)}) %collective-permute-start.12) | collective-permute-done | bytes 131104 | tf_op jit(solution)/shard_map/ppermute | solution.py:117
  49.2 4.6 %collective-permute-done.13 = f32[16,2048]{1,0:T(8,128)S(1)} collective-permute-done((f32[16,2048]{1,0:T(8,128)S(1)}, f32[16,2048]{1,0:T(8,128)S(1)}, u32[]{:S(2)}, u32[]{:S(2)}) %collective-permute-start.13) | collective-permute-done | bytes 131104 | tf_op jit(solution)/shard_map/ppermute | solution.py:147
  54.0 1.2 %collective-permute-done.14 = f32[16,2048]{1,0:T(8,128)S(1)} collective-permute-done((f32[16,2048]{1,0:T(8,128)S(1)}, f32[16,2048]{1,0:T(8,128)S(1)}, u32[]{:S(2)}, u32[]{:S(2)}) %collective-permute-start.14) | collective-permute-done | bytes 131104 | tf_op jit(solution)/shard_map/ppermute | solution.py:139
  55.5 1.2 %collective-permute-start.17 = (f32[32]{0:T(128)S(1)}, f32[32]{0:T(128)S(1)}, u32[]{:S(2)}, u32[]{:S(2)}) collective-permute-start(f32[32]{0:T(128)S(1)} %reduce_sum.62), channel_id=1, source_target_pairs={{0,12},{4,0},{8,4},{12,8},{1,13},{5,1},{9,5},{13,9},{2,14},{6,2},{... | collective-permute-start | bytes 392 | tf_op jit(solution)/shard_map/ppermute | solution.py:147
  57.1 1.4 %collective-permute-start.15 = (f32[32]{0:T(128)S(1)}, f32[32]{0:T(128)S(1)}, u32[]{:S(2)}, u32[]{:S(2)}) collective-permute-start(f32[32]{0:T(128)S(1)} %reduce_sum.62), channel_id=1, source_target_pairs={{0,4},{4,8},{8,12},{12,0},{1,5},{5,9},{9,13},{13,1},{2,6},{6,10},{... | collective-permute-start | bytes 392 | tf_op jit(solution)/shard_map/ppermute | solution.py:147
  59.0 2.1 %collective-permute-done.16 = f32[32]{0:T(128)S(1)} collective-permute-done((f32[32]{0:T(128)S(1)}, f32[32]{0:T(128)S(1)}, u32[]{:S(2)}, u32[]{:S(2)}) %collective-permute-start.16) | collective-permute-done | bytes 160 | tf_op jit(solution)/shard_map/ppermute | solution.py:147
  61.1 1.3 %collective-permute-done.15 = f32[32]{0:T(128)S(1)} collective-permute-done((f32[32]{0:T(128)S(1)}, f32[32]{0:T(128)S(1)}, u32[]{:S(2)}, u32[]{:S(2)}) %collective-permute-start.15) | collective-permute-done | bytes 160 | tf_op jit(solution)/shard_map/ppermute | solution.py:147
  62.5 2.7 %fusion.55 = bf16[32,896]{1,0:T(8,128)(2,1)S(1)} fusion(bf16[32,2048]{1,0:T(8,128)(2,1)S(1)} %multiply_convert_fusion, bf16[2048,3584]{1,0:T(8,128)(2,1)} %param.26, s32[]{:T(128)S(6)} %select_n.218), kind=kOutput, calls=%fused_computation.40 | convolution fusion | flops 117469184 | bytes 3858436 | tf_op jit(solution)/shard_map/dot_general | solution.py:157
  65.3 2.9 %fusion.52 = bf16[32,896]{1,0:T(8,128)(2,1)S(1)} fusion(bf16[32,2048]{1,0:T(8,128)(2,1)S(1)} %multiply_convert_fusion, bf16[2048,3584]{1,0:T(8,128)(2,1)} %param.25, s32[]{:T(128)S(6)} %select_n.218), kind=kOutput, calls=%fused_computation.39 | convolution fusion | flops 117469184 | bytes 3858436 | tf_op jit(solution)/shard_map/dot_general | solution.py:157
  68.1 2.9 %fusion.49 = bf16[32,896]{1,0:T(8,128)(2,1)S(1)} fusion(bf16[32,2048]{1,0:T(8,128)(2,1)S(1)} %multiply_convert_fusion, bf16[2048,3584]{1,0:T(8,128)(2,1)} %param.26, s32[]{:T(128)S(6)} %select_n.217), kind=kOutput, calls=%fused_computation.38 | convolution fusion | flops 117469184 | bytes 3858436 | tf_op jit(solution)/shard_map/dot_general | solution.py:157
  71.0 2.7 %fusion.46 = bf16[32,896]{1,0:T(8,128)(2,1)S(1)} fusion(bf16[32,2048]{1,0:T(8,128)(2,1)S(1)} %multiply_convert_fusion, bf16[2048,3584]{1,0:T(8,128)(2,1)} %param.25, s32[]{:T(128)S(6)} %select_n.217), kind=kOutput, calls=%fused_computation.37 | convolution fusion | flops 117469184 | bytes 3858436 | tf_op jit(solution)/shard_map/dot_general | solution.py:157
  73.7 2.9 %fusion.43 = bf16[32,896]{1,0:T(8,128)(2,1)S(1)} fusion(bf16[32,2048]{1,0:T(8,128)(2,1)S(1)} %multiply_convert_fusion, bf16[2048,3584]{1,0:T(8,128)(2,1)} %param.26, s32[]{:T(128)S(6)} %select_n.216), kind=kOutput, calls=%fused_computation.36 | convolution fusion | flops 117469184 | bytes 3858436 | tf_op jit(solution)/shard_map/dot_general | solution.py:157
  76.6 2.7 %fusion.40 = bf16[32,896]{1,0:T(8,128)(2,1)S(1)} fusion(bf16[32,2048]{1,0:T(8,128)(2,1)S(1)} %multiply_convert_fusion, bf16[2048,3584]{1,0:T(8,128)(2,1)} %param.25, s32[]{:T(128)S(6)} %select_n.216), kind=kOutput, calls=%fused_computation.35 | convolution fusion | flops 117469184 | bytes 3858436 | tf_op jit(solution)/shard_map/dot_general | solution.py:157
  82.2 2.7 %fusion.61 = bf16[32,896]{1,0:T(8,128)(2,1)S(1)} fusion(bf16[32,2048]{1,0:T(8,128)(2,1)S(1)} %multiply_convert_fusion, bf16[2048,3584]{1,0:T(8,128)(2,1)} %param.26, s32[]{:T(128)S(6)} %select_n.219), kind=kOutput, calls=%fused_computation.42 | convolution fusion | flops 117469184 | bytes 3858436 | tf_op jit(solution)/shard_map/dot_general | solution.py:157
  84.9 2.7 %fusion.58 = bf16[32,896]{1,0:T(8,128)(2,1)S(1)} fusion(bf16[32,2048]{1,0:T(8,128)(2,1)S(1)} %multiply_convert_fusion, bf16[2048,3584]{1,0:T(8,128)(2,1)} %param.25, s32[]{:T(128)S(6)} %select_n.219), kind=kOutput, calls=%fused_computation.41 | convolution fusion | flops 117469184 | bytes 3858436 | tf_op jit(solution)/shard_map/dot_general | solution.py:157
  87.9 2.8 %collective-permute-done.20 = bf16[32,1792]{1,0:T(8,128)(2,1)S(1)} collective-permute-done((bf16[32,1792]{1,0:T(8,128)(2,1)S(1)}, bf16[32,1792]{1,0:T(8,128)(2,1)S(1)}, u32[]{:S(2)}, u32[]{:S(2)}) %collective-permute-start.20) | collective-permute-done | bytes 114720 | tf_op jit(solution)/shard_map/ppermute | solution.py:169
  90.9 2.6 %collective-permute-start.22 = (bf16[32,896]{1,0:T(8,128)(2,1)S(1)}, bf16[32,896]{1,0:T(8,128)(2,1)S(1)}, u32[]{:S(2)}, u32[]{:S(2)}) collective-permute-start(bf16[32,896]{1,0:T(8,128)(2,1)S(1)} %fusion.94), channel_id=1, source_target_pairs={{0,4},{4,8},{8,12},{12,0},{1,5},{5,9},{9,13},{13,1},{2,6},{6,10},{... | collective-permute-start | bytes 172040 | tf_op jit(solution)/shard_map/ppermute | solution.py:184
  93.5 1.3 %collective-permute-start.21 = (bf16[32,896]{1,0:T(8,128)(2,1)S(1)}, bf16[32,896]{1,0:T(8,128)(2,1)S(1)}, u32[]{:S(2)}, u32[]{:S(2)}) collective-permute-start(bf16[32,896]{1,0:T(8,128)(2,1)S(1)} %fusion.94), channel_id=1, source_target_pairs={{0,12},{4,0},{8,4},{12,8},{1,13},{5,1},{9,5},{13,9},{2,14},{6,2},{... | collective-permute-start | bytes 172040 | tf_op jit(solution)/shard_map/ppermute | solution.py:184
  95.5 1.5 %collective-permute-done.22 = bf16[32,896]{1,0:T(8,128)(2,1)S(1)} collective-permute-done((bf16[32,896]{1,0:T(8,128)(2,1)S(1)}, bf16[32,896]{1,0:T(8,128)(2,1)S(1)}, u32[]{:S(2)}, u32[]{:S(2)}) %collective-permute-start.22) | collective-permute-done | bytes 57376 | tf_op jit(solution)/shard_map/ppermute | solution.py:184
  99.5 1.3 %collective-permute-done.24 = f32[2,8,2048]{2,1,0:T(8,128)S(1)} collective-permute-done((f32[2,8,2048]{2,1,0:T(8,128)S(1)}, f32[2,8,2048]{2,1,0:T(8,128)S(1)}, u32[]{:S(2)}, u32[]{:S(2)}) %collective-permute-start.24) | collective-permute-done | bytes 131104 | tf_op jit(solution)/shard_map/ppermute | solution.py:117
  101.9 3.3 %collective-permute-done.25 = f32[8,2048]{1,0:T(8,128)S(1)} collective-permute-done((f32[8,2048]{1,0:T(8,128)S(1)}, f32[8,2048]{1,0:T(8,128)S(1)}, u32[]{:S(2)}, u32[]{:S(2)}) %collective-permute-start.25) | collective-permute-done | bytes 65568 | tf_op jit(solution)/shard_map/ppermute | solution.py:117
  (98 shorter events, 23.4 us)
Async XLA Ops:
  0.0 27.5 %copy-start = (bf16[8,256,2,2,128]{4,3,2,1,0:T(2,128)(2,1)S(1)}, bf16[8,256,2,2,128]{4,3,2,1,0:T(2,128)(2,1)}, u32[]{:S(2)}) copy-start(bf16[8,256,2,2,128]{4,3,2,1,0:T(2,128)(2,1)} %param.28) | copy-start | bytes 6291460
  1.0 8.1 %collective-permute-start.2 = (f32[8]{0:T(128)S(1)}, f32[8]{0:T(128)S(1)}, u32[]{:S(2)}, u32[]{:S(2)}) collective-permute-start(f32[8]{0:T(128)S(1)} %fusion.98), channel_id=1, source_target_pairs={{0,12},{4,0},{8,4},{12,8},{1,13},{5,1},{9,5},{13,9},{2,14},{6,2},{... | collective-permute-start | bytes 104 | tf_op jit(solution)/shard_map/ppermute | solution.py:147
  6.1 4.4 %collective-permute-start.1 = (f32[8]{0:T(128)S(1)}, f32[8]{0:T(128)S(1)}, u32[]{:S(2)}, u32[]{:S(2)}) collective-permute-start(f32[8]{0:T(128)S(1)} %fusion.98), channel_id=1, source_target_pairs={{0,8},{4,12},{8,0},{12,4},{1,9},{5,13},{9,1},{13,5},{2,10},{6,14},... | collective-permute-start | bytes 104 | tf_op jit(solution)/shard_map/ppermute | solution.py:147
  6.1 5.3 %collective-permute-start = (f32[8]{0:T(128)S(1)}, f32[8]{0:T(128)S(1)}, u32[]{:S(2)}, u32[]{:S(2)}) collective-permute-start(f32[8]{0:T(128)S(1)} %fusion.98), channel_id=1, source_target_pairs={{0,4},{4,8},{8,12},{12,0},{1,5},{5,9},{9,13},{13,1},{2,6},{6,10},{... | collective-permute-start | bytes 104 | tf_op jit(solution)/shard_map/ppermute | solution.py:147
  12.3 1.9 %collective-permute-start.5 = (bf16[8,2048]{1,0:T(8,128)(2,1)S(1)}, bf16[8,2048]{1,0:T(8,128)(2,1)S(1)}, u32[]{:S(2)}, u32[]{:S(2)}) collective-permute-start(bf16[8,2048]{1,0:T(8,128)(2,1)S(1)} %fusion.100), channel_id=1, source_target_pairs={{0,3},{1,0},{2,1},{3,2},{4,7},{5,4},{6,5},{7,6},{8,11},{9,8},{10,9... | collective-permute-start | bytes 98312 | tf_op jit(solution)/shard_map/ppermute | solution.py:101
  12.4 4.1 %collective-permute-start.4 = (bf16[8,2048]{1,0:T(8,128)(2,1)S(1)}, bf16[8,2048]{1,0:T(8,128)(2,1)S(1)}, u32[]{:S(2)}, u32[]{:S(2)}) collective-permute-start(bf16[8,2048]{1,0:T(8,128)(2,1)S(1)} %fusion.100), channel_id=1, source_target_pairs={{0,2},{1,3},{2,0},{3,1},{4,6},{5,7},{6,4},{7,5},{8,10},{9,11},{10,... | collective-permute-start | bytes 98312 | tf_op jit(solution)/shard_map/ppermute | solution.py:101
  13.9 3.3 %collective-permute-start.3 = (bf16[8,2048]{1,0:T(8,128)(2,1)S(1)}, bf16[8,2048]{1,0:T(8,128)(2,1)S(1)}, u32[]{:S(2)}, u32[]{:S(2)}) collective-permute-start(bf16[8,2048]{1,0:T(8,128)(2,1)S(1)} %fusion.100), channel_id=1, source_target_pairs={{0,1},{1,2},{2,3},{3,0},{4,5},{5,6},{6,7},{7,4},{8,9},{9,10},{10,1... | collective-permute-start | bytes 98312 | tf_op jit(solution)/shard_map/ppermute | solution.py:101
  24.2 4.6 %collective-permute-start.6 = (f32[8,2560]{1,0:T(8,128)S(1)}, f32[8,2560]{1,0:T(8,128)S(1)}, u32[]{:S(2)}, u32[]{:S(2)}) collective-permute-start(f32[8,2560]{1,0:T(8,128)S(1)} %get-tuple-element.65), channel_id=1, source_target_pairs={{0,12},{4,0},{8,4},{12,8},{1,13},{5,1},{9,5},{13,9},{2,14},{6,2},{... | collective-permute-start | bytes 245768 | tf_op jit(solution)/shard_map/ppermute | solution.py:117
  24.8 8.2 %collective-permute-start.8 = (f32[8,2560]{1,0:T(8,128)S(1)}, f32[8,2560]{1,0:T(8,128)S(1)}, u32[]{:S(2)}, u32[]{:S(2)}) collective-permute-start(f32[8,2560]{1,0:T(8,128)S(1)} %get-tuple-element.66), channel_id=1, source_target_pairs={{0,8},{4,12},{8,0},{12,4},{1,9},{5,13},{9,1},{13,5},{2,10},{6,14},... | collective-permute-start | bytes 245768 | tf_op jit(solution)/shard_map/ppermute | solution.py:117
  25.9 7.1 %collective-permute-start.7 = (f32[8,2560]{1,0:T(8,128)S(1)}, f32[8,2560]{1,0:T(8,128)S(1)}, u32[]{:S(2)}, u32[]{:S(2)}) collective-permute-start(f32[8,2560]{1,0:T(8,128)S(1)} %get-tuple-element.67), channel_id=1, source_target_pairs={{0,4},{4,8},{8,12},{12,0},{1,5},{5,9},{9,13},{13,1},{2,6},{6,10},{... | collective-permute-start | bytes 245768 | tf_op jit(solution)/shard_map/ppermute | solution.py:117
  27.5 19.2 %copy-start.1 = (bf16[8,2048]{1,0:T(8,128)(2,1)S(1)}, bf16[8,2048]{1,0:T(8,128)(2,1)}, u32[]{:S(2)}) copy-start(bf16[8,2048]{1,0:T(8,128)(2,1)} %param.20) | copy-start | bytes 98308
  28.0 34.4 %copy-start.2 = (f32[2048]{0:T(1024)S(1)}, f32[2048]{0:T(1024)}, u32[]{:S(2)}) copy-start(f32[2048]{0:T(1024)} %param.24) | copy-start | bytes 24580
  34.5 4.2 %collective-permute-start.11 = (bf16[8,2048]{1,0:T(8,128)(2,1)S(1)}, bf16[8,2048]{1,0:T(8,128)(2,1)S(1)}, u32[]{:S(2)}, u32[]{:S(2)}) collective-permute-start(bf16[8,2048]{1,0:T(8,128)(2,1)S(1)} %bitcast.100), channel_id=1, source_target_pairs={{0,12},{4,0},{8,4},{12,8},{1,13},{5,1},{9,5},{13,9},{2,14},{6,2},{... | collective-permute-start | bytes 98312 | tf_op jit(solution)/shard_map/ppermute | solution.py:101
  35.8 5.2 %collective-permute-start.10 = (bf16[8,2048]{1,0:T(8,128)(2,1)S(1)}, bf16[8,2048]{1,0:T(8,128)(2,1)S(1)}, u32[]{:S(2)}, u32[]{:S(2)}) collective-permute-start(bf16[8,2048]{1,0:T(8,128)(2,1)S(1)} %bitcast.101), channel_id=1, source_target_pairs={{0,8},{4,12},{8,0},{12,4},{1,9},{5,13},{9,1},{13,5},{2,10},{6,14},... | collective-permute-start | bytes 98312 | tf_op jit(solution)/shard_map/ppermute | solution.py:101
  35.9 5.7 %collective-permute-start.9 = (bf16[8,2048]{1,0:T(8,128)(2,1)S(1)}, bf16[8,2048]{1,0:T(8,128)(2,1)S(1)}, u32[]{:S(2)}, u32[]{:S(2)}) collective-permute-start(bf16[8,2048]{1,0:T(8,128)(2,1)S(1)} %bitcast.102), channel_id=1, source_target_pairs={{0,4},{4,8},{8,12},{12,0},{1,5},{5,9},{9,13},{13,1},{2,6},{6,10},{... | collective-permute-start | bytes 98312 | tf_op jit(solution)/shard_map/ppermute | solution.py:101
  46.8 1.4 %collective-permute-start.12 = (f32[16,2048]{1,0:T(8,128)S(1)}, f32[16,2048]{1,0:T(8,128)S(1)}, u32[]{:S(2)}, u32[]{:S(2)}) collective-permute-start(f32[16,2048]{1,0:T(8,128)S(1)} %select_bitcast_fusion.1), channel_id=1, source_target_pairs={{0,1},{1,0},{2,3},{3,2},{4,5},{5,4},{6,7},{7,6},{8,9},{9,8},{10,11... | collective-permute-start | bytes 393224 | tf_op jit(solution)/shard_map/ppermute | solution.py:117
  48.2 5.6 %collective-permute-start.13 = (f32[16,2048]{1,0:T(8,128)S(1)}, f32[16,2048]{1,0:T(8,128)S(1)}, u32[]{:S(2)}, u32[]{:S(2)}) collective-permute-start(f32[16,2048]{1,0:T(8,128)S(1)} %bitcast_add_fusion.1), channel_id=1, source_target_pairs={{0,2},{2,0},{1,3},{3,1},{4,6},{6,4},{5,7},{7,5},{8,10},{10,8},{9,1... | collective-permute-start | bytes 393224 | tf_op jit(solution)/shard_map/ppermute | solution.py:147
  53.8 1.4 %collective-permute-start.14 = (f32[16,2048]{1,0:T(8,128)S(1)}, f32[16,2048]{1,0:T(8,128)S(1)}, u32[]{:S(2)}, u32[]{:S(2)}) collective-permute-start(f32[16,2048]{1,0:T(8,128)S(1)} %add.289), channel_id=1, source_target_pairs={{0,1},{1,0},{2,3},{3,2},{4,5},{5,4},{6,7},{7,6},{8,9},{9,8},{10,11... | collective-permute-start | bytes 393224 | tf_op jit(solution)/shard_map/ppermute | solution.py:139
  55.5 3.5 %collective-permute-start.17 = (f32[32]{0:T(128)S(1)}, f32[32]{0:T(128)S(1)}, u32[]{:S(2)}, u32[]{:S(2)}) collective-permute-start(f32[32]{0:T(128)S(1)} %reduce_sum.62), channel_id=1, source_target_pairs={{0,12},{4,0},{8,4},{12,8},{1,13},{5,1},{9,5},{13,9},{2,14},{6,2},{... | collective-permute-start | bytes 392 | tf_op jit(solution)/shard_map/ppermute | solution.py:147
  56.7 4.4 %collective-permute-start.16 = (f32[32]{0:T(128)S(1)}, f32[32]{0:T(128)S(1)}, u32[]{:S(2)}, u32[]{:S(2)}) collective-permute-start(f32[32]{0:T(128)S(1)} %reduce_sum.62), channel_id=1, source_target_pairs={{0,8},{4,12},{8,0},{12,4},{1,9},{5,13},{9,1},{13,5},{2,10},{6,14},... | collective-permute-start | bytes 392 | tf_op jit(solution)/shard_map/ppermute | solution.py:147
  57.1 5.3 %collective-permute-start.15 = (f32[32]{0:T(128)S(1)}, f32[32]{0:T(128)S(1)}, u32[]{:S(2)}, u32[]{:S(2)}) collective-permute-start(f32[32]{0:T(128)S(1)} %reduce_sum.62), channel_id=1, source_target_pairs={{0,4},{4,8},{8,12},{12,0},{1,5},{5,9},{9,13},{13,1},{2,6},{6,10},{... | collective-permute-start | bytes 392 | tf_op jit(solution)/shard_map/ppermute | solution.py:147
  65.2 29.5 %slice-start = ((s8[14680064]{0:T(1024)(128)(4,1)}), s8[4194304]{0:T(1024)(128)(4,1)S(1)}, s32[]{:S(2)}) async-start(s8[14680064]{0:T(1024)(128)(4,1)} %bitcast.85), calls=%async_computation | async-start | bytes 8388608
  68.1 26.7 %slice-start.1 = ((s8[14680064]{0:T(1024)(128)(4,1)}), s8[4194304]{0:T(1024)(128)(4,1)S(1)}, s32[]{:S(2)}) async-start(s8[14680064]{0:T(1024)(128)(4,1)} %bitcast.85), calls=%async_computation.1 | async-start | bytes 8388608
  73.7 21.1 %slice-start.2 = ((s8[14680064]{0:T(1024)(128)(4,1)}), s8[4194304]{0:T(1024)(128)(4,1)S(1)}, s32[]{:S(2)}) async-start(s8[14680064]{0:T(1024)(128)(4,1)} %bitcast.85), calls=%async_computation.2 | async-start | bytes 8388608
  79.4 8.2 %collective-permute-start.18 = (bf16[32,1792]{1,0:T(8,128)(2,1)S(1)}, bf16[32,1792]{1,0:T(8,128)(2,1)S(1)}, u32[]{:S(2)}, u32[]{:S(2)}) collective-permute-start(bf16[32,1792]{1,0:T(8,128)(2,1)S(1)} %pad_maximum_fusion.3), channel_id=1, source_target_pairs={{0,12},{4,0},{8,4},{12,8},{1,13},{5,1},{9,5},{13,9},{2,14},{6,2},{... | collective-permute-start | bytes 344072 | tf_op jit(solution)/shard_map/ppermute | solution.py:169
  80.4 7.5 %collective-permute-start.19 = (bf16[32,1792]{1,0:T(8,128)(2,1)S(1)}, bf16[32,1792]{1,0:T(8,128)(2,1)S(1)}, u32[]{:S(2)}, u32[]{:S(2)}) collective-permute-start(bf16[32,1792]{1,0:T(8,128)(2,1)S(1)} %get-tuple-element.19), channel_id=1, source_target_pairs={{0,4},{4,8},{8,12},{12,0},{1,5},{5,9},{9,13},{13,1},{2,6},{6,10},{... | collective-permute-start | bytes 344072 | tf_op jit(solution)/shard_map/ppermute | solution.py:169
  81.5 9.2 %collective-permute-start.20 = (bf16[32,1792]{1,0:T(8,128)(2,1)S(1)}, bf16[32,1792]{1,0:T(8,128)(2,1)S(1)}, u32[]{:S(2)}, u32[]{:S(2)}) collective-permute-start(bf16[32,1792]{1,0:T(8,128)(2,1)S(1)} %get-tuple-element.20), channel_id=1, source_target_pairs={{0,8},{4,12},{8,0},{12,4},{1,9},{5,13},{9,1},{13,5},{2,10},{6,14},... | collective-permute-start | bytes 344072 | tf_op jit(solution)/shard_map/ppermute | solution.py:169
  90.8 6.9 %collective-permute-start.23 = (bf16[32,896]{1,0:T(8,128)(2,1)S(1)}, bf16[32,896]{1,0:T(8,128)(2,1)S(1)}, u32[]{:S(2)}, u32[]{:S(2)}) collective-permute-start(bf16[32,896]{1,0:T(8,128)(2,1)S(1)} %fusion.94), channel_id=1, source_target_pairs={{0,8},{4,12},{8,0},{12,4},{1,9},{5,13},{9,1},{13,5},{2,10},{6,14},... | collective-permute-start | bytes 172040 | tf_op jit(solution)/shard_map/ppermute | solution.py:184
  90.9 6.1 %collective-permute-start.22 = (bf16[32,896]{1,0:T(8,128)(2,1)S(1)}, bf16[32,896]{1,0:T(8,128)(2,1)S(1)}, u32[]{:S(2)}, u32[]{:S(2)}) collective-permute-start(bf16[32,896]{1,0:T(8,128)(2,1)S(1)} %fusion.94), channel_id=1, source_target_pairs={{0,4},{4,8},{8,12},{12,0},{1,5},{5,9},{9,13},{13,1},{2,6},{6,10},{... | collective-permute-start | bytes 172040 | tf_op jit(solution)/shard_map/ppermute | solution.py:184
  93.5 5.0 %collective-permute-start.21 = (bf16[32,896]{1,0:T(8,128)(2,1)S(1)}, bf16[32,896]{1,0:T(8,128)(2,1)S(1)}, u32[]{:S(2)}, u32[]{:S(2)}) collective-permute-start(bf16[32,896]{1,0:T(8,128)(2,1)S(1)} %fusion.94), channel_id=1, source_target_pairs={{0,12},{4,0},{8,4},{12,8},{1,13},{5,1},{9,5},{13,9},{2,14},{6,2},{... | collective-permute-start | bytes 172040 | tf_op jit(solution)/shard_map/ppermute | solution.py:184
  99.4 1.4 %collective-permute-start.24 = (f32[2,8,2048]{2,1,0:T(8,128)S(1)}, f32[2,8,2048]{2,1,0:T(8,128)S(1)}, u32[]{:S(2)}, u32[]{:S(2)}) collective-permute-start(f32[2,8,2048]{2,1,0:T(8,128)S(1)} %select_bitcast_fusion), channel_id=1, source_target_pairs={{0,1},{1,0},{2,3},{3,2},{4,5},{5,4},{6,7},{7,6},{8,9},{9,8},{10,11... | collective-permute-start | bytes 393224 | tf_op jit(solution)/shard_map/ppermute | solution.py:117
  100.9 4.3 %collective-permute-start.25 = (f32[8,2048]{1,0:T(8,128)S(1)}, f32[8,2048]{1,0:T(8,128)S(1)}, u32[]{:S(2)}, u32[]{:S(2)}) collective-permute-start(f32[8,2048]{1,0:T(8,128)S(1)} %select_bitcast_fusion.7), channel_id=1, source_target_pairs={{0,2},{2,0},{1,3},{3,1},{4,6},{6,4},{5,7},{7,5},{8,10},{10,8},{9,1... | collective-permute-start | bytes 196616 | tf_op jit(solution)/shard_map/ppermute | solution.py:117
  (1 other events, 15.4 us)
